TPU v7x, 32 devices: a whole 2x2x4 slice. The times are simulated.
32 devices in a mesh: row: 2 (over core), col: 2 (over x), seq: 8 (over z, y).
Axes of the slice: x: 2, y: 2, z: 4, core: 2. Of those that a mesh axis runs over, the one named last changes fastest.
Arguments:
- states: bfloat16 [128, 4, 5120], P('col', None, 'row'), may hold values from -64 to 64
- norm_gain: float32 [5120], P('row'), may hold values from 0.1 to 1.9
- wq: bfloat16 [5120, 4096], P('row', 'col'), may hold values from -0.078125 to 0.078125
- wk: bfloat16 [5120, 1024], P('row', 'col'), may hold values from -0.21875 to 0.21875
- wv: bfloat16 [5120, 1024], P('row', 'col'), may hold values from -0.078125 to 0.078125
- wo: bfloat16 [4096, 5120], P('col', 'row'), may hold values from -0.09375 to 0.09375
- lengths: int32 [128], P('row'), may hold values from 1 to 8192, as said below
- slot_request: int32 [800], P(('row', 'seq')), may hold values from 0 to 64, as said below
- slot_block_number: int32 [800], P(('row', 'seq')), may hold values from 0 to 63, as said below
- paged_key_cache: bfloat16 [800, 128, 1024], P(('row', 'seq'), None, 'col'), may hold values from -120 to 120
- paged_value_cache: bfloat16 [800, 128, 1024], P(('row', 'seq'), None, 'col'), may hold values from -6 to 6
Outputs:
- attended: bfloat16 [128, 4, 5120], P('col', None, 'row')
- new_keys: bfloat16 [128, 4, 1024], P('row', None, 'col')
- new_values: bfloat16 [128, 4, 1024], P('row', None, 'col')
Inputs may be any that keep to these rules, and one draw needn't show every extreme that they name: `lengths`: within every 64 consecutive requests, 8 have exactly 8192 cached tokens and the others fewer than 128. `slot_request`: each request's block 0 and every block that holds a position visible to one of its steps stand in exactly one slot of its index of row; a long request has exactly 33 slots. 64 marks an empty slot; every index of row has empty slots. `slot_block_number`: 0 in empty slots.
All inputs are finite; a program needn't handle non-finite values.
Results may differ from a plain program's by a relative error of at most 0.034.
Values may be sent and summed in bfloat16 or wider, within the bound.
No kernel may reach another device: no remote copies, remote signals or barrier semaphores. Data moves between devices by JAX's collectives and lax.ppermute only.
A program may use at most 192 MiB of HBM per device.

v0:
```python
import math

import jax
import jax.numpy as jnp
from jax import lax
from jax.sharding import PartitionSpec as P

D = 5120
HEAD_SIZE = 128
WINDOW = 4096
SINK = 4
QUERY_PER_KEY = 4


EPSILON = 1e-05
NEGATIVE_FILL = -1e30
ROPE_BASE = 100000000.0


def rotary_apply(values, token_positions):
    half_dim = values.shape[-1] // 2
    frequency = ROPE_BASE ** (-(jnp.arange(half_dim, dtype=jnp.float32) * 2.0 / values.shape[-1]))
    angles = (token_positions.astype(jnp.float32)[..., None] * frequency)[..., None, :]
    cosine = jnp.cos(angles)
    sine_part = jnp.sin(angles)
    lower = values[..., :half_dim]
    upper = values[..., half_dim:]
    return jnp.concatenate(
        [lower * cosine - upper * sine_part, upper * cosine + lower * sine_part], -1
    )


def slot_parts(query_rows, lengths, slot_request, slot_block_number, key_rows, value_rows):
    req_count = query_rows.shape[0]
    step_count = query_rows.shape[1]
    block_len = key_rows.shape[1]
    picked = jnp.minimum(slot_request, req_count - 1)
    in_use = slot_request < req_count
    slot_queries = query_rows[picked]
    scores = jnp.einsum(
        "nsagh,nbah->nasgb", slot_queries, key_rows, preferred_element_type=jnp.float32
    ) * (1.0 / math.sqrt(HEAD_SIZE))
    key_pos = (
        slot_block_number[:, None] * block_len + jnp.arange(block_len, dtype=jnp.int32)[None, :]
    )
    own_len = lengths[picked]
    query_pos = own_len[:, None] + jnp.arange(step_count, dtype=jnp.int32)[None, :]
    visible = (
        in_use[:, None, None]
        & (key_pos[:, None, :] < own_len[:, None, None])
        & ((key_pos[:, None, :] < SINK) | (key_pos[:, None, :] > query_pos[:, :, None] - WINDOW))
    )
    visible = visible[:, None, :, None, :]
    slot_peak = jnp.max(jnp.where(visible, scores, NEGATIVE_FILL), -1)
    weights = jnp.where(visible, jnp.exp(scores - slot_peak[..., None]), 0.0)
    slot_total = jnp.sum(weights, -1)
    slot_acc = jnp.einsum(
        "nasgb,nbah->nasgh",
        weights.astype(jnp.bfloat16),
        value_rows,
        preferred_element_type=jnp.float32,
    )
    member = slot_request[None, :] == jnp.arange(req_count, dtype=jnp.int32)[:, None]
    local_peak = jnp.max(
        jnp.where(member[:, :, None, None, None], slot_peak[None], NEGATIVE_FILL), 1
    )
    return (local_peak, (slot_peak, slot_total, slot_acc, member, picked))


def pool_sums(held, running_peak):
    slot_peak, slot_total, slot_acc, member, picked = held
    factor = jnp.exp(slot_peak - running_peak[picked])
    as_member = member.astype(jnp.float32)
    running_totals = jnp.einsum(
        "rn,nasg->rasg", as_member, slot_total * factor, precision=lax.Precision.HIGHEST
    )
    weighted_values = jnp.einsum(
        "rn,nasgh->rasgh", as_member, slot_acc * factor[..., None], precision=lax.Precision.HIGHEST
    )
    return (running_totals, weighted_values)


def fresh_part(query_rows, key_all, value_all):
    step_count = query_rows.shape[1]
    used = key_all.shape[1]
    scores = jnp.einsum(
        "rsagh,ruah->rasgu", query_rows, key_all, preferred_element_type=jnp.float32
    ) * (1.0 / math.sqrt(HEAD_SIZE))
    causal = (
        jnp.arange(used, dtype=jnp.int32)[None, :]
        <= jnp.arange(step_count, dtype=jnp.int32)[:, None]
    )
    causal = causal[None, None, :, None, :]
    running_peak = jnp.max(jnp.where(causal, scores, NEGATIVE_FILL), -1)
    weights = jnp.where(causal, jnp.exp(scores - running_peak[..., None]), 0.0)
    running_totals = jnp.sum(weights, -1)
    weighted_values = jnp.einsum(
        "rasgu,ruah->rasgh",
        weights.astype(jnp.bfloat16),
        value_all,
        preferred_element_type=jnp.float32,
    )
    return (running_peak, running_totals, weighted_values)


def merge_parts(earlier, later):
    running_peak = jnp.maximum(earlier[0], later[0])
    first_factor = jnp.exp(earlier[0] - running_peak)
    second_factor = jnp.exp(later[0] - running_peak)
    running_totals = earlier[1] * first_factor + later[1] * second_factor
    weighted_values = earlier[2] * first_factor[..., None] + later[2] * second_factor[..., None]
    return (running_peak, running_totals, weighted_values)


def on_device(
    states,
    norm_gain,
    wq,
    wk,
    wv,
    wo,
    lengths,
    slot_request,
    slot_block_number,
    paged_key_cache,
    paged_value_cache,
):
    q_width = wq.shape[1]
    k_width = wk.shape[1]
    heads_kv = k_width // HEAD_SIZE
    req_count = lengths.shape[0]
    block_len = paged_key_cache.shape[1]
    key_rows = paged_key_cache.reshape(paged_key_cache.shape[0], block_len, heads_kv, HEAD_SIZE)
    value_rows = paged_value_cache.reshape(
        paged_value_cache.shape[0], block_len, heads_kv, HEAD_SIZE
    )
    step_count = states.shape[1]
    as_float = states.astype(jnp.float32)
    squares = lax.psum(jnp.sum(as_float * as_float, -1), "row")
    normed = (as_float * lax.rsqrt(squares / D + EPSILON)[..., None] * norm_gain).astype(
        jnp.bfloat16
    )
    gathered = lax.all_gather(normed, "col", axis=0, tiled=True)
    piece_rows = gathered.reshape(req_count * lax.axis_size("row") * step_count, -1)
    parts_out = [
        jnp.dot(piece_rows, matrix, preferred_element_type=jnp.float32) for matrix in (wq, wk, wv)
    ]
    output_projected = lax.psum_scatter(
        jnp.concatenate(parts_out, axis=-1)
        .reshape(req_count * lax.axis_size("row"), step_count, -1)
        .astype(jnp.bfloat16),
        "row",
        scatter_dimension=0,
        tiled=True,
    ).astype(jnp.float32)
    token_positions = lengths[:, None] + jnp.arange(step_count, dtype=jnp.int32)[None, :]
    query_rows = rotary_apply(
        output_projected[..., :q_width].reshape(req_count, step_count, -1, HEAD_SIZE),
        token_positions,
    ).astype(jnp.bfloat16)
    query_rows = query_rows.reshape(req_count, step_count, heads_kv, QUERY_PER_KEY, HEAD_SIZE)
    current_key = rotary_apply(
        output_projected[..., q_width : q_width + k_width].reshape(
            req_count, step_count, heads_kv, HEAD_SIZE
        ),
        token_positions,
    ).astype(jnp.bfloat16)
    current_value = (
        output_projected[..., q_width + k_width :]
        .reshape(req_count, step_count, heads_kv, HEAD_SIZE)
        .astype(jnp.bfloat16)
    )
    local_peak, held = slot_parts(
        query_rows, lengths, slot_request, slot_block_number, key_rows, value_rows
    )
    running_peak = lax.pmax(local_peak, "seq")
    running_totals, weighted_values = pool_sums(held, running_peak)
    running_totals, weighted_values = (
        lax.psum(running_totals.astype(jnp.bfloat16), "seq").astype(jnp.float32),
        lax.psum(weighted_values.astype(jnp.bfloat16), "seq").astype(jnp.float32),
    )
    fresh = fresh_part(query_rows, current_key, current_value)
    running_peak, running_totals, weighted_values = merge_parts(
        (running_peak, running_totals, weighted_values), fresh
    )
    heads_out = (
        (weighted_values / running_totals[..., None])
        .transpose(0, 2, 1, 3, 4)
        .reshape(req_count, step_count, -1)
        .astype(jnp.bfloat16)
    )
    piece_rows = lax.all_gather(heads_out, "row", axis=0, tiled=True)
    row_count = piece_rows.shape[0]
    product = jnp.dot(
        piece_rows.reshape(row_count * step_count, -1), wo, preferred_element_type=jnp.float32
    )
    partials = product.reshape(row_count, step_count, -1)
    attended = lax.psum_scatter(
        partials.astype(jnp.bfloat16), "col", scatter_dimension=0, tiled=True
    )
    return (
        attended,
        current_key.reshape(req_count, step_count, k_width),
        current_value.reshape(req_count, step_count, k_width),
    )


def solution(mesh):
    in_specs = (
        P("col", None, "row"),
        P("row"),
        P("row", "col"),
        P("row", "col"),
        P("row", "col"),
        P("col", "row"),
        P("row"),
        P(("row", "seq")),
        P(("row", "seq")),
        P(("row", "seq"), None, "col"),
        P(("row", "seq"), None, "col"),
    )
    out_specs = (P("col", None, "row"), P("row", None, "col"), P("row", None, "col"))
    return jax.shard_map(
        on_device, mesh=mesh, in_specs=in_specs, out_specs=out_specs, check_vma=False
    )
```

profile of v0, /device:TPU:0, one launch (start us, length us, event | category | flops | bytes accessed | tf_op | source)
XLA Modules:
  0.0 341.6 jit_solution(11022406717256435798)
XLA Ops:
  7.2 2.2 fusion.9
  9.5 2.6 psum.21
  12.1 0.1 copy.130
  12.2 3.1 fusion.11
  15.4 41.7 %all-gather.3.cloned.1.call-done = bf16[128,4,2560]{2,1,0:T(4,128)(2,1)} async-done(((bf16[64,4,2560]{2,1,0:T(4,128)(2,1)}), bf16[128,4,2560]{2,1,0:T(4,128)(2,1)}) %all-gather.3.cloned.1.call-update) | async-done | bytes 2621456 | tf_op jit(solution)/shard_map/all_gather | solution.py:143
  57.1 5.3 %reshape.218 = bf16[512,2560]{1,0:T(8,128)(2,1)} reshape(bf16[128,4,2560]{2,1,0:T(4,128)(2,1)} %all-gather.3.cloned.1.call-done) | data formatting | bytes 5242880 | tf_op jit(solution)/shard_map/reshape | solution.py:144
  62.5 3.4 convolution_convert_fusion.1
  65.9 1.5 convolution_convert_fusion.2
  67.4 8.5 %convolution_convert_fusion = bf16[512,2048]{1,0:T(8,128)(2,1)S(1)} fusion(bf16[512,2560]{1,0:T(8,128)(2,1)S(1)} %copy-done.4, bf16[2560,2048]{1,0:T(8,128)(2,1)} %param.13), kind=kOutput, calls=%fused_computation.13 | convolution fusion | flops 5369757696 | bytes 15204352 | tf_op jit(solution)/shard_map/dot_general | solution.py:146
  75.9 0.3 pad_maximum_fusion
  76.2 2.7 convert_element_type.70
  79.0 0.6 copy-done.12
  79.6 0.8 gather_fusion
  80.4 0.1 add_convert_fusion.1
  80.4 1.6 multiply_cosine_fusion
  82.0 12.3 %reshape.220 = bf16[50,128,4,128]{3,2,1,0:T(4,128)(2,1)} reshape(bf16[50,128,512]{2,1,0:T(8,128)(2,1)} %param.20) | data formatting | bytes 13107200 | tf_op jit(solution)/shard_map/reshape | solution.py:133
  94.3 12.4 %reshape.221 = bf16[50,128,4,128]{3,2,1,0:T(4,128)(2,1)} reshape(bf16[50,128,512]{2,1,0:T(8,128)(2,1)} %param.21) | data formatting | bytes 13107200 | tf_op jit(solution)/shard_map/reshape | solution.py:134
  106.8 0.6 dynamic-slice
  108.0 0.6 iota_compare_fusion.3
  108.6 0.7 iota_compare_fusion
  109.3 0.1 compare_and_fusion
  109.4 0.1 iota_add_fusion
  109.4 0.1 add_add_fusion
  109.5 0.1 or_and_fusion
  109.7 1.8 dynamic-slice_convert_fusion
  111.6 1.7 slice.34
  113.3 0.5 copy-done.3
  113.8 1.2 multiply_subtract_fusion
  115.0 2.4 reshape.258
  117.4 0.8 fusion.50
  118.3 0.6 subtract_convert_fusion
  118.8 1.4 pad_maximum_fusion.1
  120.3 0.6 copy.168
  120.9 2.2 gather_fusion.1
  123.0 10.3 %fusion.33 = f32[64,4,4,4,4]{3,4,2,1,0:T(4,128)S(1)} fusion(bf16[64,4,4,4,128]{4,3,2,0,1:T(4,128)(2,1)S(1)} %pad_maximum_fusion.1, bf16[64,4,4,64]{3,1,2,0:T(4,128)(2,1)} %get-tuple-element.34, bf16[64,4,4,64]{3,1,2,0:T(4,128)(2,1)S(1)} %get-tuple-element.33), kind=kOutput, calls=%fused_computation.49 | convolution fusion | flops 4718592 | bytes 1376256 | tf_op jit(solution)/shard_map/rsagh,ruah->rasgu/dot_general | solution.py:86
  133.3 1.4 copy.144
  134.8 6.8 %select_reduce_fusion.1 = (f32[50,4,4,4]{3,2,1,0:T(4,128)S(1)}, f32[50,4,4,4,128]{4,3,2,1,0:T(4,128)S(1)}) fusion(pred[50,4,128]{2,1,0:T(4,128)(4,1)S(1)} %or_and_fusion, bf16[50,4,4,4,128]{4,3,1,2,0:T(4,128)(2,1)} %gather_fusion.1, bf16[50,128,4,128,1]{3,2,1,0,4:T(4,128)(2,1)} %bitcast.60), kind=kOutput, calls=%fused_computation.27 | convolution fusion | flops 106083200 | bytes 9049600 | tf_op jit(solution)/shard_map/nsagh,nbah->nasgb/dot_general | solution.py:40
  141.6 1.0 select_reduce_fusion
  142.6 37.0 %pmax.7 = f32[64,4,4,4]{0,3,2,1:T(4,128)S(1)} all-reduce(f32[64,4,4,4]{0,3,2,1:T(4,128)S(1)} %select_reduce_fusion), channel_id=1, replica_groups=mesh['row'=2,'col'=2,'seq'=8] {'seq'}, use_global_device_ids=true, to_apply=%region_5.6 | all-reduce | flops 4096 | bytes 32768 | tf_op jit(solution)/shard_map/pmax | solution.py:176
  179.7 2.7 fusion.24
  182.4 0.4 copy.142
  182.8 0.9 gather_fusion.2
  183.7 0.1 fusion.49
  183.8 4.5 %fusion.20 = f32[50,4,4,4,128]{4,3,2,1,0:T(4,128)S(1)} fusion(bf16[50,128,4,128,1]{3,2,1,0,4:T(4,128)(2,1)} %bitcast.59, f32[50,4,4,4,128]{4,3,2,1,0:T(4,128)S(1)} %get-tuple-element.42, f32[50,4,4,4]{3,2,1,0:T(4,128)S(1)} %bitcast.67, f32[50,4,4,4]{3,2,1,0:T(4,128)S(1)} %get-tuple-element.41, pred[50,4,128]{2,1,0:T(4,128)(4,1)} %copy-done.9), kind=kOutput, calls=%fused_computation.30 | convolution fusion | flops 106905600 | bytes 9881600 | tf_op jit(solution)/shard_map/nasgb,nbah->nasgh/dot_general | solution.py:57
  188.4 3.2 fusion.17
  191.7 0.2 select_reduce_fusion.2
  191.8 1.8 slice.47
  193.7 0.2 fusion.36
  193.9 1.9 copy.148
  195.8 0.3 copy.151
  196.1 0.2 fusion.41
  196.4 33.6 %psum.23 = bf16[64,4,4,4]{0,3,2,1:T(4,128)(2,1)S(1)} all-reduce(bf16[64,4,4,4]{0,3,2,1:T(4,128)(2,1)S(1)} %convert_element_type.80), channel_id=1, replica_groups=mesh['row'=2,'col'=2,'seq'=8] {'seq'}, use_global_device_ids=true, to_apply=%region_9.10 | all-reduce | flops 4096 | bytes 16384 | tf_op jit(solution)/shard_map/psum | solution.py:179
  230.0 0.6 fusion.31
  230.6 35.7 %all-reduce.4.cloned.1.call-done = bf16[64,4,4,4,128]{4,0,3,2,1:T(8,128)(2,1)} async-done(((bf16[64,4,4,4,128]{4,0,3,2,1:T(8,128)(2,1)}), bf16[64,4,4,4,128]{4,0,3,2,1:T(8,128)(2,1)}) %all-reduce.4.cloned.1.call-update) | async-done | bytes 1048592 | tf_op jit(solution)/shard_map/psum | solution.py:180
  266.3 3.4 fusion.23
  269.7 0.8 copy.154
  270.5 1.6 convert_element_type.84
  272.2 10.3 %all-gather.5.cloned.1.call-done = bf16[128,4,2048]{2,0,1:T(8,128)(2,1)} async-done(((bf16[64,4,2048]{2,0,1:T(8,128)(2,1)}), bf16[128,4,2048]{2,0,1:T(8,128)(2,1)}) %all-gather.5.cloned.1.call-update) | async-done | bytes 2097168 | tf_op jit(solution)/shard_map/all_gather | solution.py:192
  282.5 10.0 %fusion.6 = bf16[128,4,2560]{2,0,1:T(8,128)(2,1)} fusion(bf16[128,4,2048]{2,0,1:T(8,128)(2,1)} %all-gather.5.cloned.1.call-done, bf16[2048,2560]{1,0:T(8,128)(2,1)} %param.16), kind=kOutput, calls=%fused_computation.9 | convolution fusion | flops 5370019840 | bytes 15204352 | tf_op jit(solution)/shard_map/dot_general | solution.py:194
  292.5 0.9 copy-done.6
  293.5 0.1 copy-done.7
  293.5 1.1 fusion.51
  294.6 36.9 %reduce-scatter.2.cloned.1.call-done = bf16[64,4,2560]{2,0,1:T(8,128)(2,1)} async-done(((bf16[128,4,2560]{2,0,1:T(8,128)(2,1)}), bf16[64,4,2560]{2,0,1:T(8,128)(2,1)}) %reduce-scatter.2.cloned.1.call-update) | async-done | bytes 1310736 | tf_op jit(solution)/shard_map/reduce_scatter | solution.py:198
  331.4 3.4 copy.155
  (55 shorter events, 0.6 us)
Async XLA Ops:
  7.2 55.3 %copy-start = (bf16[2560,512]{1,0:T(8,128)(2,1)S(1)}, bf16[2560,512]{1,0:T(8,128)(2,1)}, u32[]{:S(2)}) copy-start(bf16[2560,512]{1,0:T(8,128)(2,1)} %param.15) | copy-start | bytes 7864324
  7.2 50.0 %all-gather.3.cloned.1.call-start = ((), (), s32[]{:S(2)}) async-start(), calls=%async_computation.1 | async-start | bytes 3932160 | tf_op jit(solution)/shard_map/all_gather | solution.py:143
  15.4 94.3 %all-reduce.6.cloned.1.call-start = ((), (), s32[]{:S(2)}) async-start(), calls=%async_computation.5 | async-start | bytes 6291456
  62.5 3.4 %copy-start.4 = (bf16[512,2560]{1,0:T(8,128)(2,1)S(1)}, bf16[512,2560]{1,0:T(8,128)(2,1)}, u32[]{:S(2)}) copy-start(bf16[512,2560]{1,0:T(8,128)(2,1)} %reshape.218) | copy-start | bytes 7864324
  62.5 3.4 %copy-start.15 = (bf16[2560,512]{1,0:T(8,128)(2,1)S(1)}, bf16[2560,512]{1,0:T(8,128)(2,1)}, u32[]{:S(2)}) copy-start(bf16[2560,512]{1,0:T(8,128)(2,1)} %param.14) | copy-start | bytes 7864324
  78.9 0.7 copy-start.12
  78.9 0.7 copy-start.2
  78.9 187.4 %all-reduce.4.cloned.1.call-start = ((), (), s32[]{:S(2)}) async-start(), calls=%async_computation.2 | async-start | bytes 2097152 | tf_op jit(solution)/shard_map/psum | solution.py:180
  79.6 41.3 %copy-start.11 = (s32[1024]{0:T(1024)}, s32[1024]{0:T(1024)S(1)}, u32[]{:S(2)}) copy-start(s32[1024]{0:T(1024)S(1)} %pad_clamp_fusion) | copy-start | bytes 12292
  94.3 12.4 %copy-start.17 = (u32[32]{0:T(128)S(1)}, u32[32]{0:T(128)}, u32[]{:S(2)}) copy-start(u32[32]{0:T(128)} %constant.40) | copy-start | bytes 388
  94.3 14.3 %copy-start.16 = (s32[50]{0:T(128)S(1)}, s32[50]{0:T(128)}, u32[]{:S(2)}) copy-start(s32[50]{0:T(128)} %param.19) | copy-start | bytes 604
  109.7 25.1 %copy-start.9 = (pred[50,4,128]{2,1,0:T(4,128)(4,1)}, pred[50,4,128]{2,1,0:T(4,128)(4,1)S(1)}, u32[]{:S(2)}) copy-start(pred[50,4,128]{2,1,0:T(4,128)(4,1)S(1)} %or_and_fusion) | copy-start | bytes 76804
  111.5 2.3 copy-start.3
  115.0 8.0 %copy-start.5 = (bf16[64,4,4,64]{3,1,2,0:T(4,128)(2,1)}, bf16[64,4,4,64]{3,1,2,0:T(4,128)(2,1)S(1)}, u32[]{:S(2)}) copy-start(bf16[64,4,4,64]{3,1,2,0:T(4,128)(2,1)S(1)} %get-tuple-element.33) | copy-start | bytes 393220
  134.7 6.9 %copy-start.10 = (pred[64,50]{0,1:T(8,128)(4,1)S(1)}, pred[64,50]{0,1:T(8,128)(4,1)}, u32[]{:S(2)}) copy-start(pred[64,50]{0,1:T(8,128)(4,1)} %iota_compare_fusion) | copy-start | bytes 9604
  183.8 4.6 %copy-start.13 = (s32[50]{0:T(128)S(1)}, s32[50]{0:T(128)}, u32[]{:S(2)}) copy-start(s32[50]{0:T(128)} %param.18) | copy-start | bytes 604
  188.4 3.3 copy-start.14
  191.6 90.9 %all-gather.5.cloned.1.call-start = ((), (), s32[]{:S(2)}) async-start(), calls=%async_computation.3 | async-start | bytes 3145728 | tf_op jit(solution)/shard_map/all_gather | solution.py:192
  193.9 36.1 %copy-start.8 = (bf16[64,4,512]{2,1,0:T(4,128)(2,1)S(1)}, bf16[64,4,512]{2,1,0:T(4,128)(2,1)}, u32[]{:S(2)}) copy-start(bf16[64,4,512]{2,1,0:T(4,128)(2,1)} %slice.47) | copy-start | bytes 786436
  272.1 59.3 %reduce-scatter.2.cloned.1.call-start = ((), (), s32[]{:S(2)}) async-start(), calls=%async_computation.4 | async-start | bytes 3932160 | tf_op jit(solution)/shard_map/reduce_scatter | solution.py:198
  292.5 0.9 copy-start.6
  292.5 1.0 copy-start.7
  293.5 41.3 %copy-start.1 = (bf16[2560,512]{1,0:T(8,128)(2,1)S(1)}, bf16[2560,512]{1,0:T(8,128)(2,1)}, u32[]{:S(2)}) copy-start(bf16[2560,512]{1,0:T(8,128)(2,1)} %param.15) | copy-start | bytes 7864324
Sparse Core Ops, SparseCore 0:
  15.5 41.5 all-gather.2
  79.0 23.2 all-reduce.5
  191.7 74.5 all-reduce.3
  272.3 10.1 all-gather.4
  292.7 38.7 reduce-scatter.1
where the time goes:
time: 348 us; the launch traced here: 342 us
  waiting for transfers between devices  125 us (36%)
  blocking collectives  73.2 us (21%)
  local copies, waits for them, and re-layouts  56.7 us (16%)
  matrix products  49.1 us (14%)
  other arithmetic  22.7 us (7%)
  between operations  15 us (4%)
    all_gather x1, waiting for transfers between devices, on_device(): gathered = lax.all_gather(normed, 'col', axis=0, tiled=True)  41.7 us
    pmax x1, blocking collectives, on_device(): running_peak = lax.pmax(local_peak, 'seq')  37 us
    reduce_scatter x1, waiting for transfers between devices, on_device(): lax.psum_scatter(partials.astype(jnp.bfloat16), 'col', scatter_dimension=...  36.9 us
    psum x1, waiting for transfers between devices, on_device(): lax.psum(weighted_values.astype(jnp.bfloat16), 'seq').astype(jnp.float32)  35.7 us
    psum x1, blocking collectives, on_device(): lax.psum(running_totals.astype(jnp.bfloat16), 'seq').astype(jnp.float32)  33.6 us
    dot_general x3, matrix products, on_device(): jnp.dot(piece_rows, matrix, preferred_element_type=jnp.float32)  13.4 us
    reshape x1, local copies, waits for them, and re-layouts, on_device(): paged_value_cache.reshape(paged_value_cache.shape[0], block_len, heads_kv...  12.4 us
    reshape x1, local copies, waits for them, and re-layouts, on_device(): paged_key_cache.reshape(paged_key_cache.shape[0], block_len, heads_kv, HE...  12.3 us
  transfers between devices with their start and end apart: 5, of which 4 were waited for; matrix products, arithmetic and copies ran while one was open for 10% of the time, Pallas kernels for 0%

commit v1 on v0

--- a/solution.py
+++ b/solution.py
@@ -110,6 +110,39 @@
     running_totals = earlier[1] * first_factor + later[1] * second_factor
     weighted_values = earlier[2] * first_factor[..., None] + later[2] * second_factor[..., None]
     return (running_peak, running_totals, weighted_values)
+
+
+def seq_merge(peak, total, acc, n_seq, seq_index):
+    stages = n_seq.bit_length() - 1
+    assert 1 << stages == n_seq
+    req_count = peak.shape[0]
+    per = req_count // n_seq
+    rest = peak.shape[1:]
+    split = [2] * stages + [per]
+    stats = jnp.stack([peak, total], 0).reshape([2] + split + list(rest))
+    values = acc.reshape(split + list(acc.shape[1:]))
+    for bit in range(stages):
+        axis = stages - 1 - bit
+        mine = (seq_index >> bit) & 1
+        pairs = [(s, s ^ (1 << bit)) for s in range(n_seq)]
+        keep_stats = lax.dynamic_index_in_dim(stats, mine, axis + 1, keepdims=True)
+        send_stats = lax.dynamic_index_in_dim(stats, 1 - mine, axis + 1, keepdims=True)
+        keep_values = lax.dynamic_index_in_dim(values, mine, axis, keepdims=True)
+        send_values = lax.dynamic_index_in_dim(values, 1 - mine, axis, keepdims=True)
+        got_stats = lax.ppermute(send_stats, "seq", pairs)
+        got_values = lax.ppermute(send_values.astype(jnp.bfloat16), "seq", pairs).astype(
+            jnp.float32
+        )
+        top = jnp.maximum(keep_stats[0], got_stats[0])
+        keep_factor = jnp.exp(keep_stats[0] - top)
+        got_factor = jnp.exp(got_stats[0] - top)
+        stats = jnp.stack(
+            [top, keep_stats[1] * keep_factor + got_stats[1] * got_factor], 0
+        )
+        values = keep_values * keep_factor[..., None] + got_values * got_factor[..., None]
+    stats = stats.reshape((2, per) + tuple(rest))
+    values = values.reshape((per,) + tuple(acc.shape[1:]))
+    return (stats[0], stats[1], values)
 
 
 def on_device(
@@ -173,31 +206,39 @@
     local_peak, held = slot_parts(
         query_rows, lengths, slot_request, slot_block_number, key_rows, value_rows
     )
-    running_peak = lax.pmax(local_peak, "seq")
-    running_totals, weighted_values = pool_sums(held, running_peak)
-    running_totals, weighted_values = (
-        lax.psum(running_totals.astype(jnp.bfloat16), "seq").astype(jnp.float32),
-        lax.psum(weighted_values.astype(jnp.bfloat16), "seq").astype(jnp.float32),
-    )
-    fresh = fresh_part(query_rows, current_key, current_value)
+    local_totals, local_values = pool_sums(held, local_peak)
+    n_seq = lax.axis_size("seq")
+    per = req_count // n_seq
+    seq_index = lax.axis_index("seq")
+    mine = seq_index * per
+    running_peak, running_totals, weighted_values = seq_merge(
+        local_peak, local_totals, local_values, n_seq, seq_index
+    )
+    own_queries = lax.dynamic_slice_in_dim(query_rows, mine, per, 0)
+    fresh = fresh_part(
+        own_queries,
+        lax.dynamic_slice_in_dim(current_key, mine, per, 0),
+        lax.dynamic_slice_in_dim(current_value, mine, per, 0),
+    )
     running_peak, running_totals, weighted_values = merge_parts(
         (running_peak, running_totals, weighted_values), fresh
     )
     heads_out = (
         (weighted_values / running_totals[..., None])
         .transpose(0, 2, 1, 3, 4)
-        .reshape(req_count, step_count, -1)
+        .reshape(per, step_count, -1)
         .astype(jnp.bfloat16)
     )
-    piece_rows = lax.all_gather(heads_out, "row", axis=0, tiled=True)
-    row_count = piece_rows.shape[0]
+    piece_rows = lax.all_gather(heads_out, "row", axis=0, tiled=False)
+    n_row = piece_rows.shape[0]
     product = jnp.dot(
-        piece_rows.reshape(row_count * step_count, -1), wo, preferred_element_type=jnp.float32
-    )
-    partials = product.reshape(row_count, step_count, -1)
-    attended = lax.psum_scatter(
+        piece_rows.reshape(n_row * per * step_count, -1), wo, preferred_element_type=jnp.float32
+    )
+    partials = product.reshape(n_row, per, step_count, -1)
+    own_out = lax.psum_scatter(
         partials.astype(jnp.bfloat16), "col", scatter_dimension=0, tiled=True
-    )
+    ).reshape(per, step_count, -1)
+    attended = lax.all_gather(own_out, "seq", axis=0, tiled=True)
     return (
         attended,
         current_key.reshape(req_count, step_count, k_width),

time: 348 us -> 267 us (0.77); the launches traced: 342 us -> 266 us
  blocking collectives: 73.2 us -> 4.57 us
  waiting for transfers between devices: 125 us -> 108 us
  matrix products: 49.1 us -> 37.9 us
  starting transfers between devices: 0.21 us -> 10.7 us
  local copies, waits for them, and re-layouts: 56.7 us -> 62.8 us
  other arithmetic: 22.7 us -> 26.2 us
    pmax x1 -> x0, blocking collectives: 37 us -> none  [on_device(): running_peak = lax.pmax(local_peak, 'seq')]
    psum x1 -> x0, waiting for transfers between devices: 35.7 us -> none  [on_device(): lax.psum(weighted_values.astype(jnp.bfloat16), 'seq').astype(jnp.float32)]
    psum x1 -> x0, blocking collectives: 33.6 us -> none  [on_device(): lax.psum(running_totals.astype(jnp.bfloat16), 'seq').astype(jnp.float32)]
    all_gather x1, waiting for transfers between devices: 10.3 us -> 41 us  [on_device(): attended = lax.all_gather(own_out, 'seq', axis=0, tiled=True)]
    reduce_scatter x1, waiting for transfers between devices: 36.9 us -> 11.6 us  [on_device(): lax.psum_scatter(partials.astype(jnp.bfloat16), 'col', scatter_dimension=...]
    ppermute x0 -> x6, waiting for transfers between devices: none -> 14.1 us  [the longest x3 12.6 us: seq_merge(): lax.ppermute(send_values.astype(jnp.bfloat16), 'seq', pairs)]
    ppermute x0 -> x6, starting transfers between devices: none -> 10.4 us  [the longest x3 5.79 us: seq_merge(): got_stats = lax.ppermute(send_stats, 'seq', pairs)]
    dot_general x1, matrix products: 10.3 us -> 1.25 us  [fresh_part(): jnp.einsum('rsagh,ruah->rasgu', query_rows, key_all, preferred_element_ty...]
  transfers between devices with their start and end apart: 5 -> 10, of which waited for: 4 -> 7; matrix products, arithmetic and copies ran while one was open for 10% -> 18% of each run, Pallas kernels for 0% -> 0%
where the time goes in v1:
time: 267 us; the launch traced here: 266 us
  waiting for transfers between devices  108 us (40%)
  local copies, waits for them, and re-layouts  62.8 us (24%)
  matrix products  37.9 us (14%)
  other arithmetic  26.2 us (10%)
  between operations  14.9 us (6%)
  starting transfers between devices  10.7 us (4%)
  blocking collectives  4.57 us (2%)
    all_gather x1, waiting for transfers between devices, on_device(): gathered = lax.all_gather(normed, 'col', axis=0, tiled=True)  41.7 us
    all_gather x1, waiting for transfers between devices, on_device(): attended = lax.all_gather(own_out, 'seq', axis=0, tiled=True)  41 us
    dot_general x3, matrix products, on_device(): jnp.dot(piece_rows, matrix, preferred_element_type=jnp.float32)  13.4 us
    ppermute x3, waiting for transfers between devices, seq_merge(): lax.ppermute(send_values.astype(jnp.bfloat16), 'seq', pairs)  12.6 us
    reshape x1, local copies, waits for them, and re-layouts, on_device(): paged_value_cache.reshape(paged_value_cache.shape[0], block_len, heads_kv...  12.4 us
    reshape x1, local copies, waits for them, and re-layouts, on_device(): paged_key_cache.reshape(paged_key_cache.shape[0], block_len, heads_kv, HE...  12.4 us
    reduce_scatter x1, waiting for transfers between devices, on_device(): lax.psum_scatter(partials.astype(jnp.bfloat16), 'col', scatter_dimension=...  11.6 us
    dot_general x1, matrix products, slot_parts(): jnp.einsum('nsagh,nbah->nasgb', slot_queries, key_rows, preferred_element...  7.94 us
  transfers between devices with their start and end apart: 10, of which 7 were waited for; matrix products, arithmetic and copies ran while one was open for 18% of the time, Pallas kernels for 0%

profile of v1, /device:TPU:0, one launch (start us, length us, event | category | flops | bytes accessed | tf_op | source)
XLA Modules:
  0.0 265.6 jit_solution(17505629479722814669)
XLA Ops:
  7.2 2.2 fusion.9
  9.5 2.6 psum.7
  12.2 3.1 %fusion.11 = bf16[64,4,2560]{2,1,0:T(4,128)(2,1)} fusion(bf16[64,4,2560]{2,1,0:T(4,128)(2,1)} %param.11, f32[2560]{0:T(1024)} %param.12, f32[64,4]{1,0:T(8,128)S(1)} %copy.273), kind=kLoop, calls=%fused_computation.16 | loop fusion | flops 2621440 | bytes 2632704 | tf_op jit(solution)/shard_map/convert_element_type | solution.py:173
  15.4 41.7 %all-gather.4.cloned.1.call-done = bf16[128,4,2560]{2,1,0:T(4,128)(2,1)} async-done(((bf16[64,4,2560]{2,1,0:T(4,128)(2,1)}), bf16[128,4,2560]{2,1,0:T(4,128)(2,1)}) %all-gather.4.cloned.1.call-update) | async-done | bytes 2621456 | tf_op jit(solution)/shard_map/all_gather | solution.py:176
  57.1 5.3 %reshape.465 = bf16[512,2560]{1,0:T(8,128)(2,1)} reshape(bf16[128,4,2560]{2,1,0:T(4,128)(2,1)} %all-gather.4.cloned.1.call-done) | data formatting | bytes 5242880 | tf_op jit(solution)/shard_map/reshape | solution.py:177
  62.5 3.4 %convolution_convert_fusion.1 = bf16[512,512]{1,0:T(8,128)(2,1)S(1)} fusion(bf16[512,2560]{1,0:T(8,128)(2,1)} %reshape.465, bf16[2560,512]{1,0:T(8,128)(2,1)S(1)} %copy-done), kind=kOutput, calls=%fused_computation.26 | convolution fusion | flops 1342439424 | bytes 5767168 | tf_op jit(solution)/shard_map/dot_general | solution.py:179
  65.9 1.5 convolution_convert_fusion.2
  67.4 8.5 %convolution_convert_fusion = bf16[512,2048]{1,0:T(8,128)(2,1)S(1)} fusion(bf16[512,2560]{1,0:T(8,128)(2,1)S(1)} %copy-done.5, bf16[2560,2048]{1,0:T(8,128)(2,1)} %param.13), kind=kOutput, calls=%fused_computation.13 | convolution fusion | flops 5369757696 | bytes 15204352 | tf_op jit(solution)/shard_map/dot_general | solution.py:179
  75.9 1.8 pad_maximum_fusion
  77.7 6.1 %convert_element_type.83 = bf16[128,4,3072]{2,1,0:T(4,128)(2,1)} reshape(bf16[512,3072]{1,0:T(8,128)(2,1)} %pad_maximum_fusion) | data formatting | bytes 6291456 | tf_op jit(solution)/shard_map/convert_element_type | solution.py:184
  84.5 0.8 gather_fusion
  85.4 1.1 multiply_cosine_fusion
  86.5 12.4 %reshape.467 = bf16[50,128,4,128]{3,2,1,0:T(4,128)(2,1)} reshape(bf16[50,128,512]{2,1,0:T(8,128)(2,1)} %param.20) | data formatting | bytes 13107200 | tf_op jit(solution)/shard_map/reshape | solution.py:166
  98.9 12.4 %reshape.468 = bf16[50,128,4,128]{3,2,1,0:T(4,128)(2,1)} reshape(bf16[50,128,512]{2,1,0:T(8,128)(2,1)} %param.21) | data formatting | bytes 13107200 | tf_op jit(solution)/shard_map/reshape | solution.py:167
  111.2 0.6 dynamic-slice
  113.0 1.8 dynamic-slice_convert_fusion
  114.8 0.9 slice_bitcast_fusion.2
  115.8 0.8 copy-done.3
  116.6 1.5 slice.92
  118.1 2.3 reshape.509
  120.4 0.7 fusion.76
  121.2 0.6 subtract_convert_fusion
  121.7 1.4 pad_maximum_fusion.1
  123.2 0.6 copy.329
  123.7 2.2 gather_fusion.1
  125.9 7.9 %select_reduce_fusion.1 = (f32[50,4,4,4]{3,2,1,0:T(4,128)S(1)}, f32[50,4,4,4,128]{4,3,2,1,0:T(4,128)}) fusion(pred[50,4,128]{2,1,0:T(4,128)(4,1)S(1)} %or_and_fusion, bf16[50,4,4,4,128]{4,3,1,2,0:T(4,128)(2,1)} %gather_fusion.1, bf16[50,128,4,128,1]{3,2,1,0,4:T(4,128)(2,1)} %bitcast.123), kind=kOutput, calls=%fused_computation.23 | convolution fusion | flops 106083200 | bytes 9049600 | tf_op jit(solution)/shard_map/nsagh,nbah->nasgb/dot_general | solution.py:40
  133.9 1.3 select_reduce_fusion
  135.1 1.1 stack.10
  136.6 0.5 multiply_subtract_fusion
  137.4 1.2 fusion.36
  138.7 0.5 copy.303
  139.4 0.8 fusion.40
  140.2 0.8 copy_dynamic-update-slice_fusion.1
  141.0 3.2 %fusion.18 = f32[50,4,4,4]{3,2,1,0:T(4,128)S(1)} fusion(f32[50,4,4,4,128]{4,3,2,1,0:T(4,128)} %get-tuple-element.60, f32[50,4,4,4]{3,2,1,0:T(4,128)S(1)} %get-tuple-element.59, pred[50,4,128]{2,1,0:T(4,128)(4,1)S(1)} %or_and_fusion), kind=kLoop, calls=%fused_computation.33 | loop fusion | flops 1635200 | bytes 1689600 | tf_op jit(solution)/shard_map/reduce_sum | solution.py:56
  144.1 0.8 gather_fusion.2
  145.0 0.8 fusion.75
  146.8 0.8 constant_dynamic-slice_fusion.1
  147.6 1.6 collective-permute-start
  149.2 4.7 %fusion.14 = f32[50,4,4,4,128]{4,3,2,1,0:T(4,128)S(1)} fusion(bf16[50,128,4,128,1]{3,2,1,0,4:T(4,128)(2,1)} %bitcast.122, f32[50,4,4,4,128]{4,3,2,1,0:T(4,128)} %get-tuple-element.60, f32[50,4,4,4]{3,2,1,0:T(4,128)} %bitcast.135, f32[50,4,4,4]{3,2,1,0:T(4,128)S(1)} %get-tuple-element.59, pred[50,4,128]{2,1,0:T(4,128)(4,1)S(1)} %copy-done.16), kind=kOutput, calls=%fused_computation.25 | convolution fusion | flops 106905600 | bytes 9881600 | tf_op jit(solution)/shard_map/nasgb,nbah->nasgh/dot_general | solution.py:57
  153.9 2.2 fusion.12
  156.1 1.1 constant_dynamic-slice_fusion.2
  157.4 1.1 copy.308
  158.8 0.5 collective-permute-start.1
  159.3 1.1 fusion.33
  160.5 1.6 collective-permute-start.2
  162.1 1.0 fusion.28
  163.1 0.5 copy.292
  164.0 1.5 collective-permute-done.2
  165.6 2.6 collective-permute-start.4
  168.2 4.1 %collective-permute-done.1 = bf16[2,2,1,8,4,4,4,128]{7,6,5,4,3,2,1,0:T(4,128)(2,1)} collective-permute-done((bf16[2,2,1,8,4,4,4,128]{7,6,5,4,3,2,1,0:T(4,128)(2,1)S(1)}, bf16[2,2,1,8,4,4,4,128]{7,6,5,4,3,2,1,0:T(4,128)(2,1)}, u32[]{:S(2)}, u32[]{:S(2)}) %collective-permute-start.1) | collective-permute-done | bytes 524320 | tf_op jit(solution)/shard_map/ppermute | solution.py:133
  172.3 2.5 fusion.17
  174.9 1.6 collective-permute-start.3
  177.1 4.6 %collective-permute-done.3 = bf16[2,1,1,8,4,4,4,128]{7,6,5,4,3,2,1,0:T(4,128)(2,1)S(1)} collective-permute-done((bf16[2,1,1,8,4,4,4,128]{7,6,5,4,3,2,1,0:T(4,128)(2,1)S(1)}, bf16[2,1,1,8,4,4,4,128]{7,6,5,4,3,2,1,0:T(4,128)(2,1)S(1)}, u32[]{:S(2)}, u32[]{:S(2)}) %collective-permute-start.3) | collective-permute-done | bytes 262176 | tf_op jit(solution)/shard_map/ppermute | solution.py:133
  181.7 0.6 multiply_add_fusion.1
  182.4 2.5 collective-permute-start.5
  185.8 3.9 %collective-permute-done.5 = bf16[1,1,1,8,4,4,4,128]{7,6,5,4,3,2,1,0:T(4,128)(2,1)S(1)} collective-permute-done((bf16[1,1,1,8,4,4,4,128]{7,6,5,4,3,2,1,0:T(4,128)(2,1)S(1)}, bf16[1,1,1,8,4,4,4,128]{7,6,5,4,3,2,1,0:T(4,128)(2,1)S(1)}, u32[]{:S(2)}, u32[]{:S(2)}) %collective-permute-start.5) | collective-permute-done | bytes 131104 | tf_op jit(solution)/shard_map/ppermute | solution.py:133
  189.7 1.6 fusion.38
  191.5 2.0 all_gather.11
  193.5 6.6 %fusion.6 = bf16[2,8,4,2560]{3,1,2,0:T(8,128)(2,1)} fusion(bf16[2,8,4,2048]{3,1,2,0:T(8,128)(2,1)S(1)} %all_gather.11, bf16[2048,2560]{1,0:T(8,128)(2,1)} %param.16), kind=kOutput, calls=%fused_computation.9 | convolution fusion | flops 671252480 | bytes 11075584 | tf_op jit(solution)/shard_map/dot_general | solution.py:234
  200.2 11.6 %reduce-scatter.2.cloned.1.call-done = bf16[1,8,4,2560]{3,1,2,0:T(8,128)(2,1)} async-done(((bf16[2,8,4,2560]{3,1,2,0:T(8,128)(2,1)}), bf16[1,8,4,2560]{3,1,2,0:T(8,128)(2,1)}) %reduce-scatter.2.cloned.1.call-update) | async-done | bytes 163856 | tf_op jit(solution)/shard_map/reduce_scatter | solution.py:238
  211.8 1.8 slice.146
  213.6 1.1 fusion.87
  214.7 41.0 %all-gather.6.cloned.1.call-done = bf16[1,64,4,2560]{3,1,2,0:T(8,128)(2,1)} async-done(((bf16[1,8,4,2560]{3,1,2,0:T(8,128)(2,1)}), bf16[1,64,4,2560]{3,1,2,0:T(8,128)(2,1)}) %all-gather.6.cloned.1.call-update) | async-done | bytes 1310736 | tf_op jit(solution)/shard_map/all_gather | solution.py:241
  255.7 3.4 %copy.315 = bf16[64,4,2560]{2,1,0:T(4,128)(2,1)} copy(bf16[64,4,2560]{2,0,1:T(8,128)(2,1)} %bitcast.132) | data formatting | bytes 2621440
  (97 shorter events, 6.5 us)
Async XLA Ops:
  7.2 55.3 %copy-start = (bf16[2560,512]{1,0:T(8,128)(2,1)S(1)}, bf16[2560,512]{1,0:T(8,128)(2,1)}, u32[]{:S(2)}) copy-start(bf16[2560,512]{1,0:T(8,128)(2,1)} %param.15) | copy-start | bytes 7864324
  7.2 50.0 %all-gather.4.cloned.1.call-start = ((), (), s32[]{:S(2)}) async-start(), calls=%async_computation.1 | async-start | bytes 3932160 | tf_op jit(solution)/shard_map/all_gather | solution.py:176
  15.4 97.6 %all-reduce.3.cloned.1.call-start = ((), (), s32[]{:S(2)}) async-start(), calls=%async_computation.4 | async-start | bytes 6291456
  62.5 3.4 %copy-start.5 = (bf16[512,2560]{1,0:T(8,128)(2,1)S(1)}, bf16[512,2560]{1,0:T(8,128)(2,1)}, u32[]{:S(2)}) copy-start(bf16[512,2560]{1,0:T(8,128)(2,1)} %reshape.465) | copy-start | bytes 7864324
  62.5 3.4 %copy-start.18 = (bf16[2560,512]{1,0:T(8,128)(2,1)S(1)}, bf16[2560,512]{1,0:T(8,128)(2,1)}, u32[]{:S(2)}) copy-start(bf16[2560,512]{1,0:T(8,128)(2,1)} %param.14) | copy-start | bytes 7864324
  83.8 0.7 copy-start.17
  83.8 0.7 copy-start.2
  83.8 127.9 %reduce-scatter.2.cloned.1.call-start = ((), (), s32[]{:S(2)}) async-start(), calls=%async_computation.2 | async-start | bytes 491520 | tf_op jit(solution)/shard_map/reduce_scatter | solution.py:238
  98.8 12.4 %copy-start.20 = (u32[32]{0:T(128)S(1)}, u32[32]{0:T(128)}, u32[]{:S(2)}) copy-start(u32[32]{0:T(128)} %constant.92) | copy-start | bytes 388
  98.8 13.6 %copy-start.19 = (s32[50]{0:T(128)S(1)}, s32[50]{0:T(128)}, u32[]{:S(2)}) copy-start(s32[50]{0:T(128)} %param.19) | copy-start | bytes 604
  113.0 28.0 %copy-start.15 = (pred[50,4,128]{2,1,0:T(4,128)(4,1)}, pred[50,4,128]{2,1,0:T(4,128)(4,1)S(1)}, u32[]{:S(2)}) copy-start(pred[50,4,128]{2,1,0:T(4,128)(4,1)S(1)} %or_and_fusion) | copy-start | bytes 76804
  114.8 1.7 copy-start.3
  137.1 3.1 %copy-start.8 = (f32[1,2,2,2,8,4,4,4]{4,3,2,1,7,6,5,0:T(2,128)S(1)}, f32[1,2,2,2,8,4,4,4]{4,3,2,1,7,6,5,0:T(2,128)}, u32[]{:S(2)}) copy-start(f32[1,2,2,2,8,4,4,4]{4,3,2,1,7,6,5,0:T(2,128)} %stack.10) | copy-start | bytes 49156
  139.4 1.6 copy-start.11
  144.9 1.8 copy-start.6
  145.0 4.2 %copy-start.16 = (pred[50,4,128]{2,1,0:T(4,128)(4,1)S(1)}, pred[50,4,128]{2,1,0:T(4,128)(4,1)}, u32[]{:S(2)}) copy-start(pred[50,4,128]{2,1,0:T(4,128)(4,1)} %copy-done.15) | copy-start | bytes 76804
  146.8 2.4 copy-start.7
  147.6 11.7 %collective-permute-start = (f32[2,2,2,1,8,4,4,4]{4,7,6,5,2,1,3,0:T(4,128)}, f32[2,2,2,1,8,4,4,4]{4,7,6,5,2,1,3,0:T(4,128)S(1)}, u32[]{:S(2)}, u32[]{:S(2)}) collective-permute-start(f32[2,2,2,1,8,4,4,4]{4,7,6,5,2,1,3,0:T(4,128)} %constant_dynamic-slice_fusion.1), channel_id=1, source_target_pairs={{0,1},{1,0},{2,3},{3,2},{4,5},{5,4},{6,7},{7,6},{8,9},{9,8},{10,11... | collective-permute-start | bytes 49160 | tf_op jit(solution)/shard_map/ppermute | solution.py:132
  158.5 13.8 %copy-start.4 = (f32[2,2,1,8,4,4,4,128]{7,3,2,1,0,6,5,4:T(8,128)S(1)}, f32[2,2,1,8,4,4,4,128]{7,3,2,1,0,6,5,4:T(8,128)}, u32[]{:S(2)}) copy-start(f32[2,2,1,8,4,4,4,128]{7,3,2,1,0,6,5,4:T(8,128)} %constant_dynamic-slice_fusion.2) | copy-start | bytes 3145732
  158.8 13.5 %collective-permute-start.1 = (bf16[2,2,1,8,4,4,4,128]{7,6,5,4,3,2,1,0:T(4,128)(2,1)S(1)}, bf16[2,2,1,8,4,4,4,128]{7,6,5,4,3,2,1,0:T(4,128)(2,1)}, u32[]{:S(2)}, u32[]{:S(2)}) collective-permute-start(bf16[2,2,1,8,4,4,4,128]{7,6,5,4,3,2,1,0:T(4,128)(2,1)S(1)} %copy.358), channel_id=1, source_target_pairs={{0,1},{1,0},{2,3},{3,2},{4,5},{5,4},{6,7},{7,6},{8,9},{9,8},{10,11... | collective-permute-start | bytes 1572872 | tf_op jit(solution)/shard_map/ppermute | solution.py:133
  160.5 5.0 %collective-permute-start.2 = (f32[2,2,1,1,8,4,4,4]{4,7,6,5,3,2,1,0:T(4,128)S(1)}, f32[2,2,1,1,8,4,4,4]{4,7,6,5,3,2,1,0:T(4,128)S(1)}, u32[]{:S(2)}, u32[]{:S(2)}) collective-permute-start(f32[2,2,1,1,8,4,4,4]{4,7,6,5,3,2,1,0:T(4,128)S(1)} %get-tuple-element.49), channel_id=1, source_target_pairs={{0,2},{1,3},{2,0},{3,1},{4,6},{5,7},{6,4},{7,5},{8,10},{9,11},{10,... | collective-permute-start | bytes 24584 | tf_op jit(solution)/shard_map/ppermute | solution.py:132
  165.5 2.7 %copy-start.9 = (f32[2,2,1,1,8,4,4,4]{4,7,6,5,3,2,1,0:T(4,128)}, f32[2,2,1,1,8,4,4,4]{4,7,6,5,3,2,1,0:T(4,128)S(1)}, u32[]{:S(2)}) copy-start(f32[2,2,1,1,8,4,4,4]{4,7,6,5,3,2,1,0:T(4,128)S(1)} %collective-permute-done.2) | copy-start | bytes 24580
  165.6 11.4 %collective-permute-start.4 = (f32[2,1,1,1,8,4,4,4]{4,7,6,5,3,2,1,0:T(4,128)S(1)}, f32[2,1,1,1,8,4,4,4]{4,7,6,5,3,2,1,0:T(4,128)S(1)}, u32[]{:S(2)}, u32[]{:S(2)}) collective-permute-start(f32[2,1,1,1,8,4,4,4]{4,7,6,5,3,2,1,0:T(4,128)S(1)} %get-tuple-element.53), channel_id=1, source_target_pairs={{0,4},{1,5},{2,6},{3,7},{4,0},{5,1},{6,2},{7,3},{8,12},{9,13},{10,... | collective-permute-start | bytes 12296 | tf_op jit(solution)/shard_map/ppermute | solution.py:132
  172.3 4.2 %copy-start.10 = (f32[2,2,1,1,8,4,4,4]{4,7,6,5,3,2,1,0:T(4,128)S(1)}, f32[2,2,1,1,8,4,4,4]{4,7,6,5,3,2,1,0:T(4,128)}, u32[]{:S(2)}) copy-start(f32[2,2,1,1,8,4,4,4]{4,7,6,5,3,2,1,0:T(4,128)} %copy-done.9) | copy-start | bytes 24580
  174.8 10.1 %copy-start.12 = (f32[8,4,4,4]{0,3,2,1:T(4,128)S(1)}, f32[8,4,4,4]{0,3,2,1:T(4,128)}, u32[]{:S(2)}) copy-start(f32[8,4,4,4]{0,3,2,1:T(4,128)} %copy-done.11) | copy-start | bytes 6148
  174.8 10.1 %copy-start.14 = (f32[8,4,4,4]{0,3,2,1:T(4,128)S(1)}, f32[8,4,4,4]{0,3,2,1:T(4,128)}, u32[]{:S(2)}) copy-start(f32[8,4,4,4]{0,3,2,1:T(4,128)} %get-tuple-element.51) | copy-start | bytes 6148
  174.8 15.0 %copy-start.13 = (bf16[8,4,4,4,4]{4,3,2,1,0:T(4,128)(2,1)S(1)}, bf16[8,4,4,4,4]{4,3,2,1,0:T(4,128)(2,1)}, u32[]{:S(2)}) copy-start(bf16[8,4,4,4,4]{4,3,2,1,0:T(4,128)(2,1)} %copy.308) | copy-start | bytes 12292
  174.9 6.8 %collective-permute-start.3 = (bf16[2,1,1,8,4,4,4,128]{7,6,5,4,3,2,1,0:T(4,128)(2,1)S(1)}, bf16[2,1,1,8,4,4,4,128]{7,6,5,4,3,2,1,0:T(4,128)(2,1)S(1)}, u32[]{:S(2)}, u32[]{:S(2)}) collective-permute-start(bf16[2,1,1,8,4,4,4,128]{7,6,5,4,3,2,1,0:T(4,128)(2,1)S(1)} %dynamic-slice_convert_fusion.1), channel_id=1, source_target_pairs={{0,2},{1,3},{2,0},{3,1},{4,6},{5,7},{6,4},{7,5},{8,10},{9,11},{10,... | collective-permute-start | bytes 786440 | tf_op jit(solution)/shard_map/ppermute | solution.py:133
  182.4 7.3 %collective-permute-start.5 = (bf16[1,1,1,8,4,4,4,128]{7,6,5,4,3,2,1,0:T(4,128)(2,1)S(1)}, bf16[1,1,1,8,4,4,4,128]{7,6,5,4,3,2,1,0:T(4,128)(2,1)S(1)}, u32[]{:S(2)}, u32[]{:S(2)}) collective-permute-start(bf16[1,1,1,8,4,4,4,128]{7,6,5,4,3,2,1,0:T(4,128)(2,1)S(1)} %dynamic-slice_convert_fusion.2), channel_id=1, source_target_pairs={{0,4},{1,5},{2,6},{3,7},{4,0},{5,1},{6,2},{7,3},{8,12},{9,13},{10,... | collective-permute-start | bytes 393224 | tf_op jit(solution)/shard_map/ppermute | solution.py:133
  200.1 58.9 %copy-start.1 = (bf16[2560,512]{1,0:T(8,128)(2,1)S(1)}, bf16[2560,512]{1,0:T(8,128)(2,1)}, u32[]{:S(2)}) copy-start(bf16[2560,512]{1,0:T(8,128)(2,1)} %param.15) | copy-start | bytes 7864324
  200.1 55.5 %all-gather.6.cloned.1.call-start = ((), (), s32[]{:S(2)}) async-start(), calls=%async_computation.3 | async-start | bytes 1474560 | tf_op jit(solution)/shard_map/all_gather | solution.py:241
Sparse Core Ops, SparseCore 0:
  15.5 41.5 all-gather.3
  84.0 23.1 all-reduce.2
  200.3 11.4 reduce-scatter.1
  213.8 41.7 all-gather.5

commit v2 on v1

--- a/solution.py
+++ b/solution.py
@@ -110,6 +110,46 @@
     running_totals = earlier[1] * first_factor + later[1] * second_factor
     weighted_values = earlier[2] * first_factor[..., None] + later[2] * second_factor[..., None]
     return (running_peak, running_totals, weighted_values)
+
+
+def pair_gather(part, axis_name):
+    n = lax.axis_size(axis_name)
+    assert n == 2
+    side = lax.axis_index(axis_name)
+    other = lax.ppermute(part, axis_name, [(0, 1), (1, 0)])
+    return jnp.where(
+        side == 0,
+        jnp.concatenate([part, other], 0),
+        jnp.concatenate([other, part], 0),
+    )
+
+
+def pair_scatter(parts, axis_name):
+    n = lax.axis_size(axis_name)
+    assert n == 2 and parts.shape[0] == 2
+    side = lax.axis_index(axis_name)
+    keep = lax.dynamic_index_in_dim(parts, side, 0, keepdims=True)
+    send = lax.dynamic_index_in_dim(parts, 1 - side, 0, keepdims=True)
+    got = lax.ppermute(send, axis_name, [(0, 1), (1, 0)])
+    return (keep.astype(jnp.float32) + got.astype(jnp.float32)).astype(parts.dtype)
+
+
+def doubling_gather(part, axis_name):
+    n = lax.axis_size(axis_name)
+    stages = n.bit_length() - 1
+    assert 1 << stages == n
+    index = lax.axis_index(axis_name)
+    block = part[None]
+    for bit in reversed(range(stages)):
+        pairs = [(s, s ^ (1 << bit)) for s in range(n)]
+        got = lax.ppermute(block, axis_name, pairs)
+        low = ((index >> bit) & 1) == 0
+        block = jnp.where(
+            low, jnp.stack([block, got], 0), jnp.stack([got, block], 0)
+        )
+    block = block.reshape((2,) * stages + part.shape)
+    block = block.transpose(tuple(reversed(range(stages))) + tuple(range(stages, stages + part.ndim)))
+    return block.reshape((n * part.shape[0],) + part.shape[1:])
 
 
 def seq_merge(peak, total, acc, n_seq, seq_index):
@@ -173,7 +213,7 @@
     normed = (as_float * lax.rsqrt(squares / D + EPSILON)[..., None] * norm_gain).astype(
         jnp.bfloat16
     )
-    gathered = lax.all_gather(normed, "col", axis=0, tiled=True)
+    gathered = pair_gather(normed, "col")
     piece_rows = gathered.reshape(req_count * lax.axis_size("row") * step_count, -1)
     parts_out = [
         jnp.dot(piece_rows, matrix, preferred_element_type=jnp.float32) for matrix in (wq, wk, wv)
@@ -235,10 +275,8 @@
         piece_rows.reshape(n_row * per * step_count, -1), wo, preferred_element_type=jnp.float32
     )
     partials = product.reshape(n_row, per, step_count, -1)
-    own_out = lax.psum_scatter(
-        partials.astype(jnp.bfloat16), "col", scatter_dimension=0, tiled=True
-    ).reshape(per, step_count, -1)
-    attended = lax.all_gather(own_out, "seq", axis=0, tiled=True)
+    own_out = pair_scatter(partials.astype(jnp.bfloat16), "col").reshape(per, step_count, -1)
+    attended = doubling_gather(own_out, "seq")
     return (
         attended,
         current_key.reshape(req_count, step_count, k_width),

time: 267 us -> 249 us (0.933)
  waiting for transfers between devices: 108 us -> 74.6 us
  starting transfers between devices: 10.7 us -> 19 us
  other arithmetic: 26.2 us -> 34.4 us
    all_gather x2 -> x0, waiting for transfers between devices: 82.7 us -> none  [the longest x1 41.7 us: on_device(): gathered = lax.all_gather(normed, 'col', axis=0, tiled=True)]
    ppermute x0 -> x5, waiting for transfers between devices: none -> 62 us  [the longest x1 29.4 us: pair_gather(): other = lax.ppermute(part, axis_name, [(0, 1), (1, 0)])]
    reduce_scatter x1 -> x0, waiting for transfers between devices: 11.6 us -> none  [on_device(): lax.psum_scatter(partials.astype(jnp.bfloat16), 'col', scatter_dimension=...]
    ppermute x0 -> x5, starting transfers between devices: none -> 7.62 us  [the longest x3 3.25 us: doubling_gather(): got = lax.ppermute(block, axis_name, pairs)]
    select_n x0 -> x4, other arithmetic: none -> 6.7 us  [the longest x1 6.46 us: pair_gather(): jnp.where(side == 0, jnp.concatenate([part, other], 0), jnp.concatenate([...]
    reshape x1 -> x0, local copies, waits for them, and re-layouts: 5.31 us -> none  [on_device(): gathered.reshape(req_count * lax.axis_size('row') * step_count, -1)]
    select_n x0 -> x1, local copies, waits for them, and re-layouts: none -> 5.31 us  [pair_gather(): jnp.where(side == 0, jnp.concatenate([part, other], 0), jnp.concatenate([...]
    unnamed x46 -> x48, local copies, waits for them, and re-layouts: 6.27 us -> 6.02 us
  transfers between devices with their start and end apart: 10 -> 12, of which waited for: 7 -> 9; matrix products, arithmetic and copies ran while one was open for 18% -> 19% of each run, Pallas kernels for 0% -> 0%
where the time goes in v2:
time: 249 us; the launch traced here: 248 us
  waiting for transfers between devices  74.6 us (30%)
  local copies, waits for them, and re-layouts  62.8 us (25%)
  matrix products  37.2 us (15%)
  other arithmetic  34.4 us (14%)
  starting transfers between devices  19 us (8%)
  between operations  15.2 us (6%)
  blocking collectives  4.83 us (2%)
    ppermute x1, waiting for transfers between devices, pair_gather(): other = lax.ppermute(part, axis_name, [(0, 1), (1, 0)])  29.4 us
    ppermute x3, waiting for transfers between devices, doubling_gather(): got = lax.ppermute(block, axis_name, pairs)  27.8 us
    dot_general x3, matrix products, on_device(): jnp.dot(piece_rows, matrix, preferred_element_type=jnp.float32)  13.4 us
    reshape x1, local copies, waits for them, and re-layouts, on_device(): paged_value_cache.reshape(paged_value_cache.shape[0], block_len, heads_kv...  12.4 us
    reshape x1, local copies, waits for them, and re-layouts, on_device(): paged_key_cache.reshape(paged_key_cache.shape[0], block_len, heads_kv, HE...  12.3 us
    ppermute x3, waiting for transfers between devices, seq_merge(): lax.ppermute(send_values.astype(jnp.bfloat16), 'seq', pairs)  11.4 us
    dot_general x1, matrix products, slot_parts(): jnp.einsum('nsagh,nbah->nasgb', slot_queries, key_rows, preferred_element...  7.95 us
    ppermute x3, starting transfers between devices, seq_merge(): got_stats = lax.ppermute(send_stats, 'seq', pairs)  6.61 us
  transfers between devices with their start and end apart: 12, of which 9 were waited for; matrix products, arithmetic and copies ran while one was open for 19% of the time, Pallas kernels for 0%

profile of v2, /device:TPU:0, one launch (start us, length us, event | category | flops | bytes accessed | tf_op | source)
XLA Modules:
  0.0 248.1 jit_solution(11768956404636167960)
XLA Ops:
  7.2 2.2 fusion.9
  9.5 2.6 %psum.7 = f32[64,4]{0,1:T(4,128)S(1)} all-reduce(f32[64,4]{0,1:T(4,128)S(1)} %copy.277), channel_id=1, replica_groups=mesh['row'=2,'col'=2,'seq'=8] {'row'}, use_global_device_ids=true, to_apply=%region_1.0 | all-reduce | flops 256 | bytes 2048 | tf_op jit(solution)/shard_map/psum | solution.py:212
  12.2 3.1 %fusion.11 = bf16[64,4,2560]{2,1,0:T(4,128)(2,1)} fusion(bf16[64,4,2560]{2,1,0:T(4,128)(2,1)} %param.11, f32[2560]{0:T(1024)} %param.12, f32[64,4]{1,0:T(8,128)S(1)} %copy.278), kind=kLoop, calls=%fused_computation.16 | loop fusion | flops 2621440 | bytes 2632704 | tf_op jit(solution)/shard_map/convert_element_type | solution.py:213
  15.3 2.8 %collective-permute-start = (bf16[64,4,2560]{2,1,0:T(4,128)(2,1)}, bf16[64,4,2560]{2,1,0:T(4,128)(2,1)}, u32[]{:S(2)}, u32[]{:S(2)}) collective-permute-start(bf16[64,4,2560]{2,1,0:T(4,128)(2,1)} %fusion.11), channel_id=1, source_target_pairs={{0,8},{8,0},{1,9},{9,1},{2,10},{10,2},{3,11},{11,3},{4,12},{12,4},... | collective-permute-start | bytes 3932168 | tf_op jit(solution)/shard_map/ppermute | solution.py:119
  18.2 29.4 %collective-permute-done = bf16[64,4,2560]{2,1,0:T(4,128)(2,1)} collective-permute-done((bf16[64,4,2560]{2,1,0:T(4,128)(2,1)}, bf16[64,4,2560]{2,1,0:T(4,128)(2,1)}, u32[]{:S(2)}, u32[]{:S(2)}) %collective-permute-start) | collective-permute-done | bytes 1310752 | tf_op jit(solution)/shard_map/ppermute | solution.py:119
  47.6 6.5 %maximum_select_fusion = bf16[128,4,2560]{2,1,0:T(4,128)(2,1)} fusion(bf16[64,4,2560]{2,1,0:T(4,128)(2,1)} %collective-permute-done, bf16[64,4,2560]{2,1,0:T(4,128)(2,1)} %fusion.11, pred[]{:T(512)S(6)} %eq.35), kind=kLoop, calls=%fused_computation.17 | loop fusion | flops 3932160 | bytes 5242881 | tf_op jit(solution)/shard_map/jit(_where)/select_n | solution.py:120
  54.0 5.3 %select_n.170 = bf16[512,2560]{1,0:T(8,128)(2,1)} reshape(bf16[128,4,2560]{2,1,0:T(4,128)(2,1)} %maximum_select_fusion) | data formatting | bytes 5242880 | tf_op jit(solution)/shard_map/jit(_where)/select_n | solution.py:120
  59.4 3.4 %convolution_convert_fusion.1 = bf16[512,512]{1,0:T(8,128)(2,1)S(1)} fusion(bf16[512,2560]{1,0:T(8,128)(2,1)} %select_n.170, bf16[2560,512]{1,0:T(8,128)(2,1)S(1)} %copy-done), kind=kOutput, calls=%fused_computation.29 | convolution fusion | flops 1342439424 | bytes 5767168 | tf_op jit(solution)/shard_map/dot_general | solution.py:219
  62.8 1.5 convolution_convert_fusion.2
  64.3 8.5 %convolution_convert_fusion = bf16[512,2048]{1,0:T(8,128)(2,1)S(1)} fusion(bf16[512,2560]{1,0:T(8,128)(2,1)S(1)} %copy-done.5, bf16[2560,2048]{1,0:T(8,128)(2,1)} %param.13), kind=kOutput, calls=%fused_computation.13 | convolution fusion | flops 5369757696 | bytes 15204352 | tf_op jit(solution)/shard_map/dot_general | solution.py:219
  72.8 1.8 pad_maximum_fusion
  74.6 6.1 %convert_element_type.92 = bf16[128,4,3072]{2,1,0:T(4,128)(2,1)} reshape(bf16[512,3072]{1,0:T(8,128)(2,1)} %pad_maximum_fusion) | data formatting | bytes 6291456 | tf_op jit(solution)/shard_map/convert_element_type | solution.py:224
  81.4 0.8 gather_fusion
  82.3 1.1 multiply_cosine_fusion
  83.4 12.3 %reshape.892 = bf16[50,128,4,128]{3,2,1,0:T(4,128)(2,1)} reshape(bf16[50,128,512]{2,1,0:T(8,128)(2,1)} %param.20) | data formatting | bytes 13107200 | tf_op jit(solution)/shard_map/reshape | solution.py:206
  95.7 12.4 %reshape.893 = bf16[50,128,4,128]{3,2,1,0:T(4,128)(2,1)} reshape(bf16[50,128,512]{2,1,0:T(8,128)(2,1)} %param.21) | data formatting | bytes 13107200 | tf_op jit(solution)/shard_map/reshape | solution.py:207
  109.9 1.8 dynamic-slice_convert_fusion
  111.7 0.9 slice_bitcast_fusion.2
  112.7 0.8 copy-done.3
  113.4 1.5 slice.92
  115.0 2.5 %reshape.933 = f32[64,4,16,128]{3,2,1,0:T(8,128)S(1)} reshape(f32[64,4,2048]{2,1,0:T(4,128)} %slice.92) | data formatting | bytes 4194304 | tf_op jit(solution)/shard_map/reshape | solution.py:231
  118.8 1.4 pad_maximum_fusion.1
  120.8 2.2 gather_fusion.1
  123.0 7.9 %select_reduce_fusion.1 = (f32[50,4,4,4]{3,2,1,0:T(4,128)S(1)}, f32[50,4,4,4,128]{4,3,2,1,0:T(4,128)}) fusion(pred[50,4,128]{2,1,0:T(4,128)(4,1)S(1)} %or_and_fusion, bf16[50,4,4,4,128]{4,3,1,2,0:T(4,128)(2,1)} %gather_fusion.1, bf16[50,128,4,128,1]{3,2,1,0,4:T(4,128)(2,1)} %bitcast.134), kind=kOutput, calls=%fused_computation.24 | convolution fusion | flops 106083200 | bytes 9049600 | tf_op jit(solution)/shard_map/nsagh,nbah->nasgb/dot_general | solution.py:40
  130.9 1.0 select_reduce_fusion
  132.0 1.1 stack.72
  134.3 1.2 fusion.37
  136.2 0.8 fusion.41
  137.0 0.8 copy_dynamic-update-slice_fusion.1
  137.8 3.4 %fusion.19 = f32[50,4,4,4]{3,2,1,0:T(4,128)S(1)} fusion(f32[50,4,4,4,128]{4,3,2,1,0:T(4,128)} %get-tuple-element.59, f32[50,4,4,4]{3,2,1,0:T(4,128)S(1)} %get-tuple-element.58, pred[50,4,128]{2,1,0:T(4,128)(4,1)S(1)} %or_and_fusion), kind=kLoop, calls=%fused_computation.36 | loop fusion | flops 1635200 | bytes 1689600 | tf_op jit(solution)/shard_map/reduce_sum | solution.py:56
  141.2 0.8 gather_fusion.2
  142.0 0.8 fusion.78
  143.9 0.8 constant_dynamic-slice_fusion.2
  144.7 1.8 collective-permute-start.1
  146.5 4.7 %fusion.14 = f32[50,4,4,4,128]{4,3,2,1,0:T(4,128)S(1)} fusion(bf16[50,128,4,128,1]{3,2,1,0,4:T(4,128)(2,1)} %bitcast.133, f32[50,4,4,4,128]{4,3,2,1,0:T(4,128)} %get-tuple-element.59, f32[50,4,4,4]{3,2,1,0:T(4,128)} %bitcast.153, f32[50,4,4,4]{3,2,1,0:T(4,128)S(1)} %get-tuple-element.58, pred[50,4,128]{2,1,0:T(4,128)(4,1)S(1)} %copy-done.17), kind=kOutput, calls=%fused_computation.26 | convolution fusion | flops 106905600 | bytes 9881600 | tf_op jit(solution)/shard_map/nasgb,nbah->nasgh/dot_general | solution.py:57
  151.2 2.2 fusion.12
  153.4 1.1 constant_dynamic-slice_fusion.3
  154.6 1.1 copy.313
  156.4 1.1 fusion.34
  157.5 1.9 collective-permute-start.3
  159.4 1.0 fusion.29
  161.3 1.2 collective-permute-done.3
  162.7 3.0 %collective-permute-start.5 = (f32[2,1,1,1,8,4,4,4]{4,7,6,5,3,2,1,0:T(4,128)S(1)}, f32[2,1,1,1,8,4,4,4]{4,7,6,5,3,2,1,0:T(4,128)S(1)}, u32[]{:S(2)}, u32[]{:S(2)}) collective-permute-start(f32[2,1,1,1,8,4,4,4]{4,7,6,5,3,2,1,0:T(4,128)S(1)} %get-tuple-element.52), channel_id=1, source_target_pairs={{0,4},{1,5},{2,6},{3,7},{4,0},{5,1},{6,2},{7,3},{8,12},{9,13},{10,... | collective-permute-start | bytes 12296 | tf_op jit(solution)/shard_map/ppermute | solution.py:172
  165.6 3.5 %collective-permute-done.2 = bf16[2,2,1,8,4,4,4,128]{7,6,5,4,3,2,1,0:T(4,128)(2,1)} collective-permute-done((bf16[2,2,1,8,4,4,4,128]{7,6,5,4,3,2,1,0:T(4,128)(2,1)S(1)}, bf16[2,2,1,8,4,4,4,128]{7,6,5,4,3,2,1,0:T(4,128)(2,1)}, u32[]{:S(2)}, u32[]{:S(2)}) %collective-permute-start.2) | collective-permute-done | bytes 524320 | tf_op jit(solution)/shard_map/ppermute | solution.py:173
  169.1 2.2 fusion.18
  171.5 1.7 collective-permute-start.4
  173.8 4.1 %collective-permute-done.4 = bf16[2,1,1,8,4,4,4,128]{7,6,5,4,3,2,1,0:T(4,128)(2,1)S(1)} collective-permute-done((bf16[2,1,1,8,4,4,4,128]{7,6,5,4,3,2,1,0:T(4,128)(2,1)S(1)}, bf16[2,1,1,8,4,4,4,128]{7,6,5,4,3,2,1,0:T(4,128)(2,1)S(1)}, u32[]{:S(2)}, u32[]{:S(2)}) %collective-permute-start.4) | collective-permute-done | bytes 262176 | tf_op jit(solution)/shard_map/ppermute | solution.py:173
  178.7 2.7 %collective-permute-start.6 = (bf16[1,1,1,8,4,4,4,128]{7,6,5,4,3,2,1,0:T(4,128)(2,1)S(1)}, bf16[1,1,1,8,4,4,4,128]{7,6,5,4,3,2,1,0:T(4,128)(2,1)S(1)}, u32[]{:S(2)}, u32[]{:S(2)}) collective-permute-start(bf16[1,1,1,8,4,4,4,128]{7,6,5,4,3,2,1,0:T(4,128)(2,1)S(1)} %dynamic-slice_convert_fusion.2), channel_id=1, source_target_pairs={{0,4},{1,5},{2,6},{3,7},{4,0},{5,1},{6,2},{7,3},{8,12},{9,13},{10,... | collective-permute-start | bytes 393224 | tf_op jit(solution)/shard_map/ppermute | solution.py:173
  182.3 3.7 %collective-permute-done.6 = bf16[1,1,1,8,4,4,4,128]{7,6,5,4,3,2,1,0:T(4,128)(2,1)S(1)} collective-permute-done((bf16[1,1,1,8,4,4,4,128]{7,6,5,4,3,2,1,0:T(4,128)(2,1)S(1)}, bf16[1,1,1,8,4,4,4,128]{7,6,5,4,3,2,1,0:T(4,128)(2,1)S(1)}, u32[]{:S(2)}, u32[]{:S(2)}) %collective-permute-start.6) | collective-permute-done | bytes 131104 | tf_op jit(solution)/shard_map/ppermute | solution.py:173
  186.0 1.6 fusion.39
  187.8 2.3 all_gather.4
  190.0 5.9 %fusion.6 = bf16[2,8,4,2560]{3,1,2,0:T(8,128)(2,1)S(1)} fusion(bf16[2,8,4,2048]{3,1,2,0:T(8,128)(2,1)S(1)} %all_gather.4, bf16[2048,2560]{1,0:T(8,128)(2,1)} %param.16), kind=kOutput, calls=%fused_computation.9 | convolution fusion | flops 671252480 | bytes 11075584 | tf_op jit(solution)/shard_map/dot_general | solution.py:274
  195.9 1.6 collective-permute-start.7
  197.5 4.8 %collective-permute-done.7 = bf16[1,8,4,2560]{3,1,2,0:T(8,128)(2,1)S(1)} collective-permute-done((bf16[1,8,4,2560]{3,1,2,0:T(8,128)(2,1)S(1)}, bf16[1,8,4,2560]{3,1,2,0:T(8,128)(2,1)S(1)}, u32[]{:S(2)}, u32[]{:S(2)}) %collective-permute-start.7) | collective-permute-done | bytes 163872 | tf_op jit(solution)/shard_map/ppermute | solution.py:133
  202.3 1.4 collective-permute-start.8
  203.7 8.5 %collective-permute-done.8 = bf16[1,8,4,2560]{3,1,2,0:T(8,128)(2,1)S(1)} collective-permute-done((bf16[1,8,4,2560]{3,1,2,0:T(8,128)(2,1)S(1)}, bf16[1,8,4,2560]{3,1,2,0:T(8,128)(2,1)S(1)}, u32[]{:S(2)}, u32[]{:S(2)}) %collective-permute-start.8) | collective-permute-done | bytes 163872 | tf_op jit(solution)/shard_map/ppermute | solution.py:145
  212.4 8.6 %collective-permute-done.9 = bf16[2,1,8,4,2560]{4,2,3,1,0:T(8,128)(2,1)S(1)} collective-permute-done((bf16[2,1,8,4,2560]{4,2,3,1,0:T(8,128)(2,1)S(1)}, bf16[2,1,8,4,2560]{4,2,3,1,0:T(8,128)(2,1)S(1)}, u32[]{:S(2)}, u32[]{:S(2)}) %collective-permute-start.9) | collective-permute-done | bytes 327712 | tf_op jit(solution)/shard_map/ppermute | solution.py:145
  221.1 1.8 collective-permute-start.10
  222.9 1.8 slice.146
  224.7 1.1 fusion.90
  225.9 10.7 %collective-permute-done.10 = bf16[2,2,1,8,4,2560]{5,3,4,1,2,0:T(8,128)(2,1)S(1)} collective-permute-done((bf16[2,2,1,8,4,2560]{5,3,4,1,2,0:T(8,128)(2,1)S(1)}, bf16[2,2,1,8,4,2560]{5,3,4,1,2,0:T(8,128)(2,1)S(1)}, u32[]{:S(2)}, u32[]{:S(2)}) %collective-permute-start.10) | collective-permute-done | bytes 655392 | tf_op jit(solution)/shard_map/ppermute | solution.py:145
  236.5 0.8 copy-done.9
  237.4 1.7 fusion.17
  239.2 2.1 copy.321
  (109 shorter events, 11.7 us)
Async XLA Ops:
  7.2 52.2 %copy-start = (bf16[2560,512]{1,0:T(8,128)(2,1)S(1)}, bf16[2560,512]{1,0:T(8,128)(2,1)}, u32[]{:S(2)}) copy-start(bf16[2560,512]{1,0:T(8,128)(2,1)} %param.15) | copy-start | bytes 7864324
  7.2 102.7 %all-reduce.3.cloned.1.call-start = ((), (), s32[]{:S(2)}) async-start(), calls=%async_computation | async-start | bytes 6291456
  15.3 32.2 %collective-permute-start = (bf16[64,4,2560]{2,1,0:T(4,128)(2,1)}, bf16[64,4,2560]{2,1,0:T(4,128)(2,1)}, u32[]{:S(2)}, u32[]{:S(2)}) collective-permute-start(bf16[64,4,2560]{2,1,0:T(4,128)(2,1)} %fusion.11), channel_id=1, source_target_pairs={{0,8},{8,0},{1,9},{9,1},{2,10},{10,2},{3,11},{11,3},{4,12},{12,4},... | collective-permute-start | bytes 3932168 | tf_op jit(solution)/shard_map/ppermute | solution.py:119
  59.4 3.4 %copy-start.5 = (bf16[512,2560]{1,0:T(8,128)(2,1)S(1)}, bf16[512,2560]{1,0:T(8,128)(2,1)}, u32[]{:S(2)}) copy-start(bf16[512,2560]{1,0:T(8,128)(2,1)} %select_n.170) | copy-start | bytes 7864324
  59.4 3.4 %copy-start.19 = (bf16[2560,512]{1,0:T(8,128)(2,1)S(1)}, bf16[2560,512]{1,0:T(8,128)(2,1)}, u32[]{:S(2)}) copy-start(bf16[2560,512]{1,0:T(8,128)(2,1)} %param.14) | copy-start | bytes 7864324
  80.7 0.7 copy-start.18
  80.7 0.7 copy-start.2
  95.7 12.4 %copy-start.21 = (u32[32]{0:T(128)S(1)}, u32[32]{0:T(128)}, u32[]{:S(2)}) copy-start(u32[32]{0:T(128)} %constant.104) | copy-start | bytes 388
  95.7 13.7 %copy-start.20 = (s32[50]{0:T(128)S(1)}, s32[50]{0:T(128)}, u32[]{:S(2)}) copy-start(s32[50]{0:T(128)} %param.19) | copy-start | bytes 604
  109.8 28.0 %copy-start.16 = (pred[50,4,128]{2,1,0:T(4,128)(4,1)}, pred[50,4,128]{2,1,0:T(4,128)(4,1)S(1)}, u32[]{:S(2)}) copy-start(pred[50,4,128]{2,1,0:T(4,128)(4,1)S(1)} %or_and_fusion) | copy-start | bytes 76804
  111.7 1.7 copy-start.3
  133.9 3.1 %copy-start.8 = (f32[1,2,2,2,8,4,4,4]{4,3,2,1,7,6,5,0:T(2,128)S(1)}, f32[1,2,2,2,8,4,4,4]{4,3,2,1,7,6,5,0:T(2,128)}, u32[]{:S(2)}) copy-start(f32[1,2,2,2,8,4,4,4]{4,3,2,1,7,6,5,0:T(2,128)} %stack.72) | copy-start | bytes 49156
  136.2 1.6 copy-start.12
  142.0 1.8 copy-start.6
  142.0 4.4 %copy-start.17 = (pred[50,4,128]{2,1,0:T(4,128)(4,1)S(1)}, pred[50,4,128]{2,1,0:T(4,128)(4,1)}, u32[]{:S(2)}) copy-start(pred[50,4,128]{2,1,0:T(4,128)(4,1)} %copy-done.16) | copy-start | bytes 76804
  143.9 2.6 %copy-start.7 = (f32[2,2,2,2,8,4,4,4]{4,7,6,5,2,1,3,0:T(4,128)}, f32[2,2,2,2,8,4,4,4]{4,7,6,5,2,1,3,0:T(4,128)S(1)}, u32[]{:S(2)}) copy-start(f32[2,2,2,2,8,4,4,4]{4,7,6,5,2,1,3,0:T(4,128)S(1)} %copy_dynamic-update-slice_fusion) | copy-start | bytes 98308
  144.7 11.7 %collective-permute-start.1 = (f32[2,2,2,1,8,4,4,4]{4,7,6,5,2,1,3,0:T(4,128)}, f32[2,2,2,1,8,4,4,4]{4,7,6,5,2,1,3,0:T(4,128)S(1)}, u32[]{:S(2)}, u32[]{:S(2)}) collective-permute-start(f32[2,2,2,1,8,4,4,4]{4,7,6,5,2,1,3,0:T(4,128)} %constant_dynamic-slice_fusion.2), channel_id=1, source_target_pairs={{0,1},{1,0},{2,3},{3,2},{4,5},{5,4},{6,7},{7,6},{8,9},{9,8},{10,11... | collective-permute-start | bytes 49160 | tf_op jit(solution)/shard_map/ppermute | solution.py:172
  155.8 13.4 %copy-start.4 = (f32[2,2,1,8,4,4,4,128]{7,3,2,1,0,6,5,4:T(8,128)S(1)}, f32[2,2,1,8,4,4,4,128]{7,3,2,1,0,6,5,4:T(8,128)}, u32[]{:S(2)}) copy-start(f32[2,2,1,8,4,4,4,128]{7,3,2,1,0,6,5,4:T(8,128)} %constant_dynamic-slice_fusion.3) | copy-start | bytes 3145732
  156.0 13.1 %collective-permute-start.2 = (bf16[2,2,1,8,4,4,4,128]{7,6,5,4,3,2,1,0:T(4,128)(2,1)S(1)}, bf16[2,2,1,8,4,4,4,128]{7,6,5,4,3,2,1,0:T(4,128)(2,1)}, u32[]{:S(2)}, u32[]{:S(2)}) collective-permute-start(bf16[2,2,1,8,4,4,4,128]{7,6,5,4,3,2,1,0:T(4,128)(2,1)S(1)} %copy.364), channel_id=1, source_target_pairs={{0,1},{1,0},{2,3},{3,2},{4,5},{5,4},{6,7},{7,6},{8,9},{9,8},{10,11... | collective-permute-start | bytes 1572872 | tf_op jit(solution)/shard_map/ppermute | solution.py:173
  157.5 5.0 %collective-permute-start.3 = (f32[2,2,1,1,8,4,4,4]{4,7,6,5,3,2,1,0:T(4,128)S(1)}, f32[2,2,1,1,8,4,4,4]{4,7,6,5,3,2,1,0:T(4,128)S(1)}, u32[]{:S(2)}, u32[]{:S(2)}) collective-permute-start(f32[2,2,1,1,8,4,4,4]{4,7,6,5,3,2,1,0:T(4,128)S(1)} %get-tuple-element.48), channel_id=1, source_target_pairs={{0,2},{1,3},{2,0},{3,1},{4,6},{5,7},{6,4},{7,5},{8,10},{9,11},{10,... | collective-permute-start | bytes 24584 | tf_op jit(solution)/shard_map/ppermute | solution.py:172
  162.6 3.1 %copy-start.10 = (f32[2,2,1,1,8,4,4,4]{4,7,6,5,3,2,1,0:T(4,128)}, f32[2,2,1,1,8,4,4,4]{4,7,6,5,3,2,1,0:T(4,128)S(1)}, u32[]{:S(2)}) copy-start(f32[2,2,1,1,8,4,4,4]{4,7,6,5,3,2,1,0:T(4,128)S(1)} %collective-permute-done.3) | copy-start | bytes 24580
  162.7 11.1 %collective-permute-start.5 = (f32[2,1,1,1,8,4,4,4]{4,7,6,5,3,2,1,0:T(4,128)S(1)}, f32[2,1,1,1,8,4,4,4]{4,7,6,5,3,2,1,0:T(4,128)S(1)}, u32[]{:S(2)}, u32[]{:S(2)}) collective-permute-start(f32[2,1,1,1,8,4,4,4]{4,7,6,5,3,2,1,0:T(4,128)S(1)} %get-tuple-element.52), channel_id=1, source_target_pairs={{0,4},{1,5},{2,6},{3,7},{4,0},{5,1},{6,2},{7,3},{8,12},{9,13},{10,... | collective-permute-start | bytes 12296 | tf_op jit(solution)/shard_map/ppermute | solution.py:172
  169.1 4.1 %copy-start.11 = (f32[2,2,1,1,8,4,4,4]{4,7,6,5,3,2,1,0:T(4,128)S(1)}, f32[2,2,1,1,8,4,4,4]{4,7,6,5,3,2,1,0:T(4,128)}, u32[]{:S(2)}) copy-start(f32[2,2,1,1,8,4,4,4]{4,7,6,5,3,2,1,0:T(4,128)} %copy-done.10) | copy-start | bytes 24580
  171.4 10.0 %copy-start.13 = (f32[8,4,4,4]{0,3,2,1:T(4,128)S(1)}, f32[8,4,4,4]{0,3,2,1:T(4,128)}, u32[]{:S(2)}) copy-start(f32[8,4,4,4]{0,3,2,1:T(4,128)} %copy-done.12) | copy-start | bytes 6148
  171.4 10.0 %copy-start.15 = (f32[8,4,4,4]{0,3,2,1:T(4,128)S(1)}, f32[8,4,4,4]{0,3,2,1:T(4,128)}, u32[]{:S(2)}) copy-start(f32[8,4,4,4]{0,3,2,1:T(4,128)} %get-tuple-element.50) | copy-start | bytes 6148
  171.4 14.6 %copy-start.14 = (bf16[8,4,4,4,4]{4,3,2,1,0:T(4,128)(2,1)S(1)}, bf16[8,4,4,4,4]{4,3,2,1,0:T(4,128)(2,1)}, u32[]{:S(2)}) copy-start(bf16[8,4,4,4,4]{4,3,2,1,0:T(4,128)(2,1)} %copy.313) | copy-start | bytes 12292
  171.5 6.5 %collective-permute-start.4 = (bf16[2,1,1,8,4,4,4,128]{7,6,5,4,3,2,1,0:T(4,128)(2,1)S(1)}, bf16[2,1,1,8,4,4,4,128]{7,6,5,4,3,2,1,0:T(4,128)(2,1)S(1)}, u32[]{:S(2)}, u32[]{:S(2)}) collective-permute-start(bf16[2,1,1,8,4,4,4,128]{7,6,5,4,3,2,1,0:T(4,128)(2,1)S(1)} %dynamic-slice_convert_fusion.1), channel_id=1, source_target_pairs={{0,2},{1,3},{2,0},{3,1},{4,6},{5,7},{6,4},{7,5},{8,10},{9,11},{10,... | collective-permute-start | bytes 786440 | tf_op jit(solution)/shard_map/ppermute | solution.py:173
  178.7 7.3 %collective-permute-start.6 = (bf16[1,1,1,8,4,4,4,128]{7,6,5,4,3,2,1,0:T(4,128)(2,1)S(1)}, bf16[1,1,1,8,4,4,4,128]{7,6,5,4,3,2,1,0:T(4,128)(2,1)S(1)}, u32[]{:S(2)}, u32[]{:S(2)}) collective-permute-start(bf16[1,1,1,8,4,4,4,128]{7,6,5,4,3,2,1,0:T(4,128)(2,1)S(1)} %dynamic-slice_convert_fusion.2), channel_id=1, source_target_pairs={{0,4},{1,5},{2,6},{3,7},{4,0},{5,1},{6,2},{7,3},{8,12},{9,13},{10,... | collective-permute-start | bytes 393224 | tf_op jit(solution)/shard_map/ppermute | solution.py:173
  195.9 6.3 %collective-permute-start.7 = (bf16[1,8,4,2560]{3,1,2,0:T(8,128)(2,1)S(1)}, bf16[1,8,4,2560]{3,1,2,0:T(8,128)(2,1)S(1)}, u32[]{:S(2)}, u32[]{:S(2)}) collective-permute-start(bf16[1,8,4,2560]{3,1,2,0:T(8,128)(2,1)S(1)} %constant_dynamic-slice_fusion), channel_id=1, source_target_pairs={{0,8},{8,0},{1,9},{9,1},{2,10},{10,2},{3,11},{11,3},{4,12},{12,4},... | collective-permute-start | bytes 491528 | tf_op jit(solution)/shard_map/ppermute | solution.py:133
  202.3 9.9 %collective-permute-start.8 = (bf16[1,8,4,2560]{3,1,2,0:T(8,128)(2,1)S(1)}, bf16[1,8,4,2560]{3,1,2,0:T(8,128)(2,1)S(1)}, u32[]{:S(2)}, u32[]{:S(2)}) collective-permute-start(bf16[1,8,4,2560]{3,1,2,0:T(8,128)(2,1)S(1)} %add_convert_fusion.1), channel_id=1, source_target_pairs={{0,4},{1,5},{2,6},{3,7},{4,0},{5,1},{6,2},{7,3},{8,12},{9,13},{10,... | collective-permute-start | bytes 491528 | tf_op jit(solution)/shard_map/ppermute | solution.py:145
  212.2 8.7 %collective-permute-start.9 = (bf16[2,1,8,4,2560]{4,2,3,1,0:T(8,128)(2,1)S(1)}, bf16[2,1,8,4,2560]{4,2,3,1,0:T(8,128)(2,1)S(1)}, u32[]{:S(2)}, u32[]{:S(2)}) collective-permute-start(bf16[2,1,8,4,2560]{4,2,3,1,0:T(8,128)(2,1)S(1)} %maximum_select_fusion.5), channel_id=1, source_target_pairs={{0,2},{1,3},{2,0},{3,1},{4,6},{5,7},{6,4},{7,5},{8,10},{9,11},{10,... | collective-permute-start | bytes 983048 | tf_op jit(solution)/shard_map/ppermute | solution.py:145
  221.1 15.5 %collective-permute-start.10 = (bf16[2,2,1,8,4,2560]{5,3,4,1,2,0:T(8,128)(2,1)S(1)}, bf16[2,2,1,8,4,2560]{5,3,4,1,2,0:T(8,128)(2,1)S(1)}, u32[]{:S(2)}, u32[]{:S(2)}) collective-permute-start(bf16[2,2,1,8,4,2560]{5,3,4,1,2,0:T(8,128)(2,1)S(1)} %maximum_select_fusion.3), channel_id=1, source_target_pairs={{0,1},{1,0},{2,3},{3,2},{4,5},{5,4},{6,7},{7,6},{8,9},{9,8},{10,11... | collective-permute-start | bytes 1966088 | tf_op jit(solution)/shard_map/ppermute | solution.py:145
  236.5 0.8 copy-start.9
  237.4 3.9 %copy-start.1 = (bf16[2560,512]{1,0:T(8,128)(2,1)S(1)}, bf16[2560,512]{1,0:T(8,128)(2,1)}, u32[]{:S(2)}) copy-start(bf16[2560,512]{1,0:T(8,128)(2,1)} %param.15) | copy-start | bytes 7864324
Sparse Core Ops, SparseCore 0:
  80.9 24.7 all-reduce.2

commit v3 on v2

--- a/solution.py
+++ b/solution.py
@@ -208,24 +208,27 @@
         paged_value_cache.shape[0], block_len, heads_kv, HEAD_SIZE
     )
     step_count = states.shape[1]
-    as_float = states.astype(jnp.float32)
+    token_count = states.shape[0] * step_count
+    as_float = states.reshape(token_count, -1).astype(jnp.float32)
     squares = lax.psum(jnp.sum(as_float * as_float, -1), "row")
-    normed = (as_float * lax.rsqrt(squares / D + EPSILON)[..., None] * norm_gain).astype(
+    normed = (as_float * lax.rsqrt(squares / D + EPSILON)[:, None] * norm_gain).astype(
         jnp.bfloat16
     )
     gathered = pair_gather(normed, "col")
-    piece_rows = gathered.reshape(req_count * lax.axis_size("row") * step_count, -1)
+    gathered, key_rows, value_rows = lax.optimization_barrier((gathered, key_rows, value_rows))
     parts_out = [
-        jnp.dot(piece_rows, matrix, preferred_element_type=jnp.float32) for matrix in (wq, wk, wv)
+        jnp.dot(gathered, matrix, preferred_element_type=jnp.float32) for matrix in (wq, wk, wv)
     ]
-    output_projected = lax.psum_scatter(
-        jnp.concatenate(parts_out, axis=-1)
-        .reshape(req_count * lax.axis_size("row"), step_count, -1)
-        .astype(jnp.bfloat16),
-        "row",
-        scatter_dimension=0,
-        tiled=True,
-    ).astype(jnp.float32)
+    output_projected = (
+        lax.psum_scatter(
+            jnp.concatenate(parts_out, axis=-1).astype(jnp.bfloat16),
+            "row",
+            scatter_dimension=0,
+            tiled=True,
+        )
+        .astype(jnp.float32)
+        .reshape(req_count, step_count, -1)
+    )
     token_positions = lengths[:, None] + jnp.arange(step_count, dtype=jnp.int32)[None, :]
     query_rows = rotary_apply(
         output_projected[..., :q_width].reshape(req_count, step_count, -1, HEAD_SIZE),

time: 249 us -> 224 us (0.90)
  waiting for transfers between devices: 74.6 us -> 63.9 us
  other arithmetic: 34.4 us -> 29 us
  matrix products: 37.2 us -> 32.6 us
    ppermute x1, waiting for transfers between devices: 29.4 us -> 5.05 us  [pair_gather(): other = lax.ppermute(part, axis_name, [(0, 1), (1, 0)])]
    reduce_scatter x0 -> x1, waiting for transfers between devices: none -> 9.4 us  [on_device(): lax.psum_scatter(jnp.concatenate(parts_out, axis=-1).astype(jnp.bfloat16)...]
    select_n x1 -> x0, local copies, waits for them, and re-layouts: 5.31 us -> none  [pair_gather(): jnp.where(side == 0, jnp.concatenate([part, other], 0), jnp.concatenate([...]
    dot_general x3, matrix products: 13.4 us -> 8.8 us  [on_device(): jnp.dot(gathered, matrix, preferred_element_type=jnp.float32)]
    reshape x0 -> x1, local copies, waits for them, and re-layouts: none -> 4.2 us  [on_device(): output_projected = lax.psum_scatter(jnp.concatenate(parts_out, axis=-1).a...]
    select_n x1, other arithmetic: 6.46 us -> 2.94 us  [pair_gather(): jnp.where(side == 0, jnp.concatenate([part, other], 0), jnp.concatenate([...]
    convert_element_type x1, local copies, waits for them, and re-layouts: 6.12 us -> 3.49 us  [on_device(): as_float = states.reshape(token_count, -1).astype(jnp.float32)]
    unnamed x48 -> x49, local copies, waits for them, and re-layouts: 6.02 us -> 5.33 us
  transfers between devices with their start and end apart: 12 -> 12, of which waited for: 9 -> 10; matrix products, arithmetic and copies ran while one was open for 19% -> 21% of each run, Pallas kernels for 0% -> 0%
where the time goes in v3:
time: 224 us; the launch traced here: 223 us
  waiting for transfers between devices  63.9 us (29%)
  local copies, waits for them, and re-layouts  61.6 us (28%)
  matrix products  32.6 us (15%)
  other arithmetic  29 us (13%)
  starting transfers between devices  16.6 us (7%)
  between operations  14.6 us (7%)
  blocking collectives  4.84 us (2%)
    ppermute x3, waiting for transfers between devices, doubling_gather(): got = lax.ppermute(block, axis_name, pairs)  29.2 us
    ppermute x3, waiting for transfers between devices, seq_merge(): lax.ppermute(send_values.astype(jnp.bfloat16), 'seq', pairs)  13.8 us
    reshape x1, local copies, waits for them, and re-layouts, on_device(): paged_value_cache.reshape(paged_value_cache.shape[0], block_len, heads_kv...  12.2 us
    reshape x1, local copies, waits for them, and re-layouts, on_device(): paged_key_cache.reshape(paged_key_cache.shape[0], block_len, heads_kv, HE...  12.2 us
    reduce_scatter x1, waiting for transfers between devices, on_device(): lax.psum_scatter(jnp.concatenate(parts_out, axis=-1).astype(jnp.bfloat16)...  9.4 us
    dot_general x3, matrix products, on_device(): jnp.dot(gathered, matrix, preferred_element_type=jnp.float32)  8.8 us
    dot_general x1, matrix products, slot_parts(): jnp.einsum('nsagh,nbah->nasgb', slot_queries, key_rows, preferred_element...  7.94 us
    ppermute x3, starting transfers between devices, seq_merge(): got_stats = lax.ppermute(send_stats, 'seq', pairs)  6.14 us
  transfers between devices with their start and end apart: 12, of which 10 were waited for; matrix products, arithmetic and copies ran while one was open for 21% of the time, Pallas kernels for 0%

profile of v3, /device:TPU:0, one launch (start us, length us, event | category | flops | bytes accessed | tf_op | source)
XLA Modules:
  0.0 223.1 jit_solution(10864319200849631849)
XLA Ops:
  7.2 2.2 multiply_reduce_fusion
  9.5 3.5 %reshape.903 = f32[256,2560]{1,0:T(8,128)} reshape(bf16[64,4,2560]{2,1,0:T(4,128)(2,1)} %param.11) | data formatting | bytes 3932160 | tf_op jit(solution)/shard_map/convert_element_type | solution.py:212
  13.0 2.6 %psum.7 = f32[256]{0:T(256)S(1)} all-reduce(f32[256]{0:T(256)S(1)} %reduce_sum.30), channel_id=1, replica_groups=mesh['row'=2,'col'=2,'seq'=8] {'row'}, use_global_device_ids=true, to_apply=%region_1.0 | all-reduce | flops 256 | bytes 2048 | tf_op jit(solution)/shard_map/psum | solution.py:213
  15.6 3.1 %multiply_convert_fusion = bf16[256,2560]{1,0:T(8,128)(2,1)} fusion(f32[256,2560]{1,0:T(8,128)} %reshape.903, f32[2560]{0:T(1024)S(1)} %copy-done.16, f32[256]{0:T(256)S(1)} %add_rsqrt_fusion), kind=kLoop, calls=%fused_computation.13 | loop fusion | flops 1966080 | bytes 3943424 | tf_op jit(solution)/shard_map/convert_element_type | solution.py:214
  18.7 2.8 %collective-permute-start = (bf16[256,2560]{1,0:T(8,128)(2,1)}, bf16[256,2560]{1,0:T(8,128)(2,1)}, u32[]{:S(2)}, u32[]{:S(2)}) collective-permute-start(bf16[256,2560]{1,0:T(8,128)(2,1)} %multiply_convert_fusion), channel_id=1, source_target_pairs={{0,8},{8,0},{1,9},{9,1},{2,10},{10,2},{3,11},{11,3},{4,12},{12,4},... | collective-permute-start | bytes 3932168 | tf_op jit(solution)/shard_map/ppermute | solution.py:119
  21.6 12.2 %reshape.894 = bf16[50,128,4,128]{3,2,1,0:T(4,128)(2,1)} reshape(bf16[50,128,512]{2,1,0:T(8,128)(2,1)} %param.20) | data formatting | bytes 13107200 | tf_op jit(solution)/shard_map/reshape | solution.py:206
  33.7 12.2 %reshape.895 = bf16[50,128,4,128]{3,2,1,0:T(4,128)(2,1)} reshape(bf16[50,128,512]{2,1,0:T(8,128)(2,1)} %param.21) | data formatting | bytes 13107200 | tf_op jit(solution)/shard_map/reshape | solution.py:207
  45.9 5.1 %collective-permute-done = bf16[256,2560]{1,0:T(8,128)(2,1)} collective-permute-done((bf16[256,2560]{1,0:T(8,128)(2,1)}, bf16[256,2560]{1,0:T(8,128)(2,1)}, u32[]{:S(2)}, u32[]{:S(2)}) %collective-permute-start) | collective-permute-done | bytes 1310752 | tf_op jit(solution)/shard_map/ppermute | solution.py:119
  51.0 2.9 %maximum_select_fusion = bf16[512,2560]{1,0:T(8,128)(2,1)S(1)} fusion(bf16[256,2560]{1,0:T(8,128)(2,1)} %collective-permute-done, bf16[256,2560]{1,0:T(8,128)(2,1)} %multiply_convert_fusion, pred[]{:T(512)S(6)} %eq.35), kind=kLoop, calls=%fused_computation.12 | loop fusion | flops 11796480 | bytes 5242881 | tf_op jit(solution)/shard_map/jit(_where)/select_n | solution.py:120
  54.0 1.5 convolution_convert_fusion.1
  55.7 1.5 convolution_convert_fusion.2
  57.7 5.8 %convolution_convert_fusion = bf16[512,2048]{1,0:T(8,128)(2,1)S(1)} fusion(bf16[512,2560]{1,0:T(8,128)(2,1)S(1)} %maximum_select_fusion, bf16[2560,2048]{1,0:T(8,128)(2,1)S(1)} %bitcast.156), kind=kOutput, calls=%fused_computation.11 | convolution fusion | flops 5369757696 | bytes 15204352 | tf_op jit(solution)/shard_map/dot_general | solution.py:220
  63.5 1.8 pad_maximum_fusion
  66.0 0.8 gather_fusion
  66.8 1.1 multiply_cosine_fusion
  68.5 9.4 %reduce-scatter.2.cloned.1.call-done = bf16[256,3072]{1,0:T(8,128)(2,1)} async-done(((bf16[512,3072]{1,0:T(8,128)(2,1)}), bf16[256,3072]{1,0:T(8,128)(2,1)}) %reduce-scatter.2.cloned.1.call-update) | async-done | bytes 1572880 | tf_op jit(solution)/shard_map/reduce_scatter | solution.py:223
  77.9 4.2 %reshape.905 = f32[64,4,3072]{2,1,0:T(4,128)} reshape(bf16[256,3072]{1,0:T(8,128)(2,1)} %reduce-scatter.2.cloned.1.call-done) | data formatting | bytes 4718592 | tf_op jit(solution)/shard_map/reshape | solution.py:230
  82.1 1.8 slice_bitcast_fusion.2
  83.9 1.1 slice_bitcast_fusion
  85.0 3.2 %slice.92 = f32[64,4,2048]{2,1,0:T(4,128)} slice(f32[64,4,3072]{2,1,0:T(4,128)} %reshape.905), slice={[0:64], [0:4], [0:2048]} | slice | bytes 4194304 | tf_op jit(solution)/shard_map/slice | solution.py:234
  88.2 2.5 %reshape.941 = f32[64,4,16,128]{3,2,1,0:T(8,128)S(1)} reshape(f32[64,4,2048]{2,1,0:T(4,128)} %slice.92) | data formatting | bytes 4194304 | tf_op jit(solution)/shard_map/reshape | solution.py:234
  90.7 0.7 fusion.76
  92.0 1.4 pad_maximum_fusion.1
  94.0 2.2 gather_fusion.1
  96.2 7.9 %select_reduce_fusion.1 = (f32[50,4,4,4]{3,2,1,0:T(4,128)S(1)}, f32[50,4,4,4,128]{4,3,2,1,0:T(4,128)}) fusion(pred[50,4,128]{2,1,0:T(4,128)(4,1)S(1)} %or_and_fusion, bf16[50,4,4,4,128]{4,3,1,2,0:T(4,128)(2,1)} %gather_fusion.1, bf16[50,128,4,128,1]{3,2,1,0,4:T(4,128)(2,1)} %bitcast.133), kind=kOutput, calls=%fused_computation.21 | convolution fusion | flops 106083200 | bytes 9049600 | tf_op jit(solution)/shard_map/nsagh,nbah->nasgb/dot_general | solution.py:40
  104.1 1.0 select_reduce_fusion
  105.1 1.1 stack.72
  107.5 1.2 fusion.34
  109.4 0.8 fusion.38
  110.2 0.8 copy_dynamic-update-slice_fusion.1
  111.0 3.4 %fusion.16 = f32[50,4,4,4]{3,2,1,0:T(4,128)S(1)} fusion(f32[50,4,4,4,128]{4,3,2,1,0:T(4,128)} %get-tuple-element.62, f32[50,4,4,4]{3,2,1,0:T(4,128)S(1)} %get-tuple-element.61, pred[50,4,128]{2,1,0:T(4,128)(4,1)S(1)} %or_and_fusion), kind=kLoop, calls=%fused_computation.32 | loop fusion | flops 1635200 | bytes 1689600 | tf_op jit(solution)/shard_map/reduce_sum | solution.py:56
  114.4 0.8 gather_fusion.2
  115.2 0.8 fusion.75
  117.1 0.8 constant_dynamic-slice_fusion.2
  117.9 1.7 collective-permute-start.1
  119.6 4.7 %fusion.11 = f32[50,4,4,4,128]{4,3,2,1,0:T(4,128)S(1)} fusion(bf16[50,128,4,128,1]{3,2,1,0,4:T(4,128)(2,1)} %bitcast.132, f32[50,4,4,4,128]{4,3,2,1,0:T(4,128)} %get-tuple-element.62, f32[50,4,4,4]{3,2,1,0:T(4,128)} %bitcast.152, f32[50,4,4,4]{3,2,1,0:T(4,128)S(1)} %get-tuple-element.61, pred[50,4,128]{2,1,0:T(4,128)(4,1)S(1)} %copy-done.15), kind=kOutput, calls=%fused_computation.22 | convolution fusion | flops 106905600 | bytes 9881600 | tf_op jit(solution)/shard_map/nasgb,nbah->nasgh/dot_general | solution.py:57
  124.4 2.2 fusion.9
  126.5 1.1 constant_dynamic-slice_fusion.3
  127.8 1.1 copy.266
  129.6 1.1 fusion.31
  130.7 1.8 collective-permute-start.3
  132.5 1.0 fusion.26
  134.4 1.6 collective-permute-done.3
  136.1 2.6 %collective-permute-start.5 = (f32[2,1,1,1,8,4,4,4]{4,7,6,5,3,2,1,0:T(4,128)S(1)}, f32[2,1,1,1,8,4,4,4]{4,7,6,5,3,2,1,0:T(4,128)S(1)}, u32[]{:S(2)}, u32[]{:S(2)}) collective-permute-start(f32[2,1,1,1,8,4,4,4]{4,7,6,5,3,2,1,0:T(4,128)S(1)} %get-tuple-element.55), channel_id=1, source_target_pairs={{0,4},{1,5},{2,6},{3,7},{4,0},{5,1},{6,2},{7,3},{8,12},{9,13},{10,... | collective-permute-start | bytes 12296 | tf_op jit(solution)/shard_map/ppermute | solution.py:172
  138.8 4.5 %collective-permute-done.2 = bf16[2,2,1,8,4,4,4,128]{7,6,5,4,3,2,1,0:T(4,128)(2,1)} collective-permute-done((bf16[2,2,1,8,4,4,4,128]{7,6,5,4,3,2,1,0:T(4,128)(2,1)S(1)}, bf16[2,2,1,8,4,4,4,128]{7,6,5,4,3,2,1,0:T(4,128)(2,1)}, u32[]{:S(2)}, u32[]{:S(2)}) %collective-permute-start.2) | collective-permute-done | bytes 524320 | tf_op jit(solution)/shard_map/ppermute | solution.py:173
  143.2 2.2 %fusion.15 = f32[2,2,1,8,4,4,4,128]{7,6,5,4,3,2,1,0:T(4,128)S(1)} fusion(f32[2,2,1,8,4,4,4,128]{7,3,2,1,0,6,5,4:T(8,128)S(1)} %copy-done.3, bf16[2,2,1,8,4,4,4,128]{7,6,5,4,3,2,1,0:T(4,128)(2,1)} %collective-permute-done.2, f32[2,2,8,4,4,4]{5,4,3,2,1,0:T(4,128)S(1)} %copy.252, f32[2,2,8,4,4,4]{5,4,3,2,1,0:T(4,128)S(1)} %copy.250), kind=kLoop, calls=%fused_computation.31 | loop fusion | flops 1048576 | bytes 2637824 | tf_op jit(solution)/shard_map/add | solution.py:182
  145.6 1.6 collective-permute-start.4
  147.8 5.3 %collective-permute-done.4 = bf16[2,1,1,8,4,4,4,128]{7,6,5,4,3,2,1,0:T(4,128)(2,1)S(1)} collective-permute-done((bf16[2,1,1,8,4,4,4,128]{7,6,5,4,3,2,1,0:T(4,128)(2,1)S(1)}, bf16[2,1,1,8,4,4,4,128]{7,6,5,4,3,2,1,0:T(4,128)(2,1)S(1)}, u32[]{:S(2)}, u32[]{:S(2)}) %collective-permute-start.4) | collective-permute-done | bytes 262176 | tf_op jit(solution)/shard_map/ppermute | solution.py:173
  153.8 2.5 %collective-permute-start.6 = (bf16[1,1,1,8,4,4,4,128]{7,6,5,4,3,2,1,0:T(4,128)(2,1)S(1)}, bf16[1,1,1,8,4,4,4,128]{7,6,5,4,3,2,1,0:T(4,128)(2,1)S(1)}, u32[]{:S(2)}, u32[]{:S(2)}) collective-permute-start(bf16[1,1,1,8,4,4,4,128]{7,6,5,4,3,2,1,0:T(4,128)(2,1)S(1)} %dynamic-slice_convert_fusion.1), channel_id=1, source_target_pairs={{0,4},{1,5},{2,6},{3,7},{4,0},{5,1},{6,2},{7,3},{8,12},{9,13},{10,... | collective-permute-start | bytes 393224 | tf_op jit(solution)/shard_map/ppermute | solution.py:173
  157.2 4.0 %collective-permute-done.6 = bf16[1,1,1,8,4,4,4,128]{7,6,5,4,3,2,1,0:T(4,128)(2,1)S(1)} collective-permute-done((bf16[1,1,1,8,4,4,4,128]{7,6,5,4,3,2,1,0:T(4,128)(2,1)S(1)}, bf16[1,1,1,8,4,4,4,128]{7,6,5,4,3,2,1,0:T(4,128)(2,1)S(1)}, u32[]{:S(2)}, u32[]{:S(2)}) %collective-permute-start.6) | collective-permute-done | bytes 131104 | tf_op jit(solution)/shard_map/ppermute | solution.py:173
  161.2 1.6 fusion.36
  163.0 2.3 %all_gather.4 = bf16[2,8,4,2048]{3,1,2,0:T(8,128)(2,1)S(1)} all-gather(bf16[1,8,4,2048]{3,1,2,0:T(8,128)(2,1)S(1)} %convert_element_type.109), channel_id=1, replica_groups=mesh['row'=2,'col'=2,'seq'=8] {'row'}, dimensions={0}, use_global_device_ids=true | all-gather | bytes 393216 | tf_op jit(solution)/shard_map/all_gather | solution.py:275
  165.2 5.9 %fusion.6 = bf16[2,8,4,2560]{3,1,2,0:T(8,128)(2,1)S(1)} fusion(bf16[2,8,4,2048]{3,1,2,0:T(8,128)(2,1)S(1)} %all_gather.4, bf16[2048,2560]{1,0:T(8,128)(2,1)} %param.16), kind=kOutput, calls=%fused_computation.9 | convolution fusion | flops 671252480 | bytes 11075584 | tf_op jit(solution)/shard_map/dot_general | solution.py:277
  171.1 1.5 collective-permute-start.7
  172.7 4.8 %collective-permute-done.7 = bf16[1,8,4,2560]{3,1,2,0:T(8,128)(2,1)S(1)} collective-permute-done((bf16[1,8,4,2560]{3,1,2,0:T(8,128)(2,1)S(1)}, bf16[1,8,4,2560]{3,1,2,0:T(8,128)(2,1)S(1)}, u32[]{:S(2)}, u32[]{:S(2)}) %collective-permute-start.7) | collective-permute-done | bytes 163872 | tf_op jit(solution)/shard_map/ppermute | solution.py:133
  177.5 1.1 collective-permute-start.8
  178.5 8.8 %collective-permute-done.8 = bf16[1,8,4,2560]{3,1,2,0:T(8,128)(2,1)S(1)} collective-permute-done((bf16[1,8,4,2560]{3,1,2,0:T(8,128)(2,1)S(1)}, bf16[1,8,4,2560]{3,1,2,0:T(8,128)(2,1)S(1)}, u32[]{:S(2)}, u32[]{:S(2)}) %collective-permute-start.8) | collective-permute-done | bytes 163872 | tf_op jit(solution)/shard_map/ppermute | solution.py:145
  187.6 8.8 %collective-permute-done.9 = bf16[2,1,8,4,2560]{4,2,3,1,0:T(8,128)(2,1)S(1)} collective-permute-done((bf16[2,1,8,4,2560]{4,2,3,1,0:T(8,128)(2,1)S(1)}, bf16[2,1,8,4,2560]{4,2,3,1,0:T(8,128)(2,1)S(1)}, u32[]{:S(2)}, u32[]{:S(2)}) %collective-permute-start.9) | collective-permute-done | bytes 327712 | tf_op jit(solution)/shard_map/ppermute | solution.py:145
  197.0 1.8 slice.146
  198.9 1.1 fusion.87
  200.0 11.5 %collective-permute-done.10 = bf16[2,2,1,8,4,2560]{5,3,4,1,2,0:T(8,128)(2,1)S(1)} collective-permute-done((bf16[2,2,1,8,4,2560]{5,3,4,1,2,0:T(8,128)(2,1)S(1)}, bf16[2,2,1,8,4,2560]{5,3,4,1,2,0:T(8,128)(2,1)S(1)}, u32[]{:S(2)}, u32[]{:S(2)}) %collective-permute-start.10) | collective-permute-done | bytes 655392 | tf_op jit(solution)/shard_map/ppermute | solution.py:145
  211.6 0.8 copy-done.7
  212.4 1.7 fusion.14
  214.2 2.1 copy.274
  (109 shorter events, 11.5 us)
Async XLA Ops:
  7.2 46.8 %copy-start = (bf16[2560,512]{1,0:T(8,128)(2,1)S(1)}, bf16[2560,512]{1,0:T(8,128)(2,1)}, u32[]{:S(2)}) copy-start(bf16[2560,512]{1,0:T(8,128)(2,1)} %param.15) | copy-start | bytes 7864324
  7.2 70.7 %reduce-scatter.2.cloned.1.call-start = ((), (), s32[]{:S(2)}) async-start(), calls=%async_computation.1 | async-start | bytes 4718592 | tf_op jit(solution)/shard_map/reduce_scatter | solution.py:223
  9.5 6.2 %copy-start.16 = (f32[2560]{0:T(1024)S(1)}, f32[2560]{0:T(1024)}, u32[]{:S(2)}) copy-start(f32[2560]{0:T(1024)} %param.12) | copy-start | bytes 30724
  18.7 32.2 %collective-permute-start = (bf16[256,2560]{1,0:T(8,128)(2,1)}, bf16[256,2560]{1,0:T(8,128)(2,1)}, u32[]{:S(2)}, u32[]{:S(2)}) collective-permute-start(bf16[256,2560]{1,0:T(8,128)(2,1)} %multiply_convert_fusion), channel_id=1, source_target_pairs={{0,8},{8,0},{1,9},{9,1},{2,10},{10,2},{3,11},{11,3},{4,12},{12,4},... | collective-permute-start | bytes 3932168 | tf_op jit(solution)/shard_map/ppermute | solution.py:119
  51.0 6.2 %slice-start = ((s8[10485760]{0:T(1024)(128)(4,1)}), s8[4194304]{0:T(1024)(128)(4,1)S(1)}, s32[]{:S(2)}) async-start(s8[10485760]{0:T(1024)(128)(4,1)} %bitcast.155), calls=%async_computation.2 | async-start | bytes 8388608
  53.9 1.7 copy-start.18
  53.9 3.3 %slice-start.1 = ((s8[10485760]{0:T(1024)(128)(4,1)}), s8[4194304]{0:T(1024)(128)(4,1)S(1)}, s32[]{:S(2)}) async-start(s8[10485760]{0:T(1024)(128)(4,1)} %bitcast.155), calls=%async_computation.3 | async-start | bytes 8388608
  55.7 2.0 slice-start.2
  65.3 0.7 copy-start.17
  65.3 0.7 copy-start.2
  65.3 2.7 %copy-start.19 = (s32[50]{0:T(128)S(1)}, s32[50]{0:T(128)}, u32[]{:S(2)}) copy-start(s32[50]{0:T(128)} %param.19) | copy-start | bytes 604
  68.5 42.5 %copy-start.14 = (pred[50,4,128]{2,1,0:T(4,128)(4,1)}, pred[50,4,128]{2,1,0:T(4,128)(4,1)S(1)}, u32[]{:S(2)}) copy-start(pred[50,4,128]{2,1,0:T(4,128)(4,1)S(1)} %or_and_fusion) | copy-start | bytes 76804
  107.1 3.1 %copy-start.6 = (f32[1,2,2,2,8,4,4,4]{4,3,2,1,7,6,5,0:T(2,128)S(1)}, f32[1,2,2,2,8,4,4,4]{4,3,2,1,7,6,5,0:T(2,128)}, u32[]{:S(2)}) copy-start(f32[1,2,2,2,8,4,4,4]{4,3,2,1,7,6,5,0:T(2,128)} %stack.72) | copy-start | bytes 49156
  109.4 1.6 copy-start.10
  115.2 1.8 copy-start.4
  115.2 4.4 %copy-start.15 = (pred[50,4,128]{2,1,0:T(4,128)(4,1)S(1)}, pred[50,4,128]{2,1,0:T(4,128)(4,1)}, u32[]{:S(2)}) copy-start(pred[50,4,128]{2,1,0:T(4,128)(4,1)} %copy-done.14) | copy-start | bytes 76804
  117.1 2.5 %copy-start.5 = (f32[2,2,2,2,8,4,4,4]{4,7,6,5,2,1,3,0:T(4,128)}, f32[2,2,2,2,8,4,4,4]{4,7,6,5,2,1,3,0:T(4,128)S(1)}, u32[]{:S(2)}) copy-start(f32[2,2,2,2,8,4,4,4]{4,7,6,5,2,1,3,0:T(4,128)S(1)} %copy_dynamic-update-slice_fusion) | copy-start | bytes 98308
  117.9 11.7 %collective-permute-start.1 = (f32[2,2,2,1,8,4,4,4]{4,7,6,5,2,1,3,0:T(4,128)}, f32[2,2,2,1,8,4,4,4]{4,7,6,5,2,1,3,0:T(4,128)S(1)}, u32[]{:S(2)}, u32[]{:S(2)}) collective-permute-start(f32[2,2,2,1,8,4,4,4]{4,7,6,5,2,1,3,0:T(4,128)} %constant_dynamic-slice_fusion.2), channel_id=1, source_target_pairs={{0,1},{1,0},{2,3},{3,2},{4,5},{5,4},{6,7},{7,6},{8,9},{9,8},{10,11... | collective-permute-start | bytes 49160 | tf_op jit(solution)/shard_map/ppermute | solution.py:172
  128.9 14.3 %copy-start.3 = (f32[2,2,1,8,4,4,4,128]{7,3,2,1,0,6,5,4:T(8,128)S(1)}, f32[2,2,1,8,4,4,4,128]{7,3,2,1,0,6,5,4:T(8,128)}, u32[]{:S(2)}) copy-start(f32[2,2,1,8,4,4,4,128]{7,3,2,1,0,6,5,4:T(8,128)} %constant_dynamic-slice_fusion.3) | copy-start | bytes 3145732
  129.2 14.0 %collective-permute-start.2 = (bf16[2,2,1,8,4,4,4,128]{7,6,5,4,3,2,1,0:T(4,128)(2,1)S(1)}, bf16[2,2,1,8,4,4,4,128]{7,6,5,4,3,2,1,0:T(4,128)(2,1)}, u32[]{:S(2)}, u32[]{:S(2)}) collective-permute-start(bf16[2,2,1,8,4,4,4,128]{7,6,5,4,3,2,1,0:T(4,128)(2,1)S(1)} %copy.317), channel_id=1, source_target_pairs={{0,1},{1,0},{2,3},{3,2},{4,5},{5,4},{6,7},{7,6},{8,9},{9,8},{10,11... | collective-permute-start | bytes 1572872 | tf_op jit(solution)/shard_map/ppermute | solution.py:173
  130.7 5.3 %collective-permute-start.3 = (f32[2,2,1,1,8,4,4,4]{4,7,6,5,3,2,1,0:T(4,128)S(1)}, f32[2,2,1,1,8,4,4,4]{4,7,6,5,3,2,1,0:T(4,128)S(1)}, u32[]{:S(2)}, u32[]{:S(2)}) collective-permute-start(f32[2,2,1,1,8,4,4,4]{4,7,6,5,3,2,1,0:T(4,128)S(1)} %get-tuple-element.51), channel_id=1, source_target_pairs={{0,2},{1,3},{2,0},{3,1},{4,6},{5,7},{6,4},{7,5},{8,10},{9,11},{10,... | collective-permute-start | bytes 24584 | tf_op jit(solution)/shard_map/ppermute | solution.py:172
  136.0 2.8 %copy-start.8 = (f32[2,2,1,1,8,4,4,4]{4,7,6,5,3,2,1,0:T(4,128)}, f32[2,2,1,1,8,4,4,4]{4,7,6,5,3,2,1,0:T(4,128)S(1)}, u32[]{:S(2)}) copy-start(f32[2,2,1,1,8,4,4,4]{4,7,6,5,3,2,1,0:T(4,128)S(1)} %collective-permute-done.3) | copy-start | bytes 24580
  136.1 11.6 %collective-permute-start.5 = (f32[2,1,1,1,8,4,4,4]{4,7,6,5,3,2,1,0:T(4,128)S(1)}, f32[2,1,1,1,8,4,4,4]{4,7,6,5,3,2,1,0:T(4,128)S(1)}, u32[]{:S(2)}, u32[]{:S(2)}) collective-permute-start(f32[2,1,1,1,8,4,4,4]{4,7,6,5,3,2,1,0:T(4,128)S(1)} %get-tuple-element.55), channel_id=1, source_target_pairs={{0,4},{1,5},{2,6},{3,7},{4,0},{5,1},{6,2},{7,3},{8,12},{9,13},{10,... | collective-permute-start | bytes 12296 | tf_op jit(solution)/shard_map/ppermute | solution.py:172
  143.2 4.0 %copy-start.9 = (f32[2,2,1,1,8,4,4,4]{4,7,6,5,3,2,1,0:T(4,128)S(1)}, f32[2,2,1,1,8,4,4,4]{4,7,6,5,3,2,1,0:T(4,128)}, u32[]{:S(2)}) copy-start(f32[2,2,1,1,8,4,4,4]{4,7,6,5,3,2,1,0:T(4,128)} %copy-done.8) | copy-start | bytes 24580
  145.5 10.8 %copy-start.11 = (f32[8,4,4,4]{0,3,2,1:T(4,128)S(1)}, f32[8,4,4,4]{0,3,2,1:T(4,128)}, u32[]{:S(2)}) copy-start(f32[8,4,4,4]{0,3,2,1:T(4,128)} %copy-done.10) | copy-start | bytes 6148
  145.5 10.7 %copy-start.13 = (f32[8,4,4,4]{0,3,2,1:T(4,128)S(1)}, f32[8,4,4,4]{0,3,2,1:T(4,128)}, u32[]{:S(2)}) copy-start(f32[8,4,4,4]{0,3,2,1:T(4,128)} %get-tuple-element.53) | copy-start | bytes 6148
  145.5 15.7 %copy-start.12 = (bf16[8,4,4,4,4]{4,3,2,1,0:T(4,128)(2,1)S(1)}, bf16[8,4,4,4,4]{4,3,2,1,0:T(4,128)(2,1)}, u32[]{:S(2)}) copy-start(bf16[8,4,4,4,4]{4,3,2,1,0:T(4,128)(2,1)} %copy.266) | copy-start | bytes 12292
  145.6 7.5 %collective-permute-start.4 = (bf16[2,1,1,8,4,4,4,128]{7,6,5,4,3,2,1,0:T(4,128)(2,1)S(1)}, bf16[2,1,1,8,4,4,4,128]{7,6,5,4,3,2,1,0:T(4,128)(2,1)S(1)}, u32[]{:S(2)}, u32[]{:S(2)}) collective-permute-start(bf16[2,1,1,8,4,4,4,128]{7,6,5,4,3,2,1,0:T(4,128)(2,1)S(1)} %dynamic-slice_convert_fusion), channel_id=1, source_target_pairs={{0,2},{1,3},{2,0},{3,1},{4,6},{5,7},{6,4},{7,5},{8,10},{9,11},{10,... | collective-permute-start | bytes 786440 | tf_op jit(solution)/shard_map/ppermute | solution.py:173
  153.8 7.4 %collective-permute-start.6 = (bf16[1,1,1,8,4,4,4,128]{7,6,5,4,3,2,1,0:T(4,128)(2,1)S(1)}, bf16[1,1,1,8,4,4,4,128]{7,6,5,4,3,2,1,0:T(4,128)(2,1)S(1)}, u32[]{:S(2)}, u32[]{:S(2)}) collective-permute-start(bf16[1,1,1,8,4,4,4,128]{7,6,5,4,3,2,1,0:T(4,128)(2,1)S(1)} %dynamic-slice_convert_fusion.1), channel_id=1, source_target_pairs={{0,4},{1,5},{2,6},{3,7},{4,0},{5,1},{6,2},{7,3},{8,12},{9,13},{10,... | collective-permute-start | bytes 393224 | tf_op jit(solution)/shard_map/ppermute | solution.py:173
  171.1 6.3 %collective-permute-start.7 = (bf16[1,8,4,2560]{3,1,2,0:T(8,128)(2,1)S(1)}, bf16[1,8,4,2560]{3,1,2,0:T(8,128)(2,1)S(1)}, u32[]{:S(2)}, u32[]{:S(2)}) collective-permute-start(bf16[1,8,4,2560]{3,1,2,0:T(8,128)(2,1)S(1)} %constant_dynamic-slice_fusion), channel_id=1, source_target_pairs={{0,8},{8,0},{1,9},{9,1},{2,10},{10,2},{3,11},{11,3},{4,12},{12,4},... | collective-permute-start | bytes 491528 | tf_op jit(solution)/shard_map/ppermute | solution.py:133
  177.5 9.9 %collective-permute-start.8 = (bf16[1,8,4,2560]{3,1,2,0:T(8,128)(2,1)S(1)}, bf16[1,8,4,2560]{3,1,2,0:T(8,128)(2,1)S(1)}, u32[]{:S(2)}, u32[]{:S(2)}) collective-permute-start(bf16[1,8,4,2560]{3,1,2,0:T(8,128)(2,1)S(1)} %add_convert_fusion.1), channel_id=1, source_target_pairs={{0,4},{1,5},{2,6},{3,7},{4,0},{5,1},{6,2},{7,3},{8,12},{9,13},{10,... | collective-permute-start | bytes 491528 | tf_op jit(solution)/shard_map/ppermute | solution.py:145
  187.4 9.0 %collective-permute-start.9 = (bf16[2,1,8,4,2560]{4,2,3,1,0:T(8,128)(2,1)S(1)}, bf16[2,1,8,4,2560]{4,2,3,1,0:T(8,128)(2,1)S(1)}, u32[]{:S(2)}, u32[]{:S(2)}) collective-permute-start(bf16[2,1,8,4,2560]{4,2,3,1,0:T(8,128)(2,1)S(1)} %maximum_select_fusion.5), channel_id=1, source_target_pairs={{0,2},{1,3},{2,0},{3,1},{4,6},{5,7},{6,4},{7,5},{8,10},{9,11},{10,... | collective-permute-start | bytes 983048 | tf_op jit(solution)/shard_map/ppermute | solution.py:145
  196.5 15.1 %collective-permute-start.10 = (bf16[2,2,1,8,4,2560]{5,3,4,1,2,0:T(8,128)(2,1)S(1)}, bf16[2,2,1,8,4,2560]{5,3,4,1,2,0:T(8,128)(2,1)S(1)}, u32[]{:S(2)}, u32[]{:S(2)}) collective-permute-start(bf16[2,2,1,8,4,2560]{5,3,4,1,2,0:T(8,128)(2,1)S(1)} %maximum_select_fusion.3), channel_id=1, source_target_pairs={{0,1},{1,0},{2,3},{3,2},{4,5},{5,4},{6,7},{7,6},{8,9},{9,8},{10,11... | collective-permute-start | bytes 1966088 | tf_op jit(solution)/shard_map/ppermute | solution.py:145
  211.6 0.8 copy-start.7
  212.4 3.9 %copy-start.1 = (bf16[2560,512]{1,0:T(8,128)(2,1)S(1)}, bf16[2560,512]{1,0:T(8,128)(2,1)}, u32[]{:S(2)}) copy-start(bf16[2560,512]{1,0:T(8,128)(2,1)} %param.15) | copy-start | bytes 7864324
Sparse Core Ops, SparseCore 0:
  65.4 12.3 reduce-scatter.1

commit v4 on v3

--- a/solution.py
+++ b/solution.py
@@ -124,14 +124,15 @@
     )
 
 
-def pair_scatter(parts, axis_name):
+def pair_scatter(parts, axis_name, rounded=True):
     n = lax.axis_size(axis_name)
     assert n == 2 and parts.shape[0] == 2
     side = lax.axis_index(axis_name)
     keep = lax.dynamic_index_in_dim(parts, side, 0, keepdims=True)
     send = lax.dynamic_index_in_dim(parts, 1 - side, 0, keepdims=True)
     got = lax.ppermute(send, axis_name, [(0, 1), (1, 0)])
-    return (keep.astype(jnp.float32) + got.astype(jnp.float32)).astype(parts.dtype)
+    total = (keep.astype(jnp.float32) + got.astype(jnp.float32))[0]
+    return total.astype(parts.dtype) if rounded else total
 
 
 def doubling_gather(part, axis_name):
@@ -209,24 +210,42 @@
     )
     step_count = states.shape[1]
     token_count = states.shape[0] * step_count
-    as_float = states.reshape(token_count, -1).astype(jnp.float32)
+    own_states = states.reshape(token_count, -1)
+    side = lax.axis_index("col")
+    swap = [(0, 1), (1, 0)]
+    other_states = lax.ppermute(own_states, "col", swap)
+    as_float = own_states.astype(jnp.float32)
     squares = lax.psum(jnp.sum(as_float * as_float, -1), "row")
-    normed = (as_float * lax.rsqrt(squares / D + EPSILON)[:, None] * norm_gain).astype(
-        jnp.bfloat16
-    )
-    gathered = pair_gather(normed, "col")
+    other_squares = lax.ppermute(squares, "col", swap)
+
+    def rms_norm(rows, sums):
+        scale = lax.rsqrt(sums / D + EPSILON)[:, None]
+        return (rows.astype(jnp.float32) * scale * norm_gain).astype(jnp.bfloat16)
+
+    first = side == 0
+    gathered = jnp.concatenate(
+        [
+            rms_norm(
+                jnp.where(first, own_states, other_states), jnp.where(first, squares, other_squares)
+            ),
+            rms_norm(
+                jnp.where(first, other_states, own_states), jnp.where(first, other_squares, squares)
+            ),
+        ],
+        0,
+    )
     gathered, key_rows, value_rows = lax.optimization_barrier((gathered, key_rows, value_rows))
     parts_out = [
         jnp.dot(gathered, matrix, preferred_element_type=jnp.float32) for matrix in (wq, wk, wv)
     ]
     output_projected = (
-        lax.psum_scatter(
-            jnp.concatenate(parts_out, axis=-1).astype(jnp.bfloat16),
+        pair_scatter(
+            jnp.concatenate(parts_out, axis=-1)
+            .astype(jnp.bfloat16)
+            .reshape(lax.axis_size("row"), token_count, -1),
             "row",
-            scatter_dimension=0,
-            tiled=True,
+            rounded=False,
         )
-        .astype(jnp.float32)
         .reshape(req_count, step_count, -1)
     )
     token_positions = lengths[:, None] + jnp.arange(step_count, dtype=jnp.int32)[None, :]

time: 224 us -> 198 us (0.88)
  waiting for transfers between devices: 63.9 us -> 49.5 us
  between operations: 14.6 us -> 1.24 us
  other arithmetic: 29 us -> 26.4 us
  starting transfers between devices: 16.6 us -> 18.9 us
    reduce_scatter x1 -> x0, waiting for transfers between devices: 9.4 us -> none  [on_device(): lax.psum_scatter(jnp.concatenate(parts_out, axis=-1).astype(jnp.bfloat16)...]
    ppermute x1 -> x2, waiting for transfers between devices: 5.05 us -> 0.01 us  [the longest x1 0.01 us: on_device(): other_states = lax.ppermute(own_states, 'col', swap)]
    another operation x0 -> x1, local copies, waits for them, and re-layouts: none -> 4.79 us  [on_device(): output_projected = pair_scatter(jnp.concatenate(parts_out, axis=-1).astyp...]
    convert_element_type x1 -> x0, local copies, waits for them, and re-layouts: 3.49 us -> none  [on_device(): as_float = states.reshape(token_count, -1).astype(jnp.float32)]
    select_n x1 -> x0, other arithmetic: 2.94 us -> none  [pair_gather(): jnp.where(side == 0, jnp.concatenate([part, other], 0), jnp.concatenate([...]
    ppermute x1 -> x2, waiting for transfers between devices: 4.79 us -> 7.24 us  [pair_scatter(): got = lax.ppermute(send, axis_name, [(0, 1), (1, 0)])]
  transfers between devices with their start and end apart: 12 -> 13, of which waited for: 10 -> 9; matrix products, arithmetic and copies ran while one was open for 21% -> 25% of each run, Pallas kernels for 0% -> 0%
where the time goes in v4:
time: 198 us; the launch traced here: 197 us
  local copies, waits for them, and re-layouts  63.2 us (32%)
  waiting for transfers between devices  49.5 us (25%)
  matrix products  32.6 us (16%)
  other arithmetic  26.4 us (13%)
  starting transfers between devices  18.9 us (10%)
  blocking collectives  4.72 us (2%)
    ppermute x3, waiting for transfers between devices, doubling_gather(): got = lax.ppermute(block, axis_name, pairs)  27.8 us
    ppermute x3, waiting for transfers between devices, seq_merge(): lax.ppermute(send_values.astype(jnp.bfloat16), 'seq', pairs)  13.1 us
    reshape x1, local copies, waits for them, and re-layouts, on_device(): paged_key_cache.reshape(paged_key_cache.shape[0], block_len, heads_kv, HE...  12.2 us
    reshape x1, local copies, waits for them, and re-layouts, on_device(): paged_value_cache.reshape(paged_value_cache.shape[0], block_len, heads_kv...  12.2 us
    dot_general x3, matrix products, on_device(): jnp.dot(gathered, matrix, preferred_element_type=jnp.float32)  8.8 us
    dot_general x1, matrix products, slot_parts(): jnp.einsum('nsagh,nbah->nasgb', slot_queries, key_rows, preferred_element...  7.93 us
    ppermute x2, waiting for transfers between devices, pair_scatter(): got = lax.ppermute(send, axis_name, [(0, 1), (1, 0)])  7.24 us
    ppermute x3, starting transfers between devices, seq_merge(): got_stats = lax.ppermute(send_stats, 'seq', pairs)  6.84 us
  transfers between devices with their start and end apart: 13, of which 9 were waited for; matrix products, arithmetic and copies ran while one was open for 25% of the time, Pallas kernels for 0%

profile of v4, /device:TPU:0, one launch (start us, length us, event | category | flops | bytes accessed | tf_op | source)
XLA Modules:
  0.0 196.5 jit_solution(7173218585345063486)
XLA Ops:
  0.7 3.5 %reshape.893 = bf16[256,2560]{1,0:T(8,128)(2,1)} reshape(bf16[64,4,2560]{2,1,0:T(4,128)(2,1)} %param.11) | data formatting | bytes 2621440 | tf_op jit(solution)/shard_map/reshape | solution.py:213
  4.2 2.9 %collective-permute-start = (bf16[256,2560]{1,0:T(8,128)(2,1)}, bf16[256,2560]{1,0:T(8,128)(2,1)}, u32[]{:S(2)}, u32[]{:S(2)}) collective-permute-start(bf16[256,2560]{1,0:T(8,128)(2,1)} %reshape.893), channel_id=1, source_target_pairs={{0,8},{8,0},{1,9},{9,1},{2,10},{10,2},{3,11},{11,3},{4,12},{12,4},... | collective-permute-start | bytes 3932168 | tf_op jit(solution)/shard_map/ppermute | solution.py:216
  7.1 2.1 %multiply_reduce_fusion = f32[64,4]{1,0:T(8,128)S(1)} fusion(bf16[64,4,2560]{2,1,0:T(4,128)(2,1)} %param.11), kind=kLoop, calls=%fused_computation.16 | loop fusion | flops 1965824 | bytes 1311744 | tf_op jit(solution)/shard_map/reduce_sum | solution.py:218
  9.3 2.5 %psum.7 = f32[256]{0:T(256)S(1)} all-reduce(f32[256]{0:T(256)S(1)} %reduce_sum.30), channel_id=1, replica_groups=mesh['row'=2,'col'=2,'seq'=8] {'row'}, use_global_device_ids=true, to_apply=%region_1.0 | all-reduce | flops 256 | bytes 2048 | tf_op jit(solution)/shard_map/psum | solution.py:218
  11.9 1.1 multiply_cosine_fusion
  13.0 0.8 gather_fusion
  13.8 12.2 %reshape.894 = bf16[50,128,4,128]{3,2,1,0:T(4,128)(2,1)} reshape(bf16[50,128,512]{2,1,0:T(8,128)(2,1)} %param.20) | data formatting | bytes 13107200 | tf_op jit(solution)/shard_map/reshape | solution.py:207
  26.0 12.2 %reshape.895 = bf16[50,128,4,128]{3,2,1,0:T(4,128)(2,1)} reshape(bf16[50,128,512]{2,1,0:T(8,128)(2,1)} %param.21) | data formatting | bytes 13107200 | tf_op jit(solution)/shard_map/reshape | solution.py:208
  38.3 2.7 %multiply_convert_fusion.1 = (bf16[256,2560]{1,0:T(8,128)(2,1)S(1)}, bf16[256,2560]{1,0:T(8,128)(2,1)S(1)}) fusion(f32[2560]{0:T(1024)S(1)} %copy-done.16, f32[256]{0:T(256)S(1)} %get-tuple-element.61, bf16[256,2560]{1,0:T(8,128)(2,1)} %reshape.893, bf16[256,2560]{1,0:T(8,128)(2,1)} %collective-permute-done, pred[]{:T(512)S(6)} %eq.35, ...), kind=kLoop, calls=%fused_computation.15 | loop fusion | flops 6553600 | bytes 5255169 | tf_op jit(solution)/shard_map/convert_element_type | solution.py:223
  41.2 1.5 convolution_convert_fusion.1
  43.0 1.5 convolution_convert_fusion.2
  45.2 0.8 slice-done.2
  46.0 5.8 %convolution_convert_fusion = bf16[512,2048]{1,0:T(8,128)(2,1)S(1)} fusion(bf16[512,2560]{1,0:T(8,128)(2,1)S(1)} %pad_maximum_fusion.1, bf16[2560,2048]{1,0:T(8,128)(2,1)S(1)} %bitcast.162), kind=kOutput, calls=%fused_computation.12 | convolution fusion | flops 5369757696 | bytes 15204352 | tf_op jit(solution)/shard_map/dot_general | solution.py:239
  53.3 2.5 %collective-permute-done.2 = bf16[1,256,3072]{2,1,0:T(8,128)(2,1)S(1)} collective-permute-done((bf16[1,256,3072]{2,1,0:T(8,128)(2,1)S(1)}, bf16[1,256,3072]{2,1,0:T(8,128)(2,1)S(1)}, u32[]{:S(2)}, u32[]{:S(2)}) %collective-permute-start.2) | collective-permute-done | bytes 1572896 | tf_op jit(solution)/shard_map/ppermute | solution.py:133
  55.7 2.2 %convert_add_fusion = f32[1,256,3072]{2,1,0:T(8,128)} fusion(bf16[1,256,3072]{2,1,0:T(8,128)(2,1)S(1)} %collective-permute-done.2, bf16[2,256,3072]{2,1,0:T(8,128)(2,1)S(1)} %pad_maximum_fusion, s32[]{:T(128)S(6)} %select_n.193), kind=kLoop, calls=%fused_computation.11 | loop fusion | flops 2359296 | bytes 6291460 | tf_op jit(solution)/shard_map/add | solution.py:134
  57.9 4.8 %reshape_squeeze.3 = f32[64,4,3072]{2,1,0:T(4,128)} reshape(f32[1,256,3072]{2,1,0:T(8,128)} %convert_add_fusion) | data formatting | bytes 6291456 | tf_op jit(solution)/shard_map/reshape;squeeze | solution.py:249
  62.7 1.8 slice_bitcast_fusion.2
  64.5 1.1 slice_bitcast_fusion
  65.6 3.2 %slice.92 = f32[64,4,2048]{2,1,0:T(4,128)} slice(f32[64,4,3072]{2,1,0:T(4,128)} %reshape_squeeze.3), slice={[0:64], [0:4], [0:2048]} | slice | bytes 4194304 | tf_op jit(solution)/shard_map/slice | solution.py:253
  68.8 2.5 %reshape.936 = f32[64,4,16,128]{3,2,1,0:T(8,128)S(1)} reshape(f32[64,4,2048]{2,1,0:T(4,128)} %slice.92) | data formatting | bytes 4194304 | tf_op jit(solution)/shard_map/reshape | solution.py:253
  71.3 0.7 fusion.76
  72.6 1.4 pad_maximum_fusion.2
  74.6 2.2 %gather_fusion.1 = bf16[50,4,4,4,128]{4,3,1,2,0:T(4,128)(2,1)} fusion(bf16[64,4,4,4,128]{4,3,1,2,0:T(4,128)(2,1)S(1)} %copy.272, s32[1024]{0:T(1024)S(1)} %pad_clamp_fusion), kind=kCustom, calls=%fused_computation.1 | custom fusion | bytes 1638600 | tf_op jit(solution)/shard_map/gather | solution.py:39
  76.8 7.9 %select_reduce_fusion.1 = (f32[50,4,4,4]{3,2,1,0:T(4,128)S(1)}, f32[50,4,4,4,128]{4,3,2,1,0:T(4,128)}) fusion(pred[50,4,128]{2,1,0:T(4,128)(4,1)S(1)} %or_and_fusion, bf16[50,4,4,4,128]{4,3,1,2,0:T(4,128)(2,1)} %gather_fusion.1, bf16[50,128,4,128,1]{3,2,1,0,4:T(4,128)(2,1)} %bitcast.136), kind=kOutput, calls=%fused_computation.23 | convolution fusion | flops 106083200 | bytes 9049600 | tf_op jit(solution)/shard_map/nsagh,nbah->nasgb/dot_general | solution.py:40
  84.7 1.0 select_reduce_fusion
  85.8 1.1 stack.72
  88.1 1.2 fusion.34
  90.0 0.8 fusion.38
  90.8 0.8 copy_dynamic-update-slice_fusion.1
  91.6 3.4 %fusion.16 = f32[50,4,4,4]{3,2,1,0:T(4,128)S(1)} fusion(f32[50,4,4,4,128]{4,3,2,1,0:T(4,128)} %get-tuple-element.66, f32[50,4,4,4]{3,2,1,0:T(4,128)S(1)} %get-tuple-element.65, pred[50,4,128]{2,1,0:T(4,128)(4,1)S(1)} %or_and_fusion), kind=kLoop, calls=%fused_computation.34 | loop fusion | flops 1635200 | bytes 1689600 | tf_op jit(solution)/shard_map/reduce_sum | solution.py:56
  95.0 0.8 gather_fusion.2
  95.8 0.8 fusion.75
  97.7 0.8 constant_dynamic-slice_fusion.2
  98.5 2.0 %collective-permute-start.3 = (f32[2,2,2,1,8,4,4,4]{4,7,6,5,2,1,3,0:T(4,128)}, f32[2,2,2,1,8,4,4,4]{4,7,6,5,2,1,3,0:T(4,128)S(1)}, u32[]{:S(2)}, u32[]{:S(2)}) collective-permute-start(f32[2,2,2,1,8,4,4,4]{4,7,6,5,2,1,3,0:T(4,128)} %constant_dynamic-slice_fusion.2), channel_id=1, source_target_pairs={{0,1},{1,0},{2,3},{3,2},{4,5},{5,4},{6,7},{7,6},{8,9},{9,8},{10,11... | collective-permute-start | bytes 49160 | tf_op jit(solution)/shard_map/ppermute | solution.py:173
  100.6 4.7 %fusion.11 = f32[50,4,4,4,128]{4,3,2,1,0:T(4,128)S(1)} fusion(bf16[50,128,4,128,1]{3,2,1,0,4:T(4,128)(2,1)} %bitcast.135, f32[50,4,4,4,128]{4,3,2,1,0:T(4,128)} %get-tuple-element.66, f32[50,4,4,4]{3,2,1,0:T(4,128)} %bitcast.158, f32[50,4,4,4]{3,2,1,0:T(4,128)S(1)} %get-tuple-element.65, pred[50,4,128]{2,1,0:T(4,128)(4,1)S(1)} %copy-done.15), kind=kOutput, calls=%fused_computation.24 | convolution fusion | flops 106905600 | bytes 9881600 | tf_op jit(solution)/shard_map/nasgb,nbah->nasgh/dot_general | solution.py:57
  105.3 2.2 %fusion.9 = f32[64,4,4,4,128]{4,0,3,2,1:T(8,128)S(1)} fusion(f32[50,4,4,4,128]{4,3,2,1,0:T(4,128)S(1)} %fusion.11, s32[50]{0:T(128)S(1)} %copy-done.17), kind=kOutput, calls=%fused_computation.19 | convolution fusion | flops 314576000 | bytes 3735752 | tf_op jit(solution)/shard_map/rn,nasgh->rasgh/dot_general | solution.py:77
  107.5 1.1 constant_dynamic-slice_fusion.3
  108.7 1.1 copy.252
  110.3 1.1 fusion.31
  111.5 2.0 %collective-permute-start.5 = (f32[2,2,1,1,8,4,4,4]{4,7,6,5,3,2,1,0:T(4,128)S(1)}, f32[2,2,1,1,8,4,4,4]{4,7,6,5,3,2,1,0:T(4,128)S(1)}, u32[]{:S(2)}, u32[]{:S(2)}) collective-permute-start(f32[2,2,1,1,8,4,4,4]{4,7,6,5,3,2,1,0:T(4,128)S(1)} %get-tuple-element.53), channel_id=1, source_target_pairs={{0,2},{1,3},{2,0},{3,1},{4,6},{5,7},{6,4},{7,5},{8,10},{9,11},{10,... | collective-permute-start | bytes 24584 | tf_op jit(solution)/shard_map/ppermute | solution.py:173
  113.5 1.0 fusion.26
  115.4 1.4 collective-permute-done.5
  116.9 2.8 %collective-permute-start.7 = (f32[2,1,1,1,8,4,4,4]{4,7,6,5,3,2,1,0:T(4,128)S(1)}, f32[2,1,1,1,8,4,4,4]{4,7,6,5,3,2,1,0:T(4,128)S(1)}, u32[]{:S(2)}, u32[]{:S(2)}) collective-permute-start(f32[2,1,1,1,8,4,4,4]{4,7,6,5,3,2,1,0:T(4,128)S(1)} %get-tuple-element.57), channel_id=1, source_target_pairs={{0,4},{1,5},{2,6},{3,7},{4,0},{5,1},{6,2},{7,3},{8,12},{9,13},{10,... | collective-permute-start | bytes 12296 | tf_op jit(solution)/shard_map/ppermute | solution.py:173
  119.7 4.3 %collective-permute-done.4 = bf16[2,2,1,8,4,4,4,128]{7,6,5,4,3,2,1,0:T(4,128)(2,1)} collective-permute-done((bf16[2,2,1,8,4,4,4,128]{7,6,5,4,3,2,1,0:T(4,128)(2,1)S(1)}, bf16[2,2,1,8,4,4,4,128]{7,6,5,4,3,2,1,0:T(4,128)(2,1)}, u32[]{:S(2)}, u32[]{:S(2)}) %collective-permute-start.4) | collective-permute-done | bytes 524320 | tf_op jit(solution)/shard_map/ppermute | solution.py:174
  124.0 2.2 %fusion.15 = f32[2,2,1,8,4,4,4,128]{7,6,5,4,3,2,1,0:T(4,128)S(1)} fusion(f32[2,2,1,8,4,4,4,128]{7,3,2,1,0,6,5,4:T(8,128)S(1)} %copy-done.3, bf16[2,2,1,8,4,4,4,128]{7,6,5,4,3,2,1,0:T(4,128)(2,1)} %collective-permute-done.4, f32[2,2,8,4,4,4]{5,4,3,2,1,0:T(4,128)S(1)} %copy.238, f32[2,2,8,4,4,4]{5,4,3,2,1,0:T(4,128)S(1)} %copy.236), kind=kLoop, calls=%fused_computation.33 | loop fusion | flops 1048576 | bytes 2637824 | tf_op jit(solution)/shard_map/add | solution.py:183
  126.4 1.6 collective-permute-start.6
  128.7 5.0 %collective-permute-done.6 = bf16[2,1,1,8,4,4,4,128]{7,6,5,4,3,2,1,0:T(4,128)(2,1)S(1)} collective-permute-done((bf16[2,1,1,8,4,4,4,128]{7,6,5,4,3,2,1,0:T(4,128)(2,1)S(1)}, bf16[2,1,1,8,4,4,4,128]{7,6,5,4,3,2,1,0:T(4,128)(2,1)S(1)}, u32[]{:S(2)}, u32[]{:S(2)}) %collective-permute-start.6) | collective-permute-done | bytes 262176 | tf_op jit(solution)/shard_map/ppermute | solution.py:174
  134.3 2.6 %collective-permute-start.8 = (bf16[1,1,1,8,4,4,4,128]{7,6,5,4,3,2,1,0:T(4,128)(2,1)S(1)}, bf16[1,1,1,8,4,4,4,128]{7,6,5,4,3,2,1,0:T(4,128)(2,1)S(1)}, u32[]{:S(2)}, u32[]{:S(2)}) collective-permute-start(bf16[1,1,1,8,4,4,4,128]{7,6,5,4,3,2,1,0:T(4,128)(2,1)S(1)} %dynamic-slice_convert_fusion.1), channel_id=1, source_target_pairs={{0,4},{1,5},{2,6},{3,7},{4,0},{5,1},{6,2},{7,3},{8,12},{9,13},{10,... | collective-permute-start | bytes 393224 | tf_op jit(solution)/shard_map/ppermute | solution.py:174
  137.9 3.8 %collective-permute-done.8 = bf16[1,1,1,8,4,4,4,128]{7,6,5,4,3,2,1,0:T(4,128)(2,1)S(1)} collective-permute-done((bf16[1,1,1,8,4,4,4,128]{7,6,5,4,3,2,1,0:T(4,128)(2,1)S(1)}, bf16[1,1,1,8,4,4,4,128]{7,6,5,4,3,2,1,0:T(4,128)(2,1)S(1)}, u32[]{:S(2)}, u32[]{:S(2)}) %collective-permute-start.8) | collective-permute-done | bytes 131104 | tf_op jit(solution)/shard_map/ppermute | solution.py:174
  141.7 1.6 fusion.36
  143.5 2.3 %all_gather.4 = bf16[2,8,4,2048]{3,1,2,0:T(8,128)(2,1)S(1)} all-gather(bf16[1,8,4,2048]{3,1,2,0:T(8,128)(2,1)S(1)} %convert_element_type.126), channel_id=1, replica_groups=mesh['row'=2,'col'=2,'seq'=8] {'row'}, dimensions={0}, use_global_device_ids=true | all-gather | bytes 393216 | tf_op jit(solution)/shard_map/all_gather | solution.py:294
  145.7 5.9 %fusion.6 = bf16[2,8,4,2560]{3,1,2,0:T(8,128)(2,1)S(1)} fusion(bf16[2,8,4,2048]{3,1,2,0:T(8,128)(2,1)S(1)} %all_gather.4, bf16[2048,2560]{1,0:T(8,128)(2,1)} %param.16), kind=kOutput, calls=%fused_computation.9 | convolution fusion | flops 671252480 | bytes 11075584 | tf_op jit(solution)/shard_map/dot_general | solution.py:296
  151.6 1.6 collective-permute-start.9
  153.2 4.8 %collective-permute-done.9 = bf16[1,8,4,2560]{3,1,2,0:T(8,128)(2,1)S(1)} collective-permute-done((bf16[1,8,4,2560]{3,1,2,0:T(8,128)(2,1)S(1)}, bf16[1,8,4,2560]{3,1,2,0:T(8,128)(2,1)S(1)}, u32[]{:S(2)}, u32[]{:S(2)}) %collective-permute-start.9) | collective-permute-done | bytes 163872 | tf_op jit(solution)/shard_map/ppermute | solution.py:133
  158.0 1.3 collective-permute-start.10
  159.3 8.6 %collective-permute-done.10 = bf16[1,8,4,2560]{3,1,2,0:T(8,128)(2,1)S(1)} collective-permute-done((bf16[1,8,4,2560]{3,1,2,0:T(8,128)(2,1)S(1)}, bf16[1,8,4,2560]{3,1,2,0:T(8,128)(2,1)S(1)}, u32[]{:S(2)}, u32[]{:S(2)}) %collective-permute-start.10) | collective-permute-done | bytes 163872 | tf_op jit(solution)/shard_map/ppermute | solution.py:146
  168.1 8.7 %collective-permute-done.11 = bf16[2,1,8,4,2560]{4,2,3,1,0:T(8,128)(2,1)S(1)} collective-permute-done((bf16[2,1,8,4,2560]{4,2,3,1,0:T(8,128)(2,1)S(1)}, bf16[2,1,8,4,2560]{4,2,3,1,0:T(8,128)(2,1)S(1)}, u32[]{:S(2)}, u32[]{:S(2)}) %collective-permute-start.11) | collective-permute-done | bytes 327712 | tf_op jit(solution)/shard_map/ppermute | solution.py:146
  176.8 1.5 collective-permute-start.12
  178.3 1.8 slice.146
  180.1 1.1 fusion.87
  181.3 10.5 %collective-permute-done.12 = bf16[2,2,1,8,4,2560]{5,3,4,1,2,0:T(8,128)(2,1)S(1)} collective-permute-done((bf16[2,2,1,8,4,2560]{5,3,4,1,2,0:T(8,128)(2,1)S(1)}, bf16[2,2,1,8,4,2560]{5,3,4,1,2,0:T(8,128)(2,1)S(1)}, u32[]{:S(2)}, u32[]{:S(2)}) %collective-permute-start.12) | collective-permute-done | bytes 655392 | tf_op jit(solution)/shard_map/ppermute | solution.py:146
  191.8 0.8 copy-done.7
  192.7 1.7 fusion.14
  194.5 2.1 %copy.260 = bf16[64,4,2560]{2,1,0:T(4,128)(2,1)} copy(bf16[64,4,2560]{2,0,1:T(8,128)(2,1)S(1)} %bitcast.139) | data formatting | bytes 2621440
  (112 shorter events, 11.5 us)
Async XLA Ops:
  0.6 40.5 %copy-start = (bf16[2560,512]{1,0:T(8,128)(2,1)S(1)}, bf16[2560,512]{1,0:T(8,128)(2,1)}, u32[]{:S(2)}) copy-start(bf16[2560,512]{1,0:T(8,128)(2,1)} %param.15) | copy-start | bytes 7864324
  0.6 11.2 %copy-start.17 = (s32[50]{0:T(128)S(1)}, s32[50]{0:T(128)}, u32[]{:S(2)}) copy-start(s32[50]{0:T(128)} %param.18) | copy-start | bytes 604
  0.7 11.2 %copy-start.2 = (s32[64]{0:T(128)S(1)}, s32[64]{0:T(128)}, u32[]{:S(2)}) copy-start(s32[64]{0:T(128)} %param.17) | copy-start | bytes 772
  4.2 34.0 %collective-permute-start = (bf16[256,2560]{1,0:T(8,128)(2,1)}, bf16[256,2560]{1,0:T(8,128)(2,1)}, u32[]{:S(2)}, u32[]{:S(2)}) collective-permute-start(bf16[256,2560]{1,0:T(8,128)(2,1)} %reshape.893), channel_id=1, source_target_pairs={{0,8},{8,0},{1,9},{9,1},{2,10},{10,2},{3,11},{11,3},{4,12},{12,4},... | collective-permute-start | bytes 3932168 | tf_op jit(solution)/shard_map/ppermute | solution.py:216
  11.8 26.4 %collective-permute-start.1 = (f32[256]{0:T(256)S(1)}, f32[256]{0:T(256)S(1)}, u32[]{:S(2)}, u32[]{:S(2)}) collective-permute-start(f32[256]{0:T(256)S(1)} %psum.7), channel_id=1, source_target_pairs={{0,8},{8,0},{1,9},{9,1},{2,10},{10,2},{3,11},{11,3},{4,12},{12,4},... | collective-permute-start | bytes 3080 | tf_op jit(solution)/shard_map/ppermute | solution.py:219
  26.0 12.2 %copy-start.16 = (f32[2560]{0:T(1024)S(1)}, f32[2560]{0:T(1024)}, u32[]{:S(2)}) copy-start(f32[2560]{0:T(1024)} %param.12) | copy-start | bytes 30724
  40.9 3.6 %slice-start = ((s8[10485760]{0:T(1024)(128)(4,1)}), s8[4194304]{0:T(1024)(128)(4,1)S(1)}, s32[]{:S(2)}) async-start(s8[10485760]{0:T(1024)(128)(4,1)} %bitcast.161), calls=%async_computation | async-start | bytes 8388608
  41.1 1.9 copy-start.18
  41.2 4.0 %slice-start.1 = ((s8[10485760]{0:T(1024)(128)(4,1)}), s8[4194304]{0:T(1024)(128)(4,1)S(1)}, s32[]{:S(2)}) async-start(s8[10485760]{0:T(1024)(128)(4,1)} %bitcast.161), calls=%async_computation.1 | async-start | bytes 8388608
  43.0 3.0 %slice-start.2 = ((s8[10485760]{0:T(1024)(128)(4,1)}), s8[2097152]{0:T(1024)(128)(4,1)S(1)}, s32[]{:S(2)}) async-start(s8[10485760]{0:T(1024)(128)(4,1)} %bitcast.161), calls=%async_computation.2 | async-start | bytes 4194304
  52.1 0.7 copy-start.19
  52.3 3.5 %collective-permute-start.2 = (bf16[1,256,3072]{2,1,0:T(8,128)(2,1)S(1)}, bf16[1,256,3072]{2,1,0:T(8,128)(2,1)S(1)}, u32[]{:S(2)}, u32[]{:S(2)}) collective-permute-start(bf16[1,256,3072]{2,1,0:T(8,128)(2,1)S(1)} %constant_dynamic-slice_fusion.4), channel_id=1, source_target_pairs={{0,16},{16,0},{1,17},{17,1},{2,18},{18,2},{3,19},{19,3},{4,20},{20... | collective-permute-start | bytes 4718600 | tf_op jit(solution)/shard_map/ppermute | solution.py:133
  53.2 38.4 %copy-start.14 = (pred[50,4,128]{2,1,0:T(4,128)(4,1)}, pred[50,4,128]{2,1,0:T(4,128)(4,1)S(1)}, u32[]{:S(2)}) copy-start(pred[50,4,128]{2,1,0:T(4,128)(4,1)S(1)} %or_and_fusion) | copy-start | bytes 76804
  87.7 3.1 %copy-start.6 = (f32[1,2,2,2,8,4,4,4]{4,3,2,1,7,6,5,0:T(2,128)S(1)}, f32[1,2,2,2,8,4,4,4]{4,3,2,1,7,6,5,0:T(2,128)}, u32[]{:S(2)}) copy-start(f32[1,2,2,2,8,4,4,4]{4,3,2,1,7,6,5,0:T(2,128)} %stack.72) | copy-start | bytes 49156
  90.0 1.6 copy-start.10
  95.8 1.8 copy-start.4
  95.8 4.7 %copy-start.15 = (pred[50,4,128]{2,1,0:T(4,128)(4,1)S(1)}, pred[50,4,128]{2,1,0:T(4,128)(4,1)}, u32[]{:S(2)}) copy-start(pred[50,4,128]{2,1,0:T(4,128)(4,1)} %copy-done.14) | copy-start | bytes 76804
  97.7 2.9 %copy-start.5 = (f32[2,2,2,2,8,4,4,4]{4,7,6,5,2,1,3,0:T(4,128)}, f32[2,2,2,2,8,4,4,4]{4,7,6,5,2,1,3,0:T(4,128)S(1)}, u32[]{:S(2)}) copy-start(f32[2,2,2,2,8,4,4,4]{4,7,6,5,2,1,3,0:T(4,128)S(1)} %copy_dynamic-update-slice_fusion) | copy-start | bytes 98308
  98.5 11.8 %collective-permute-start.3 = (f32[2,2,2,1,8,4,4,4]{4,7,6,5,2,1,3,0:T(4,128)}, f32[2,2,2,1,8,4,4,4]{4,7,6,5,2,1,3,0:T(4,128)S(1)}, u32[]{:S(2)}, u32[]{:S(2)}) collective-permute-start(f32[2,2,2,1,8,4,4,4]{4,7,6,5,2,1,3,0:T(4,128)} %constant_dynamic-slice_fusion.2), channel_id=1, source_target_pairs={{0,1},{1,0},{2,3},{3,2},{4,5},{5,4},{6,7},{7,6},{8,9},{9,8},{10,11... | collective-permute-start | bytes 49160 | tf_op jit(solution)/shard_map/ppermute | solution.py:173
  109.9 14.1 %copy-start.3 = (f32[2,2,1,8,4,4,4,128]{7,3,2,1,0,6,5,4:T(8,128)S(1)}, f32[2,2,1,8,4,4,4,128]{7,3,2,1,0,6,5,4:T(8,128)}, u32[]{:S(2)}) copy-start(f32[2,2,1,8,4,4,4,128]{7,3,2,1,0,6,5,4:T(8,128)} %constant_dynamic-slice_fusion.3) | copy-start | bytes 3145732
  110.2 13.9 %collective-permute-start.4 = (bf16[2,2,1,8,4,4,4,128]{7,6,5,4,3,2,1,0:T(4,128)(2,1)S(1)}, bf16[2,2,1,8,4,4,4,128]{7,6,5,4,3,2,1,0:T(4,128)(2,1)}, u32[]{:S(2)}, u32[]{:S(2)}) collective-permute-start(bf16[2,2,1,8,4,4,4,128]{7,6,5,4,3,2,1,0:T(4,128)(2,1)S(1)} %copy.301), channel_id=1, source_target_pairs={{0,1},{1,0},{2,3},{3,2},{4,5},{5,4},{6,7},{7,6},{8,9},{9,8},{10,11... | collective-permute-start | bytes 1572872 | tf_op jit(solution)/shard_map/ppermute | solution.py:174
  111.5 5.3 %collective-permute-start.5 = (f32[2,2,1,1,8,4,4,4]{4,7,6,5,3,2,1,0:T(4,128)S(1)}, f32[2,2,1,1,8,4,4,4]{4,7,6,5,3,2,1,0:T(4,128)S(1)}, u32[]{:S(2)}, u32[]{:S(2)}) collective-permute-start(f32[2,2,1,1,8,4,4,4]{4,7,6,5,3,2,1,0:T(4,128)S(1)} %get-tuple-element.53), channel_id=1, source_target_pairs={{0,2},{1,3},{2,0},{3,1},{4,6},{5,7},{6,4},{7,5},{8,10},{9,11},{10,... | collective-permute-start | bytes 24584 | tf_op jit(solution)/shard_map/ppermute | solution.py:173
  116.8 2.9 %copy-start.8 = (f32[2,2,1,1,8,4,4,4]{4,7,6,5,3,2,1,0:T(4,128)}, f32[2,2,1,1,8,4,4,4]{4,7,6,5,3,2,1,0:T(4,128)S(1)}, u32[]{:S(2)}) copy-start(f32[2,2,1,1,8,4,4,4]{4,7,6,5,3,2,1,0:T(4,128)S(1)} %collective-permute-done.5) | copy-start | bytes 24580
  116.9 11.7 %collective-permute-start.7 = (f32[2,1,1,1,8,4,4,4]{4,7,6,5,3,2,1,0:T(4,128)S(1)}, f32[2,1,1,1,8,4,4,4]{4,7,6,5,3,2,1,0:T(4,128)S(1)}, u32[]{:S(2)}, u32[]{:S(2)}) collective-permute-start(f32[2,1,1,1,8,4,4,4]{4,7,6,5,3,2,1,0:T(4,128)S(1)} %get-tuple-element.57), channel_id=1, source_target_pairs={{0,4},{1,5},{2,6},{3,7},{4,0},{5,1},{6,2},{7,3},{8,12},{9,13},{10,... | collective-permute-start | bytes 12296 | tf_op jit(solution)/shard_map/ppermute | solution.py:173
  124.0 4.0 %copy-start.9 = (f32[2,2,1,1,8,4,4,4]{4,7,6,5,3,2,1,0:T(4,128)S(1)}, f32[2,2,1,1,8,4,4,4]{4,7,6,5,3,2,1,0:T(4,128)}, u32[]{:S(2)}) copy-start(f32[2,2,1,1,8,4,4,4]{4,7,6,5,3,2,1,0:T(4,128)} %copy-done.8) | copy-start | bytes 24580
  126.3 10.7 %copy-start.11 = (f32[8,4,4,4]{0,3,2,1:T(4,128)S(1)}, f32[8,4,4,4]{0,3,2,1:T(4,128)}, u32[]{:S(2)}) copy-start(f32[8,4,4,4]{0,3,2,1:T(4,128)} %copy-done.10) | copy-start | bytes 6148
  126.3 10.7 %copy-start.13 = (f32[8,4,4,4]{0,3,2,1:T(4,128)S(1)}, f32[8,4,4,4]{0,3,2,1:T(4,128)}, u32[]{:S(2)}) copy-start(f32[8,4,4,4]{0,3,2,1:T(4,128)} %get-tuple-element.55) | copy-start | bytes 6148
  126.3 15.4 %copy-start.12 = (bf16[8,4,4,4,4]{4,3,2,1,0:T(4,128)(2,1)S(1)}, bf16[8,4,4,4,4]{4,3,2,1,0:T(4,128)(2,1)}, u32[]{:S(2)}) copy-start(bf16[8,4,4,4,4]{4,3,2,1,0:T(4,128)(2,1)} %copy.252) | copy-start | bytes 12292
  126.4 7.3 %collective-permute-start.6 = (bf16[2,1,1,8,4,4,4,128]{7,6,5,4,3,2,1,0:T(4,128)(2,1)S(1)}, bf16[2,1,1,8,4,4,4,128]{7,6,5,4,3,2,1,0:T(4,128)(2,1)S(1)}, u32[]{:S(2)}, u32[]{:S(2)}) collective-permute-start(bf16[2,1,1,8,4,4,4,128]{7,6,5,4,3,2,1,0:T(4,128)(2,1)S(1)} %dynamic-slice_convert_fusion), channel_id=1, source_target_pairs={{0,2},{1,3},{2,0},{3,1},{4,6},{5,7},{6,4},{7,5},{8,10},{9,11},{10,... | collective-permute-start | bytes 786440 | tf_op jit(solution)/shard_map/ppermute | solution.py:174
  134.3 7.3 %collective-permute-start.8 = (bf16[1,1,1,8,4,4,4,128]{7,6,5,4,3,2,1,0:T(4,128)(2,1)S(1)}, bf16[1,1,1,8,4,4,4,128]{7,6,5,4,3,2,1,0:T(4,128)(2,1)S(1)}, u32[]{:S(2)}, u32[]{:S(2)}) collective-permute-start(bf16[1,1,1,8,4,4,4,128]{7,6,5,4,3,2,1,0:T(4,128)(2,1)S(1)} %dynamic-slice_convert_fusion.1), channel_id=1, source_target_pairs={{0,4},{1,5},{2,6},{3,7},{4,0},{5,1},{6,2},{7,3},{8,12},{9,13},{10,... | collective-permute-start | bytes 393224 | tf_op jit(solution)/shard_map/ppermute | solution.py:174
  151.6 6.3 %collective-permute-start.9 = (bf16[1,8,4,2560]{3,1,2,0:T(8,128)(2,1)S(1)}, bf16[1,8,4,2560]{3,1,2,0:T(8,128)(2,1)S(1)}, u32[]{:S(2)}, u32[]{:S(2)}) collective-permute-start(bf16[1,8,4,2560]{3,1,2,0:T(8,128)(2,1)S(1)} %constant_dynamic-slice_fusion), channel_id=1, source_target_pairs={{0,8},{8,0},{1,9},{9,1},{2,10},{10,2},{3,11},{11,3},{4,12},{12,4},... | collective-permute-start | bytes 491528 | tf_op jit(solution)/shard_map/ppermute | solution.py:133
  158.0 9.9 %collective-permute-start.10 = (bf16[1,8,4,2560]{3,1,2,0:T(8,128)(2,1)S(1)}, bf16[1,8,4,2560]{3,1,2,0:T(8,128)(2,1)S(1)}, u32[]{:S(2)}, u32[]{:S(2)}) collective-permute-start(bf16[1,8,4,2560]{3,1,2,0:T(8,128)(2,1)S(1)} %add_convert_fusion.1), channel_id=1, source_target_pairs={{0,4},{1,5},{2,6},{3,7},{4,0},{5,1},{6,2},{7,3},{8,12},{9,13},{10,... | collective-permute-start | bytes 491528 | tf_op jit(solution)/shard_map/ppermute | solution.py:146
  167.9 8.8 %collective-permute-start.11 = (bf16[2,1,8,4,2560]{4,2,3,1,0:T(8,128)(2,1)S(1)}, bf16[2,1,8,4,2560]{4,2,3,1,0:T(8,128)(2,1)S(1)}, u32[]{:S(2)}, u32[]{:S(2)}) collective-permute-start(bf16[2,1,8,4,2560]{4,2,3,1,0:T(8,128)(2,1)S(1)} %maximum_select_fusion.4), channel_id=1, source_target_pairs={{0,2},{1,3},{2,0},{3,1},{4,6},{5,7},{6,4},{7,5},{8,10},{9,11},{10,... | collective-permute-start | bytes 983048 | tf_op jit(solution)/shard_map/ppermute | solution.py:146
  176.8 15.0 %collective-permute-start.12 = (bf16[2,2,1,8,4,2560]{5,3,4,1,2,0:T(8,128)(2,1)S(1)}, bf16[2,2,1,8,4,2560]{5,3,4,1,2,0:T(8,128)(2,1)S(1)}, u32[]{:S(2)}, u32[]{:S(2)}) collective-permute-start(bf16[2,2,1,8,4,2560]{5,3,4,1,2,0:T(8,128)(2,1)S(1)} %maximum_select_fusion.2), channel_id=1, source_target_pairs={{0,1},{1,0},{2,3},{3,2},{4,5},{5,4},{6,7},{7,6},{8,9},{9,8},{10,11... | collective-permute-start | bytes 1966088 | tf_op jit(solution)/shard_map/ppermute | solution.py:146
  191.8 0.8 copy-start.7
  192.7 3.9 %copy-start.1 = (bf16[2560,512]{1,0:T(8,128)(2,1)S(1)}, bf16[2560,512]{1,0:T(8,128)(2,1)}, u32[]{:S(2)}) copy-start(bf16[2560,512]{1,0:T(8,128)(2,1)} %param.15) | copy-start | bytes 7864324

commit v5 on v4

--- a/solution.py
+++ b/solution.py
@@ -1,8 +1,11 @@
 import math
+from functools import partial
 
 import jax
 import jax.numpy as jnp
 from jax import lax
+from jax.experimental import pallas as pl
+from jax.experimental.pallas import tpu as pltpu
 from jax.sharding import PartitionSpec as P
 
 D = 5120
@@ -110,6 +113,81 @@
     running_totals = earlier[1] * first_factor + later[1] * second_factor
     weighted_values = earlier[2] * first_factor[..., None] + later[2] * second_factor[..., None]
     return (running_peak, running_totals, weighted_values)
+
+
+def slot_kernel(len_ref, blk_ref, q_ref, k_ref, v_ref, peak_ref, tot_ref, acc_ref, *, ns, heads, qpk):
+    base = pl.program_id(0) * ns
+    rows = q_ref.shape[1]
+    width = k_ref.shape[1]
+    head = k_ref.shape[2] // heads
+    row = lax.broadcasted_iota(jnp.int32, (rows, width), 0)
+    col = lax.broadcasted_iota(jnp.int32, (rows, width), 1)
+    head_of = (row // qpk) % heads
+    step_of = row // (heads * qpk)
+
+    def body(i, carry):
+        length = len_ref[base + i]
+        key_pos = blk_ref[base + i] * width + col
+        query_pos = length + step_of
+        visible = (key_pos < length) & ((key_pos < SINK) | (key_pos > query_pos - WINDOW))
+        q = q_ref[i]
+        k = k_ref[i]
+        v = v_ref[i]
+        scores = jnp.zeros((rows, width), jnp.float32)
+        for a in range(heads):
+            part = lax.dot_general(
+                q,
+                k[:, a * head : (a + 1) * head],
+                (((1,), (1,)), ((), ())),
+                preferred_element_type=jnp.float32,
+            )
+            scores = jnp.where(head_of == a, part, scores)
+        scores = scores * (1.0 / math.sqrt(HEAD_SIZE))
+        peak = jnp.max(jnp.where(visible, scores, NEGATIVE_FILL), axis=1, keepdims=True)
+        weights = jnp.where(visible, jnp.exp(scores - peak), 0.0)
+        total = jnp.sum(weights, axis=1, keepdims=True)
+        rounded = weights.astype(jnp.bfloat16)
+        acc = jnp.zeros((rows, head), jnp.float32)
+        for a in range(heads):
+            part = jnp.dot(
+                rounded, v[:, a * head : (a + 1) * head], preferred_element_type=jnp.float32
+            )
+            acc = jnp.where(head_of[:, :head] == a, part, acc)
+        peak_ref[i] = peak
+        tot_ref[i] = total
+        acc_ref[i] = acc
+        return carry
+
+    lax.fori_loop(0, ns, body, 0)
+
+
+def slot_attention(slot_queries, slot_lengths, block_numbers, keys, values, heads, qpk):
+    n_slots, rows, head = slot_queries.shape
+    width = keys.shape[1]
+    ns = max(d for d in range(1, 11) if n_slots % d == 0)
+    grid_spec = pltpu.PrefetchScalarGridSpec(
+        num_scalar_prefetch=2,
+        grid=(n_slots // ns,),
+        in_specs=[
+            pl.BlockSpec((ns, rows, head), lambda n, lr, br: (n, 0, 0)),
+            pl.BlockSpec((ns, width, keys.shape[2]), lambda n, lr, br: (n, 0, 0)),
+            pl.BlockSpec((ns, width, values.shape[2]), lambda n, lr, br: (n, 0, 0)),
+        ],
+        out_specs=[
+            pl.BlockSpec((ns, rows, 1), lambda n, lr, br: (n, 0, 0)),
+            pl.BlockSpec((ns, rows, 1), lambda n, lr, br: (n, 0, 0)),
+            pl.BlockSpec((ns, rows, head), lambda n, lr, br: (n, 0, 0)),
+        ],
+    )
+    return pl.pallas_call(
+        partial(slot_kernel, ns=ns, heads=heads, qpk=qpk),
+        grid_spec=grid_spec,
+        out_shape=[
+            jax.ShapeDtypeStruct((n_slots, rows, 1), jnp.float32),
+            jax.ShapeDtypeStruct((n_slots, rows, 1), jnp.float32),
+            jax.ShapeDtypeStruct((n_slots, rows, head), jnp.float32),
+        ],
+    )(slot_lengths, block_numbers, slot_queries, keys, values)
 
 
 def pair_gather(part, axis_name):
@@ -234,7 +312,6 @@
         ],
         0,
     )
-    gathered, key_rows, value_rows = lax.optimization_barrier((gathered, key_rows, value_rows))
     parts_out = [
         jnp.dot(gathered, matrix, preferred_element_type=jnp.float32) for matrix in (wq, wk, wv)
     ]
@@ -265,10 +342,31 @@
         .reshape(req_count, step_count, heads_kv, HEAD_SIZE)
         .astype(jnp.bfloat16)
     )
-    local_peak, held = slot_parts(
-        query_rows, lengths, slot_request, slot_block_number, key_rows, value_rows
-    )
-    local_totals, local_values = pool_sums(held, local_peak)
+    picked = jnp.minimum(slot_request, req_count - 1)
+    in_use = slot_request < req_count
+    slot_lengths = jnp.where(in_use, lengths[picked], 0)
+    flat_queries = query_rows.reshape(req_count, -1, HEAD_SIZE)
+    slot_peak, slot_total, slot_acc = slot_attention(
+        flat_queries[picked],
+        slot_lengths,
+        slot_block_number,
+        paged_key_cache,
+        paged_value_cache,
+        heads_kv,
+        QUERY_PER_KEY,
+    )
+    slot_peak = slot_peak[..., 0]
+    slot_total = slot_total[..., 0]
+    member = slot_request[None, :] == jnp.arange(req_count, dtype=jnp.int32)[:, None]
+    local_peak = jnp.max(jnp.where(member[:, :, None], slot_peak[None], NEGATIVE_FILL), 1)
+    factor = jnp.exp(slot_peak - local_peak[picked])
+    as_member = member.astype(jnp.float32)
+    local_totals = jnp.einsum(
+        "rn,nj->rj", as_member, slot_total * factor, precision=lax.Precision.HIGHEST
+    )
+    local_values = jnp.einsum(
+        "rn,njh->rjh", as_member, slot_acc * factor[..., None], precision=lax.Precision.HIGHEST
+    )
     n_seq = lax.axis_size("seq")
     per = req_count // n_seq
     seq_index = lax.axis_index("seq")
@@ -276,6 +374,10 @@
     running_peak, running_totals, weighted_values = seq_merge(
         local_peak, local_totals, local_values, n_seq, seq_index
     )
+    order = (per, step_count, heads_kv, QUERY_PER_KEY)
+    running_peak = running_peak.reshape(order).transpose(0, 2, 1, 3)
+    running_totals = running_totals.reshape(order).transpose(0, 2, 1, 3)
+    weighted_values = weighted_values.reshape(order + (HEAD_SIZE,)).transpose(0, 2, 1, 3, 4)
     own_queries = lax.dynamic_slice_in_dim(query_rows, mine, per, 0)
     fresh = fresh_part(
         own_queries,

time: 198 us -> 205 us (1.035)
  waiting for transfers between devices: 49.5 us -> 76.5 us
  local copies, waits for them, and re-layouts: 63.2 us -> 36.4 us
  Pallas kernels: 0 us -> 24.9 us
  matrix products: 32.6 us -> 18.9 us
    pallas_call x0 -> x1, Pallas kernels: none -> 24.9 us  [slot_attention(): pl.pallas_call(partial(slot_kernel, ns=ns, heads=heads, qpk=qpk), grid_sp...]
    ppermute x1, waiting for transfers between devices: 0.01 us -> 24.4 us  [on_device(): other_squares = lax.ppermute(squares, 'col', swap)]
    reshape x2 -> x0, local copies, waits for them, and re-layouts: 24.4 us -> none  [the longest x1 12.2 us: on_device(): paged_key_cache.reshape(paged_key_cache.shape[0], block_len, heads_kv, HE...]
    dot_general x3 -> x2, matrix products: 14.8 us -> 2.37 us  [the longest x1 2.17 us: on_device(): jnp.einsum('rn,njh->rjh', as_member, slot_acc * factor[..., None], precis...]
    reduce_sum x1, other arithmetic: 3.4 us -> 0.19 us  [fresh_part(): running_totals = jnp.sum(weights, -1)]
    ppermute x3, waiting for transfers between devices: 13.1 us -> 15.8 us  [seq_merge(): lax.ppermute(send_values.astype(jnp.bfloat16), 'seq', pairs)]
    mul x2, other arithmetic: 0.85 us -> 3.47 us  [the longest x1 2.97 us: on_device(): slot_total * factor]
    gather x3 -> x4, local copies, waits for them, and re-layouts: 3.74 us -> 4.71 us  [the longest x2 2.37 us: on_device(): factor = jnp.exp(slot_peak - local_peak[picked])]
  transfers between devices with their start and end apart: 13 -> 13, of which waited for: 9 -> 10; matrix products, arithmetic and copies ran while one was open for 25% -> 7% of each run, Pallas kernels for 0% -> 0%
where the time goes in v5:
time: 205 us
  waiting for transfers between devices  76.5 us (37%)
  local copies, waits for them, and re-layouts  36.4 us (18%)
  other arithmetic  25.1 us (12%)
  Pallas kernels  24.9 us (12%)
  matrix products  18.9 us (9%)
  starting transfers between devices  17.5 us (9%)
  blocking collectives  4.46 us (2%)
    ppermute x3, waiting for transfers between devices, doubling_gather(): got = lax.ppermute(block, axis_name, pairs)  28.8 us
    pallas_call x1, Pallas kernels, slot_attention(): pl.pallas_call(partial(slot_kernel, ns=ns, heads=heads, qpk=qpk), grid_sp...  24.9 us
    ppermute x1, waiting for transfers between devices, on_device(): other_squares = lax.ppermute(squares, 'col', swap)  24.4 us
    ppermute x3, waiting for transfers between devices, seq_merge(): lax.ppermute(send_values.astype(jnp.bfloat16), 'seq', pairs)  15.8 us
    dot_general x3, matrix products, on_device(): jnp.dot(gathered, matrix, preferred_element_type=jnp.float32)  8.8 us
    ppermute x3, starting transfers between devices, seq_merge(): got_stats = lax.ppermute(send_stats, 'seq', pairs)  6.64 us
    unnamed x28, local copies, waits for them, and re-layouts  6.38 us
    dot_general x1, matrix products, on_device(): jnp.dot(piece_rows.reshape(n_row * per * step_count, -1), wo, preferred_e...  5.87 us
  transfers between devices with their start and end apart: 13, of which 10 were waited for; matrix products, arithmetic and copies ran while one was open for 7% of the time, Pallas kernels for 0%

profile of v5, /device:TPU:0, one launch (start us, length us, event | category | flops | bytes accessed | tf_op | source)
XLA Modules:
  0.0 204.8 jit_solution(1681539615259679685)
XLA Ops:
  0.7 3.5 %reshape.769 = bf16[256,2560]{1,0:T(8,128)(2,1)} reshape(bf16[64,4,2560]{2,1,0:T(4,128)(2,1)} %param.11) | data formatting | bytes 2621440 | tf_op jit(solution)/shard_map/reshape | solution.py:291
  4.2 2.9 %collective-permute-start = (bf16[256,2560]{1,0:T(8,128)(2,1)}, bf16[256,2560]{1,0:T(8,128)(2,1)}, u32[]{:S(2)}, u32[]{:S(2)}) collective-permute-start(bf16[256,2560]{1,0:T(8,128)(2,1)} %reshape.769), channel_id=1, source_target_pairs={{0,8},{8,0},{1,9},{9,1},{2,10},{10,2},{3,11},{11,3},{4,12},{12,4},... | collective-permute-start | bytes 3932168 | tf_op jit(solution)/shard_map/ppermute | solution.py:294
  7.1 2.1 %multiply_reduce_fusion = f32[64,4]{1,0:T(8,128)S(1)} fusion(bf16[64,4,2560]{2,1,0:T(4,128)(2,1)} %param.11), kind=kLoop, calls=%fused_computation.12 | loop fusion | flops 1965824 | bytes 1311744 | tf_op jit(solution)/shard_map/reduce_sum | solution.py:296
  9.3 2.5 %psum.7 = f32[256]{0:T(256)S(1)} all-reduce(f32[256]{0:T(256)S(1)} %reduce_sum.23), channel_id=1, replica_groups=mesh['row'=2,'col'=2,'seq'=8] {'row'}, use_global_device_ids=true, to_apply=%region_1.0 | all-reduce | flops 256 | bytes 2048 | tf_op jit(solution)/shard_map/psum | solution.py:296
  11.8 24.4 %collective-permute-done.1 = f32[256]{0:T(256)S(1)} collective-permute-done((f32[256]{0:T(256)S(1)}, f32[256]{0:T(256)S(1)}, u32[]{:S(2)}, u32[]{:S(2)}) %collective-permute-start.1) | collective-permute-done | bytes 1056 | tf_op jit(solution)/shard_map/ppermute | solution.py:297
  36.3 2.8 %multiply_convert_fusion.1 = (bf16[256,2560]{1,0:T(8,128)(2,1)S(1)}, bf16[256,2560]{1,0:T(8,128)(2,1)S(1)}) fusion(f32[2560]{0:T(1024)S(1)} %copy-done.7, f32[256]{0:T(256)S(1)} %get-tuple-element.61, bf16[256,2560]{1,0:T(8,128)(2,1)} %reshape.769, bf16[256,2560]{1,0:T(8,128)(2,1)} %collective-permute-done, pred[]{:T(512)S(6)} %eq.72, ...), kind=kLoop, calls=%fused_computation.11 | loop fusion | flops 6553600 | bytes 5255169 | tf_op jit(solution)/shard_map/convert_element_type | solution.py:301
  39.1 1.5 convolution_convert_fusion.2
  40.7 1.5 convolution_convert_fusion.1
  42.2 0.4 slice-done.1
  42.6 0.8 slice-done.2
  43.4 5.8 %convolution_convert_fusion = bf16[512,2048]{1,0:T(8,128)(2,1)S(1)} fusion(bf16[2560,2048]{1,0:T(8,128)(2,1)S(1)} %bitcast.178, bf16[256,2560]{1,0:T(8,128)(2,1)S(1)} %get-tuple-element.38, bf16[256,2560]{1,0:T(8,128)(2,1)S(1)} %get-tuple-element.37), kind=kOutput, calls=%fused_computation.8 | convolution fusion | flops 5375000576 | bytes 15204352 | tf_op jit(solution)/shard_map/dot_general | solution.py:316
  49.5 1.6 copy-done.3
  51.1 1.3 constant_dynamic-slice_fusion.3
  52.4 0.8 gather_fusion
  53.3 1.1 multiply_cosine_fusion
  54.5 0.5 compare_select_fusion.1.len_ref
  55.1 1.0 collective-permute-done.2
  56.0 3.6 %convert_add_fusion = f32[1,256,3072]{2,1,0:T(8,128)} fusion(bf16[1,256,3072]{2,1,0:T(8,128)(2,1)S(1)} %collective-permute-done.2, bf16[2,256,3072]{2,1,0:T(8,128)(2,1)} %copy-done.3, s32[]{:T(128)S(6)} %select_n.191), kind=kLoop, calls=%fused_computation.7 | loop fusion | flops 2359296 | bytes 6291460 | tf_op jit(solution)/shard_map/add | solution.py:212
  59.6 4.8 %reshape_squeeze.9 = f32[64,4,3072]{2,1,0:T(4,128)} reshape(f32[1,256,3072]{2,1,0:T(8,128)} %convert_add_fusion) | data formatting | bytes 6291456 | tf_op jit(solution)/shard_map/reshape;squeeze | solution.py:326
  64.4 1.1 slice_bitcast_fusion.3
  65.5 1.1 slice_bitcast_fusion
  66.6 3.2 %slice.92 = f32[64,4,2048]{2,1,0:T(4,128)} slice(f32[64,4,3072]{2,1,0:T(4,128)} %reshape_squeeze.9), slice={[0:64], [0:4], [0:2048]} | slice | bytes 4194304 | tf_op jit(solution)/shard_map/slice | solution.py:330
  69.9 0.5 multiply_subtract_fusion
  70.4 2.3 %reshape.806 = f32[64,4,16,128]{3,2,1,0:T(8,128)S(1)} reshape(f32[64,4,2048]{2,1,0:T(4,128)} %slice.92) | data formatting | bytes 4194304 | tf_op jit(solution)/shard_map/reshape | solution.py:330
  72.7 0.7 fusion.62
  73.5 0.6 add_convert_fusion
  74.0 1.3 copy.187
  75.3 1.3 copy.186
  77.0 1.3 fusion.15
  78.3 0.5 copy.211
  79.2 2.1 %pad_maximum_fusion.2 = bf16[64,64,128]{2,1,0:T(8,128)(2,1)S(1)} fusion(bf16[64,64,64]{2,1,0:T(8,128)(2,1)} %bitcast.160, bf16[64,64,64]{2,1,0:T(8,128)(2,1)} %bitcast.161), kind=kLoop, calls=%fused_computation.30 | loop fusion | flops 2097152 | bytes 2097152 | tf_op jit(solution)/shard_map/concatenate | solution.py:31
  81.3 1.6 gather_fusion.1
  82.9 24.9 %shard_map.130 = (f32[50,64,1]{2,1,0:T(8,128)}, f32[50,64,1]{2,1,0:T(8,128)}, f32[50,64,128]{2,1,0:T(8,128)}) custom-call(s32[50]{0:T(128)} %compare_select_fusion.1.len_ref, s32[50]{0:T(128)} %blk_ref.1, bf16[50,64,128]{2,1,0:T(8,128)(2,1)} %gather_fusion.1, bf16[50,128,512]{2,1,0:T(8,128)(2,1)} %k_ref.1, bf16[50,128,512]{2,1,0:T(8,128)(2,1)} %v_ref.1), custom_call_target="tpu_custom_call" | custom-call | tf_op jit(solution)/shard_map/pallas_call | solution.py:182
  107.8 2.0 %reduce.1 = f32[50,64]{1,0:T(8,128)S(1)} reduce(f32[50,64,1]{2,1,0:T(8,128)} %get-tuple-element.7, f32[]{:T(128)} %constant.111), dimensions={2}, to_apply=%get-tuple-element.7.reduce_sub_computation | reduce | bytes 25604 | tf_op jit(solution)/shard_map/pallas_call | solution.py:182
  109.9 0.9 select_reduce_fusion
  110.8 0.6 gather_fusion.2
  111.4 1.8 copy.188
  113.2 3.0 %multiply_reduce_fusion.1 = (f32[50,64]{1,0:T(8,128)S(1)}, f32[50,64]{1,0:T(8,128)S(1)}) fusion(f32[50,64,1]{2,1,0:T(8,128)} %get-tuple-element.8, f32[50,64,1]{2,1,0:T(8,128)S(1)} %copy-done.4, f32[50,64,1]{2,1,0:T(8,128)} %copy.188), kind=kLoop, calls=%fused_computation.17 | loop fusion | flops 6400 | bytes 64000 | tf_op jit(solution)/shard_map/mul | solution.py:365
  116.4 1.8 collective-permute-start.3
  118.2 0.5 broadcast_multiply_fusion
  118.7 2.2 %fusion.5 = f32[64,64,128]{2,0,1:T(8,128)S(1)} fusion(f32[50,64,128]{2,1,0:T(8,128)S(1)} %broadcast_multiply_fusion, s32[50]{0:T(128)S(1)} %copy-done.8), kind=kOutput, calls=%fused_computation.15 | convolution fusion | flops 314576000 | bytes 3735752 | tf_op jit(solution)/shard_map/rn,njh->rjh/dot_general | solution.py:367
  120.9 1.4 copy-done.5
  122.4 0.5 copy.217
  123.4 1.9 collective-permute-start.5
  125.5 1.7 collective-permute-done.5
  127.2 2.9 %collective-permute-start.7 = (f32[2,1,1,1,8,64]{5,4,3,2,1,0:T(8,128)S(1)}, f32[2,1,1,1,8,64]{5,4,3,2,1,0:T(8,128)S(1)}, u32[]{:S(2)}, u32[]{:S(2)}) collective-permute-start(f32[2,1,1,1,8,64]{5,4,3,2,1,0:T(8,128)S(1)} %get-tuple-element.60), channel_id=1, source_target_pairs={{0,4},{1,5},{2,6},{3,7},{4,0},{5,1},{6,2},{7,3},{8,12},{9,13},{10,... | collective-permute-start | bytes 12296 | tf_op jit(solution)/shard_map/ppermute | solution.py:251
  130.3 6.4 %collective-permute-done.4 = bf16[2,2,1,8,64,128]{5,3,4,2,1,0:T(8,128)(2,1)S(1)} collective-permute-done((bf16[2,2,1,8,64,128]{5,3,4,2,1,0:T(8,128)(2,1)S(1)}, bf16[2,2,1,8,64,128]{5,3,4,2,1,0:T(8,128)(2,1)S(1)}, u32[]{:S(2)}, u32[]{:S(2)}) %collective-permute-start.4) | collective-permute-done | bytes 524320 | tf_op jit(solution)/shard_map/ppermute | solution.py:252
  136.8 1.8 fusion.12
  138.6 1.6 collective-permute-start.6
  140.5 5.3 %collective-permute-done.6 = bf16[2,1,1,8,64,128]{5,3,4,2,1,0:T(8,128)(2,1)S(1)} collective-permute-done((bf16[2,1,1,8,64,128]{5,3,4,2,1,0:T(8,128)(2,1)S(1)}, bf16[2,1,1,8,64,128]{5,3,4,2,1,0:T(8,128)(2,1)S(1)}, u32[]{:S(2)}, u32[]{:S(2)}) %collective-permute-start.6) | collective-permute-done | bytes 262176 | tf_op jit(solution)/shard_map/ppermute | solution.py:252
  146.2 2.7 %collective-permute-start.8 = (bf16[1,1,1,8,64,128]{5,3,4,2,1,0:T(8,128)(2,1)S(1)}, bf16[1,1,1,8,64,128]{5,3,4,2,1,0:T(8,128)(2,1)S(1)}, u32[]{:S(2)}, u32[]{:S(2)}) collective-permute-start(bf16[1,1,1,8,64,128]{5,3,4,2,1,0:T(8,128)(2,1)S(1)} %dynamic-slice_convert_fusion.1), channel_id=1, source_target_pairs={{0,4},{1,5},{2,6},{3,7},{4,0},{5,1},{6,2},{7,3},{8,12},{9,13},{10,... | collective-permute-start | bytes 393224 | tf_op jit(solution)/shard_map/ppermute | solution.py:252
  149.5 4.0 %collective-permute-done.8 = bf16[1,1,1,8,64,128]{5,3,4,2,1,0:T(8,128)(2,1)S(1)} collective-permute-done((bf16[1,1,1,8,64,128]{5,3,4,2,1,0:T(8,128)(2,1)S(1)}, bf16[1,1,1,8,64,128]{5,3,4,2,1,0:T(8,128)(2,1)S(1)}, u32[]{:S(2)}, u32[]{:S(2)}) %collective-permute-start.8) | collective-permute-done | bytes 131104 | tf_op jit(solution)/shard_map/ppermute | solution.py:252
  153.8 0.5 fusion.11
  154.4 2.0 all_gather.4
  156.4 5.9 %fusion.2 = bf16[2,8,4,2560]{3,1,2,0:T(8,128)(2,1)S(1)} fusion(bf16[2,8,4,2048]{3,1,2,0:T(8,128)(2,1)S(1)} %all_gather.4, bf16[2048,2560]{1,0:T(8,128)(2,1)} %param.16), kind=kOutput, calls=%fused_computation.5 | convolution fusion | flops 671252480 | bytes 11075584 | tf_op jit(solution)/shard_map/dot_general | solution.py:398
  162.3 1.5 collective-permute-start.9
  163.8 4.8 %collective-permute-done.9 = bf16[1,8,4,2560]{3,1,2,0:T(8,128)(2,1)S(1)} collective-permute-done((bf16[1,8,4,2560]{3,1,2,0:T(8,128)(2,1)S(1)}, bf16[1,8,4,2560]{3,1,2,0:T(8,128)(2,1)S(1)}, u32[]{:S(2)}, u32[]{:S(2)}) %collective-permute-start.9) | collective-permute-done | bytes 163872 | tf_op jit(solution)/shard_map/ppermute | solution.py:211
  168.7 1.4 collective-permute-start.10
  170.0 8.5 %collective-permute-done.10 = bf16[1,8,4,2560]{3,1,2,0:T(8,128)(2,1)S(1)} collective-permute-done((bf16[1,8,4,2560]{3,1,2,0:T(8,128)(2,1)S(1)}, bf16[1,8,4,2560]{3,1,2,0:T(8,128)(2,1)S(1)}, u32[]{:S(2)}, u32[]{:S(2)}) %collective-permute-start.10) | collective-permute-done | bytes 163872 | tf_op jit(solution)/shard_map/ppermute | solution.py:224
  178.7 8.6 %collective-permute-done.11 = bf16[2,1,8,4,2560]{4,2,3,1,0:T(8,128)(2,1)S(1)} collective-permute-done((bf16[2,1,8,4,2560]{4,2,3,1,0:T(8,128)(2,1)S(1)}, bf16[2,1,8,4,2560]{4,2,3,1,0:T(8,128)(2,1)S(1)}, u32[]{:S(2)}, u32[]{:S(2)}) %collective-permute-start.11) | collective-permute-done | bytes 327712 | tf_op jit(solution)/shard_map/ppermute | solution.py:224
  187.8 1.8 slice.167
  189.6 1.1 fusion.68
  190.8 11.6 %collective-permute-done.12 = bf16[2,2,1,8,4,2560]{5,3,4,1,2,0:T(8,128)(2,1)S(1)} collective-permute-done((bf16[2,2,1,8,4,2560]{5,3,4,1,2,0:T(8,128)(2,1)S(1)}, bf16[2,2,1,8,4,2560]{5,3,4,1,2,0:T(8,128)(2,1)S(1)}, u32[]{:S(2)}, u32[]{:S(2)}) %collective-permute-start.12) | collective-permute-done | bytes 655392 | tf_op jit(solution)/shard_map/ppermute | solution.py:224
  202.7 2.1 %copy.225 = bf16[64,4,2560]{2,1,0:T(4,128)(2,1)} copy(bf16[64,4,2560]{2,0,1:T(8,128)(2,1)S(1)} %bitcast.159) | data formatting | bytes 2621440
  (84 shorter events, 5.4 us)
Async XLA Ops:
  0.6 38.5 %copy-start = (bf16[2560,512]{1,0:T(8,128)(2,1)S(1)}, bf16[2560,512]{1,0:T(8,128)(2,1)}, u32[]{:S(2)}) copy-start(bf16[2560,512]{1,0:T(8,128)(2,1)} %param.14) | copy-start | bytes 7864324
  0.6 35.6 %copy-start.7 = (f32[2560]{0:T(1024)S(1)}, f32[2560]{0:T(1024)}, u32[]{:S(2)}) copy-start(f32[2560]{0:T(1024)} %param.12) | copy-start | bytes 30724
  4.2 32.0 %collective-permute-start = (bf16[256,2560]{1,0:T(8,128)(2,1)}, bf16[256,2560]{1,0:T(8,128)(2,1)}, u32[]{:S(2)}, u32[]{:S(2)}) collective-permute-start(bf16[256,2560]{1,0:T(8,128)(2,1)} %reshape.769), channel_id=1, source_target_pairs={{0,8},{8,0},{1,9},{9,1},{2,10},{10,2},{3,11},{11,3},{4,12},{12,4},... | collective-permute-start | bytes 3932168 | tf_op jit(solution)/shard_map/ppermute | solution.py:294
  11.8 24.4 %collective-permute-start.1 = (f32[256]{0:T(256)S(1)}, f32[256]{0:T(256)S(1)}, u32[]{:S(2)}, u32[]{:S(2)}) collective-permute-start(f32[256]{0:T(256)S(1)} %psum.7), channel_id=1, source_target_pairs={{0,8},{8,0},{1,9},{9,1},{2,10},{10,2},{3,11},{11,3},{4,12},{12,4},... | collective-permute-start | bytes 3080 | tf_op jit(solution)/shard_map/ppermute | solution.py:297
  36.3 4.4 %copy-start.9 = (bf16[2560,512]{1,0:T(8,128)(2,1)S(1)}, bf16[2560,512]{1,0:T(8,128)(2,1)}, u32[]{:S(2)}) copy-start(bf16[2560,512]{1,0:T(8,128)(2,1)} %param.15) | copy-start | bytes 7864324
  39.1 3.1 %slice-start = ((s8[10485760]{0:T(1024)(128)(4,1)}), s8[4194304]{0:T(1024)(128)(4,1)S(1)}, s32[]{:S(2)}) async-start(s8[10485760]{0:T(1024)(128)(4,1)} %bitcast.177), calls=%async_computation | async-start | bytes 8388608
  39.1 3.5 %slice-start.1 = ((s8[10485760]{0:T(1024)(128)(4,1)}), s8[4194304]{0:T(1024)(128)(4,1)S(1)}, s32[]{:S(2)}) async-start(s8[10485760]{0:T(1024)(128)(4,1)} %bitcast.177), calls=%async_computation.1 | async-start | bytes 8388608
  40.7 2.7 %slice-start.2 = ((s8[10485760]{0:T(1024)(128)(4,1)}), s8[2097152]{0:T(1024)(128)(4,1)S(1)}, s32[]{:S(2)}) async-start(s8[10485760]{0:T(1024)(128)(4,1)} %bitcast.177), calls=%async_computation.2 | async-start | bytes 4194304
  49.5 1.6 copy-start.3
  51.1 1.3 copy-start.8
  51.1 1.3 copy-start.2
  52.4 3.6 %collective-permute-start.2 = (bf16[1,256,3072]{2,1,0:T(8,128)(2,1)}, bf16[1,256,3072]{2,1,0:T(8,128)(2,1)S(1)}, u32[]{:S(2)}, u32[]{:S(2)}) collective-permute-start(bf16[1,256,3072]{2,1,0:T(8,128)(2,1)} %constant_dynamic-slice_fusion.3), channel_id=1, source_target_pairs={{0,16},{16,0},{1,17},{17,1},{2,18},{18,2},{3,19},{19,3},{4,20},{20... | collective-permute-start | bytes 4718600 | tf_op jit(solution)/shard_map/ppermute | solution.py:211
  107.8 5.4 %copy-start.4 = (f32[50,64,1]{2,1,0:T(8,128)S(1)}, f32[50,64,1]{2,1,0:T(8,128)}, u32[]{:S(2)}) copy-start(f32[50,64,1]{2,1,0:T(8,128)} %get-tuple-element.7) | copy-start | bytes 38404
  113.2 5.1 %copy-start.6 = (f32[50,64,128]{2,1,0:T(8,128)S(1)}, f32[50,64,128]{2,1,0:T(8,128)}, u32[]{:S(2)}) copy-start(f32[50,64,128]{2,1,0:T(8,128)} %get-tuple-element.6) | copy-start | bytes 4915204
  116.4 7.0 %collective-permute-start.3 = (f32[2,2,2,1,8,64]{5,4,3,2,1,0:T(8,128)S(1)}, f32[2,2,2,1,8,64]{5,4,3,2,1,0:T(8,128)S(1)}, u32[]{:S(2)}, u32[]{:S(2)}) collective-permute-start(f32[2,2,2,1,8,64]{5,4,3,2,1,0:T(8,128)S(1)} %get-tuple-element.50), channel_id=1, source_target_pairs={{0,1},{1,0},{2,3},{3,2},{4,5},{5,4},{6,7},{7,6},{8,9},{9,8},{10,11... | collective-permute-start | bytes 49160 | tf_op jit(solution)/shard_map/ppermute | solution.py:251
  120.9 1.4 copy-start.5
  123.0 13.8 %collective-permute-start.4 = (bf16[2,2,1,8,64,128]{5,3,4,2,1,0:T(8,128)(2,1)S(1)}, bf16[2,2,1,8,64,128]{5,3,4,2,1,0:T(8,128)(2,1)S(1)}, u32[]{:S(2)}, u32[]{:S(2)}) collective-permute-start(bf16[2,2,1,8,64,128]{5,3,4,2,1,0:T(8,128)(2,1)S(1)} %copy.276), channel_id=1, source_target_pairs={{0,1},{1,0},{2,3},{3,2},{4,5},{5,4},{6,7},{7,6},{8,9},{9,8},{10,11... | collective-permute-start | bytes 1572872 | tf_op jit(solution)/shard_map/ppermute | solution.py:252
  123.4 3.8 %collective-permute-start.5 = (f32[2,2,1,1,8,64]{5,4,3,2,1,0:T(8,128)S(1)}, f32[2,2,1,1,8,64]{5,4,3,2,1,0:T(8,128)S(1)}, u32[]{:S(2)}, u32[]{:S(2)}) collective-permute-start(f32[2,2,1,1,8,64]{5,4,3,2,1,0:T(8,128)S(1)} %get-tuple-element.56), channel_id=1, source_target_pairs={{0,2},{1,3},{2,0},{3,1},{4,6},{5,7},{6,4},{7,5},{8,10},{9,11},{10,... | collective-permute-start | bytes 24584 | tf_op jit(solution)/shard_map/ppermute | solution.py:251
  127.2 13.0 %collective-permute-start.7 = (f32[2,1,1,1,8,64]{5,4,3,2,1,0:T(8,128)S(1)}, f32[2,1,1,1,8,64]{5,4,3,2,1,0:T(8,128)S(1)}, u32[]{:S(2)}, u32[]{:S(2)}) collective-permute-start(f32[2,1,1,1,8,64]{5,4,3,2,1,0:T(8,128)S(1)} %get-tuple-element.60), channel_id=1, source_target_pairs={{0,4},{1,5},{2,6},{3,7},{4,0},{5,1},{6,2},{7,3},{8,12},{9,13},{10,... | collective-permute-start | bytes 12296 | tf_op jit(solution)/shard_map/ppermute | solution.py:251
  138.6 7.3 %collective-permute-start.6 = (bf16[2,1,1,8,64,128]{5,3,4,2,1,0:T(8,128)(2,1)S(1)}, bf16[2,1,1,8,64,128]{5,3,4,2,1,0:T(8,128)(2,1)S(1)}, u32[]{:S(2)}, u32[]{:S(2)}) collective-permute-start(bf16[2,1,1,8,64,128]{5,3,4,2,1,0:T(8,128)(2,1)S(1)} %dynamic-slice_convert_fusion), channel_id=1, source_target_pairs={{0,2},{1,3},{2,0},{3,1},{4,6},{5,7},{6,4},{7,5},{8,10},{9,11},{10,... | collective-permute-start | bytes 786440 | tf_op jit(solution)/shard_map/ppermute | solution.py:252
  146.2 7.3 %collective-permute-start.8 = (bf16[1,1,1,8,64,128]{5,3,4,2,1,0:T(8,128)(2,1)S(1)}, bf16[1,1,1,8,64,128]{5,3,4,2,1,0:T(8,128)(2,1)S(1)}, u32[]{:S(2)}, u32[]{:S(2)}) collective-permute-start(bf16[1,1,1,8,64,128]{5,3,4,2,1,0:T(8,128)(2,1)S(1)} %dynamic-slice_convert_fusion.1), channel_id=1, source_target_pairs={{0,4},{1,5},{2,6},{3,7},{4,0},{5,1},{6,2},{7,3},{8,12},{9,13},{10,... | collective-permute-start | bytes 393224 | tf_op jit(solution)/shard_map/ppermute | solution.py:252
  162.3 6.3 %collective-permute-start.9 = (bf16[1,8,4,2560]{3,1,2,0:T(8,128)(2,1)S(1)}, bf16[1,8,4,2560]{3,1,2,0:T(8,128)(2,1)S(1)}, u32[]{:S(2)}, u32[]{:S(2)}) collective-permute-start(bf16[1,8,4,2560]{3,1,2,0:T(8,128)(2,1)S(1)} %constant_dynamic-slice_fusion), channel_id=1, source_target_pairs={{0,8},{8,0},{1,9},{9,1},{2,10},{10,2},{3,11},{11,3},{4,12},{12,4},... | collective-permute-start | bytes 491528 | tf_op jit(solution)/shard_map/ppermute | solution.py:211
  168.7 9.9 %collective-permute-start.10 = (bf16[1,8,4,2560]{3,1,2,0:T(8,128)(2,1)S(1)}, bf16[1,8,4,2560]{3,1,2,0:T(8,128)(2,1)S(1)}, u32[]{:S(2)}, u32[]{:S(2)}) collective-permute-start(bf16[1,8,4,2560]{3,1,2,0:T(8,128)(2,1)S(1)} %add_convert_fusion.1), channel_id=1, source_target_pairs={{0,4},{1,5},{2,6},{3,7},{4,0},{5,1},{6,2},{7,3},{8,12},{9,13},{10,... | collective-permute-start | bytes 491528 | tf_op jit(solution)/shard_map/ppermute | solution.py:224
  178.6 8.8 %collective-permute-start.11 = (bf16[2,1,8,4,2560]{4,2,3,1,0:T(8,128)(2,1)S(1)}, bf16[2,1,8,4,2560]{4,2,3,1,0:T(8,128)(2,1)S(1)}, u32[]{:S(2)}, u32[]{:S(2)}) collective-permute-start(bf16[2,1,8,4,2560]{4,2,3,1,0:T(8,128)(2,1)S(1)} %maximum_select_fusion.4), channel_id=1, source_target_pairs={{0,2},{1,3},{2,0},{3,1},{4,6},{5,7},{6,4},{7,5},{8,10},{9,11},{10,... | collective-permute-start | bytes 983048 | tf_op jit(solution)/shard_map/ppermute | solution.py:224
  187.5 14.9 %collective-permute-start.12 = (bf16[2,2,1,8,4,2560]{5,3,4,1,2,0:T(8,128)(2,1)S(1)}, bf16[2,2,1,8,4,2560]{5,3,4,1,2,0:T(8,128)(2,1)S(1)}, u32[]{:S(2)}, u32[]{:S(2)}) collective-permute-start(bf16[2,2,1,8,4,2560]{5,3,4,1,2,0:T(8,128)(2,1)S(1)} %maximum_select_fusion.2), channel_id=1, source_target_pairs={{0,1},{1,0},{2,3},{3,2},{4,5},{5,4},{6,7},{7,6},{8,9},{9,8},{10,11... | collective-permute-start | bytes 1966088 | tf_op jit(solution)/shard_map/ppermute | solution.py:224
  202.4 2.4 %copy-start.1 = (bf16[2560,512]{1,0:T(8,128)(2,1)S(1)}, bf16[2560,512]{1,0:T(8,128)(2,1)}, u32[]{:S(2)}) copy-start(bf16[2560,512]{1,0:T(8,128)(2,1)} %param.14) | copy-start | bytes 7864324

commit v6 on v5

--- a/solution.py
+++ b/solution.py
@@ -118,12 +118,12 @@
 def slot_kernel(len_ref, blk_ref, q_ref, k_ref, v_ref, peak_ref, tot_ref, acc_ref, *, ns, heads, qpk):
     base = pl.program_id(0) * ns
     rows = q_ref.shape[1]
+    group = rows // heads
     width = k_ref.shape[1]
     head = k_ref.shape[2] // heads
     row = lax.broadcasted_iota(jnp.int32, (rows, width), 0)
     col = lax.broadcasted_iota(jnp.int32, (rows, width), 1)
-    head_of = (row // qpk) % heads
-    step_of = row // (heads * qpk)
+    step_of = (row % group) // qpk
 
     def body(i, carry):
         length = len_ref[base + i]
@@ -133,32 +133,39 @@
         q = q_ref[i]
         k = k_ref[i]
         v = v_ref[i]
-        scores = jnp.zeros((rows, width), jnp.float32)
-        for a in range(heads):
-            part = lax.dot_general(
-                q,
-                k[:, a * head : (a + 1) * head],
-                (((1,), (1,)), ((), ())),
-                preferred_element_type=jnp.float32,
-            )
-            scores = jnp.where(head_of == a, part, scores)
-        scores = scores * (1.0 / math.sqrt(HEAD_SIZE))
+        scores = jnp.concatenate(
+            [
+                lax.dot_general(
+                    q[a * group : (a + 1) * group],
+                    k[:, a * head : (a + 1) * head],
+                    (((1,), (1,)), ((), ())),
+                    preferred_element_type=jnp.float32,
+                )
+                for a in range(heads)
+            ],
+            0,
+        ) * (1.0 / math.sqrt(HEAD_SIZE))
         peak = jnp.max(jnp.where(visible, scores, NEGATIVE_FILL), axis=1, keepdims=True)
         weights = jnp.where(visible, jnp.exp(scores - peak), 0.0)
         total = jnp.sum(weights, axis=1, keepdims=True)
         rounded = weights.astype(jnp.bfloat16)
-        acc = jnp.zeros((rows, head), jnp.float32)
-        for a in range(heads):
-            part = jnp.dot(
-                rounded, v[:, a * head : (a + 1) * head], preferred_element_type=jnp.float32
-            )
-            acc = jnp.where(head_of[:, :head] == a, part, acc)
+        acc = jnp.concatenate(
+            [
+                jnp.dot(
+                    rounded[a * group : (a + 1) * group],
+                    v[:, a * head : (a + 1) * head],
+                    preferred_element_type=jnp.float32,
+                )
+                for a in range(heads)
+            ],
+            0,
+        )
         peak_ref[i] = peak
         tot_ref[i] = total
         acc_ref[i] = acc
         return carry
 
-    lax.fori_loop(0, ns, body, 0)
+    lax.fori_loop(0, ns, body, 0, unroll=True)
 
 
 def slot_attention(slot_queries, slot_lengths, block_numbers, keys, values, heads, qpk):
@@ -345,7 +352,7 @@
     picked = jnp.minimum(slot_request, req_count - 1)
     in_use = slot_request < req_count
     slot_lengths = jnp.where(in_use, lengths[picked], 0)
-    flat_queries = query_rows.reshape(req_count, -1, HEAD_SIZE)
+    flat_queries = query_rows.transpose(0, 2, 1, 3, 4).reshape(req_count, -1, HEAD_SIZE)
     slot_peak, slot_total, slot_acc = slot_attention(
         flat_queries[picked],
         slot_lengths,
@@ -374,10 +381,10 @@
     running_peak, running_totals, weighted_values = seq_merge(
         local_peak, local_totals, local_values, n_seq, seq_index
     )
-    order = (per, step_count, heads_kv, QUERY_PER_KEY)
-    running_peak = running_peak.reshape(order).transpose(0, 2, 1, 3)
-    running_totals = running_totals.reshape(order).transpose(0, 2, 1, 3)
-    weighted_values = weighted_values.reshape(order + (HEAD_SIZE,)).transpose(0, 2, 1, 3, 4)
+    order = (per, heads_kv, step_count, QUERY_PER_KEY)
+    running_peak = running_peak.reshape(order)
+    running_totals = running_totals.reshape(order)
+    weighted_values = weighted_values.reshape(order + (HEAD_SIZE,))
     own_queries = lax.dynamic_slice_in_dim(query_rows, mine, per, 0)
     fresh = fresh_part(
         own_queries,

time: 205 us -> 196 us (0.956)
  Pallas kernels: 24.9 us -> 17.3 us
    pallas_call x1, Pallas kernels: 24.9 us -> 17.3 us  [slot_attention(): pl.pallas_call(partial(slot_kernel, ns=ns, heads=heads, qpk=qpk), grid_sp...]
    another operation x2 -> x0, local copies, waits for them, and re-layouts: 2.58 us -> none
    unnamed x28 -> x27, local copies, waits for them, and re-layouts: 6.38 us -> 6.29 us
  transfers between devices with their start and end apart: 13 -> 13, of which waited for: 10 -> 10; matrix products, arithmetic and copies ran while one was open for 7% -> 8% of each run, Pallas kernels for 0% -> 0%
where the time goes in v6:
time: 196 us; the launch traced here: 195 us
  waiting for transfers between devices  75.5 us (39%)
  local copies, waits for them, and re-layouts  34.5 us (18%)
  other arithmetic  25.8 us (13%)
  matrix products  18.8 us (10%)
  starting transfers between devices  17.5 us (9%)
  Pallas kernels  17.3 us (9%)
  blocking collectives  4.46 us (2%)
    ppermute x3, waiting for transfers between devices, doubling_gather(): got = lax.ppermute(block, axis_name, pairs)  28.7 us
    ppermute x1, waiting for transfers between devices, on_device(): other_squares = lax.ppermute(squares, 'col', swap)  24.4 us
    pallas_call x1, Pallas kernels, slot_attention(): pl.pallas_call(partial(slot_kernel, ns=ns, heads=heads, qpk=qpk), grid_sp...  17.3 us
    ppermute x3, waiting for transfers between devices, seq_merge(): lax.ppermute(send_values.astype(jnp.bfloat16), 'seq', pairs)  15 us
    dot_general x3, matrix products, on_device(): jnp.dot(gathered, matrix, preferred_element_type=jnp.float32)  8.8 us
    ppermute x3, starting transfers between devices, seq_merge(): got_stats = lax.ppermute(send_stats, 'seq', pairs)  6.63 us
    unnamed x27, local copies, waits for them, and re-layouts  6.29 us
    dot_general x1, matrix products, on_device(): jnp.dot(piece_rows.reshape(n_row * per * step_count, -1), wo, preferred_e...  5.88 us
  transfers between devices with their start and end apart: 13, of which 10 were waited for; matrix products, arithmetic and copies ran while one was open for 8% of the time, Pallas kernels for 0%

profile of v6, /device:TPU:0, one launch (start us, length us, event | category | flops | bytes accessed | tf_op | source)
XLA Modules:
  0.0 195.0 jit_solution(4860187712952625000)
XLA Ops:
  0.7 3.5 %reshape.810 = bf16[256,2560]{1,0:T(8,128)(2,1)} reshape(bf16[64,4,2560]{2,1,0:T(4,128)(2,1)} %param.11) | data formatting | bytes 2621440 | tf_op jit(solution)/shard_map/reshape | solution.py:298
  4.2 2.9 %collective-permute-start = (bf16[256,2560]{1,0:T(8,128)(2,1)}, bf16[256,2560]{1,0:T(8,128)(2,1)}, u32[]{:S(2)}, u32[]{:S(2)}) collective-permute-start(bf16[256,2560]{1,0:T(8,128)(2,1)} %reshape.810), channel_id=1, source_target_pairs={{0,8},{8,0},{1,9},{9,1},{2,10},{10,2},{3,11},{11,3},{4,12},{12,4},... | collective-permute-start | bytes 3932168 | tf_op jit(solution)/shard_map/ppermute | solution.py:301
  7.1 2.1 %multiply_reduce_fusion = f32[64,4]{1,0:T(8,128)S(1)} fusion(bf16[64,4,2560]{2,1,0:T(4,128)(2,1)} %param.11), kind=kLoop, calls=%fused_computation.12 | loop fusion | flops 1965824 | bytes 1311744 | tf_op jit(solution)/shard_map/reduce_sum | solution.py:303
  9.3 2.5 %psum.7 = f32[256]{0:T(256)S(1)} all-reduce(f32[256]{0:T(256)S(1)} %reduce_sum.21), channel_id=1, replica_groups=mesh['row'=2,'col'=2,'seq'=8] {'row'}, use_global_device_ids=true, to_apply=%region_1.0 | all-reduce | flops 256 | bytes 2048 | tf_op jit(solution)/shard_map/psum | solution.py:303
  11.8 24.4 %collective-permute-done.1 = f32[256]{0:T(256)S(1)} collective-permute-done((f32[256]{0:T(256)S(1)}, f32[256]{0:T(256)S(1)}, u32[]{:S(2)}, u32[]{:S(2)}) %collective-permute-start.1) | collective-permute-done | bytes 1056 | tf_op jit(solution)/shard_map/ppermute | solution.py:304
  36.3 2.8 %multiply_convert_fusion.1 = (bf16[256,2560]{1,0:T(8,128)(2,1)S(1)}, bf16[256,2560]{1,0:T(8,128)(2,1)S(1)}) fusion(f32[2560]{0:T(1024)S(1)} %copy-done.7, f32[256]{0:T(256)S(1)} %get-tuple-element.61, bf16[256,2560]{1,0:T(8,128)(2,1)} %reshape.810, bf16[256,2560]{1,0:T(8,128)(2,1)} %collective-permute-done, pred[]{:T(512)S(6)} %eq.72, ...), kind=kLoop, calls=%fused_computation.11 | loop fusion | flops 6553600 | bytes 5255169 | tf_op jit(solution)/shard_map/convert_element_type | solution.py:308
  39.1 1.5 convolution_convert_fusion.2
  40.7 1.5 convolution_convert_fusion.1
  42.6 0.8 slice-done.2
  43.4 5.8 %convolution_convert_fusion = bf16[512,2048]{1,0:T(8,128)(2,1)S(1)} fusion(bf16[2560,2048]{1,0:T(8,128)(2,1)S(1)} %bitcast.168, bf16[256,2560]{1,0:T(8,128)(2,1)S(1)} %get-tuple-element.38, bf16[256,2560]{1,0:T(8,128)(2,1)S(1)} %get-tuple-element.37), kind=kOutput, calls=%fused_computation.8 | convolution fusion | flops 5375000576 | bytes 15204352 | tf_op jit(solution)/shard_map/dot_general | solution.py:323
  49.5 1.6 copy-done.3
  51.1 1.3 constant_dynamic-slice_fusion.1
  52.4 0.8 gather_fusion
  53.3 1.1 multiply_cosine_fusion
  54.5 0.5 compare_select_fusion.1.len_ref
  55.1 1.0 collective-permute-done.2
  56.0 3.6 %convert_add_fusion = f32[1,256,3072]{2,1,0:T(8,128)} fusion(bf16[1,256,3072]{2,1,0:T(8,128)(2,1)S(1)} %collective-permute-done.2, bf16[2,256,3072]{2,1,0:T(8,128)(2,1)} %copy-done.3, s32[]{:T(128)S(6)} %select_n.191), kind=kLoop, calls=%fused_computation.7 | loop fusion | flops 2359296 | bytes 6291460 | tf_op jit(solution)/shard_map/add | solution.py:219
  59.6 4.8 %reshape_squeeze.7 = f32[64,4,3072]{2,1,0:T(4,128)} reshape(f32[1,256,3072]{2,1,0:T(8,128)} %convert_add_fusion) | data formatting | bytes 6291456 | tf_op jit(solution)/shard_map/reshape;squeeze | solution.py:333
  64.4 1.1 slice_bitcast_fusion.3
  65.5 1.1 slice_bitcast_fusion
  66.6 3.2 %slice.92 = f32[64,4,2048]{2,1,0:T(4,128)} slice(f32[64,4,3072]{2,1,0:T(4,128)} %reshape_squeeze.7), slice={[0:64], [0:4], [0:2048]} | slice | bytes 4194304 | tf_op jit(solution)/shard_map/slice | solution.py:337
  69.9 0.5 multiply_subtract_fusion
  70.4 2.3 %reshape.848 = f32[64,4,16,128]{3,2,1,0:T(8,128)S(1)} reshape(f32[64,4,2048]{2,1,0:T(4,128)} %slice.92) | data formatting | bytes 4194304 | tf_op jit(solution)/shard_map/reshape | solution.py:337
  72.7 0.7 fusion.58
  73.5 0.6 subtract_convert_fusion
  74.0 1.4 pad_maximum_fusion.2
  75.5 0.6 copy.215
  76.4 1.2 fusion.13
  77.6 0.5 copy.191
  78.1 1.6 gather_fusion.1
  79.9 0.8 fusion.15
  80.7 17.3 %shard_map.130 = (f32[50,64,1]{2,1,0:T(8,128)}, f32[50,64,1]{2,1,0:T(8,128)}, f32[50,64,128]{2,1,0:T(8,128)}) custom-call(s32[50]{0:T(128)} %compare_select_fusion.1.len_ref, s32[50]{0:T(128)} %blk_ref.1, bf16[50,64,128]{2,1,0:T(8,128)(2,1)} %gather_fusion.1, bf16[50,128,512]{2,1,0:T(8,128)(2,1)} %k_ref.1, bf16[50,128,512]{2,1,0:T(8,128)(2,1)} %v_ref.1), custom_call_target="tpu_custom_call" | custom-call | tf_op jit(solution)/shard_map/pallas_call | solution.py:189
  98.0 2.0 %reduce.1 = f32[50,64]{1,0:T(8,128)S(1)} reduce(f32[50,64,1]{2,1,0:T(8,128)} %get-tuple-element.7, f32[]{:T(128)} %constant.111), dimensions={2}, to_apply=%get-tuple-element.7.reduce_sub_computation | reduce | bytes 25604 | tf_op jit(solution)/shard_map/pallas_call | solution.py:189
  100.1 0.9 select_reduce_fusion
  101.0 0.6 gather_fusion.2
  101.6 1.8 copy.173
  103.4 3.0 %multiply_reduce_fusion.1 = (f32[50,64]{1,0:T(8,128)S(1)}, f32[50,64]{1,0:T(8,128)S(1)}) fusion(f32[50,64,1]{2,1,0:T(8,128)} %get-tuple-element.8, f32[50,64,1]{2,1,0:T(8,128)S(1)} %copy-done.4, f32[50,64,1]{2,1,0:T(8,128)} %copy.173), kind=kLoop, calls=%fused_computation.17 | loop fusion | flops 6400 | bytes 64000 | tf_op jit(solution)/shard_map/mul | solution.py:372
  106.6 1.8 collective-permute-start.3
  108.4 0.5 broadcast_multiply_fusion
  108.9 2.2 %fusion.5 = f32[64,64,128]{2,0,1:T(8,128)S(1)} fusion(f32[50,64,128]{2,1,0:T(8,128)S(1)} %broadcast_multiply_fusion, s32[50]{0:T(128)S(1)} %copy-done.8), kind=kOutput, calls=%fused_computation.15 | convolution fusion | flops 314576000 | bytes 3735752 | tf_op jit(solution)/shard_map/rn,njh->rjh/dot_general | solution.py:374
  111.1 1.4 copy-done.5
  112.6 0.5 copy.196
  113.5 1.9 collective-permute-start.5
  115.7 1.6 collective-permute-done.5
  117.3 2.9 %collective-permute-start.7 = (f32[2,1,1,1,8,64]{5,4,3,2,1,0:T(8,128)S(1)}, f32[2,1,1,1,8,64]{5,4,3,2,1,0:T(8,128)S(1)}, u32[]{:S(2)}, u32[]{:S(2)}) collective-permute-start(f32[2,1,1,1,8,64]{5,4,3,2,1,0:T(8,128)S(1)} %get-tuple-element.60), channel_id=1, source_target_pairs={{0,4},{1,5},{2,6},{3,7},{4,0},{5,1},{6,2},{7,3},{8,12},{9,13},{10,... | collective-permute-start | bytes 12296 | tf_op jit(solution)/shard_map/ppermute | solution.py:258
  120.5 6.4 %collective-permute-done.4 = bf16[2,2,1,8,64,128]{5,3,2,1,0,4:T(8,128)(2,1)S(1)} collective-permute-done((bf16[2,2,1,8,64,128]{5,3,2,1,0,4:T(8,128)(2,1)S(1)}, bf16[2,2,1,8,64,128]{5,3,2,1,0,4:T(8,128)(2,1)S(1)}, u32[]{:S(2)}, u32[]{:S(2)}) %collective-permute-start.4) | collective-permute-done | bytes 524320 | tf_op jit(solution)/shard_map/ppermute | solution.py:259
  126.9 1.8 multiply_add_fusion
  128.8 1.6 collective-permute-start.6
  130.7 5.3 %collective-permute-done.6 = bf16[2,1,1,8,64,128]{5,3,2,1,0,4:T(8,128)(2,1)S(1)} collective-permute-done((bf16[2,1,1,8,64,128]{5,3,2,1,0,4:T(8,128)(2,1)S(1)}, bf16[2,1,1,8,64,128]{5,3,2,1,0,4:T(8,128)(2,1)S(1)}, u32[]{:S(2)}, u32[]{:S(2)}) %collective-permute-start.6) | collective-permute-done | bytes 262176 | tf_op jit(solution)/shard_map/ppermute | solution.py:259
  136.4 2.7 %collective-permute-start.8 = (bf16[1,1,1,8,64,128]{5,3,2,1,0,4:T(8,128)(2,1)S(1)}, bf16[1,1,1,8,64,128]{5,3,2,1,0,4:T(8,128)(2,1)S(1)}, u32[]{:S(2)}, u32[]{:S(2)}) collective-permute-start(bf16[1,1,1,8,64,128]{5,3,2,1,0,4:T(8,128)(2,1)S(1)} %dynamic-slice_convert_fusion.2), channel_id=1, source_target_pairs={{0,4},{1,5},{2,6},{3,7},{4,0},{5,1},{6,2},{7,3},{8,12},{9,13},{10,... | collective-permute-start | bytes 393224 | tf_op jit(solution)/shard_map/ppermute | solution.py:259
  139.1 0.8 multiply_add_fusion.4
  140.5 3.3 %collective-permute-done.8 = bf16[1,1,1,8,64,128]{5,3,2,1,0,4:T(8,128)(2,1)S(1)} collective-permute-done((bf16[1,1,1,8,64,128]{5,3,2,1,0,4:T(8,128)(2,1)S(1)}, bf16[1,1,1,8,64,128]{5,3,2,1,0,4:T(8,128)(2,1)S(1)}, u32[]{:S(2)}, u32[]{:S(2)}) %collective-permute-start.8) | collective-permute-done | bytes 131104 | tf_op jit(solution)/shard_map/ppermute | solution.py:259
  144.0 0.5 fusion.11
  144.7 2.0 %all_gather.4 = bf16[2,8,4,2048]{3,1,2,0:T(8,128)(2,1)S(1)} all-gather(bf16[1,8,4,2048]{3,1,2,0:T(8,128)(2,1)S(1)} %convert_element_type.122), channel_id=1, replica_groups=mesh['row'=2,'col'=2,'seq'=8] {'row'}, dimensions={0}, use_global_device_ids=true | all-gather | bytes 393216 | tf_op jit(solution)/shard_map/all_gather | solution.py:403
  146.6 5.9 %fusion.2 = bf16[2,8,4,2560]{3,1,2,0:T(8,128)(2,1)S(1)} fusion(bf16[2,8,4,2048]{3,1,2,0:T(8,128)(2,1)S(1)} %all_gather.4, bf16[2048,2560]{1,0:T(8,128)(2,1)} %param.16), kind=kOutput, calls=%fused_computation.5 | convolution fusion | flops 671252480 | bytes 11075584 | tf_op jit(solution)/shard_map/dot_general | solution.py:405
  152.5 1.6 collective-permute-start.9
  154.1 4.8 %collective-permute-done.9 = bf16[1,8,4,2560]{3,1,2,0:T(8,128)(2,1)S(1)} collective-permute-done((bf16[1,8,4,2560]{3,1,2,0:T(8,128)(2,1)S(1)}, bf16[1,8,4,2560]{3,1,2,0:T(8,128)(2,1)S(1)}, u32[]{:S(2)}, u32[]{:S(2)}) %collective-permute-start.9) | collective-permute-done | bytes 163872 | tf_op jit(solution)/shard_map/ppermute | solution.py:218
  158.9 1.4 collective-permute-start.10
  160.3 8.5 %collective-permute-done.10 = bf16[1,8,4,2560]{3,1,2,0:T(8,128)(2,1)S(1)} collective-permute-done((bf16[1,8,4,2560]{3,1,2,0:T(8,128)(2,1)S(1)}, bf16[1,8,4,2560]{3,1,2,0:T(8,128)(2,1)S(1)}, u32[]{:S(2)}, u32[]{:S(2)}) %collective-permute-start.10) | collective-permute-done | bytes 163872 | tf_op jit(solution)/shard_map/ppermute | solution.py:231
  169.0 8.6 %collective-permute-done.11 = bf16[2,1,8,4,2560]{4,2,3,1,0:T(8,128)(2,1)S(1)} collective-permute-done((bf16[2,1,8,4,2560]{4,2,3,1,0:T(8,128)(2,1)S(1)}, bf16[2,1,8,4,2560]{4,2,3,1,0:T(8,128)(2,1)S(1)}, u32[]{:S(2)}, u32[]{:S(2)}) %collective-permute-start.11) | collective-permute-done | bytes 327712 | tf_op jit(solution)/shard_map/ppermute | solution.py:231
  178.0 1.8 slice.167
  179.9 1.1 fusion.64
  181.1 11.5 %collective-permute-done.12 = bf16[2,2,1,8,4,2560]{5,3,4,1,2,0:T(8,128)(2,1)S(1)} collective-permute-done((bf16[2,2,1,8,4,2560]{5,3,4,1,2,0:T(8,128)(2,1)S(1)}, bf16[2,2,1,8,4,2560]{5,3,4,1,2,0:T(8,128)(2,1)S(1)}, u32[]{:S(2)}, u32[]{:S(2)}) %collective-permute-start.12) | collective-permute-done | bytes 655392 | tf_op jit(solution)/shard_map/ppermute | solution.py:231
  192.9 2.1 %copy.205 = bf16[64,4,2560]{2,1,0:T(4,128)(2,1)} copy(bf16[64,4,2560]{2,0,1:T(8,128)(2,1)S(1)} %bitcast.143) | data formatting | bytes 2621440
  (83 shorter events, 5.6 us)
Async XLA Ops:
  0.6 38.5 %copy-start = (bf16[2560,512]{1,0:T(8,128)(2,1)S(1)}, bf16[2560,512]{1,0:T(8,128)(2,1)}, u32[]{:S(2)}) copy-start(bf16[2560,512]{1,0:T(8,128)(2,1)} %param.14) | copy-start | bytes 7864324
  0.6 35.6 %copy-start.7 = (f32[2560]{0:T(1024)S(1)}, f32[2560]{0:T(1024)}, u32[]{:S(2)}) copy-start(f32[2560]{0:T(1024)} %param.12) | copy-start | bytes 30724
  4.2 32.0 %collective-permute-start = (bf16[256,2560]{1,0:T(8,128)(2,1)}, bf16[256,2560]{1,0:T(8,128)(2,1)}, u32[]{:S(2)}, u32[]{:S(2)}) collective-permute-start(bf16[256,2560]{1,0:T(8,128)(2,1)} %reshape.810), channel_id=1, source_target_pairs={{0,8},{8,0},{1,9},{9,1},{2,10},{10,2},{3,11},{11,3},{4,12},{12,4},... | collective-permute-start | bytes 3932168 | tf_op jit(solution)/shard_map/ppermute | solution.py:301
  11.8 24.4 %collective-permute-start.1 = (f32[256]{0:T(256)S(1)}, f32[256]{0:T(256)S(1)}, u32[]{:S(2)}, u32[]{:S(2)}) collective-permute-start(f32[256]{0:T(256)S(1)} %psum.7), channel_id=1, source_target_pairs={{0,8},{8,0},{1,9},{9,1},{2,10},{10,2},{3,11},{11,3},{4,12},{12,4},... | collective-permute-start | bytes 3080 | tf_op jit(solution)/shard_map/ppermute | solution.py:304
  36.3 4.4 %copy-start.9 = (bf16[2560,512]{1,0:T(8,128)(2,1)S(1)}, bf16[2560,512]{1,0:T(8,128)(2,1)}, u32[]{:S(2)}) copy-start(bf16[2560,512]{1,0:T(8,128)(2,1)} %param.15) | copy-start | bytes 7864324
  39.1 3.1 %slice-start = ((s8[10485760]{0:T(1024)(128)(4,1)}), s8[4194304]{0:T(1024)(128)(4,1)S(1)}, s32[]{:S(2)}) async-start(s8[10485760]{0:T(1024)(128)(4,1)} %bitcast.167), calls=%async_computation | async-start | bytes 8388608
  39.1 3.5 %slice-start.1 = ((s8[10485760]{0:T(1024)(128)(4,1)}), s8[4194304]{0:T(1024)(128)(4,1)S(1)}, s32[]{:S(2)}) async-start(s8[10485760]{0:T(1024)(128)(4,1)} %bitcast.167), calls=%async_computation.1 | async-start | bytes 8388608
  40.7 2.7 %slice-start.2 = ((s8[10485760]{0:T(1024)(128)(4,1)}), s8[2097152]{0:T(1024)(128)(4,1)S(1)}, s32[]{:S(2)}) async-start(s8[10485760]{0:T(1024)(128)(4,1)} %bitcast.167), calls=%async_computation.2 | async-start | bytes 4194304
  49.5 1.6 copy-start.3
  51.1 1.3 copy-start.8
  51.1 1.3 copy-start.2
  52.4 3.6 %collective-permute-start.2 = (bf16[1,256,3072]{2,1,0:T(8,128)(2,1)}, bf16[1,256,3072]{2,1,0:T(8,128)(2,1)S(1)}, u32[]{:S(2)}, u32[]{:S(2)}) collective-permute-start(bf16[1,256,3072]{2,1,0:T(8,128)(2,1)} %constant_dynamic-slice_fusion.1), channel_id=1, source_target_pairs={{0,16},{16,0},{1,17},{17,1},{2,18},{18,2},{3,19},{19,3},{4,20},{20... | collective-permute-start | bytes 4718600 | tf_op jit(solution)/shard_map/ppermute | solution.py:218
  98.0 5.4 %copy-start.4 = (f32[50,64,1]{2,1,0:T(8,128)S(1)}, f32[50,64,1]{2,1,0:T(8,128)}, u32[]{:S(2)}) copy-start(f32[50,64,1]{2,1,0:T(8,128)} %get-tuple-element.7) | copy-start | bytes 38404
  103.4 5.1 %copy-start.6 = (f32[50,64,128]{2,1,0:T(8,128)S(1)}, f32[50,64,128]{2,1,0:T(8,128)}, u32[]{:S(2)}) copy-start(f32[50,64,128]{2,1,0:T(8,128)} %get-tuple-element.6) | copy-start | bytes 4915204
  106.6 6.9 %collective-permute-start.3 = (f32[2,2,2,1,8,64]{5,4,3,2,1,0:T(8,128)S(1)}, f32[2,2,2,1,8,64]{5,4,3,2,1,0:T(8,128)S(1)}, u32[]{:S(2)}, u32[]{:S(2)}) collective-permute-start(f32[2,2,2,1,8,64]{5,4,3,2,1,0:T(8,128)S(1)} %get-tuple-element.50), channel_id=1, source_target_pairs={{0,1},{1,0},{2,3},{3,2},{4,5},{5,4},{6,7},{7,6},{8,9},{9,8},{10,11... | collective-permute-start | bytes 49160 | tf_op jit(solution)/shard_map/ppermute | solution.py:258
  111.1 1.4 copy-start.5
  113.1 13.7 %collective-permute-start.4 = (bf16[2,2,1,8,64,128]{5,3,2,1,0,4:T(8,128)(2,1)S(1)}, bf16[2,2,1,8,64,128]{5,3,2,1,0,4:T(8,128)(2,1)S(1)}, u32[]{:S(2)}, u32[]{:S(2)}) collective-permute-start(bf16[2,2,1,8,64,128]{5,3,2,1,0,4:T(8,128)(2,1)S(1)} %dynamic-slice_convert_fusion), channel_id=1, source_target_pairs={{0,1},{1,0},{2,3},{3,2},{4,5},{5,4},{6,7},{7,6},{8,9},{9,8},{10,11... | collective-permute-start | bytes 1572872 | tf_op jit(solution)/shard_map/ppermute | solution.py:259
  113.5 3.8 %collective-permute-start.5 = (f32[2,2,1,1,8,64]{5,4,3,2,1,0:T(8,128)S(1)}, f32[2,2,1,1,8,64]{5,4,3,2,1,0:T(8,128)S(1)}, u32[]{:S(2)}, u32[]{:S(2)}) collective-permute-start(f32[2,2,1,1,8,64]{5,4,3,2,1,0:T(8,128)S(1)} %get-tuple-element.56), channel_id=1, source_target_pairs={{0,2},{1,3},{2,0},{3,1},{4,6},{5,7},{6,4},{7,5},{8,10},{9,11},{10,... | collective-permute-start | bytes 24584 | tf_op jit(solution)/shard_map/ppermute | solution.py:258
  117.3 13.1 %collective-permute-start.7 = (f32[2,1,1,1,8,64]{5,4,3,2,1,0:T(8,128)S(1)}, f32[2,1,1,1,8,64]{5,4,3,2,1,0:T(8,128)S(1)}, u32[]{:S(2)}, u32[]{:S(2)}) collective-permute-start(f32[2,1,1,1,8,64]{5,4,3,2,1,0:T(8,128)S(1)} %get-tuple-element.60), channel_id=1, source_target_pairs={{0,4},{1,5},{2,6},{3,7},{4,0},{5,1},{6,2},{7,3},{8,12},{9,13},{10,... | collective-permute-start | bytes 12296 | tf_op jit(solution)/shard_map/ppermute | solution.py:258
  128.8 7.3 %collective-permute-start.6 = (bf16[2,1,1,8,64,128]{5,3,2,1,0,4:T(8,128)(2,1)S(1)}, bf16[2,1,1,8,64,128]{5,3,2,1,0,4:T(8,128)(2,1)S(1)}, u32[]{:S(2)}, u32[]{:S(2)}) collective-permute-start(bf16[2,1,1,8,64,128]{5,3,2,1,0,4:T(8,128)(2,1)S(1)} %dynamic-slice_convert_fusion.1), channel_id=1, source_target_pairs={{0,2},{1,3},{2,0},{3,1},{4,6},{5,7},{6,4},{7,5},{8,10},{9,11},{10,... | collective-permute-start | bytes 786440 | tf_op jit(solution)/shard_map/ppermute | solution.py:259
  136.4 7.3 %collective-permute-start.8 = (bf16[1,1,1,8,64,128]{5,3,2,1,0,4:T(8,128)(2,1)S(1)}, bf16[1,1,1,8,64,128]{5,3,2,1,0,4:T(8,128)(2,1)S(1)}, u32[]{:S(2)}, u32[]{:S(2)}) collective-permute-start(bf16[1,1,1,8,64,128]{5,3,2,1,0,4:T(8,128)(2,1)S(1)} %dynamic-slice_convert_fusion.2), channel_id=1, source_target_pairs={{0,4},{1,5},{2,6},{3,7},{4,0},{5,1},{6,2},{7,3},{8,12},{9,13},{10,... | collective-permute-start | bytes 393224 | tf_op jit(solution)/shard_map/ppermute | solution.py:259
  152.5 6.3 %collective-permute-start.9 = (bf16[1,8,4,2560]{3,1,2,0:T(8,128)(2,1)S(1)}, bf16[1,8,4,2560]{3,1,2,0:T(8,128)(2,1)S(1)}, u32[]{:S(2)}, u32[]{:S(2)}) collective-permute-start(bf16[1,8,4,2560]{3,1,2,0:T(8,128)(2,1)S(1)} %constant_dynamic-slice_fusion), channel_id=1, source_target_pairs={{0,8},{8,0},{1,9},{9,1},{2,10},{10,2},{3,11},{11,3},{4,12},{12,4},... | collective-permute-start | bytes 491528 | tf_op jit(solution)/shard_map/ppermute | solution.py:218
  158.9 9.9 %collective-permute-start.10 = (bf16[1,8,4,2560]{3,1,2,0:T(8,128)(2,1)S(1)}, bf16[1,8,4,2560]{3,1,2,0:T(8,128)(2,1)S(1)}, u32[]{:S(2)}, u32[]{:S(2)}) collective-permute-start(bf16[1,8,4,2560]{3,1,2,0:T(8,128)(2,1)S(1)} %add_convert_fusion.1), channel_id=1, source_target_pairs={{0,4},{1,5},{2,6},{3,7},{4,0},{5,1},{6,2},{7,3},{8,12},{9,13},{10,... | collective-permute-start | bytes 491528 | tf_op jit(solution)/shard_map/ppermute | solution.py:231
  168.9 8.8 %collective-permute-start.11 = (bf16[2,1,8,4,2560]{4,2,3,1,0:T(8,128)(2,1)S(1)}, bf16[2,1,8,4,2560]{4,2,3,1,0:T(8,128)(2,1)S(1)}, u32[]{:S(2)}, u32[]{:S(2)}) collective-permute-start(bf16[2,1,8,4,2560]{4,2,3,1,0:T(8,128)(2,1)S(1)} %maximum_select_fusion.4), channel_id=1, source_target_pairs={{0,2},{1,3},{2,0},{3,1},{4,6},{5,7},{6,4},{7,5},{8,10},{9,11},{10,... | collective-permute-start | bytes 983048 | tf_op jit(solution)/shard_map/ppermute | solution.py:231
  177.7 14.9 %collective-permute-start.12 = (bf16[2,2,1,8,4,2560]{5,3,4,1,2,0:T(8,128)(2,1)S(1)}, bf16[2,2,1,8,4,2560]{5,3,4,1,2,0:T(8,128)(2,1)S(1)}, u32[]{:S(2)}, u32[]{:S(2)}) collective-permute-start(bf16[2,2,1,8,4,2560]{5,3,4,1,2,0:T(8,128)(2,1)S(1)} %maximum_select_fusion.2), channel_id=1, source_target_pairs={{0,1},{1,0},{2,3},{3,2},{4,5},{5,4},{6,7},{7,6},{8,9},{9,8},{10,11... | collective-permute-start | bytes 1966088 | tf_op jit(solution)/shard_map/ppermute | solution.py:231
  192.6 2.4 %copy-start.1 = (bf16[2560,512]{1,0:T(8,128)(2,1)S(1)}, bf16[2560,512]{1,0:T(8,128)(2,1)}, u32[]{:S(2)}) copy-start(bf16[2560,512]{1,0:T(8,128)(2,1)} %param.14) | copy-start | bytes 7864324

commit v7 on v6

--- a/solution.py
+++ b/solution.py
@@ -298,7 +298,14 @@
     own_states = states.reshape(token_count, -1)
     side = lax.axis_index("col")
     swap = [(0, 1), (1, 0)]
-    other_states = lax.ppermute(own_states, "col", swap)
+    half = token_count // 2
+    other_states = jnp.concatenate(
+        [
+            lax.ppermute(own_states[:half], "col", swap),
+            lax.ppermute(own_states[half:], "col", swap),
+        ],
+        0,
+    )
     as_float = own_states.astype(jnp.float32)
     squares = lax.psum(jnp.sum(as_float * as_float, -1), "row")
     other_squares = lax.ppermute(squares, "col", swap)

time: 196 us -> 197 us (level)
  local copies, waits for them, and re-layouts: 34.5 us -> 41.6 us
  waiting for transfers between devices: 75.5 us -> 69.2 us
  starting transfers between devices: 17.5 us -> 19.5 us
    ppermute x1, waiting for transfers between devices: 24.4 us -> 18 us  [on_device(): other_squares = lax.ppermute(squares, 'col', swap)]
    slice x0 -> x3, local copies, waits for them, and re-layouts: none -> 5.95 us  [the longest x2 3.74 us: on_device(): own_states[half:]]
    ppermute x1, starting transfers between devices: 0.01 us -> 2.02 us  [on_device(): other_squares = lax.ppermute(squares, 'col', swap)]
    unnamed x27 -> x30, local copies, waits for them, and re-layouts: 6.29 us -> 7.37 us
  transfers between devices with their start and end apart: 13 -> 14, of which waited for: 10 -> 10; matrix products, arithmetic and copies ran while one was open for 8% -> 11% of each run, Pallas kernels for 0% -> 0%
where the time goes in v7:
time: 197 us; the launch traced here: 196 us
  waiting for transfers between devices  69.2 us (35%)
  local copies, waits for them, and re-layouts  41.6 us (21%)
  other arithmetic  23.9 us (12%)
  starting transfers between devices  19.5 us (10%)
  matrix products  18.8 us (10%)
  Pallas kernels  17.3 us (9%)
  blocking collectives  4.46 us (2%)
    ppermute x3, waiting for transfers between devices, doubling_gather(): got = lax.ppermute(block, axis_name, pairs)  28.8 us
    ppermute x1, waiting for transfers between devices, on_device(): other_squares = lax.ppermute(squares, 'col', swap)  18 us
    pallas_call x1, Pallas kernels, slot_attention(): pl.pallas_call(partial(slot_kernel, ns=ns, heads=heads, qpk=qpk), grid_sp...  17.3 us
    ppermute x3, waiting for transfers between devices, seq_merge(): lax.ppermute(send_values.astype(jnp.bfloat16), 'seq', pairs)  15 us
    dot_general x3, matrix products, on_device(): jnp.dot(gathered, matrix, preferred_element_type=jnp.float32)  8.8 us
    unnamed x30, local copies, waits for them, and re-layouts  7.37 us
    ppermute x3, starting transfers between devices, seq_merge(): got_stats = lax.ppermute(send_stats, 'seq', pairs)  6.64 us
    dot_general x1, matrix products, on_device(): jnp.dot(piece_rows.reshape(n_row * per * step_count, -1), wo, preferred_e...  5.88 us
  transfers between devices with their start and end apart: 14, of which 10 were waited for; matrix products, arithmetic and copies ran while one was open for 11% of the time, Pallas kernels for 0%

profile of v7, /device:TPU:0, one launch (start us, length us, event | category | flops | bytes accessed | tf_op | source)
XLA Modules:
  0.0 195.9 jit_solution(7874015693054887294)
XLA Ops:
  0.6 2.7 %fusion.59 = (bf16[32,4,2560]{2,1,0:T(4,128)(2,1)S(1)}, bf16[32,4,2560]{2,1,0:T(4,128)(2,1)}) fusion(bf16[64,4,2560]{2,1,0:T(4,128)(2,1)} %param.11), kind=kLoop, calls=%fused_computation.143 | loop fusion | bytes 2621440 | tf_op jit(solution)/shard_map/slice | solution.py:305
  3.4 2.2 %slice.80 = bf16[128,2560]{1,0:T(8,128)(2,1)} reshape(bf16[32,4,2560]{2,1,0:T(4,128)(2,1)} %get-tuple-element.42) | data formatting | bytes 1310720 | tf_op jit(solution)/shard_map/slice | solution.py:304
  5.6 2.9 %collective-permute-start = (bf16[128,2560]{1,0:T(8,128)(2,1)}, bf16[128,2560]{1,0:T(8,128)(2,1)}, u32[]{:S(2)}, u32[]{:S(2)}) collective-permute-start(bf16[128,2560]{1,0:T(8,128)(2,1)} %slice.80), channel_id=1, source_target_pairs={{0,8},{8,0},{1,9},{9,1},{2,10},{10,2},{3,11},{11,3},{4,12},{12,4},... | collective-permute-start | bytes 1966088 | tf_op jit(solution)/shard_map/ppermute | solution.py:304
  8.5 1.0 slice.82
  9.5 2.1 %multiply_reduce_fusion = f32[64,4]{1,0:T(8,128)S(1)} fusion(bf16[64,4,2560]{2,1,0:T(4,128)(2,1)} %param.11), kind=kLoop, calls=%fused_computation.12 | loop fusion | flops 1965824 | bytes 1311744 | tf_op jit(solution)/shard_map/reduce_sum | solution.py:310
  11.7 2.5 %psum.7 = f32[256]{0:T(256)S(1)} all-reduce(f32[256]{0:T(256)S(1)} %reduce_sum.21), channel_id=1, replica_groups=mesh['row'=2,'col'=2,'seq'=8] {'row'}, use_global_device_ids=true, to_apply=%region_1.0 | all-reduce | flops 256 | bytes 2048 | tf_op jit(solution)/shard_map/psum | solution.py:310
  14.2 2.0 %collective-permute-start.2 = (f32[256]{0:T(256)S(1)}, f32[256]{0:T(256)S(1)}, u32[]{:S(2)}, u32[]{:S(2)}) collective-permute-start(f32[256]{0:T(256)S(1)} %psum.7), channel_id=1, source_target_pairs={{0,8},{8,0},{1,9},{9,1},{2,10},{10,2},{3,11},{11,3},{4,12},{12,4},... | collective-permute-start | bytes 3080 | tf_op jit(solution)/shard_map/ppermute | solution.py:311
  16.2 3.4 %reshape.812 = bf16[256,2560]{1,0:T(8,128)(2,1)} reshape(bf16[64,4,2560]{2,1,0:T(4,128)(2,1)} %param.11) | data formatting | bytes 2621440 | tf_op jit(solution)/shard_map/reshape | solution.py:298
  19.6 18.0 %collective-permute-done.2 = f32[256]{0:T(256)S(1)} collective-permute-done((f32[256]{0:T(256)S(1)}, f32[256]{0:T(256)S(1)}, u32[]{:S(2)}, u32[]{:S(2)}) %collective-permute-start.2) | collective-permute-done | bytes 1056 | tf_op jit(solution)/shard_map/ppermute | solution.py:311
  37.6 1.1 constant_dynamic-update-slice_fusion.1
  38.8 1.0 multiply_convert_fusion.1
  39.8 1.5 convolution_convert_fusion.2
  41.4 1.5 convolution_convert_fusion.1
  43.4 0.7 slice-done.2
  44.0 5.8 %convolution_convert_fusion = bf16[512,2048]{1,0:T(8,128)(2,1)S(1)} fusion(bf16[2560,2048]{1,0:T(8,128)(2,1)S(1)} %bitcast.168, bf16[256,2560]{1,0:T(8,128)(2,1)S(1)} %get-tuple-element.38, bf16[256,2560]{1,0:T(8,128)(2,1)S(1)} %get-tuple-element.37), kind=kOutput, calls=%fused_computation.8 | convolution fusion | flops 5375000576 | bytes 15204352 | tf_op jit(solution)/shard_map/dot_general | solution.py:330
  50.1 1.6 copy-done.3
  51.8 1.3 constant_dynamic-slice_fusion.1
  53.1 0.8 gather_fusion
  54.0 1.1 multiply_cosine_fusion
  55.1 0.5 compare_select_fusion.1.len_ref
  55.7 1.0 collective-permute-done.3
  56.7 3.6 %convert_add_fusion = f32[1,256,3072]{2,1,0:T(8,128)} fusion(bf16[1,256,3072]{2,1,0:T(8,128)(2,1)S(1)} %collective-permute-done.3, bf16[2,256,3072]{2,1,0:T(8,128)(2,1)} %copy-done.3, s32[]{:T(128)S(6)} %select_n.191), kind=kLoop, calls=%fused_computation.7 | loop fusion | flops 2359296 | bytes 6291460 | tf_op jit(solution)/shard_map/add | solution.py:219
  60.3 4.8 %reshape_squeeze.7 = f32[64,4,3072]{2,1,0:T(4,128)} reshape(f32[1,256,3072]{2,1,0:T(8,128)} %convert_add_fusion) | data formatting | bytes 6291456 | tf_op jit(solution)/shard_map/reshape;squeeze | solution.py:340
  65.1 1.1 slice_bitcast_fusion.3
  66.2 1.1 slice_bitcast_fusion
  67.3 3.2 %slice.108 = f32[64,4,2048]{2,1,0:T(4,128)} slice(f32[64,4,3072]{2,1,0:T(4,128)} %reshape_squeeze.7), slice={[0:64], [0:4], [0:2048]} | slice | bytes 4194304 | tf_op jit(solution)/shard_map/slice | solution.py:344
  71.0 2.5 %reshape.850 = f32[64,4,16,128]{3,2,1,0:T(8,128)S(1)} reshape(f32[64,4,2048]{2,1,0:T(4,128)} %slice.108) | data formatting | bytes 4194304 | tf_op jit(solution)/shard_map/reshape | solution.py:344
  73.5 0.7 fusion.58
  74.3 0.6 subtract_convert_fusion
  74.8 1.4 pad_maximum_fusion.2
  76.3 0.6 copy.215
  77.2 1.2 fusion.13
  79.0 1.6 gather_fusion.1
  80.7 0.8 fusion.15
  81.5 17.3 %shard_map.130 = (f32[50,64,1]{2,1,0:T(8,128)}, f32[50,64,1]{2,1,0:T(8,128)}, f32[50,64,128]{2,1,0:T(8,128)}) custom-call(s32[50]{0:T(128)} %compare_select_fusion.1.len_ref, s32[50]{0:T(128)} %blk_ref.1, bf16[50,64,128]{2,1,0:T(8,128)(2,1)} %gather_fusion.1, bf16[50,128,512]{2,1,0:T(8,128)(2,1)} %k_ref.1, bf16[50,128,512]{2,1,0:T(8,128)(2,1)} %v_ref.1), custom_call_target="tpu_custom_call" | custom-call | tf_op jit(solution)/shard_map/pallas_call | solution.py:189
  98.8 2.0 %reduce.1 = f32[50,64]{1,0:T(8,128)S(1)} reduce(f32[50,64,1]{2,1,0:T(8,128)} %get-tuple-element.7, f32[]{:T(128)} %constant.111), dimensions={2}, to_apply=%get-tuple-element.7.reduce_sub_computation | reduce | bytes 25604 | tf_op jit(solution)/shard_map/pallas_call | solution.py:189
  100.9 0.9 select_reduce_fusion
  101.8 0.6 gather_fusion.2
  102.4 1.8 copy.173
  104.2 3.0 %multiply_reduce_fusion.1 = (f32[50,64]{1,0:T(8,128)S(1)}, f32[50,64]{1,0:T(8,128)S(1)}) fusion(f32[50,64,1]{2,1,0:T(8,128)} %get-tuple-element.8, f32[50,64,1]{2,1,0:T(8,128)S(1)} %copy-done.4, f32[50,64,1]{2,1,0:T(8,128)} %copy.173), kind=kLoop, calls=%fused_computation.17 | loop fusion | flops 6400 | bytes 64000 | tf_op jit(solution)/shard_map/mul | solution.py:379
  107.4 1.8 collective-permute-start.4
  109.7 2.2 %fusion.5 = f32[64,64,128]{2,0,1:T(8,128)S(1)} fusion(f32[50,64,128]{2,1,0:T(8,128)S(1)} %broadcast_multiply_fusion, s32[50]{0:T(128)S(1)} %copy-done.9), kind=kOutput, calls=%fused_computation.15 | convolution fusion | flops 314576000 | bytes 3735752 | tf_op jit(solution)/shard_map/rn,njh->rjh/dot_general | solution.py:381
  111.9 1.4 copy-done.5
  114.3 1.9 collective-permute-start.6
  116.5 1.6 collective-permute-done.6
  118.1 2.9 %collective-permute-start.8 = (f32[2,1,1,1,8,64]{5,4,3,2,1,0:T(8,128)S(1)}, f32[2,1,1,1,8,64]{5,4,3,2,1,0:T(8,128)S(1)}, u32[]{:S(2)}, u32[]{:S(2)}) collective-permute-start(f32[2,1,1,1,8,64]{5,4,3,2,1,0:T(8,128)S(1)} %get-tuple-element.62), channel_id=1, source_target_pairs={{0,4},{1,5},{2,6},{3,7},{4,0},{5,1},{6,2},{7,3},{8,12},{9,13},{10,... | collective-permute-start | bytes 12296 | tf_op jit(solution)/shard_map/ppermute | solution.py:258
  121.3 6.4 %collective-permute-done.5 = bf16[2,2,1,8,64,128]{5,3,2,1,0,4:T(8,128)(2,1)S(1)} collective-permute-done((bf16[2,2,1,8,64,128]{5,3,2,1,0,4:T(8,128)(2,1)S(1)}, bf16[2,2,1,8,64,128]{5,3,2,1,0,4:T(8,128)(2,1)S(1)}, u32[]{:S(2)}, u32[]{:S(2)}) %collective-permute-start.5) | collective-permute-done | bytes 524320 | tf_op jit(solution)/shard_map/ppermute | solution.py:259
  127.7 1.8 multiply_add_fusion
  129.6 1.6 collective-permute-start.7
  131.5 5.3 %collective-permute-done.7 = bf16[2,1,1,8,64,128]{5,3,2,1,0,4:T(8,128)(2,1)S(1)} collective-permute-done((bf16[2,1,1,8,64,128]{5,3,2,1,0,4:T(8,128)(2,1)S(1)}, bf16[2,1,1,8,64,128]{5,3,2,1,0,4:T(8,128)(2,1)S(1)}, u32[]{:S(2)}, u32[]{:S(2)}) %collective-permute-start.7) | collective-permute-done | bytes 262176 | tf_op jit(solution)/shard_map/ppermute | solution.py:259
  137.2 2.7 %collective-permute-start.9 = (bf16[1,1,1,8,64,128]{5,3,2,1,0,4:T(8,128)(2,1)S(1)}, bf16[1,1,1,8,64,128]{5,3,2,1,0,4:T(8,128)(2,1)S(1)}, u32[]{:S(2)}, u32[]{:S(2)}) collective-permute-start(bf16[1,1,1,8,64,128]{5,3,2,1,0,4:T(8,128)(2,1)S(1)} %dynamic-slice_convert_fusion.2), channel_id=1, source_target_pairs={{0,4},{1,5},{2,6},{3,7},{4,0},{5,1},{6,2},{7,3},{8,12},{9,13},{10,... | collective-permute-start | bytes 393224 | tf_op jit(solution)/shard_map/ppermute | solution.py:259
  139.9 0.8 multiply_add_fusion.4
  141.3 3.3 %collective-permute-done.9 = bf16[1,1,1,8,64,128]{5,3,2,1,0,4:T(8,128)(2,1)S(1)} collective-permute-done((bf16[1,1,1,8,64,128]{5,3,2,1,0,4:T(8,128)(2,1)S(1)}, bf16[1,1,1,8,64,128]{5,3,2,1,0,4:T(8,128)(2,1)S(1)}, u32[]{:S(2)}, u32[]{:S(2)}) %collective-permute-start.9) | collective-permute-done | bytes 131104 | tf_op jit(solution)/shard_map/ppermute | solution.py:259
  145.4 2.0 %all_gather.4 = bf16[2,8,4,2048]{3,1,2,0:T(8,128)(2,1)S(1)} all-gather(bf16[1,8,4,2048]{3,1,2,0:T(8,128)(2,1)S(1)} %convert_element_type.122), channel_id=1, replica_groups=mesh['row'=2,'col'=2,'seq'=8] {'row'}, dimensions={0}, use_global_device_ids=true | all-gather | bytes 393216 | tf_op jit(solution)/shard_map/all_gather | solution.py:410
  147.4 5.9 %fusion.2 = bf16[2,8,4,2560]{3,1,2,0:T(8,128)(2,1)S(1)} fusion(bf16[2,8,4,2048]{3,1,2,0:T(8,128)(2,1)S(1)} %all_gather.4, bf16[2048,2560]{1,0:T(8,128)(2,1)} %param.16), kind=kOutput, calls=%fused_computation.5 | convolution fusion | flops 671252480 | bytes 11075584 | tf_op jit(solution)/shard_map/dot_general | solution.py:412
  153.3 1.5 collective-permute-start.10
  154.9 4.8 %collective-permute-done.10 = bf16[1,8,4,2560]{3,1,2,0:T(8,128)(2,1)S(1)} collective-permute-done((bf16[1,8,4,2560]{3,1,2,0:T(8,128)(2,1)S(1)}, bf16[1,8,4,2560]{3,1,2,0:T(8,128)(2,1)S(1)}, u32[]{:S(2)}, u32[]{:S(2)}) %collective-permute-start.10) | collective-permute-done | bytes 163872 | tf_op jit(solution)/shard_map/ppermute | solution.py:218
  159.7 1.4 collective-permute-start.11
  161.1 8.5 %collective-permute-done.11 = bf16[1,8,4,2560]{3,1,2,0:T(8,128)(2,1)S(1)} collective-permute-done((bf16[1,8,4,2560]{3,1,2,0:T(8,128)(2,1)S(1)}, bf16[1,8,4,2560]{3,1,2,0:T(8,128)(2,1)S(1)}, u32[]{:S(2)}, u32[]{:S(2)}) %collective-permute-start.11) | collective-permute-done | bytes 163872 | tf_op jit(solution)/shard_map/ppermute | solution.py:231
  169.8 8.6 %collective-permute-done.12 = bf16[2,1,8,4,2560]{4,2,3,1,0:T(8,128)(2,1)S(1)} collective-permute-done((bf16[2,1,8,4,2560]{4,2,3,1,0:T(8,128)(2,1)S(1)}, bf16[2,1,8,4,2560]{4,2,3,1,0:T(8,128)(2,1)S(1)}, u32[]{:S(2)}, u32[]{:S(2)}) %collective-permute-start.12) | collective-permute-done | bytes 327712 | tf_op jit(solution)/shard_map/ppermute | solution.py:231
  178.8 1.8 slice.183
  180.6 1.1 fusion.65
  181.8 11.6 %collective-permute-done.13 = bf16[2,2,1,8,4,2560]{5,3,4,1,2,0:T(8,128)(2,1)S(1)} collective-permute-done((bf16[2,2,1,8,4,2560]{5,3,4,1,2,0:T(8,128)(2,1)S(1)}, bf16[2,2,1,8,4,2560]{5,3,4,1,2,0:T(8,128)(2,1)S(1)}, u32[]{:S(2)}, u32[]{:S(2)}) %collective-permute-start.13) | collective-permute-done | bytes 655392 | tf_op jit(solution)/shard_map/ppermute | solution.py:231
  193.8 2.1 %copy.205 = bf16[64,4,2560]{2,1,0:T(4,128)(2,1)} copy(bf16[64,4,2560]{2,0,1:T(8,128)(2,1)S(1)} %bitcast.143) | data formatting | bytes 2621440
  (92 shorter events, 8.2 us)
Async XLA Ops:
  0.6 39.2 %copy-start = (bf16[2560,512]{1,0:T(8,128)(2,1)S(1)}, bf16[2560,512]{1,0:T(8,128)(2,1)}, u32[]{:S(2)}) copy-start(bf16[2560,512]{1,0:T(8,128)(2,1)} %param.14) | copy-start | bytes 7864324
  5.6 32.0 %collective-permute-start = (bf16[128,2560]{1,0:T(8,128)(2,1)}, bf16[128,2560]{1,0:T(8,128)(2,1)}, u32[]{:S(2)}, u32[]{:S(2)}) collective-permute-start(bf16[128,2560]{1,0:T(8,128)(2,1)} %slice.80), channel_id=1, source_target_pairs={{0,8},{8,0},{1,9},{9,1},{2,10},{10,2},{3,11},{11,3},{4,12},{12,4},... | collective-permute-start | bytes 1966088 | tf_op jit(solution)/shard_map/ppermute | solution.py:304
  9.5 29.2 %collective-permute-start.1 = (bf16[128,2560]{1,0:T(8,128)(2,1)}, bf16[128,2560]{1,0:T(8,128)(2,1)S(1)}, u32[]{:S(2)}, u32[]{:S(2)}) collective-permute-start(bf16[128,2560]{1,0:T(8,128)(2,1)} %slice.82), channel_id=1, source_target_pairs={{0,8},{8,0},{1,9},{9,1},{2,10},{10,2},{3,11},{11,3},{4,12},{12,4},... | collective-permute-start | bytes 1966088 | tf_op jit(solution)/shard_map/ppermute | solution.py:305
  14.2 23.4 %collective-permute-start.2 = (f32[256]{0:T(256)S(1)}, f32[256]{0:T(256)S(1)}, u32[]{:S(2)}, u32[]{:S(2)}) collective-permute-start(f32[256]{0:T(256)S(1)} %psum.7), channel_id=1, source_target_pairs={{0,8},{8,0},{1,9},{9,1},{2,10},{10,2},{3,11},{11,3},{4,12},{12,4},... | collective-permute-start | bytes 3080 | tf_op jit(solution)/shard_map/ppermute | solution.py:311
  16.2 22.6 %copy-start.8 = (f32[2560]{0:T(1024)S(1)}, f32[2560]{0:T(1024)}, u32[]{:S(2)}) copy-start(f32[2560]{0:T(1024)} %param.12) | copy-start | bytes 30724
  19.6 19.2 %copy-start.6 = (bf16[256,2560]{1,0:T(8,128)(2,1)S(1)}, bf16[256,2560]{1,0:T(8,128)(2,1)}, u32[]{:S(2)}) copy-start(bf16[256,2560]{1,0:T(8,128)(2,1)} %reshape.812) | copy-start | bytes 3932164
  38.8 2.5 %copy-start.10 = (bf16[2560,512]{1,0:T(8,128)(2,1)S(1)}, bf16[2560,512]{1,0:T(8,128)(2,1)}, u32[]{:S(2)}) copy-start(bf16[2560,512]{1,0:T(8,128)(2,1)} %param.15) | copy-start | bytes 7864324
  39.8 3.1 %slice-start = ((s8[10485760]{0:T(1024)(128)(4,1)}), s8[4194304]{0:T(1024)(128)(4,1)S(1)}, s32[]{:S(2)}) async-start(s8[10485760]{0:T(1024)(128)(4,1)} %bitcast.167), calls=%async_computation | async-start | bytes 8388608
  39.8 3.6 %slice-start.1 = ((s8[10485760]{0:T(1024)(128)(4,1)}), s8[4194304]{0:T(1024)(128)(4,1)S(1)}, s32[]{:S(2)}) async-start(s8[10485760]{0:T(1024)(128)(4,1)} %bitcast.167), calls=%async_computation.1 | async-start | bytes 8388608
  41.3 2.7 %slice-start.2 = ((s8[10485760]{0:T(1024)(128)(4,1)}), s8[2097152]{0:T(1024)(128)(4,1)S(1)}, s32[]{:S(2)}) async-start(s8[10485760]{0:T(1024)(128)(4,1)} %bitcast.167), calls=%async_computation.2 | async-start | bytes 4194304
  50.1 1.6 copy-start.3
  51.8 1.3 copy-start.9
  51.8 1.3 copy-start.2
  53.1 3.6 %collective-permute-start.3 = (bf16[1,256,3072]{2,1,0:T(8,128)(2,1)}, bf16[1,256,3072]{2,1,0:T(8,128)(2,1)S(1)}, u32[]{:S(2)}, u32[]{:S(2)}) collective-permute-start(bf16[1,256,3072]{2,1,0:T(8,128)(2,1)} %constant_dynamic-slice_fusion.1), channel_id=1, source_target_pairs={{0,16},{16,0},{1,17},{17,1},{2,18},{18,2},{3,19},{19,3},{4,20},{20... | collective-permute-start | bytes 4718600 | tf_op jit(solution)/shard_map/ppermute | solution.py:218
  98.8 5.4 %copy-start.4 = (f32[50,64,1]{2,1,0:T(8,128)S(1)}, f32[50,64,1]{2,1,0:T(8,128)}, u32[]{:S(2)}) copy-start(f32[50,64,1]{2,1,0:T(8,128)} %get-tuple-element.7) | copy-start | bytes 38404
  104.2 5.1 %copy-start.7 = (f32[50,64,128]{2,1,0:T(8,128)S(1)}, f32[50,64,128]{2,1,0:T(8,128)}, u32[]{:S(2)}) copy-start(f32[50,64,128]{2,1,0:T(8,128)} %get-tuple-element.6) | copy-start | bytes 4915204
  107.4 6.8 %collective-permute-start.4 = (f32[2,2,2,1,8,64]{5,4,3,2,1,0:T(8,128)S(1)}, f32[2,2,2,1,8,64]{5,4,3,2,1,0:T(8,128)S(1)}, u32[]{:S(2)}, u32[]{:S(2)}) collective-permute-start(f32[2,2,2,1,8,64]{5,4,3,2,1,0:T(8,128)S(1)} %get-tuple-element.52), channel_id=1, source_target_pairs={{0,1},{1,0},{2,3},{3,2},{4,5},{5,4},{6,7},{7,6},{8,9},{9,8},{10,11... | collective-permute-start | bytes 49160 | tf_op jit(solution)/shard_map/ppermute | solution.py:258
  111.9 1.4 copy-start.5
  113.9 13.8 %collective-permute-start.5 = (bf16[2,2,1,8,64,128]{5,3,2,1,0,4:T(8,128)(2,1)S(1)}, bf16[2,2,1,8,64,128]{5,3,2,1,0,4:T(8,128)(2,1)S(1)}, u32[]{:S(2)}, u32[]{:S(2)}) collective-permute-start(bf16[2,2,1,8,64,128]{5,3,2,1,0,4:T(8,128)(2,1)S(1)} %dynamic-slice_convert_fusion), channel_id=1, source_target_pairs={{0,1},{1,0},{2,3},{3,2},{4,5},{5,4},{6,7},{7,6},{8,9},{9,8},{10,11... | collective-permute-start | bytes 1572872 | tf_op jit(solution)/shard_map/ppermute | solution.py:259
  114.3 3.8 %collective-permute-start.6 = (f32[2,2,1,1,8,64]{5,4,3,2,1,0:T(8,128)S(1)}, f32[2,2,1,1,8,64]{5,4,3,2,1,0:T(8,128)S(1)}, u32[]{:S(2)}, u32[]{:S(2)}) collective-permute-start(f32[2,2,1,1,8,64]{5,4,3,2,1,0:T(8,128)S(1)} %get-tuple-element.58), channel_id=1, source_target_pairs={{0,2},{1,3},{2,0},{3,1},{4,6},{5,7},{6,4},{7,5},{8,10},{9,11},{10,... | collective-permute-start | bytes 24584 | tf_op jit(solution)/shard_map/ppermute | solution.py:258
  118.1 13.1 %collective-permute-start.8 = (f32[2,1,1,1,8,64]{5,4,3,2,1,0:T(8,128)S(1)}, f32[2,1,1,1,8,64]{5,4,3,2,1,0:T(8,128)S(1)}, u32[]{:S(2)}, u32[]{:S(2)}) collective-permute-start(f32[2,1,1,1,8,64]{5,4,3,2,1,0:T(8,128)S(1)} %get-tuple-element.62), channel_id=1, source_target_pairs={{0,4},{1,5},{2,6},{3,7},{4,0},{5,1},{6,2},{7,3},{8,12},{9,13},{10,... | collective-permute-start | bytes 12296 | tf_op jit(solution)/shard_map/ppermute | solution.py:258
  129.6 7.3 %collective-permute-start.7 = (bf16[2,1,1,8,64,128]{5,3,2,1,0,4:T(8,128)(2,1)S(1)}, bf16[2,1,1,8,64,128]{5,3,2,1,0,4:T(8,128)(2,1)S(1)}, u32[]{:S(2)}, u32[]{:S(2)}) collective-permute-start(bf16[2,1,1,8,64,128]{5,3,2,1,0,4:T(8,128)(2,1)S(1)} %dynamic-slice_convert_fusion.1), channel_id=1, source_target_pairs={{0,2},{1,3},{2,0},{3,1},{4,6},{5,7},{6,4},{7,5},{8,10},{9,11},{10,... | collective-permute-start | bytes 786440 | tf_op jit(solution)/shard_map/ppermute | solution.py:259
  137.2 7.3 %collective-permute-start.9 = (bf16[1,1,1,8,64,128]{5,3,2,1,0,4:T(8,128)(2,1)S(1)}, bf16[1,1,1,8,64,128]{5,3,2,1,0,4:T(8,128)(2,1)S(1)}, u32[]{:S(2)}, u32[]{:S(2)}) collective-permute-start(bf16[1,1,1,8,64,128]{5,3,2,1,0,4:T(8,128)(2,1)S(1)} %dynamic-slice_convert_fusion.2), channel_id=1, source_target_pairs={{0,4},{1,5},{2,6},{3,7},{4,0},{5,1},{6,2},{7,3},{8,12},{9,13},{10,... | collective-permute-start | bytes 393224 | tf_op jit(solution)/shard_map/ppermute | solution.py:259
  153.3 6.3 %collective-permute-start.10 = (bf16[1,8,4,2560]{3,1,2,0:T(8,128)(2,1)S(1)}, bf16[1,8,4,2560]{3,1,2,0:T(8,128)(2,1)S(1)}, u32[]{:S(2)}, u32[]{:S(2)}) collective-permute-start(bf16[1,8,4,2560]{3,1,2,0:T(8,128)(2,1)S(1)} %constant_dynamic-slice_fusion), channel_id=1, source_target_pairs={{0,8},{8,0},{1,9},{9,1},{2,10},{10,2},{3,11},{11,3},{4,12},{12,4},... | collective-permute-start | bytes 491528 | tf_op jit(solution)/shard_map/ppermute | solution.py:218
  159.7 9.9 %collective-permute-start.11 = (bf16[1,8,4,2560]{3,1,2,0:T(8,128)(2,1)S(1)}, bf16[1,8,4,2560]{3,1,2,0:T(8,128)(2,1)S(1)}, u32[]{:S(2)}, u32[]{:S(2)}) collective-permute-start(bf16[1,8,4,2560]{3,1,2,0:T(8,128)(2,1)S(1)} %add_convert_fusion.1), channel_id=1, source_target_pairs={{0,4},{1,5},{2,6},{3,7},{4,0},{5,1},{6,2},{7,3},{8,12},{9,13},{10,... | collective-permute-start | bytes 491528 | tf_op jit(solution)/shard_map/ppermute | solution.py:231
  169.7 8.8 %collective-permute-start.12 = (bf16[2,1,8,4,2560]{4,2,3,1,0:T(8,128)(2,1)S(1)}, bf16[2,1,8,4,2560]{4,2,3,1,0:T(8,128)(2,1)S(1)}, u32[]{:S(2)}, u32[]{:S(2)}) collective-permute-start(bf16[2,1,8,4,2560]{4,2,3,1,0:T(8,128)(2,1)S(1)} %maximum_select_fusion.4), channel_id=1, source_target_pairs={{0,2},{1,3},{2,0},{3,1},{4,6},{5,7},{6,4},{7,5},{8,10},{9,11},{10,... | collective-permute-start | bytes 983048 | tf_op jit(solution)/shard_map/ppermute | solution.py:231
  178.5 14.9 %collective-permute-start.13 = (bf16[2,2,1,8,4,2560]{5,3,4,1,2,0:T(8,128)(2,1)S(1)}, bf16[2,2,1,8,4,2560]{5,3,4,1,2,0:T(8,128)(2,1)S(1)}, u32[]{:S(2)}, u32[]{:S(2)}) collective-permute-start(bf16[2,2,1,8,4,2560]{5,3,4,1,2,0:T(8,128)(2,1)S(1)} %maximum_select_fusion.2), channel_id=1, source_target_pairs={{0,1},{1,0},{2,3},{3,2},{4,5},{5,4},{6,7},{7,6},{8,9},{9,8},{10,11... | collective-permute-start | bytes 1966088 | tf_op jit(solution)/shard_map/ppermute | solution.py:231
  193.4 2.4 %copy-start.1 = (bf16[2560,512]{1,0:T(8,128)(2,1)S(1)}, bf16[2560,512]{1,0:T(8,128)(2,1)}, u32[]{:S(2)}) copy-start(bf16[2560,512]{1,0:T(8,128)(2,1)} %param.14) | copy-start | bytes 7864324

commit v8 on v6

--- a/solution.py
+++ b/solution.py
@@ -322,6 +322,315 @@
     parts_out = [
         jnp.dot(gathered, matrix, preferred_element_type=jnp.float32) for matrix in (wq, wk, wv)
     ]
+    head_count = (q_width + 2 * k_width) // HEAD_SIZE
+    output_projected = pair_scatter(
+        jnp.concatenate(parts_out, axis=-1)
+        .astype(jnp.bfloat16)
+        .reshape(lax.axis_size("row"), token_count, -1),
+        "row",
+        rounded=False,
+    ).reshape(token_count, head_count, HEAD_SIZE)
+    q_heads = q_width // HEAD_SIZE
+    token_positions = (
+        lengths[:, None] + jnp.arange(step_count, dtype=jnp.int32)[None, :]
+    ).reshape(token_count)
+    query_rows = rotary_apply(output_projected[:, :q_heads], token_positions).astype(jnp.bfloat16)
+    query_rows = query_rows.reshape(req_count, step_count, heads_kv, QUERY_PER_KEY, HEAD_SIZE)
+    current_key = (
+        rotary_apply(output_projected[:, q_heads : q_heads + heads_kv], token_positions)
+        .astype(jnp.bfloat16)
+        .reshape(req_count, step_count, heads_kv, HEAD_SIZE)
+    )
+    current_value = (
+        output_projected[:, q_heads + heads_kv :]
+        .astype(jnp.bfloat16)
+        .reshape(req_count, step_count, heads_kv, HEAD_SIZE)
+    )
+    picked = jnp.minimum(slot_request, req_count - 1)
+    in_use = slot_request < req_count
+    slot_queries = query_rows[picked]
+    scores = jnp.einsum(
+        "nsagh,nbah->nasgb", slot_queries, key_rows, preferred_element_type=jnp.float32
+    ) * (1.0 / math.sqrt(HEAD_SIZE))
+    key_pos = (
+        slot_block_number[:, None] * block_len + jnp.arange(block_len, dtype=jnp.int32)[None, :]
+    )
+    own_len = lengths[picked]
+    query_pos = own_len[:, None] + jnp.arange(step_count, dtype=jnp.int32)[None, :]
+    visible = (
+        in_use[:, None, None]
+        & (key_pos[:, None, :] < own_len[:, None, None])
+        & ((key_pos[:, None, :] < SINK) | (key_pos[:, None, :] > query_pos[:, :, None] - WINDOW))
+    )
+    visible = visible[:, None, :, None, :]
+    slot_peak = jnp.max(jnp.where(visible, scores, NEGATIVE_FILL), -1)
+    weights = jnp.where(visible, jnp.exp(scores - slot_peak[..., None]), 0.0)
+    slot_total = jnp.sum(weights, -1)
+    slot_acc = jnp.einsum(
+        "nasgb,nbah->nasgh",
+        weights.astype(jnp.bfloat16),
+        value_rows,
+        preferred_element_type=jnp.float32,
+    )
+    member = slot_request[None, :] == jnp.arange(req_count, dtype=jnp.int32)[:, None]
+    local_peak = jnp.max(
+        jnp.where(member[:, :, None, None, None], slot_peak[None], NEGATIVE_FILL), 1
+    )
+    return (local_peak, (slot_peak, slot_total, slot_acc, member, picked))
+
+
+def pool_sums(held, running_peak):
+    slot_peak, slot_total, slot_acc, member, picked = held
+    factor = jnp.exp(slot_peak - running_peak[picked])
+    as_member = member.astype(jnp.float32)
+    running_totals = jnp.einsum(
+        "rn,nasg->rasg", as_member, slot_total * factor, precision=lax.Precision.HIGHEST
+    )
+    weighted_values = jnp.einsum(
+        "rn,nasgh->rasgh", as_member, slot_acc * factor[..., None], precision=lax.Precision.HIGHEST
+    )
+    return (running_totals, weighted_values)
+
+
+def fresh_part(query_rows, key_all, value_all):
+    step_count = query_rows.shape[1]
+    used = key_all.shape[1]
+    scores = jnp.einsum(
+        "rsagh,ruah->rasgu", query_rows, key_all, preferred_element_type=jnp.float32
+    ) * (1.0 / math.sqrt(HEAD_SIZE))
+    causal = (
+        jnp.arange(used, dtype=jnp.int32)[None, :]
+        <= jnp.arange(step_count, dtype=jnp.int32)[:, None]
+    )
+    causal = causal[None, None, :, None, :]
+    running_peak = jnp.max(jnp.where(causal, scores, NEGATIVE_FILL), -1)
+    weights = jnp.where(causal, jnp.exp(scores - running_peak[..., None]), 0.0)
+    running_totals = jnp.sum(weights, -1)
+    weighted_values = jnp.einsum(
+        "rasgu,ruah->rasgh",
+        weights.astype(jnp.bfloat16),
+        value_all,
+        preferred_element_type=jnp.float32,
+    )
+    return (running_peak, running_totals, weighted_values)
+
+
+def merge_parts(earlier, later):
+    running_peak = jnp.maximum(earlier[0], later[0])
+    first_factor = jnp.exp(earlier[0] - running_peak)
+    second_factor = jnp.exp(later[0] - running_peak)
+    running_totals = earlier[1] * first_factor + later[1] * second_factor
+    weighted_values = earlier[2] * first_factor[..., None] + later[2] * second_factor[..., None]
+    return (running_peak, running_totals, weighted_values)
+
+
+def slot_kernel(len_ref, blk_ref, q_ref, k_ref, v_ref, peak_ref, tot_ref, acc_ref, *, ns, heads, qpk):
+    base = pl.program_id(0) * ns
+    rows = q_ref.shape[1]
+    group = rows // heads
+    width = k_ref.shape[1]
+    head = k_ref.shape[2] // heads
+    row = lax.broadcasted_iota(jnp.int32, (rows, width), 0)
+    col = lax.broadcasted_iota(jnp.int32, (rows, width), 1)
+    step_of = (row % group) // qpk
+
+    def body(i, carry):
+        length = len_ref[base + i]
+        key_pos = blk_ref[base + i] * width + col
+        query_pos = length + step_of
+        visible = (key_pos < length) & ((key_pos < SINK) | (key_pos > query_pos - WINDOW))
+        q = q_ref[i]
+        k = k_ref[i]
+        v = v_ref[i]
+        scores = jnp.concatenate(
+            [
+                lax.dot_general(
+                    q[a * group : (a + 1) * group],
+                    k[:, a * head : (a + 1) * head],
+                    (((1,), (1,)), ((), ())),
+                    preferred_element_type=jnp.float32,
+                )
+                for a in range(heads)
+            ],
+            0,
+        ) * (1.0 / math.sqrt(HEAD_SIZE))
+        peak = jnp.max(jnp.where(visible, scores, NEGATIVE_FILL), axis=1, keepdims=True)
+        weights = jnp.where(visible, jnp.exp(scores - peak), 0.0)
+        total = jnp.sum(weights, axis=1, keepdims=True)
+        rounded = weights.astype(jnp.bfloat16)
+        acc = jnp.concatenate(
+            [
+                jnp.dot(
+                    rounded[a * group : (a + 1) * group],
+                    v[:, a * head : (a + 1) * head],
+                    preferred_element_type=jnp.float32,
+                )
+                for a in range(heads)
+            ],
+            0,
+        )
+        peak_ref[i] = peak
+        tot_ref[i] = total
+        acc_ref[i] = acc
+        return carry
+
+    lax.fori_loop(0, ns, body, 0, unroll=True)
+
+
+def slot_attention(slot_queries, slot_lengths, block_numbers, keys, values, heads, qpk):
+    n_slots, rows, head = slot_queries.shape
+    width = keys.shape[1]
+    ns = max(d for d in range(1, 11) if n_slots % d == 0)
+    grid_spec = pltpu.PrefetchScalarGridSpec(
+        num_scalar_prefetch=2,
+        grid=(n_slots // ns,),
+        in_specs=[
+            pl.BlockSpec((ns, rows, head), lambda n, lr, br: (n, 0, 0)),
+            pl.BlockSpec((ns, width, keys.shape[2]), lambda n, lr, br: (n, 0, 0)),
+            pl.BlockSpec((ns, width, values.shape[2]), lambda n, lr, br: (n, 0, 0)),
+        ],
+        out_specs=[
+            pl.BlockSpec((ns, rows, 1), lambda n, lr, br: (n, 0, 0)),
+            pl.BlockSpec((ns, rows, 1), lambda n, lr, br: (n, 0, 0)),
+            pl.BlockSpec((ns, rows, head), lambda n, lr, br: (n, 0, 0)),
+        ],
+    )
+    return pl.pallas_call(
+        partial(slot_kernel, ns=ns, heads=heads, qpk=qpk),
+        grid_spec=grid_spec,
+        out_shape=[
+            jax.ShapeDtypeStruct((n_slots, rows, 1), jnp.float32),
+            jax.ShapeDtypeStruct((n_slots, rows, 1), jnp.float32),
+            jax.ShapeDtypeStruct((n_slots, rows, head), jnp.float32),
+        ],
+    )(slot_lengths, block_numbers, slot_queries, keys, values)
+
+
+def pair_gather(part, axis_name):
+    n = lax.axis_size(axis_name)
+    assert n == 2
+    side = lax.axis_index(axis_name)
+    other = lax.ppermute(part, axis_name, [(0, 1), (1, 0)])
+    return jnp.where(
+        side == 0,
+        jnp.concatenate([part, other], 0),
+        jnp.concatenate([other, part], 0),
+    )
+
+
+def pair_scatter(parts, axis_name, rounded=True):
+    n = lax.axis_size(axis_name)
+    assert n == 2 and parts.shape[0] == 2
+    side = lax.axis_index(axis_name)
+    keep = lax.dynamic_index_in_dim(parts, side, 0, keepdims=True)
+    send = lax.dynamic_index_in_dim(parts, 1 - side, 0, keepdims=True)
+    got = lax.ppermute(send, axis_name, [(0, 1), (1, 0)])
+    total = (keep.astype(jnp.float32) + got.astype(jnp.float32))[0]
+    return total.astype(parts.dtype) if rounded else total
+
+
+def doubling_gather(part, axis_name):
+    n = lax.axis_size(axis_name)
+    stages = n.bit_length() - 1
+    assert 1 << stages == n
+    index = lax.axis_index(axis_name)
+    block = part[None]
+    for bit in reversed(range(stages)):
+        pairs = [(s, s ^ (1 << bit)) for s in range(n)]
+        got = lax.ppermute(block, axis_name, pairs)
+        low = ((index >> bit) & 1) == 0
+        block = jnp.where(
+            low, jnp.stack([block, got], 0), jnp.stack([got, block], 0)
+        )
+    block = block.reshape((2,) * stages + part.shape)
+    block = block.transpose(tuple(reversed(range(stages))) + tuple(range(stages, stages + part.ndim)))
+    return block.reshape((n * part.shape[0],) + part.shape[1:])
+
+
+def seq_merge(peak, total, acc, n_seq, seq_index):
+    stages = n_seq.bit_length() - 1
+    assert 1 << stages == n_seq
+    req_count = peak.shape[0]
+    per = req_count // n_seq
+    rest = peak.shape[1:]
+    split = [2] * stages + [per]
+    stats = jnp.stack([peak, total], 0).reshape([2] + split + list(rest))
+    values = acc.reshape(split + list(acc.shape[1:]))
+    for bit in range(stages):
+        axis = stages - 1 - bit
+        mine = (seq_index >> bit) & 1
+        pairs = [(s, s ^ (1 << bit)) for s in range(n_seq)]
+        keep_stats = lax.dynamic_index_in_dim(stats, mine, axis + 1, keepdims=True)
+        send_stats = lax.dynamic_index_in_dim(stats, 1 - mine, axis + 1, keepdims=True)
+        keep_values = lax.dynamic_index_in_dim(values, mine, axis, keepdims=True)
+        send_values = lax.dynamic_index_in_dim(values, 1 - mine, axis, keepdims=True)
+        got_stats = lax.ppermute(send_stats, "seq", pairs)
+        got_values = lax.ppermute(send_values.astype(jnp.bfloat16), "seq", pairs).astype(
+            jnp.float32
+        )
+        top = jnp.maximum(keep_stats[0], got_stats[0])
+        keep_factor = jnp.exp(keep_stats[0] - top)
+        got_factor = jnp.exp(got_stats[0] - top)
+        stats = jnp.stack(
+            [top, keep_stats[1] * keep_factor + got_stats[1] * got_factor], 0
+        )
+        values = keep_values * keep_factor[..., None] + got_values * got_factor[..., None]
+    stats = stats.reshape((2, per) + tuple(rest))
+    values = values.reshape((per,) + tuple(acc.shape[1:]))
+    return (stats[0], stats[1], values)
+
+
+def on_device(
+    states,
+    norm_gain,
+    wq,
+    wk,
+    wv,
+    wo,
+    lengths,
+    slot_request,
+    slot_block_number,
+    paged_key_cache,
+    paged_value_cache,
+):
+    q_width = wq.shape[1]
+    k_width = wk.shape[1]
+    heads_kv = k_width // HEAD_SIZE
+    req_count = lengths.shape[0]
+    block_len = paged_key_cache.shape[1]
+    key_rows = paged_key_cache.reshape(paged_key_cache.shape[0], block_len, heads_kv, HEAD_SIZE)
+    value_rows = paged_value_cache.reshape(
+        paged_value_cache.shape[0], block_len, heads_kv, HEAD_SIZE
+    )
+    step_count = states.shape[1]
+    token_count = states.shape[0] * step_count
+    own_states = states.reshape(token_count, -1)
+    side = lax.axis_index("col")
+    swap = [(0, 1), (1, 0)]
+    other_states = lax.ppermute(own_states, "col", swap)
+    as_float = own_states.astype(jnp.float32)
+    squares = lax.psum(jnp.sum(as_float * as_float, -1), "row")
+    other_squares = lax.ppermute(squares, "col", swap)
+
+    def rms_norm(rows, sums):
+        scale = lax.rsqrt(sums / D + EPSILON)[:, None]
+        return (rows.astype(jnp.float32) * scale * norm_gain).astype(jnp.bfloat16)
+
+    first = side == 0
+    gathered = jnp.concatenate(
+        [
+            rms_norm(
+                jnp.where(first, own_states, other_states), jnp.where(first, squares, other_squares)
+            ),
+            rms_norm(
+                jnp.where(first, other_states, own_states), jnp.where(first, other_squares, squares)
+            ),
+        ],
+        0,
+    )
+    parts_out = [
+        jnp.dot(gathered, matrix, preferred_element_type=jnp.float32) for matrix in (wq, wk, wv)
+    ]
     output_projected = (
         pair_scatter(
             jnp.concatenate(parts_out, axis=-1)

time: 196 us -> 196 us (level)
  no operation moved by 1% of the time
where the time goes in v8:
time: 196 us; the launch traced here: 195 us
  waiting for transfers between devices  75.5 us (39%)
  local copies, waits for them, and re-layouts  34.5 us (18%)
  other arithmetic  25.8 us (13%)
  matrix products  18.8 us (10%)
  starting transfers between devices  17.5 us (9%)
  Pallas kernels  17.3 us (9%)
  blocking collectives  4.46 us (2%)
    ppermute x3, waiting for transfers between devices, doubling_gather(): got = lax.ppermute(block, axis_name, pairs)  28.7 us
    ppermute x1, waiting for transfers between devices, on_device(): other_squares = lax.ppermute(squares, 'col', swap)  24.4 us
    pallas_call x1, Pallas kernels, slot_attention(): pl.pallas_call(partial(slot_kernel, ns=ns, heads=heads, qpk=qpk), grid_sp...  17.3 us
    ppermute x3, waiting for transfers between devices, seq_merge(): lax.ppermute(send_values.astype(jnp.bfloat16), 'seq', pairs)  15 us
    dot_general x3, matrix products, on_device(): jnp.dot(gathered, matrix, preferred_element_type=jnp.float32)  8.8 us
    ppermute x3, starting transfers between devices, seq_merge(): got_stats = lax.ppermute(send_stats, 'seq', pairs)  6.63 us
    unnamed x27, local copies, waits for them, and re-layouts  6.29 us
    dot_general x1, matrix products, on_device(): jnp.dot(piece_rows.reshape(n_row * per * step_count, -1), wo, preferred_e...  5.88 us
  transfers between devices with their start and end apart: 13, of which 10 were waited for; matrix products, arithmetic and copies ran while one was open for 8% of the time, Pallas kernels for 0%

profile of v8, /device:TPU:0, one launch (start us, length us, event | category | flops | bytes accessed | tf_op | source)
XLA Modules:
  0.0 195.0 jit_solution(4860187712952625000)
XLA Ops:
  0.7 3.5 %reshape.810 = bf16[256,2560]{1,0:T(8,128)(2,1)} reshape(bf16[64,4,2560]{2,1,0:T(4,128)(2,1)} %param.11) | data formatting | bytes 2621440 | tf_op jit(solution)/shard_map/reshape | solution.py:607
  4.2 2.9 %collective-permute-start = (bf16[256,2560]{1,0:T(8,128)(2,1)}, bf16[256,2560]{1,0:T(8,128)(2,1)}, u32[]{:S(2)}, u32[]{:S(2)}) collective-permute-start(bf16[256,2560]{1,0:T(8,128)(2,1)} %reshape.810), channel_id=1, source_target_pairs={{0,8},{8,0},{1,9},{9,1},{2,10},{10,2},{3,11},{11,3},{4,12},{12,4},... | collective-permute-start | bytes 3932168 | tf_op jit(solution)/shard_map/ppermute | solution.py:610
  7.1 2.1 %multiply_reduce_fusion = f32[64,4]{1,0:T(8,128)S(1)} fusion(bf16[64,4,2560]{2,1,0:T(4,128)(2,1)} %param.11), kind=kLoop, calls=%fused_computation.12 | loop fusion | flops 1965824 | bytes 1311744 | tf_op jit(solution)/shard_map/reduce_sum | solution.py:612
  9.3 2.5 %psum.7 = f32[256]{0:T(256)S(1)} all-reduce(f32[256]{0:T(256)S(1)} %reduce_sum.21), channel_id=1, replica_groups=mesh['row'=2,'col'=2,'seq'=8] {'row'}, use_global_device_ids=true, to_apply=%region_1.0 | all-reduce | flops 256 | bytes 2048 | tf_op jit(solution)/shard_map/psum | solution.py:612
  11.8 24.4 %collective-permute-done.1 = f32[256]{0:T(256)S(1)} collective-permute-done((f32[256]{0:T(256)S(1)}, f32[256]{0:T(256)S(1)}, u32[]{:S(2)}, u32[]{:S(2)}) %collective-permute-start.1) | collective-permute-done | bytes 1056 | tf_op jit(solution)/shard_map/ppermute | solution.py:613
  36.3 2.8 %multiply_convert_fusion.1 = (bf16[256,2560]{1,0:T(8,128)(2,1)S(1)}, bf16[256,2560]{1,0:T(8,128)(2,1)S(1)}) fusion(f32[2560]{0:T(1024)S(1)} %copy-done.7, f32[256]{0:T(256)S(1)} %get-tuple-element.61, bf16[256,2560]{1,0:T(8,128)(2,1)} %reshape.810, bf16[256,2560]{1,0:T(8,128)(2,1)} %collective-permute-done, pred[]{:T(512)S(6)} %eq.72, ...), kind=kLoop, calls=%fused_computation.11 | loop fusion | flops 6553600 | bytes 5255169 | tf_op jit(solution)/shard_map/convert_element_type | solution.py:617
  39.1 1.5 convolution_convert_fusion.2
  40.7 1.5 convolution_convert_fusion.1
  42.6 0.8 slice-done.2
  43.4 5.8 %convolution_convert_fusion = bf16[512,2048]{1,0:T(8,128)(2,1)S(1)} fusion(bf16[2560,2048]{1,0:T(8,128)(2,1)S(1)} %bitcast.168, bf16[256,2560]{1,0:T(8,128)(2,1)S(1)} %get-tuple-element.38, bf16[256,2560]{1,0:T(8,128)(2,1)S(1)} %get-tuple-element.37), kind=kOutput, calls=%fused_computation.8 | convolution fusion | flops 5375000576 | bytes 15204352 | tf_op jit(solution)/shard_map/dot_general | solution.py:632
  49.5 1.6 copy-done.3
  51.1 1.3 constant_dynamic-slice_fusion.1
  52.4 0.8 gather_fusion
  53.3 1.1 multiply_cosine_fusion
  54.5 0.5 compare_select_fusion.1.len_ref
  55.1 1.0 collective-permute-done.2
  56.0 3.6 %convert_add_fusion = f32[1,256,3072]{2,1,0:T(8,128)} fusion(bf16[1,256,3072]{2,1,0:T(8,128)(2,1)S(1)} %collective-permute-done.2, bf16[2,256,3072]{2,1,0:T(8,128)(2,1)} %copy-done.3, s32[]{:T(128)S(6)} %select_n.191), kind=kLoop, calls=%fused_computation.7 | loop fusion | flops 2359296 | bytes 6291460 | tf_op jit(solution)/shard_map/add | solution.py:528
  59.6 4.8 %reshape_squeeze.7 = f32[64,4,3072]{2,1,0:T(4,128)} reshape(f32[1,256,3072]{2,1,0:T(8,128)} %convert_add_fusion) | data formatting | bytes 6291456 | tf_op jit(solution)/shard_map/reshape;squeeze | solution.py:642
  64.4 1.1 slice_bitcast_fusion.3
  65.5 1.1 slice_bitcast_fusion
  66.6 3.2 %slice.92 = f32[64,4,2048]{2,1,0:T(4,128)} slice(f32[64,4,3072]{2,1,0:T(4,128)} %reshape_squeeze.7), slice={[0:64], [0:4], [0:2048]} | slice | bytes 4194304 | tf_op jit(solution)/shard_map/slice | solution.py:646
  69.9 0.5 multiply_subtract_fusion
  70.4 2.3 %reshape.848 = f32[64,4,16,128]{3,2,1,0:T(8,128)S(1)} reshape(f32[64,4,2048]{2,1,0:T(4,128)} %slice.92) | data formatting | bytes 4194304 | tf_op jit(solution)/shard_map/reshape | solution.py:646
  72.7 0.7 fusion.58
  73.5 0.6 subtract_convert_fusion
  74.0 1.4 pad_maximum_fusion.2
  75.5 0.6 copy.215
  76.4 1.2 fusion.13
  77.6 0.5 copy.191
  78.1 1.6 gather_fusion.1
  79.9 0.8 fusion.15
  80.7 17.3 %shard_map.130 = (f32[50,64,1]{2,1,0:T(8,128)}, f32[50,64,1]{2,1,0:T(8,128)}, f32[50,64,128]{2,1,0:T(8,128)}) custom-call(s32[50]{0:T(128)} %compare_select_fusion.1.len_ref, s32[50]{0:T(128)} %blk_ref.1, bf16[50,64,128]{2,1,0:T(8,128)(2,1)} %gather_fusion.1, bf16[50,128,512]{2,1,0:T(8,128)(2,1)} %k_ref.1, bf16[50,128,512]{2,1,0:T(8,128)(2,1)} %v_ref.1), custom_call_target="tpu_custom_call" | custom-call | tf_op jit(solution)/shard_map/pallas_call | solution.py:498
  98.0 2.0 %reduce.1 = f32[50,64]{1,0:T(8,128)S(1)} reduce(f32[50,64,1]{2,1,0:T(8,128)} %get-tuple-element.7, f32[]{:T(128)} %constant.111), dimensions={2}, to_apply=%get-tuple-element.7.reduce_sub_computation | reduce | bytes 25604 | tf_op jit(solution)/shard_map/pallas_call | solution.py:498
  100.1 0.9 select_reduce_fusion
  101.0 0.6 gather_fusion.2
  101.6 1.8 copy.173
  103.4 3.0 %multiply_reduce_fusion.1 = (f32[50,64]{1,0:T(8,128)S(1)}, f32[50,64]{1,0:T(8,128)S(1)}) fusion(f32[50,64,1]{2,1,0:T(8,128)} %get-tuple-element.8, f32[50,64,1]{2,1,0:T(8,128)S(1)} %copy-done.4, f32[50,64,1]{2,1,0:T(8,128)} %copy.173), kind=kLoop, calls=%fused_computation.17 | loop fusion | flops 6400 | bytes 64000 | tf_op jit(solution)/shard_map/mul | solution.py:681
  106.6 1.8 collective-permute-start.3
  108.4 0.5 broadcast_multiply_fusion
  108.9 2.2 %fusion.5 = f32[64,64,128]{2,0,1:T(8,128)S(1)} fusion(f32[50,64,128]{2,1,0:T(8,128)S(1)} %broadcast_multiply_fusion, s32[50]{0:T(128)S(1)} %copy-done.8), kind=kOutput, calls=%fused_computation.15 | convolution fusion | flops 314576000 | bytes 3735752 | tf_op jit(solution)/shard_map/rn,njh->rjh/dot_general | solution.py:683
  111.1 1.4 copy-done.5
  112.6 0.5 copy.196
  113.5 1.9 collective-permute-start.5
  115.7 1.6 collective-permute-done.5
  117.3 2.9 %collective-permute-start.7 = (f32[2,1,1,1,8,64]{5,4,3,2,1,0:T(8,128)S(1)}, f32[2,1,1,1,8,64]{5,4,3,2,1,0:T(8,128)S(1)}, u32[]{:S(2)}, u32[]{:S(2)}) collective-permute-start(f32[2,1,1,1,8,64]{5,4,3,2,1,0:T(8,128)S(1)} %get-tuple-element.60), channel_id=1, source_target_pairs={{0,4},{1,5},{2,6},{3,7},{4,0},{5,1},{6,2},{7,3},{8,12},{9,13},{10,... | collective-permute-start | bytes 12296 | tf_op jit(solution)/shard_map/ppermute | solution.py:567
  120.5 6.4 %collective-permute-done.4 = bf16[2,2,1,8,64,128]{5,3,2,1,0,4:T(8,128)(2,1)S(1)} collective-permute-done((bf16[2,2,1,8,64,128]{5,3,2,1,0,4:T(8,128)(2,1)S(1)}, bf16[2,2,1,8,64,128]{5,3,2,1,0,4:T(8,128)(2,1)S(1)}, u32[]{:S(2)}, u32[]{:S(2)}) %collective-permute-start.4) | collective-permute-done | bytes 524320 | tf_op jit(solution)/shard_map/ppermute | solution.py:568
  126.9 1.8 multiply_add_fusion
  128.8 1.6 collective-permute-start.6
  130.7 5.3 %collective-permute-done.6 = bf16[2,1,1,8,64,128]{5,3,2,1,0,4:T(8,128)(2,1)S(1)} collective-permute-done((bf16[2,1,1,8,64,128]{5,3,2,1,0,4:T(8,128)(2,1)S(1)}, bf16[2,1,1,8,64,128]{5,3,2,1,0,4:T(8,128)(2,1)S(1)}, u32[]{:S(2)}, u32[]{:S(2)}) %collective-permute-start.6) | collective-permute-done | bytes 262176 | tf_op jit(solution)/shard_map/ppermute | solution.py:568
  136.4 2.7 %collective-permute-start.8 = (bf16[1,1,1,8,64,128]{5,3,2,1,0,4:T(8,128)(2,1)S(1)}, bf16[1,1,1,8,64,128]{5,3,2,1,0,4:T(8,128)(2,1)S(1)}, u32[]{:S(2)}, u32[]{:S(2)}) collective-permute-start(bf16[1,1,1,8,64,128]{5,3,2,1,0,4:T(8,128)(2,1)S(1)} %dynamic-slice_convert_fusion.2), channel_id=1, source_target_pairs={{0,4},{1,5},{2,6},{3,7},{4,0},{5,1},{6,2},{7,3},{8,12},{9,13},{10,... | collective-permute-start | bytes 393224 | tf_op jit(solution)/shard_map/ppermute | solution.py:568
  139.1 0.8 multiply_add_fusion.4
  140.5 3.3 %collective-permute-done.8 = bf16[1,1,1,8,64,128]{5,3,2,1,0,4:T(8,128)(2,1)S(1)} collective-permute-done((bf16[1,1,1,8,64,128]{5,3,2,1,0,4:T(8,128)(2,1)S(1)}, bf16[1,1,1,8,64,128]{5,3,2,1,0,4:T(8,128)(2,1)S(1)}, u32[]{:S(2)}, u32[]{:S(2)}) %collective-permute-start.8) | collective-permute-done | bytes 131104 | tf_op jit(solution)/shard_map/ppermute | solution.py:568
  144.0 0.5 fusion.11
  144.7 2.0 %all_gather.4 = bf16[2,8,4,2048]{3,1,2,0:T(8,128)(2,1)S(1)} all-gather(bf16[1,8,4,2048]{3,1,2,0:T(8,128)(2,1)S(1)} %convert_element_type.122), channel_id=1, replica_groups=mesh['row'=2,'col'=2,'seq'=8] {'row'}, dimensions={0}, use_global_device_ids=true | all-gather | bytes 393216 | tf_op jit(solution)/shard_map/all_gather | solution.py:712
  146.6 5.9 %fusion.2 = bf16[2,8,4,2560]{3,1,2,0:T(8,128)(2,1)S(1)} fusion(bf16[2,8,4,2048]{3,1,2,0:T(8,128)(2,1)S(1)} %all_gather.4, bf16[2048,2560]{1,0:T(8,128)(2,1)} %param.16), kind=kOutput, calls=%fused_computation.5 | convolution fusion | flops 671252480 | bytes 11075584 | tf_op jit(solution)/shard_map/dot_general | solution.py:714
  152.5 1.6 collective-permute-start.9
  154.1 4.8 %collective-permute-done.9 = bf16[1,8,4,2560]{3,1,2,0:T(8,128)(2,1)S(1)} collective-permute-done((bf16[1,8,4,2560]{3,1,2,0:T(8,128)(2,1)S(1)}, bf16[1,8,4,2560]{3,1,2,0:T(8,128)(2,1)S(1)}, u32[]{:S(2)}, u32[]{:S(2)}) %collective-permute-start.9) | collective-permute-done | bytes 163872 | tf_op jit(solution)/shard_map/ppermute | solution.py:527
  158.9 1.4 collective-permute-start.10
  160.3 8.5 %collective-permute-done.10 = bf16[1,8,4,2560]{3,1,2,0:T(8,128)(2,1)S(1)} collective-permute-done((bf16[1,8,4,2560]{3,1,2,0:T(8,128)(2,1)S(1)}, bf16[1,8,4,2560]{3,1,2,0:T(8,128)(2,1)S(1)}, u32[]{:S(2)}, u32[]{:S(2)}) %collective-permute-start.10) | collective-permute-done | bytes 163872 | tf_op jit(solution)/shard_map/ppermute | solution.py:540
  169.0 8.6 %collective-permute-done.11 = bf16[2,1,8,4,2560]{4,2,3,1,0:T(8,128)(2,1)S(1)} collective-permute-done((bf16[2,1,8,4,2560]{4,2,3,1,0:T(8,128)(2,1)S(1)}, bf16[2,1,8,4,2560]{4,2,3,1,0:T(8,128)(2,1)S(1)}, u32[]{:S(2)}, u32[]{:S(2)}) %collective-permute-start.11) | collective-permute-done | bytes 327712 | tf_op jit(solution)/shard_map/ppermute | solution.py:540
  178.0 1.8 slice.167
  179.9 1.1 fusion.64
  181.1 11.5 %collective-permute-done.12 = bf16[2,2,1,8,4,2560]{5,3,4,1,2,0:T(8,128)(2,1)S(1)} collective-permute-done((bf16[2,2,1,8,4,2560]{5,3,4,1,2,0:T(8,128)(2,1)S(1)}, bf16[2,2,1,8,4,2560]{5,3,4,1,2,0:T(8,128)(2,1)S(1)}, u32[]{:S(2)}, u32[]{:S(2)}) %collective-permute-start.12) | collective-permute-done | bytes 655392 | tf_op jit(solution)/shard_map/ppermute | solution.py:540
  192.9 2.1 %copy.205 = bf16[64,4,2560]{2,1,0:T(4,128)(2,1)} copy(bf16[64,4,2560]{2,0,1:T(8,128)(2,1)S(1)} %bitcast.143) | data formatting | bytes 2621440
  (83 shorter events, 5.6 us)
Async XLA Ops:
  0.6 38.5 %copy-start = (bf16[2560,512]{1,0:T(8,128)(2,1)S(1)}, bf16[2560,512]{1,0:T(8,128)(2,1)}, u32[]{:S(2)}) copy-start(bf16[2560,512]{1,0:T(8,128)(2,1)} %param.14) | copy-start | bytes 7864324
  0.6 35.6 %copy-start.7 = (f32[2560]{0:T(1024)S(1)}, f32[2560]{0:T(1024)}, u32[]{:S(2)}) copy-start(f32[2560]{0:T(1024)} %param.12) | copy-start | bytes 30724
  4.2 32.0 %collective-permute-start = (bf16[256,2560]{1,0:T(8,128)(2,1)}, bf16[256,2560]{1,0:T(8,128)(2,1)}, u32[]{:S(2)}, u32[]{:S(2)}) collective-permute-start(bf16[256,2560]{1,0:T(8,128)(2,1)} %reshape.810), channel_id=1, source_target_pairs={{0,8},{8,0},{1,9},{9,1},{2,10},{10,2},{3,11},{11,3},{4,12},{12,4},... | collective-permute-start | bytes 3932168 | tf_op jit(solution)/shard_map/ppermute | solution.py:610
  11.8 24.4 %collective-permute-start.1 = (f32[256]{0:T(256)S(1)}, f32[256]{0:T(256)S(1)}, u32[]{:S(2)}, u32[]{:S(2)}) collective-permute-start(f32[256]{0:T(256)S(1)} %psum.7), channel_id=1, source_target_pairs={{0,8},{8,0},{1,9},{9,1},{2,10},{10,2},{3,11},{11,3},{4,12},{12,4},... | collective-permute-start | bytes 3080 | tf_op jit(solution)/shard_map/ppermute | solution.py:613
  36.3 4.4 %copy-start.9 = (bf16[2560,512]{1,0:T(8,128)(2,1)S(1)}, bf16[2560,512]{1,0:T(8,128)(2,1)}, u32[]{:S(2)}) copy-start(bf16[2560,512]{1,0:T(8,128)(2,1)} %param.15) | copy-start | bytes 7864324
  39.1 3.1 %slice-start = ((s8[10485760]{0:T(1024)(128)(4,1)}), s8[4194304]{0:T(1024)(128)(4,1)S(1)}, s32[]{:S(2)}) async-start(s8[10485760]{0:T(1024)(128)(4,1)} %bitcast.167), calls=%async_computation | async-start | bytes 8388608
  39.1 3.5 %slice-start.1 = ((s8[10485760]{0:T(1024)(128)(4,1)}), s8[4194304]{0:T(1024)(128)(4,1)S(1)}, s32[]{:S(2)}) async-start(s8[10485760]{0:T(1024)(128)(4,1)} %bitcast.167), calls=%async_computation.1 | async-start | bytes 8388608
  40.7 2.7 %slice-start.2 = ((s8[10485760]{0:T(1024)(128)(4,1)}), s8[2097152]{0:T(1024)(128)(4,1)S(1)}, s32[]{:S(2)}) async-start(s8[10485760]{0:T(1024)(128)(4,1)} %bitcast.167), calls=%async_computation.2 | async-start | bytes 4194304
  49.5 1.6 copy-start.3
  51.1 1.3 copy-start.8
  51.1 1.3 copy-start.2
  52.4 3.6 %collective-permute-start.2 = (bf16[1,256,3072]{2,1,0:T(8,128)(2,1)}, bf16[1,256,3072]{2,1,0:T(8,128)(2,1)S(1)}, u32[]{:S(2)}, u32[]{:S(2)}) collective-permute-start(bf16[1,256,3072]{2,1,0:T(8,128)(2,1)} %constant_dynamic-slice_fusion.1), channel_id=1, source_target_pairs={{0,16},{16,0},{1,17},{17,1},{2,18},{18,2},{3,19},{19,3},{4,20},{20... | collective-permute-start | bytes 4718600 | tf_op jit(solution)/shard_map/ppermute | solution.py:527
  98.0 5.4 %copy-start.4 = (f32[50,64,1]{2,1,0:T(8,128)S(1)}, f32[50,64,1]{2,1,0:T(8,128)}, u32[]{:S(2)}) copy-start(f32[50,64,1]{2,1,0:T(8,128)} %get-tuple-element.7) | copy-start | bytes 38404
  103.4 5.1 %copy-start.6 = (f32[50,64,128]{2,1,0:T(8,128)S(1)}, f32[50,64,128]{2,1,0:T(8,128)}, u32[]{:S(2)}) copy-start(f32[50,64,128]{2,1,0:T(8,128)} %get-tuple-element.6) | copy-start | bytes 4915204
  106.6 6.9 %collective-permute-start.3 = (f32[2,2,2,1,8,64]{5,4,3,2,1,0:T(8,128)S(1)}, f32[2,2,2,1,8,64]{5,4,3,2,1,0:T(8,128)S(1)}, u32[]{:S(2)}, u32[]{:S(2)}) collective-permute-start(f32[2,2,2,1,8,64]{5,4,3,2,1,0:T(8,128)S(1)} %get-tuple-element.50), channel_id=1, source_target_pairs={{0,1},{1,0},{2,3},{3,2},{4,5},{5,4},{6,7},{7,6},{8,9},{9,8},{10,11... | collective-permute-start | bytes 49160 | tf_op jit(solution)/shard_map/ppermute | solution.py:567
  111.1 1.4 copy-start.5
  113.1 13.7 %collective-permute-start.4 = (bf16[2,2,1,8,64,128]{5,3,2,1,0,4:T(8,128)(2,1)S(1)}, bf16[2,2,1,8,64,128]{5,3,2,1,0,4:T(8,128)(2,1)S(1)}, u32[]{:S(2)}, u32[]{:S(2)}) collective-permute-start(bf16[2,2,1,8,64,128]{5,3,2,1,0,4:T(8,128)(2,1)S(1)} %dynamic-slice_convert_fusion), channel_id=1, source_target_pairs={{0,1},{1,0},{2,3},{3,2},{4,5},{5,4},{6,7},{7,6},{8,9},{9,8},{10,11... | collective-permute-start | bytes 1572872 | tf_op jit(solution)/shard_map/ppermute | solution.py:568
  113.5 3.8 %collective-permute-start.5 = (f32[2,2,1,1,8,64]{5,4,3,2,1,0:T(8,128)S(1)}, f32[2,2,1,1,8,64]{5,4,3,2,1,0:T(8,128)S(1)}, u32[]{:S(2)}, u32[]{:S(2)}) collective-permute-start(f32[2,2,1,1,8,64]{5,4,3,2,1,0:T(8,128)S(1)} %get-tuple-element.56), channel_id=1, source_target_pairs={{0,2},{1,3},{2,0},{3,1},{4,6},{5,7},{6,4},{7,5},{8,10},{9,11},{10,... | collective-permute-start | bytes 24584 | tf_op jit(solution)/shard_map/ppermute | solution.py:567
  117.3 13.1 %collective-permute-start.7 = (f32[2,1,1,1,8,64]{5,4,3,2,1,0:T(8,128)S(1)}, f32[2,1,1,1,8,64]{5,4,3,2,1,0:T(8,128)S(1)}, u32[]{:S(2)}, u32[]{:S(2)}) collective-permute-start(f32[2,1,1,1,8,64]{5,4,3,2,1,0:T(8,128)S(1)} %get-tuple-element.60), channel_id=1, source_target_pairs={{0,4},{1,5},{2,6},{3,7},{4,0},{5,1},{6,2},{7,3},{8,12},{9,13},{10,... | collective-permute-start | bytes 12296 | tf_op jit(solution)/shard_map/ppermute | solution.py:567
  128.8 7.3 %collective-permute-start.6 = (bf16[2,1,1,8,64,128]{5,3,2,1,0,4:T(8,128)(2,1)S(1)}, bf16[2,1,1,8,64,128]{5,3,2,1,0,4:T(8,128)(2,1)S(1)}, u32[]{:S(2)}, u32[]{:S(2)}) collective-permute-start(bf16[2,1,1,8,64,128]{5,3,2,1,0,4:T(8,128)(2,1)S(1)} %dynamic-slice_convert_fusion.1), channel_id=1, source_target_pairs={{0,2},{1,3},{2,0},{3,1},{4,6},{5,7},{6,4},{7,5},{8,10},{9,11},{10,... | collective-permute-start | bytes 786440 | tf_op jit(solution)/shard_map/ppermute | solution.py:568
  136.4 7.3 %collective-permute-start.8 = (bf16[1,1,1,8,64,128]{5,3,2,1,0,4:T(8,128)(2,1)S(1)}, bf16[1,1,1,8,64,128]{5,3,2,1,0,4:T(8,128)(2,1)S(1)}, u32[]{:S(2)}, u32[]{:S(2)}) collective-permute-start(bf16[1,1,1,8,64,128]{5,3,2,1,0,4:T(8,128)(2,1)S(1)} %dynamic-slice_convert_fusion.2), channel_id=1, source_target_pairs={{0,4},{1,5},{2,6},{3,7},{4,0},{5,1},{6,2},{7,3},{8,12},{9,13},{10,... | collective-permute-start | bytes 393224 | tf_op jit(solution)/shard_map/ppermute | solution.py:568
  152.5 6.3 %collective-permute-start.9 = (bf16[1,8,4,2560]{3,1,2,0:T(8,128)(2,1)S(1)}, bf16[1,8,4,2560]{3,1,2,0:T(8,128)(2,1)S(1)}, u32[]{:S(2)}, u32[]{:S(2)}) collective-permute-start(bf16[1,8,4,2560]{3,1,2,0:T(8,128)(2,1)S(1)} %constant_dynamic-slice_fusion), channel_id=1, source_target_pairs={{0,8},{8,0},{1,9},{9,1},{2,10},{10,2},{3,11},{11,3},{4,12},{12,4},... | collective-permute-start | bytes 491528 | tf_op jit(solution)/shard_map/ppermute | solution.py:527
  158.9 9.9 %collective-permute-start.10 = (bf16[1,8,4,2560]{3,1,2,0:T(8,128)(2,1)S(1)}, bf16[1,8,4,2560]{3,1,2,0:T(8,128)(2,1)S(1)}, u32[]{:S(2)}, u32[]{:S(2)}) collective-permute-start(bf16[1,8,4,2560]{3,1,2,0:T(8,128)(2,1)S(1)} %add_convert_fusion.1), channel_id=1, source_target_pairs={{0,4},{1,5},{2,6},{3,7},{4,0},{5,1},{6,2},{7,3},{8,12},{9,13},{10,... | collective-permute-start | bytes 491528 | tf_op jit(solution)/shard_map/ppermute | solution.py:540
  168.9 8.8 %collective-permute-start.11 = (bf16[2,1,8,4,2560]{4,2,3,1,0:T(8,128)(2,1)S(1)}, bf16[2,1,8,4,2560]{4,2,3,1,0:T(8,128)(2,1)S(1)}, u32[]{:S(2)}, u32[]{:S(2)}) collective-permute-start(bf16[2,1,8,4,2560]{4,2,3,1,0:T(8,128)(2,1)S(1)} %maximum_select_fusion.4), channel_id=1, source_target_pairs={{0,2},{1,3},{2,0},{3,1},{4,6},{5,7},{6,4},{7,5},{8,10},{9,11},{10,... | collective-permute-start | bytes 983048 | tf_op jit(solution)/shard_map/ppermute | solution.py:540
  177.7 14.9 %collective-permute-start.12 = (bf16[2,2,1,8,4,2560]{5,3,4,1,2,0:T(8,128)(2,1)S(1)}, bf16[2,2,1,8,4,2560]{5,3,4,1,2,0:T(8,128)(2,1)S(1)}, u32[]{:S(2)}, u32[]{:S(2)}) collective-permute-start(bf16[2,2,1,8,4,2560]{5,3,4,1,2,0:T(8,128)(2,1)S(1)} %maximum_select_fusion.2), channel_id=1, source_target_pairs={{0,1},{1,0},{2,3},{3,2},{4,5},{5,4},{6,7},{7,6},{8,9},{9,8},{10,11... | collective-permute-start | bytes 1966088 | tf_op jit(solution)/shard_map/ppermute | solution.py:540
  192.6 2.4 %copy-start.1 = (bf16[2560,512]{1,0:T(8,128)(2,1)S(1)}, bf16[2560,512]{1,0:T(8,128)(2,1)}, u32[]{:S(2)}) copy-start(bf16[2560,512]{1,0:T(8,128)(2,1)} %param.14) | copy-start | bytes 7864324

commit v9 on v8

--- a/solution.py
+++ b/solution.py
@@ -295,16 +295,17 @@
     )
     step_count = states.shape[1]
     token_count = states.shape[0] * step_count
-    own_states = states.reshape(token_count, -1)
     side = lax.axis_index("col")
     swap = [(0, 1), (1, 0)]
-    other_states = lax.ppermute(own_states, "col", swap)
-    as_float = own_states.astype(jnp.float32)
-    squares = lax.psum(jnp.sum(as_float * as_float, -1), "row")
+    other_states = lax.ppermute(states, "col", swap)
+    as_float = states.astype(jnp.float32)
+    squares = lax.psum(jnp.sum(as_float * as_float, -1), "row").reshape(token_count)
     other_squares = lax.ppermute(squares, "col", swap)
+    own_states = states
 
     def rms_norm(rows, sums):
         scale = lax.rsqrt(sums / D + EPSILON)[:, None]
+        rows = rows.reshape(token_count, -1)
         return (rows.astype(jnp.float32) * scale * norm_gain).astype(jnp.bfloat16)
 
     first = side == 0
@@ -604,16 +605,17 @@
     )
     step_count = states.shape[1]
     token_count = states.shape[0] * step_count
-    own_states = states.reshape(token_count, -1)
     side = lax.axis_index("col")
     swap = [(0, 1), (1, 0)]
-    other_states = lax.ppermute(own_states, "col", swap)
-    as_float = own_states.astype(jnp.float32)
-    squares = lax.psum(jnp.sum(as_float * as_float, -1), "row")
+    other_states = lax.ppermute(states, "col", swap)
+    as_float = states.astype(jnp.float32)
+    squares = lax.psum(jnp.sum(as_float * as_float, -1), "row").reshape(token_count)
     other_squares = lax.ppermute(squares, "col", swap)
+    own_states = states
 
     def rms_norm(rows, sums):
         scale = lax.rsqrt(sums / D + EPSILON)[:, None]
+        rows = rows.reshape(token_count, -1)
         return (rows.astype(jnp.float32) * scale * norm_gain).astype(jnp.bfloat16)
 
     first = side == 0

time: 196 us -> 206 us (1.051)
  other arithmetic: 25.8 us -> 31 us
  local copies, waits for them, and re-layouts: 34.5 us -> 39.1 us
    convert_element_type x0 -> x2, local copies, waits for them, and re-layouts: none -> 7.98 us  [rms_norm(): return (rows.astype(jnp.float32) * scale * norm_gain).astype(jnp.bfloat16)]
    convert_element_type x1 -> x2, other arithmetic: 2.83 us -> 8.01 us  [rms_norm(): return (rows.astype(jnp.float32) * scale * norm_gain).astype(jnp.bfloat16)]
    reshape x1, local copies, waits for them, and re-layouts: 3.53 us -> 0.1 us  [on_device(): lax.psum(jnp.sum(as_float * as_float, -1), 'row').reshape(token_count)]
  transfers between devices with their start and end apart: 13 -> 13, of which waited for: 10 -> 10; matrix products, arithmetic and copies ran while one was open for 8% -> 7% of each run, Pallas kernels for 0% -> 0%
where the time goes in v9:
time: 206 us; the launch traced here: 205 us
  waiting for transfers between devices  75.4 us (37%)
  local copies, waits for them, and re-layouts  39.1 us (19%)
  other arithmetic  31 us (15%)
  matrix products  18.8 us (9%)
  starting transfers between devices  17.7 us (9%)
  Pallas kernels  17.3 us (8%)
  blocking collectives  4.46 us (2%)
    ppermute x3, waiting for transfers between devices, doubling_gather(): got = lax.ppermute(block, axis_name, pairs)  28.7 us
    ppermute x1, waiting for transfers between devices, on_device(): other_squares = lax.ppermute(squares, 'col', swap)  24.3 us
    pallas_call x1, Pallas kernels, slot_attention(): pl.pallas_call(partial(slot_kernel, ns=ns, heads=heads, qpk=qpk), grid_sp...  17.3 us
    ppermute x3, waiting for transfers between devices, seq_merge(): lax.ppermute(send_values.astype(jnp.bfloat16), 'seq', pairs)  15 us
    dot_general x3, matrix products, on_device(): jnp.dot(gathered, matrix, preferred_element_type=jnp.float32)  8.79 us
    convert_element_type x2, other arithmetic, rms_norm(): return (rows.astype(jnp.float32) * scale * norm_gain).astype(jnp.bfloat16)  8.01 us
    convert_element_type x2, local copies, waits for them, and re-layouts, rms_norm(): return (rows.astype(jnp.float32) * scale * norm_gain).astype(jnp.bfloat16)  7.98 us
    ppermute x3, starting transfers between devices, seq_merge(): got_stats = lax.ppermute(send_stats, 'seq', pairs)  6.62 us
  transfers between devices with their start and end apart: 13, of which 10 were waited for; matrix products, arithmetic and copies ran while one was open for 7% of the time, Pallas kernels for 0%

profile of v9, /device:TPU:0, one launch (start us, length us, event | category | flops | bytes accessed | tf_op | source)
XLA Modules:
  0.0 204.8 jit_solution(13368201900537118845)
XLA Ops:
  0.6 3.0 %collective-permute-start = (bf16[64,4,2560]{2,1,0:T(4,128)(2,1)}, bf16[64,4,2560]{2,1,0:T(4,128)(2,1)}, u32[]{:S(2)}, u32[]{:S(2)}) collective-permute-start(bf16[64,4,2560]{2,1,0:T(4,128)(2,1)} %param.11), channel_id=1, source_target_pairs={{0,8},{8,0},{1,9},{9,1},{2,10},{10,2},{3,11},{11,3},{4,12},{12,4},... | collective-permute-start | bytes 3932168 | tf_op jit(solution)/shard_map/ppermute | solution.py:610
  3.7 2.1 %multiply_reduce_fusion = f32[64,4]{1,0:T(8,128)S(1)} fusion(bf16[64,4,2560]{2,1,0:T(4,128)(2,1)} %param.11), kind=kLoop, calls=%fused_computation.12 | loop fusion | flops 1965824 | bytes 1311744 | tf_op jit(solution)/shard_map/reduce_sum | solution.py:612
  5.9 2.5 %psum.7 = f32[256]{0:T(256)S(1)} all-reduce(f32[256]{0:T(256)S(1)} %reshape.815), channel_id=1, replica_groups=mesh['row'=2,'col'=2,'seq'=8] {'row'}, use_global_device_ids=true, to_apply=%region_1.0 | all-reduce | flops 256 | bytes 2048 | tf_op jit(solution)/shard_map/psum | solution.py:612
  8.5 24.3 %collective-permute-done.1 = f32[256]{0:T(256)S(1)} collective-permute-done((f32[256]{0:T(256)S(1)}, f32[256]{0:T(256)S(1)}, u32[]{:S(2)}, u32[]{:S(2)}) %collective-permute-start.1) | collective-permute-done | bytes 1056 | tf_op jit(solution)/shard_map/ppermute | solution.py:613
  32.8 4.8 %select_convert_fusion.1 = (f32[64,4,2560]{2,1,0:T(4,128)}, f32[64,4,2560]{2,1,0:T(4,128)}) fusion(bf16[64,4,2560]{2,1,0:T(4,128)(2,1)} %param.11, bf16[64,4,2560]{2,1,0:T(4,128)(2,1)} %collective-permute-done, pred[]{:T(512)S(6)} %eq.72), kind=kLoop, calls=%fused_computation.23 | loop fusion | flops 2621440 | bytes 7864321 | tf_op jit(solution)/shard_map/convert_element_type | solution.py:619
  37.6 4.0 %reshape.821 = f32[256,2560]{1,0:T(8,128)} reshape(f32[64,4,2560]{2,1,0:T(4,128)} %get-tuple-element.37) | data formatting | bytes 5242880 | tf_op jit(solution)/shard_map/convert_element_type | solution.py:619
  41.6 4.0 %reshape.822 = f32[256,2560]{1,0:T(8,128)} reshape(f32[64,4,2560]{2,1,0:T(4,128)} %get-tuple-element.38) | data formatting | bytes 5242880 | tf_op jit(solution)/shard_map/convert_element_type | solution.py:619
  45.6 3.2 %multiply_convert_fusion.1 = (bf16[256,2560]{1,0:T(8,128)(2,1)S(1)}, bf16[256,2560]{1,0:T(8,128)(2,1)S(1)}) fusion(f32[256,2560]{1,0:T(8,128)} %reshape.821, f32[2560]{0:T(1024)S(1)} %copy-done.7, f32[256]{0:T(256)S(1)} %get-tuple-element.63, f32[256,2560]{1,0:T(8,128)} %reshape.822, f32[256]{0:T(256)S(1)} %get-tuple-element.64), kind=kLoop, calls=%fused_computation.11 | loop fusion | flops 3932160 | bytes 7876608 | tf_op jit(solution)/shard_map/convert_element_type | solution.py:619
  48.8 1.5 convolution_convert_fusion.2
  50.3 1.5 convolution_convert_fusion.1
  52.2 0.8 slice-done.2
  53.0 5.8 %convolution_convert_fusion = bf16[512,2048]{1,0:T(8,128)(2,1)S(1)} fusion(bf16[2560,2048]{1,0:T(8,128)(2,1)S(1)} %bitcast.168, bf16[256,2560]{1,0:T(8,128)(2,1)S(1)} %get-tuple-element.62, bf16[256,2560]{1,0:T(8,128)(2,1)S(1)} %get-tuple-element.61), kind=kOutput, calls=%fused_computation.8 | convolution fusion | flops 5375000576 | bytes 15204352 | tf_op jit(solution)/shard_map/dot_general | solution.py:634
  59.1 1.6 copy-done.3
  60.8 1.3 constant_dynamic-slice_fusion.1
  62.1 0.8 gather_fusion
  62.9 1.1 multiply_cosine_fusion
  64.1 0.5 compare_select_fusion.1.len_ref
  64.7 1.0 collective-permute-done.2
  65.7 3.6 %convert_add_fusion = f32[1,256,3072]{2,1,0:T(8,128)} fusion(bf16[1,256,3072]{2,1,0:T(8,128)(2,1)S(1)} %collective-permute-done.2, bf16[2,256,3072]{2,1,0:T(8,128)(2,1)} %copy-done.3, s32[]{:T(128)S(6)} %select_n.191), kind=kLoop, calls=%fused_computation.7 | loop fusion | flops 2359296 | bytes 6291460 | tf_op jit(solution)/shard_map/add | solution.py:529
  69.3 4.8 %reshape_squeeze.7 = f32[64,4,3072]{2,1,0:T(4,128)} reshape(f32[1,256,3072]{2,1,0:T(8,128)} %convert_add_fusion) | data formatting | bytes 6291456 | tf_op jit(solution)/shard_map/reshape;squeeze | solution.py:644
  74.0 1.1 slice_bitcast_fusion.3
  75.2 1.1 slice_bitcast_fusion
  76.3 3.2 %slice.92 = f32[64,4,2048]{2,1,0:T(4,128)} slice(f32[64,4,3072]{2,1,0:T(4,128)} %reshape_squeeze.7), slice={[0:64], [0:4], [0:2048]} | slice | bytes 4194304 | tf_op jit(solution)/shard_map/slice | solution.py:648
  79.5 0.5 multiply_subtract_fusion
  80.0 2.5 %reshape.855 = f32[64,4,16,128]{3,2,1,0:T(8,128)S(1)} reshape(f32[64,4,2048]{2,1,0:T(4,128)} %slice.92) | data formatting | bytes 4194304 | tf_op jit(solution)/shard_map/reshape | solution.py:648
  82.5 0.7 fusion.58
  83.3 0.6 subtract_convert_fusion
  83.8 1.4 pad_maximum_fusion.2
  85.3 0.6 copy.215
  86.2 1.2 fusion.13
  87.4 0.5 copy.191
  87.9 1.6 gather_fusion.1
  89.7 0.8 fusion.15
  90.5 17.3 %shard_map.130 = (f32[50,64,1]{2,1,0:T(8,128)}, f32[50,64,1]{2,1,0:T(8,128)}, f32[50,64,128]{2,1,0:T(8,128)}) custom-call(s32[50]{0:T(128)} %compare_select_fusion.1.len_ref, s32[50]{0:T(128)} %blk_ref.1, bf16[50,64,128]{2,1,0:T(8,128)(2,1)} %gather_fusion.1, bf16[50,128,512]{2,1,0:T(8,128)(2,1)} %k_ref.1, bf16[50,128,512]{2,1,0:T(8,128)(2,1)} %v_ref.1), custom_call_target="tpu_custom_call" | custom-call | tf_op jit(solution)/shard_map/pallas_call | solution.py:499
  107.8 2.0 %reduce = f32[50,64]{1,0:T(8,128)S(1)} reduce(f32[50,64,1]{2,1,0:T(8,128)} %get-tuple-element.7, f32[]{:T(128)} %constant.111), dimensions={2}, to_apply=%get-tuple-element.7.reduce_sub_computation | reduce | bytes 25604 | tf_op jit(solution)/shard_map/pallas_call | solution.py:499
  109.9 0.9 select_reduce_fusion
  110.8 0.6 gather_fusion.2
  111.4 1.8 copy.173
  113.2 3.0 %multiply_reduce_fusion.1 = (f32[50,64]{1,0:T(8,128)S(1)}, f32[50,64]{1,0:T(8,128)S(1)}) fusion(f32[50,64,1]{2,1,0:T(8,128)} %get-tuple-element.8, f32[50,64,1]{2,1,0:T(8,128)S(1)} %copy-done.4, f32[50,64,1]{2,1,0:T(8,128)} %copy.173), kind=kLoop, calls=%fused_computation.17 | loop fusion | flops 6400 | bytes 64000 | tf_op jit(solution)/shard_map/mul | solution.py:683
  116.4 1.8 collective-permute-start.3
  118.3 0.5 broadcast_multiply_fusion
  118.8 2.2 %fusion.5 = f32[64,64,128]{2,0,1:T(8,128)S(1)} fusion(f32[50,64,128]{2,1,0:T(8,128)S(1)} %broadcast_multiply_fusion, s32[50]{0:T(128)S(1)} %copy-done.8), kind=kOutput, calls=%fused_computation.15 | convolution fusion | flops 314576000 | bytes 3735752 | tf_op jit(solution)/shard_map/rn,njh->rjh/dot_general | solution.py:685
  120.9 1.4 copy-done.5
  123.3 1.9 collective-permute-start.5
  125.5 1.6 collective-permute-done.5
  127.2 2.9 %collective-permute-start.7 = (f32[2,1,1,1,8,64]{5,4,3,2,1,0:T(8,128)S(1)}, f32[2,1,1,1,8,64]{5,4,3,2,1,0:T(8,128)S(1)}, u32[]{:S(2)}, u32[]{:S(2)}) collective-permute-start(f32[2,1,1,1,8,64]{5,4,3,2,1,0:T(8,128)S(1)} %get-tuple-element.60), channel_id=1, source_target_pairs={{0,4},{1,5},{2,6},{3,7},{4,0},{5,1},{6,2},{7,3},{8,12},{9,13},{10,... | collective-permute-start | bytes 12296 | tf_op jit(solution)/shard_map/ppermute | solution.py:568
  130.3 6.4 %collective-permute-done.4 = bf16[2,2,1,8,64,128]{5,3,2,1,0,4:T(8,128)(2,1)S(1)} collective-permute-done((bf16[2,2,1,8,64,128]{5,3,2,1,0,4:T(8,128)(2,1)S(1)}, bf16[2,2,1,8,64,128]{5,3,2,1,0,4:T(8,128)(2,1)S(1)}, u32[]{:S(2)}, u32[]{:S(2)}) %collective-permute-start.4) | collective-permute-done | bytes 524320 | tf_op jit(solution)/shard_map/ppermute | solution.py:569
  136.7 1.8 multiply_add_fusion
  138.6 1.6 collective-permute-start.6
  140.5 5.3 %collective-permute-done.6 = bf16[2,1,1,8,64,128]{5,3,2,1,0,4:T(8,128)(2,1)S(1)} collective-permute-done((bf16[2,1,1,8,64,128]{5,3,2,1,0,4:T(8,128)(2,1)S(1)}, bf16[2,1,1,8,64,128]{5,3,2,1,0,4:T(8,128)(2,1)S(1)}, u32[]{:S(2)}, u32[]{:S(2)}) %collective-permute-start.6) | collective-permute-done | bytes 262176 | tf_op jit(solution)/shard_map/ppermute | solution.py:569
  146.2 2.7 %collective-permute-start.8 = (bf16[1,1,1,8,64,128]{5,3,2,1,0,4:T(8,128)(2,1)S(1)}, bf16[1,1,1,8,64,128]{5,3,2,1,0,4:T(8,128)(2,1)S(1)}, u32[]{:S(2)}, u32[]{:S(2)}) collective-permute-start(bf16[1,1,1,8,64,128]{5,3,2,1,0,4:T(8,128)(2,1)S(1)} %dynamic-slice_convert_fusion.2), channel_id=1, source_target_pairs={{0,4},{1,5},{2,6},{3,7},{4,0},{5,1},{6,2},{7,3},{8,12},{9,13},{10,... | collective-permute-start | bytes 393224 | tf_op jit(solution)/shard_map/ppermute | solution.py:569
  148.9 0.8 multiply_add_fusion.4
  150.3 3.3 %collective-permute-done.8 = bf16[1,1,1,8,64,128]{5,3,2,1,0,4:T(8,128)(2,1)S(1)} collective-permute-done((bf16[1,1,1,8,64,128]{5,3,2,1,0,4:T(8,128)(2,1)S(1)}, bf16[1,1,1,8,64,128]{5,3,2,1,0,4:T(8,128)(2,1)S(1)}, u32[]{:S(2)}, u32[]{:S(2)}) %collective-permute-start.8) | collective-permute-done | bytes 131104 | tf_op jit(solution)/shard_map/ppermute | solution.py:569
  154.5 2.0 all_gather.4
  156.4 5.9 %fusion.2 = bf16[2,8,4,2560]{3,1,2,0:T(8,128)(2,1)S(1)} fusion(bf16[2,8,4,2048]{3,1,2,0:T(8,128)(2,1)S(1)} %all_gather.4, bf16[2048,2560]{1,0:T(8,128)(2,1)} %param.16), kind=kOutput, calls=%fused_computation.5 | convolution fusion | flops 671252480 | bytes 11075584 | tf_op jit(solution)/shard_map/dot_general | solution.py:716
  162.4 1.6 collective-permute-start.9
  163.9 4.8 %collective-permute-done.9 = bf16[1,8,4,2560]{3,1,2,0:T(8,128)(2,1)S(1)} collective-permute-done((bf16[1,8,4,2560]{3,1,2,0:T(8,128)(2,1)S(1)}, bf16[1,8,4,2560]{3,1,2,0:T(8,128)(2,1)S(1)}, u32[]{:S(2)}, u32[]{:S(2)}) %collective-permute-start.9) | collective-permute-done | bytes 163872 | tf_op jit(solution)/shard_map/ppermute | solution.py:528
  168.7 1.4 collective-permute-start.10
  170.1 8.5 %collective-permute-done.10 = bf16[1,8,4,2560]{3,1,2,0:T(8,128)(2,1)S(1)} collective-permute-done((bf16[1,8,4,2560]{3,1,2,0:T(8,128)(2,1)S(1)}, bf16[1,8,4,2560]{3,1,2,0:T(8,128)(2,1)S(1)}, u32[]{:S(2)}, u32[]{:S(2)}) %collective-permute-start.10) | collective-permute-done | bytes 163872 | tf_op jit(solution)/shard_map/ppermute | solution.py:541
  178.8 8.6 %collective-permute-done.11 = bf16[2,1,8,4,2560]{4,2,3,1,0:T(8,128)(2,1)S(1)} collective-permute-done((bf16[2,1,8,4,2560]{4,2,3,1,0:T(8,128)(2,1)S(1)}, bf16[2,1,8,4,2560]{4,2,3,1,0:T(8,128)(2,1)S(1)}, u32[]{:S(2)}, u32[]{:S(2)}) %collective-permute-start.11) | collective-permute-done | bytes 327712 | tf_op jit(solution)/shard_map/ppermute | solution.py:541
  187.8 1.8 slice.167
  189.7 1.1 fusion.64
  190.8 11.5 %collective-permute-done.12 = bf16[2,2,1,8,4,2560]{5,3,4,1,2,0:T(8,128)(2,1)S(1)} collective-permute-done((bf16[2,2,1,8,4,2560]{5,3,4,1,2,0:T(8,128)(2,1)S(1)}, bf16[2,2,1,8,4,2560]{5,3,4,1,2,0:T(8,128)(2,1)S(1)}, u32[]{:S(2)}, u32[]{:S(2)}) %collective-permute-start.12) | collective-permute-done | bytes 655392 | tf_op jit(solution)/shard_map/ppermute | solution.py:541
  202.8 2.1 %copy.205 = bf16[64,4,2560]{2,1,0:T(4,128)(2,1)} copy(bf16[64,4,2560]{2,0,1:T(8,128)(2,1)S(1)} %bitcast.143) | data formatting | bytes 2621440
  (85 shorter events, 6.7 us)
Async XLA Ops:
  0.6 48.1 %copy-start = (bf16[2560,512]{1,0:T(8,128)(2,1)S(1)}, bf16[2560,512]{1,0:T(8,128)(2,1)}, u32[]{:S(2)}) copy-start(bf16[2560,512]{1,0:T(8,128)(2,1)} %param.14) | copy-start | bytes 7864324
  0.6 32.1 %collective-permute-start = (bf16[64,4,2560]{2,1,0:T(4,128)(2,1)}, bf16[64,4,2560]{2,1,0:T(4,128)(2,1)}, u32[]{:S(2)}, u32[]{:S(2)}) collective-permute-start(bf16[64,4,2560]{2,1,0:T(4,128)(2,1)} %param.11), channel_id=1, source_target_pairs={{0,8},{8,0},{1,9},{9,1},{2,10},{10,2},{3,11},{11,3},{4,12},{12,4},... | collective-permute-start | bytes 3932168 | tf_op jit(solution)/shard_map/ppermute | solution.py:610
  8.3 24.4 %collective-permute-start.1 = (f32[256]{0:T(256)S(1)}, f32[256]{0:T(256)S(1)}, u32[]{:S(2)}, u32[]{:S(2)}) collective-permute-start(f32[256]{0:T(256)S(1)} %psum.7), channel_id=1, source_target_pairs={{0,8},{8,0},{1,9},{9,1},{2,10},{10,2},{3,11},{11,3},{4,12},{12,4},... | collective-permute-start | bytes 3080 | tf_op jit(solution)/shard_map/ppermute | solution.py:613
  41.6 4.0 %copy-start.7 = (f32[2560]{0:T(1024)S(1)}, f32[2560]{0:T(1024)}, u32[]{:S(2)}) copy-start(f32[2560]{0:T(1024)} %param.12) | copy-start | bytes 30724
  45.6 4.7 %copy-start.9 = (bf16[2560,512]{1,0:T(8,128)(2,1)S(1)}, bf16[2560,512]{1,0:T(8,128)(2,1)}, u32[]{:S(2)}) copy-start(bf16[2560,512]{1,0:T(8,128)(2,1)} %param.15) | copy-start | bytes 7864324
  48.8 3.1 %slice-start = ((s8[10485760]{0:T(1024)(128)(4,1)}), s8[4194304]{0:T(1024)(128)(4,1)S(1)}, s32[]{:S(2)}) async-start(s8[10485760]{0:T(1024)(128)(4,1)} %bitcast.167), calls=%async_computation | async-start | bytes 8388608
  48.8 3.4 %slice-start.1 = ((s8[10485760]{0:T(1024)(128)(4,1)}), s8[4194304]{0:T(1024)(128)(4,1)S(1)}, s32[]{:S(2)}) async-start(s8[10485760]{0:T(1024)(128)(4,1)} %bitcast.167), calls=%async_computation.1 | async-start | bytes 8388608
  50.3 2.7 %slice-start.2 = ((s8[10485760]{0:T(1024)(128)(4,1)}), s8[2097152]{0:T(1024)(128)(4,1)S(1)}, s32[]{:S(2)}) async-start(s8[10485760]{0:T(1024)(128)(4,1)} %bitcast.167), calls=%async_computation.2 | async-start | bytes 4194304
  59.1 1.6 copy-start.3
  60.8 1.3 copy-start.8
  60.8 1.3 copy-start.2
  62.0 3.6 %collective-permute-start.2 = (bf16[1,256,3072]{2,1,0:T(8,128)(2,1)}, bf16[1,256,3072]{2,1,0:T(8,128)(2,1)S(1)}, u32[]{:S(2)}, u32[]{:S(2)}) collective-permute-start(bf16[1,256,3072]{2,1,0:T(8,128)(2,1)} %constant_dynamic-slice_fusion.1), channel_id=1, source_target_pairs={{0,16},{16,0},{1,17},{17,1},{2,18},{18,2},{3,19},{19,3},{4,20},{20... | collective-permute-start | bytes 4718600 | tf_op jit(solution)/shard_map/ppermute | solution.py:528
  107.8 5.4 %copy-start.4 = (f32[50,64,1]{2,1,0:T(8,128)S(1)}, f32[50,64,1]{2,1,0:T(8,128)}, u32[]{:S(2)}) copy-start(f32[50,64,1]{2,1,0:T(8,128)} %get-tuple-element.7) | copy-start | bytes 38404
  113.2 5.0 %copy-start.6 = (f32[50,64,128]{2,1,0:T(8,128)S(1)}, f32[50,64,128]{2,1,0:T(8,128)}, u32[]{:S(2)}) copy-start(f32[50,64,128]{2,1,0:T(8,128)} %get-tuple-element.6) | copy-start | bytes 4915204
  116.4 6.9 %collective-permute-start.3 = (f32[2,2,2,1,8,64]{5,4,3,2,1,0:T(8,128)S(1)}, f32[2,2,2,1,8,64]{5,4,3,2,1,0:T(8,128)S(1)}, u32[]{:S(2)}, u32[]{:S(2)}) collective-permute-start(f32[2,2,2,1,8,64]{5,4,3,2,1,0:T(8,128)S(1)} %get-tuple-element.50), channel_id=1, source_target_pairs={{0,1},{1,0},{2,3},{3,2},{4,5},{5,4},{6,7},{7,6},{8,9},{9,8},{10,11... | collective-permute-start | bytes 49160 | tf_op jit(solution)/shard_map/ppermute | solution.py:568
  120.9 1.4 copy-start.5
  122.9 13.7 %collective-permute-start.4 = (bf16[2,2,1,8,64,128]{5,3,2,1,0,4:T(8,128)(2,1)S(1)}, bf16[2,2,1,8,64,128]{5,3,2,1,0,4:T(8,128)(2,1)S(1)}, u32[]{:S(2)}, u32[]{:S(2)}) collective-permute-start(bf16[2,2,1,8,64,128]{5,3,2,1,0,4:T(8,128)(2,1)S(1)} %dynamic-slice_convert_fusion), channel_id=1, source_target_pairs={{0,1},{1,0},{2,3},{3,2},{4,5},{5,4},{6,7},{7,6},{8,9},{9,8},{10,11... | collective-permute-start | bytes 1572872 | tf_op jit(solution)/shard_map/ppermute | solution.py:569
  123.3 3.8 %collective-permute-start.5 = (f32[2,2,1,1,8,64]{5,4,3,2,1,0:T(8,128)S(1)}, f32[2,2,1,1,8,64]{5,4,3,2,1,0:T(8,128)S(1)}, u32[]{:S(2)}, u32[]{:S(2)}) collective-permute-start(f32[2,2,1,1,8,64]{5,4,3,2,1,0:T(8,128)S(1)} %get-tuple-element.56), channel_id=1, source_target_pairs={{0,2},{1,3},{2,0},{3,1},{4,6},{5,7},{6,4},{7,5},{8,10},{9,11},{10,... | collective-permute-start | bytes 24584 | tf_op jit(solution)/shard_map/ppermute | solution.py:568
  127.2 13.1 %collective-permute-start.7 = (f32[2,1,1,1,8,64]{5,4,3,2,1,0:T(8,128)S(1)}, f32[2,1,1,1,8,64]{5,4,3,2,1,0:T(8,128)S(1)}, u32[]{:S(2)}, u32[]{:S(2)}) collective-permute-start(f32[2,1,1,1,8,64]{5,4,3,2,1,0:T(8,128)S(1)} %get-tuple-element.60), channel_id=1, source_target_pairs={{0,4},{1,5},{2,6},{3,7},{4,0},{5,1},{6,2},{7,3},{8,12},{9,13},{10,... | collective-permute-start | bytes 12296 | tf_op jit(solution)/shard_map/ppermute | solution.py:568
  138.6 7.3 %collective-permute-start.6 = (bf16[2,1,1,8,64,128]{5,3,2,1,0,4:T(8,128)(2,1)S(1)}, bf16[2,1,1,8,64,128]{5,3,2,1,0,4:T(8,128)(2,1)S(1)}, u32[]{:S(2)}, u32[]{:S(2)}) collective-permute-start(bf16[2,1,1,8,64,128]{5,3,2,1,0,4:T(8,128)(2,1)S(1)} %dynamic-slice_convert_fusion.1), channel_id=1, source_target_pairs={{0,2},{1,3},{2,0},{3,1},{4,6},{5,7},{6,4},{7,5},{8,10},{9,11},{10,... | collective-permute-start | bytes 786440 | tf_op jit(solution)/shard_map/ppermute | solution.py:569
  146.2 7.3 %collective-permute-start.8 = (bf16[1,1,1,8,64,128]{5,3,2,1,0,4:T(8,128)(2,1)S(1)}, bf16[1,1,1,8,64,128]{5,3,2,1,0,4:T(8,128)(2,1)S(1)}, u32[]{:S(2)}, u32[]{:S(2)}) collective-permute-start(bf16[1,1,1,8,64,128]{5,3,2,1,0,4:T(8,128)(2,1)S(1)} %dynamic-slice_convert_fusion.2), channel_id=1, source_target_pairs={{0,4},{1,5},{2,6},{3,7},{4,0},{5,1},{6,2},{7,3},{8,12},{9,13},{10,... | collective-permute-start | bytes 393224 | tf_op jit(solution)/shard_map/ppermute | solution.py:569
  162.4 6.3 %collective-permute-start.9 = (bf16[1,8,4,2560]{3,1,2,0:T(8,128)(2,1)S(1)}, bf16[1,8,4,2560]{3,1,2,0:T(8,128)(2,1)S(1)}, u32[]{:S(2)}, u32[]{:S(2)}) collective-permute-start(bf16[1,8,4,2560]{3,1,2,0:T(8,128)(2,1)S(1)} %constant_dynamic-slice_fusion), channel_id=1, source_target_pairs={{0,8},{8,0},{1,9},{9,1},{2,10},{10,2},{3,11},{11,3},{4,12},{12,4},... | collective-permute-start | bytes 491528 | tf_op jit(solution)/shard_map/ppermute | solution.py:528
  168.7 9.9 %collective-permute-start.10 = (bf16[1,8,4,2560]{3,1,2,0:T(8,128)(2,1)S(1)}, bf16[1,8,4,2560]{3,1,2,0:T(8,128)(2,1)S(1)}, u32[]{:S(2)}, u32[]{:S(2)}) collective-permute-start(bf16[1,8,4,2560]{3,1,2,0:T(8,128)(2,1)S(1)} %add_convert_fusion.1), channel_id=1, source_target_pairs={{0,4},{1,5},{2,6},{3,7},{4,0},{5,1},{6,2},{7,3},{8,12},{9,13},{10,... | collective-permute-start | bytes 491528 | tf_op jit(solution)/shard_map/ppermute | solution.py:541
  178.7 8.8 %collective-permute-start.11 = (bf16[2,1,8,4,2560]{4,2,3,1,0:T(8,128)(2,1)S(1)}, bf16[2,1,8,4,2560]{4,2,3,1,0:T(8,128)(2,1)S(1)}, u32[]{:S(2)}, u32[]{:S(2)}) collective-permute-start(bf16[2,1,8,4,2560]{4,2,3,1,0:T(8,128)(2,1)S(1)} %maximum_select_fusion.4), channel_id=1, source_target_pairs={{0,2},{1,3},{2,0},{3,1},{4,6},{5,7},{6,4},{7,5},{8,10},{9,11},{10,... | collective-permute-start | bytes 983048 | tf_op jit(solution)/shard_map/ppermute | solution.py:541
  187.5 14.9 %collective-permute-start.12 = (bf16[2,2,1,8,4,2560]{5,3,4,1,2,0:T(8,128)(2,1)S(1)}, bf16[2,2,1,8,4,2560]{5,3,4,1,2,0:T(8,128)(2,1)S(1)}, u32[]{:S(2)}, u32[]{:S(2)}) collective-permute-start(bf16[2,2,1,8,4,2560]{5,3,4,1,2,0:T(8,128)(2,1)S(1)} %maximum_select_fusion.2), channel_id=1, source_target_pairs={{0,1},{1,0},{2,3},{3,2},{4,5},{5,4},{6,7},{7,6},{8,9},{9,8},{10,11... | collective-permute-start | bytes 1966088 | tf_op jit(solution)/shard_map/ppermute | solution.py:541
  202.4 2.4 %copy-start.1 = (bf16[2560,512]{1,0:T(8,128)(2,1)S(1)}, bf16[2560,512]{1,0:T(8,128)(2,1)}, u32[]{:S(2)}) copy-start(bf16[2560,512]{1,0:T(8,128)(2,1)} %param.14) | copy-start | bytes 7864324

commit v10 on v6

--- a/solution.py
+++ b/solution.py
@@ -322,32 +322,29 @@
     parts_out = [
         jnp.dot(gathered, matrix, preferred_element_type=jnp.float32) for matrix in (wq, wk, wv)
     ]
-    output_projected = (
-        pair_scatter(
-            jnp.concatenate(parts_out, axis=-1)
-            .astype(jnp.bfloat16)
-            .reshape(lax.axis_size("row"), token_count, -1),
-            "row",
-            rounded=False,
-        )
-        .reshape(req_count, step_count, -1)
-    )
-    token_positions = lengths[:, None] + jnp.arange(step_count, dtype=jnp.int32)[None, :]
-    query_rows = rotary_apply(
-        output_projected[..., :q_width].reshape(req_count, step_count, -1, HEAD_SIZE),
-        token_positions,
-    ).astype(jnp.bfloat16)
+    head_count = (q_width + 2 * k_width) // HEAD_SIZE
+    output_projected = pair_scatter(
+        jnp.concatenate(parts_out, axis=-1)
+        .astype(jnp.bfloat16)
+        .reshape(lax.axis_size("row"), token_count, -1),
+        "row",
+        rounded=False,
+    ).reshape(token_count, head_count, HEAD_SIZE)
+    q_heads = q_width // HEAD_SIZE
+    token_positions = (
+        lengths[:, None] + jnp.arange(step_count, dtype=jnp.int32)[None, :]
+    ).reshape(token_count)
+    query_rows = rotary_apply(output_projected[:, :q_heads], token_positions).astype(jnp.bfloat16)
     query_rows = query_rows.reshape(req_count, step_count, heads_kv, QUERY_PER_KEY, HEAD_SIZE)
-    current_key = rotary_apply(
-        output_projected[..., q_width : q_width + k_width].reshape(
-            req_count, step_count, heads_kv, HEAD_SIZE
-        ),
-        token_positions,
-    ).astype(jnp.bfloat16)
+    current_key = (
+        rotary_apply(output_projected[:, q_heads : q_heads + heads_kv], token_positions)
+        .astype(jnp.bfloat16)
+        .reshape(req_count, step_count, heads_kv, HEAD_SIZE)
+    )
     current_value = (
-        output_projected[..., q_width + k_width :]
+        output_projected[:, q_heads + heads_kv :]
+        .astype(jnp.bfloat16)
         .reshape(req_count, step_count, heads_kv, HEAD_SIZE)
-        .astype(jnp.bfloat16)
     )
     picked = jnp.minimum(slot_request, req_count - 1)
     in_use = slot_request < req_count

time: 196 us -> 182 us (0.929)
  local copies, waits for them, and re-layouts: 34.5 us -> 22.4 us
  other arithmetic: 25.8 us -> 22.6 us
    slice x3 -> x1, local copies, waits for them, and re-layouts: 5.8 us -> 0.12 us  [on_device(): output_projected[:, q_heads + heads_kv:].astype(jnp.bfloat16)]
    another operation x1, local copies, waits for them, and re-layouts: 4.79 us -> 0.8 us  [on_device(): current_value.reshape(req_count, step_count, k_width)]
    add x1 -> x0, other arithmetic: 3.59 us -> none  [pair_scatter(): total = (keep.astype(jnp.float32) + got.astype(jnp.float32))[0]]
    reshape x2 -> x0, local copies, waits for them, and re-layouts: 3.41 us -> none  [the longest x1 2.34 us: on_device(): output_projected[..., :q_width]]
    unnamed x27 -> x30, local copies, waits for them, and re-layouts: 6.29 us -> 6.82 us
where the time goes in v10:
time: 182 us; the launch traced here: 181 us
  waiting for transfers between devices  77 us (42%)
  other arithmetic  22.6 us (12%)
  local copies, waits for them, and re-layouts  22.4 us (12%)
  matrix products  18.8 us (10%)
  starting transfers between devices  17.5 us (10%)
  Pallas kernels  17.2 us (9%)
  blocking collectives  4.46 us (2%)
    ppermute x3, waiting for transfers between devices, doubling_gather(): got = lax.ppermute(block, axis_name, pairs)  29.7 us
    ppermute x1, waiting for transfers between devices, on_device(): other_squares = lax.ppermute(squares, 'col', swap)  24.4 us
    pallas_call x1, Pallas kernels, slot_attention(): pl.pallas_call(partial(slot_kernel, ns=ns, heads=heads, qpk=qpk), grid_sp...  17.2 us
    ppermute x3, waiting for transfers between devices, seq_merge(): lax.ppermute(send_values.astype(jnp.bfloat16), 'seq', pairs)  15 us
    dot_general x3, matrix products, on_device(): jnp.dot(gathered, matrix, preferred_element_type=jnp.float32)  8.8 us
    unnamed x30, local copies, waits for them, and re-layouts  6.82 us
    ppermute x3, starting transfers between devices, seq_merge(): got_stats = lax.ppermute(send_stats, 'seq', pairs)  6.64 us
    ppermute x2, waiting for transfers between devices, pair_scatter(): got = lax.ppermute(send, axis_name, [(0, 1), (1, 0)])  6.22 us
  transfers between devices with their start and end apart: 13, of which 10 were waited for; matrix products, arithmetic and copies ran while one was open for 8% of the time, Pallas kernels for 0%

profile of v10, /device:TPU:0, one launch (start us, length us, event | category | flops | bytes accessed | tf_op | source)
XLA Modules:
  0.0 181.2 jit_solution(6282568540332369445)
XLA Ops:
  0.7 3.5 %reshape.846 = bf16[256,2560]{1,0:T(8,128)(2,1)} reshape(bf16[64,4,2560]{2,1,0:T(4,128)(2,1)} %param.11) | data formatting | bytes 2621440 | tf_op jit(solution)/shard_map/reshape | solution.py:298
  4.2 2.9 %collective-permute-start = (bf16[256,2560]{1,0:T(8,128)(2,1)}, bf16[256,2560]{1,0:T(8,128)(2,1)}, u32[]{:S(2)}, u32[]{:S(2)}) collective-permute-start(bf16[256,2560]{1,0:T(8,128)(2,1)} %reshape.846), channel_id=1, source_target_pairs={{0,8},{8,0},{1,9},{9,1},{2,10},{10,2},{3,11},{11,3},{4,12},{12,4},... | collective-permute-start | bytes 3932168 | tf_op jit(solution)/shard_map/ppermute | solution.py:301
  7.1 2.1 %multiply_reduce_fusion = f32[64,4]{1,0:T(8,128)S(1)} fusion(bf16[64,4,2560]{2,1,0:T(4,128)(2,1)} %param.11), kind=kLoop, calls=%fused_computation.12 | loop fusion | flops 1965824 | bytes 1311744 | tf_op jit(solution)/shard_map/reduce_sum | solution.py:303
  9.3 2.5 %psum.7 = f32[256]{0:T(256)S(1)} all-reduce(f32[256]{0:T(256)S(1)} %reduce_sum.21), channel_id=1, replica_groups=mesh['row'=2,'col'=2,'seq'=8] {'row'}, use_global_device_ids=true, to_apply=%region_1.0 | all-reduce | flops 256 | bytes 2048 | tf_op jit(solution)/shard_map/psum | solution.py:303
  11.8 24.4 %collective-permute-done.1 = f32[256]{0:T(256)S(1)} collective-permute-done((f32[256]{0:T(256)S(1)}, f32[256]{0:T(256)S(1)}, u32[]{:S(2)}, u32[]{:S(2)}) %collective-permute-start.1) | collective-permute-done | bytes 1056 | tf_op jit(solution)/shard_map/ppermute | solution.py:304
  36.3 2.8 %multiply_convert_fusion.1 = (bf16[256,2560]{1,0:T(8,128)(2,1)S(1)}, bf16[256,2560]{1,0:T(8,128)(2,1)S(1)}) fusion(f32[2560]{0:T(1024)S(1)} %copy-done.8, f32[256]{0:T(256)S(1)} %get-tuple-element.54, bf16[256,2560]{1,0:T(8,128)(2,1)} %reshape.846, bf16[256,2560]{1,0:T(8,128)(2,1)} %collective-permute-done, pred[]{:T(512)S(6)} %eq.72, ...), kind=kLoop, calls=%fused_computation.11 | loop fusion | flops 6553600 | bytes 5255169 | tf_op jit(solution)/shard_map/convert_element_type | solution.py:308
  39.1 1.5 convolution_convert_fusion.2
  40.7 1.5 convolution_convert_fusion.1
  42.2 0.4 slice-done.1
  42.6 0.8 slice-done.2
  43.4 5.8 %convolution_convert_fusion = bf16[512,2048]{1,0:T(8,128)(2,1)S(1)} fusion(bf16[2560,2048]{1,0:T(8,128)(2,1)S(1)} %bitcast.175, bf16[256,2560]{1,0:T(8,128)(2,1)S(1)} %get-tuple-element.37, bf16[256,2560]{1,0:T(8,128)(2,1)S(1)} %get-tuple-element.36), kind=kOutput, calls=%fused_computation.8 | convolution fusion | flops 5375000576 | bytes 15204352 | tf_op jit(solution)/shard_map/dot_general | solution.py:323
  49.2 0.3 pad_maximum_fusion
  49.5 1.6 copy-done.3
  51.1 1.3 constant_dynamic-slice_fusion.2
  52.4 0.8 gather_fusion
  53.4 0.5 compare_select_fusion.1.len_ref
  54.0 0.5 multiply_cosine_fusion
  54.6 1.5 collective-permute-done.2
  56.0 1.9 %add_bitcast_fusion = f32[32,8,24,128]{3,1,2,0:T(8,128)S(1)} fusion(bf16[1,256,3072]{2,1,0:T(8,128)(2,1)S(1)} %collective-permute-done.2, bf16[2,256,3072]{2,1,0:T(8,128)(2,1)} %copy-done.3, s32[]{:T(128)S(6)} %select_n.191), kind=kLoop, calls=%fused_computation.7 | loop fusion | flops 2359296 | bytes 6291460
  57.9 0.6 copy.198
  58.6 0.4 add_convert_fusion.1
  59.1 0.8 subtract_convert_fusion
  59.9 1.4 pad_maximum_fusion.2
  61.3 0.5 copy.182
  62.0 1.3 fusion.13
  63.3 0.5 copy.161
  64.0 0.8 fusion.15
  64.8 1.6 gather_fusion.1
  66.3 17.2 %shard_map.130 = (f32[50,64,1]{2,1,0:T(8,128)}, f32[50,64,1]{2,1,0:T(8,128)}, f32[50,64,128]{2,1,0:T(8,128)}) custom-call(s32[50]{0:T(128)} %compare_select_fusion.1.len_ref, s32[50]{0:T(128)} %blk_ref.1, bf16[50,64,128]{2,1,0:T(8,128)(2,1)} %gather_fusion.1, bf16[50,128,512]{2,1,0:T(8,128)(2,1)} %k_ref.1, bf16[50,128,512]{2,1,0:T(8,128)(2,1)} %v_ref.1), custom_call_target="tpu_custom_call" | custom-call | tf_op jit(solution)/shard_map/pallas_call | solution.py:189
  83.6 2.0 %reduce.1 = f32[50,64]{1,0:T(8,128)S(1)} reduce(f32[50,64,1]{2,1,0:T(8,128)} %get-tuple-element.7, f32[]{:T(128)} %constant.111), dimensions={2}, to_apply=%get-tuple-element.7.reduce_sub_computation | reduce | bytes 25604 | tf_op jit(solution)/shard_map/pallas_call | solution.py:189
  85.6 0.9 select_reduce_fusion
  86.5 0.6 gather_fusion.2
  87.1 1.8 copy.139
  88.9 3.0 %multiply_reduce_fusion.1 = (f32[50,64]{1,0:T(8,128)S(1)}, f32[50,64]{1,0:T(8,128)S(1)}) fusion(f32[50,64,1]{2,1,0:T(8,128)} %get-tuple-element.8, f32[50,64,1]{2,1,0:T(8,128)S(1)} %copy-done.4, f32[50,64,1]{2,1,0:T(8,128)} %copy.139), kind=kLoop, calls=%fused_computation.17 | loop fusion | flops 6400 | bytes 64000 | tf_op jit(solution)/shard_map/mul | solution.py:369
  92.1 1.8 %collective-permute-start.3 = (f32[2,2,2,1,8,64]{5,4,3,2,1,0:T(8,128)S(1)}, f32[2,2,2,1,8,64]{5,4,3,2,1,0:T(8,128)S(1)}, u32[]{:S(2)}, u32[]{:S(2)}) collective-permute-start(f32[2,2,2,1,8,64]{5,4,3,2,1,0:T(8,128)S(1)} %get-tuple-element.45), channel_id=1, source_target_pairs={{0,1},{1,0},{2,3},{3,2},{4,5},{5,4},{6,7},{7,6},{8,9},{9,8},{10,11... | collective-permute-start | bytes 49160 | tf_op jit(solution)/shard_map/ppermute | solution.py:258
  94.0 0.5 broadcast_multiply_fusion
  94.5 2.2 %fusion.5 = f32[64,64,128]{2,0,1:T(8,128)S(1)} fusion(f32[50,64,128]{2,1,0:T(8,128)S(1)} %broadcast_multiply_fusion, s32[50]{0:T(128)S(1)} %copy-done.9), kind=kOutput, calls=%fused_computation.15 | convolution fusion | flops 314576000 | bytes 3735752 | tf_op jit(solution)/shard_map/rn,njh->rjh/dot_general | solution.py:371
  96.7 1.3 copy-done.5
  98.1 0.6 constant_dynamic-slice_fusion
  98.8 0.5 copy.168
  99.6 1.9 %collective-permute-start.5 = (f32[2,2,1,1,8,64]{5,4,3,2,1,0:T(8,128)S(1)}, f32[2,2,1,1,8,64]{5,4,3,2,1,0:T(8,128)S(1)}, u32[]{:S(2)}, u32[]{:S(2)}) collective-permute-start(f32[2,2,1,1,8,64]{5,4,3,2,1,0:T(8,128)S(1)} %get-tuple-element.49), channel_id=1, source_target_pairs={{0,2},{1,3},{2,0},{3,1},{4,6},{5,7},{6,4},{7,5},{8,10},{9,11},{10,... | collective-permute-start | bytes 24584 | tf_op jit(solution)/shard_map/ppermute | solution.py:258
  101.8 1.6 collective-permute-done.5
  103.5 2.9 %collective-permute-start.7 = (f32[2,1,1,1,8,64]{5,4,3,2,1,0:T(8,128)S(1)}, f32[2,1,1,1,8,64]{5,4,3,2,1,0:T(8,128)S(1)}, u32[]{:S(2)}, u32[]{:S(2)}) collective-permute-start(f32[2,1,1,1,8,64]{5,4,3,2,1,0:T(8,128)S(1)} %get-tuple-element.53), channel_id=1, source_target_pairs={{0,4},{1,5},{2,6},{3,7},{4,0},{5,1},{6,2},{7,3},{8,12},{9,13},{10,... | collective-permute-start | bytes 12296 | tf_op jit(solution)/shard_map/ppermute | solution.py:258
  106.6 6.4 %collective-permute-done.4 = bf16[2,2,1,8,64,128]{5,3,2,1,0,4:T(8,128)(2,1)S(1)} collective-permute-done((bf16[2,2,1,8,64,128]{5,3,2,1,0,4:T(8,128)(2,1)S(1)}, bf16[2,2,1,8,64,128]{5,3,2,1,0,4:T(8,128)(2,1)S(1)}, u32[]{:S(2)}, u32[]{:S(2)}) %collective-permute-start.4) | collective-permute-done | bytes 524320 | tf_op jit(solution)/shard_map/ppermute | solution.py:259
  113.0 1.8 %multiply_add_fusion = f32[2,2,1,8,64,128]{5,3,2,1,0,4:T(8,128)S(1)} fusion(bf16[2,2,1,8,64,128]{5,3,2,1,0,4:T(8,128)(2,1)S(1)} %collective-permute-done.4, f32[2,2,2,8,64,128]{5,3,2,1,0,4:T(8,128)} %bitcast.146, s32[]{:T(128)S(6)} %select_n.194, f32[2,2,8,64]{2,1,0,3:T(2,128)S(1)} %copy.143, f32[2,2,8,64]{2,1,0,3:T(2,128)S(1)} %copy.142), kind=kLoop, calls=%fused_computation.31 | loop fusion | flops 1048576 | bytes 2637828 | tf_op jit(solution)/shard_map/add | solution.py:268
  114.9 1.6 collective-permute-start.6
  116.9 5.3 %collective-permute-done.6 = bf16[2,1,1,8,64,128]{5,3,2,1,0,4:T(8,128)(2,1)S(1)} collective-permute-done((bf16[2,1,1,8,64,128]{5,3,2,1,0,4:T(8,128)(2,1)S(1)}, bf16[2,1,1,8,64,128]{5,3,2,1,0,4:T(8,128)(2,1)S(1)}, u32[]{:S(2)}, u32[]{:S(2)}) %collective-permute-start.6) | collective-permute-done | bytes 262176 | tf_op jit(solution)/shard_map/ppermute | solution.py:259
  122.2 0.3 multiply_add_fusion.1
  122.6 2.7 %collective-permute-start.8 = (bf16[1,1,1,8,64,128]{5,3,2,1,0,4:T(8,128)(2,1)S(1)}, bf16[1,1,1,8,64,128]{5,3,2,1,0,4:T(8,128)(2,1)S(1)}, u32[]{:S(2)}, u32[]{:S(2)}) collective-permute-start(bf16[1,1,1,8,64,128]{5,3,2,1,0,4:T(8,128)(2,1)S(1)} %dynamic-slice_convert_fusion.2), channel_id=1, source_target_pairs={{0,4},{1,5},{2,6},{3,7},{4,0},{5,1},{6,2},{7,3},{8,12},{9,13},{10,... | collective-permute-start | bytes 393224 | tf_op jit(solution)/shard_map/ppermute | solution.py:259
  125.2 0.8 multiply_add_fusion.3
  126.6 3.3 %collective-permute-done.8 = bf16[1,1,1,8,64,128]{5,3,2,1,0,4:T(8,128)(2,1)S(1)} collective-permute-done((bf16[1,1,1,8,64,128]{5,3,2,1,0,4:T(8,128)(2,1)S(1)}, bf16[1,1,1,8,64,128]{5,3,2,1,0,4:T(8,128)(2,1)S(1)}, u32[]{:S(2)}, u32[]{:S(2)}) %collective-permute-start.8) | collective-permute-done | bytes 131104 | tf_op jit(solution)/shard_map/ppermute | solution.py:259
  130.2 0.5 fusion.11
  130.8 2.0 %all_gather.4 = bf16[2,8,4,2048]{3,1,2,0:T(8,128)(2,1)S(1)} all-gather(bf16[1,8,4,2048]{3,1,2,0:T(8,128)(2,1)S(1)} %convert_element_type.116), channel_id=1, replica_groups=mesh['row'=2,'col'=2,'seq'=8] {'row'}, dimensions={0}, use_global_device_ids=true | all-gather | bytes 393216 | tf_op jit(solution)/shard_map/all_gather | solution.py:400
  132.8 5.9 %fusion.2 = bf16[2,8,4,2560]{3,1,2,0:T(8,128)(2,1)S(1)} fusion(bf16[2,8,4,2048]{3,1,2,0:T(8,128)(2,1)S(1)} %all_gather.4, bf16[2048,2560]{1,0:T(8,128)(2,1)} %param.16), kind=kOutput, calls=%fused_computation.5 | convolution fusion | flops 671252480 | bytes 11075584 | tf_op jit(solution)/shard_map/dot_general | solution.py:402
  138.7 1.5 collective-permute-start.9
  140.2 4.8 %collective-permute-done.9 = bf16[1,8,4,2560]{3,1,2,0:T(8,128)(2,1)S(1)} collective-permute-done((bf16[1,8,4,2560]{3,1,2,0:T(8,128)(2,1)S(1)}, bf16[1,8,4,2560]{3,1,2,0:T(8,128)(2,1)S(1)}, u32[]{:S(2)}, u32[]{:S(2)}) %collective-permute-start.9) | collective-permute-done | bytes 163872 | tf_op jit(solution)/shard_map/ppermute | solution.py:218
  145.1 1.4 collective-permute-start.10
  146.4 8.5 %collective-permute-done.10 = bf16[1,8,4,2560]{3,1,2,0:T(8,128)(2,1)S(1)} collective-permute-done((bf16[1,8,4,2560]{3,1,2,0:T(8,128)(2,1)S(1)}, bf16[1,8,4,2560]{3,1,2,0:T(8,128)(2,1)S(1)}, u32[]{:S(2)}, u32[]{:S(2)}) %collective-permute-start.10) | collective-permute-done | bytes 163872 | tf_op jit(solution)/shard_map/ppermute | solution.py:231
  155.1 8.6 %collective-permute-done.11 = bf16[2,1,8,4,2560]{4,2,3,1,0:T(8,128)(2,1)S(1)} collective-permute-done((bf16[2,1,8,4,2560]{4,2,3,1,0:T(8,128)(2,1)S(1)}, bf16[2,1,8,4,2560]{4,2,3,1,0:T(8,128)(2,1)S(1)}, u32[]{:S(2)}, u32[]{:S(2)}) %collective-permute-start.11) | collective-permute-done | bytes 327712 | tf_op jit(solution)/shard_map/ppermute | solution.py:231
  164.2 0.8 reshape_reshape.8
  165.0 0.4 pad_maximum_fusion.6
  165.3 0.8 convert_element_type.121
  166.2 12.5 %collective-permute-done.12 = bf16[2,2,1,8,4,2560]{5,3,4,1,2,0:T(8,128)(2,1)S(1)} collective-permute-done((bf16[2,2,1,8,4,2560]{5,3,4,1,2,0:T(8,128)(2,1)S(1)}, bf16[2,2,1,8,4,2560]{5,3,4,1,2,0:T(8,128)(2,1)S(1)}, u32[]{:S(2)}, u32[]{:S(2)}) %collective-permute-start.12) | collective-permute-done | bytes 655392 | tf_op jit(solution)/shard_map/ppermute | solution.py:231
  179.1 2.1 %copy.177 = bf16[64,4,2560]{2,1,0:T(4,128)(2,1)} copy(bf16[64,4,2560]{2,0,1:T(8,128)(2,1)S(1)} %bitcast.147) | data formatting | bytes 2621440
  (83 shorter events, 4.6 us)
Async XLA Ops:
  0.6 38.5 %copy-start = (bf16[2560,512]{1,0:T(8,128)(2,1)S(1)}, bf16[2560,512]{1,0:T(8,128)(2,1)}, u32[]{:S(2)}) copy-start(bf16[2560,512]{1,0:T(8,128)(2,1)} %param.14) | copy-start | bytes 7864324
  0.6 35.6 %copy-start.8 = (f32[2560]{0:T(1024)S(1)}, f32[2560]{0:T(1024)}, u32[]{:S(2)}) copy-start(f32[2560]{0:T(1024)} %param.12) | copy-start | bytes 30724
  4.2 32.0 %collective-permute-start = (bf16[256,2560]{1,0:T(8,128)(2,1)}, bf16[256,2560]{1,0:T(8,128)(2,1)}, u32[]{:S(2)}, u32[]{:S(2)}) collective-permute-start(bf16[256,2560]{1,0:T(8,128)(2,1)} %reshape.846), channel_id=1, source_target_pairs={{0,8},{8,0},{1,9},{9,1},{2,10},{10,2},{3,11},{11,3},{4,12},{12,4},... | collective-permute-start | bytes 3932168 | tf_op jit(solution)/shard_map/ppermute | solution.py:301
  11.8 24.4 %collective-permute-start.1 = (f32[256]{0:T(256)S(1)}, f32[256]{0:T(256)S(1)}, u32[]{:S(2)}, u32[]{:S(2)}) collective-permute-start(f32[256]{0:T(256)S(1)} %psum.7), channel_id=1, source_target_pairs={{0,8},{8,0},{1,9},{9,1},{2,10},{10,2},{3,11},{11,3},{4,12},{12,4},... | collective-permute-start | bytes 3080 | tf_op jit(solution)/shard_map/ppermute | solution.py:304
  36.3 4.4 %copy-start.10 = (bf16[2560,512]{1,0:T(8,128)(2,1)S(1)}, bf16[2560,512]{1,0:T(8,128)(2,1)}, u32[]{:S(2)}) copy-start(bf16[2560,512]{1,0:T(8,128)(2,1)} %param.15) | copy-start | bytes 7864324
  39.1 3.1 %slice-start = ((s8[10485760]{0:T(1024)(128)(4,1)}), s8[4194304]{0:T(1024)(128)(4,1)S(1)}, s32[]{:S(2)}) async-start(s8[10485760]{0:T(1024)(128)(4,1)} %bitcast.174), calls=%async_computation | async-start | bytes 8388608
  39.1 3.5 %slice-start.1 = ((s8[10485760]{0:T(1024)(128)(4,1)}), s8[4194304]{0:T(1024)(128)(4,1)S(1)}, s32[]{:S(2)}) async-start(s8[10485760]{0:T(1024)(128)(4,1)} %bitcast.174), calls=%async_computation.1 | async-start | bytes 8388608
  40.7 2.7 %slice-start.2 = ((s8[10485760]{0:T(1024)(128)(4,1)}), s8[2097152]{0:T(1024)(128)(4,1)S(1)}, s32[]{:S(2)}) async-start(s8[10485760]{0:T(1024)(128)(4,1)} %bitcast.174), calls=%async_computation.2 | async-start | bytes 4194304
  49.5 1.6 copy-start.3
  51.1 1.3 copy-start.9
  51.1 1.3 copy-start.2
  52.4 3.6 %collective-permute-start.2 = (bf16[1,256,3072]{2,1,0:T(8,128)(2,1)}, bf16[1,256,3072]{2,1,0:T(8,128)(2,1)S(1)}, u32[]{:S(2)}, u32[]{:S(2)}) collective-permute-start(bf16[1,256,3072]{2,1,0:T(8,128)(2,1)} %constant_dynamic-slice_fusion.2), channel_id=1, source_target_pairs={{0,16},{16,0},{1,17},{17,1},{2,18},{18,2},{3,19},{19,3},{4,20},{20... | collective-permute-start | bytes 4718600 | tf_op jit(solution)/shard_map/ppermute | solution.py:218
  83.6 5.4 %copy-start.4 = (f32[50,64,1]{2,1,0:T(8,128)S(1)}, f32[50,64,1]{2,1,0:T(8,128)}, u32[]{:S(2)}) copy-start(f32[50,64,1]{2,1,0:T(8,128)} %get-tuple-element.7) | copy-start | bytes 38404
  88.9 5.1 %copy-start.6 = (f32[50,64,128]{2,1,0:T(8,128)S(1)}, f32[50,64,128]{2,1,0:T(8,128)}, u32[]{:S(2)}) copy-start(f32[50,64,128]{2,1,0:T(8,128)} %get-tuple-element.6) | copy-start | bytes 4915204
  92.1 7.4 %collective-permute-start.3 = (f32[2,2,2,1,8,64]{5,4,3,2,1,0:T(8,128)S(1)}, f32[2,2,2,1,8,64]{5,4,3,2,1,0:T(8,128)S(1)}, u32[]{:S(2)}, u32[]{:S(2)}) collective-permute-start(f32[2,2,2,1,8,64]{5,4,3,2,1,0:T(8,128)S(1)} %get-tuple-element.45), channel_id=1, source_target_pairs={{0,1},{1,0},{2,3},{3,2},{4,5},{5,4},{6,7},{7,6},{8,9},{9,8},{10,11... | collective-permute-start | bytes 49160 | tf_op jit(solution)/shard_map/ppermute | solution.py:258
  96.7 1.3 copy-start.5
  99.3 13.8 %collective-permute-start.4 = (bf16[2,2,1,8,64,128]{5,3,2,1,0,4:T(8,128)(2,1)S(1)}, bf16[2,2,1,8,64,128]{5,3,2,1,0,4:T(8,128)(2,1)S(1)}, u32[]{:S(2)}, u32[]{:S(2)}) collective-permute-start(bf16[2,2,1,8,64,128]{5,3,2,1,0,4:T(8,128)(2,1)S(1)} %dynamic-slice_convert_fusion), channel_id=1, source_target_pairs={{0,1},{1,0},{2,3},{3,2},{4,5},{5,4},{6,7},{7,6},{8,9},{9,8},{10,11... | collective-permute-start | bytes 1572872 | tf_op jit(solution)/shard_map/ppermute | solution.py:259
  99.6 3.8 %collective-permute-start.5 = (f32[2,2,1,1,8,64]{5,4,3,2,1,0:T(8,128)S(1)}, f32[2,2,1,1,8,64]{5,4,3,2,1,0:T(8,128)S(1)}, u32[]{:S(2)}, u32[]{:S(2)}) collective-permute-start(f32[2,2,1,1,8,64]{5,4,3,2,1,0:T(8,128)S(1)} %get-tuple-element.49), channel_id=1, source_target_pairs={{0,2},{1,3},{2,0},{3,1},{4,6},{5,7},{6,4},{7,5},{8,10},{9,11},{10,... | collective-permute-start | bytes 24584 | tf_op jit(solution)/shard_map/ppermute | solution.py:258
  103.5 13.1 %collective-permute-start.7 = (f32[2,1,1,1,8,64]{5,4,3,2,1,0:T(8,128)S(1)}, f32[2,1,1,1,8,64]{5,4,3,2,1,0:T(8,128)S(1)}, u32[]{:S(2)}, u32[]{:S(2)}) collective-permute-start(f32[2,1,1,1,8,64]{5,4,3,2,1,0:T(8,128)S(1)} %get-tuple-element.53), channel_id=1, source_target_pairs={{0,4},{1,5},{2,6},{3,7},{4,0},{5,1},{6,2},{7,3},{8,12},{9,13},{10,... | collective-permute-start | bytes 12296 | tf_op jit(solution)/shard_map/ppermute | solution.py:258
  114.8 15.3 %copy-start.7 = (bf16[8,4,4,128]{3,2,1,0:T(4,128)(2,1)S(1)}, bf16[8,4,4,128]{3,2,1,0:T(4,128)(2,1)}, u32[]{:S(2)}) copy-start(bf16[8,4,4,128]{3,2,1,0:T(4,128)(2,1)} %constant_dynamic-slice_fusion) | copy-start | bytes 98308
  114.9 7.3 %collective-permute-start.6 = (bf16[2,1,1,8,64,128]{5,3,2,1,0,4:T(8,128)(2,1)S(1)}, bf16[2,1,1,8,64,128]{5,3,2,1,0,4:T(8,128)(2,1)S(1)}, u32[]{:S(2)}, u32[]{:S(2)}) collective-permute-start(bf16[2,1,1,8,64,128]{5,3,2,1,0,4:T(8,128)(2,1)S(1)} %dynamic-slice_convert_fusion.1), channel_id=1, source_target_pairs={{0,2},{1,3},{2,0},{3,1},{4,6},{5,7},{6,4},{7,5},{8,10},{9,11},{10,... | collective-permute-start | bytes 786440 | tf_op jit(solution)/shard_map/ppermute | solution.py:259
  122.6 7.3 %collective-permute-start.8 = (bf16[1,1,1,8,64,128]{5,3,2,1,0,4:T(8,128)(2,1)S(1)}, bf16[1,1,1,8,64,128]{5,3,2,1,0,4:T(8,128)(2,1)S(1)}, u32[]{:S(2)}, u32[]{:S(2)}) collective-permute-start(bf16[1,1,1,8,64,128]{5,3,2,1,0,4:T(8,128)(2,1)S(1)} %dynamic-slice_convert_fusion.2), channel_id=1, source_target_pairs={{0,4},{1,5},{2,6},{3,7},{4,0},{5,1},{6,2},{7,3},{8,12},{9,13},{10,... | collective-permute-start | bytes 393224 | tf_op jit(solution)/shard_map/ppermute | solution.py:259
  138.7 6.3 %collective-permute-start.9 = (bf16[1,8,4,2560]{3,1,2,0:T(8,128)(2,1)S(1)}, bf16[1,8,4,2560]{3,1,2,0:T(8,128)(2,1)S(1)}, u32[]{:S(2)}, u32[]{:S(2)}) collective-permute-start(bf16[1,8,4,2560]{3,1,2,0:T(8,128)(2,1)S(1)} %constant_dynamic-slice_fusion.1), channel_id=1, source_target_pairs={{0,8},{8,0},{1,9},{9,1},{2,10},{10,2},{3,11},{11,3},{4,12},{12,4},... | collective-permute-start | bytes 491528 | tf_op jit(solution)/shard_map/ppermute | solution.py:218
  145.1 9.9 %collective-permute-start.10 = (bf16[1,8,4,2560]{3,1,2,0:T(8,128)(2,1)S(1)}, bf16[1,8,4,2560]{3,1,2,0:T(8,128)(2,1)S(1)}, u32[]{:S(2)}, u32[]{:S(2)}) collective-permute-start(bf16[1,8,4,2560]{3,1,2,0:T(8,128)(2,1)S(1)} %add_convert_fusion.2), channel_id=1, source_target_pairs={{0,4},{1,5},{2,6},{3,7},{4,0},{5,1},{6,2},{7,3},{8,12},{9,13},{10,... | collective-permute-start | bytes 491528 | tf_op jit(solution)/shard_map/ppermute | solution.py:231
  155.0 8.8 %collective-permute-start.11 = (bf16[2,1,8,4,2560]{4,2,3,1,0:T(8,128)(2,1)S(1)}, bf16[2,1,8,4,2560]{4,2,3,1,0:T(8,128)(2,1)S(1)}, u32[]{:S(2)}, u32[]{:S(2)}) collective-permute-start(bf16[2,1,8,4,2560]{4,2,3,1,0:T(8,128)(2,1)S(1)} %maximum_select_fusion.4), channel_id=1, source_target_pairs={{0,2},{1,3},{2,0},{3,1},{4,6},{5,7},{6,4},{7,5},{8,10},{9,11},{10,... | collective-permute-start | bytes 983048 | tf_op jit(solution)/shard_map/ppermute | solution.py:231
  163.9 14.9 %collective-permute-start.12 = (bf16[2,2,1,8,4,2560]{5,3,4,1,2,0:T(8,128)(2,1)S(1)}, bf16[2,2,1,8,4,2560]{5,3,4,1,2,0:T(8,128)(2,1)S(1)}, u32[]{:S(2)}, u32[]{:S(2)}) collective-permute-start(bf16[2,2,1,8,4,2560]{5,3,4,1,2,0:T(8,128)(2,1)S(1)} %maximum_select_fusion.2), channel_id=1, source_target_pairs={{0,1},{1,0},{2,3},{3,2},{4,5},{5,4},{6,7},{7,6},{8,9},{9,8},{10,11... | collective-permute-start | bytes 1966088 | tf_op jit(solution)/shard_map/ppermute | solution.py:231
  178.8 2.4 %copy-start.1 = (bf16[2560,512]{1,0:T(8,128)(2,1)S(1)}, bf16[2560,512]{1,0:T(8,128)(2,1)}, u32[]{:S(2)}) copy-start(bf16[2560,512]{1,0:T(8,128)(2,1)} %param.14) | copy-start | bytes 7864324

commit v11 on v10

--- a/solution.py
+++ b/solution.py
@@ -308,25 +308,21 @@
         return (rows.astype(jnp.float32) * scale * norm_gain).astype(jnp.bfloat16)
 
     first = side == 0
-    gathered = jnp.concatenate(
-        [
-            rms_norm(
-                jnp.where(first, own_states, other_states), jnp.where(first, squares, other_squares)
-            ),
-            rms_norm(
-                jnp.where(first, other_states, own_states), jnp.where(first, other_squares, squares)
-            ),
-        ],
-        0,
-    )
-    parts_out = [
-        jnp.dot(gathered, matrix, preferred_element_type=jnp.float32) for matrix in (wq, wk, wv)
-    ]
+
+    def project(rows):
+        return jnp.concatenate(
+            [jnp.dot(rows, matrix, preferred_element_type=jnp.float32) for matrix in (wq, wk, wv)],
+            axis=-1,
+        ).astype(jnp.bfloat16)
+
+    own_part = project(rms_norm(own_states, squares))
+    other_part = project(rms_norm(other_states, other_squares))
+    parts_out = jnp.where(
+        first, jnp.stack([own_part, other_part], 0), jnp.stack([other_part, own_part], 0)
+    )
     head_count = (q_width + 2 * k_width) // HEAD_SIZE
     output_projected = pair_scatter(
-        jnp.concatenate(parts_out, axis=-1)
-        .astype(jnp.bfloat16)
-        .reshape(lax.axis_size("row"), token_count, -1),
+        parts_out,
         "row",
         rounded=False,
     ).reshape(token_count, head_count, HEAD_SIZE)

time: 182 us -> 187 us (1.027)
  matrix products: 18.8 us -> 33.3 us
  waiting for transfers between devices: 77 us -> 72.6 us
  other arithmetic: 22.6 us -> 20.4 us
    ppermute x1, waiting for transfers between devices: 24.4 us -> 0.01 us  [on_device(): other_squares = lax.ppermute(squares, 'col', swap)]
    ppermute x1, waiting for transfers between devices: 0.01 us -> 19.1 us  [on_device(): other_states = lax.ppermute(own_states, 'col', swap)]
    dot_general x3 -> x6, matrix products: 8.8 us -> 23.3 us  [project(): jnp.dot(rows, matrix, preferred_element_type=jnp.float32)]
    ppermute x1, starting transfers between devices: 2.94 us -> 0.01 us  [on_device(): other_states = lax.ppermute(own_states, 'col', swap)]
    convert_element_type x1 -> x0, other arithmetic: 2.83 us -> none  [rms_norm(): return (rows.astype(jnp.float32) * scale * norm_gain).astype(jnp.bfloat16)]
    ppermute x1, starting transfers between devices: 0.01 us -> 2.82 us  [on_device(): other_squares = lax.ppermute(squares, 'col', swap)]
  transfers between devices with their start and end apart: 13 -> 13, of which waited for: 10 -> 10; matrix products, arithmetic and copies ran while one was open for 8% -> 15% of each run, Pallas kernels for 0% -> 0%
where the time goes in v11:
time: 187 us
  waiting for transfers between devices  72.6 us (39%)
  matrix products  33.3 us (18%)
  local copies, waits for them, and re-layouts  21.3 us (11%)
  other arithmetic  20.4 us (11%)
  Pallas kernels  17.3 us (9%)
  starting transfers between devices  16.2 us (9%)
  blocking collectives  4.58 us (2%)
    ppermute x3, waiting for transfers between devices, doubling_gather(): got = lax.ppermute(block, axis_name, pairs)  29.4 us
    dot_general x6, matrix products, project(): jnp.dot(rows, matrix, preferred_element_type=jnp.float32)  23.3 us
    ppermute x1, waiting for transfers between devices, on_device(): other_states = lax.ppermute(own_states, 'col', swap)  19.1 us
    pallas_call x1, Pallas kernels, slot_attention(): pl.pallas_call(partial(slot_kernel, ns=ns, heads=heads, qpk=qpk), grid_sp...  17.3 us
    ppermute x3, waiting for transfers between devices, seq_merge(): lax.ppermute(send_values.astype(jnp.bfloat16), 'seq', pairs)  15 us
    ppermute x2, waiting for transfers between devices, pair_scatter(): got = lax.ppermute(send, axis_name, [(0, 1), (1, 0)])  7.17 us
    ppermute x3, starting transfers between devices, seq_merge(): got_stats = lax.ppermute(send_stats, 'seq', pairs)  5.88 us
    dot_general x1, matrix products, on_device(): jnp.dot(piece_rows.reshape(n_row * per * step_count, -1), wo, preferred_e...  5.87 us
  transfers between devices with their start and end apart: 13, of which 10 were waited for; matrix products, arithmetic and copies ran while one was open for 15% of the time, Pallas kernels for 0%

profile of v11, /device:TPU:0, one launch (start us, length us, event | category | flops | bytes accessed | tf_op | source)
XLA Modules:
  0.0 186.9 jit_solution(13877875335088714494)
XLA Ops:
  0.7 2.2 %multiply_reduce_fusion = f32[64,4]{1,0:T(8,128)S(1)} fusion(bf16[64,4,2560]{2,1,0:T(4,128)(2,1)} %param.11), kind=kLoop, calls=%fused_computation.10 | loop fusion | flops 1965824 | bytes 1311744 | tf_op jit(solution)/shard_map/reduce_sum | solution.py:303
  3.0 2.6 %psum.7 = f32[256]{0:T(256)S(1)} all-reduce(f32[256]{0:T(256)S(1)} %reduce_sum.21), channel_id=1, replica_groups=mesh['row'=2,'col'=2,'seq'=8] {'row'}, use_global_device_ids=true, to_apply=%region_1.0 | all-reduce | flops 256 | bytes 2048 | tf_op jit(solution)/shard_map/psum | solution.py:303
  5.6 2.8 %collective-permute-start.1 = (f32[256]{0:T(256)S(1)}, f32[256]{0:T(256)S(1)}, u32[]{:S(2)}, u32[]{:S(2)}) collective-permute-start(f32[256]{0:T(256)S(1)} %psum.7), channel_id=1, source_target_pairs={{0,8},{8,0},{1,9},{9,1},{2,10},{10,2},{3,11},{11,3},{4,12},{12,4},... | collective-permute-start | bytes 3080 | tf_op jit(solution)/shard_map/ppermute | solution.py:304
  8.4 3.4 %reshape.929 = bf16[256,2560]{1,0:T(8,128)(2,1)} reshape(bf16[64,4,2560]{2,1,0:T(4,128)(2,1)} %param.11) | data formatting | bytes 2621440 | tf_op jit(solution)/shard_map/reshape | solution.py:298
  11.8 2.3 %fusion.12 = bf16[1,256,512]{2,1,0:T(8,128)(2,1)S(1)} fusion(bf16[2560,512]{1,0:T(8,128)(2,1)S(1)} %copy-done, bf16[256,2560]{1,0:T(8,128)(2,1)} %reshape.929, f32[2560]{0:T(1024)S(1)} %copy-done.13, f32[256]{0:T(256)S(1)} %add_rsqrt_fusion.1), kind=kOutput, calls=%fused_computation.31 | convolution fusion | flops 673841152 | bytes 4205568 | tf_op jit(solution)/shard_map/dot_general | solution.py:314
  14.3 0.9 fusion.13
  15.2 8.3 %fusion.5 = bf16[1,256,2048]{2,1,0:T(8,128)(2,1)} fusion(bf16[2560,2048]{1,0:T(8,128)(2,1)} %param.13, bf16[256,2560]{1,0:T(8,128)(2,1)} %reshape.929, f32[2560]{0:T(1024)S(1)} %copy-done.13, f32[256]{0:T(256)S(1)} %add_rsqrt_fusion.1), kind=kOutput, calls=%fused_computation.13 | convolution fusion | flops 2687500288 | bytes 12856320 | tf_op jit(solution)/shard_map/dot_general | solution.py:314
  23.5 19.1 %collective-permute-done = bf16[256,2560]{1,0:T(8,128)(2,1)} collective-permute-done((bf16[256,2560]{1,0:T(8,128)(2,1)}, bf16[256,2560]{1,0:T(8,128)(2,1)}, u32[]{:S(2)}, u32[]{:S(2)}) %collective-permute-start) | collective-permute-done | bytes 1310752 | tf_op jit(solution)/shard_map/ppermute | solution.py:301
  42.7 2.2 %fusion.14 = bf16[1,256,512]{2,1,0:T(8,128)(2,1)S(1)} fusion(bf16[2560,512]{1,0:T(8,128)(2,1)S(1)} %copy-done, bf16[256,2560]{1,0:T(8,128)(2,1)} %collective-permute-done, f32[256]{0:T(256)S(1)} %add_rsqrt_fusion, f32[2560]{0:T(1024)S(1)} %copy-done.13), kind=kOutput, calls=%fused_computation.33 | convolution fusion | flops 673841152 | bytes 4205568 | tf_op jit(solution)/shard_map/dot_general | solution.py:314
  44.9 2.2 %fusion.15 = bf16[1,256,512]{2,1,0:T(8,128)(2,1)S(1)} fusion(bf16[2560,512]{1,0:T(8,128)(2,1)S(1)} %copy-done.12, bf16[256,2560]{1,0:T(8,128)(2,1)} %collective-permute-done, f32[256]{0:T(256)S(1)} %add_rsqrt_fusion, f32[2560]{0:T(1024)S(1)} %copy-done.13), kind=kOutput, calls=%fused_computation.34 | convolution fusion | flops 673841152 | bytes 4205568 | tf_op jit(solution)/shard_map/dot_general | solution.py:314
  47.1 7.4 %fusion.6 = bf16[1,256,2048]{2,1,0:T(8,128)(2,1)S(1)} fusion(bf16[2560,2048]{1,0:T(8,128)(2,1)} %param.13, bf16[256,2560]{1,0:T(8,128)(2,1)} %collective-permute-done, f32[256]{0:T(256)S(1)} %add_rsqrt_fusion, f32[2560]{0:T(1024)S(1)} %copy-done.13), kind=kOutput, calls=%fused_computation.14 | convolution fusion | flops 2687500288 | bytes 12856320 | tf_op jit(solution)/shard_map/dot_general | solution.py:314
  54.5 0.8 maximum_select_fusion
  55.4 1.6 copy-done.3
  57.0 1.3 constant_dynamic-slice_fusion.2
  58.3 0.8 gather_fusion
  59.3 0.5 compare_select_fusion.1.len_ref
  59.9 0.5 multiply_cosine_fusion
  60.4 1.5 collective-permute-done.2
  61.9 1.9 %add_bitcast_fusion = f32[32,8,24,128]{3,1,2,0:T(8,128)S(1)} fusion(bf16[1,256,3072]{2,1,0:T(8,128)(2,1)S(1)} %collective-permute-done.2, bf16[2,256,3072]{2,1,0:T(8,128)(2,1)} %copy-done.3, s32[]{:T(128)S(6)} %select_n.171), kind=kLoop, calls=%fused_computation.7 | loop fusion | flops 2359296 | bytes 6291460
  63.8 0.6 copy.198
  64.5 0.4 add_convert_fusion.1
  65.0 0.8 subtract_convert_fusion
  65.7 1.4 pad_maximum_fusion
  67.2 0.5 copy.182
  67.9 1.3 fusion.19
  69.1 0.5 copy.161
  69.8 0.8 fusion.21
  70.6 1.6 gather_fusion.1
  72.2 17.3 %shard_map.130 = (f32[50,64,1]{2,1,0:T(8,128)}, f32[50,64,1]{2,1,0:T(8,128)}, f32[50,64,128]{2,1,0:T(8,128)}) custom-call(s32[50]{0:T(128)} %compare_select_fusion.1.len_ref, s32[50]{0:T(128)} %blk_ref.1, bf16[50,64,128]{2,1,0:T(8,128)(2,1)} %gather_fusion.1, bf16[50,128,512]{2,1,0:T(8,128)(2,1)} %k_ref.1, bf16[50,128,512]{2,1,0:T(8,128)(2,1)} %v_ref.1), custom_call_target="tpu_custom_call" | custom-call | tf_op jit(solution)/shard_map/pallas_call | solution.py:189
  89.5 2.0 %reduce.1 = f32[50,64]{1,0:T(8,128)S(1)} reduce(f32[50,64,1]{2,1,0:T(8,128)} %get-tuple-element.7, f32[]{:T(128)} %constant.111), dimensions={2}, to_apply=%get-tuple-element.7.reduce_sub_computation | reduce | bytes 25604 | tf_op jit(solution)/shard_map/pallas_call | solution.py:189
  91.5 0.9 select_reduce_fusion
  92.5 0.6 gather_fusion.2
  93.1 1.8 copy.139
  94.9 3.0 %multiply_reduce_fusion.1 = (f32[50,64]{1,0:T(8,128)S(1)}, f32[50,64]{1,0:T(8,128)S(1)}) fusion(f32[50,64,1]{2,1,0:T(8,128)} %get-tuple-element.8, f32[50,64,1]{2,1,0:T(8,128)S(1)} %copy-done.4, f32[50,64,1]{2,1,0:T(8,128)} %copy.139), kind=kLoop, calls=%fused_computation.19 | loop fusion | flops 6400 | bytes 64000 | tf_op jit(solution)/shard_map/mul | solution.py:365
  98.1 1.6 collective-permute-start.3
  99.7 0.5 broadcast_multiply_fusion
  100.2 2.2 %fusion.7 = f32[64,64,128]{2,0,1:T(8,128)S(1)} fusion(f32[50,64,128]{2,1,0:T(8,128)S(1)} %broadcast_multiply_fusion, s32[50]{0:T(128)S(1)} %copy-done.10), kind=kOutput, calls=%fused_computation.17 | convolution fusion | flops 314576000 | bytes 3735752 | tf_op jit(solution)/shard_map/rn,njh->rjh/dot_general | solution.py:367
  102.4 1.3 copy-done.5
  103.8 0.6 constant_dynamic-slice_fusion
  104.5 0.5 copy.168
  104.9 0.6 collective-permute-start.4
  105.6 1.6 collective-permute-start.5
  107.5 1.9 collective-permute-done.5
  109.4 2.7 %collective-permute-start.7 = (f32[2,1,1,1,8,64]{5,4,3,2,1,0:T(8,128)S(1)}, f32[2,1,1,1,8,64]{5,4,3,2,1,0:T(8,128)S(1)}, u32[]{:S(2)}, u32[]{:S(2)}) collective-permute-start(f32[2,1,1,1,8,64]{5,4,3,2,1,0:T(8,128)S(1)} %get-tuple-element.51), channel_id=1, source_target_pairs={{0,4},{1,5},{2,6},{3,7},{4,0},{5,1},{6,2},{7,3},{8,12},{9,13},{10,... | collective-permute-start | bytes 12296 | tf_op jit(solution)/shard_map/ppermute | solution.py:258
  112.3 6.4 %collective-permute-done.4 = bf16[2,2,1,8,64,128]{5,3,2,1,0,4:T(8,128)(2,1)S(1)} collective-permute-done((bf16[2,2,1,8,64,128]{5,3,2,1,0,4:T(8,128)(2,1)S(1)}, bf16[2,2,1,8,64,128]{5,3,2,1,0,4:T(8,128)(2,1)S(1)}, u32[]{:S(2)}, u32[]{:S(2)}) %collective-permute-start.4) | collective-permute-done | bytes 524320 | tf_op jit(solution)/shard_map/ppermute | solution.py:259
  118.7 1.8 multiply_add_fusion
  120.6 1.6 collective-permute-start.6
  122.5 5.3 %collective-permute-done.6 = bf16[2,1,1,8,64,128]{5,3,2,1,0,4:T(8,128)(2,1)S(1)} collective-permute-done((bf16[2,1,1,8,64,128]{5,3,2,1,0,4:T(8,128)(2,1)S(1)}, bf16[2,1,1,8,64,128]{5,3,2,1,0,4:T(8,128)(2,1)S(1)}, u32[]{:S(2)}, u32[]{:S(2)}) %collective-permute-start.6) | collective-permute-done | bytes 262176 | tf_op jit(solution)/shard_map/ppermute | solution.py:259
  128.3 2.7 %collective-permute-start.8 = (bf16[1,1,1,8,64,128]{5,3,2,1,0,4:T(8,128)(2,1)S(1)}, bf16[1,1,1,8,64,128]{5,3,2,1,0,4:T(8,128)(2,1)S(1)}, u32[]{:S(2)}, u32[]{:S(2)}) collective-permute-start(bf16[1,1,1,8,64,128]{5,3,2,1,0,4:T(8,128)(2,1)S(1)} %dynamic-slice_convert_fusion.2), channel_id=1, source_target_pairs={{0,4},{1,5},{2,6},{3,7},{4,0},{5,1},{6,2},{7,3},{8,12},{9,13},{10,... | collective-permute-start | bytes 393224 | tf_op jit(solution)/shard_map/ppermute | solution.py:259
  130.9 0.8 multiply_add_fusion.3
  132.3 3.3 %collective-permute-done.8 = bf16[1,1,1,8,64,128]{5,3,2,1,0,4:T(8,128)(2,1)S(1)} collective-permute-done((bf16[1,1,1,8,64,128]{5,3,2,1,0,4:T(8,128)(2,1)S(1)}, bf16[1,1,1,8,64,128]{5,3,2,1,0,4:T(8,128)(2,1)S(1)}, u32[]{:S(2)}, u32[]{:S(2)}) %collective-permute-start.8) | collective-permute-done | bytes 131104 | tf_op jit(solution)/shard_map/ppermute | solution.py:259
  135.9 0.5 fusion.17
  136.5 2.0 %all_gather.4 = bf16[2,8,4,2048]{3,1,2,0:T(8,128)(2,1)S(1)} all-gather(bf16[1,8,4,2048]{3,1,2,0:T(8,128)(2,1)S(1)} %convert_element_type.130), channel_id=1, replica_groups=mesh['row'=2,'col'=2,'seq'=8] {'row'}, dimensions={0}, use_global_device_ids=true | all-gather | bytes 393216 | tf_op jit(solution)/shard_map/all_gather | solution.py:396
  138.5 5.9 %fusion.2 = bf16[2,8,4,2560]{3,1,2,0:T(8,128)(2,1)S(1)} fusion(bf16[2,8,4,2048]{3,1,2,0:T(8,128)(2,1)S(1)} %all_gather.4, bf16[2048,2560]{1,0:T(8,128)(2,1)} %param.16), kind=kOutput, calls=%fused_computation.5 | convolution fusion | flops 671252480 | bytes 11075584 | tf_op jit(solution)/shard_map/dot_general | solution.py:398
  144.4 0.6 collective-permute-start.9
  145.0 5.7 %collective-permute-done.9 = bf16[1,8,4,2560]{3,1,2,0:T(8,128)(2,1)S(1)} collective-permute-done((bf16[1,8,4,2560]{3,1,2,0:T(8,128)(2,1)S(1)}, bf16[1,8,4,2560]{3,1,2,0:T(8,128)(2,1)S(1)}, u32[]{:S(2)}, u32[]{:S(2)}) %collective-permute-start.9) | collective-permute-done | bytes 163872 | tf_op jit(solution)/shard_map/ppermute | solution.py:218
  150.8 1.4 collective-permute-start.10
  152.1 8.5 %collective-permute-done.10 = bf16[1,8,4,2560]{3,1,2,0:T(8,128)(2,1)S(1)} collective-permute-done((bf16[1,8,4,2560]{3,1,2,0:T(8,128)(2,1)S(1)}, bf16[1,8,4,2560]{3,1,2,0:T(8,128)(2,1)S(1)}, u32[]{:S(2)}, u32[]{:S(2)}) %collective-permute-start.10) | collective-permute-done | bytes 163872 | tf_op jit(solution)/shard_map/ppermute | solution.py:231
  160.8 8.6 %collective-permute-done.11 = bf16[2,1,8,4,2560]{4,2,3,1,0:T(8,128)(2,1)S(1)} collective-permute-done((bf16[2,1,8,4,2560]{4,2,3,1,0:T(8,128)(2,1)S(1)}, bf16[2,1,8,4,2560]{4,2,3,1,0:T(8,128)(2,1)S(1)}, u32[]{:S(2)}, u32[]{:S(2)}) %collective-permute-start.11) | collective-permute-done | bytes 327712 | tf_op jit(solution)/shard_map/ppermute | solution.py:231
  169.6 0.6 collective-permute-start.12
  170.2 0.8 reshape_reshape.8
  171.3 0.8 convert_element_type.135
  172.2 12.2 %collective-permute-done.12 = bf16[2,2,1,8,4,2560]{5,3,4,1,2,0:T(8,128)(2,1)S(1)} collective-permute-done((bf16[2,2,1,8,4,2560]{5,3,4,1,2,0:T(8,128)(2,1)S(1)}, bf16[2,2,1,8,4,2560]{5,3,4,1,2,0:T(8,128)(2,1)S(1)}, u32[]{:S(2)}, u32[]{:S(2)}) %collective-permute-start.12) | collective-permute-done | bytes 655392 | tf_op jit(solution)/shard_map/ppermute | solution.py:231
  184.8 2.1 %copy.177 = bf16[64,4,2560]{2,1,0:T(4,128)(2,1)} copy(bf16[64,4,2560]{2,0,1:T(8,128)(2,1)S(1)} %bitcast.159) | data formatting | bytes 2621440
  (85 shorter events, 4.9 us)
Async XLA Ops:
  0.6 11.2 %copy-start = (bf16[2560,512]{1,0:T(8,128)(2,1)S(1)}, bf16[2560,512]{1,0:T(8,128)(2,1)}, u32[]{:S(2)}) copy-start(bf16[2560,512]{1,0:T(8,128)(2,1)} %param.14) | copy-start | bytes 7864324
  0.6 11.1 %copy-start.13 = (f32[2560]{0:T(1024)S(1)}, f32[2560]{0:T(1024)}, u32[]{:S(2)}) copy-start(f32[2560]{0:T(1024)} %param.12) | copy-start | bytes 30724
  5.6 17.9 %collective-permute-start.1 = (f32[256]{0:T(256)S(1)}, f32[256]{0:T(256)S(1)}, u32[]{:S(2)}, u32[]{:S(2)}) collective-permute-start(f32[256]{0:T(256)S(1)} %psum.7), channel_id=1, source_target_pairs={{0,8},{8,0},{1,9},{9,1},{2,10},{10,2},{3,11},{11,3},{4,12},{12,4},... | collective-permute-start | bytes 3080 | tf_op jit(solution)/shard_map/ppermute | solution.py:304
  11.8 30.9 %collective-permute-start = (bf16[256,2560]{1,0:T(8,128)(2,1)}, bf16[256,2560]{1,0:T(8,128)(2,1)}, u32[]{:S(2)}, u32[]{:S(2)}) collective-permute-start(bf16[256,2560]{1,0:T(8,128)(2,1)} %reshape.929), channel_id=1, source_target_pairs={{0,8},{8,0},{1,9},{9,1},{2,10},{10,2},{3,11},{11,3},{4,12},{12,4},... | collective-permute-start | bytes 3932168 | tf_op jit(solution)/shard_map/ppermute | solution.py:301
  11.8 2.4 %copy-start.7 = (bf16[256,2560]{1,0:T(8,128)(2,1)S(1)}, bf16[256,2560]{1,0:T(8,128)(2,1)}, u32[]{:S(2)}) copy-start(bf16[256,2560]{1,0:T(8,128)(2,1)} %reshape.929) | copy-start | bytes 3932164
  11.8 2.5 %copy-start.11 = (bf16[2560,512]{1,0:T(8,128)(2,1)S(1)}, bf16[2560,512]{1,0:T(8,128)(2,1)}, u32[]{:S(2)}) copy-start(bf16[2560,512]{1,0:T(8,128)(2,1)} %param.15) | copy-start | bytes 7864324
  23.5 21.3 %copy-start.12 = (bf16[2560,512]{1,0:T(8,128)(2,1)S(1)}, bf16[2560,512]{1,0:T(8,128)(2,1)}, u32[]{:S(2)}) copy-start(bf16[2560,512]{1,0:T(8,128)(2,1)} %param.15) | copy-start | bytes 7864324
  47.1 7.4 %copy-start.8 = (bf16[1,256,2048]{2,1,0:T(8,128)(2,1)S(1)}, bf16[1,256,2048]{2,1,0:T(8,128)(2,1)}, u32[]{:S(2)}) copy-start(bf16[1,256,2048]{2,1,0:T(8,128)(2,1)} %fusion.5) | copy-start | bytes 3145732
  55.4 1.7 copy-start.3
  57.0 1.3 copy-start.10
  57.0 1.3 copy-start.2
  58.3 3.6 %collective-permute-start.2 = (bf16[1,256,3072]{2,1,0:T(8,128)(2,1)}, bf16[1,256,3072]{2,1,0:T(8,128)(2,1)S(1)}, u32[]{:S(2)}, u32[]{:S(2)}) collective-permute-start(bf16[1,256,3072]{2,1,0:T(8,128)(2,1)} %constant_dynamic-slice_fusion.2), channel_id=1, source_target_pairs={{0,16},{16,0},{1,17},{17,1},{2,18},{18,2},{3,19},{19,3},{4,20},{20... | collective-permute-start | bytes 4718600 | tf_op jit(solution)/shard_map/ppermute | solution.py:218
  89.5 5.4 %copy-start.4 = (f32[50,64,1]{2,1,0:T(8,128)S(1)}, f32[50,64,1]{2,1,0:T(8,128)}, u32[]{:S(2)}) copy-start(f32[50,64,1]{2,1,0:T(8,128)} %get-tuple-element.7) | copy-start | bytes 38404
  94.9 4.8 %copy-start.6 = (f32[50,64,128]{2,1,0:T(8,128)S(1)}, f32[50,64,128]{2,1,0:T(8,128)}, u32[]{:S(2)}) copy-start(f32[50,64,128]{2,1,0:T(8,128)} %get-tuple-element.6) | copy-start | bytes 4915204
  98.1 7.5 %collective-permute-start.3 = (f32[2,2,2,1,8,64]{5,4,3,2,1,0:T(8,128)S(1)}, f32[2,2,2,1,8,64]{5,4,3,2,1,0:T(8,128)S(1)}, u32[]{:S(2)}, u32[]{:S(2)}) collective-permute-start(f32[2,2,2,1,8,64]{5,4,3,2,1,0:T(8,128)S(1)} %get-tuple-element.43), channel_id=1, source_target_pairs={{0,1},{1,0},{2,3},{3,2},{4,5},{5,4},{6,7},{7,6},{8,9},{9,8},{10,11... | collective-permute-start | bytes 49160 | tf_op jit(solution)/shard_map/ppermute | solution.py:258
  102.3 1.3 copy-start.5
  104.9 13.8 %collective-permute-start.4 = (bf16[2,2,1,8,64,128]{5,3,2,1,0,4:T(8,128)(2,1)S(1)}, bf16[2,2,1,8,64,128]{5,3,2,1,0,4:T(8,128)(2,1)S(1)}, u32[]{:S(2)}, u32[]{:S(2)}) collective-permute-start(bf16[2,2,1,8,64,128]{5,3,2,1,0,4:T(8,128)(2,1)S(1)} %dynamic-slice_convert_fusion), channel_id=1, source_target_pairs={{0,1},{1,0},{2,3},{3,2},{4,5},{5,4},{6,7},{7,6},{8,9},{9,8},{10,11... | collective-permute-start | bytes 1572872 | tf_op jit(solution)/shard_map/ppermute | solution.py:259
  105.6 3.8 %collective-permute-start.5 = (f32[2,2,1,1,8,64]{5,4,3,2,1,0:T(8,128)S(1)}, f32[2,2,1,1,8,64]{5,4,3,2,1,0:T(8,128)S(1)}, u32[]{:S(2)}, u32[]{:S(2)}) collective-permute-start(f32[2,2,1,1,8,64]{5,4,3,2,1,0:T(8,128)S(1)} %get-tuple-element.47), channel_id=1, source_target_pairs={{0,2},{1,3},{2,0},{3,1},{4,6},{5,7},{6,4},{7,5},{8,10},{9,11},{10,... | collective-permute-start | bytes 24584 | tf_op jit(solution)/shard_map/ppermute | solution.py:258
  109.4 12.9 %collective-permute-start.7 = (f32[2,1,1,1,8,64]{5,4,3,2,1,0:T(8,128)S(1)}, f32[2,1,1,1,8,64]{5,4,3,2,1,0:T(8,128)S(1)}, u32[]{:S(2)}, u32[]{:S(2)}) collective-permute-start(f32[2,1,1,1,8,64]{5,4,3,2,1,0:T(8,128)S(1)} %get-tuple-element.51), channel_id=1, source_target_pairs={{0,4},{1,5},{2,6},{3,7},{4,0},{5,1},{6,2},{7,3},{8,12},{9,13},{10,... | collective-permute-start | bytes 12296 | tf_op jit(solution)/shard_map/ppermute | solution.py:258
  120.5 15.3 %copy-start.9 = (bf16[8,4,4,128]{3,2,1,0:T(4,128)(2,1)S(1)}, bf16[8,4,4,128]{3,2,1,0:T(4,128)(2,1)}, u32[]{:S(2)}) copy-start(bf16[8,4,4,128]{3,2,1,0:T(4,128)(2,1)} %constant_dynamic-slice_fusion) | copy-start | bytes 98308
  120.6 7.3 %collective-permute-start.6 = (bf16[2,1,1,8,64,128]{5,3,2,1,0,4:T(8,128)(2,1)S(1)}, bf16[2,1,1,8,64,128]{5,3,2,1,0,4:T(8,128)(2,1)S(1)}, u32[]{:S(2)}, u32[]{:S(2)}) collective-permute-start(bf16[2,1,1,8,64,128]{5,3,2,1,0,4:T(8,128)(2,1)S(1)} %dynamic-slice_convert_fusion.1), channel_id=1, source_target_pairs={{0,2},{1,3},{2,0},{3,1},{4,6},{5,7},{6,4},{7,5},{8,10},{9,11},{10,... | collective-permute-start | bytes 786440 | tf_op jit(solution)/shard_map/ppermute | solution.py:259
  128.3 7.3 %collective-permute-start.8 = (bf16[1,1,1,8,64,128]{5,3,2,1,0,4:T(8,128)(2,1)S(1)}, bf16[1,1,1,8,64,128]{5,3,2,1,0,4:T(8,128)(2,1)S(1)}, u32[]{:S(2)}, u32[]{:S(2)}) collective-permute-start(bf16[1,1,1,8,64,128]{5,3,2,1,0,4:T(8,128)(2,1)S(1)} %dynamic-slice_convert_fusion.2), channel_id=1, source_target_pairs={{0,4},{1,5},{2,6},{3,7},{4,0},{5,1},{6,2},{7,3},{8,12},{9,13},{10,... | collective-permute-start | bytes 393224 | tf_op jit(solution)/shard_map/ppermute | solution.py:259
  144.4 6.3 %collective-permute-start.9 = (bf16[1,8,4,2560]{3,1,2,0:T(8,128)(2,1)S(1)}, bf16[1,8,4,2560]{3,1,2,0:T(8,128)(2,1)S(1)}, u32[]{:S(2)}, u32[]{:S(2)}) collective-permute-start(bf16[1,8,4,2560]{3,1,2,0:T(8,128)(2,1)S(1)} %constant_dynamic-slice_fusion.1), channel_id=1, source_target_pairs={{0,8},{8,0},{1,9},{9,1},{2,10},{10,2},{3,11},{11,3},{4,12},{12,4},... | collective-permute-start | bytes 491528 | tf_op jit(solution)/shard_map/ppermute | solution.py:218
  150.8 9.9 %collective-permute-start.10 = (bf16[1,8,4,2560]{3,1,2,0:T(8,128)(2,1)S(1)}, bf16[1,8,4,2560]{3,1,2,0:T(8,128)(2,1)S(1)}, u32[]{:S(2)}, u32[]{:S(2)}) collective-permute-start(bf16[1,8,4,2560]{3,1,2,0:T(8,128)(2,1)S(1)} %add_convert_fusion.2), channel_id=1, source_target_pairs={{0,4},{1,5},{2,6},{3,7},{4,0},{5,1},{6,2},{7,3},{8,12},{9,13},{10,... | collective-permute-start | bytes 491528 | tf_op jit(solution)/shard_map/ppermute | solution.py:231
  160.7 8.8 %collective-permute-start.11 = (bf16[2,1,8,4,2560]{4,2,3,1,0:T(8,128)(2,1)S(1)}, bf16[2,1,8,4,2560]{4,2,3,1,0:T(8,128)(2,1)S(1)}, u32[]{:S(2)}, u32[]{:S(2)}) collective-permute-start(bf16[2,1,8,4,2560]{4,2,3,1,0:T(8,128)(2,1)S(1)} %maximum_select_fusion.5), channel_id=1, source_target_pairs={{0,2},{1,3},{2,0},{3,1},{4,6},{5,7},{6,4},{7,5},{8,10},{9,11},{10,... | collective-permute-start | bytes 983048 | tf_op jit(solution)/shard_map/ppermute | solution.py:231
  169.6 14.9 %collective-permute-start.12 = (bf16[2,2,1,8,4,2560]{5,3,4,1,2,0:T(8,128)(2,1)S(1)}, bf16[2,2,1,8,4,2560]{5,3,4,1,2,0:T(8,128)(2,1)S(1)}, u32[]{:S(2)}, u32[]{:S(2)}) collective-permute-start(bf16[2,2,1,8,4,2560]{5,3,4,1,2,0:T(8,128)(2,1)S(1)} %maximum_select_fusion.3), channel_id=1, source_target_pairs={{0,1},{1,0},{2,3},{3,2},{4,5},{5,4},{6,7},{7,6},{8,9},{9,8},{10,11... | collective-permute-start | bytes 1966088 | tf_op jit(solution)/shard_map/ppermute | solution.py:231
  184.4 2.4 %copy-start.1 = (bf16[2560,512]{1,0:T(8,128)(2,1)S(1)}, bf16[2560,512]{1,0:T(8,128)(2,1)}, u32[]{:S(2)}) copy-start(bf16[2560,512]{1,0:T(8,128)(2,1)} %param.14) | copy-start | bytes 7864324

commit v12 on v10

--- a/solution.py
+++ b/solution.py
@@ -115,8 +115,17 @@
     return (running_peak, running_totals, weighted_values)
 
 
-def slot_kernel(len_ref, blk_ref, q_ref, k_ref, v_ref, peak_ref, tot_ref, acc_ref, *, ns, heads, qpk):
+def slot_kernel(
+    req_ref, len_ref, blk_ref, q_ref, k_ref, v_ref, peak_ref, tot_ref, acc_ref, *, ns, heads, qpk
+):
+    @pl.when(pl.program_id(0) == 0)
+    def _():
+        peak_ref[...] = jnp.full(peak_ref.shape, NEGATIVE_FILL, jnp.float32)
+        tot_ref[...] = jnp.zeros(tot_ref.shape, jnp.float32)
+        acc_ref[...] = jnp.zeros(acc_ref.shape, jnp.float32)
+
     base = pl.program_id(0) * ns
+    req_count = q_ref.shape[0]
     rows = q_ref.shape[1]
     group = rows // heads
     width = k_ref.shape[1]
@@ -126,76 +135,87 @@
     step_of = (row % group) // qpk
 
     def body(i, carry):
-        length = len_ref[base + i]
-        key_pos = blk_ref[base + i] * width + col
-        query_pos = length + step_of
-        visible = (key_pos < length) & ((key_pos < SINK) | (key_pos > query_pos - WINDOW))
-        q = q_ref[i]
-        k = k_ref[i]
-        v = v_ref[i]
-        scores = jnp.concatenate(
-            [
-                lax.dot_general(
-                    q[a * group : (a + 1) * group],
-                    k[:, a * head : (a + 1) * head],
-                    (((1,), (1,)), ((), ())),
-                    preferred_element_type=jnp.float32,
-                )
-                for a in range(heads)
-            ],
-            0,
-        ) * (1.0 / math.sqrt(HEAD_SIZE))
-        peak = jnp.max(jnp.where(visible, scores, NEGATIVE_FILL), axis=1, keepdims=True)
-        weights = jnp.where(visible, jnp.exp(scores - peak), 0.0)
-        total = jnp.sum(weights, axis=1, keepdims=True)
-        rounded = weights.astype(jnp.bfloat16)
-        acc = jnp.concatenate(
-            [
-                jnp.dot(
-                    rounded[a * group : (a + 1) * group],
-                    v[:, a * head : (a + 1) * head],
-                    preferred_element_type=jnp.float32,
-                )
-                for a in range(heads)
-            ],
-            0,
-        )
-        peak_ref[i] = peak
-        tot_ref[i] = total
-        acc_ref[i] = acc
+        req = req_ref[base + i]
+
+        @pl.when(req < req_count)
+        def _():
+            owner = jnp.minimum(req, req_count - 1)
+            length = len_ref[owner]
+            key_pos = blk_ref[base + i] * width + col
+            query_pos = length + step_of
+            visible = (key_pos < length) & ((key_pos < SINK) | (key_pos > query_pos - WINDOW))
+            q = q_ref[owner]
+            k = k_ref[i]
+            v = v_ref[i]
+            scores = jnp.concatenate(
+                [
+                    lax.dot_general(
+                        q[a * group : (a + 1) * group],
+                        k[:, a * head : (a + 1) * head],
+                        (((1,), (1,)), ((), ())),
+                        preferred_element_type=jnp.float32,
+                    )
+                    for a in range(heads)
+                ],
+                0,
+            ) * (1.0 / math.sqrt(HEAD_SIZE))
+            peak = jnp.max(jnp.where(visible, scores, NEGATIVE_FILL), axis=1, keepdims=True)
+            weights = jnp.where(visible, jnp.exp(scores - peak), 0.0)
+            total = jnp.sum(weights, axis=1, keepdims=True)
+            rounded = weights.astype(jnp.bfloat16)
+            acc = jnp.concatenate(
+                [
+                    jnp.dot(
+                        rounded[a * group : (a + 1) * group],
+                        v[:, a * head : (a + 1) * head],
+                        preferred_element_type=jnp.float32,
+                    )
+                    for a in range(heads)
+                ],
+                0,
+            )
+            old = peak_ref[owner]
+            top = jnp.maximum(old, peak)
+            old_factor = jnp.exp(old - top)
+            new_factor = jnp.exp(peak - top)
+            tot_ref[owner] = tot_ref[owner] * old_factor + total * new_factor
+            acc_ref[owner] = acc_ref[owner] * old_factor + acc * new_factor
+            peak_ref[owner] = top
+
         return carry
 
     lax.fori_loop(0, ns, body, 0, unroll=True)
 
 
-def slot_attention(slot_queries, slot_lengths, block_numbers, keys, values, heads, qpk):
-    n_slots, rows, head = slot_queries.shape
+def slot_attention(queries, lengths, slot_request, block_numbers, keys, values, heads, qpk):
+    req_count, rows, head = queries.shape
+    n_slots = keys.shape[0]
     width = keys.shape[1]
     ns = max(d for d in range(1, 11) if n_slots % d == 0)
+    fixed = lambda n, sr, lr, br: (0, 0, 0)
     grid_spec = pltpu.PrefetchScalarGridSpec(
-        num_scalar_prefetch=2,
+        num_scalar_prefetch=3,
         grid=(n_slots // ns,),
         in_specs=[
-            pl.BlockSpec((ns, rows, head), lambda n, lr, br: (n, 0, 0)),
-            pl.BlockSpec((ns, width, keys.shape[2]), lambda n, lr, br: (n, 0, 0)),
-            pl.BlockSpec((ns, width, values.shape[2]), lambda n, lr, br: (n, 0, 0)),
+            pl.BlockSpec((req_count, rows, head), fixed),
+            pl.BlockSpec((ns, width, keys.shape[2]), lambda n, sr, lr, br: (n, 0, 0)),
+            pl.BlockSpec((ns, width, values.shape[2]), lambda n, sr, lr, br: (n, 0, 0)),
         ],
         out_specs=[
-            pl.BlockSpec((ns, rows, 1), lambda n, lr, br: (n, 0, 0)),
-            pl.BlockSpec((ns, rows, 1), lambda n, lr, br: (n, 0, 0)),
-            pl.BlockSpec((ns, rows, head), lambda n, lr, br: (n, 0, 0)),
+            pl.BlockSpec((req_count, rows, 1), fixed),
+            pl.BlockSpec((req_count, rows, 1), fixed),
+            pl.BlockSpec((req_count, rows, head), fixed),
         ],
     )
     return pl.pallas_call(
         partial(slot_kernel, ns=ns, heads=heads, qpk=qpk),
         grid_spec=grid_spec,
         out_shape=[
-            jax.ShapeDtypeStruct((n_slots, rows, 1), jnp.float32),
-            jax.ShapeDtypeStruct((n_slots, rows, 1), jnp.float32),
-            jax.ShapeDtypeStruct((n_slots, rows, head), jnp.float32),
+            jax.ShapeDtypeStruct((req_count, rows, 1), jnp.float32),
+            jax.ShapeDtypeStruct((req_count, rows, 1), jnp.float32),
+            jax.ShapeDtypeStruct((req_count, rows, head), jnp.float32),
         ],
-    )(slot_lengths, block_numbers, slot_queries, keys, values)
-
+    )(slot_request, lengths, block_numbers, queries, keys, values)
 
 def pair_gather(part, axis_name):
     n = lax.axis_size(axis_name)
@@ -346,31 +366,18 @@
         .astype(jnp.bfloat16)
         .reshape(req_count, step_count, heads_kv, HEAD_SIZE)
     )
-    picked = jnp.minimum(slot_request, req_count - 1)
-    in_use = slot_request < req_count
-    slot_lengths = jnp.where(in_use, lengths[picked], 0)
-    flat_queries = query_rows.transpose(0, 2, 1, 3, 4).reshape(req_count, -1, HEAD_SIZE)
-    slot_peak, slot_total, slot_acc = slot_attention(
-        flat_queries[picked],
-        slot_lengths,
+    local_peak, local_totals, local_values = slot_attention(
+        query_rows.transpose(0, 2, 1, 3, 4).reshape(req_count, -1, HEAD_SIZE),
+        lengths,
+        slot_request,
         slot_block_number,
         paged_key_cache,
         paged_value_cache,
         heads_kv,
         QUERY_PER_KEY,
     )
-    slot_peak = slot_peak[..., 0]
-    slot_total = slot_total[..., 0]
-    member = slot_request[None, :] == jnp.arange(req_count, dtype=jnp.int32)[:, None]
-    local_peak = jnp.max(jnp.where(member[:, :, None], slot_peak[None], NEGATIVE_FILL), 1)
-    factor = jnp.exp(slot_peak - local_peak[picked])
-    as_member = member.astype(jnp.float32)
-    local_totals = jnp.einsum(
-        "rn,nj->rj", as_member, slot_total * factor, precision=lax.Precision.HIGHEST
-    )
-    local_values = jnp.einsum(
-        "rn,njh->rjh", as_member, slot_acc * factor[..., None], precision=lax.Precision.HIGHEST
-    )
+    local_peak = local_peak[..., 0]
+    local_totals = local_totals[..., 0]
     n_seq = lax.axis_size("seq")
     per = req_count // n_seq
     seq_index = lax.axis_index("seq")

time: 182 us -> 179 us (0.984)
  waiting for transfers between devices: 77 us -> 85.6 us
  local copies, waits for them, and re-layouts: 22.4 us -> 16.2 us
  other arithmetic: 22.6 us -> 17.5 us
  Pallas kernels: 17.2 us -> 21 us
  matrix products: 18.8 us -> 16.2 us
    gather x4 -> x0, local copies, waits for them, and re-layouts: 4.72 us -> none  [the longest x2 2.38 us: on_device(): factor = jnp.exp(slot_peak - local_peak[picked])]
    pallas_call x1, Pallas kernels: 17.2 us -> 21 us  [slot_attention(): pl.pallas_call(partial(slot_kernel, ns=ns, heads=heads, qpk=qpk), grid_sp...]
    mul x2 -> x0, other arithmetic: 3.47 us -> none  [the longest x1 2.97 us: on_device(): slot_total * factor]
    ppermute x3, waiting for transfers between devices: 1.61 us -> 4.56 us  [seq_merge(): got_stats = lax.ppermute(send_stats, 'seq', pairs)]
    dot_general x2 -> x0, matrix products: 2.38 us -> none  [the longest x1 2.18 us: on_device(): jnp.einsum('rn,njh->rjh', as_member, slot_acc * factor[..., None], precis...]
    ppermute x3, waiting for transfers between devices: 15 us -> 17.2 us  [seq_merge(): lax.ppermute(send_values.astype(jnp.bfloat16), 'seq', pairs)]
    ppermute x3, waiting for transfers between devices: 29.7 us -> 31.8 us  [doubling_gather(): got = lax.ppermute(block, axis_name, pairs)]
    unnamed x30 -> x24, local copies, waits for them, and re-layouts: 6.82 us -> 5.49 us
  transfers between devices with their start and end apart: 13 -> 13, of which waited for: 10 -> 11; matrix products, arithmetic and copies ran while one was open for 8% -> 4% of each run, Pallas kernels for 0% -> 0%
where the time goes in v12:
time: 179 us
  waiting for transfers between devices  85.6 us (48%)
  Pallas kernels  21 us (12%)
  other arithmetic  17.5 us (10%)
  starting transfers between devices  16.8 us (9%)
  local copies, waits for them, and re-layouts  16.2 us (9%)
  matrix products  16.2 us (9%)
  blocking collectives  4.46 us (2%)
    ppermute x3, waiting for transfers between devices, doubling_gather(): got = lax.ppermute(block, axis_name, pairs)  31.8 us
    ppermute x1, waiting for transfers between devices, on_device(): other_squares = lax.ppermute(squares, 'col', swap)  24.4 us
    pallas_call x1, Pallas kernels, slot_attention(): pl.pallas_call(partial(slot_kernel, ns=ns, heads=heads, qpk=qpk), grid_sp...  21 us
    ppermute x3, waiting for transfers between devices, seq_merge(): lax.ppermute(send_values.astype(jnp.bfloat16), 'seq', pairs)  17.2 us
    dot_general x3, matrix products, on_device(): jnp.dot(gathered, matrix, preferred_element_type=jnp.float32)  8.8 us
    ppermute x3, starting transfers between devices, seq_merge(): got_stats = lax.ppermute(send_stats, 'seq', pairs)  7.83 us
    ppermute x2, waiting for transfers between devices, pair_scatter(): got = lax.ppermute(send, axis_name, [(0, 1), (1, 0)])  7.63 us
    dot_general x1, matrix products, on_device(): jnp.dot(piece_rows.reshape(n_row * per * step_count, -1), wo, preferred_e...  5.88 us
  transfers between devices with their start and end apart: 13, of which 11 were waited for; matrix products, arithmetic and copies ran while one was open for 4% of the time, Pallas kernels for 0%

profile of v12, /device:TPU:0, one launch (start us, length us, event | category | flops | bytes accessed | tf_op | source)
XLA Modules:
  0.0 178.8 jit_solution(16658837114396569122)
XLA Ops:
  0.7 3.5 %reshape.797 = bf16[256,2560]{1,0:T(8,128)(2,1)} reshape(bf16[64,4,2560]{2,1,0:T(4,128)(2,1)} %param.11) | data formatting | bytes 2621440 | tf_op jit(solution)/shard_map/reshape | solution.py:318
  4.2 2.9 %collective-permute-start = (bf16[256,2560]{1,0:T(8,128)(2,1)}, bf16[256,2560]{1,0:T(8,128)(2,1)}, u32[]{:S(2)}, u32[]{:S(2)}) collective-permute-start(bf16[256,2560]{1,0:T(8,128)(2,1)} %reshape.797), channel_id=1, source_target_pairs={{0,8},{8,0},{1,9},{9,1},{2,10},{10,2},{3,11},{11,3},{4,12},{12,4},... | collective-permute-start | bytes 3932168 | tf_op jit(solution)/shard_map/ppermute | solution.py:321
  7.1 2.1 %multiply_reduce_fusion = f32[64,4]{1,0:T(8,128)S(1)} fusion(bf16[64,4,2560]{2,1,0:T(4,128)(2,1)} %param.11), kind=kLoop, calls=%fused_computation.9 | loop fusion | flops 1965824 | bytes 1311744 | tf_op jit(solution)/shard_map/reduce_sum | solution.py:323
  9.3 2.5 %psum.7 = f32[256]{0:T(256)S(1)} all-reduce(f32[256]{0:T(256)S(1)} %reduce_sum.21), channel_id=1, replica_groups=mesh['row'=2,'col'=2,'seq'=8] {'row'}, use_global_device_ids=true, to_apply=%region_1.0 | all-reduce | flops 256 | bytes 2048 | tf_op jit(solution)/shard_map/psum | solution.py:323
  11.8 24.4 %collective-permute-done.1 = f32[256]{0:T(256)S(1)} collective-permute-done((f32[256]{0:T(256)S(1)}, f32[256]{0:T(256)S(1)}, u32[]{:S(2)}, u32[]{:S(2)}) %collective-permute-start.1) | collective-permute-done | bytes 1056 | tf_op jit(solution)/shard_map/ppermute | solution.py:324
  36.3 2.8 %multiply_convert_fusion.1 = (bf16[256,2560]{1,0:T(8,128)(2,1)S(1)}, bf16[256,2560]{1,0:T(8,128)(2,1)S(1)}) fusion(f32[2560]{0:T(1024)S(1)} %copy-done.5, f32[256]{0:T(256)S(1)} %get-tuple-element.49, bf16[256,2560]{1,0:T(8,128)(2,1)} %reshape.797, bf16[256,2560]{1,0:T(8,128)(2,1)} %collective-permute-done, pred[]{:T(512)S(6)} %eq.15, ...), kind=kLoop, calls=%fused_computation.8 | loop fusion | flops 6553600 | bytes 5255169 | tf_op jit(solution)/shard_map/convert_element_type | solution.py:328
  39.1 1.5 convolution_convert_fusion.2
  40.7 1.5 convolution_convert_fusion.1
  42.2 0.4 slice-done.1
  42.6 0.8 slice-done.2
  43.4 5.8 %convolution_convert_fusion = bf16[512,2048]{1,0:T(8,128)(2,1)S(1)} fusion(bf16[2560,2048]{1,0:T(8,128)(2,1)S(1)} %bitcast.165, bf16[256,2560]{1,0:T(8,128)(2,1)S(1)} %get-tuple-element.32, bf16[256,2560]{1,0:T(8,128)(2,1)S(1)} %get-tuple-element.31), kind=kOutput, calls=%fused_computation.5 | convolution fusion | flops 5375000576 | bytes 15204352 | tf_op jit(solution)/shard_map/dot_general | solution.py:343
  49.2 0.3 pad_maximum_fusion
  49.5 1.6 copy-done.2
  51.1 1.3 constant_dynamic-slice_fusion.2
  52.5 0.1 convert_element_type.105
  52.6 0.5 multiply_cosine_fusion
  53.2 2.9 %collective-permute-done.2 = bf16[1,256,3072]{2,1,0:T(8,128)(2,1)S(1)} collective-permute-done((bf16[1,256,3072]{2,1,0:T(8,128)(2,1)}, bf16[1,256,3072]{2,1,0:T(8,128)(2,1)S(1)}, u32[]{:S(2)}, u32[]{:S(2)}) %collective-permute-start.2) | collective-permute-done | bytes 1572896 | tf_op jit(solution)/shard_map/ppermute | solution.py:238
  56.0 1.9 %add_bitcast_fusion = f32[32,8,24,128]{3,1,2,0:T(8,128)S(1)} fusion(bf16[1,256,3072]{2,1,0:T(8,128)(2,1)S(1)} %collective-permute-done.2, bf16[2,256,3072]{2,1,0:T(8,128)(2,1)} %copy-done.2, s32[]{:T(128)S(6)} %select_n.176), kind=kLoop, calls=%fused_computation.4 | loop fusion | flops 2359296 | bytes 6291460
  58.0 0.6 copy.125
  58.5 0.1 slice.161
  58.7 0.4 add_convert_fusion.1
  59.1 0.8 subtract_convert_fusion
  59.9 1.4 pad_maximum_fusion.2
  61.3 0.5 copy.109
  62.0 1.3 fusion.7
  63.3 0.5 copy.89
  63.8 0.2 select_reduce_fusion
  64.0 0.2 fusion.11
  64.2 21.0 %shard_map.130 = (f32[64,64,1]{2,1,0:T(8,128)}, f32[64,64,1]{2,1,0:T(8,128)}, f32[64,64,128]{2,1,0:T(8,128)}) custom-call(s32[50]{0:T(128)} %req_ref.1, s32[64]{0:T(128)} %len_ref.1, s32[50]{0:T(128)} %blk_ref.1, bf16[64,64,128]{2,1,0:T(8,128)(2,1)} %bitcast.136, bf16[50,128,512]{2,1,0:T(8,128)(2,1)} %k_ref.1, bf16[50,128,512]{2,1,0:T(8,128)(2,1)} %v_ref.1), custom_call_target="tpu_custom_call" | custom-call | tf_op jit(solution)/shard_map/pallas_call | solution.py:210
  85.2 2.4 %reduce.1 = f32[64,64]{1,0:T(8,128)S(1)} reduce(f32[64,64,1]{2,1,0:T(8,128)} %get-tuple-element.7, f32[]{:T(128)} %constant.102), dimensions={2}, to_apply=%get-tuple-element.7.reduce_sub_computation | reduce | bytes 32772 | tf_op jit(solution)/shard_map/pallas_call | solution.py:210
  87.5 0.6 reduce.2
  88.2 3.4 %collective-permute-start.3 = (f32[2,2,2,1,8,64]{5,4,3,2,1,0:T(8,128)S(1)}, f32[2,2,2,1,8,64]{5,4,3,2,1,0:T(8,128)S(1)}, u32[]{:S(2)}, u32[]{:S(2)}) collective-permute-start(f32[2,2,2,1,8,64]{5,4,3,2,1,0:T(8,128)S(1)} %get-tuple-element.40), channel_id=1, source_target_pairs={{0,1},{1,0},{2,3},{3,2},{4,5},{5,4},{6,7},{7,6},{8,9},{9,8},{10,11... | collective-permute-start | bytes 49160 | tf_op jit(solution)/shard_map/ppermute | solution.py:278
  91.5 1.3 dynamic-slice_convert_fusion
  92.9 0.5 copy.96
  93.5 2.7 %collective-permute-start.5 = (f32[2,2,1,1,8,64]{5,4,3,2,1,0:T(8,128)S(1)}, f32[2,2,1,1,8,64]{5,4,3,2,1,0:T(8,128)S(1)}, u32[]{:S(2)}, u32[]{:S(2)}) collective-permute-start(f32[2,2,1,1,8,64]{5,4,3,2,1,0:T(8,128)S(1)} %get-tuple-element.44), channel_id=1, source_target_pairs={{0,2},{1,3},{2,0},{3,1},{4,6},{5,7},{6,4},{7,5},{8,10},{9,11},{10,... | collective-permute-start | bytes 24584 | tf_op jit(solution)/shard_map/ppermute | solution.py:278
  96.2 1.7 collective-permute-done.5
  98.0 1.7 collective-permute-start.7
  99.7 2.9 %collective-permute-done.7 = f32[2,1,1,1,8,64]{5,4,3,2,1,0:T(8,128)S(1)} collective-permute-done((f32[2,1,1,1,8,64]{5,4,3,2,1,0:T(8,128)S(1)}, f32[2,1,1,1,8,64]{5,4,3,2,1,0:T(8,128)S(1)}, u32[]{:S(2)}, u32[]{:S(2)}) %collective-permute-start.7) | collective-permute-done | bytes 4128 | tf_op jit(solution)/shard_map/ppermute | solution.py:278
  102.8 4.3 %collective-permute-done.4 = bf16[2,2,1,8,64,128]{5,4,3,2,1,0:T(8,128)(2,1)S(1)} collective-permute-done((bf16[2,2,1,8,64,128]{5,4,3,2,1,0:T(8,128)(2,1)S(1)}, bf16[2,2,1,8,64,128]{5,4,3,2,1,0:T(8,128)(2,1)S(1)}, u32[]{:S(2)}, u32[]{:S(2)}) %collective-permute-start.4) | collective-permute-done | bytes 524320 | tf_op jit(solution)/shard_map/ppermute | solution.py:279
  107.1 1.8 %multiply_add_fusion = f32[2,2,1,8,64,128]{5,4,3,2,1,0:T(8,128)S(1)} fusion(bf16[2,2,1,8,64,128]{5,4,3,2,1,0:T(8,128)(2,1)S(1)} %collective-permute-done.4, f32[2,2,2,8,64,128]{5,4,3,2,1,0:T(8,128)} %bitcast.148, s32[]{:T(128)S(6)} %select_n.178, f32[2,2,8,64]{3,2,1,0:T(8,128)S(1)} %get-tuple-element.38, f32[2,2,8,64]{3,2,1,0:T(8,128)S(1)} %get-tuple-element.37), kind=kLoop, calls=%fused_computation.18 | loop fusion | flops 1048576 | bytes 2637828 | tf_op jit(solution)/shard_map/add | solution.py:288
  109.1 0.2 copy.92
  109.3 0.2 copy.98
  109.5 0.2 copy.102
  109.6 0.2 convolution_multiply_fusion
  109.9 6.4 %collective-permute-done.6 = bf16[2,1,1,8,64,128]{5,4,3,2,1,0:T(8,128)(2,1)S(1)} collective-permute-done((bf16[2,1,1,8,64,128]{5,4,3,2,1,0:T(8,128)(2,1)S(1)}, bf16[2,1,1,8,64,128]{5,4,3,2,1,0:T(8,128)(2,1)S(1)}, u32[]{:S(2)}, u32[]{:S(2)}) %collective-permute-start.6) | collective-permute-done | bytes 262176 | tf_op jit(solution)/shard_map/ppermute | solution.py:279
  116.3 0.3 multiply_add_fusion.1
  116.6 2.7 %collective-permute-start.8 = (bf16[1,1,1,8,64,128]{5,4,3,2,1,0:T(8,128)(2,1)S(1)}, bf16[1,1,1,8,64,128]{5,4,3,2,1,0:T(8,128)(2,1)S(1)}, u32[]{:S(2)}, u32[]{:S(2)}) collective-permute-start(bf16[1,1,1,8,64,128]{5,4,3,2,1,0:T(8,128)(2,1)S(1)} %dynamic-slice_convert_fusion.2), channel_id=1, source_target_pairs={{0,4},{1,5},{2,6},{3,7},{4,0},{5,1},{6,2},{7,3},{8,12},{9,13},{10,... | collective-permute-start | bytes 393224 | tf_op jit(solution)/shard_map/ppermute | solution.py:279
  119.3 6.4 %collective-permute-done.8 = bf16[1,1,1,8,64,128]{5,4,3,2,1,0:T(8,128)(2,1)S(1)} collective-permute-done((bf16[1,1,1,8,64,128]{5,4,3,2,1,0:T(8,128)(2,1)S(1)}, bf16[1,1,1,8,64,128]{5,4,3,2,1,0:T(8,128)(2,1)S(1)}, u32[]{:S(2)}, u32[]{:S(2)}) %collective-permute-start.8) | collective-permute-done | bytes 131104 | tf_op jit(solution)/shard_map/ppermute | solution.py:279
  125.8 0.2 multiply_add_fusion.2
  126.0 0.3 fusion.9
  126.5 2.0 %all_gather.4 = bf16[2,8,4,2048]{3,1,2,0:T(8,128)(2,1)S(1)} all-gather(bf16[1,8,4,2048]{3,1,2,0:T(8,128)(2,1)S(1)} %convert_element_type.115), channel_id=1, replica_groups=mesh['row'=2,'col'=2,'seq'=8] {'row'}, dimensions={0}, use_global_device_ids=true | all-gather | bytes 393216 | tf_op jit(solution)/shard_map/all_gather | solution.py:407
  128.5 5.9 %fusion.2 = bf16[2,8,4,2560]{3,1,2,0:T(8,128)(2,1)S(1)} fusion(bf16[2,8,4,2048]{3,1,2,0:T(8,128)(2,1)S(1)} %all_gather.4, bf16[2048,2560]{1,0:T(8,128)(2,1)} %param.16), kind=kOutput, calls=%fused_computation.2 | convolution fusion | flops 671252480 | bytes 11075584 | tf_op jit(solution)/shard_map/dot_general | solution.py:409
  134.4 1.6 collective-permute-start.9
  135.9 4.8 %collective-permute-done.9 = bf16[1,8,4,2560]{3,1,2,0:T(8,128)(2,1)S(1)} collective-permute-done((bf16[1,8,4,2560]{3,1,2,0:T(8,128)(2,1)S(1)}, bf16[1,8,4,2560]{3,1,2,0:T(8,128)(2,1)S(1)}, u32[]{:S(2)}, u32[]{:S(2)}) %collective-permute-start.9) | collective-permute-done | bytes 163872 | tf_op jit(solution)/shard_map/ppermute | solution.py:238
  140.8 9.8 %collective-permute-done.10 = bf16[1,8,4,2560]{3,1,2,0:T(8,128)(2,1)S(1)} collective-permute-done((bf16[1,8,4,2560]{3,1,2,0:T(8,128)(2,1)S(1)}, bf16[1,8,4,2560]{3,1,2,0:T(8,128)(2,1)S(1)}, u32[]{:S(2)}, u32[]{:S(2)}) %collective-permute-start.10) | collective-permute-done | bytes 163872 | tf_op jit(solution)/shard_map/ppermute | solution.py:251
  150.8 9.6 %collective-permute-done.11 = bf16[2,1,8,4,2560]{4,2,3,1,0:T(8,128)(2,1)S(1)} collective-permute-done((bf16[2,1,8,4,2560]{4,2,3,1,0:T(8,128)(2,1)S(1)}, bf16[2,1,8,4,2560]{4,2,3,1,0:T(8,128)(2,1)S(1)}, u32[]{:S(2)}, u32[]{:S(2)}) %collective-permute-start.11) | collective-permute-done | bytes 327712 | tf_op jit(solution)/shard_map/ppermute | solution.py:251
  160.5 1.4 collective-permute-start.12
  161.9 0.8 reshape_reshape.8
  162.7 0.4 pad_maximum_fusion.6
  163.0 0.8 convert_element_type.120
  164.0 12.4 %collective-permute-done.12 = bf16[2,2,1,8,4,2560]{5,3,4,1,2,0:T(8,128)(2,1)S(1)} collective-permute-done((bf16[2,2,1,8,4,2560]{5,3,4,1,2,0:T(8,128)(2,1)S(1)}, bf16[2,2,1,8,4,2560]{5,3,4,1,2,0:T(8,128)(2,1)S(1)}, u32[]{:S(2)}, u32[]{:S(2)}) %collective-permute-start.12) | collective-permute-done | bytes 655392 | tf_op jit(solution)/shard_map/ppermute | solution.py:251
  176.4 0.2 fusion.5
  176.6 0.1 copy.104
  176.7 2.1 %copy.105 = bf16[64,4,2560]{2,1,0:T(4,128)(2,1)} copy(bf16[64,4,2560]{2,0,1:T(8,128)(2,1)S(1)} %bitcast.135) | data formatting | bytes 2621440
  (58 shorter events, 1.7 us)
Async XLA Ops:
  0.6 38.5 %copy-start = (bf16[2560,512]{1,0:T(8,128)(2,1)S(1)}, bf16[2560,512]{1,0:T(8,128)(2,1)}, u32[]{:S(2)}) copy-start(bf16[2560,512]{1,0:T(8,128)(2,1)} %param.14) | copy-start | bytes 7864324
  0.6 35.6 %copy-start.5 = (f32[2560]{0:T(1024)S(1)}, f32[2560]{0:T(1024)}, u32[]{:S(2)}) copy-start(f32[2560]{0:T(1024)} %param.12) | copy-start | bytes 30724
  4.2 32.0 %collective-permute-start = (bf16[256,2560]{1,0:T(8,128)(2,1)}, bf16[256,2560]{1,0:T(8,128)(2,1)}, u32[]{:S(2)}, u32[]{:S(2)}) collective-permute-start(bf16[256,2560]{1,0:T(8,128)(2,1)} %reshape.797), channel_id=1, source_target_pairs={{0,8},{8,0},{1,9},{9,1},{2,10},{10,2},{3,11},{11,3},{4,12},{12,4},... | collective-permute-start | bytes 3932168 | tf_op jit(solution)/shard_map/ppermute | solution.py:321
  11.8 24.4 %collective-permute-start.1 = (f32[256]{0:T(256)S(1)}, f32[256]{0:T(256)S(1)}, u32[]{:S(2)}, u32[]{:S(2)}) collective-permute-start(f32[256]{0:T(256)S(1)} %psum.7), channel_id=1, source_target_pairs={{0,8},{8,0},{1,9},{9,1},{2,10},{10,2},{3,11},{11,3},{4,12},{12,4},... | collective-permute-start | bytes 3080 | tf_op jit(solution)/shard_map/ppermute | solution.py:324
  36.3 4.4 %copy-start.7 = (bf16[2560,512]{1,0:T(8,128)(2,1)S(1)}, bf16[2560,512]{1,0:T(8,128)(2,1)}, u32[]{:S(2)}) copy-start(bf16[2560,512]{1,0:T(8,128)(2,1)} %param.15) | copy-start | bytes 7864324
  39.1 3.1 %slice-start = ((s8[10485760]{0:T(1024)(128)(4,1)}), s8[4194304]{0:T(1024)(128)(4,1)S(1)}, s32[]{:S(2)}) async-start(s8[10485760]{0:T(1024)(128)(4,1)} %bitcast.164), calls=%async_computation | async-start | bytes 8388608
  39.1 3.5 %slice-start.1 = ((s8[10485760]{0:T(1024)(128)(4,1)}), s8[4194304]{0:T(1024)(128)(4,1)S(1)}, s32[]{:S(2)}) async-start(s8[10485760]{0:T(1024)(128)(4,1)} %bitcast.164), calls=%async_computation.1 | async-start | bytes 8388608
  40.7 2.7 %slice-start.2 = ((s8[10485760]{0:T(1024)(128)(4,1)}), s8[2097152]{0:T(1024)(128)(4,1)S(1)}, s32[]{:S(2)}) async-start(s8[10485760]{0:T(1024)(128)(4,1)} %bitcast.164), calls=%async_computation.2 | async-start | bytes 4194304
  49.5 1.6 copy-start.2
  51.1 1.3 copy-start.6
  52.4 3.6 %collective-permute-start.2 = (bf16[1,256,3072]{2,1,0:T(8,128)(2,1)}, bf16[1,256,3072]{2,1,0:T(8,128)(2,1)S(1)}, u32[]{:S(2)}, u32[]{:S(2)}) collective-permute-start(bf16[1,256,3072]{2,1,0:T(8,128)(2,1)} %constant_dynamic-slice_fusion.2), channel_id=1, source_target_pairs={{0,16},{16,0},{1,17},{17,1},{2,18},{18,2},{3,19},{19,3},{4,20},{20... | collective-permute-start | bytes 4718600 | tf_op jit(solution)/shard_map/ppermute | solution.py:238
  61.8 2.4 %copy-start.3 = (bf16[64,4,4,4,128]{4,3,1,2,0:T(4,128)(2,1)}, bf16[64,4,4,4,128]{4,3,1,2,0:T(4,128)(2,1)S(1)}, u32[]{:S(2)}) copy-start(bf16[64,4,4,4,128]{4,3,1,2,0:T(4,128)(2,1)S(1)} %copy.109) | copy-start | bytes 3145732
  85.2 2.4 %copy-start.4 = (f32[64,64,1]{2,1,0:T(8,128)S(1)}, f32[64,64,1]{2,1,0:T(8,128)}, u32[]{:S(2)}) copy-start(f32[64,64,1]{2,1,0:T(8,128)} %get-tuple-element.8) | copy-start | bytes 49156
  88.2 5.3 %collective-permute-start.3 = (f32[2,2,2,1,8,64]{5,4,3,2,1,0:T(8,128)S(1)}, f32[2,2,2,1,8,64]{5,4,3,2,1,0:T(8,128)S(1)}, u32[]{:S(2)}, u32[]{:S(2)}) collective-permute-start(f32[2,2,2,1,8,64]{5,4,3,2,1,0:T(8,128)S(1)} %get-tuple-element.40), channel_id=1, source_target_pairs={{0,1},{1,0},{2,3},{3,2},{4,5},{5,4},{6,7},{7,6},{8,9},{9,8},{10,11... | collective-permute-start | bytes 49160 | tf_op jit(solution)/shard_map/ppermute | solution.py:278
  93.4 13.7 %collective-permute-start.4 = (bf16[2,2,1,8,64,128]{5,4,3,2,1,0:T(8,128)(2,1)S(1)}, bf16[2,2,1,8,64,128]{5,4,3,2,1,0:T(8,128)(2,1)S(1)}, u32[]{:S(2)}, u32[]{:S(2)}) collective-permute-start(bf16[2,2,1,8,64,128]{5,4,3,2,1,0:T(8,128)(2,1)S(1)} %dynamic-slice_convert_fusion), channel_id=1, source_target_pairs={{0,1},{1,0},{2,3},{3,2},{4,5},{5,4},{6,7},{7,6},{8,9},{9,8},{10,11... | collective-permute-start | bytes 1572872 | tf_op jit(solution)/shard_map/ppermute | solution.py:279
  93.5 4.4 %collective-permute-start.5 = (f32[2,2,1,1,8,64]{5,4,3,2,1,0:T(8,128)S(1)}, f32[2,2,1,1,8,64]{5,4,3,2,1,0:T(8,128)S(1)}, u32[]{:S(2)}, u32[]{:S(2)}) collective-permute-start(f32[2,2,1,1,8,64]{5,4,3,2,1,0:T(8,128)S(1)} %get-tuple-element.44), channel_id=1, source_target_pairs={{0,2},{1,3},{2,0},{3,1},{4,6},{5,7},{6,4},{7,5},{8,10},{9,11},{10,... | collective-permute-start | bytes 24584 | tf_op jit(solution)/shard_map/ppermute | solution.py:278
  98.0 4.6 %collective-permute-start.7 = (f32[2,1,1,1,8,64]{5,4,3,2,1,0:T(8,128)S(1)}, f32[2,1,1,1,8,64]{5,4,3,2,1,0:T(8,128)S(1)}, u32[]{:S(2)}, u32[]{:S(2)}) collective-permute-start(f32[2,1,1,1,8,64]{5,4,3,2,1,0:T(8,128)S(1)} %get-tuple-element.48), channel_id=1, source_target_pairs={{0,4},{1,5},{2,6},{3,7},{4,0},{5,1},{6,2},{7,3},{8,12},{9,13},{10,... | collective-permute-start | bytes 12296 | tf_op jit(solution)/shard_map/ppermute | solution.py:278
  109.0 7.3 %collective-permute-start.6 = (bf16[2,1,1,8,64,128]{5,4,3,2,1,0:T(8,128)(2,1)S(1)}, bf16[2,1,1,8,64,128]{5,4,3,2,1,0:T(8,128)(2,1)S(1)}, u32[]{:S(2)}, u32[]{:S(2)}) collective-permute-start(bf16[2,1,1,8,64,128]{5,4,3,2,1,0:T(8,128)(2,1)S(1)} %dynamic-slice_convert_fusion.1), channel_id=1, source_target_pairs={{0,2},{1,3},{2,0},{3,1},{4,6},{5,7},{6,4},{7,5},{8,10},{9,11},{10,... | collective-permute-start | bytes 786440 | tf_op jit(solution)/shard_map/ppermute | solution.py:279
  116.6 9.2 %collective-permute-start.8 = (bf16[1,1,1,8,64,128]{5,4,3,2,1,0:T(8,128)(2,1)S(1)}, bf16[1,1,1,8,64,128]{5,4,3,2,1,0:T(8,128)(2,1)S(1)}, u32[]{:S(2)}, u32[]{:S(2)}) collective-permute-start(bf16[1,1,1,8,64,128]{5,4,3,2,1,0:T(8,128)(2,1)S(1)} %dynamic-slice_convert_fusion.2), channel_id=1, source_target_pairs={{0,4},{1,5},{2,6},{3,7},{4,0},{5,1},{6,2},{7,3},{8,12},{9,13},{10,... | collective-permute-start | bytes 393224 | tf_op jit(solution)/shard_map/ppermute | solution.py:279
  134.4 6.3 %collective-permute-start.9 = (bf16[1,8,4,2560]{3,1,2,0:T(8,128)(2,1)S(1)}, bf16[1,8,4,2560]{3,1,2,0:T(8,128)(2,1)S(1)}, u32[]{:S(2)}, u32[]{:S(2)}) collective-permute-start(bf16[1,8,4,2560]{3,1,2,0:T(8,128)(2,1)S(1)} %constant_dynamic-slice_fusion.1), channel_id=1, source_target_pairs={{0,8},{8,0},{1,9},{9,1},{2,10},{10,2},{3,11},{11,3},{4,12},{12,4},... | collective-permute-start | bytes 491528 | tf_op jit(solution)/shard_map/ppermute | solution.py:238
  140.7 9.9 %collective-permute-start.10 = (bf16[1,8,4,2560]{3,1,2,0:T(8,128)(2,1)S(1)}, bf16[1,8,4,2560]{3,1,2,0:T(8,128)(2,1)S(1)}, u32[]{:S(2)}, u32[]{:S(2)}) collective-permute-start(bf16[1,8,4,2560]{3,1,2,0:T(8,128)(2,1)S(1)} %add_convert_fusion.2), channel_id=1, source_target_pairs={{0,4},{1,5},{2,6},{3,7},{4,0},{5,1},{6,2},{7,3},{8,12},{9,13},{10,... | collective-permute-start | bytes 491528 | tf_op jit(solution)/shard_map/ppermute | solution.py:251
  150.7 9.7 %collective-permute-start.11 = (bf16[2,1,8,4,2560]{4,2,3,1,0:T(8,128)(2,1)S(1)}, bf16[2,1,8,4,2560]{4,2,3,1,0:T(8,128)(2,1)S(1)}, u32[]{:S(2)}, u32[]{:S(2)}) collective-permute-start(bf16[2,1,8,4,2560]{4,2,3,1,0:T(8,128)(2,1)S(1)} %maximum_select_fusion.4), channel_id=1, source_target_pairs={{0,2},{1,3},{2,0},{3,1},{4,6},{5,7},{6,4},{7,5},{8,10},{9,11},{10,... | collective-permute-start | bytes 983048 | tf_op jit(solution)/shard_map/ppermute | solution.py:251
  160.5 15.9 %collective-permute-start.12 = (bf16[2,2,1,8,4,2560]{5,3,4,1,2,0:T(8,128)(2,1)S(1)}, bf16[2,2,1,8,4,2560]{5,3,4,1,2,0:T(8,128)(2,1)S(1)}, u32[]{:S(2)}, u32[]{:S(2)}) collective-permute-start(bf16[2,2,1,8,4,2560]{5,3,4,1,2,0:T(8,128)(2,1)S(1)} %maximum_select_fusion.2), channel_id=1, source_target_pairs={{0,1},{1,0},{2,3},{3,2},{4,5},{5,4},{6,7},{7,6},{8,9},{9,8},{10,11... | collective-permute-start | bytes 1966088 | tf_op jit(solution)/shard_map/ppermute | solution.py:251
  176.4 2.4 %copy-start.1 = (bf16[2560,512]{1,0:T(8,128)(2,1)S(1)}, bf16[2560,512]{1,0:T(8,128)(2,1)}, u32[]{:S(2)}) copy-start(bf16[2560,512]{1,0:T(8,128)(2,1)} %param.14) | copy-start | bytes 7864324

commit v13 on v10

--- a/solution.py
+++ b/solution.py
@@ -115,8 +115,17 @@
     return (running_peak, running_totals, weighted_values)
 
 
-def slot_kernel(len_ref, blk_ref, q_ref, k_ref, v_ref, peak_ref, tot_ref, acc_ref, *, ns, heads, qpk):
+def slot_kernel(
+    req_ref, len_ref, blk_ref, q_ref, k_ref, v_ref, peak_ref, tot_ref, acc_ref, *, ns, heads, qpk
+):
+    @pl.when(pl.program_id(0) == 0)
+    def _():
+        peak_ref[...] = jnp.full(peak_ref.shape, NEGATIVE_FILL, jnp.float32)
+        tot_ref[...] = jnp.zeros(tot_ref.shape, jnp.float32)
+        acc_ref[...] = jnp.zeros(acc_ref.shape, jnp.float32)
+
     base = pl.program_id(0) * ns
+    req_count = q_ref.shape[0]
     rows = q_ref.shape[1]
     group = rows // heads
     width = k_ref.shape[1]
@@ -125,12 +134,19 @@
     col = lax.broadcasted_iota(jnp.int32, (rows, width), 1)
     step_of = (row % group) // qpk
 
-    def body(i, carry):
-        length = len_ref[base + i]
+    results = []
+    for i in range(ns):
+        req = req_ref[base + i]
+        owner = jnp.minimum(req, req_count - 1)
+        length = len_ref[owner]
         key_pos = blk_ref[base + i] * width + col
         query_pos = length + step_of
-        visible = (key_pos < length) & ((key_pos < SINK) | (key_pos > query_pos - WINDOW))
-        q = q_ref[i]
+        visible = (
+            (req < req_count)
+            & (key_pos < length)
+            & ((key_pos < SINK) | (key_pos > query_pos - WINDOW))
+        )
+        q = q_ref[owner]
         k = k_ref[i]
         v = v_ref[i]
         scores = jnp.concatenate(
@@ -160,42 +176,45 @@
             ],
             0,
         )
-        peak_ref[i] = peak
-        tot_ref[i] = total
-        acc_ref[i] = acc
-        return carry
-
-    lax.fori_loop(0, ns, body, 0, unroll=True)
-
-
-def slot_attention(slot_queries, slot_lengths, block_numbers, keys, values, heads, qpk):
-    n_slots, rows, head = slot_queries.shape
+        results.append((owner, peak, total, acc))
+    for owner, peak, total, acc in results:
+        old = peak_ref[owner]
+        top = jnp.maximum(old, peak)
+        old_factor = jnp.exp(old - top)
+        new_factor = jnp.exp(peak - top)
+        tot_ref[owner] = tot_ref[owner] * old_factor + total * new_factor
+        acc_ref[owner] = acc_ref[owner] * old_factor + acc * new_factor
+        peak_ref[owner] = top
+
+def slot_attention(queries, lengths, slot_request, block_numbers, keys, values, heads, qpk):
+    req_count, rows, head = queries.shape
+    n_slots = keys.shape[0]
     width = keys.shape[1]
     ns = max(d for d in range(1, 11) if n_slots % d == 0)
+    fixed = lambda n, sr, lr, br: (0, 0, 0)
     grid_spec = pltpu.PrefetchScalarGridSpec(
-        num_scalar_prefetch=2,
+        num_scalar_prefetch=3,
         grid=(n_slots // ns,),
         in_specs=[
-            pl.BlockSpec((ns, rows, head), lambda n, lr, br: (n, 0, 0)),
-            pl.BlockSpec((ns, width, keys.shape[2]), lambda n, lr, br: (n, 0, 0)),
-            pl.BlockSpec((ns, width, values.shape[2]), lambda n, lr, br: (n, 0, 0)),
+            pl.BlockSpec((req_count, rows, head), fixed),
+            pl.BlockSpec((ns, width, keys.shape[2]), lambda n, sr, lr, br: (n, 0, 0)),
+            pl.BlockSpec((ns, width, values.shape[2]), lambda n, sr, lr, br: (n, 0, 0)),
         ],
         out_specs=[
-            pl.BlockSpec((ns, rows, 1), lambda n, lr, br: (n, 0, 0)),
-            pl.BlockSpec((ns, rows, 1), lambda n, lr, br: (n, 0, 0)),
-            pl.BlockSpec((ns, rows, head), lambda n, lr, br: (n, 0, 0)),
+            pl.BlockSpec((req_count, rows, 1), fixed),
+            pl.BlockSpec((req_count, rows, 1), fixed),
+            pl.BlockSpec((req_count, rows, head), fixed),
         ],
     )
     return pl.pallas_call(
         partial(slot_kernel, ns=ns, heads=heads, qpk=qpk),
         grid_spec=grid_spec,
         out_shape=[
-            jax.ShapeDtypeStruct((n_slots, rows, 1), jnp.float32),
-            jax.ShapeDtypeStruct((n_slots, rows, 1), jnp.float32),
-            jax.ShapeDtypeStruct((n_slots, rows, head), jnp.float32),
+            jax.ShapeDtypeStruct((req_count, rows, 1), jnp.float32),
+            jax.ShapeDtypeStruct((req_count, rows, 1), jnp.float32),
+            jax.ShapeDtypeStruct((req_count, rows, head), jnp.float32),
         ],
-    )(slot_lengths, block_numbers, slot_queries, keys, values)
-
+    )(slot_request, lengths, block_numbers, queries, keys, values)
 
 def pair_gather(part, axis_name):
     n = lax.axis_size(axis_name)
@@ -346,31 +365,18 @@
         .astype(jnp.bfloat16)
         .reshape(req_count, step_count, heads_kv, HEAD_SIZE)
     )
-    picked = jnp.minimum(slot_request, req_count - 1)
-    in_use = slot_request < req_count
-    slot_lengths = jnp.where(in_use, lengths[picked], 0)
-    flat_queries = query_rows.transpose(0, 2, 1, 3, 4).reshape(req_count, -1, HEAD_SIZE)
-    slot_peak, slot_total, slot_acc = slot_attention(
-        flat_queries[picked],
-        slot_lengths,
+    local_peak, local_totals, local_values = slot_attention(
+        query_rows.transpose(0, 2, 1, 3, 4).reshape(req_count, -1, HEAD_SIZE),
+        lengths,
+        slot_request,
         slot_block_number,
         paged_key_cache,
         paged_value_cache,
         heads_kv,
         QUERY_PER_KEY,
     )
-    slot_peak = slot_peak[..., 0]
-    slot_total = slot_total[..., 0]
-    member = slot_request[None, :] == jnp.arange(req_count, dtype=jnp.int32)[:, None]
-    local_peak = jnp.max(jnp.where(member[:, :, None], slot_peak[None], NEGATIVE_FILL), 1)
-    factor = jnp.exp(slot_peak - local_peak[picked])
-    as_member = member.astype(jnp.float32)
-    local_totals = jnp.einsum(
-        "rn,nj->rj", as_member, slot_total * factor, precision=lax.Precision.HIGHEST
-    )
-    local_values = jnp.einsum(
-        "rn,njh->rjh", as_member, slot_acc * factor[..., None], precision=lax.Precision.HIGHEST
-    )
+    local_peak = local_peak[..., 0]
+    local_totals = local_totals[..., 0]
     n_seq = lax.axis_size("seq")
     per = req_count // n_seq
     seq_index = lax.axis_index("seq")

time: 182 us -> 173 us (0.951)
  local copies, waits for them, and re-layouts: 22.4 us -> 16.2 us
  other arithmetic: 22.6 us -> 17.5 us
  waiting for transfers between devices: 77 us -> 79.7 us
  matrix products: 18.8 us -> 16.2 us
  Pallas kernels: 17.2 us -> 19.7 us
    gather x4 -> x0, local copies, waits for them, and re-layouts: 4.72 us -> none  [the longest x2 2.38 us: on_device(): factor = jnp.exp(slot_peak - local_peak[picked])]
    mul x2 -> x0, other arithmetic: 3.47 us -> none  [the longest x1 2.97 us: on_device(): slot_total * factor]
    pallas_call x1, Pallas kernels: 17.2 us -> 19.7 us  [slot_attention(): pl.pallas_call(partial(slot_kernel, ns=ns, heads=heads, qpk=qpk), grid_sp...]
    dot_general x2 -> x0, matrix products: 2.38 us -> none  [the longest x1 2.18 us: on_device(): jnp.einsum('rn,njh->rjh', as_member, slot_acc * factor[..., None], precis...]
    ppermute x3, waiting for transfers between devices: 1.61 us -> 3.59 us  [seq_merge(): got_stats = lax.ppermute(send_stats, 'seq', pairs)]
    unnamed x30 -> x24, local copies, waits for them, and re-layouts: 6.82 us -> 5.49 us
  transfers between devices with their start and end apart: 13 -> 13, of which waited for: 10 -> 11; matrix products, arithmetic and copies ran while one was open for 8% -> 5% of each run, Pallas kernels for 0% -> 0%
where the time goes in v13:
time: 173 us; the launch traced here: 172 us
  waiting for transfers between devices  79.7 us (46%)
  Pallas kernels  19.7 us (11%)
  other arithmetic  17.5 us (10%)
  starting transfers between devices  17.4 us (10%)
  local copies, waits for them, and re-layouts  16.2 us (9%)
  matrix products  16.2 us (9%)
  blocking collectives  4.46 us (3%)
    ppermute x3, waiting for transfers between devices, doubling_gather(): got = lax.ppermute(block, axis_name, pairs)  29.7 us
    ppermute x1, waiting for transfers between devices, on_device(): other_squares = lax.ppermute(squares, 'col', swap)  24.4 us
    pallas_call x1, Pallas kernels, slot_attention(): pl.pallas_call(partial(slot_kernel, ns=ns, heads=heads, qpk=qpk), grid_sp...  19.7 us
    ppermute x3, waiting for transfers between devices, seq_merge(): lax.ppermute(send_values.astype(jnp.bfloat16), 'seq', pairs)  14.3 us
    dot_general x3, matrix products, on_device(): jnp.dot(gathered, matrix, preferred_element_type=jnp.float32)  8.8 us
    ppermute x2, waiting for transfers between devices, pair_scatter(): got = lax.ppermute(send, axis_name, [(0, 1), (1, 0)])  7.63 us
    ppermute x3, starting transfers between devices, seq_merge(): got_stats = lax.ppermute(send_stats, 'seq', pairs)  6.64 us
    dot_general x1, matrix products, on_device(): jnp.dot(piece_rows.reshape(n_row * per * step_count, -1), wo, preferred_e...  5.88 us
  transfers between devices with their start and end apart: 13, of which 11 were waited for; matrix products, arithmetic and copies ran while one was open for 5% of the time, Pallas kernels for 0%

profile of v13, /device:TPU:0, one launch (start us, length us, event | category | flops | bytes accessed | tf_op | source)
XLA Modules:
  0.0 172.3 jit_solution(8887688232217766413)
XLA Ops:
  0.7 3.5 %reshape.797 = bf16[256,2560]{1,0:T(8,128)(2,1)} reshape(bf16[64,4,2560]{2,1,0:T(4,128)(2,1)} %param.11) | data formatting | bytes 2621440 | tf_op jit(solution)/shard_map/reshape | solution.py:317
  4.2 2.9 %collective-permute-start = (bf16[256,2560]{1,0:T(8,128)(2,1)}, bf16[256,2560]{1,0:T(8,128)(2,1)}, u32[]{:S(2)}, u32[]{:S(2)}) collective-permute-start(bf16[256,2560]{1,0:T(8,128)(2,1)} %reshape.797), channel_id=1, source_target_pairs={{0,8},{8,0},{1,9},{9,1},{2,10},{10,2},{3,11},{11,3},{4,12},{12,4},... | collective-permute-start | bytes 3932168 | tf_op jit(solution)/shard_map/ppermute | solution.py:320
  7.1 2.1 %multiply_reduce_fusion = f32[64,4]{1,0:T(8,128)S(1)} fusion(bf16[64,4,2560]{2,1,0:T(4,128)(2,1)} %param.11), kind=kLoop, calls=%fused_computation.9 | loop fusion | flops 1965824 | bytes 1311744 | tf_op jit(solution)/shard_map/reduce_sum | solution.py:322
  9.3 2.5 %psum.7 = f32[256]{0:T(256)S(1)} all-reduce(f32[256]{0:T(256)S(1)} %reduce_sum.21), channel_id=1, replica_groups=mesh['row'=2,'col'=2,'seq'=8] {'row'}, use_global_device_ids=true, to_apply=%region_1.0 | all-reduce | flops 256 | bytes 2048 | tf_op jit(solution)/shard_map/psum | solution.py:322
  11.8 24.4 %collective-permute-done.1 = f32[256]{0:T(256)S(1)} collective-permute-done((f32[256]{0:T(256)S(1)}, f32[256]{0:T(256)S(1)}, u32[]{:S(2)}, u32[]{:S(2)}) %collective-permute-start.1) | collective-permute-done | bytes 1056 | tf_op jit(solution)/shard_map/ppermute | solution.py:323
  36.3 2.8 %multiply_convert_fusion.1 = (bf16[256,2560]{1,0:T(8,128)(2,1)S(1)}, bf16[256,2560]{1,0:T(8,128)(2,1)S(1)}) fusion(f32[2560]{0:T(1024)S(1)} %copy-done.5, f32[256]{0:T(256)S(1)} %get-tuple-element.49, bf16[256,2560]{1,0:T(8,128)(2,1)} %reshape.797, bf16[256,2560]{1,0:T(8,128)(2,1)} %collective-permute-done, pred[]{:T(512)S(6)} %eq.15, ...), kind=kLoop, calls=%fused_computation.8 | loop fusion | flops 6553600 | bytes 5255169 | tf_op jit(solution)/shard_map/convert_element_type | solution.py:327
  39.1 1.5 convolution_convert_fusion.2
  40.7 1.5 convolution_convert_fusion.1
  42.2 0.4 slice-done.1
  42.6 0.8 slice-done.2
  43.4 5.8 %convolution_convert_fusion = bf16[512,2048]{1,0:T(8,128)(2,1)S(1)} fusion(bf16[2560,2048]{1,0:T(8,128)(2,1)S(1)} %bitcast.165, bf16[256,2560]{1,0:T(8,128)(2,1)S(1)} %get-tuple-element.32, bf16[256,2560]{1,0:T(8,128)(2,1)S(1)} %get-tuple-element.31), kind=kOutput, calls=%fused_computation.5 | convolution fusion | flops 5375000576 | bytes 15204352 | tf_op jit(solution)/shard_map/dot_general | solution.py:342
  49.2 0.3 pad_maximum_fusion
  49.5 1.6 copy-done.2
  51.1 1.3 constant_dynamic-slice_fusion.2
  52.6 0.5 multiply_cosine_fusion
  53.2 2.9 %collective-permute-done.2 = bf16[1,256,3072]{2,1,0:T(8,128)(2,1)S(1)} collective-permute-done((bf16[1,256,3072]{2,1,0:T(8,128)(2,1)}, bf16[1,256,3072]{2,1,0:T(8,128)(2,1)S(1)}, u32[]{:S(2)}, u32[]{:S(2)}) %collective-permute-start.2) | collective-permute-done | bytes 1572896 | tf_op jit(solution)/shard_map/ppermute | solution.py:237
  56.0 1.9 %add_bitcast_fusion = f32[32,8,24,128]{3,1,2,0:T(8,128)S(1)} fusion(bf16[1,256,3072]{2,1,0:T(8,128)(2,1)S(1)} %collective-permute-done.2, bf16[2,256,3072]{2,1,0:T(8,128)(2,1)} %copy-done.2, s32[]{:T(128)S(6)} %select_n.176), kind=kLoop, calls=%fused_computation.4 | loop fusion | flops 2359296 | bytes 6291460
  58.0 0.6 copy.125
  58.7 0.4 add_convert_fusion.1
  59.1 0.8 subtract_convert_fusion
  59.9 1.4 pad_maximum_fusion.2
  61.3 0.5 copy.109
  62.0 1.3 fusion.7
  63.3 0.5 copy.89
  63.8 0.2 select_reduce_fusion
  64.0 0.2 fusion.11
  64.2 19.7 %shard_map.130 = (f32[64,64,1]{2,1,0:T(8,128)}, f32[64,64,1]{2,1,0:T(8,128)}, f32[64,64,128]{2,1,0:T(8,128)}) custom-call(s32[50]{0:T(128)} %req_ref.1, s32[64]{0:T(128)} %len_ref.1, s32[50]{0:T(128)} %blk_ref.1, bf16[64,64,128]{2,1,0:T(8,128)(2,1)} %bitcast.136, bf16[50,128,512]{2,1,0:T(8,128)(2,1)} %k_ref.1, bf16[50,128,512]{2,1,0:T(8,128)(2,1)} %v_ref.1), custom_call_target="tpu_custom_call" | custom-call | tf_op jit(solution)/shard_map/pallas_call | solution.py:209
  83.9 2.4 %reduce.1 = f32[64,64]{1,0:T(8,128)S(1)} reduce(f32[64,64,1]{2,1,0:T(8,128)} %get-tuple-element.7, f32[]{:T(128)} %constant.102), dimensions={2}, to_apply=%get-tuple-element.7.reduce_sub_computation | reduce | bytes 32772 | tf_op jit(solution)/shard_map/pallas_call | solution.py:209
  86.2 0.6 reduce.2
  86.9 1.8 %collective-permute-start.3 = (f32[2,2,2,1,8,64]{5,4,3,2,1,0:T(8,128)S(1)}, f32[2,2,2,1,8,64]{5,4,3,2,1,0:T(8,128)S(1)}, u32[]{:S(2)}, u32[]{:S(2)}) collective-permute-start(f32[2,2,2,1,8,64]{5,4,3,2,1,0:T(8,128)S(1)} %get-tuple-element.40), channel_id=1, source_target_pairs={{0,1},{1,0},{2,3},{3,2},{4,5},{5,4},{6,7},{7,6},{8,9},{9,8},{10,11... | collective-permute-start | bytes 49160 | tf_op jit(solution)/shard_map/ppermute | solution.py:277
  88.7 1.3 dynamic-slice_convert_fusion
  90.0 0.5 copy.96
  90.5 0.3 collective-permute-start.4
  90.9 1.9 %collective-permute-start.5 = (f32[2,2,1,1,8,64]{5,4,3,2,1,0:T(8,128)S(1)}, f32[2,2,1,1,8,64]{5,4,3,2,1,0:T(8,128)S(1)}, u32[]{:S(2)}, u32[]{:S(2)}) collective-permute-start(f32[2,2,1,1,8,64]{5,4,3,2,1,0:T(8,128)S(1)} %get-tuple-element.44), channel_id=1, source_target_pairs={{0,2},{1,3},{2,0},{3,1},{4,6},{5,7},{6,4},{7,5},{8,10},{9,11},{10,... | collective-permute-start | bytes 24584 | tf_op jit(solution)/shard_map/ppermute | solution.py:277
  92.8 1.9 %collective-permute-done.5 = f32[2,2,1,1,8,64]{5,4,3,2,1,0:T(8,128)S(1)} collective-permute-done((f32[2,2,1,1,8,64]{5,4,3,2,1,0:T(8,128)S(1)}, f32[2,2,1,1,8,64]{5,4,3,2,1,0:T(8,128)S(1)}, u32[]{:S(2)}, u32[]{:S(2)}) %collective-permute-start.5) | collective-permute-done | bytes 8224 | tf_op jit(solution)/shard_map/ppermute | solution.py:277
  94.7 2.9 %collective-permute-start.7 = (f32[2,1,1,1,8,64]{5,4,3,2,1,0:T(8,128)S(1)}, f32[2,1,1,1,8,64]{5,4,3,2,1,0:T(8,128)S(1)}, u32[]{:S(2)}, u32[]{:S(2)}) collective-permute-start(f32[2,1,1,1,8,64]{5,4,3,2,1,0:T(8,128)S(1)} %get-tuple-element.48), channel_id=1, source_target_pairs={{0,4},{1,5},{2,6},{3,7},{4,0},{5,1},{6,2},{7,3},{8,12},{9,13},{10,... | collective-permute-start | bytes 12296 | tf_op jit(solution)/shard_map/ppermute | solution.py:277
  97.7 1.7 collective-permute-done.7
  99.5 4.8 %collective-permute-done.4 = bf16[2,2,1,8,64,128]{5,4,3,2,1,0:T(8,128)(2,1)S(1)} collective-permute-done((bf16[2,2,1,8,64,128]{5,4,3,2,1,0:T(8,128)(2,1)S(1)}, bf16[2,2,1,8,64,128]{5,4,3,2,1,0:T(8,128)(2,1)S(1)}, u32[]{:S(2)}, u32[]{:S(2)}) %collective-permute-start.4) | collective-permute-done | bytes 524320 | tf_op jit(solution)/shard_map/ppermute | solution.py:278
  104.3 1.8 %multiply_add_fusion = f32[2,2,1,8,64,128]{5,4,3,2,1,0:T(8,128)S(1)} fusion(bf16[2,2,1,8,64,128]{5,4,3,2,1,0:T(8,128)(2,1)S(1)} %collective-permute-done.4, f32[2,2,2,8,64,128]{5,4,3,2,1,0:T(8,128)} %bitcast.148, s32[]{:T(128)S(6)} %select_n.178, f32[2,2,8,64]{3,2,1,0:T(8,128)S(1)} %get-tuple-element.38, f32[2,2,8,64]{3,2,1,0:T(8,128)S(1)} %get-tuple-element.37), kind=kLoop, calls=%fused_computation.18 | loop fusion | flops 1048576 | bytes 2637828 | tf_op jit(solution)/shard_map/add | solution.py:287
  106.2 1.6 collective-permute-start.6
  107.8 0.2 copy.92
  108.0 0.2 copy.98
  108.2 0.2 copy.102
  108.4 0.2 convolution_multiply_fusion
  108.6 4.8 %collective-permute-done.6 = bf16[2,1,1,8,64,128]{5,4,3,2,1,0:T(8,128)(2,1)S(1)} collective-permute-done((bf16[2,1,1,8,64,128]{5,4,3,2,1,0:T(8,128)(2,1)S(1)}, bf16[2,1,1,8,64,128]{5,4,3,2,1,0:T(8,128)(2,1)S(1)}, u32[]{:S(2)}, u32[]{:S(2)}) %collective-permute-start.6) | collective-permute-done | bytes 262176 | tf_op jit(solution)/shard_map/ppermute | solution.py:278
  113.4 0.3 multiply_add_fusion.1
  113.8 2.7 %collective-permute-start.8 = (bf16[1,1,1,8,64,128]{5,4,3,2,1,0:T(8,128)(2,1)S(1)}, bf16[1,1,1,8,64,128]{5,4,3,2,1,0:T(8,128)(2,1)S(1)}, u32[]{:S(2)}, u32[]{:S(2)}) collective-permute-start(bf16[1,1,1,8,64,128]{5,4,3,2,1,0:T(8,128)(2,1)S(1)} %dynamic-slice_convert_fusion.2), channel_id=1, source_target_pairs={{0,4},{1,5},{2,6},{3,7},{4,0},{5,1},{6,2},{7,3},{8,12},{9,13},{10,... | collective-permute-start | bytes 393224 | tf_op jit(solution)/shard_map/ppermute | solution.py:278
  116.5 4.7 %collective-permute-done.8 = bf16[1,1,1,8,64,128]{5,4,3,2,1,0:T(8,128)(2,1)S(1)} collective-permute-done((bf16[1,1,1,8,64,128]{5,4,3,2,1,0:T(8,128)(2,1)S(1)}, bf16[1,1,1,8,64,128]{5,4,3,2,1,0:T(8,128)(2,1)S(1)}, u32[]{:S(2)}, u32[]{:S(2)}) %collective-permute-start.8) | collective-permute-done | bytes 131104 | tf_op jit(solution)/shard_map/ppermute | solution.py:278
  121.2 0.2 multiply_add_fusion.2
  121.4 0.3 fusion.9
  121.8 2.0 %all_gather.4 = bf16[2,8,4,2048]{3,1,2,0:T(8,128)(2,1)S(1)} all-gather(bf16[1,8,4,2048]{3,1,2,0:T(8,128)(2,1)S(1)} %convert_element_type.115), channel_id=1, replica_groups=mesh['row'=2,'col'=2,'seq'=8] {'row'}, dimensions={0}, use_global_device_ids=true | all-gather | bytes 393216 | tf_op jit(solution)/shard_map/all_gather | solution.py:406
  123.8 5.9 %fusion.2 = bf16[2,8,4,2560]{3,1,2,0:T(8,128)(2,1)S(1)} fusion(bf16[2,8,4,2048]{3,1,2,0:T(8,128)(2,1)S(1)} %all_gather.4, bf16[2048,2560]{1,0:T(8,128)(2,1)} %param.16), kind=kOutput, calls=%fused_computation.2 | convolution fusion | flops 671252480 | bytes 11075584 | tf_op jit(solution)/shard_map/dot_general | solution.py:408
  129.7 1.6 collective-permute-start.9
  131.3 4.8 %collective-permute-done.9 = bf16[1,8,4,2560]{3,1,2,0:T(8,128)(2,1)S(1)} collective-permute-done((bf16[1,8,4,2560]{3,1,2,0:T(8,128)(2,1)S(1)}, bf16[1,8,4,2560]{3,1,2,0:T(8,128)(2,1)S(1)}, u32[]{:S(2)}, u32[]{:S(2)}) %collective-permute-start.9) | collective-permute-done | bytes 163872 | tf_op jit(solution)/shard_map/ppermute | solution.py:237
  136.1 1.3 collective-permute-start.10
  137.5 8.6 %collective-permute-done.10 = bf16[1,8,4,2560]{3,1,2,0:T(8,128)(2,1)S(1)} collective-permute-done((bf16[1,8,4,2560]{3,1,2,0:T(8,128)(2,1)S(1)}, bf16[1,8,4,2560]{3,1,2,0:T(8,128)(2,1)S(1)}, u32[]{:S(2)}, u32[]{:S(2)}) %collective-permute-start.10) | collective-permute-done | bytes 163872 | tf_op jit(solution)/shard_map/ppermute | solution.py:250
  146.2 8.6 %collective-permute-done.11 = bf16[2,1,8,4,2560]{4,2,3,1,0:T(8,128)(2,1)S(1)} collective-permute-done((bf16[2,1,8,4,2560]{4,2,3,1,0:T(8,128)(2,1)S(1)}, bf16[2,1,8,4,2560]{4,2,3,1,0:T(8,128)(2,1)S(1)}, u32[]{:S(2)}, u32[]{:S(2)}) %collective-permute-start.11) | collective-permute-done | bytes 327712 | tf_op jit(solution)/shard_map/ppermute | solution.py:250
  154.9 0.3 collective-permute-start.12
  155.2 0.8 reshape_reshape.8
  156.0 0.4 pad_maximum_fusion.6
  156.4 0.8 convert_element_type.120
  157.3 12.5 %collective-permute-done.12 = bf16[2,2,1,8,4,2560]{5,3,4,1,2,0:T(8,128)(2,1)S(1)} collective-permute-done((bf16[2,2,1,8,4,2560]{5,3,4,1,2,0:T(8,128)(2,1)S(1)}, bf16[2,2,1,8,4,2560]{5,3,4,1,2,0:T(8,128)(2,1)S(1)}, u32[]{:S(2)}, u32[]{:S(2)}) %collective-permute-start.12) | collective-permute-done | bytes 655392 | tf_op jit(solution)/shard_map/ppermute | solution.py:250
  169.8 0.2 fusion.5
  170.2 2.1 %copy.105 = bf16[64,4,2560]{2,1,0:T(4,128)(2,1)} copy(bf16[64,4,2560]{2,0,1:T(8,128)(2,1)S(1)} %bitcast.135) | data formatting | bytes 2621440
  (58 shorter events, 1.8 us)
Async XLA Ops:
  0.6 38.5 %copy-start = (bf16[2560,512]{1,0:T(8,128)(2,1)S(1)}, bf16[2560,512]{1,0:T(8,128)(2,1)}, u32[]{:S(2)}) copy-start(bf16[2560,512]{1,0:T(8,128)(2,1)} %param.14) | copy-start | bytes 7864324
  0.6 35.6 %copy-start.5 = (f32[2560]{0:T(1024)S(1)}, f32[2560]{0:T(1024)}, u32[]{:S(2)}) copy-start(f32[2560]{0:T(1024)} %param.12) | copy-start | bytes 30724
  4.2 32.0 %collective-permute-start = (bf16[256,2560]{1,0:T(8,128)(2,1)}, bf16[256,2560]{1,0:T(8,128)(2,1)}, u32[]{:S(2)}, u32[]{:S(2)}) collective-permute-start(bf16[256,2560]{1,0:T(8,128)(2,1)} %reshape.797), channel_id=1, source_target_pairs={{0,8},{8,0},{1,9},{9,1},{2,10},{10,2},{3,11},{11,3},{4,12},{12,4},... | collective-permute-start | bytes 3932168 | tf_op jit(solution)/shard_map/ppermute | solution.py:320
  11.8 24.4 %collective-permute-start.1 = (f32[256]{0:T(256)S(1)}, f32[256]{0:T(256)S(1)}, u32[]{:S(2)}, u32[]{:S(2)}) collective-permute-start(f32[256]{0:T(256)S(1)} %psum.7), channel_id=1, source_target_pairs={{0,8},{8,0},{1,9},{9,1},{2,10},{10,2},{3,11},{11,3},{4,12},{12,4},... | collective-permute-start | bytes 3080 | tf_op jit(solution)/shard_map/ppermute | solution.py:323
  36.3 4.4 %copy-start.7 = (bf16[2560,512]{1,0:T(8,128)(2,1)S(1)}, bf16[2560,512]{1,0:T(8,128)(2,1)}, u32[]{:S(2)}) copy-start(bf16[2560,512]{1,0:T(8,128)(2,1)} %param.15) | copy-start | bytes 7864324
  39.1 3.1 %slice-start = ((s8[10485760]{0:T(1024)(128)(4,1)}), s8[4194304]{0:T(1024)(128)(4,1)S(1)}, s32[]{:S(2)}) async-start(s8[10485760]{0:T(1024)(128)(4,1)} %bitcast.164), calls=%async_computation | async-start | bytes 8388608
  39.1 3.5 %slice-start.1 = ((s8[10485760]{0:T(1024)(128)(4,1)}), s8[4194304]{0:T(1024)(128)(4,1)S(1)}, s32[]{:S(2)}) async-start(s8[10485760]{0:T(1024)(128)(4,1)} %bitcast.164), calls=%async_computation.1 | async-start | bytes 8388608
  40.7 2.7 %slice-start.2 = ((s8[10485760]{0:T(1024)(128)(4,1)}), s8[2097152]{0:T(1024)(128)(4,1)S(1)}, s32[]{:S(2)}) async-start(s8[10485760]{0:T(1024)(128)(4,1)} %bitcast.164), calls=%async_computation.2 | async-start | bytes 4194304
  49.5 1.6 copy-start.2
  51.1 1.3 copy-start.6
  52.4 3.6 %collective-permute-start.2 = (bf16[1,256,3072]{2,1,0:T(8,128)(2,1)}, bf16[1,256,3072]{2,1,0:T(8,128)(2,1)S(1)}, u32[]{:S(2)}, u32[]{:S(2)}) collective-permute-start(bf16[1,256,3072]{2,1,0:T(8,128)(2,1)} %constant_dynamic-slice_fusion.2), channel_id=1, source_target_pairs={{0,16},{16,0},{1,17},{17,1},{2,18},{18,2},{3,19},{19,3},{4,20},{20... | collective-permute-start | bytes 4718600 | tf_op jit(solution)/shard_map/ppermute | solution.py:237
  61.8 2.4 %copy-start.3 = (bf16[64,4,4,4,128]{4,3,1,2,0:T(4,128)(2,1)}, bf16[64,4,4,4,128]{4,3,1,2,0:T(4,128)(2,1)S(1)}, u32[]{:S(2)}) copy-start(bf16[64,4,4,4,128]{4,3,1,2,0:T(4,128)(2,1)S(1)} %copy.109) | copy-start | bytes 3145732
  83.9 2.4 %copy-start.4 = (f32[64,64,1]{2,1,0:T(8,128)S(1)}, f32[64,64,1]{2,1,0:T(8,128)}, u32[]{:S(2)}) copy-start(f32[64,64,1]{2,1,0:T(8,128)} %get-tuple-element.8) | copy-start | bytes 49156
  86.9 4.0 %collective-permute-start.3 = (f32[2,2,2,1,8,64]{5,4,3,2,1,0:T(8,128)S(1)}, f32[2,2,2,1,8,64]{5,4,3,2,1,0:T(8,128)S(1)}, u32[]{:S(2)}, u32[]{:S(2)}) collective-permute-start(f32[2,2,2,1,8,64]{5,4,3,2,1,0:T(8,128)S(1)} %get-tuple-element.40), channel_id=1, source_target_pairs={{0,1},{1,0},{2,3},{3,2},{4,5},{5,4},{6,7},{7,6},{8,9},{9,8},{10,11... | collective-permute-start | bytes 49160 | tf_op jit(solution)/shard_map/ppermute | solution.py:277
  90.5 13.8 %collective-permute-start.4 = (bf16[2,2,1,8,64,128]{5,4,3,2,1,0:T(8,128)(2,1)S(1)}, bf16[2,2,1,8,64,128]{5,4,3,2,1,0:T(8,128)(2,1)S(1)}, u32[]{:S(2)}, u32[]{:S(2)}) collective-permute-start(bf16[2,2,1,8,64,128]{5,4,3,2,1,0:T(8,128)(2,1)S(1)} %dynamic-slice_convert_fusion), channel_id=1, source_target_pairs={{0,1},{1,0},{2,3},{3,2},{4,5},{5,4},{6,7},{7,6},{8,9},{9,8},{10,11... | collective-permute-start | bytes 1572872 | tf_op jit(solution)/shard_map/ppermute | solution.py:278
  90.9 3.8 %collective-permute-start.5 = (f32[2,2,1,1,8,64]{5,4,3,2,1,0:T(8,128)S(1)}, f32[2,2,1,1,8,64]{5,4,3,2,1,0:T(8,128)S(1)}, u32[]{:S(2)}, u32[]{:S(2)}) collective-permute-start(f32[2,2,1,1,8,64]{5,4,3,2,1,0:T(8,128)S(1)} %get-tuple-element.44), channel_id=1, source_target_pairs={{0,2},{1,3},{2,0},{3,1},{4,6},{5,7},{6,4},{7,5},{8,10},{9,11},{10,... | collective-permute-start | bytes 24584 | tf_op jit(solution)/shard_map/ppermute | solution.py:277
  94.7 4.6 %collective-permute-start.7 = (f32[2,1,1,1,8,64]{5,4,3,2,1,0:T(8,128)S(1)}, f32[2,1,1,1,8,64]{5,4,3,2,1,0:T(8,128)S(1)}, u32[]{:S(2)}, u32[]{:S(2)}) collective-permute-start(f32[2,1,1,1,8,64]{5,4,3,2,1,0:T(8,128)S(1)} %get-tuple-element.48), channel_id=1, source_target_pairs={{0,4},{1,5},{2,6},{3,7},{4,0},{5,1},{6,2},{7,3},{8,12},{9,13},{10,... | collective-permute-start | bytes 12296 | tf_op jit(solution)/shard_map/ppermute | solution.py:277
  106.2 7.3 %collective-permute-start.6 = (bf16[2,1,1,8,64,128]{5,4,3,2,1,0:T(8,128)(2,1)S(1)}, bf16[2,1,1,8,64,128]{5,4,3,2,1,0:T(8,128)(2,1)S(1)}, u32[]{:S(2)}, u32[]{:S(2)}) collective-permute-start(bf16[2,1,1,8,64,128]{5,4,3,2,1,0:T(8,128)(2,1)S(1)} %dynamic-slice_convert_fusion.1), channel_id=1, source_target_pairs={{0,2},{1,3},{2,0},{3,1},{4,6},{5,7},{6,4},{7,5},{8,10},{9,11},{10,... | collective-permute-start | bytes 786440 | tf_op jit(solution)/shard_map/ppermute | solution.py:278
  113.8 7.3 %collective-permute-start.8 = (bf16[1,1,1,8,64,128]{5,4,3,2,1,0:T(8,128)(2,1)S(1)}, bf16[1,1,1,8,64,128]{5,4,3,2,1,0:T(8,128)(2,1)S(1)}, u32[]{:S(2)}, u32[]{:S(2)}) collective-permute-start(bf16[1,1,1,8,64,128]{5,4,3,2,1,0:T(8,128)(2,1)S(1)} %dynamic-slice_convert_fusion.2), channel_id=1, source_target_pairs={{0,4},{1,5},{2,6},{3,7},{4,0},{5,1},{6,2},{7,3},{8,12},{9,13},{10,... | collective-permute-start | bytes 393224 | tf_op jit(solution)/shard_map/ppermute | solution.py:278
  129.7 6.3 %collective-permute-start.9 = (bf16[1,8,4,2560]{3,1,2,0:T(8,128)(2,1)S(1)}, bf16[1,8,4,2560]{3,1,2,0:T(8,128)(2,1)S(1)}, u32[]{:S(2)}, u32[]{:S(2)}) collective-permute-start(bf16[1,8,4,2560]{3,1,2,0:T(8,128)(2,1)S(1)} %constant_dynamic-slice_fusion.1), channel_id=1, source_target_pairs={{0,8},{8,0},{1,9},{9,1},{2,10},{10,2},{3,11},{11,3},{4,12},{12,4},... | collective-permute-start | bytes 491528 | tf_op jit(solution)/shard_map/ppermute | solution.py:237
  136.1 9.9 %collective-permute-start.10 = (bf16[1,8,4,2560]{3,1,2,0:T(8,128)(2,1)S(1)}, bf16[1,8,4,2560]{3,1,2,0:T(8,128)(2,1)S(1)}, u32[]{:S(2)}, u32[]{:S(2)}) collective-permute-start(bf16[1,8,4,2560]{3,1,2,0:T(8,128)(2,1)S(1)} %add_convert_fusion.2), channel_id=1, source_target_pairs={{0,4},{1,5},{2,6},{3,7},{4,0},{5,1},{6,2},{7,3},{8,12},{9,13},{10,... | collective-permute-start | bytes 491528 | tf_op jit(solution)/shard_map/ppermute | solution.py:250
  146.0 8.8 %collective-permute-start.11 = (bf16[2,1,8,4,2560]{4,2,3,1,0:T(8,128)(2,1)S(1)}, bf16[2,1,8,4,2560]{4,2,3,1,0:T(8,128)(2,1)S(1)}, u32[]{:S(2)}, u32[]{:S(2)}) collective-permute-start(bf16[2,1,8,4,2560]{4,2,3,1,0:T(8,128)(2,1)S(1)} %maximum_select_fusion.4), channel_id=1, source_target_pairs={{0,2},{1,3},{2,0},{3,1},{4,6},{5,7},{6,4},{7,5},{8,10},{9,11},{10,... | collective-permute-start | bytes 983048 | tf_op jit(solution)/shard_map/ppermute | solution.py:250
  154.9 14.9 %collective-permute-start.12 = (bf16[2,2,1,8,4,2560]{5,3,4,1,2,0:T(8,128)(2,1)S(1)}, bf16[2,2,1,8,4,2560]{5,3,4,1,2,0:T(8,128)(2,1)S(1)}, u32[]{:S(2)}, u32[]{:S(2)}) collective-permute-start(bf16[2,2,1,8,4,2560]{5,3,4,1,2,0:T(8,128)(2,1)S(1)} %maximum_select_fusion.2), channel_id=1, source_target_pairs={{0,1},{1,0},{2,3},{3,2},{4,5},{5,4},{6,7},{7,6},{8,9},{9,8},{10,11... | collective-permute-start | bytes 1966088 | tf_op jit(solution)/shard_map/ppermute | solution.py:250
  169.8 2.4 %copy-start.1 = (bf16[2560,512]{1,0:T(8,128)(2,1)S(1)}, bf16[2560,512]{1,0:T(8,128)(2,1)}, u32[]{:S(2)}) copy-start(bf16[2560,512]{1,0:T(8,128)(2,1)} %param.14) | copy-start | bytes 7864324

commit v14 on v13

--- a/solution.py
+++ b/solution.py
@@ -257,6 +257,23 @@
     return block.reshape((n * part.shape[0],) + part.shape[1:])
 
 
+def pack_message(stats, values):
+    lanes = jnp.concatenate([stats[0], stats[1]], -1)
+    high = lax.reduce_precision(lanes, exponent_bits=8, mantissa_bits=7)
+    rest = lanes - high
+    middle = lax.reduce_precision(rest, exponent_bits=8, mantissa_bits=7)
+    low = rest - middle
+    extra = jnp.stack([high, middle, low], -2).astype(jnp.bfloat16)
+    return jnp.concatenate([values.astype(jnp.bfloat16), extra], -2)
+
+
+def unpack_message(message, rows):
+    values = message[..., :rows, :].astype(jnp.float32)
+    extra = message[..., rows:, :].astype(jnp.float32)
+    lanes = extra[..., 0, :] + (extra[..., 1, :] + extra[..., 2, :])
+    return jnp.stack([lanes[..., :rows], lanes[..., rows:]], 0), values
+
+
 def seq_merge(peak, total, acc, n_seq, seq_index):
     stages = n_seq.bit_length() - 1
     assert 1 << stages == n_seq
@@ -274,10 +291,15 @@
         send_stats = lax.dynamic_index_in_dim(stats, 1 - mine, axis + 1, keepdims=True)
         keep_values = lax.dynamic_index_in_dim(values, mine, axis, keepdims=True)
         send_values = lax.dynamic_index_in_dim(values, 1 - mine, axis, keepdims=True)
-        got_stats = lax.ppermute(send_stats, "seq", pairs)
-        got_values = lax.ppermute(send_values.astype(jnp.bfloat16), "seq", pairs).astype(
-            jnp.float32
-        )
+        if 2 * rest[-1] == values.shape[-1]:
+            got_stats, got_values = unpack_message(
+                lax.ppermute(pack_message(send_stats, send_values), "seq", pairs), rest[-1]
+            )
+        else:
+            got_stats = lax.ppermute(send_stats, "seq", pairs)
+            got_values = lax.ppermute(send_values.astype(jnp.bfloat16), "seq", pairs).astype(
+                jnp.float32
+            )
         top = jnp.maximum(keep_stats[0], got_stats[0])
         keep_factor = jnp.exp(keep_stats[0] - top)
         got_factor = jnp.exp(got_stats[0] - top)

time: 173 us -> 195 us (1.13)
  other arithmetic: 17.5 us -> 34.1 us
  local copies, waits for them, and re-layouts: 16.2 us -> 29.2 us
  waiting for transfers between devices: 79.7 us -> 74.5 us
  starting transfers between devices: 17.4 us -> 12.8 us
    ppermute x6 -> x3, waiting for transfers between devices: 17.9 us -> 11.1 us  [seq_merge(): lax.ppermute(pack_message(send_stats, send_values), 'seq', pairs)]
    ppermute x6 -> x3, starting transfers between devices: 11.2 us -> 6.16 us  [seq_merge(): lax.ppermute(pack_message(send_stats, send_values), 'seq', pairs)]
    mul x0 -> x6, local copies, waits for them, and re-layouts: none -> 3.92 us  [the longest x3 2.32 us: seq_merge(): got_values * got_factor[..., None]]
    dynamic_slice x0 -> x2, local copies, waits for them, and re-layouts: none -> 3.63 us  [the longest x1 2.32 us: seq_merge(): keep_values = lax.dynamic_index_in_dim(values, mine, axis, keepdims=True)]
    add x3, other arithmetic: 2.36 us -> 4.92 us  [seq_merge(): keep_values * keep_factor[..., None] + got_values * got_factor[..., None]]
    concatenate x0 -> x3, other arithmetic: none -> 2.38 us  [pack_message(): return jnp.concatenate([values.astype(jnp.bfloat16), extra], -2)]
    reduce_sum x0 -> x1, other arithmetic: none -> 2.09 us  [fresh_part(): running_totals = jnp.sum(weights, -1)]
    unnamed x24 -> x37, local copies, waits for them, and re-layouts: 5.49 us -> 6.73 us
  transfers between devices with their start and end apart: 13 -> 10, of which waited for: 11 -> 8; matrix products, arithmetic and copies ran while one was open for 5% -> 10% of each run, Pallas kernels for 0% -> 0%
where the time goes in v14:
time: 195 us; the launch traced here: 194 us
  waiting for transfers between devices  74.5 us (38%)
  other arithmetic  34.1 us (17%)
  local copies, waits for them, and re-layouts  29.2 us (15%)
  Pallas kernels  19.6 us (10%)
  matrix products  18.1 us (9%)
  starting transfers between devices  12.8 us (7%)
  blocking collectives  4.46 us (2%)
    ppermute x3, waiting for transfers between devices, doubling_gather(): got = lax.ppermute(block, axis_name, pairs)  31.3 us
    ppermute x1, waiting for transfers between devices, on_device(): other_squares = lax.ppermute(squares, 'col', swap)  24.4 us
    pallas_call x1, Pallas kernels, slot_attention(): pl.pallas_call(partial(slot_kernel, ns=ns, heads=heads, qpk=qpk), grid_sp...  19.6 us
    ppermute x3, waiting for transfers between devices, seq_merge(): lax.ppermute(pack_message(send_stats, send_values), 'seq', pairs)  11.1 us
    dot_general x3, matrix products, on_device(): jnp.dot(gathered, matrix, preferred_element_type=jnp.float32)  8.8 us
    ppermute x2, waiting for transfers between devices, pair_scatter(): got = lax.ppermute(send, axis_name, [(0, 1), (1, 0)])  7.69 us
    unnamed x37, local copies, waits for them, and re-layouts  6.73 us
    ppermute x3, starting transfers between devices, seq_merge(): lax.ppermute(pack_message(send_stats, send_values), 'seq', pairs)  6.16 us
  transfers between devices with their start and end apart: 10, of which 8 were waited for; matrix products, arithmetic and copies ran while one was open for 10% of the time, Pallas kernels for 0%

profile of v14, /device:TPU:0, one launch (start us, length us, event | category | flops | bytes accessed | tf_op | source)
XLA Modules:
  0.0 193.9 jit_solution(13953277156401543896)
XLA Ops:
  0.7 3.5 %reshape.1689 = bf16[256,2560]{1,0:T(8,128)(2,1)} reshape(bf16[64,4,2560]{2,1,0:T(4,128)(2,1)} %param.11) | data formatting | bytes 2621440 | tf_op jit(solution)/shard_map/reshape | solution.py:339
  4.2 2.9 %collective-permute-start = (bf16[256,2560]{1,0:T(8,128)(2,1)}, bf16[256,2560]{1,0:T(8,128)(2,1)}, u32[]{:S(2)}, u32[]{:S(2)}) collective-permute-start(bf16[256,2560]{1,0:T(8,128)(2,1)} %reshape.1689), channel_id=1, source_target_pairs={{0,8},{8,0},{1,9},{9,1},{2,10},{10,2},{3,11},{11,3},{4,12},{12,4},... | collective-permute-start | bytes 3932168 | tf_op jit(solution)/shard_map/ppermute | solution.py:342
  7.1 2.1 %multiply_reduce_fusion = f32[64,4]{1,0:T(8,128)S(1)} fusion(bf16[64,4,2560]{2,1,0:T(4,128)(2,1)} %param.11), kind=kLoop, calls=%fused_computation.9 | loop fusion | flops 1965824 | bytes 1311744 | tf_op jit(solution)/shard_map/reduce_sum | solution.py:344
  9.3 2.5 %psum.7 = f32[256]{0:T(256)S(1)} all-reduce(f32[256]{0:T(256)S(1)} %reduce_sum.21), channel_id=1, replica_groups=mesh['row'=2,'col'=2,'seq'=8] {'row'}, use_global_device_ids=true, to_apply=%region_1.0 | all-reduce | flops 256 | bytes 2048 | tf_op jit(solution)/shard_map/psum | solution.py:344
  11.8 24.4 %collective-permute-done.1 = f32[256]{0:T(256)S(1)} collective-permute-done((f32[256]{0:T(256)S(1)}, f32[256]{0:T(256)S(1)}, u32[]{:S(2)}, u32[]{:S(2)}) %collective-permute-start.1) | collective-permute-done | bytes 1056 | tf_op jit(solution)/shard_map/ppermute | solution.py:345
  36.3 2.8 %multiply_convert_fusion.1 = (bf16[256,2560]{1,0:T(8,128)(2,1)S(1)}, bf16[256,2560]{1,0:T(8,128)(2,1)S(1)}) fusion(f32[2560]{0:T(1024)S(1)} %copy-done.11, f32[256]{0:T(256)S(1)} %get-tuple-element.58, bf16[256,2560]{1,0:T(8,128)(2,1)} %reshape.1689, bf16[256,2560]{1,0:T(8,128)(2,1)} %collective-permute-done, pred[]{:T(512)S(6)} %eq.15, ...), kind=kLoop, calls=%fused_computation.8 | loop fusion | flops 6553600 | bytes 5255169 | tf_op jit(solution)/shard_map/convert_element_type | solution.py:349
  39.1 1.5 convolution_convert_fusion.2
  40.7 1.5 convolution_convert_fusion.1
  42.6 0.8 slice-done.2
  43.4 5.8 %convolution_convert_fusion = bf16[512,2048]{1,0:T(8,128)(2,1)S(1)} fusion(bf16[2560,2048]{1,0:T(8,128)(2,1)S(1)} %bitcast.233, bf16[256,2560]{1,0:T(8,128)(2,1)S(1)} %get-tuple-element.32, bf16[256,2560]{1,0:T(8,128)(2,1)S(1)} %get-tuple-element.31), kind=kOutput, calls=%fused_computation.5 | convolution fusion | flops 5375000576 | bytes 15204352 | tf_op jit(solution)/shard_map/dot_general | solution.py:364
  49.5 1.3 constant_dynamic-slice_fusion.4
  51.5 3.0 %collective-permute-done.2 = bf16[1,256,3072]{2,1,0:T(8,128)(2,1)} collective-permute-done((bf16[1,256,3072]{2,1,0:T(8,128)(2,1)}, bf16[1,256,3072]{2,1,0:T(8,128)(2,1)}, u32[]{:S(2)}, u32[]{:S(2)}) %collective-permute-start.2) | collective-permute-done | bytes 1572896 | tf_op jit(solution)/shard_map/ppermute | solution.py:237
  54.5 1.9 add_bitcast_fusion
  57.1 0.8 subtract_convert_fusion
  57.8 1.4 pad_maximum_fusion.2
  59.3 1.4 copy.157
  60.7 19.6 %shard_map.130 = (f32[64,64,1]{2,1,0:T(8,128)}, f32[64,64,1]{2,1,0:T(8,128)}, f32[64,64,128]{2,1,0:T(8,128)}) custom-call(s32[50]{0:T(128)} %req_ref.1, s32[64]{0:T(128)} %len_ref.1, s32[50]{0:T(128)} %blk_ref.1, bf16[64,64,128]{2,1,0:T(8,128)(2,1)} %bitcast.193, bf16[50,128,512]{2,1,0:T(8,128)(2,1)} %k_ref.1, bf16[50,128,512]{2,1,0:T(8,128)(2,1)} %v_ref.1), custom_call_target="tpu_custom_call" | custom-call | tf_op jit(solution)/shard_map/pallas_call | solution.py:209
  80.3 2.2 %reduce.1 = f32[64,64]{1,0:T(8,128)S(1)} reduce(f32[64,64,1]{2,1,0:T(8,128)} %get-tuple-element.7, f32[]{:T(128)} %constant.102), dimensions={2}, to_apply=%get-tuple-element.7.reduce_sub_computation | reduce | bytes 32772 | tf_op jit(solution)/shard_map/pallas_call | solution.py:209
  82.5 2.2 %reduce.2 = f32[64,64]{1,0:T(8,128)S(1)} reduce(f32[64,64,1]{2,1,0:T(8,128)} %get-tuple-element.8, f32[]{:T(128)} %constant.102), dimensions={2}, to_apply=%get-tuple-element.8.reduce_sub_computation | reduce | bytes 32772 | tf_op jit(solution)/shard_map/pallas_call | solution.py:209
  84.8 1.3 constant_dynamic-slice_fusion.2
  86.5 0.9 pad_maximum_fusion.6
  87.5 1.8 collective-permute-start.3
  89.8 2.3 %constant_dynamic-slice_fusion.3 = f32[2,2,1,8,64,128]{5,4,3,2,1,0:T(8,128)} fusion(f32[2,2,2,8,64,128]{5,4,3,2,1,0:T(8,128)} %bitcast.205, s32[]{:T(128)S(6)} %select_n.178), kind=kLoop, calls=%fused_computation.129 | loop fusion | bytes 2097156 | tf_op jit(solution)/shard_map/jit(dynamic_index_in_dim)/dynamic_slice | solution.py:292
  92.1 10.2 %collective-permute-done.3 = bf16[2,2,1,8,67,128]{5,3,4,2,1,0:T(8,128)(2,1)} collective-permute-done((bf16[2,2,1,8,67,128]{5,3,4,2,1,0:T(8,128)(2,1)}, bf16[2,2,1,8,67,128]{5,3,4,2,1,0:T(8,128)(2,1)}, u32[]{:S(2)}, u32[]{:S(2)}) %collective-permute-start.3) | collective-permute-done | bytes 548896 | tf_op jit(solution)/shard_map/ppermute | solution.py:296
  102.3 0.7 slice_convert_fusion.1
  103.1 0.6 fusion.46
  105.0 0.8 copy.119
  105.9 2.3 %fusion.10 = f32[2,2,1,8,64,128]{5,3,4,2,1,0:T(8,128)S(1)} fusion(f32[2,2,1,8,64,128]{5,4,3,2,1,0:T(8,128)} %constant_dynamic-slice_fusion.3, bf16[2,2,1,8,67,128]{5,3,4,2,1,0:T(8,128)(2,1)} %collective-permute-done.3, f32[2,2,8,64]{2,3,1,0:T(8,128)S(1)} %copy.119, f32[2,2,8,64]{2,3,1,0:T(8,128)S(1)} %copy.118), kind=kLoop, calls=%fused_computation.24 | loop fusion | flops 1048576 | bytes 2637824 | tf_op jit(solution)/shard_map/add | solution.py:309
  108.2 1.0 copy-done.2
  109.3 0.8 pad_maximum_fusion.7
  110.1 1.8 collective-permute-start.4
  111.9 1.4 add_convert_fusion.1
  113.2 0.7 copy-done.3
  114.1 2.9 %fusion.11 = f32[8,4,4,4,4]{3,4,2,1,0:T(4,128)} fusion(bf16[64,4,4,4,128]{4,3,1,2,0:T(4,128)(2,1)} %copy.157, s32[]{:T(128)S(6)} %select_n.184, bf16[64,4,4,64]{3,1,2,0:T(4,128)(2,1)S(1)} %copy.135, bf16[64,4,4,64]{3,1,2,0:T(4,128)(2,1)S(1)} %copy.136), kind=kOutput, calls=%fused_computation.47 | convolution fusion | flops 589824 | bytes 402432 | tf_op jit(solution)/shard_map/rsagh,ruah->rasgu/dot_general | solution.py:89
  117.1 1.4 copy.137
  118.5 1.4 select_reduce_fusion
  119.9 0.7 slice_convert_fusion.2
  120.7 0.6 fusion.57
  121.3 1.4 copy.125
  122.7 1.4 copy.126
  124.2 1.4 multiply_add_fusion
  125.7 0.7 pad_maximum_fusion.9
  126.4 2.6 %collective-permute-start.5 = (bf16[1,1,1,8,67,128]{5,3,4,2,1,0:T(8,128)(2,1)}, bf16[1,1,1,8,67,128]{5,3,4,2,1,0:T(8,128)(2,1)}, u32[]{:S(2)}, u32[]{:S(2)}) collective-permute-start(bf16[1,1,1,8,67,128]{5,3,4,2,1,0:T(8,128)(2,1)} %pad_maximum_fusion.9), channel_id=1, source_target_pairs={{0,4},{1,5},{2,6},{3,7},{4,0},{5,1},{6,2},{7,3},{8,12},{9,13},{10,... | collective-permute-start | bytes 411656 | tf_op jit(solution)/shard_map/ppermute | solution.py:296
  129.0 2.1 %fusion.13 = (f32[8,4,4,4]{0,3,2,1:T(4,128)}, bf16[8,4,4,4,4]{0,4,3,2,1:T(4,128)(2,1)}) fusion(f32[8,4,4,4,4]{0,4,3,2,1:T(4,128)S(1)} %copy.137, f32[8,4,4,4]{0,3,2,1:T(4,128)} %select_reduce_fusion, pred[4,4]{1,0:T(4,128)(4,1)} %iota_compare_fusion), kind=kLoop, calls=%fused_computation.53 | loop fusion | flops 9728 | bytes 16400 | tf_op jit(solution)/shard_map/reduce_sum | solution.py:99
  131.1 0.8 slice.315
  131.9 1.3 copy.144
  133.3 0.8 constant_dynamic-slice_fusion
  134.0 0.9 collective-permute-done.5
  135.0 0.7 slice_convert_fusion.3
  136.1 1.2 multiply_add_fusion.1
  137.4 0.8 multiply_add_fusion.2
  139.3 2.0 %all_gather.4 = bf16[2,8,4,2048]{3,1,2,0:T(8,128)(2,1)S(1)} all-gather(bf16[1,8,4,2048]{3,1,2,0:T(8,128)(2,1)S(1)} %convert_element_type.154), channel_id=1, replica_groups=mesh['row'=2,'col'=2,'seq'=8] {'row'}, dimensions={0}, use_global_device_ids=true | all-gather | bytes 393216 | tf_op jit(solution)/shard_map/all_gather | solution.py:428
  141.3 5.9 %fusion.2 = bf16[2,8,4,2560]{3,1,2,0:T(8,128)(2,1)S(1)} fusion(bf16[2,8,4,2048]{3,1,2,0:T(8,128)(2,1)S(1)} %all_gather.4, bf16[2048,2560]{1,0:T(8,128)(2,1)} %param.16), kind=kOutput, calls=%fused_computation.2 | convolution fusion | flops 671252480 | bytes 11075584 | tf_op jit(solution)/shard_map/dot_general | solution.py:430
  147.2 1.6 collective-permute-start.6
  148.8 4.7 %collective-permute-done.6 = bf16[1,8,4,2560]{3,1,2,0:T(8,128)(2,1)S(1)} collective-permute-done((bf16[1,8,4,2560]{3,1,2,0:T(8,128)(2,1)S(1)}, bf16[1,8,4,2560]{3,1,2,0:T(8,128)(2,1)S(1)}, u32[]{:S(2)}, u32[]{:S(2)}) %collective-permute-start.6) | collective-permute-done | bytes 163872 | tf_op jit(solution)/shard_map/ppermute | solution.py:237
  154.0 9.5 %collective-permute-done.7 = bf16[1,8,4,2560]{3,1,2,0:T(8,128)(2,1)S(1)} collective-permute-done((bf16[1,8,4,2560]{3,1,2,0:T(8,128)(2,1)S(1)}, bf16[1,8,4,2560]{3,1,2,0:T(8,128)(2,1)S(1)}, u32[]{:S(2)}, u32[]{:S(2)}) %collective-permute-start.7) | collective-permute-done | bytes 163872 | tf_op jit(solution)/shard_map/ppermute | solution.py:250
  163.7 9.6 %collective-permute-done.8 = bf16[2,1,8,4,2560]{4,2,3,1,0:T(8,128)(2,1)S(1)} collective-permute-done((bf16[2,1,8,4,2560]{4,2,3,1,0:T(8,128)(2,1)S(1)}, bf16[2,1,8,4,2560]{4,2,3,1,0:T(8,128)(2,1)S(1)}, u32[]{:S(2)}, u32[]{:S(2)}) %collective-permute-start.8) | collective-permute-done | bytes 327712 | tf_op jit(solution)/shard_map/ppermute | solution.py:250
  173.3 1.6 collective-permute-start.9
  174.9 0.8 reshape_reshape.8
  176.1 0.8 convert_element_type.159
  177.0 12.2 %collective-permute-done.9 = bf16[2,2,1,8,4,2560]{5,3,4,1,2,0:T(8,128)(2,1)S(1)} collective-permute-done((bf16[2,2,1,8,4,2560]{5,3,4,1,2,0:T(8,128)(2,1)S(1)}, bf16[2,2,1,8,4,2560]{5,3,4,1,2,0:T(8,128)(2,1)S(1)}, u32[]{:S(2)}, u32[]{:S(2)}) %collective-permute-start.9) | collective-permute-done | bytes 655392 | tf_op jit(solution)/shard_map/ppermute | solution.py:250
  189.2 0.8 copy-done.8
  190.0 1.7 fusion.5
  191.8 2.1 %copy.153 = bf16[64,4,2560]{2,1,0:T(4,128)(2,1)} copy(bf16[64,4,2560]{2,0,1:T(8,128)(2,1)S(1)} %bitcast.192) | data formatting | bytes 2621440
  (90 shorter events, 8.0 us)
Async XLA Ops:
  0.6 38.5 %copy-start = (bf16[2560,512]{1,0:T(8,128)(2,1)S(1)}, bf16[2560,512]{1,0:T(8,128)(2,1)}, u32[]{:S(2)}) copy-start(bf16[2560,512]{1,0:T(8,128)(2,1)} %param.14) | copy-start | bytes 7864324
  0.6 35.6 %copy-start.11 = (f32[2560]{0:T(1024)S(1)}, f32[2560]{0:T(1024)}, u32[]{:S(2)}) copy-start(f32[2560]{0:T(1024)} %param.12) | copy-start | bytes 30724
  4.2 32.0 %collective-permute-start = (bf16[256,2560]{1,0:T(8,128)(2,1)}, bf16[256,2560]{1,0:T(8,128)(2,1)}, u32[]{:S(2)}, u32[]{:S(2)}) collective-permute-start(bf16[256,2560]{1,0:T(8,128)(2,1)} %reshape.1689), channel_id=1, source_target_pairs={{0,8},{8,0},{1,9},{9,1},{2,10},{10,2},{3,11},{11,3},{4,12},{12,4},... | collective-permute-start | bytes 3932168 | tf_op jit(solution)/shard_map/ppermute | solution.py:342
  11.8 24.4 %collective-permute-start.1 = (f32[256]{0:T(256)S(1)}, f32[256]{0:T(256)S(1)}, u32[]{:S(2)}, u32[]{:S(2)}) collective-permute-start(f32[256]{0:T(256)S(1)} %psum.7), channel_id=1, source_target_pairs={{0,8},{8,0},{1,9},{9,1},{2,10},{10,2},{3,11},{11,3},{4,12},{12,4},... | collective-permute-start | bytes 3080 | tf_op jit(solution)/shard_map/ppermute | solution.py:345
  36.3 4.4 %copy-start.13 = (bf16[2560,512]{1,0:T(8,128)(2,1)S(1)}, bf16[2560,512]{1,0:T(8,128)(2,1)}, u32[]{:S(2)}) copy-start(bf16[2560,512]{1,0:T(8,128)(2,1)} %param.15) | copy-start | bytes 7864324
  39.1 3.1 %slice-start = ((s8[10485760]{0:T(1024)(128)(4,1)}), s8[4194304]{0:T(1024)(128)(4,1)S(1)}, s32[]{:S(2)}) async-start(s8[10485760]{0:T(1024)(128)(4,1)} %bitcast.232), calls=%async_computation | async-start | bytes 8388608
  39.1 3.5 %slice-start.1 = ((s8[10485760]{0:T(1024)(128)(4,1)}), s8[4194304]{0:T(1024)(128)(4,1)S(1)}, s32[]{:S(2)}) async-start(s8[10485760]{0:T(1024)(128)(4,1)} %bitcast.232), calls=%async_computation.1 | async-start | bytes 8388608
  40.7 2.7 %slice-start.2 = ((s8[10485760]{0:T(1024)(128)(4,1)}), s8[2097152]{0:T(1024)(128)(4,1)S(1)}, s32[]{:S(2)}) async-start(s8[10485760]{0:T(1024)(128)(4,1)} %bitcast.232), calls=%async_computation.2 | async-start | bytes 4194304
  49.5 1.3 copy-start.12
  50.8 3.8 %collective-permute-start.2 = (bf16[1,256,3072]{2,1,0:T(8,128)(2,1)}, bf16[1,256,3072]{2,1,0:T(8,128)(2,1)}, u32[]{:S(2)}, u32[]{:S(2)}) collective-permute-start(bf16[1,256,3072]{2,1,0:T(8,128)(2,1)} %constant_dynamic-slice_fusion.4), channel_id=1, source_target_pairs={{0,16},{16,0},{1,17},{17,1},{2,18},{18,2},{3,19},{19,3},{4,20},{20... | collective-permute-start | bytes 4718600 | tf_op jit(solution)/shard_map/ppermute | solution.py:237
  51.5 5.5 %copy-start.7 = (f32[256,64]{1,0:T(8,128)}, f32[256,64]{1,0:T(8,128)S(1)}, u32[]{:S(2)}) copy-start(f32[256,64]{1,0:T(8,128)S(1)} %get-tuple-element.61) | copy-start | bytes 196612
  87.5 14.8 %collective-permute-start.3 = (bf16[2,2,1,8,67,128]{5,3,4,2,1,0:T(8,128)(2,1)}, bf16[2,2,1,8,67,128]{5,3,4,2,1,0:T(8,128)(2,1)}, u32[]{:S(2)}, u32[]{:S(2)}) collective-permute-start(bf16[2,2,1,8,67,128]{5,3,4,2,1,0:T(8,128)(2,1)} %pad_maximum_fusion.6), channel_id=1, source_target_pairs={{0,1},{1,0},{2,3},{3,2},{4,5},{5,4},{6,7},{7,6},{8,9},{9,8},{10,11... | collective-permute-start | bytes 1646600 | tf_op jit(solution)/shard_map/ppermute | solution.py:296
  105.9 3.3 %copy-start.9 = (f32[2,8,1,64]{3,1,0,2:T(8,128)S(1)}, f32[2,8,1,64]{3,1,0,2:T(8,128)}, u32[]{:S(2)}) copy-start(f32[2,8,1,64]{3,1,0,2:T(8,128)} %slice_bitcast_fusion.5) | copy-start | bytes 12292
  105.9 3.3 %copy-start.10 = (f32[2,8,1,64]{3,1,0,2:T(8,128)S(1)}, f32[2,8,1,64]{3,1,0,2:T(8,128)}, u32[]{:S(2)}) copy-start(f32[2,8,1,64]{3,1,0,2:T(8,128)} %slice_bitcast_fusion.6) | copy-start | bytes 12292
  108.2 1.0 copy-start.2
  110.1 9.8 %collective-permute-start.4 = (bf16[2,1,1,8,67,128]{5,3,4,2,1,0:T(8,128)(2,1)}, bf16[2,1,1,8,67,128]{5,3,4,2,1,0:T(8,128)(2,1)}, u32[]{:S(2)}, u32[]{:S(2)}) collective-permute-start(bf16[2,1,1,8,67,128]{5,3,4,2,1,0:T(8,128)(2,1)} %pad_maximum_fusion.7), channel_id=1, source_target_pairs={{0,2},{1,3},{2,0},{3,1},{4,6},{5,7},{6,4},{7,5},{8,10},{9,11},{10,... | collective-permute-start | bytes 823304 | tf_op jit(solution)/shard_map/ppermute | solution.py:296
  113.2 0.7 copy-start.3
  125.6 6.3 %copy-start.5 = (f32[2,1,1,8,64,128]{5,3,4,2,1,0:T(8,128)}, f32[2,1,1,8,64,128]{5,3,4,2,1,0:T(8,128)S(1)}, u32[]{:S(2)}) copy-start(f32[2,1,1,8,64,128]{5,3,4,2,1,0:T(8,128)S(1)} %multiply_add_fusion) | copy-start | bytes 1572868
  126.4 8.5 %collective-permute-start.5 = (bf16[1,1,1,8,67,128]{5,3,4,2,1,0:T(8,128)(2,1)}, bf16[1,1,1,8,67,128]{5,3,4,2,1,0:T(8,128)(2,1)}, u32[]{:S(2)}, u32[]{:S(2)}) collective-permute-start(bf16[1,1,1,8,67,128]{5,3,4,2,1,0:T(8,128)(2,1)} %pad_maximum_fusion.9), channel_id=1, source_target_pairs={{0,4},{1,5},{2,6},{3,7},{4,0},{5,1},{6,2},{7,3},{8,12},{9,13},{10,... | collective-permute-start | bytes 411656 | tf_op jit(solution)/shard_map/ppermute | solution.py:296
  147.2 27.8 %copy-start.6 = (bf16[256,4,128]{2,1,0:T(4,128)(2,1)S(1)}, bf16[256,4,128]{2,1,0:T(4,128)(2,1)}, u32[]{:S(2)}) copy-start(bf16[256,4,128]{2,1,0:T(4,128)(2,1)} %slice.315) | copy-start | bytes 786436
  147.2 28.5 %copy-start.4 = (bf16[256,4,64]{2,1,0:T(4,128)(2,1)S(1)}, bf16[256,4,64]{2,1,0:T(4,128)(2,1)}, u32[]{:S(2)}) copy-start(bf16[256,4,64]{2,1,0:T(4,128)(2,1)} %copy-done.3) | copy-start | bytes 393220
  147.2 6.3 %collective-permute-start.6 = (bf16[1,8,4,2560]{3,1,2,0:T(8,128)(2,1)S(1)}, bf16[1,8,4,2560]{3,1,2,0:T(8,128)(2,1)S(1)}, u32[]{:S(2)}, u32[]{:S(2)}) collective-permute-start(bf16[1,8,4,2560]{3,1,2,0:T(8,128)(2,1)S(1)} %constant_dynamic-slice_fusion.1), channel_id=1, source_target_pairs={{0,8},{8,0},{1,9},{9,1},{2,10},{10,2},{3,11},{11,3},{4,12},{12,4},... | collective-permute-start | bytes 491528 | tf_op jit(solution)/shard_map/ppermute | solution.py:237
  153.6 9.9 %collective-permute-start.7 = (bf16[1,8,4,2560]{3,1,2,0:T(8,128)(2,1)S(1)}, bf16[1,8,4,2560]{3,1,2,0:T(8,128)(2,1)S(1)}, u32[]{:S(2)}, u32[]{:S(2)}) collective-permute-start(bf16[1,8,4,2560]{3,1,2,0:T(8,128)(2,1)S(1)} %add_convert_fusion.2), channel_id=1, source_target_pairs={{0,4},{1,5},{2,6},{3,7},{4,0},{5,1},{6,2},{7,3},{8,12},{9,13},{10,... | collective-permute-start | bytes 491528 | tf_op jit(solution)/shard_map/ppermute | solution.py:250
  163.5 9.7 %collective-permute-start.8 = (bf16[2,1,8,4,2560]{4,2,3,1,0:T(8,128)(2,1)S(1)}, bf16[2,1,8,4,2560]{4,2,3,1,0:T(8,128)(2,1)S(1)}, u32[]{:S(2)}, u32[]{:S(2)}) collective-permute-start(bf16[2,1,8,4,2560]{4,2,3,1,0:T(8,128)(2,1)S(1)} %maximum_select_fusion.4), channel_id=1, source_target_pairs={{0,2},{1,3},{2,0},{3,1},{4,6},{5,7},{6,4},{7,5},{8,10},{9,11},{10,... | collective-permute-start | bytes 983048 | tf_op jit(solution)/shard_map/ppermute | solution.py:250
  173.3 15.9 %collective-permute-start.9 = (bf16[2,2,1,8,4,2560]{5,3,4,1,2,0:T(8,128)(2,1)S(1)}, bf16[2,2,1,8,4,2560]{5,3,4,1,2,0:T(8,128)(2,1)S(1)}, u32[]{:S(2)}, u32[]{:S(2)}) collective-permute-start(bf16[2,2,1,8,4,2560]{5,3,4,1,2,0:T(8,128)(2,1)S(1)} %maximum_select_fusion.2), channel_id=1, source_target_pairs={{0,1},{1,0},{2,3},{3,2},{4,5},{5,4},{6,7},{7,6},{8,9},{9,8},{10,11... | collective-permute-start | bytes 1966088 | tf_op jit(solution)/shard_map/ppermute | solution.py:250
  189.2 0.8 copy-start.8
  190.0 3.9 %copy-start.1 = (bf16[2560,512]{1,0:T(8,128)(2,1)S(1)}, bf16[2560,512]{1,0:T(8,128)(2,1)}, u32[]{:S(2)}) copy-start(bf16[2560,512]{1,0:T(8,128)(2,1)} %param.14) | copy-start | bytes 7864324

commit v15 on v13

--- a/solution.py
+++ b/solution.py
@@ -245,7 +245,8 @@
     assert 1 << stages == n
     index = lax.axis_index(axis_name)
     block = part[None]
-    for bit in reversed(range(stages)):
+    order = [stages - 1] + list(range(stages - 1))
+    for bit in order:
         pairs = [(s, s ^ (1 << bit)) for s in range(n)]
         got = lax.ppermute(block, axis_name, pairs)
         low = ((index >> bit) & 1) == 0
@@ -253,7 +254,11 @@
             low, jnp.stack([block, got], 0), jnp.stack([got, block], 0)
         )
     block = block.reshape((2,) * stages + part.shape)
-    block = block.transpose(tuple(reversed(range(stages))) + tuple(range(stages, stages + part.ndim)))
+    axes = list(reversed(order))
+    block = block.transpose(
+        tuple(axes.index(stages - 1 - p) for p in range(stages))
+        + tuple(range(stages, stages + part.ndim))
+    )
     return block.reshape((n * part.shape[0],) + part.shape[1:])
 
 

time: 173 us -> 173 us (level)
  no operation moved by 1% of the time
where the time goes in v15:
time: 173 us; the launch traced here: 172 us
  waiting for transfers between devices  79.3 us (46%)
  Pallas kernels  19.7 us (11%)
  starting transfers between devices  17.9 us (10%)
  other arithmetic  17.5 us (10%)
  local copies, waits for them, and re-layouts  16.2 us (9%)
  matrix products  16.2 us (9%)
  blocking collectives  4.46 us (3%)
    ppermute x3, waiting for transfers between devices, doubling_gather(): got = lax.ppermute(block, axis_name, pairs)  29.3 us
    ppermute x1, waiting for transfers between devices, on_device(): other_squares = lax.ppermute(squares, 'col', swap)  24.4 us
    pallas_call x1, Pallas kernels, slot_attention(): pl.pallas_call(partial(slot_kernel, ns=ns, heads=heads, qpk=qpk), grid_sp...  19.7 us
    ppermute x3, waiting for transfers between devices, seq_merge(): lax.ppermute(send_values.astype(jnp.bfloat16), 'seq', pairs)  14.3 us
    dot_general x3, matrix products, on_device(): jnp.dot(gathered, matrix, preferred_element_type=jnp.float32)  8.8 us
    ppermute x2, waiting for transfers between devices, pair_scatter(): got = lax.ppermute(send, axis_name, [(0, 1), (1, 0)])  7.63 us
    ppermute x3, starting transfers between devices, seq_merge(): got_stats = lax.ppermute(send_stats, 'seq', pairs)  6.64 us
    dot_general x1, matrix products, on_device(): jnp.dot(piece_rows.reshape(n_row * per * step_count, -1), wo, preferred_e...  5.88 us
  transfers between devices with their start and end apart: 13, of which 11 were waited for; matrix products, arithmetic and copies ran while one was open for 5% of the time, Pallas kernels for 0%

profile of v15, /device:TPU:0, one launch (start us, length us, event | category | flops | bytes accessed | tf_op | source)
XLA Modules:
  0.0 172.3 jit_solution(8500794384433531199)
XLA Ops:
  0.7 3.5 %reshape.797 = bf16[256,2560]{1,0:T(8,128)(2,1)} reshape(bf16[64,4,2560]{2,1,0:T(4,128)(2,1)} %param.11) | data formatting | bytes 2621440 | tf_op jit(solution)/shard_map/reshape | solution.py:322
  4.2 2.9 %collective-permute-start = (bf16[256,2560]{1,0:T(8,128)(2,1)}, bf16[256,2560]{1,0:T(8,128)(2,1)}, u32[]{:S(2)}, u32[]{:S(2)}) collective-permute-start(bf16[256,2560]{1,0:T(8,128)(2,1)} %reshape.797), channel_id=1, source_target_pairs={{0,8},{8,0},{1,9},{9,1},{2,10},{10,2},{3,11},{11,3},{4,12},{12,4},... | collective-permute-start | bytes 3932168 | tf_op jit(solution)/shard_map/ppermute | solution.py:325
  7.1 2.1 %multiply_reduce_fusion = f32[64,4]{1,0:T(8,128)S(1)} fusion(bf16[64,4,2560]{2,1,0:T(4,128)(2,1)} %param.11), kind=kLoop, calls=%fused_computation.9 | loop fusion | flops 1965824 | bytes 1311744 | tf_op jit(solution)/shard_map/reduce_sum | solution.py:327
  9.3 2.5 %psum.7 = f32[256]{0:T(256)S(1)} all-reduce(f32[256]{0:T(256)S(1)} %reduce_sum.21), channel_id=1, replica_groups=mesh['row'=2,'col'=2,'seq'=8] {'row'}, use_global_device_ids=true, to_apply=%region_1.0 | all-reduce | flops 256 | bytes 2048 | tf_op jit(solution)/shard_map/psum | solution.py:327
  11.8 24.4 %collective-permute-done.1 = f32[256]{0:T(256)S(1)} collective-permute-done((f32[256]{0:T(256)S(1)}, f32[256]{0:T(256)S(1)}, u32[]{:S(2)}, u32[]{:S(2)}) %collective-permute-start.1) | collective-permute-done | bytes 1056 | tf_op jit(solution)/shard_map/ppermute | solution.py:328
  36.3 2.8 %multiply_convert_fusion.1 = (bf16[256,2560]{1,0:T(8,128)(2,1)S(1)}, bf16[256,2560]{1,0:T(8,128)(2,1)S(1)}) fusion(f32[2560]{0:T(1024)S(1)} %copy-done.5, f32[256]{0:T(256)S(1)} %get-tuple-element.49, bf16[256,2560]{1,0:T(8,128)(2,1)} %reshape.797, bf16[256,2560]{1,0:T(8,128)(2,1)} %collective-permute-done, pred[]{:T(512)S(6)} %eq.15, ...), kind=kLoop, calls=%fused_computation.8 | loop fusion | flops 6553600 | bytes 5255169 | tf_op jit(solution)/shard_map/convert_element_type | solution.py:332
  39.1 1.5 convolution_convert_fusion.2
  40.7 1.5 convolution_convert_fusion.1
  42.2 0.4 slice-done.1
  42.6 0.8 slice-done.2
  43.4 5.8 %convolution_convert_fusion = bf16[512,2048]{1,0:T(8,128)(2,1)S(1)} fusion(bf16[2560,2048]{1,0:T(8,128)(2,1)S(1)} %bitcast.165, bf16[256,2560]{1,0:T(8,128)(2,1)S(1)} %get-tuple-element.32, bf16[256,2560]{1,0:T(8,128)(2,1)S(1)} %get-tuple-element.31), kind=kOutput, calls=%fused_computation.5 | convolution fusion | flops 5375000576 | bytes 15204352 | tf_op jit(solution)/shard_map/dot_general | solution.py:347
  49.2 0.3 pad_maximum_fusion
  49.5 1.6 copy-done.2
  51.1 1.3 constant_dynamic-slice_fusion.2
  52.6 0.5 multiply_cosine_fusion
  53.2 2.9 %collective-permute-done.2 = bf16[1,256,3072]{2,1,0:T(8,128)(2,1)S(1)} collective-permute-done((bf16[1,256,3072]{2,1,0:T(8,128)(2,1)}, bf16[1,256,3072]{2,1,0:T(8,128)(2,1)S(1)}, u32[]{:S(2)}, u32[]{:S(2)}) %collective-permute-start.2) | collective-permute-done | bytes 1572896 | tf_op jit(solution)/shard_map/ppermute | solution.py:237
  56.0 1.9 %add_bitcast_fusion = f32[32,8,24,128]{3,1,2,0:T(8,128)S(1)} fusion(bf16[1,256,3072]{2,1,0:T(8,128)(2,1)S(1)} %collective-permute-done.2, bf16[2,256,3072]{2,1,0:T(8,128)(2,1)} %copy-done.2, s32[]{:T(128)S(6)} %select_n.176), kind=kLoop, calls=%fused_computation.4 | loop fusion | flops 2359296 | bytes 6291460
  58.0 0.6 copy.125
  58.7 0.4 add_convert_fusion.1
  59.1 0.8 subtract_convert_fusion
  59.9 1.4 pad_maximum_fusion.2
  61.3 0.5 copy.109
  62.0 1.3 fusion.7
  63.3 0.5 copy.89
  63.8 0.2 select_reduce_fusion
  64.0 0.2 fusion.11
  64.2 19.7 %shard_map.130 = (f32[64,64,1]{2,1,0:T(8,128)}, f32[64,64,1]{2,1,0:T(8,128)}, f32[64,64,128]{2,1,0:T(8,128)}) custom-call(s32[50]{0:T(128)} %req_ref.1, s32[64]{0:T(128)} %len_ref.1, s32[50]{0:T(128)} %blk_ref.1, bf16[64,64,128]{2,1,0:T(8,128)(2,1)} %bitcast.136, bf16[50,128,512]{2,1,0:T(8,128)(2,1)} %k_ref.1, bf16[50,128,512]{2,1,0:T(8,128)(2,1)} %v_ref.1), custom_call_target="tpu_custom_call" | custom-call | tf_op jit(solution)/shard_map/pallas_call | solution.py:209
  83.9 2.4 %reduce.1 = f32[64,64]{1,0:T(8,128)S(1)} reduce(f32[64,64,1]{2,1,0:T(8,128)} %get-tuple-element.7, f32[]{:T(128)} %constant.102), dimensions={2}, to_apply=%get-tuple-element.7.reduce_sub_computation | reduce | bytes 32772 | tf_op jit(solution)/shard_map/pallas_call | solution.py:209
  86.2 0.6 reduce.2
  86.9 1.8 %collective-permute-start.3 = (f32[2,2,2,1,8,64]{5,4,3,2,1,0:T(8,128)S(1)}, f32[2,2,2,1,8,64]{5,4,3,2,1,0:T(8,128)S(1)}, u32[]{:S(2)}, u32[]{:S(2)}) collective-permute-start(f32[2,2,2,1,8,64]{5,4,3,2,1,0:T(8,128)S(1)} %get-tuple-element.40), channel_id=1, source_target_pairs={{0,1},{1,0},{2,3},{3,2},{4,5},{5,4},{6,7},{7,6},{8,9},{9,8},{10,11... | collective-permute-start | bytes 49160 | tf_op jit(solution)/shard_map/ppermute | solution.py:282
  88.7 1.3 dynamic-slice_convert_fusion
  90.0 0.5 copy.96
  90.5 0.3 collective-permute-start.4
  90.9 1.9 %collective-permute-start.5 = (f32[2,2,1,1,8,64]{5,4,3,2,1,0:T(8,128)S(1)}, f32[2,2,1,1,8,64]{5,4,3,2,1,0:T(8,128)S(1)}, u32[]{:S(2)}, u32[]{:S(2)}) collective-permute-start(f32[2,2,1,1,8,64]{5,4,3,2,1,0:T(8,128)S(1)} %get-tuple-element.44), channel_id=1, source_target_pairs={{0,2},{1,3},{2,0},{3,1},{4,6},{5,7},{6,4},{7,5},{8,10},{9,11},{10,... | collective-permute-start | bytes 24584 | tf_op jit(solution)/shard_map/ppermute | solution.py:282
  92.8 1.9 %collective-permute-done.5 = f32[2,2,1,1,8,64]{5,4,3,2,1,0:T(8,128)S(1)} collective-permute-done((f32[2,2,1,1,8,64]{5,4,3,2,1,0:T(8,128)S(1)}, f32[2,2,1,1,8,64]{5,4,3,2,1,0:T(8,128)S(1)}, u32[]{:S(2)}, u32[]{:S(2)}) %collective-permute-start.5) | collective-permute-done | bytes 8224 | tf_op jit(solution)/shard_map/ppermute | solution.py:282
  94.7 2.9 %collective-permute-start.7 = (f32[2,1,1,1,8,64]{5,4,3,2,1,0:T(8,128)S(1)}, f32[2,1,1,1,8,64]{5,4,3,2,1,0:T(8,128)S(1)}, u32[]{:S(2)}, u32[]{:S(2)}) collective-permute-start(f32[2,1,1,1,8,64]{5,4,3,2,1,0:T(8,128)S(1)} %get-tuple-element.48), channel_id=1, source_target_pairs={{0,4},{1,5},{2,6},{3,7},{4,0},{5,1},{6,2},{7,3},{8,12},{9,13},{10,... | collective-permute-start | bytes 12296 | tf_op jit(solution)/shard_map/ppermute | solution.py:282
  97.7 1.7 collective-permute-done.7
  99.5 4.8 %collective-permute-done.4 = bf16[2,2,1,8,64,128]{5,4,3,2,1,0:T(8,128)(2,1)S(1)} collective-permute-done((bf16[2,2,1,8,64,128]{5,4,3,2,1,0:T(8,128)(2,1)S(1)}, bf16[2,2,1,8,64,128]{5,4,3,2,1,0:T(8,128)(2,1)S(1)}, u32[]{:S(2)}, u32[]{:S(2)}) %collective-permute-start.4) | collective-permute-done | bytes 524320 | tf_op jit(solution)/shard_map/ppermute | solution.py:283
  104.3 1.8 %multiply_add_fusion = f32[2,2,1,8,64,128]{5,4,3,2,1,0:T(8,128)S(1)} fusion(bf16[2,2,1,8,64,128]{5,4,3,2,1,0:T(8,128)(2,1)S(1)} %collective-permute-done.4, f32[2,2,2,8,64,128]{5,4,3,2,1,0:T(8,128)} %bitcast.148, s32[]{:T(128)S(6)} %select_n.178, f32[2,2,8,64]{3,2,1,0:T(8,128)S(1)} %get-tuple-element.38, f32[2,2,8,64]{3,2,1,0:T(8,128)S(1)} %get-tuple-element.37), kind=kLoop, calls=%fused_computation.18 | loop fusion | flops 1048576 | bytes 2637828 | tf_op jit(solution)/shard_map/add | solution.py:292
  106.2 1.6 collective-permute-start.6
  107.8 0.2 copy.92
  108.0 0.2 copy.98
  108.4 0.2 convolution_multiply_fusion
  108.6 4.8 %collective-permute-done.6 = bf16[2,1,1,8,64,128]{5,4,3,2,1,0:T(8,128)(2,1)S(1)} collective-permute-done((bf16[2,1,1,8,64,128]{5,4,3,2,1,0:T(8,128)(2,1)S(1)}, bf16[2,1,1,8,64,128]{5,4,3,2,1,0:T(8,128)(2,1)S(1)}, u32[]{:S(2)}, u32[]{:S(2)}) %collective-permute-start.6) | collective-permute-done | bytes 262176 | tf_op jit(solution)/shard_map/ppermute | solution.py:283
  113.4 0.3 multiply_add_fusion.1
  113.8 2.7 %collective-permute-start.8 = (bf16[1,1,1,8,64,128]{5,4,3,2,1,0:T(8,128)(2,1)S(1)}, bf16[1,1,1,8,64,128]{5,4,3,2,1,0:T(8,128)(2,1)S(1)}, u32[]{:S(2)}, u32[]{:S(2)}) collective-permute-start(bf16[1,1,1,8,64,128]{5,4,3,2,1,0:T(8,128)(2,1)S(1)} %dynamic-slice_convert_fusion.2), channel_id=1, source_target_pairs={{0,4},{1,5},{2,6},{3,7},{4,0},{5,1},{6,2},{7,3},{8,12},{9,13},{10,... | collective-permute-start | bytes 393224 | tf_op jit(solution)/shard_map/ppermute | solution.py:283
  116.5 4.7 %collective-permute-done.8 = bf16[1,1,1,8,64,128]{5,4,3,2,1,0:T(8,128)(2,1)S(1)} collective-permute-done((bf16[1,1,1,8,64,128]{5,4,3,2,1,0:T(8,128)(2,1)S(1)}, bf16[1,1,1,8,64,128]{5,4,3,2,1,0:T(8,128)(2,1)S(1)}, u32[]{:S(2)}, u32[]{:S(2)}) %collective-permute-start.8) | collective-permute-done | bytes 131104 | tf_op jit(solution)/shard_map/ppermute | solution.py:283
  121.2 0.2 multiply_add_fusion.2
  121.4 0.3 fusion.9
  121.8 2.0 %all_gather.4 = bf16[2,8,4,2048]{3,1,2,0:T(8,128)(2,1)S(1)} all-gather(bf16[1,8,4,2048]{3,1,2,0:T(8,128)(2,1)S(1)} %convert_element_type.115), channel_id=1, replica_groups=mesh['row'=2,'col'=2,'seq'=8] {'row'}, dimensions={0}, use_global_device_ids=true | all-gather | bytes 393216 | tf_op jit(solution)/shard_map/all_gather | solution.py:411
  123.8 5.9 %fusion.2 = bf16[2,8,4,2560]{3,1,2,0:T(8,128)(2,1)S(1)} fusion(bf16[2,8,4,2048]{3,1,2,0:T(8,128)(2,1)S(1)} %all_gather.4, bf16[2048,2560]{1,0:T(8,128)(2,1)} %param.16), kind=kOutput, calls=%fused_computation.2 | convolution fusion | flops 671252480 | bytes 11075584 | tf_op jit(solution)/shard_map/dot_general | solution.py:413
  129.7 1.6 collective-permute-start.9
  131.3 4.8 %collective-permute-done.9 = bf16[1,8,4,2560]{3,1,2,0:T(8,128)(2,1)S(1)} collective-permute-done((bf16[1,8,4,2560]{3,1,2,0:T(8,128)(2,1)S(1)}, bf16[1,8,4,2560]{3,1,2,0:T(8,128)(2,1)S(1)}, u32[]{:S(2)}, u32[]{:S(2)}) %collective-permute-start.9) | collective-permute-done | bytes 163872 | tf_op jit(solution)/shard_map/ppermute | solution.py:237
  136.1 1.3 collective-permute-start.10
  137.5 8.6 %collective-permute-done.10 = bf16[1,8,4,2560]{3,1,2,0:T(8,128)(2,1)S(1)} collective-permute-done((bf16[1,8,4,2560]{3,1,2,0:T(8,128)(2,1)S(1)}, bf16[1,8,4,2560]{3,1,2,0:T(8,128)(2,1)S(1)}, u32[]{:S(2)}, u32[]{:S(2)}) %collective-permute-start.10) | collective-permute-done | bytes 163872 | tf_op jit(solution)/shard_map/ppermute | solution.py:251
  146.0 0.4 collective-permute-start.11
  146.5 8.3 %collective-permute-done.11 = bf16[2,1,8,4,2560]{4,2,3,1,0:T(8,128)(2,1)S(1)} collective-permute-done((bf16[2,1,8,4,2560]{4,2,3,1,0:T(8,128)(2,1)S(1)}, bf16[2,1,8,4,2560]{4,2,3,1,0:T(8,128)(2,1)S(1)}, u32[]{:S(2)}, u32[]{:S(2)}) %collective-permute-start.11) | collective-permute-done | bytes 327712 | tf_op jit(solution)/shard_map/ppermute | solution.py:251
  154.9 0.3 collective-permute-start.12
  155.3 0.8 reshape_reshape.8
  156.1 0.4 pad_maximum_fusion.6
  156.4 0.8 convert_element_type.120
  157.4 12.5 %collective-permute-done.12 = bf16[2,2,1,8,4,2560]{5,3,4,1,2,0:T(8,128)(2,1)S(1)} collective-permute-done((bf16[2,2,1,8,4,2560]{5,3,4,1,2,0:T(8,128)(2,1)S(1)}, bf16[2,2,1,8,4,2560]{5,3,4,1,2,0:T(8,128)(2,1)S(1)}, u32[]{:S(2)}, u32[]{:S(2)}) %collective-permute-start.12) | collective-permute-done | bytes 655392 | tf_op jit(solution)/shard_map/ppermute | solution.py:251
  169.8 0.2 fusion.5
  170.2 2.1 %copy.105 = bf16[64,4,2560]{2,1,0:T(4,128)(2,1)} copy(bf16[64,4,2560]{2,0,1:T(8,128)(2,1)S(1)} %bitcast.135) | data formatting | bytes 2621440
  (58 shorter events, 1.9 us)
Async XLA Ops:
  0.6 38.5 %copy-start = (bf16[2560,512]{1,0:T(8,128)(2,1)S(1)}, bf16[2560,512]{1,0:T(8,128)(2,1)}, u32[]{:S(2)}) copy-start(bf16[2560,512]{1,0:T(8,128)(2,1)} %param.14) | copy-start | bytes 7864324
  0.6 35.6 %copy-start.5 = (f32[2560]{0:T(1024)S(1)}, f32[2560]{0:T(1024)}, u32[]{:S(2)}) copy-start(f32[2560]{0:T(1024)} %param.12) | copy-start | bytes 30724
  4.2 32.0 %collective-permute-start = (bf16[256,2560]{1,0:T(8,128)(2,1)}, bf16[256,2560]{1,0:T(8,128)(2,1)}, u32[]{:S(2)}, u32[]{:S(2)}) collective-permute-start(bf16[256,2560]{1,0:T(8,128)(2,1)} %reshape.797), channel_id=1, source_target_pairs={{0,8},{8,0},{1,9},{9,1},{2,10},{10,2},{3,11},{11,3},{4,12},{12,4},... | collective-permute-start | bytes 3932168 | tf_op jit(solution)/shard_map/ppermute | solution.py:325
  11.8 24.4 %collective-permute-start.1 = (f32[256]{0:T(256)S(1)}, f32[256]{0:T(256)S(1)}, u32[]{:S(2)}, u32[]{:S(2)}) collective-permute-start(f32[256]{0:T(256)S(1)} %psum.7), channel_id=1, source_target_pairs={{0,8},{8,0},{1,9},{9,1},{2,10},{10,2},{3,11},{11,3},{4,12},{12,4},... | collective-permute-start | bytes 3080 | tf_op jit(solution)/shard_map/ppermute | solution.py:328
  36.3 4.4 %copy-start.7 = (bf16[2560,512]{1,0:T(8,128)(2,1)S(1)}, bf16[2560,512]{1,0:T(8,128)(2,1)}, u32[]{:S(2)}) copy-start(bf16[2560,512]{1,0:T(8,128)(2,1)} %param.15) | copy-start | bytes 7864324
  39.1 3.1 %slice-start = ((s8[10485760]{0:T(1024)(128)(4,1)}), s8[4194304]{0:T(1024)(128)(4,1)S(1)}, s32[]{:S(2)}) async-start(s8[10485760]{0:T(1024)(128)(4,1)} %bitcast.164), calls=%async_computation | async-start | bytes 8388608
  39.1 3.5 %slice-start.1 = ((s8[10485760]{0:T(1024)(128)(4,1)}), s8[4194304]{0:T(1024)(128)(4,1)S(1)}, s32[]{:S(2)}) async-start(s8[10485760]{0:T(1024)(128)(4,1)} %bitcast.164), calls=%async_computation.1 | async-start | bytes 8388608
  40.7 2.7 %slice-start.2 = ((s8[10485760]{0:T(1024)(128)(4,1)}), s8[2097152]{0:T(1024)(128)(4,1)S(1)}, s32[]{:S(2)}) async-start(s8[10485760]{0:T(1024)(128)(4,1)} %bitcast.164), calls=%async_computation.2 | async-start | bytes 4194304
  49.5 1.6 copy-start.2
  51.1 1.3 copy-start.6
  52.4 3.6 %collective-permute-start.2 = (bf16[1,256,3072]{2,1,0:T(8,128)(2,1)}, bf16[1,256,3072]{2,1,0:T(8,128)(2,1)S(1)}, u32[]{:S(2)}, u32[]{:S(2)}) collective-permute-start(bf16[1,256,3072]{2,1,0:T(8,128)(2,1)} %constant_dynamic-slice_fusion.2), channel_id=1, source_target_pairs={{0,16},{16,0},{1,17},{17,1},{2,18},{18,2},{3,19},{19,3},{4,20},{20... | collective-permute-start | bytes 4718600 | tf_op jit(solution)/shard_map/ppermute | solution.py:237
  61.8 2.4 %copy-start.3 = (bf16[64,4,4,4,128]{4,3,1,2,0:T(4,128)(2,1)}, bf16[64,4,4,4,128]{4,3,1,2,0:T(4,128)(2,1)S(1)}, u32[]{:S(2)}) copy-start(bf16[64,4,4,4,128]{4,3,1,2,0:T(4,128)(2,1)S(1)} %copy.109) | copy-start | bytes 3145732
  83.9 2.4 %copy-start.4 = (f32[64,64,1]{2,1,0:T(8,128)S(1)}, f32[64,64,1]{2,1,0:T(8,128)}, u32[]{:S(2)}) copy-start(f32[64,64,1]{2,1,0:T(8,128)} %get-tuple-element.8) | copy-start | bytes 49156
  86.9 4.0 %collective-permute-start.3 = (f32[2,2,2,1,8,64]{5,4,3,2,1,0:T(8,128)S(1)}, f32[2,2,2,1,8,64]{5,4,3,2,1,0:T(8,128)S(1)}, u32[]{:S(2)}, u32[]{:S(2)}) collective-permute-start(f32[2,2,2,1,8,64]{5,4,3,2,1,0:T(8,128)S(1)} %get-tuple-element.40), channel_id=1, source_target_pairs={{0,1},{1,0},{2,3},{3,2},{4,5},{5,4},{6,7},{7,6},{8,9},{9,8},{10,11... | collective-permute-start | bytes 49160 | tf_op jit(solution)/shard_map/ppermute | solution.py:282
  90.5 13.8 %collective-permute-start.4 = (bf16[2,2,1,8,64,128]{5,4,3,2,1,0:T(8,128)(2,1)S(1)}, bf16[2,2,1,8,64,128]{5,4,3,2,1,0:T(8,128)(2,1)S(1)}, u32[]{:S(2)}, u32[]{:S(2)}) collective-permute-start(bf16[2,2,1,8,64,128]{5,4,3,2,1,0:T(8,128)(2,1)S(1)} %dynamic-slice_convert_fusion), channel_id=1, source_target_pairs={{0,1},{1,0},{2,3},{3,2},{4,5},{5,4},{6,7},{7,6},{8,9},{9,8},{10,11... | collective-permute-start | bytes 1572872 | tf_op jit(solution)/shard_map/ppermute | solution.py:283
  90.9 3.8 %collective-permute-start.5 = (f32[2,2,1,1,8,64]{5,4,3,2,1,0:T(8,128)S(1)}, f32[2,2,1,1,8,64]{5,4,3,2,1,0:T(8,128)S(1)}, u32[]{:S(2)}, u32[]{:S(2)}) collective-permute-start(f32[2,2,1,1,8,64]{5,4,3,2,1,0:T(8,128)S(1)} %get-tuple-element.44), channel_id=1, source_target_pairs={{0,2},{1,3},{2,0},{3,1},{4,6},{5,7},{6,4},{7,5},{8,10},{9,11},{10,... | collective-permute-start | bytes 24584 | tf_op jit(solution)/shard_map/ppermute | solution.py:282
  94.7 4.6 %collective-permute-start.7 = (f32[2,1,1,1,8,64]{5,4,3,2,1,0:T(8,128)S(1)}, f32[2,1,1,1,8,64]{5,4,3,2,1,0:T(8,128)S(1)}, u32[]{:S(2)}, u32[]{:S(2)}) collective-permute-start(f32[2,1,1,1,8,64]{5,4,3,2,1,0:T(8,128)S(1)} %get-tuple-element.48), channel_id=1, source_target_pairs={{0,4},{1,5},{2,6},{3,7},{4,0},{5,1},{6,2},{7,3},{8,12},{9,13},{10,... | collective-permute-start | bytes 12296 | tf_op jit(solution)/shard_map/ppermute | solution.py:282
  106.2 7.3 %collective-permute-start.6 = (bf16[2,1,1,8,64,128]{5,4,3,2,1,0:T(8,128)(2,1)S(1)}, bf16[2,1,1,8,64,128]{5,4,3,2,1,0:T(8,128)(2,1)S(1)}, u32[]{:S(2)}, u32[]{:S(2)}) collective-permute-start(bf16[2,1,1,8,64,128]{5,4,3,2,1,0:T(8,128)(2,1)S(1)} %dynamic-slice_convert_fusion.1), channel_id=1, source_target_pairs={{0,2},{1,3},{2,0},{3,1},{4,6},{5,7},{6,4},{7,5},{8,10},{9,11},{10,... | collective-permute-start | bytes 786440 | tf_op jit(solution)/shard_map/ppermute | solution.py:283
  113.8 7.3 %collective-permute-start.8 = (bf16[1,1,1,8,64,128]{5,4,3,2,1,0:T(8,128)(2,1)S(1)}, bf16[1,1,1,8,64,128]{5,4,3,2,1,0:T(8,128)(2,1)S(1)}, u32[]{:S(2)}, u32[]{:S(2)}) collective-permute-start(bf16[1,1,1,8,64,128]{5,4,3,2,1,0:T(8,128)(2,1)S(1)} %dynamic-slice_convert_fusion.2), channel_id=1, source_target_pairs={{0,4},{1,5},{2,6},{3,7},{4,0},{5,1},{6,2},{7,3},{8,12},{9,13},{10,... | collective-permute-start | bytes 393224 | tf_op jit(solution)/shard_map/ppermute | solution.py:283
  129.7 6.3 %collective-permute-start.9 = (bf16[1,8,4,2560]{3,1,2,0:T(8,128)(2,1)S(1)}, bf16[1,8,4,2560]{3,1,2,0:T(8,128)(2,1)S(1)}, u32[]{:S(2)}, u32[]{:S(2)}) collective-permute-start(bf16[1,8,4,2560]{3,1,2,0:T(8,128)(2,1)S(1)} %constant_dynamic-slice_fusion.1), channel_id=1, source_target_pairs={{0,8},{8,0},{1,9},{9,1},{2,10},{10,2},{3,11},{11,3},{4,12},{12,4},... | collective-permute-start | bytes 491528 | tf_op jit(solution)/shard_map/ppermute | solution.py:237
  136.1 9.9 %collective-permute-start.10 = (bf16[1,8,4,2560]{3,1,2,0:T(8,128)(2,1)S(1)}, bf16[1,8,4,2560]{3,1,2,0:T(8,128)(2,1)S(1)}, u32[]{:S(2)}, u32[]{:S(2)}) collective-permute-start(bf16[1,8,4,2560]{3,1,2,0:T(8,128)(2,1)S(1)} %add_convert_fusion.2), channel_id=1, source_target_pairs={{0,4},{1,5},{2,6},{3,7},{4,0},{5,1},{6,2},{7,3},{8,12},{9,13},{10,... | collective-permute-start | bytes 491528 | tf_op jit(solution)/shard_map/ppermute | solution.py:251
  146.0 8.8 %collective-permute-start.11 = (bf16[2,1,8,4,2560]{4,2,3,1,0:T(8,128)(2,1)S(1)}, bf16[2,1,8,4,2560]{4,2,3,1,0:T(8,128)(2,1)S(1)}, u32[]{:S(2)}, u32[]{:S(2)}) collective-permute-start(bf16[2,1,8,4,2560]{4,2,3,1,0:T(8,128)(2,1)S(1)} %maximum_select_fusion.4), channel_id=1, source_target_pairs={{0,1},{1,0},{2,3},{3,2},{4,5},{5,4},{6,7},{7,6},{8,9},{9,8},{10,11... | collective-permute-start | bytes 983048 | tf_op jit(solution)/shard_map/ppermute | solution.py:251
  154.9 14.9 %collective-permute-start.12 = (bf16[2,2,1,8,4,2560]{5,3,4,1,2,0:T(8,128)(2,1)S(1)}, bf16[2,2,1,8,4,2560]{5,3,4,1,2,0:T(8,128)(2,1)S(1)}, u32[]{:S(2)}, u32[]{:S(2)}) collective-permute-start(bf16[2,2,1,8,4,2560]{5,3,4,1,2,0:T(8,128)(2,1)S(1)} %maximum_select_fusion.2), channel_id=1, source_target_pairs={{0,2},{1,3},{2,0},{3,1},{4,6},{5,7},{6,4},{7,5},{8,10},{9,11},{10,... | collective-permute-start | bytes 1966088 | tf_op jit(solution)/shard_map/ppermute | solution.py:251
  169.8 2.4 %copy-start.1 = (bf16[2560,512]{1,0:T(8,128)(2,1)S(1)}, bf16[2560,512]{1,0:T(8,128)(2,1)}, u32[]{:S(2)}) copy-start(bf16[2560,512]{1,0:T(8,128)(2,1)} %param.14) | copy-start | bytes 7864324

commit v16 on v15

--- a/solution.py
+++ b/solution.py
@@ -239,13 +239,15 @@
     return total.astype(parts.dtype) if rounded else total
 
 
-def doubling_gather(part, axis_name):
+def doubling_gather(part, axis_name, swap_last=False):
     n = lax.axis_size(axis_name)
     stages = n.bit_length() - 1
     assert 1 << stages == n
     index = lax.axis_index(axis_name)
     block = part[None]
-    order = [stages - 1] + list(range(stages - 1))
+    order = list(reversed(range(stages)))
+    if swap_last and stages >= 2:
+        order[-2], order[-1] = order[-1], order[-2]
     for bit in order:
         pairs = [(s, s ^ (1 << bit)) for s in range(n)]
         got = lax.ppermute(block, axis_name, pairs)
@@ -415,7 +417,14 @@
     )
     partials = product.reshape(n_row, per, step_count, -1)
     own_out = pair_scatter(partials.astype(jnp.bfloat16), "col").reshape(per, step_count, -1)
-    attended = doubling_gather(own_out, "seq")
+    split = own_out.shape[-1] // 2
+    attended = jnp.concatenate(
+        [
+            doubling_gather(own_out[..., :split], "seq"),
+            doubling_gather(own_out[..., split:], "seq", swap_last=True),
+        ],
+        -1,
+    )
     return (
         attended,
         current_key.reshape(req_count, step_count, k_width),

time: 173 us -> 162 us (0.936)
  waiting for transfers between devices: 79.3 us -> 64 us
  starting transfers between devices: 17.9 us -> 22.7 us
    ppermute x3 -> x6, waiting for transfers between devices: 29.3 us -> 14.8 us  [doubling_gather(): got = lax.ppermute(block, axis_name, pairs)]
    ppermute x3 -> x6, starting transfers between devices: 2.11 us -> 6.96 us  [doubling_gather(): got = lax.ppermute(block, axis_name, pairs)]
  transfers between devices with their start and end apart: 13 -> 16, of which waited for: 11 -> 13; matrix products, arithmetic and copies ran while one was open for 5% -> 5% of each run, Pallas kernels for 0% -> 0%
where the time goes in v16:
time: 162 us
  waiting for transfers between devices  64 us (40%)
  starting transfers between devices  22.7 us (14%)
  Pallas kernels  19.7 us (12%)
  other arithmetic  17.5 us (11%)
  local copies, waits for them, and re-layouts  16.2 us (10%)
  matrix products  16.2 us (10%)
  blocking collectives  4.46 us (3%)
    ppermute x1, waiting for transfers between devices, on_device(): other_squares = lax.ppermute(squares, 'col', swap)  24.4 us
    pallas_call x1, Pallas kernels, slot_attention(): pl.pallas_call(partial(slot_kernel, ns=ns, heads=heads, qpk=qpk), grid_sp...  19.7 us
    ppermute x6, waiting for transfers between devices, doubling_gather(): got = lax.ppermute(block, axis_name, pairs)  14.8 us
    ppermute x3, waiting for transfers between devices, seq_merge(): lax.ppermute(send_values.astype(jnp.bfloat16), 'seq', pairs)  14.3 us
    dot_general x3, matrix products, on_device(): jnp.dot(gathered, matrix, preferred_element_type=jnp.float32)  8.8 us
    ppermute x6, starting transfers between devices, doubling_gather(): got = lax.ppermute(block, axis_name, pairs)  6.96 us
    ppermute x2, waiting for transfers between devices, pair_scatter(): got = lax.ppermute(send, axis_name, [(0, 1), (1, 0)])  6.82 us
    ppermute x3, starting transfers between devices, seq_merge(): got_stats = lax.ppermute(send_stats, 'seq', pairs)  6.64 us
  transfers between devices with their start and end apart: 16, of which 13 were waited for; matrix products, arithmetic and copies ran while one was open for 5% of the time, Pallas kernels for 0%

profile of v16, /device:TPU:0, one launch (start us, length us, event | category | flops | bytes accessed | tf_op | source)
XLA Modules:
  0.0 161.9 jit_solution(15915754771641673325)
XLA Ops:
  0.7 3.5 %reshape.1228 = bf16[256,2560]{1,0:T(8,128)(2,1)} reshape(bf16[64,4,2560]{2,1,0:T(4,128)(2,1)} %param.11) | data formatting | bytes 2621440 | tf_op jit(solution)/shard_map/reshape | solution.py:324
  4.2 2.9 %collective-permute-start = (bf16[256,2560]{1,0:T(8,128)(2,1)}, bf16[256,2560]{1,0:T(8,128)(2,1)}, u32[]{:S(2)}, u32[]{:S(2)}) collective-permute-start(bf16[256,2560]{1,0:T(8,128)(2,1)} %reshape.1228), channel_id=1, source_target_pairs={{0,8},{8,0},{1,9},{9,1},{2,10},{10,2},{3,11},{11,3},{4,12},{12,4},... | collective-permute-start | bytes 3932168 | tf_op jit(solution)/shard_map/ppermute | solution.py:327
  7.1 2.1 %multiply_reduce_fusion = f32[64,4]{1,0:T(8,128)S(1)} fusion(bf16[64,4,2560]{2,1,0:T(4,128)(2,1)} %param.11), kind=kLoop, calls=%fused_computation.9 | loop fusion | flops 1965824 | bytes 1311744 | tf_op jit(solution)/shard_map/reduce_sum | solution.py:329
  9.3 2.5 %psum.7 = f32[256]{0:T(256)S(1)} all-reduce(f32[256]{0:T(256)S(1)} %reduce_sum.21), channel_id=1, replica_groups=mesh['row'=2,'col'=2,'seq'=8] {'row'}, use_global_device_ids=true, to_apply=%region_1.0 | all-reduce | flops 256 | bytes 2048 | tf_op jit(solution)/shard_map/psum | solution.py:329
  11.8 24.4 %collective-permute-done.1 = f32[256]{0:T(256)S(1)} collective-permute-done((f32[256]{0:T(256)S(1)}, f32[256]{0:T(256)S(1)}, u32[]{:S(2)}, u32[]{:S(2)}) %collective-permute-start.1) | collective-permute-done | bytes 1056 | tf_op jit(solution)/shard_map/ppermute | solution.py:330
  36.3 2.8 %multiply_convert_fusion.1 = (bf16[256,2560]{1,0:T(8,128)(2,1)S(1)}, bf16[256,2560]{1,0:T(8,128)(2,1)S(1)}) fusion(f32[2560]{0:T(1024)S(1)} %copy-done.5, f32[256]{0:T(256)S(1)} %get-tuple-element.55, bf16[256,2560]{1,0:T(8,128)(2,1)} %reshape.1228, bf16[256,2560]{1,0:T(8,128)(2,1)} %collective-permute-done, pred[]{:T(512)S(6)} %eq.18, ...), kind=kLoop, calls=%fused_computation.8 | loop fusion | flops 6553600 | bytes 5255169 | tf_op jit(solution)/shard_map/convert_element_type | solution.py:334
  39.1 1.5 convolution_convert_fusion.2
  40.7 1.5 convolution_convert_fusion.1
  42.2 0.4 slice-done.1
  42.6 0.8 slice-done.2
  43.4 5.8 %convolution_convert_fusion = bf16[512,2048]{1,0:T(8,128)(2,1)S(1)} fusion(bf16[2560,2048]{1,0:T(8,128)(2,1)S(1)} %bitcast.207, bf16[256,2560]{1,0:T(8,128)(2,1)S(1)} %get-tuple-element.32, bf16[256,2560]{1,0:T(8,128)(2,1)S(1)} %get-tuple-element.31), kind=kOutput, calls=%fused_computation.5 | convolution fusion | flops 5375000576 | bytes 15204352 | tf_op jit(solution)/shard_map/dot_general | solution.py:349
  49.2 0.3 pad_maximum_fusion
  49.5 1.6 %copy-done.2 = bf16[2,256,3072]{2,1,0:T(8,128)(2,1)} copy-done((bf16[2,256,3072]{2,1,0:T(8,128)(2,1)}, bf16[2,256,3072]{2,1,0:T(8,128)(2,1)S(1)}, u32[]{:S(2)}) %copy-start.2) | copy-done | bytes 3145752
  51.1 1.3 constant_dynamic-slice_fusion.2
  52.6 0.5 multiply_cosine_fusion
  53.2 2.9 %collective-permute-done.2 = bf16[1,256,3072]{2,1,0:T(8,128)(2,1)S(1)} collective-permute-done((bf16[1,256,3072]{2,1,0:T(8,128)(2,1)}, bf16[1,256,3072]{2,1,0:T(8,128)(2,1)S(1)}, u32[]{:S(2)}, u32[]{:S(2)}) %collective-permute-start.2) | collective-permute-done | bytes 1572896 | tf_op jit(solution)/shard_map/ppermute | solution.py:237
  56.0 1.9 %add_bitcast_fusion = f32[32,8,24,128]{3,1,2,0:T(8,128)S(1)} fusion(bf16[1,256,3072]{2,1,0:T(8,128)(2,1)S(1)} %collective-permute-done.2, bf16[2,256,3072]{2,1,0:T(8,128)(2,1)} %copy-done.2, s32[]{:T(128)S(6)} %select_n.253), kind=kLoop, calls=%fused_computation.4 | loop fusion | flops 2359296 | bytes 6291460
  58.0 0.6 copy.140
  58.7 0.4 add_convert_fusion.1
  59.1 0.8 subtract_convert_fusion
  59.9 1.4 pad_maximum_fusion.3
  61.3 0.5 copy.124
  62.0 1.3 fusion.10
  63.3 0.5 copy.100
  64.2 19.7 %shard_map.130 = (f32[64,64,1]{2,1,0:T(8,128)}, f32[64,64,1]{2,1,0:T(8,128)}, f32[64,64,128]{2,1,0:T(8,128)}) custom-call(s32[50]{0:T(128)} %req_ref.1, s32[64]{0:T(128)} %len_ref.1, s32[50]{0:T(128)} %blk_ref.1, bf16[64,64,128]{2,1,0:T(8,128)(2,1)} %bitcast.173, bf16[50,128,512]{2,1,0:T(8,128)(2,1)} %k_ref.1, bf16[50,128,512]{2,1,0:T(8,128)(2,1)} %v_ref.1), custom_call_target="tpu_custom_call" | custom-call | tf_op jit(solution)/shard_map/pallas_call | solution.py:209
  83.8 2.4 %reduce.1 = f32[64,64]{1,0:T(8,128)S(1)} reduce(f32[64,64,1]{2,1,0:T(8,128)} %get-tuple-element.7, f32[]{:T(128)} %constant.102), dimensions={2}, to_apply=%get-tuple-element.7.reduce_sub_computation | reduce | bytes 32772 | tf_op jit(solution)/shard_map/pallas_call | solution.py:209
  86.2 0.6 reduce.2
  86.8 1.8 %collective-permute-start.3 = (f32[2,2,2,1,8,64]{5,4,3,2,1,0:T(8,128)S(1)}, f32[2,2,2,1,8,64]{5,4,3,2,1,0:T(8,128)S(1)}, u32[]{:S(2)}, u32[]{:S(2)}) collective-permute-start(f32[2,2,2,1,8,64]{5,4,3,2,1,0:T(8,128)S(1)} %get-tuple-element.46), channel_id=1, source_target_pairs={{0,1},{1,0},{2,3},{3,2},{4,5},{5,4},{6,7},{7,6},{8,9},{9,8},{10,11... | collective-permute-start | bytes 49160 | tf_op jit(solution)/shard_map/ppermute | solution.py:284
  88.7 1.3 dynamic-slice_convert_fusion
  90.0 0.5 copy.107
  90.5 0.3 collective-permute-start.4
  90.9 1.9 %collective-permute-start.5 = (f32[2,2,1,1,8,64]{5,4,3,2,1,0:T(8,128)S(1)}, f32[2,2,1,1,8,64]{5,4,3,2,1,0:T(8,128)S(1)}, u32[]{:S(2)}, u32[]{:S(2)}) collective-permute-start(f32[2,2,1,1,8,64]{5,4,3,2,1,0:T(8,128)S(1)} %get-tuple-element.50), channel_id=1, source_target_pairs={{0,2},{1,3},{2,0},{3,1},{4,6},{5,7},{6,4},{7,5},{8,10},{9,11},{10,... | collective-permute-start | bytes 24584 | tf_op jit(solution)/shard_map/ppermute | solution.py:284
  92.8 1.9 %collective-permute-done.5 = f32[2,2,1,1,8,64]{5,4,3,2,1,0:T(8,128)S(1)} collective-permute-done((f32[2,2,1,1,8,64]{5,4,3,2,1,0:T(8,128)S(1)}, f32[2,2,1,1,8,64]{5,4,3,2,1,0:T(8,128)S(1)}, u32[]{:S(2)}, u32[]{:S(2)}) %collective-permute-start.5) | collective-permute-done | bytes 8224 | tf_op jit(solution)/shard_map/ppermute | solution.py:284
  94.7 2.9 %collective-permute-start.7 = (f32[2,1,1,1,8,64]{5,4,3,2,1,0:T(8,128)S(1)}, f32[2,1,1,1,8,64]{5,4,3,2,1,0:T(8,128)S(1)}, u32[]{:S(2)}, u32[]{:S(2)}) collective-permute-start(f32[2,1,1,1,8,64]{5,4,3,2,1,0:T(8,128)S(1)} %get-tuple-element.54), channel_id=1, source_target_pairs={{0,4},{1,5},{2,6},{3,7},{4,0},{5,1},{6,2},{7,3},{8,12},{9,13},{10,... | collective-permute-start | bytes 12296 | tf_op jit(solution)/shard_map/ppermute | solution.py:284
  97.6 1.7 %collective-permute-done.7 = f32[2,1,1,1,8,64]{5,4,3,2,1,0:T(8,128)S(1)} collective-permute-done((f32[2,1,1,1,8,64]{5,4,3,2,1,0:T(8,128)S(1)}, f32[2,1,1,1,8,64]{5,4,3,2,1,0:T(8,128)S(1)}, u32[]{:S(2)}, u32[]{:S(2)}) %collective-permute-start.7) | collective-permute-done | bytes 4128 | tf_op jit(solution)/shard_map/ppermute | solution.py:284
  99.5 4.7 %collective-permute-done.4 = bf16[2,2,1,8,64,128]{5,4,3,2,1,0:T(8,128)(2,1)S(1)} collective-permute-done((bf16[2,2,1,8,64,128]{5,4,3,2,1,0:T(8,128)(2,1)S(1)}, bf16[2,2,1,8,64,128]{5,4,3,2,1,0:T(8,128)(2,1)S(1)}, u32[]{:S(2)}, u32[]{:S(2)}) %collective-permute-start.4) | collective-permute-done | bytes 524320 | tf_op jit(solution)/shard_map/ppermute | solution.py:285
  104.3 1.8 %multiply_add_fusion = f32[2,2,1,8,64,128]{5,4,3,2,1,0:T(8,128)S(1)} fusion(bf16[2,2,1,8,64,128]{5,4,3,2,1,0:T(8,128)(2,1)S(1)} %collective-permute-done.4, f32[2,2,2,8,64,128]{5,4,3,2,1,0:T(8,128)} %bitcast.183, s32[]{:T(128)S(6)} %select_n.255, f32[2,2,8,64]{3,2,1,0:T(8,128)S(1)} %get-tuple-element.44, f32[2,2,8,64]{3,2,1,0:T(8,128)S(1)} %get-tuple-element.43), kind=kLoop, calls=%fused_computation.17 | loop fusion | flops 1048576 | bytes 2637828 | tf_op jit(solution)/shard_map/add | solution.py:294
  106.2 1.6 %collective-permute-start.6 = (bf16[2,1,1,8,64,128]{5,4,3,2,1,0:T(8,128)(2,1)S(1)}, bf16[2,1,1,8,64,128]{5,4,3,2,1,0:T(8,128)(2,1)S(1)}, u32[]{:S(2)}, u32[]{:S(2)}) collective-permute-start(bf16[2,1,1,8,64,128]{5,4,3,2,1,0:T(8,128)(2,1)S(1)} %dynamic-slice_convert_fusion.1), channel_id=1, source_target_pairs={{0,2},{1,3},{2,0},{3,1},{4,6},{5,7},{6,4},{7,5},{8,10},{9,11},{10,... | collective-permute-start | bytes 786440 | tf_op jit(solution)/shard_map/ppermute | solution.py:285
  108.3 0.2 convolution_multiply_fusion
  108.6 4.8 %collective-permute-done.6 = bf16[2,1,1,8,64,128]{5,4,3,2,1,0:T(8,128)(2,1)S(1)} collective-permute-done((bf16[2,1,1,8,64,128]{5,4,3,2,1,0:T(8,128)(2,1)S(1)}, bf16[2,1,1,8,64,128]{5,4,3,2,1,0:T(8,128)(2,1)S(1)}, u32[]{:S(2)}, u32[]{:S(2)}) %collective-permute-start.6) | collective-permute-done | bytes 262176 | tf_op jit(solution)/shard_map/ppermute | solution.py:285
  113.4 0.3 multiply_add_fusion.1
  113.8 2.7 %collective-permute-start.8 = (bf16[1,1,1,8,64,128]{5,4,3,2,1,0:T(8,128)(2,1)S(1)}, bf16[1,1,1,8,64,128]{5,4,3,2,1,0:T(8,128)(2,1)S(1)}, u32[]{:S(2)}, u32[]{:S(2)}) collective-permute-start(bf16[1,1,1,8,64,128]{5,4,3,2,1,0:T(8,128)(2,1)S(1)} %dynamic-slice_convert_fusion.2), channel_id=1, source_target_pairs={{0,4},{1,5},{2,6},{3,7},{4,0},{5,1},{6,2},{7,3},{8,12},{9,13},{10,... | collective-permute-start | bytes 393224 | tf_op jit(solution)/shard_map/ppermute | solution.py:285
  116.5 4.7 %collective-permute-done.8 = bf16[1,1,1,8,64,128]{5,4,3,2,1,0:T(8,128)(2,1)S(1)} collective-permute-done((bf16[1,1,1,8,64,128]{5,4,3,2,1,0:T(8,128)(2,1)S(1)}, bf16[1,1,1,8,64,128]{5,4,3,2,1,0:T(8,128)(2,1)S(1)}, u32[]{:S(2)}, u32[]{:S(2)}) %collective-permute-start.8) | collective-permute-done | bytes 131104 | tf_op jit(solution)/shard_map/ppermute | solution.py:285
  121.1 0.2 multiply_add_fusion.2
  121.3 0.3 fusion.12
  121.8 2.0 %all_gather.4 = bf16[2,8,4,2048]{3,1,2,0:T(8,128)(2,1)S(1)} all-gather(bf16[1,8,4,2048]{3,1,2,0:T(8,128)(2,1)S(1)} %convert_element_type.114), channel_id=1, replica_groups=mesh['row'=2,'col'=2,'seq'=8] {'row'}, dimensions={0}, use_global_device_ids=true | all-gather | bytes 393216 | tf_op jit(solution)/shard_map/all_gather | solution.py:413
  123.8 5.9 %fusion.2 = bf16[2,8,4,2560]{3,1,2,0:T(8,128)(2,1)S(1)} fusion(bf16[2,8,4,2048]{3,1,2,0:T(8,128)(2,1)S(1)} %all_gather.4, bf16[2048,2560]{1,0:T(8,128)(2,1)} %param.16), kind=kOutput, calls=%fused_computation.2 | convolution fusion | flops 671252480 | bytes 11075584 | tf_op jit(solution)/shard_map/dot_general | solution.py:415
  129.7 1.6 collective-permute-start.9
  131.3 0.8 reshape_reshape.8
  132.1 4.0 %collective-permute-done.9 = bf16[1,8,4,2560]{3,1,2,0:T(8,128)(2,1)S(1)} collective-permute-done((bf16[1,8,4,2560]{3,1,2,0:T(8,128)(2,1)S(1)}, bf16[1,8,4,2560]{3,1,2,0:T(8,128)(2,1)S(1)}, u32[]{:S(2)}, u32[]{:S(2)}) %collective-permute-start.9) | collective-permute-done | bytes 163872 | tf_op jit(solution)/shard_map/ppermute | solution.py:237
  136.1 1.3 collective-permute-start.10
  137.5 0.4 pad_maximum_fusion.7
  137.8 0.8 convert_element_type.120
  138.6 1.6 %collective-permute-start.13 = (bf16[1,8,4,1280]{3,1,2,0:T(8,128)(2,1)S(1)}, bf16[1,8,4,1280]{3,1,2,0:T(8,128)(2,1)S(1)}, u32[]{:S(2)}, u32[]{:S(2)}) collective-permute-start(bf16[1,8,4,1280]{3,1,2,0:T(8,128)(2,1)S(1)} %get-tuple-element.39), channel_id=1, source_target_pairs={{0,4},{1,5},{2,6},{3,7},{4,0},{5,1},{6,2},{7,3},{8,12},{9,13},{10,... | collective-permute-start | bytes 245768 | tf_op jit(solution)/shard_map/ppermute | solution.py:253
  140.3 2.8 %collective-permute-done.10 = bf16[1,8,4,1280]{3,1,2,0:T(8,128)(2,1)S(1)} collective-permute-done((bf16[1,8,4,1280]{3,1,2,0:T(8,128)(2,1)S(1)}, bf16[1,8,4,1280]{3,1,2,0:T(8,128)(2,1)S(1)}, u32[]{:S(2)}, u32[]{:S(2)}) %collective-permute-start.10) | collective-permute-done | bytes 81952 | tf_op jit(solution)/shard_map/ppermute | solution.py:253
  143.1 1.4 collective-permute-start.11
  144.5 0.7 collective-permute-done.13
  145.3 0.5 collective-permute-start.14
  145.8 5.0 %collective-permute-done.14 = bf16[2,1,8,4,1280]{4,2,3,1,0:T(8,128)(2,1)S(1)} collective-permute-done((bf16[2,1,8,4,1280]{4,2,3,1,0:T(8,128)(2,1)S(1)}, bf16[2,1,8,4,1280]{4,2,3,1,0:T(8,128)(2,1)S(1)}, u32[]{:S(2)}, u32[]{:S(2)}) %collective-permute-start.14) | collective-permute-done | bytes 163872 | tf_op jit(solution)/shard_map/ppermute | solution.py:253
  150.8 1.4 collective-permute-start.15
  152.3 0.6 collective-permute-start.12
  152.9 6.0 %collective-permute-done.15 = bf16[2,2,1,8,4,1280]{5,3,4,1,2,0:T(8,128)(2,1)S(1)} collective-permute-done((bf16[2,2,1,8,4,1280]{5,3,4,1,2,0:T(8,128)(2,1)S(1)}, bf16[2,2,1,8,4,1280]{5,3,4,1,2,0:T(8,128)(2,1)S(1)}, u32[]{:S(2)}, u32[]{:S(2)}) %collective-permute-start.15) | collective-permute-done | bytes 327712 | tf_op jit(solution)/shard_map/ppermute | solution.py:253
  159.1 0.4 collective-permute-done.12
  159.8 2.1 %copy.120 = bf16[64,4,2560]{2,1,0:T(4,128)(2,1)} copy(bf16[64,4,2560]{2,0,1:T(8,128)(2,1)S(1)} %pad_maximum_fusion.2) | data formatting | bytes 2621440
  (72 shorter events, 2.8 us)
Async XLA Ops:
  0.6 38.5 %copy-start = (bf16[2560,512]{1,0:T(8,128)(2,1)S(1)}, bf16[2560,512]{1,0:T(8,128)(2,1)}, u32[]{:S(2)}) copy-start(bf16[2560,512]{1,0:T(8,128)(2,1)} %param.14) | copy-start | bytes 7864324
  0.6 35.6 %copy-start.5 = (f32[2560]{0:T(1024)S(1)}, f32[2560]{0:T(1024)}, u32[]{:S(2)}) copy-start(f32[2560]{0:T(1024)} %param.12) | copy-start | bytes 30724
  4.2 32.0 %collective-permute-start = (bf16[256,2560]{1,0:T(8,128)(2,1)}, bf16[256,2560]{1,0:T(8,128)(2,1)}, u32[]{:S(2)}, u32[]{:S(2)}) collective-permute-start(bf16[256,2560]{1,0:T(8,128)(2,1)} %reshape.1228), channel_id=1, source_target_pairs={{0,8},{8,0},{1,9},{9,1},{2,10},{10,2},{3,11},{11,3},{4,12},{12,4},... | collective-permute-start | bytes 3932168 | tf_op jit(solution)/shard_map/ppermute | solution.py:327
  11.8 24.4 %collective-permute-start.1 = (f32[256]{0:T(256)S(1)}, f32[256]{0:T(256)S(1)}, u32[]{:S(2)}, u32[]{:S(2)}) collective-permute-start(f32[256]{0:T(256)S(1)} %psum.7), channel_id=1, source_target_pairs={{0,8},{8,0},{1,9},{9,1},{2,10},{10,2},{3,11},{11,3},{4,12},{12,4},... | collective-permute-start | bytes 3080 | tf_op jit(solution)/shard_map/ppermute | solution.py:330
  36.3 4.4 %copy-start.7 = (bf16[2560,512]{1,0:T(8,128)(2,1)S(1)}, bf16[2560,512]{1,0:T(8,128)(2,1)}, u32[]{:S(2)}) copy-start(bf16[2560,512]{1,0:T(8,128)(2,1)} %param.15) | copy-start | bytes 7864324
  39.1 3.1 %slice-start = ((s8[10485760]{0:T(1024)(128)(4,1)}), s8[4194304]{0:T(1024)(128)(4,1)S(1)}, s32[]{:S(2)}) async-start(s8[10485760]{0:T(1024)(128)(4,1)} %bitcast.206), calls=%async_computation | async-start | bytes 8388608
  39.1 3.5 %slice-start.1 = ((s8[10485760]{0:T(1024)(128)(4,1)}), s8[4194304]{0:T(1024)(128)(4,1)S(1)}, s32[]{:S(2)}) async-start(s8[10485760]{0:T(1024)(128)(4,1)} %bitcast.206), calls=%async_computation.1 | async-start | bytes 8388608
  40.7 2.7 %slice-start.2 = ((s8[10485760]{0:T(1024)(128)(4,1)}), s8[2097152]{0:T(1024)(128)(4,1)S(1)}, s32[]{:S(2)}) async-start(s8[10485760]{0:T(1024)(128)(4,1)} %bitcast.206), calls=%async_computation.2 | async-start | bytes 4194304
  49.5 1.6 %copy-start.2 = (bf16[2,256,3072]{2,1,0:T(8,128)(2,1)}, bf16[2,256,3072]{2,1,0:T(8,128)(2,1)S(1)}, u32[]{:S(2)}) copy-start(bf16[2,256,3072]{2,1,0:T(8,128)(2,1)S(1)} %pad_maximum_fusion) | copy-start | bytes 9437188
  51.1 1.3 copy-start.6
  52.4 3.6 %collective-permute-start.2 = (bf16[1,256,3072]{2,1,0:T(8,128)(2,1)}, bf16[1,256,3072]{2,1,0:T(8,128)(2,1)S(1)}, u32[]{:S(2)}, u32[]{:S(2)}) collective-permute-start(bf16[1,256,3072]{2,1,0:T(8,128)(2,1)} %constant_dynamic-slice_fusion.2), channel_id=1, source_target_pairs={{0,16},{16,0},{1,17},{17,1},{2,18},{18,2},{3,19},{19,3},{4,20},{20... | collective-permute-start | bytes 4718600 | tf_op jit(solution)/shard_map/ppermute | solution.py:237
  61.8 2.4 %copy-start.3 = (bf16[64,4,4,4,128]{4,3,1,2,0:T(4,128)(2,1)}, bf16[64,4,4,4,128]{4,3,1,2,0:T(4,128)(2,1)S(1)}, u32[]{:S(2)}) copy-start(bf16[64,4,4,4,128]{4,3,1,2,0:T(4,128)(2,1)S(1)} %copy.124) | copy-start | bytes 3145732
  83.8 2.4 %copy-start.4 = (f32[64,64,1]{2,1,0:T(8,128)S(1)}, f32[64,64,1]{2,1,0:T(8,128)}, u32[]{:S(2)}) copy-start(f32[64,64,1]{2,1,0:T(8,128)} %get-tuple-element.8) | copy-start | bytes 49156
  86.8 4.0 %collective-permute-start.3 = (f32[2,2,2,1,8,64]{5,4,3,2,1,0:T(8,128)S(1)}, f32[2,2,2,1,8,64]{5,4,3,2,1,0:T(8,128)S(1)}, u32[]{:S(2)}, u32[]{:S(2)}) collective-permute-start(f32[2,2,2,1,8,64]{5,4,3,2,1,0:T(8,128)S(1)} %get-tuple-element.46), channel_id=1, source_target_pairs={{0,1},{1,0},{2,3},{3,2},{4,5},{5,4},{6,7},{7,6},{8,9},{9,8},{10,11... | collective-permute-start | bytes 49160 | tf_op jit(solution)/shard_map/ppermute | solution.py:284
  90.5 13.8 %collective-permute-start.4 = (bf16[2,2,1,8,64,128]{5,4,3,2,1,0:T(8,128)(2,1)S(1)}, bf16[2,2,1,8,64,128]{5,4,3,2,1,0:T(8,128)(2,1)S(1)}, u32[]{:S(2)}, u32[]{:S(2)}) collective-permute-start(bf16[2,2,1,8,64,128]{5,4,3,2,1,0:T(8,128)(2,1)S(1)} %dynamic-slice_convert_fusion), channel_id=1, source_target_pairs={{0,1},{1,0},{2,3},{3,2},{4,5},{5,4},{6,7},{7,6},{8,9},{9,8},{10,11... | collective-permute-start | bytes 1572872 | tf_op jit(solution)/shard_map/ppermute | solution.py:285
  90.9 3.8 %collective-permute-start.5 = (f32[2,2,1,1,8,64]{5,4,3,2,1,0:T(8,128)S(1)}, f32[2,2,1,1,8,64]{5,4,3,2,1,0:T(8,128)S(1)}, u32[]{:S(2)}, u32[]{:S(2)}) collective-permute-start(f32[2,2,1,1,8,64]{5,4,3,2,1,0:T(8,128)S(1)} %get-tuple-element.50), channel_id=1, source_target_pairs={{0,2},{1,3},{2,0},{3,1},{4,6},{5,7},{6,4},{7,5},{8,10},{9,11},{10,... | collective-permute-start | bytes 24584 | tf_op jit(solution)/shard_map/ppermute | solution.py:284
  94.7 4.6 %collective-permute-start.7 = (f32[2,1,1,1,8,64]{5,4,3,2,1,0:T(8,128)S(1)}, f32[2,1,1,1,8,64]{5,4,3,2,1,0:T(8,128)S(1)}, u32[]{:S(2)}, u32[]{:S(2)}) collective-permute-start(f32[2,1,1,1,8,64]{5,4,3,2,1,0:T(8,128)S(1)} %get-tuple-element.54), channel_id=1, source_target_pairs={{0,4},{1,5},{2,6},{3,7},{4,0},{5,1},{6,2},{7,3},{8,12},{9,13},{10,... | collective-permute-start | bytes 12296 | tf_op jit(solution)/shard_map/ppermute | solution.py:284
  106.2 7.3 %collective-permute-start.6 = (bf16[2,1,1,8,64,128]{5,4,3,2,1,0:T(8,128)(2,1)S(1)}, bf16[2,1,1,8,64,128]{5,4,3,2,1,0:T(8,128)(2,1)S(1)}, u32[]{:S(2)}, u32[]{:S(2)}) collective-permute-start(bf16[2,1,1,8,64,128]{5,4,3,2,1,0:T(8,128)(2,1)S(1)} %dynamic-slice_convert_fusion.1), channel_id=1, source_target_pairs={{0,2},{1,3},{2,0},{3,1},{4,6},{5,7},{6,4},{7,5},{8,10},{9,11},{10,... | collective-permute-start | bytes 786440 | tf_op jit(solution)/shard_map/ppermute | solution.py:285
  113.8 7.3 %collective-permute-start.8 = (bf16[1,1,1,8,64,128]{5,4,3,2,1,0:T(8,128)(2,1)S(1)}, bf16[1,1,1,8,64,128]{5,4,3,2,1,0:T(8,128)(2,1)S(1)}, u32[]{:S(2)}, u32[]{:S(2)}) collective-permute-start(bf16[1,1,1,8,64,128]{5,4,3,2,1,0:T(8,128)(2,1)S(1)} %dynamic-slice_convert_fusion.2), channel_id=1, source_target_pairs={{0,4},{1,5},{2,6},{3,7},{4,0},{5,1},{6,2},{7,3},{8,12},{9,13},{10,... | collective-permute-start | bytes 393224 | tf_op jit(solution)/shard_map/ppermute | solution.py:285
  129.7 6.3 %collective-permute-start.9 = (bf16[1,8,4,2560]{3,1,2,0:T(8,128)(2,1)S(1)}, bf16[1,8,4,2560]{3,1,2,0:T(8,128)(2,1)S(1)}, u32[]{:S(2)}, u32[]{:S(2)}) collective-permute-start(bf16[1,8,4,2560]{3,1,2,0:T(8,128)(2,1)S(1)} %constant_dynamic-slice_fusion.1), channel_id=1, source_target_pairs={{0,8},{8,0},{1,9},{9,1},{2,10},{10,2},{3,11},{11,3},{4,12},{12,4},... | collective-permute-start | bytes 491528 | tf_op jit(solution)/shard_map/ppermute | solution.py:237
  136.1 6.9 %collective-permute-start.10 = (bf16[1,8,4,1280]{3,1,2,0:T(8,128)(2,1)S(1)}, bf16[1,8,4,1280]{3,1,2,0:T(8,128)(2,1)S(1)}, u32[]{:S(2)}, u32[]{:S(2)}) collective-permute-start(bf16[1,8,4,1280]{3,1,2,0:T(8,128)(2,1)S(1)} %get-tuple-element.38), channel_id=1, source_target_pairs={{0,4},{1,5},{2,6},{3,7},{4,0},{5,1},{6,2},{7,3},{8,12},{9,13},{10,... | collective-permute-start | bytes 245768 | tf_op jit(solution)/shard_map/ppermute | solution.py:253
  138.6 6.6 %collective-permute-start.13 = (bf16[1,8,4,1280]{3,1,2,0:T(8,128)(2,1)S(1)}, bf16[1,8,4,1280]{3,1,2,0:T(8,128)(2,1)S(1)}, u32[]{:S(2)}, u32[]{:S(2)}) collective-permute-start(bf16[1,8,4,1280]{3,1,2,0:T(8,128)(2,1)S(1)} %get-tuple-element.39), channel_id=1, source_target_pairs={{0,4},{1,5},{2,6},{3,7},{4,0},{5,1},{6,2},{7,3},{8,12},{9,13},{10,... | collective-permute-start | bytes 245768 | tf_op jit(solution)/shard_map/ppermute | solution.py:253
  143.1 9.2 %collective-permute-start.11 = (bf16[2,1,8,4,1280]{4,2,3,0,1:T(8,128)(2,1)S(1)}, bf16[2,1,8,4,1280]{4,2,3,0,1:T(8,128)(2,1)S(1)}, u32[]{:S(2)}, u32[]{:S(2)}) collective-permute-start(bf16[2,1,8,4,1280]{4,2,3,0,1:T(8,128)(2,1)S(1)} %maximum_select_fusion.6), channel_id=1, source_target_pairs={{0,2},{1,3},{2,0},{3,1},{4,6},{5,7},{6,4},{7,5},{8,10},{9,11},{10,... | collective-permute-start | bytes 491528 | tf_op jit(solution)/shard_map/ppermute | solution.py:253
  145.3 5.5 %collective-permute-start.14 = (bf16[2,1,8,4,1280]{4,2,3,1,0:T(8,128)(2,1)S(1)}, bf16[2,1,8,4,1280]{4,2,3,1,0:T(8,128)(2,1)S(1)}, u32[]{:S(2)}, u32[]{:S(2)}) collective-permute-start(bf16[2,1,8,4,1280]{4,2,3,1,0:T(8,128)(2,1)S(1)} %bitcast_select_fusion), channel_id=1, source_target_pairs={{0,1},{1,0},{2,3},{3,2},{4,5},{5,4},{6,7},{7,6},{8,9},{9,8},{10,11... | collective-permute-start | bytes 491528 | tf_op jit(solution)/shard_map/ppermute | solution.py:253
  150.8 8.1 %collective-permute-start.15 = (bf16[2,2,1,8,4,1280]{5,3,4,1,2,0:T(8,128)(2,1)S(1)}, bf16[2,2,1,8,4,1280]{5,3,4,1,2,0:T(8,128)(2,1)S(1)}, u32[]{:S(2)}, u32[]{:S(2)}) collective-permute-start(bf16[2,2,1,8,4,1280]{5,3,4,1,2,0:T(8,128)(2,1)S(1)} %maximum_select_fusion.5), channel_id=1, source_target_pairs={{0,2},{1,3},{2,0},{3,1},{4,6},{5,7},{6,4},{7,5},{8,10},{9,11},{10,... | collective-permute-start | bytes 983048 | tf_op jit(solution)/shard_map/ppermute | solution.py:253
  152.3 7.2 %collective-permute-start.12 = (bf16[2,2,1,8,4,1280]{5,3,4,1,2,0:T(8,128)(2,1)S(1)}, bf16[2,2,1,8,4,1280]{5,3,4,1,2,0:T(8,128)(2,1)S(1)}, u32[]{:S(2)}, u32[]{:S(2)}) collective-permute-start(bf16[2,2,1,8,4,1280]{5,3,4,1,2,0:T(8,128)(2,1)S(1)} %maximum_select_fusion.3), channel_id=1, source_target_pairs={{0,1},{1,0},{2,3},{3,2},{4,5},{5,4},{6,7},{7,6},{8,9},{9,8},{10,11... | collective-permute-start | bytes 983048 | tf_op jit(solution)/shard_map/ppermute | solution.py:253
  159.7 2.2 %copy-start.1 = (bf16[2560,512]{1,0:T(8,128)(2,1)S(1)}, bf16[2560,512]{1,0:T(8,128)(2,1)}, u32[]{:S(2)}) copy-start(bf16[2560,512]{1,0:T(8,128)(2,1)} %param.14) | copy-start | bytes 7864324

commit v17 on v16

--- a/solution.py
+++ b/solution.py
@@ -178,13 +178,15 @@
         )
         results.append((owner, peak, total, acc))
     for owner, peak, total, acc in results:
-        old = peak_ref[owner]
+        old = jnp.transpose(peak_ref[owner])
         top = jnp.maximum(old, peak)
         old_factor = jnp.exp(old - top)
         new_factor = jnp.exp(peak - top)
-        tot_ref[owner] = tot_ref[owner] * old_factor + total * new_factor
+        tot_ref[owner] = jnp.transpose(
+            jnp.transpose(tot_ref[owner]) * old_factor + total * new_factor
+        )
         acc_ref[owner] = acc_ref[owner] * old_factor + acc * new_factor
-        peak_ref[owner] = top
+        peak_ref[owner] = jnp.transpose(top)
 
 def slot_attention(queries, lengths, slot_request, block_numbers, keys, values, heads, qpk):
     req_count, rows, head = queries.shape
@@ -201,8 +203,8 @@
             pl.BlockSpec((ns, width, values.shape[2]), lambda n, sr, lr, br: (n, 0, 0)),
         ],
         out_specs=[
-            pl.BlockSpec((req_count, rows, 1), fixed),
-            pl.BlockSpec((req_count, rows, 1), fixed),
+            pl.BlockSpec((req_count, 1, rows), fixed),
+            pl.BlockSpec((req_count, 1, rows), fixed),
             pl.BlockSpec((req_count, rows, head), fixed),
         ],
     )
@@ -210,8 +212,8 @@
         partial(slot_kernel, ns=ns, heads=heads, qpk=qpk),
         grid_spec=grid_spec,
         out_shape=[
-            jax.ShapeDtypeStruct((req_count, rows, 1), jnp.float32),
-            jax.ShapeDtypeStruct((req_count, rows, 1), jnp.float32),
+            jax.ShapeDtypeStruct((req_count, 1, rows), jnp.float32),
+            jax.ShapeDtypeStruct((req_count, 1, rows), jnp.float32),
             jax.ShapeDtypeStruct((req_count, rows, head), jnp.float32),
         ],
     )(slot_request, lengths, block_numbers, queries, keys, values)
@@ -382,8 +384,8 @@
         heads_kv,
         QUERY_PER_KEY,
     )
-    local_peak = local_peak[..., 0]
-    local_totals = local_totals[..., 0]
+    local_peak = local_peak[:, 0]
+    local_totals = local_totals[:, 0]
     n_seq = lax.axis_size("seq")
     per = req_count // n_seq
     seq_index = lax.axis_index("seq")

time: 162 us -> 163 us (level)
  Pallas kernels: 19.7 us -> 22.7 us
  other arithmetic: 17.5 us -> 15.3 us
    pallas_call x1, Pallas kernels: 19.7 us -> 22.7 us  [slot_attention(): pl.pallas_call(partial(slot_kernel, ns=ns, heads=heads, qpk=qpk), grid_sp...]
    pallas_call x2 -> x0, other arithmetic: 2.97 us -> none  [slot_attention(): pl.pallas_call(partial(slot_kernel, ns=ns, heads=heads, qpk=qpk), grid_sp...]
    unnamed x24 -> x22, local copies, waits for them, and re-layouts: 5.49 us -> 5.49 us
  transfers between devices with their start and end apart: 16 -> 16, of which waited for: 13 -> 14; matrix products, arithmetic and copies ran while one was open for 5% -> 5% of each run, Pallas kernels for 0% -> 0%
where the time goes in v17:
time: 163 us
  waiting for transfers between devices  64 us (39%)
  starting transfers between devices  22.7 us (14%)
  Pallas kernels  22.7 us (14%)
  local copies, waits for them, and re-layouts  16.2 us (10%)
  matrix products  16.2 us (10%)
  other arithmetic  15.3 us (9%)
  blocking collectives  4.46 us (3%)
    ppermute x1, waiting for transfers between devices, on_device(): other_squares = lax.ppermute(squares, 'col', swap)  24.4 us
    pallas_call x1, Pallas kernels, slot_attention(): pl.pallas_call(partial(slot_kernel, ns=ns, heads=heads, qpk=qpk), grid_sp...  22.7 us
    ppermute x6, waiting for transfers between devices, doubling_gather(): got = lax.ppermute(block, axis_name, pairs)  14.8 us
    ppermute x3, waiting for transfers between devices, seq_merge(): lax.ppermute(send_values.astype(jnp.bfloat16), 'seq', pairs)  14.3 us
    dot_general x3, matrix products, on_device(): jnp.dot(gathered, matrix, preferred_element_type=jnp.float32)  8.8 us
    ppermute x6, starting transfers between devices, doubling_gather(): got = lax.ppermute(block, axis_name, pairs)  7.01 us
    ppermute x2, waiting for transfers between devices, pair_scatter(): got = lax.ppermute(send, axis_name, [(0, 1), (1, 0)])  6.82 us
    ppermute x3, starting transfers between devices, seq_merge(): got_stats = lax.ppermute(send_stats, 'seq', pairs)  6.62 us
  transfers between devices with their start and end apart: 16, of which 14 were waited for; matrix products, arithmetic and copies ran while one was open for 5% of the time, Pallas kernels for 0%

profile of v17, /device:TPU:0, one launch (start us, length us, event | category | flops | bytes accessed | tf_op | source)
XLA Modules:
  0.0 162.7 jit_solution(12251007864203653998)
XLA Ops:
  0.7 3.5 %reshape.1228 = bf16[256,2560]{1,0:T(8,128)(2,1)} reshape(bf16[64,4,2560]{2,1,0:T(4,128)(2,1)} %param.11) | data formatting | bytes 2621440 | tf_op jit(solution)/shard_map/reshape | solution.py:326
  4.2 2.9 %collective-permute-start = (bf16[256,2560]{1,0:T(8,128)(2,1)}, bf16[256,2560]{1,0:T(8,128)(2,1)}, u32[]{:S(2)}, u32[]{:S(2)}) collective-permute-start(bf16[256,2560]{1,0:T(8,128)(2,1)} %reshape.1228), channel_id=1, source_target_pairs={{0,8},{8,0},{1,9},{9,1},{2,10},{10,2},{3,11},{11,3},{4,12},{12,4},... | collective-permute-start | bytes 3932168 | tf_op jit(solution)/shard_map/ppermute | solution.py:329
  7.1 2.1 %multiply_reduce_fusion = f32[64,4]{1,0:T(8,128)S(1)} fusion(bf16[64,4,2560]{2,1,0:T(4,128)(2,1)} %param.11), kind=kLoop, calls=%fused_computation.9 | loop fusion | flops 1965824 | bytes 1311744 | tf_op jit(solution)/shard_map/reduce_sum | solution.py:331
  9.3 2.5 %psum.7 = f32[256]{0:T(256)S(1)} all-reduce(f32[256]{0:T(256)S(1)} %reduce_sum.21), channel_id=1, replica_groups=mesh['row'=2,'col'=2,'seq'=8] {'row'}, use_global_device_ids=true, to_apply=%region_1.0 | all-reduce | flops 256 | bytes 2048 | tf_op jit(solution)/shard_map/psum | solution.py:331
  11.8 24.4 %collective-permute-done.1 = f32[256]{0:T(256)S(1)} collective-permute-done((f32[256]{0:T(256)S(1)}, f32[256]{0:T(256)S(1)}, u32[]{:S(2)}, u32[]{:S(2)}) %collective-permute-start.1) | collective-permute-done | bytes 1056 | tf_op jit(solution)/shard_map/ppermute | solution.py:332
  36.3 2.8 %multiply_convert_fusion.1 = (bf16[256,2560]{1,0:T(8,128)(2,1)S(1)}, bf16[256,2560]{1,0:T(8,128)(2,1)S(1)}) fusion(f32[2560]{0:T(1024)S(1)} %copy-done.4, f32[256]{0:T(256)S(1)} %get-tuple-element.55, bf16[256,2560]{1,0:T(8,128)(2,1)} %reshape.1228, bf16[256,2560]{1,0:T(8,128)(2,1)} %collective-permute-done, pred[]{:T(512)S(6)} %eq.18, ...), kind=kLoop, calls=%fused_computation.8 | loop fusion | flops 6553600 | bytes 5255169 | tf_op jit(solution)/shard_map/convert_element_type | solution.py:336
  39.1 1.5 convolution_convert_fusion.1
  40.7 1.5 convolution_convert_fusion.2
  42.2 0.4 slice-done.1
  42.6 0.8 slice-done.2
  43.4 5.8 %convolution_convert_fusion = bf16[512,2048]{1,0:T(8,128)(2,1)S(1)} fusion(bf16[2560,2048]{1,0:T(8,128)(2,1)S(1)} %bitcast.177, bf16[256,2560]{1,0:T(8,128)(2,1)S(1)} %get-tuple-element.32, bf16[256,2560]{1,0:T(8,128)(2,1)S(1)} %get-tuple-element.31), kind=kOutput, calls=%fused_computation.5 | convolution fusion | flops 5375000576 | bytes 15204352 | tf_op jit(solution)/shard_map/dot_general | solution.py:351
  49.2 0.3 pad_maximum_fusion
  49.5 1.6 %copy-done.2 = bf16[2,256,3072]{2,1,0:T(8,128)(2,1)} copy-done((bf16[2,256,3072]{2,1,0:T(8,128)(2,1)}, bf16[2,256,3072]{2,1,0:T(8,128)(2,1)S(1)}, u32[]{:S(2)}) %copy-start.2) | copy-done | bytes 3145752
  51.1 1.3 constant_dynamic-slice_fusion.2
  52.6 0.5 multiply_cosine_fusion
  53.1 2.9 %collective-permute-done.2 = bf16[1,256,3072]{2,1,0:T(8,128)(2,1)S(1)} collective-permute-done((bf16[1,256,3072]{2,1,0:T(8,128)(2,1)}, bf16[1,256,3072]{2,1,0:T(8,128)(2,1)S(1)}, u32[]{:S(2)}, u32[]{:S(2)}) %collective-permute-start.2) | collective-permute-done | bytes 1572896 | tf_op jit(solution)/shard_map/ppermute | solution.py:239
  56.0 1.9 %add_bitcast_fusion = f32[32,8,24,128]{3,1,2,0:T(8,128)S(1)} fusion(bf16[1,256,3072]{2,1,0:T(8,128)(2,1)S(1)} %collective-permute-done.2, bf16[2,256,3072]{2,1,0:T(8,128)(2,1)} %copy-done.2, s32[]{:T(128)S(6)} %select_n.253), kind=kLoop, calls=%fused_computation.4 | loop fusion | flops 2359296 | bytes 6291460
  57.9 0.6 copy.148
  58.5 0.8 subtract_convert_fusion
  59.3 0.4 add_convert_fusion.1
  59.9 1.4 pad_maximum_fusion.3
  61.3 0.5 copy.132
  62.0 1.3 fusion.10
  63.3 0.5 copy.108
  64.2 22.7 %shard_map.130 = (f32[64,1,64]{2,1,0:T(1,128)}, f32[64,1,64]{2,1,0:T(1,128)}, f32[64,64,128]{2,1,0:T(8,128)}) custom-call(s32[50]{0:T(128)} %req_ref.1, s32[64]{0:T(128)} %len_ref.1, s32[50]{0:T(128)} %blk_ref.1, bf16[64,64,128]{2,1,0:T(8,128)(2,1)} %bitcast.143, bf16[50,128,512]{2,1,0:T(8,128)(2,1)} %k_ref.1, bf16[50,128,512]{2,1,0:T(8,128)(2,1)} %v_ref.1), custom_call_target="tpu_custom_call" | custom-call | tf_op jit(solution)/shard_map/pallas_call | solution.py:211
  86.9 0.8 fusion.19
  87.6 1.8 %collective-permute-start.3 = (f32[2,2,2,1,8,64]{5,4,3,2,1,0:T(8,128)S(1)}, f32[2,2,2,1,8,64]{5,4,3,2,1,0:T(8,128)S(1)}, u32[]{:S(2)}, u32[]{:S(2)}) collective-permute-start(f32[2,2,2,1,8,64]{5,4,3,2,1,0:T(8,128)S(1)} %get-tuple-element.46), channel_id=1, source_target_pairs={{0,1},{1,0},{2,3},{3,2},{4,5},{5,4},{6,7},{7,6},{8,9},{9,8},{10,11... | collective-permute-start | bytes 49160 | tf_op jit(solution)/shard_map/ppermute | solution.py:286
  89.5 1.3 dynamic-slice_convert_fusion
  90.8 0.5 copy.115
  91.3 0.3 collective-permute-start.4
  91.7 1.9 %collective-permute-start.5 = (f32[2,2,1,1,8,64]{5,4,3,2,1,0:T(8,128)S(1)}, f32[2,2,1,1,8,64]{5,4,3,2,1,0:T(8,128)S(1)}, u32[]{:S(2)}, u32[]{:S(2)}) collective-permute-start(f32[2,2,1,1,8,64]{5,4,3,2,1,0:T(8,128)S(1)} %get-tuple-element.50), channel_id=1, source_target_pairs={{0,2},{1,3},{2,0},{3,1},{4,6},{5,7},{6,4},{7,5},{8,10},{9,11},{10,... | collective-permute-start | bytes 24584 | tf_op jit(solution)/shard_map/ppermute | solution.py:286
  93.6 1.9 %collective-permute-done.5 = f32[2,2,1,1,8,64]{5,4,3,2,1,0:T(8,128)S(1)} collective-permute-done((f32[2,2,1,1,8,64]{5,4,3,2,1,0:T(8,128)S(1)}, f32[2,2,1,1,8,64]{5,4,3,2,1,0:T(8,128)S(1)}, u32[]{:S(2)}, u32[]{:S(2)}) %collective-permute-start.5) | collective-permute-done | bytes 8224 | tf_op jit(solution)/shard_map/ppermute | solution.py:286
  95.5 2.9 %collective-permute-start.7 = (f32[2,1,1,1,8,64]{5,4,3,2,1,0:T(8,128)S(1)}, f32[2,1,1,1,8,64]{5,4,3,2,1,0:T(8,128)S(1)}, u32[]{:S(2)}, u32[]{:S(2)}) collective-permute-start(f32[2,1,1,1,8,64]{5,4,3,2,1,0:T(8,128)S(1)} %get-tuple-element.54), channel_id=1, source_target_pairs={{0,4},{1,5},{2,6},{3,7},{4,0},{5,1},{6,2},{7,3},{8,12},{9,13},{10,... | collective-permute-start | bytes 12296 | tf_op jit(solution)/shard_map/ppermute | solution.py:286
  98.4 1.7 %collective-permute-done.7 = f32[2,1,1,1,8,64]{5,4,3,2,1,0:T(8,128)S(1)} collective-permute-done((f32[2,1,1,1,8,64]{5,4,3,2,1,0:T(8,128)S(1)}, f32[2,1,1,1,8,64]{5,4,3,2,1,0:T(8,128)S(1)}, u32[]{:S(2)}, u32[]{:S(2)}) %collective-permute-start.7) | collective-permute-done | bytes 4128 | tf_op jit(solution)/shard_map/ppermute | solution.py:286
  100.3 4.7 %collective-permute-done.4 = bf16[2,2,1,8,64,128]{5,4,3,2,1,0:T(8,128)(2,1)S(1)} collective-permute-done((bf16[2,2,1,8,64,128]{5,4,3,2,1,0:T(8,128)(2,1)S(1)}, bf16[2,2,1,8,64,128]{5,4,3,2,1,0:T(8,128)(2,1)S(1)}, u32[]{:S(2)}, u32[]{:S(2)}) %collective-permute-start.4) | collective-permute-done | bytes 524320 | tf_op jit(solution)/shard_map/ppermute | solution.py:287
  105.0 1.8 %multiply_add_fusion = f32[2,2,1,8,64,128]{5,4,3,2,1,0:T(8,128)S(1)} fusion(bf16[2,2,1,8,64,128]{5,4,3,2,1,0:T(8,128)(2,1)S(1)} %collective-permute-done.4, f32[2,2,2,8,64,128]{5,4,3,2,1,0:T(8,128)} %bitcast.153, s32[]{:T(128)S(6)} %select_n.255, f32[2,2,8,64]{3,2,1,0:T(8,128)S(1)} %get-tuple-element.44, f32[2,2,8,64]{3,2,1,0:T(8,128)S(1)} %get-tuple-element.43), kind=kLoop, calls=%fused_computation.17 | loop fusion | flops 1048576 | bytes 2637828 | tf_op jit(solution)/shard_map/add | solution.py:296
  106.9 1.6 %collective-permute-start.6 = (bf16[2,1,1,8,64,128]{5,4,3,2,1,0:T(8,128)(2,1)S(1)}, bf16[2,1,1,8,64,128]{5,4,3,2,1,0:T(8,128)(2,1)S(1)}, u32[]{:S(2)}, u32[]{:S(2)}) collective-permute-start(bf16[2,1,1,8,64,128]{5,4,3,2,1,0:T(8,128)(2,1)S(1)} %dynamic-slice_convert_fusion.1), channel_id=1, source_target_pairs={{0,2},{1,3},{2,0},{3,1},{4,6},{5,7},{6,4},{7,5},{8,10},{9,11},{10,... | collective-permute-start | bytes 786440 | tf_op jit(solution)/shard_map/ppermute | solution.py:287
  109.1 0.2 convolution_multiply_fusion
  109.4 4.9 %collective-permute-done.6 = bf16[2,1,1,8,64,128]{5,4,3,2,1,0:T(8,128)(2,1)S(1)} collective-permute-done((bf16[2,1,1,8,64,128]{5,4,3,2,1,0:T(8,128)(2,1)S(1)}, bf16[2,1,1,8,64,128]{5,4,3,2,1,0:T(8,128)(2,1)S(1)}, u32[]{:S(2)}, u32[]{:S(2)}) %collective-permute-start.6) | collective-permute-done | bytes 262176 | tf_op jit(solution)/shard_map/ppermute | solution.py:287
  114.2 0.3 multiply_add_fusion.1
  114.6 2.6 %collective-permute-start.8 = (bf16[1,1,1,8,64,128]{5,4,3,2,1,0:T(8,128)(2,1)S(1)}, bf16[1,1,1,8,64,128]{5,4,3,2,1,0:T(8,128)(2,1)S(1)}, u32[]{:S(2)}, u32[]{:S(2)}) collective-permute-start(bf16[1,1,1,8,64,128]{5,4,3,2,1,0:T(8,128)(2,1)S(1)} %dynamic-slice_convert_fusion.2), channel_id=1, source_target_pairs={{0,4},{1,5},{2,6},{3,7},{4,0},{5,1},{6,2},{7,3},{8,12},{9,13},{10,... | collective-permute-start | bytes 393224 | tf_op jit(solution)/shard_map/ppermute | solution.py:287
  117.2 4.7 %collective-permute-done.8 = bf16[1,1,1,8,64,128]{5,4,3,2,1,0:T(8,128)(2,1)S(1)} collective-permute-done((bf16[1,1,1,8,64,128]{5,4,3,2,1,0:T(8,128)(2,1)S(1)}, bf16[1,1,1,8,64,128]{5,4,3,2,1,0:T(8,128)(2,1)S(1)}, u32[]{:S(2)}, u32[]{:S(2)}) %collective-permute-start.8) | collective-permute-done | bytes 131104 | tf_op jit(solution)/shard_map/ppermute | solution.py:287
  121.9 0.2 multiply_add_fusion.2
  122.1 0.3 fusion.12
  122.6 2.0 %all_gather.4 = bf16[2,8,4,2048]{3,1,2,0:T(8,128)(2,1)S(1)} all-gather(bf16[1,8,4,2048]{3,1,2,0:T(8,128)(2,1)S(1)} %convert_element_type.114), channel_id=1, replica_groups=mesh['row'=2,'col'=2,'seq'=8] {'row'}, dimensions={0}, use_global_device_ids=true | all-gather | bytes 393216 | tf_op jit(solution)/shard_map/all_gather | solution.py:415
  124.6 5.9 %fusion.2 = bf16[2,8,4,2560]{3,1,2,0:T(8,128)(2,1)S(1)} fusion(bf16[2,8,4,2048]{3,1,2,0:T(8,128)(2,1)S(1)} %all_gather.4, bf16[2048,2560]{1,0:T(8,128)(2,1)} %param.16), kind=kOutput, calls=%fused_computation.2 | convolution fusion | flops 671252480 | bytes 11075584 | tf_op jit(solution)/shard_map/dot_general | solution.py:417
  130.5 1.6 collective-permute-start.9
  132.1 0.8 reshape_reshape.8
  132.9 4.0 %collective-permute-done.9 = bf16[1,8,4,2560]{3,1,2,0:T(8,128)(2,1)S(1)} collective-permute-done((bf16[1,8,4,2560]{3,1,2,0:T(8,128)(2,1)S(1)}, bf16[1,8,4,2560]{3,1,2,0:T(8,128)(2,1)S(1)}, u32[]{:S(2)}, u32[]{:S(2)}) %collective-permute-start.9) | collective-permute-done | bytes 163872 | tf_op jit(solution)/shard_map/ppermute | solution.py:239
  136.9 1.3 collective-permute-start.13
  138.2 0.4 pad_maximum_fusion.7
  138.6 0.8 convert_element_type.120
  139.4 1.7 %collective-permute-start.10 = (bf16[1,8,4,1280]{3,1,2,0:T(8,128)(2,1)S(1)}, bf16[1,8,4,1280]{3,1,2,0:T(8,128)(2,1)S(1)}, u32[]{:S(2)}, u32[]{:S(2)}) collective-permute-start(bf16[1,8,4,1280]{3,1,2,0:T(8,128)(2,1)S(1)} %get-tuple-element.38), channel_id=1, source_target_pairs={{0,4},{1,5},{2,6},{3,7},{4,0},{5,1},{6,2},{7,3},{8,12},{9,13},{10,... | collective-permute-start | bytes 245768 | tf_op jit(solution)/shard_map/ppermute | solution.py:255
  141.1 2.8 %collective-permute-done.13 = bf16[1,8,4,1280]{3,1,2,0:T(8,128)(2,1)S(1)} collective-permute-done((bf16[1,8,4,1280]{3,1,2,0:T(8,128)(2,1)S(1)}, bf16[1,8,4,1280]{3,1,2,0:T(8,128)(2,1)S(1)}, u32[]{:S(2)}, u32[]{:S(2)}) %collective-permute-start.13) | collective-permute-done | bytes 81952 | tf_op jit(solution)/shard_map/ppermute | solution.py:255
  143.9 0.4 collective-permute-start.14
  144.3 1.6 collective-permute-done.10
  145.9 1.7 %collective-permute-start.11 = (bf16[2,1,8,4,1280]{4,2,3,0,1:T(8,128)(2,1)S(1)}, bf16[2,1,8,4,1280]{4,2,3,0,1:T(8,128)(2,1)S(1)}, u32[]{:S(2)}, u32[]{:S(2)}) collective-permute-start(bf16[2,1,8,4,1280]{4,2,3,0,1:T(8,128)(2,1)S(1)} %maximum_select_fusion.6), channel_id=1, source_target_pairs={{0,2},{1,3},{2,0},{3,1},{4,6},{5,7},{6,4},{7,5},{8,10},{9,11},{10,... | collective-permute-start | bytes 491528 | tf_op jit(solution)/shard_map/ppermute | solution.py:255
  147.6 1.6 %collective-permute-done.14 = bf16[2,1,8,4,1280]{4,2,3,1,0:T(8,128)(2,1)S(1)} collective-permute-done((bf16[2,1,8,4,1280]{4,2,3,1,0:T(8,128)(2,1)S(1)}, bf16[2,1,8,4,1280]{4,2,3,1,0:T(8,128)(2,1)S(1)}, u32[]{:S(2)}, u32[]{:S(2)}) %collective-permute-start.14) | collective-permute-done | bytes 163872 | tf_op jit(solution)/shard_map/ppermute | solution.py:255
  149.3 1.4 collective-permute-start.15
  150.7 2.4 %collective-permute-done.11 = bf16[2,1,8,4,1280]{4,2,3,0,1:T(8,128)(2,1)S(1)} collective-permute-done((bf16[2,1,8,4,1280]{4,2,3,0,1:T(8,128)(2,1)S(1)}, bf16[2,1,8,4,1280]{4,2,3,0,1:T(8,128)(2,1)S(1)}, u32[]{:S(2)}, u32[]{:S(2)}) %collective-permute-start.11) | collective-permute-done | bytes 163872 | tf_op jit(solution)/shard_map/ppermute | solution.py:255
  153.2 0.5 collective-permute-start.12
  153.8 4.8 %collective-permute-done.15 = bf16[2,2,1,8,4,1280]{5,3,4,1,2,0:T(8,128)(2,1)S(1)} collective-permute-done((bf16[2,2,1,8,4,1280]{5,3,4,1,2,0:T(8,128)(2,1)S(1)}, bf16[2,2,1,8,4,1280]{5,3,4,1,2,0:T(8,128)(2,1)S(1)}, u32[]{:S(2)}, u32[]{:S(2)}) %collective-permute-start.15) | collective-permute-done | bytes 327712 | tf_op jit(solution)/shard_map/ppermute | solution.py:255
  158.8 1.5 collective-permute-done.12
  160.6 2.1 %copy.128 = bf16[64,4,2560]{2,1,0:T(4,128)(2,1)} copy(bf16[64,4,2560]{2,0,1:T(8,128)(2,1)S(1)} %pad_maximum_fusion.2) | data formatting | bytes 2621440
  (68 shorter events, 2.8 us)
Async XLA Ops:
  0.6 38.5 %copy-start = (bf16[2560,512]{1,0:T(8,128)(2,1)S(1)}, bf16[2560,512]{1,0:T(8,128)(2,1)}, u32[]{:S(2)}) copy-start(bf16[2560,512]{1,0:T(8,128)(2,1)} %param.15) | copy-start | bytes 7864324
  0.6 35.6 %copy-start.4 = (f32[2560]{0:T(1024)S(1)}, f32[2560]{0:T(1024)}, u32[]{:S(2)}) copy-start(f32[2560]{0:T(1024)} %param.12) | copy-start | bytes 30724
  4.2 32.0 %collective-permute-start = (bf16[256,2560]{1,0:T(8,128)(2,1)}, bf16[256,2560]{1,0:T(8,128)(2,1)}, u32[]{:S(2)}, u32[]{:S(2)}) collective-permute-start(bf16[256,2560]{1,0:T(8,128)(2,1)} %reshape.1228), channel_id=1, source_target_pairs={{0,8},{8,0},{1,9},{9,1},{2,10},{10,2},{3,11},{11,3},{4,12},{12,4},... | collective-permute-start | bytes 3932168 | tf_op jit(solution)/shard_map/ppermute | solution.py:329
  11.8 24.4 %collective-permute-start.1 = (f32[256]{0:T(256)S(1)}, f32[256]{0:T(256)S(1)}, u32[]{:S(2)}, u32[]{:S(2)}) collective-permute-start(f32[256]{0:T(256)S(1)} %psum.7), channel_id=1, source_target_pairs={{0,8},{8,0},{1,9},{9,1},{2,10},{10,2},{3,11},{11,3},{4,12},{12,4},... | collective-permute-start | bytes 3080 | tf_op jit(solution)/shard_map/ppermute | solution.py:332
  36.3 4.4 %copy-start.6 = (bf16[2560,512]{1,0:T(8,128)(2,1)S(1)}, bf16[2560,512]{1,0:T(8,128)(2,1)}, u32[]{:S(2)}) copy-start(bf16[2560,512]{1,0:T(8,128)(2,1)} %param.14) | copy-start | bytes 7864324
  39.1 3.1 %slice-start = ((s8[10485760]{0:T(1024)(128)(4,1)}), s8[4194304]{0:T(1024)(128)(4,1)S(1)}, s32[]{:S(2)}) async-start(s8[10485760]{0:T(1024)(128)(4,1)} %bitcast.176), calls=%async_computation | async-start | bytes 8388608
  39.1 3.5 %slice-start.1 = ((s8[10485760]{0:T(1024)(128)(4,1)}), s8[4194304]{0:T(1024)(128)(4,1)S(1)}, s32[]{:S(2)}) async-start(s8[10485760]{0:T(1024)(128)(4,1)} %bitcast.176), calls=%async_computation.1 | async-start | bytes 8388608
  40.7 2.7 %slice-start.2 = ((s8[10485760]{0:T(1024)(128)(4,1)}), s8[2097152]{0:T(1024)(128)(4,1)S(1)}, s32[]{:S(2)}) async-start(s8[10485760]{0:T(1024)(128)(4,1)} %bitcast.176), calls=%async_computation.2 | async-start | bytes 4194304
  49.5 1.6 %copy-start.2 = (bf16[2,256,3072]{2,1,0:T(8,128)(2,1)}, bf16[2,256,3072]{2,1,0:T(8,128)(2,1)S(1)}, u32[]{:S(2)}) copy-start(bf16[2,256,3072]{2,1,0:T(8,128)(2,1)S(1)} %pad_maximum_fusion) | copy-start | bytes 9437188
  51.1 1.3 copy-start.5
  52.4 3.6 %collective-permute-start.2 = (bf16[1,256,3072]{2,1,0:T(8,128)(2,1)}, bf16[1,256,3072]{2,1,0:T(8,128)(2,1)S(1)}, u32[]{:S(2)}, u32[]{:S(2)}) collective-permute-start(bf16[1,256,3072]{2,1,0:T(8,128)(2,1)} %constant_dynamic-slice_fusion.2), channel_id=1, source_target_pairs={{0,16},{16,0},{1,17},{17,1},{2,18},{18,2},{3,19},{19,3},{4,20},{20... | collective-permute-start | bytes 4718600 | tf_op jit(solution)/shard_map/ppermute | solution.py:239
  61.8 2.4 %copy-start.3 = (bf16[64,4,4,4,128]{4,3,1,2,0:T(4,128)(2,1)}, bf16[64,4,4,4,128]{4,3,1,2,0:T(4,128)(2,1)S(1)}, u32[]{:S(2)}) copy-start(bf16[64,4,4,4,128]{4,3,1,2,0:T(4,128)(2,1)S(1)} %copy.132) | copy-start | bytes 3145732
  87.6 4.0 %collective-permute-start.3 = (f32[2,2,2,1,8,64]{5,4,3,2,1,0:T(8,128)S(1)}, f32[2,2,2,1,8,64]{5,4,3,2,1,0:T(8,128)S(1)}, u32[]{:S(2)}, u32[]{:S(2)}) collective-permute-start(f32[2,2,2,1,8,64]{5,4,3,2,1,0:T(8,128)S(1)} %get-tuple-element.46), channel_id=1, source_target_pairs={{0,1},{1,0},{2,3},{3,2},{4,5},{5,4},{6,7},{7,6},{8,9},{9,8},{10,11... | collective-permute-start | bytes 49160 | tf_op jit(solution)/shard_map/ppermute | solution.py:286
  91.3 13.8 %collective-permute-start.4 = (bf16[2,2,1,8,64,128]{5,4,3,2,1,0:T(8,128)(2,1)S(1)}, bf16[2,2,1,8,64,128]{5,4,3,2,1,0:T(8,128)(2,1)S(1)}, u32[]{:S(2)}, u32[]{:S(2)}) collective-permute-start(bf16[2,2,1,8,64,128]{5,4,3,2,1,0:T(8,128)(2,1)S(1)} %dynamic-slice_convert_fusion), channel_id=1, source_target_pairs={{0,1},{1,0},{2,3},{3,2},{4,5},{5,4},{6,7},{7,6},{8,9},{9,8},{10,11... | collective-permute-start | bytes 1572872 | tf_op jit(solution)/shard_map/ppermute | solution.py:287
  91.7 3.8 %collective-permute-start.5 = (f32[2,2,1,1,8,64]{5,4,3,2,1,0:T(8,128)S(1)}, f32[2,2,1,1,8,64]{5,4,3,2,1,0:T(8,128)S(1)}, u32[]{:S(2)}, u32[]{:S(2)}) collective-permute-start(f32[2,2,1,1,8,64]{5,4,3,2,1,0:T(8,128)S(1)} %get-tuple-element.50), channel_id=1, source_target_pairs={{0,2},{1,3},{2,0},{3,1},{4,6},{5,7},{6,4},{7,5},{8,10},{9,11},{10,... | collective-permute-start | bytes 24584 | tf_op jit(solution)/shard_map/ppermute | solution.py:286
  95.5 4.6 %collective-permute-start.7 = (f32[2,1,1,1,8,64]{5,4,3,2,1,0:T(8,128)S(1)}, f32[2,1,1,1,8,64]{5,4,3,2,1,0:T(8,128)S(1)}, u32[]{:S(2)}, u32[]{:S(2)}) collective-permute-start(f32[2,1,1,1,8,64]{5,4,3,2,1,0:T(8,128)S(1)} %get-tuple-element.54), channel_id=1, source_target_pairs={{0,4},{1,5},{2,6},{3,7},{4,0},{5,1},{6,2},{7,3},{8,12},{9,13},{10,... | collective-permute-start | bytes 12296 | tf_op jit(solution)/shard_map/ppermute | solution.py:286
  106.9 7.3 %collective-permute-start.6 = (bf16[2,1,1,8,64,128]{5,4,3,2,1,0:T(8,128)(2,1)S(1)}, bf16[2,1,1,8,64,128]{5,4,3,2,1,0:T(8,128)(2,1)S(1)}, u32[]{:S(2)}, u32[]{:S(2)}) collective-permute-start(bf16[2,1,1,8,64,128]{5,4,3,2,1,0:T(8,128)(2,1)S(1)} %dynamic-slice_convert_fusion.1), channel_id=1, source_target_pairs={{0,2},{1,3},{2,0},{3,1},{4,6},{5,7},{6,4},{7,5},{8,10},{9,11},{10,... | collective-permute-start | bytes 786440 | tf_op jit(solution)/shard_map/ppermute | solution.py:287
  114.6 7.3 %collective-permute-start.8 = (bf16[1,1,1,8,64,128]{5,4,3,2,1,0:T(8,128)(2,1)S(1)}, bf16[1,1,1,8,64,128]{5,4,3,2,1,0:T(8,128)(2,1)S(1)}, u32[]{:S(2)}, u32[]{:S(2)}) collective-permute-start(bf16[1,1,1,8,64,128]{5,4,3,2,1,0:T(8,128)(2,1)S(1)} %dynamic-slice_convert_fusion.2), channel_id=1, source_target_pairs={{0,4},{1,5},{2,6},{3,7},{4,0},{5,1},{6,2},{7,3},{8,12},{9,13},{10,... | collective-permute-start | bytes 393224 | tf_op jit(solution)/shard_map/ppermute | solution.py:287
  130.5 6.3 %collective-permute-start.9 = (bf16[1,8,4,2560]{3,1,2,0:T(8,128)(2,1)S(1)}, bf16[1,8,4,2560]{3,1,2,0:T(8,128)(2,1)S(1)}, u32[]{:S(2)}, u32[]{:S(2)}) collective-permute-start(bf16[1,8,4,2560]{3,1,2,0:T(8,128)(2,1)S(1)} %constant_dynamic-slice_fusion.1), channel_id=1, source_target_pairs={{0,8},{8,0},{1,9},{9,1},{2,10},{10,2},{3,11},{11,3},{4,12},{12,4},... | collective-permute-start | bytes 491528 | tf_op jit(solution)/shard_map/ppermute | solution.py:239
  136.9 6.9 %collective-permute-start.13 = (bf16[1,8,4,1280]{3,1,2,0:T(8,128)(2,1)S(1)}, bf16[1,8,4,1280]{3,1,2,0:T(8,128)(2,1)S(1)}, u32[]{:S(2)}, u32[]{:S(2)}) collective-permute-start(bf16[1,8,4,1280]{3,1,2,0:T(8,128)(2,1)S(1)} %get-tuple-element.39), channel_id=1, source_target_pairs={{0,4},{1,5},{2,6},{3,7},{4,0},{5,1},{6,2},{7,3},{8,12},{9,13},{10,... | collective-permute-start | bytes 245768 | tf_op jit(solution)/shard_map/ppermute | solution.py:255
  139.4 6.5 %collective-permute-start.10 = (bf16[1,8,4,1280]{3,1,2,0:T(8,128)(2,1)S(1)}, bf16[1,8,4,1280]{3,1,2,0:T(8,128)(2,1)S(1)}, u32[]{:S(2)}, u32[]{:S(2)}) collective-permute-start(bf16[1,8,4,1280]{3,1,2,0:T(8,128)(2,1)S(1)} %get-tuple-element.38), channel_id=1, source_target_pairs={{0,4},{1,5},{2,6},{3,7},{4,0},{5,1},{6,2},{7,3},{8,12},{9,13},{10,... | collective-permute-start | bytes 245768 | tf_op jit(solution)/shard_map/ppermute | solution.py:255
  143.9 5.4 %collective-permute-start.14 = (bf16[2,1,8,4,1280]{4,2,3,1,0:T(8,128)(2,1)S(1)}, bf16[2,1,8,4,1280]{4,2,3,1,0:T(8,128)(2,1)S(1)}, u32[]{:S(2)}, u32[]{:S(2)}) collective-permute-start(bf16[2,1,8,4,1280]{4,2,3,1,0:T(8,128)(2,1)S(1)} %bitcast_select_fusion), channel_id=1, source_target_pairs={{0,1},{1,0},{2,3},{3,2},{4,5},{5,4},{6,7},{7,6},{8,9},{9,8},{10,11... | collective-permute-start | bytes 491528 | tf_op jit(solution)/shard_map/ppermute | solution.py:255
  145.9 7.2 %collective-permute-start.11 = (bf16[2,1,8,4,1280]{4,2,3,0,1:T(8,128)(2,1)S(1)}, bf16[2,1,8,4,1280]{4,2,3,0,1:T(8,128)(2,1)S(1)}, u32[]{:S(2)}, u32[]{:S(2)}) collective-permute-start(bf16[2,1,8,4,1280]{4,2,3,0,1:T(8,128)(2,1)S(1)} %maximum_select_fusion.6), channel_id=1, source_target_pairs={{0,2},{1,3},{2,0},{3,1},{4,6},{5,7},{6,4},{7,5},{8,10},{9,11},{10,... | collective-permute-start | bytes 491528 | tf_op jit(solution)/shard_map/ppermute | solution.py:255
  149.3 9.3 %collective-permute-start.15 = (bf16[2,2,1,8,4,1280]{5,3,4,1,2,0:T(8,128)(2,1)S(1)}, bf16[2,2,1,8,4,1280]{5,3,4,1,2,0:T(8,128)(2,1)S(1)}, u32[]{:S(2)}, u32[]{:S(2)}) collective-permute-start(bf16[2,2,1,8,4,1280]{5,3,4,1,2,0:T(8,128)(2,1)S(1)} %maximum_select_fusion.5), channel_id=1, source_target_pairs={{0,2},{1,3},{2,0},{3,1},{4,6},{5,7},{6,4},{7,5},{8,10},{9,11},{10,... | collective-permute-start | bytes 983048 | tf_op jit(solution)/shard_map/ppermute | solution.py:255
  153.2 7.1 %collective-permute-start.12 = (bf16[2,2,1,8,4,1280]{5,3,4,1,2,0:T(8,128)(2,1)S(1)}, bf16[2,2,1,8,4,1280]{5,3,4,1,2,0:T(8,128)(2,1)S(1)}, u32[]{:S(2)}, u32[]{:S(2)}) collective-permute-start(bf16[2,2,1,8,4,1280]{5,3,4,1,2,0:T(8,128)(2,1)S(1)} %maximum_select_fusion.3), channel_id=1, source_target_pairs={{0,1},{1,0},{2,3},{3,2},{4,5},{5,4},{6,7},{7,6},{8,9},{9,8},{10,11... | collective-permute-start | bytes 983048 | tf_op jit(solution)/shard_map/ppermute | solution.py:255
  160.5 2.2 %copy-start.1 = (bf16[2560,512]{1,0:T(8,128)(2,1)S(1)}, bf16[2560,512]{1,0:T(8,128)(2,1)}, u32[]{:S(2)}) copy-start(bf16[2560,512]{1,0:T(8,128)(2,1)} %param.15) | copy-start | bytes 7864324

commit v18 on v16

--- a/solution.py
+++ b/solution.py
@@ -264,6 +264,33 @@
     return block.reshape((n * part.shape[0],) + part.shape[1:])
 
 
+def pack_rows(stats, values):
+    lanes = jnp.concatenate([stats[0], stats[1]], -1)
+    high = lax.reduce_precision(lanes, exponent_bits=8, mantissa_bits=7)
+    rest = lanes - high
+    middle = lax.reduce_precision(rest, exponent_bits=8, mantissa_bits=7)
+    low = rest - middle
+    pieces = jnp.stack([high, middle, low, jnp.zeros_like(low)], -2)
+    width = values.shape[-1]
+    return jnp.concatenate(
+        [
+            values.astype(jnp.bfloat16).reshape(-1, width),
+            pieces.astype(jnp.bfloat16).reshape(-1, width),
+        ],
+        0,
+    )
+
+
+def unpack_rows(message, stats_shape, values_shape):
+    width = values_shape[-1]
+    count = math.prod(values_shape) // width
+    values = message[:count].astype(jnp.float32).reshape(values_shape)
+    pieces = message[count:].astype(jnp.float32).reshape(stats_shape[1:-1] + (4, width))
+    lanes = pieces[..., 0, :] + (pieces[..., 1, :] + pieces[..., 2, :])
+    rows = stats_shape[-1]
+    return jnp.stack([lanes[..., :rows], lanes[..., rows:]], 0), values
+
+
 def seq_merge(peak, total, acc, n_seq, seq_index):
     stages = n_seq.bit_length() - 1
     assert 1 << stages == n_seq
@@ -281,10 +308,17 @@
         send_stats = lax.dynamic_index_in_dim(stats, 1 - mine, axis + 1, keepdims=True)
         keep_values = lax.dynamic_index_in_dim(values, mine, axis, keepdims=True)
         send_values = lax.dynamic_index_in_dim(values, 1 - mine, axis, keepdims=True)
-        got_stats = lax.ppermute(send_stats, "seq", pairs)
-        got_values = lax.ppermute(send_values.astype(jnp.bfloat16), "seq", pairs).astype(
-            jnp.float32
-        )
+        if 2 * rest[-1] == values.shape[-1]:
+            got_stats, got_values = unpack_rows(
+                lax.ppermute(pack_rows(send_stats, send_values), "seq", pairs),
+                send_stats.shape,
+                send_values.shape,
+            )
+        else:
+            got_stats = lax.ppermute(send_stats, "seq", pairs)
+            got_values = lax.ppermute(send_values.astype(jnp.bfloat16), "seq", pairs).astype(
+                jnp.float32
+            )
         top = jnp.maximum(keep_stats[0], got_stats[0])
         keep_factor = jnp.exp(keep_stats[0] - top)
         got_factor = jnp.exp(got_stats[0] - top)

time: 162 us -> 177 us (1.093)
  other arithmetic: 17.5 us -> 28.5 us
  local copies, waits for them, and re-layouts: 16.2 us -> 25.9 us
  starting transfers between devices: 22.7 us -> 18.3 us
  waiting for transfers between devices: 64 us -> 60.2 us
  matrix products: 16.2 us -> 18.1 us
    slice x0 -> x9, local copies, waits for them, and re-layouts: none -> 5.21 us  [the longest x3 2.96 us: unpack_rows(): values = message[:count].astype(jnp.float32).reshape(values_shape)]
    ppermute x6 -> x3, starting transfers between devices: 11.2 us -> 6.16 us  [seq_merge(): lax.ppermute(pack_rows(send_stats, send_values), 'seq', pairs)]
    ppermute x6 -> x3, waiting for transfers between devices: 17.9 us -> 14.6 us  [seq_merge(): lax.ppermute(pack_rows(send_stats, send_values), 'seq', pairs)]
    add x3, other arithmetic: 2.36 us -> 5.38 us  [seq_merge(): keep_values * keep_factor[..., None] + got_values * got_factor[..., None]]
    concatenate x0 -> x3, other arithmetic: none -> 2.32 us  [pack_rows(): jnp.concatenate([values.astype(jnp.bfloat16).reshape(-1, width), pieces.a...]
    unnamed x24 -> x36, local copies, waits for them, and re-layouts: 5.49 us -> 4.59 us
  transfers between devices with their start and end apart: 16 -> 13, of which waited for: 13 -> 10; matrix products, arithmetic and copies ran while one was open for 5% -> 9% of each run, Pallas kernels for 0% -> 0%
where the time goes in v18:
time: 177 us; the launch traced here: 176 us
  waiting for transfers between devices  60.2 us (34%)
  other arithmetic  28.5 us (16%)
  local copies, waits for them, and re-layouts  25.9 us (15%)
  Pallas kernels  19.6 us (11%)
  starting transfers between devices  18.3 us (10%)
  matrix products  18.1 us (10%)
  blocking collectives  4.46 us (3%)
    ppermute x1, waiting for transfers between devices, on_device(): other_squares = lax.ppermute(squares, 'col', swap)  24.4 us
    pallas_call x1, Pallas kernels, slot_attention(): pl.pallas_call(partial(slot_kernel, ns=ns, heads=heads, qpk=qpk), grid_sp...  19.6 us
    ppermute x3, waiting for transfers between devices, seq_merge(): lax.ppermute(pack_rows(send_stats, send_values), 'seq', pairs)  14.6 us
    ppermute x6, waiting for transfers between devices, doubling_gather(): got = lax.ppermute(block, axis_name, pairs)  14.3 us
    dot_general x3, matrix products, on_device(): jnp.dot(gathered, matrix, preferred_element_type=jnp.float32)  8.8 us
    ppermute x6, starting transfers between devices, doubling_gather(): got = lax.ppermute(block, axis_name, pairs)  7.64 us
    ppermute x2, waiting for transfers between devices, pair_scatter(): got = lax.ppermute(send, axis_name, [(0, 1), (1, 0)])  6.87 us
    ppermute x3, starting transfers between devices, seq_merge(): lax.ppermute(pack_rows(send_stats, send_values), 'seq', pairs)  6.16 us
  transfers between devices with their start and end apart: 13, of which 10 were waited for; matrix products, arithmetic and copies ran while one was open for 9% of the time, Pallas kernels for 0%

profile of v18, /device:TPU:0, one launch (start us, length us, event | category | flops | bytes accessed | tf_op | source)
XLA Modules:
  0.0 176.3 jit_solution(9006648823584956028)
XLA Ops:
  0.7 3.5 %reshape.1844 = bf16[256,2560]{1,0:T(8,128)(2,1)} reshape(bf16[64,4,2560]{2,1,0:T(4,128)(2,1)} %param.11) | data formatting | bytes 2621440 | tf_op jit(solution)/shard_map/reshape | solution.py:358
  4.2 2.9 %collective-permute-start = (bf16[256,2560]{1,0:T(8,128)(2,1)}, bf16[256,2560]{1,0:T(8,128)(2,1)}, u32[]{:S(2)}, u32[]{:S(2)}) collective-permute-start(bf16[256,2560]{1,0:T(8,128)(2,1)} %reshape.1844), channel_id=1, source_target_pairs={{0,8},{8,0},{1,9},{9,1},{2,10},{10,2},{3,11},{11,3},{4,12},{12,4},... | collective-permute-start | bytes 3932168 | tf_op jit(solution)/shard_map/ppermute | solution.py:361
  7.1 2.1 %multiply_reduce_fusion = f32[64,4]{1,0:T(8,128)S(1)} fusion(bf16[64,4,2560]{2,1,0:T(4,128)(2,1)} %param.11), kind=kLoop, calls=%fused_computation.9 | loop fusion | flops 1965824 | bytes 1311744 | tf_op jit(solution)/shard_map/reduce_sum | solution.py:363
  9.3 2.5 %psum.7 = f32[256]{0:T(256)S(1)} all-reduce(f32[256]{0:T(256)S(1)} %reduce_sum.21), channel_id=1, replica_groups=mesh['row'=2,'col'=2,'seq'=8] {'row'}, use_global_device_ids=true, to_apply=%region_1.0 | all-reduce | flops 256 | bytes 2048 | tf_op jit(solution)/shard_map/psum | solution.py:363
  11.8 24.4 %collective-permute-done.1 = f32[256]{0:T(256)S(1)} collective-permute-done((f32[256]{0:T(256)S(1)}, f32[256]{0:T(256)S(1)}, u32[]{:S(2)}, u32[]{:S(2)}) %collective-permute-start.1) | collective-permute-done | bytes 1056 | tf_op jit(solution)/shard_map/ppermute | solution.py:364
  36.3 2.8 %multiply_convert_fusion.1 = (bf16[256,2560]{1,0:T(8,128)(2,1)S(1)}, bf16[256,2560]{1,0:T(8,128)(2,1)S(1)}) fusion(f32[2560]{0:T(1024)S(1)} %copy-done.9, f32[256]{0:T(256)S(1)} %get-tuple-element.73, bf16[256,2560]{1,0:T(8,128)(2,1)} %reshape.1844, bf16[256,2560]{1,0:T(8,128)(2,1)} %collective-permute-done, pred[]{:T(512)S(6)} %eq.18, ...), kind=kLoop, calls=%fused_computation.8 | loop fusion | flops 6553600 | bytes 5255169 | tf_op jit(solution)/shard_map/convert_element_type | solution.py:368
  39.1 1.5 convolution_convert_fusion.2
  40.7 1.5 convolution_convert_fusion.1
  42.6 0.8 slice-done.2
  43.4 5.8 %convolution_convert_fusion = bf16[512,2048]{1,0:T(8,128)(2,1)S(1)} fusion(bf16[2560,2048]{1,0:T(8,128)(2,1)S(1)} %bitcast.302, bf16[256,2560]{1,0:T(8,128)(2,1)S(1)} %get-tuple-element.32, bf16[256,2560]{1,0:T(8,128)(2,1)S(1)} %get-tuple-element.31), kind=kOutput, calls=%fused_computation.5 | convolution fusion | flops 5375000576 | bytes 15204352 | tf_op jit(solution)/shard_map/dot_general | solution.py:383
  49.5 1.3 constant_dynamic-slice_fusion.2
  51.6 2.9 %collective-permute-done.2 = bf16[1,256,3072]{2,1,0:T(8,128)(2,1)} collective-permute-done((bf16[1,256,3072]{2,1,0:T(8,128)(2,1)}, bf16[1,256,3072]{2,1,0:T(8,128)(2,1)}, u32[]{:S(2)}, u32[]{:S(2)}) %collective-permute-start.2) | collective-permute-done | bytes 1572896 | tf_op jit(solution)/shard_map/ppermute | solution.py:237
  54.5 1.9 %add_bitcast_fusion = f32[32,8,24,128]{3,1,2,0:T(8,128)S(1)} fusion(bf16[1,256,3072]{2,1,0:T(8,128)(2,1)} %collective-permute-done.2, bf16[2,256,3072]{2,1,0:T(8,128)(2,1)S(1)} %pad_maximum_fusion, s32[]{:T(128)S(6)} %select_n.253), kind=kLoop, calls=%fused_computation.4 | loop fusion | flops 2359296 | bytes 6291460
  57.0 0.8 subtract_convert_fusion
  57.8 1.4 pad_maximum_fusion.3
  59.3 1.4 copy.158
  60.7 19.6 %shard_map.130 = (f32[64,64,1]{2,1,0:T(8,128)}, f32[64,64,1]{2,1,0:T(8,128)}, f32[64,64,128]{2,1,0:T(8,128)}) custom-call(s32[50]{0:T(128)} %req_ref.1, s32[64]{0:T(128)} %len_ref.1, s32[50]{0:T(128)} %blk_ref.1, bf16[64,64,128]{2,1,0:T(8,128)(2,1)} %bitcast.236, bf16[50,128,512]{2,1,0:T(8,128)(2,1)} %k_ref.1, bf16[50,128,512]{2,1,0:T(8,128)(2,1)} %v_ref.1), custom_call_target="tpu_custom_call" | custom-call | tf_op jit(solution)/shard_map/pallas_call | solution.py:209
  80.3 2.2 %reduce.1 = f32[64,64]{1,0:T(8,128)S(1)} reduce(f32[64,64,1]{2,1,0:T(8,128)} %get-tuple-element.7, f32[]{:T(128)} %constant.107), dimensions={2}, to_apply=%get-tuple-element.7.reduce_sub_computation | reduce | bytes 32772 | tf_op jit(solution)/shard_map/pallas_call | solution.py:209
  82.5 2.2 %reduce.2 = f32[64,64]{1,0:T(8,128)S(1)} reduce(f32[64,64,1]{2,1,0:T(8,128)} %get-tuple-element.8, f32[]{:T(128)} %constant.107), dimensions={2}, to_apply=%get-tuple-element.8.reduce_sub_computation | reduce | bytes 32772 | tf_op jit(solution)/shard_map/pallas_call | solution.py:209
  85.0 1.3 dynamic-slice_convert_fusion
  86.3 0.9 pad_maximum_fusion.7
  87.1 1.8 %collective-permute-start.3 = (bf16[2176,128]{1,0:T(8,128)(2,1)}, bf16[2176,128]{1,0:T(8,128)(2,1)}, u32[]{:S(2)}, u32[]{:S(2)}) collective-permute-start(bf16[2176,128]{1,0:T(8,128)(2,1)} %pad_maximum_fusion.7), channel_id=1, source_target_pairs={{0,1},{1,0},{2,3},{3,2},{4,5},{5,4},{6,7},{7,6},{8,9},{9,8},{10,11... | collective-permute-start | bytes 1671176 | tf_op jit(solution)/shard_map/ppermute | solution.py:313
  89.5 12.7 %collective-permute-done.3 = bf16[2176,128]{1,0:T(8,128)(2,1)} collective-permute-done((bf16[2176,128]{1,0:T(8,128)(2,1)}, bf16[2176,128]{1,0:T(8,128)(2,1)}, u32[]{:S(2)}, u32[]{:S(2)}) %collective-permute-start.3) | collective-permute-done | bytes 557088 | tf_op jit(solution)/shard_map/ppermute | solution.py:313
  102.2 0.8 slice.179
  103.3 1.1 slice.184
  104.4 2.8 %fusion.9 = f32[2,2,1,8,64,128]{5,4,3,2,1,0:T(8,128)} fusion(bf16[2,2,1,8,64,128]{5,4,3,2,1,0:T(8,128)(2,1)S(1)} %bitcast.245, f32[2,2,2,8,64,128]{5,4,3,2,1,0:T(8,128)} %bitcast.248, s32[]{:T(128)S(6)} %select_n.255, f32[2,2,8,64]{3,2,1,0:T(8,128)S(1)} %get-tuple-element.45, f32[2,2,8,64]{3,2,1,0:T(8,128)S(1)} %get-tuple-element.25), kind=kLoop, calls=%fused_computation.22 | loop fusion | flops 1048576 | bytes 2637828 | tf_op jit(solution)/shard_map/add | solution.py:328
  107.2 1.1 dynamic-slice_convert_fusion.1
  108.3 0.7 pad_maximum_fusion.8
  109.0 1.8 %collective-permute-start.4 = (bf16[1088,128]{1,0:T(8,128)(2,1)}, bf16[1088,128]{1,0:T(8,128)(2,1)}, u32[]{:S(2)}, u32[]{:S(2)}) collective-permute-start(bf16[1088,128]{1,0:T(8,128)(2,1)} %pad_maximum_fusion.8), channel_id=1, source_target_pairs={{0,2},{1,3},{2,0},{3,1},{4,6},{5,7},{6,4},{7,5},{8,10},{9,11},{10,... | collective-permute-start | bytes 835592 | tf_op jit(solution)/shard_map/ppermute | solution.py:313
  111.3 0.7 copy-done.2
  112.2 2.9 %fusion.16 = f32[8,4,4,4,4]{3,4,2,1,0:T(4,128)} fusion(bf16[64,4,4,4,128]{4,3,1,2,0:T(4,128)(2,1)} %copy.158, s32[]{:T(128)S(6)} %select_n.261, bf16[64,4,4,64]{3,1,2,0:T(4,128)(2,1)S(1)} %copy.132, bf16[64,4,4,64]{3,1,2,0:T(4,128)(2,1)S(1)} %copy.133), kind=kOutput, calls=%fused_computation.59 | convolution fusion | flops 589824 | bytes 402432 | tf_op jit(solution)/shard_map/rsagh,ruah->rasgu/dot_general | solution.py:89
  115.1 1.4 copy.134
  116.5 0.9 select_reduce_fusion
  117.5 0.7 slice.190
  118.4 0.7 maximum_maximum_fusion.2
  119.1 1.0 slice.195
  120.1 1.4 fusion.12
  121.5 0.7 pad_maximum_fusion.10
  122.3 2.6 %collective-permute-start.5 = (bf16[544,128]{1,0:T(8,128)(2,1)}, bf16[544,128]{1,0:T(8,128)(2,1)}, u32[]{:S(2)}, u32[]{:S(2)}) collective-permute-start(bf16[544,128]{1,0:T(8,128)(2,1)} %pad_maximum_fusion.10), channel_id=1, source_target_pairs={{0,4},{1,5},{2,6},{3,7},{4,0},{5,1},{6,2},{7,3},{8,12},{9,13},{10,... | collective-permute-start | bytes 417800 | tf_op jit(solution)/shard_map/ppermute | solution.py:313
  124.9 1.3 fusion.18
  126.2 0.8 slice.302
  127.1 1.3 copy.141
  128.4 0.8 constant_dynamic-slice_fusion
  129.2 1.9 %collective-permute-done.5 = bf16[544,128]{1,0:T(8,128)(2,1)} collective-permute-done((bf16[544,128]{1,0:T(8,128)(2,1)}, bf16[544,128]{1,0:T(8,128)(2,1)}, u32[]{:S(2)}, u32[]{:S(2)}) %collective-permute-start.5) | collective-permute-done | bytes 139296 | tf_op jit(solution)/shard_map/ppermute | solution.py:313
  131.1 0.7 slice.201
  132.1 0.8 multiply_add_fusion
  133.4 0.9 slice.205
  134.3 1.2 fusion.13
  136.1 2.0 %all_gather.4 = bf16[2,8,4,2048]{3,1,2,0:T(8,128)(2,1)S(1)} all-gather(bf16[1,8,4,2048]{3,1,2,0:T(8,128)(2,1)S(1)} %convert_element_type.132), channel_id=1, replica_groups=mesh['row'=2,'col'=2,'seq'=8] {'row'}, dimensions={0}, use_global_device_ids=true | all-gather | bytes 393216 | tf_op jit(solution)/shard_map/all_gather | solution.py:447
  138.1 5.9 %fusion.2 = bf16[2,8,4,2560]{3,1,2,0:T(8,128)(2,1)S(1)} fusion(bf16[2,8,4,2048]{3,1,2,0:T(8,128)(2,1)S(1)} %all_gather.4, bf16[2048,2560]{1,0:T(8,128)(2,1)} %param.16), kind=kOutput, calls=%fused_computation.2 | convolution fusion | flops 671252480 | bytes 11075584 | tf_op jit(solution)/shard_map/dot_general | solution.py:449
  144.1 1.6 collective-permute-start.6
  145.6 0.8 reshape_reshape.8
  146.4 4.0 %collective-permute-done.6 = bf16[1,8,4,2560]{3,1,2,0:T(8,128)(2,1)S(1)} collective-permute-done((bf16[1,8,4,2560]{3,1,2,0:T(8,128)(2,1)S(1)}, bf16[1,8,4,2560]{3,1,2,0:T(8,128)(2,1)S(1)}, u32[]{:S(2)}, u32[]{:S(2)}) %collective-permute-start.6) | collective-permute-done | bytes 163872 | tf_op jit(solution)/shard_map/ppermute | solution.py:237
  150.9 0.8 convert_element_type.138
  151.7 2.9 %collective-permute-start.10 = (bf16[1,8,4,1280]{3,1,2,0:T(8,128)(2,1)S(1)}, bf16[1,8,4,1280]{3,1,2,0:T(8,128)(2,1)S(1)}, u32[]{:S(2)}, u32[]{:S(2)}) collective-permute-start(bf16[1,8,4,1280]{3,1,2,0:T(8,128)(2,1)S(1)} %get-tuple-element.39), channel_id=1, source_target_pairs={{0,4},{1,5},{2,6},{3,7},{4,0},{5,1},{6,2},{7,3},{8,12},{9,13},{10,... | collective-permute-start | bytes 245768 | tf_op jit(solution)/shard_map/ppermute | solution.py:253
  154.6 3.9 %collective-permute-done.7 = bf16[1,8,4,1280]{3,1,2,0:T(8,128)(2,1)S(1)} collective-permute-done((bf16[1,8,4,1280]{3,1,2,0:T(8,128)(2,1)S(1)}, bf16[1,8,4,1280]{3,1,2,0:T(8,128)(2,1)S(1)}, u32[]{:S(2)}, u32[]{:S(2)}) %collective-permute-start.7) | collective-permute-done | bytes 81952 | tf_op jit(solution)/shard_map/ppermute | solution.py:253
  158.7 1.3 collective-permute-done.10
  160.0 1.6 collective-permute-start.11
  161.6 3.8 %collective-permute-done.11 = bf16[2,1,8,4,1280]{4,2,3,1,0:T(8,128)(2,1)S(1)} collective-permute-done((bf16[2,1,8,4,1280]{4,2,3,1,0:T(8,128)(2,1)S(1)}, bf16[2,1,8,4,1280]{4,2,3,1,0:T(8,128)(2,1)S(1)}, u32[]{:S(2)}, u32[]{:S(2)}) %collective-permute-start.11) | collective-permute-done | bytes 163872 | tf_op jit(solution)/shard_map/ppermute | solution.py:253
  165.4 1.4 collective-permute-start.12
  166.9 1.6 collective-permute-start.9
  168.5 4.5 %collective-permute-done.12 = bf16[2,2,1,8,4,1280]{5,3,4,1,2,0:T(8,128)(2,1)S(1)} collective-permute-done((bf16[2,2,1,8,4,1280]{5,3,4,1,2,0:T(8,128)(2,1)S(1)}, bf16[2,2,1,8,4,1280]{5,3,4,1,2,0:T(8,128)(2,1)S(1)}, u32[]{:S(2)}, u32[]{:S(2)}) %collective-permute-start.12) | collective-permute-done | bytes 327712 | tf_op jit(solution)/shard_map/ppermute | solution.py:253
  173.2 0.8 collective-permute-done.9
  174.3 2.1 %copy.154 = bf16[64,4,2560]{2,1,0:T(4,128)(2,1)} copy(bf16[64,4,2560]{2,0,1:T(8,128)(2,1)S(1)} %pad_maximum_fusion.2) | data formatting | bytes 2621440
  (108 shorter events, 7.0 us)
Async XLA Ops:
  0.6 38.5 %copy-start = (bf16[2560,512]{1,0:T(8,128)(2,1)S(1)}, bf16[2560,512]{1,0:T(8,128)(2,1)}, u32[]{:S(2)}) copy-start(bf16[2560,512]{1,0:T(8,128)(2,1)} %param.14) | copy-start | bytes 7864324
  0.6 35.6 %copy-start.9 = (f32[2560]{0:T(1024)S(1)}, f32[2560]{0:T(1024)}, u32[]{:S(2)}) copy-start(f32[2560]{0:T(1024)} %param.12) | copy-start | bytes 30724
  4.2 32.0 %collective-permute-start = (bf16[256,2560]{1,0:T(8,128)(2,1)}, bf16[256,2560]{1,0:T(8,128)(2,1)}, u32[]{:S(2)}, u32[]{:S(2)}) collective-permute-start(bf16[256,2560]{1,0:T(8,128)(2,1)} %reshape.1844), channel_id=1, source_target_pairs={{0,8},{8,0},{1,9},{9,1},{2,10},{10,2},{3,11},{11,3},{4,12},{12,4},... | collective-permute-start | bytes 3932168 | tf_op jit(solution)/shard_map/ppermute | solution.py:361
  11.8 24.4 %collective-permute-start.1 = (f32[256]{0:T(256)S(1)}, f32[256]{0:T(256)S(1)}, u32[]{:S(2)}, u32[]{:S(2)}) collective-permute-start(f32[256]{0:T(256)S(1)} %psum.7), channel_id=1, source_target_pairs={{0,8},{8,0},{1,9},{9,1},{2,10},{10,2},{3,11},{11,3},{4,12},{12,4},... | collective-permute-start | bytes 3080 | tf_op jit(solution)/shard_map/ppermute | solution.py:364
  36.3 4.4 %copy-start.13 = (bf16[2560,512]{1,0:T(8,128)(2,1)S(1)}, bf16[2560,512]{1,0:T(8,128)(2,1)}, u32[]{:S(2)}) copy-start(bf16[2560,512]{1,0:T(8,128)(2,1)} %param.15) | copy-start | bytes 7864324
  39.1 3.1 %slice-start = ((s8[10485760]{0:T(1024)(128)(4,1)}), s8[4194304]{0:T(1024)(128)(4,1)S(1)}, s32[]{:S(2)}) async-start(s8[10485760]{0:T(1024)(128)(4,1)} %bitcast.301), calls=%async_computation | async-start | bytes 8388608
  39.1 3.5 %slice-start.1 = ((s8[10485760]{0:T(1024)(128)(4,1)}), s8[4194304]{0:T(1024)(128)(4,1)S(1)}, s32[]{:S(2)}) async-start(s8[10485760]{0:T(1024)(128)(4,1)} %bitcast.301), calls=%async_computation.1 | async-start | bytes 8388608
  40.7 2.7 %slice-start.2 = ((s8[10485760]{0:T(1024)(128)(4,1)}), s8[2097152]{0:T(1024)(128)(4,1)S(1)}, s32[]{:S(2)}) async-start(s8[10485760]{0:T(1024)(128)(4,1)} %bitcast.301), calls=%async_computation.2 | async-start | bytes 4194304
  49.5 1.3 copy-start.11
  50.8 3.8 %collective-permute-start.2 = (bf16[1,256,3072]{2,1,0:T(8,128)(2,1)}, bf16[1,256,3072]{2,1,0:T(8,128)(2,1)}, u32[]{:S(2)}, u32[]{:S(2)}) collective-permute-start(bf16[1,256,3072]{2,1,0:T(8,128)(2,1)} %constant_dynamic-slice_fusion.2), channel_id=1, source_target_pairs={{0,16},{16,0},{1,17},{17,1},{2,18},{18,2},{3,19},{19,3},{4,20},{20... | collective-permute-start | bytes 4718600 | tf_op jit(solution)/shard_map/ppermute | solution.py:237
  51.1 52.1 %copy-start.10 = (bf16[4]{0:T(256)(128)(2,1)}, bf16[4]{0:T(256)(128)(2,1)S(1)}, u32[]{:S(2)}) copy-start(bf16[4]{0:T(256)(128)(2,1)S(1)} %pad.71.clone) | copy-start | bytes 28
  51.6 5.4 %copy-start.6 = (f32[256,64]{1,0:T(8,128)}, f32[256,64]{1,0:T(8,128)S(1)}, u32[]{:S(2)}) copy-start(f32[256,64]{1,0:T(8,128)S(1)} %get-tuple-element.76) | copy-start | bytes 196612
  87.1 15.0 %collective-permute-start.3 = (bf16[2176,128]{1,0:T(8,128)(2,1)}, bf16[2176,128]{1,0:T(8,128)(2,1)}, u32[]{:S(2)}, u32[]{:S(2)}) collective-permute-start(bf16[2176,128]{1,0:T(8,128)(2,1)} %pad_maximum_fusion.7), channel_id=1, source_target_pairs={{0,1},{1,0},{2,3},{3,2},{4,5},{5,4},{6,7},{7,6},{8,9},{9,8},{10,11... | collective-permute-start | bytes 1671176 | tf_op jit(solution)/shard_map/ppermute | solution.py:313
  103.0 7.9 %copy-start.7 = (f32[256,64]{1,0:T(8,128)S(1)}, f32[256,64]{1,0:T(8,128)}, u32[]{:S(2)}) copy-start(f32[256,64]{1,0:T(8,128)} %copy-done.6) | copy-start | bytes 196612
  109.0 8.5 %collective-permute-start.4 = (bf16[1088,128]{1,0:T(8,128)(2,1)}, bf16[1088,128]{1,0:T(8,128)(2,1)}, u32[]{:S(2)}, u32[]{:S(2)}) collective-permute-start(bf16[1088,128]{1,0:T(8,128)(2,1)} %pad_maximum_fusion.8), channel_id=1, source_target_pairs={{0,2},{1,3},{2,0},{3,1},{4,6},{5,7},{6,4},{7,5},{8,10},{9,11},{10,... | collective-permute-start | bytes 835592 | tf_op jit(solution)/shard_map/ppermute | solution.py:313
  111.3 0.7 copy-start.2
  116.5 8.3 %copy-start.12 = (pred[4,4]{1,0:T(4,128)(4,1)S(1)}, pred[4,4]{1,0:T(4,128)(4,1)}, u32[]{:S(2)}) copy-start(pred[4,4]{1,0:T(4,128)(4,1)} %iota_compare_fusion) | copy-start | bytes 52
  117.5 9.6 %copy-start.8 = (f32[8,4,4,4]{0,3,2,1:T(4,128)}, f32[8,4,4,4]{0,3,2,1:T(4,128)S(1)}, u32[]{:S(2)}) copy-start(f32[8,4,4,4]{0,3,2,1:T(4,128)S(1)} %select_reduce_fusion) | copy-start | bytes 6148
  121.5 5.6 %copy-start.4 = (f32[2,1,1,8,64,128]{5,4,3,2,1,0:T(8,128)}, f32[2,1,1,8,64,128]{5,4,3,2,1,0:T(8,128)S(1)}, u32[]{:S(2)}) copy-start(f32[2,1,1,8,64,128]{5,4,3,2,1,0:T(8,128)S(1)} %fusion.12) | copy-start | bytes 1572868
  122.3 8.8 %collective-permute-start.5 = (bf16[544,128]{1,0:T(8,128)(2,1)}, bf16[544,128]{1,0:T(8,128)(2,1)}, u32[]{:S(2)}, u32[]{:S(2)}) collective-permute-start(bf16[544,128]{1,0:T(8,128)(2,1)} %pad_maximum_fusion.10), channel_id=1, source_target_pairs={{0,4},{1,5},{2,6},{3,7},{4,0},{5,1},{6,2},{7,3},{8,12},{9,13},{10,... | collective-permute-start | bytes 417800 | tf_op jit(solution)/shard_map/ppermute | solution.py:313
  138.1 7.5 %copy-start.5 = (bf16[256,4,128]{2,1,0:T(4,128)(2,1)S(1)}, bf16[256,4,128]{2,1,0:T(4,128)(2,1)}, u32[]{:S(2)}) copy-start(bf16[256,4,128]{2,1,0:T(4,128)(2,1)} %slice.302) | copy-start | bytes 786436
  138.1 12.5 %copy-start.3 = (bf16[256,4,64]{2,1,0:T(4,128)(2,1)S(1)}, bf16[256,4,64]{2,1,0:T(4,128)(2,1)}, u32[]{:S(2)}) copy-start(bf16[256,4,64]{2,1,0:T(4,128)(2,1)} %copy-done.2) | copy-start | bytes 393220
  144.1 6.3 %collective-permute-start.6 = (bf16[1,8,4,2560]{3,1,2,0:T(8,128)(2,1)S(1)}, bf16[1,8,4,2560]{3,1,2,0:T(8,128)(2,1)S(1)}, u32[]{:S(2)}, u32[]{:S(2)}) collective-permute-start(bf16[1,8,4,2560]{3,1,2,0:T(8,128)(2,1)S(1)} %constant_dynamic-slice_fusion.1), channel_id=1, source_target_pairs={{0,8},{8,0},{1,9},{9,1},{2,10},{10,2},{3,11},{11,3},{4,12},{12,4},... | collective-permute-start | bytes 491528 | tf_op jit(solution)/shard_map/ppermute | solution.py:237
  150.5 8.1 %collective-permute-start.7 = (bf16[1,8,4,1280]{3,1,2,0:T(8,128)(2,1)S(1)}, bf16[1,8,4,1280]{3,1,2,0:T(8,128)(2,1)S(1)}, u32[]{:S(2)}, u32[]{:S(2)}) collective-permute-start(bf16[1,8,4,1280]{3,1,2,0:T(8,128)(2,1)S(1)} %get-tuple-element.38), channel_id=1, source_target_pairs={{0,4},{1,5},{2,6},{3,7},{4,0},{5,1},{6,2},{7,3},{8,12},{9,13},{10,... | collective-permute-start | bytes 245768 | tf_op jit(solution)/shard_map/ppermute | solution.py:253
  151.7 8.2 %collective-permute-start.10 = (bf16[1,8,4,1280]{3,1,2,0:T(8,128)(2,1)S(1)}, bf16[1,8,4,1280]{3,1,2,0:T(8,128)(2,1)S(1)}, u32[]{:S(2)}, u32[]{:S(2)}) collective-permute-start(bf16[1,8,4,1280]{3,1,2,0:T(8,128)(2,1)S(1)} %get-tuple-element.39), channel_id=1, source_target_pairs={{0,4},{1,5},{2,6},{3,7},{4,0},{5,1},{6,2},{7,3},{8,12},{9,13},{10,... | collective-permute-start | bytes 245768 | tf_op jit(solution)/shard_map/ppermute | solution.py:253
  158.6 8.2 %collective-permute-start.8 = (bf16[2,1,8,4,1280]{4,2,3,0,1:T(8,128)(2,1)S(1)}, bf16[2,1,8,4,1280]{4,2,3,0,1:T(8,128)(2,1)S(1)}, u32[]{:S(2)}, u32[]{:S(2)}) collective-permute-start(bf16[2,1,8,4,1280]{4,2,3,0,1:T(8,128)(2,1)S(1)} %maximum_select_fusion.6), channel_id=1, source_target_pairs={{0,2},{1,3},{2,0},{3,1},{4,6},{5,7},{6,4},{7,5},{8,10},{9,11},{10,... | collective-permute-start | bytes 491528 | tf_op jit(solution)/shard_map/ppermute | solution.py:253
  160.0 5.4 %collective-permute-start.11 = (bf16[2,1,8,4,1280]{4,2,3,1,0:T(8,128)(2,1)S(1)}, bf16[2,1,8,4,1280]{4,2,3,1,0:T(8,128)(2,1)S(1)}, u32[]{:S(2)}, u32[]{:S(2)}) collective-permute-start(bf16[2,1,8,4,1280]{4,2,3,1,0:T(8,128)(2,1)S(1)} %bitcast_select_fusion), channel_id=1, source_target_pairs={{0,1},{1,0},{2,3},{3,2},{4,5},{5,4},{6,7},{7,6},{8,9},{9,8},{10,11... | collective-permute-start | bytes 491528 | tf_op jit(solution)/shard_map/ppermute | solution.py:253
  165.4 7.6 %collective-permute-start.12 = (bf16[2,2,1,8,4,1280]{5,3,4,1,2,0:T(8,128)(2,1)S(1)}, bf16[2,2,1,8,4,1280]{5,3,4,1,2,0:T(8,128)(2,1)S(1)}, u32[]{:S(2)}, u32[]{:S(2)}) collective-permute-start(bf16[2,2,1,8,4,1280]{5,3,4,1,2,0:T(8,128)(2,1)S(1)} %maximum_select_fusion.5), channel_id=1, source_target_pairs={{0,2},{1,3},{2,0},{3,1},{4,6},{5,7},{6,4},{7,5},{8,10},{9,11},{10,... | collective-permute-start | bytes 983048 | tf_op jit(solution)/shard_map/ppermute | solution.py:253
  166.9 7.1 %collective-permute-start.9 = (bf16[2,2,1,8,4,1280]{5,3,4,1,2,0:T(8,128)(2,1)S(1)}, bf16[2,2,1,8,4,1280]{5,3,4,1,2,0:T(8,128)(2,1)S(1)}, u32[]{:S(2)}, u32[]{:S(2)}) collective-permute-start(bf16[2,2,1,8,4,1280]{5,3,4,1,2,0:T(8,128)(2,1)S(1)} %maximum_select_fusion.3), channel_id=1, source_target_pairs={{0,1},{1,0},{2,3},{3,2},{4,5},{5,4},{6,7},{7,6},{8,9},{9,8},{10,11... | collective-permute-start | bytes 983048 | tf_op jit(solution)/shard_map/ppermute | solution.py:253
  174.2 2.2 %copy-start.1 = (bf16[2560,512]{1,0:T(8,128)(2,1)S(1)}, bf16[2560,512]{1,0:T(8,128)(2,1)}, u32[]{:S(2)}) copy-start(bf16[2560,512]{1,0:T(8,128)(2,1)} %param.14) | copy-start | bytes 7864324

commit v19 on v16

--- a/solution.py
+++ b/solution.py
@@ -190,7 +190,7 @@
     req_count, rows, head = queries.shape
     n_slots = keys.shape[0]
     width = keys.shape[1]
-    ns = max(d for d in range(1, 11) if n_slots % d == 0)
+    ns = max(d for d in range(1, 26) if n_slots % d == 0)
     fixed = lambda n, sr, lr, br: (0, 0, 0)
     grid_spec = pltpu.PrefetchScalarGridSpec(
         num_scalar_prefetch=3,
@@ -209,6 +209,7 @@
     return pl.pallas_call(
         partial(slot_kernel, ns=ns, heads=heads, qpk=qpk),
         grid_spec=grid_spec,
+        compiler_params=pltpu.CompilerParams(vmem_limit_bytes=48 * 1024 * 1024),
         out_shape=[
             jax.ShapeDtypeStruct((req_count, rows, 1), jnp.float32),
             jax.ShapeDtypeStruct((req_count, rows, 1), jnp.float32),

time: 162 us -> 163 us (level)
    unnamed x24 -> x30, local copies, waits for them, and re-layouts: 5.49 us -> 5.21 us
where the time goes in v19:
time: 163 us
  waiting for transfers between devices  64.1 us (39%)
  starting transfers between devices  22.6 us (14%)
  Pallas kernels  19.3 us (12%)
  local copies, waits for them, and re-layouts  17.4 us (11%)
  other arithmetic  17.4 us (11%)
  matrix products  16.2 us (10%)
  blocking collectives  4.68 us (3%)
    ppermute x1, waiting for transfers between devices, on_device(): other_squares = lax.ppermute(squares, 'col', swap)  24.4 us
    pallas_call x1, Pallas kernels, slot_attention(): pl.pallas_call(partial(slot_kernel, ns=ns, heads=heads, qpk=qpk), grid_sp...  19.3 us
    ppermute x6, waiting for transfers between devices, doubling_gather(): got = lax.ppermute(block, axis_name, pairs)  14.9 us
    ppermute x3, waiting for transfers between devices, seq_merge(): lax.ppermute(send_values.astype(jnp.bfloat16), 'seq', pairs)  14.3 us
    dot_general x3, matrix products, on_device(): jnp.dot(gathered, matrix, preferred_element_type=jnp.float32)  8.8 us
    ppermute x2, waiting for transfers between devices, pair_scatter(): got = lax.ppermute(send, axis_name, [(0, 1), (1, 0)])  6.95 us
    ppermute x6, starting transfers between devices, doubling_gather(): got = lax.ppermute(block, axis_name, pairs)  6.91 us
    ppermute x3, starting transfers between devices, seq_merge(): got_stats = lax.ppermute(send_stats, 'seq', pairs)  6.64 us
  transfers between devices with their start and end apart: 16, of which 13 were waited for; matrix products, arithmetic and copies ran while one was open for 5% of the time, Pallas kernels for 0%

profile of v19, /device:TPU:0, one launch (start us, length us, event | category | flops | bytes accessed | tf_op | source)
XLA Modules:
  0.0 162.9 jit_solution(16732547690851491554)
XLA Ops:
  0.7 3.5 %reshape.1228 = bf16[256,2560]{1,0:T(8,128)(2,1)} reshape(bf16[64,4,2560]{2,1,0:T(4,128)(2,1)} %param.11) | data formatting | bytes 2621440 | tf_op jit(solution)/shard_map/reshape | solution.py:325
  4.2 2.9 %collective-permute-start = (bf16[256,2560]{1,0:T(8,128)(2,1)}, bf16[256,2560]{1,0:T(8,128)(2,1)}, u32[]{:S(2)}, u32[]{:S(2)}) collective-permute-start(bf16[256,2560]{1,0:T(8,128)(2,1)} %reshape.1228), channel_id=1, source_target_pairs={{0,8},{8,0},{1,9},{9,1},{2,10},{10,2},{3,11},{11,3},{4,12},{12,4},... | collective-permute-start | bytes 3932168 | tf_op jit(solution)/shard_map/ppermute | solution.py:328
  7.1 2.1 %multiply_reduce_fusion = f32[64,4]{1,0:T(8,128)S(1)} fusion(bf16[64,4,2560]{2,1,0:T(4,128)(2,1)} %param.11), kind=kLoop, calls=%fused_computation.9 | loop fusion | flops 1965824 | bytes 1311744 | tf_op jit(solution)/shard_map/reduce_sum | solution.py:330
  9.3 2.5 %psum.7 = f32[256]{0:T(256)S(1)} all-reduce(f32[256]{0:T(256)S(1)} %reduce_sum.21), channel_id=1, replica_groups=mesh['row'=2,'col'=2,'seq'=8] {'row'}, use_global_device_ids=true, to_apply=%region_1.0 | all-reduce | flops 256 | bytes 2048 | tf_op jit(solution)/shard_map/psum | solution.py:330
  11.8 24.4 %collective-permute-done.1 = f32[256]{0:T(256)S(1)} collective-permute-done((f32[256]{0:T(256)S(1)}, f32[256]{0:T(256)S(1)}, u32[]{:S(2)}, u32[]{:S(2)}) %collective-permute-start.1) | collective-permute-done | bytes 1056 | tf_op jit(solution)/shard_map/ppermute | solution.py:331
  36.3 2.8 %multiply_convert_fusion.1 = (bf16[256,2560]{1,0:T(8,128)(2,1)S(1)}, bf16[256,2560]{1,0:T(8,128)(2,1)S(1)}) fusion(f32[2560]{0:T(1024)S(1)} %copy-done.9, f32[256]{0:T(256)S(1)} %get-tuple-element.55, bf16[256,2560]{1,0:T(8,128)(2,1)} %reshape.1228, bf16[256,2560]{1,0:T(8,128)(2,1)} %collective-permute-done, pred[]{:T(512)S(6)} %eq.18, ...), kind=kLoop, calls=%fused_computation.8 | loop fusion | flops 6553600 | bytes 5255169 | tf_op jit(solution)/shard_map/convert_element_type | solution.py:335
  39.1 1.5 convolution_convert_fusion.2
  40.7 1.5 convolution_convert_fusion.1
  42.2 0.4 slice-done.1
  42.6 0.8 slice-done.2
  43.4 5.8 %convolution_convert_fusion = bf16[512,2048]{1,0:T(8,128)(2,1)S(1)} fusion(bf16[2560,2048]{1,0:T(8,128)(2,1)S(1)} %bitcast.207, bf16[256,2560]{1,0:T(8,128)(2,1)S(1)} %get-tuple-element.32, bf16[256,2560]{1,0:T(8,128)(2,1)S(1)} %get-tuple-element.31), kind=kOutput, calls=%fused_computation.5 | convolution fusion | flops 5375000576 | bytes 15204352 | tf_op jit(solution)/shard_map/dot_general | solution.py:350
  49.2 0.3 pad_maximum_fusion
  49.5 1.3 constant_dynamic-slice_fusion.2
  51.0 0.5 multiply_cosine_fusion
  51.5 3.0 %collective-permute-done.2 = bf16[1,256,3072]{2,1,0:T(8,128)(2,1)} collective-permute-done((bf16[1,256,3072]{2,1,0:T(8,128)(2,1)}, bf16[1,256,3072]{2,1,0:T(8,128)(2,1)}, u32[]{:S(2)}, u32[]{:S(2)}) %collective-permute-start.2) | collective-permute-done | bytes 1572896 | tf_op jit(solution)/shard_map/ppermute | solution.py:238
  54.5 1.9 %add_bitcast_fusion = f32[32,8,24,128]{3,1,2,0:T(8,128)S(1)} fusion(bf16[1,256,3072]{2,1,0:T(8,128)(2,1)} %collective-permute-done.2, bf16[2,256,3072]{2,1,0:T(8,128)(2,1)S(1)} %pad_maximum_fusion, s32[]{:T(128)S(6)} %select_n.253), kind=kLoop, calls=%fused_computation.4 | loop fusion | flops 2359296 | bytes 6291460
  56.5 0.6 copy.140
  57.0 0.8 slice.175
  57.9 0.4 add_convert_fusion.1
  58.3 0.8 subtract_convert_fusion
  59.1 1.4 pad_maximum_fusion.3
  60.5 0.5 copy.124
  61.2 1.3 fusion.10
  62.5 0.5 copy.100
  63.4 19.3 %shard_map.130 = (f32[64,64,1]{2,1,0:T(8,128)S(1)}, f32[64,64,1]{2,1,0:T(8,128)S(1)}, f32[64,64,128]{2,1,0:T(8,128)}) custom-call(s32[50]{0:T(128)S(1)} %copy-done.4, s32[64]{0:T(128)S(1)} %copy-done.3, s32[50]{0:T(128)S(1)} %copy-done.5, bf16[64,64,128]{2,1,0:T(8,128)(2,1)S(1)} %bitcast.170, bf16[50,128,512]{2,1,0:T(8,128)(2,1)} %k_ref.1, ...), custom_call_target="tpu_custom_call" | custom-call | tf_op jit(solution)/shard_map/pallas_call | solution.py:209
  82.7 1.3 copy-done.2
  84.0 2.2 %reduce.1 = f32[64,64]{1,0:T(8,128)S(1)} reduce(f32[64,64,1]{2,1,0:T(8,128)} %copy-done.2, f32[]{:T(128)} %constant.102), dimensions={2}, to_apply=%get-tuple-element.7.reduce_sub_computation | reduce | bytes 32772 | tf_op jit(solution)/shard_map/pallas_call | solution.py:209
  86.2 0.6 reduce.2
  86.8 1.8 %collective-permute-start.3 = (f32[2,2,2,1,8,64]{5,4,3,2,1,0:T(8,128)S(1)}, f32[2,2,2,1,8,64]{5,4,3,2,1,0:T(8,128)S(1)}, u32[]{:S(2)}, u32[]{:S(2)}) collective-permute-start(f32[2,2,2,1,8,64]{5,4,3,2,1,0:T(8,128)S(1)} %get-tuple-element.46), channel_id=1, source_target_pairs={{0,1},{1,0},{2,3},{3,2},{4,5},{5,4},{6,7},{7,6},{8,9},{9,8},{10,11... | collective-permute-start | bytes 49160 | tf_op jit(solution)/shard_map/ppermute | solution.py:285
  88.7 1.3 dynamic-slice_convert_fusion
  90.0 0.8 constant_dynamic-slice_fusion
  90.8 0.5 copy.107
  91.3 0.3 collective-permute-start.4
  91.6 1.9 %collective-permute-start.5 = (f32[2,2,1,1,8,64]{5,4,3,2,1,0:T(8,128)S(1)}, f32[2,2,1,1,8,64]{5,4,3,2,1,0:T(8,128)S(1)}, u32[]{:S(2)}, u32[]{:S(2)}) collective-permute-start(f32[2,2,1,1,8,64]{5,4,3,2,1,0:T(8,128)S(1)} %get-tuple-element.50), channel_id=1, source_target_pairs={{0,2},{1,3},{2,0},{3,1},{4,6},{5,7},{6,4},{7,5},{8,10},{9,11},{10,... | collective-permute-start | bytes 24584 | tf_op jit(solution)/shard_map/ppermute | solution.py:285
  93.5 1.9 %collective-permute-done.5 = f32[2,2,1,1,8,64]{5,4,3,2,1,0:T(8,128)S(1)} collective-permute-done((f32[2,2,1,1,8,64]{5,4,3,2,1,0:T(8,128)S(1)}, f32[2,2,1,1,8,64]{5,4,3,2,1,0:T(8,128)S(1)}, u32[]{:S(2)}, u32[]{:S(2)}) %collective-permute-start.5) | collective-permute-done | bytes 8224 | tf_op jit(solution)/shard_map/ppermute | solution.py:285
  95.5 2.9 %collective-permute-start.7 = (f32[2,1,1,1,8,64]{5,4,3,2,1,0:T(8,128)S(1)}, f32[2,1,1,1,8,64]{5,4,3,2,1,0:T(8,128)S(1)}, u32[]{:S(2)}, u32[]{:S(2)}) collective-permute-start(f32[2,1,1,1,8,64]{5,4,3,2,1,0:T(8,128)S(1)} %get-tuple-element.54), channel_id=1, source_target_pairs={{0,4},{1,5},{2,6},{3,7},{4,0},{5,1},{6,2},{7,3},{8,12},{9,13},{10,... | collective-permute-start | bytes 12296 | tf_op jit(solution)/shard_map/ppermute | solution.py:285
  98.4 1.7 %collective-permute-done.7 = f32[2,1,1,1,8,64]{5,4,3,2,1,0:T(8,128)S(1)} collective-permute-done((f32[2,1,1,1,8,64]{5,4,3,2,1,0:T(8,128)S(1)}, f32[2,1,1,1,8,64]{5,4,3,2,1,0:T(8,128)S(1)}, u32[]{:S(2)}, u32[]{:S(2)}) %collective-permute-start.7) | collective-permute-done | bytes 4128 | tf_op jit(solution)/shard_map/ppermute | solution.py:285
  100.3 4.8 %collective-permute-done.4 = bf16[2,2,1,8,64,128]{5,4,3,2,1,0:T(8,128)(2,1)S(1)} collective-permute-done((bf16[2,2,1,8,64,128]{5,4,3,2,1,0:T(8,128)(2,1)S(1)}, bf16[2,2,1,8,64,128]{5,4,3,2,1,0:T(8,128)(2,1)S(1)}, u32[]{:S(2)}, u32[]{:S(2)}) %collective-permute-start.4) | collective-permute-done | bytes 524320 | tf_op jit(solution)/shard_map/ppermute | solution.py:286
  105.0 1.8 %multiply_add_fusion = f32[2,2,1,8,64,128]{5,4,3,2,1,0:T(8,128)S(1)} fusion(bf16[2,2,1,8,64,128]{5,4,3,2,1,0:T(8,128)(2,1)S(1)} %collective-permute-done.4, f32[2,2,2,8,64,128]{5,4,3,2,1,0:T(8,128)} %bitcast.183, s32[]{:T(128)S(6)} %select_n.255, f32[2,2,8,64]{3,2,1,0:T(8,128)S(1)} %get-tuple-element.44, f32[2,2,8,64]{3,2,1,0:T(8,128)S(1)} %get-tuple-element.43), kind=kLoop, calls=%fused_computation.17 | loop fusion | flops 1048576 | bytes 2637828 | tf_op jit(solution)/shard_map/add | solution.py:295
  106.9 1.6 %collective-permute-start.6 = (bf16[2,1,1,8,64,128]{5,4,3,2,1,0:T(8,128)(2,1)S(1)}, bf16[2,1,1,8,64,128]{5,4,3,2,1,0:T(8,128)(2,1)S(1)}, u32[]{:S(2)}, u32[]{:S(2)}) collective-permute-start(bf16[2,1,1,8,64,128]{5,4,3,2,1,0:T(8,128)(2,1)S(1)} %dynamic-slice_convert_fusion.1), channel_id=1, source_target_pairs={{0,2},{1,3},{2,0},{3,1},{4,6},{5,7},{6,4},{7,5},{8,10},{9,11},{10,... | collective-permute-start | bytes 786440 | tf_op jit(solution)/shard_map/ppermute | solution.py:286
  109.3 4.8 %collective-permute-done.6 = bf16[2,1,1,8,64,128]{5,4,3,2,1,0:T(8,128)(2,1)S(1)} collective-permute-done((bf16[2,1,1,8,64,128]{5,4,3,2,1,0:T(8,128)(2,1)S(1)}, bf16[2,1,1,8,64,128]{5,4,3,2,1,0:T(8,128)(2,1)S(1)}, u32[]{:S(2)}, u32[]{:S(2)}) %collective-permute-start.6) | collective-permute-done | bytes 262176 | tf_op jit(solution)/shard_map/ppermute | solution.py:286
  114.2 0.3 multiply_add_fusion.1
  114.6 2.6 %collective-permute-start.8 = (bf16[1,1,1,8,64,128]{5,4,3,2,1,0:T(8,128)(2,1)S(1)}, bf16[1,1,1,8,64,128]{5,4,3,2,1,0:T(8,128)(2,1)S(1)}, u32[]{:S(2)}, u32[]{:S(2)}) collective-permute-start(bf16[1,1,1,8,64,128]{5,4,3,2,1,0:T(8,128)(2,1)S(1)} %dynamic-slice_convert_fusion.2), channel_id=1, source_target_pairs={{0,4},{1,5},{2,6},{3,7},{4,0},{5,1},{6,2},{7,3},{8,12},{9,13},{10,... | collective-permute-start | bytes 393224 | tf_op jit(solution)/shard_map/ppermute | solution.py:286
  117.2 4.7 %collective-permute-done.8 = bf16[1,1,1,8,64,128]{5,4,3,2,1,0:T(8,128)(2,1)S(1)} collective-permute-done((bf16[1,1,1,8,64,128]{5,4,3,2,1,0:T(8,128)(2,1)S(1)}, bf16[1,1,1,8,64,128]{5,4,3,2,1,0:T(8,128)(2,1)S(1)}, u32[]{:S(2)}, u32[]{:S(2)}) %collective-permute-start.8) | collective-permute-done | bytes 131104 | tf_op jit(solution)/shard_map/ppermute | solution.py:286
  122.1 0.3 fusion.12
  122.6 2.2 %all_gather.4 = bf16[2,8,4,2048]{3,1,2,0:T(8,128)(2,1)S(1)} all-gather(bf16[1,8,4,2048]{3,1,2,0:T(8,128)(2,1)S(1)} %convert_element_type.114), channel_id=1, replica_groups=mesh['row'=2,'col'=2,'seq'=8] {'row'}, dimensions={0}, use_global_device_ids=true | all-gather | bytes 393216 | tf_op jit(solution)/shard_map/all_gather | solution.py:414
  124.8 5.9 %fusion.2 = bf16[2,8,4,2560]{3,1,2,0:T(8,128)(2,1)S(1)} fusion(bf16[2,8,4,2048]{3,1,2,0:T(8,128)(2,1)S(1)} %all_gather.4, bf16[2048,2560]{1,0:T(8,128)(2,1)} %param.16), kind=kOutput, calls=%fused_computation.2 | convolution fusion | flops 671252480 | bytes 11075584 | tf_op jit(solution)/shard_map/dot_general | solution.py:416
  130.8 1.6 collective-permute-start.9
  132.3 0.8 reshape_reshape.8
  133.1 4.0 %collective-permute-done.9 = bf16[1,8,4,2560]{3,1,2,0:T(8,128)(2,1)S(1)} collective-permute-done((bf16[1,8,4,2560]{3,1,2,0:T(8,128)(2,1)S(1)}, bf16[1,8,4,2560]{3,1,2,0:T(8,128)(2,1)S(1)}, u32[]{:S(2)}, u32[]{:S(2)}) %collective-permute-start.9) | collective-permute-done | bytes 163872 | tf_op jit(solution)/shard_map/ppermute | solution.py:238
  137.2 1.3 collective-permute-start.10
  138.5 0.4 pad_maximum_fusion.7
  138.9 0.8 convert_element_type.120
  139.7 1.7 %collective-permute-start.13 = (bf16[1,8,4,1280]{3,1,2,0:T(8,128)(2,1)S(1)}, bf16[1,8,4,1280]{3,1,2,0:T(8,128)(2,1)S(1)}, u32[]{:S(2)}, u32[]{:S(2)}) collective-permute-start(bf16[1,8,4,1280]{3,1,2,0:T(8,128)(2,1)S(1)} %get-tuple-element.39), channel_id=1, source_target_pairs={{0,4},{1,5},{2,6},{3,7},{4,0},{5,1},{6,2},{7,3},{8,12},{9,13},{10,... | collective-permute-start | bytes 245768 | tf_op jit(solution)/shard_map/ppermute | solution.py:254
  141.3 2.8 %collective-permute-done.10 = bf16[1,8,4,1280]{3,1,2,0:T(8,128)(2,1)S(1)} collective-permute-done((bf16[1,8,4,1280]{3,1,2,0:T(8,128)(2,1)S(1)}, bf16[1,8,4,1280]{3,1,2,0:T(8,128)(2,1)S(1)}, u32[]{:S(2)}, u32[]{:S(2)}) %collective-permute-start.10) | collective-permute-done | bytes 81952 | tf_op jit(solution)/shard_map/ppermute | solution.py:254
  144.2 1.4 collective-permute-start.11
  145.6 0.7 collective-permute-done.13
  146.3 0.5 collective-permute-start.14
  146.9 5.0 %collective-permute-done.14 = bf16[2,1,8,4,1280]{4,2,3,1,0:T(8,128)(2,1)S(1)} collective-permute-done((bf16[2,1,8,4,1280]{4,2,3,1,0:T(8,128)(2,1)S(1)}, bf16[2,1,8,4,1280]{4,2,3,1,0:T(8,128)(2,1)S(1)}, u32[]{:S(2)}, u32[]{:S(2)}) %collective-permute-start.14) | collective-permute-done | bytes 163872 | tf_op jit(solution)/shard_map/ppermute | solution.py:254
  151.9 1.4 collective-permute-start.15
  153.3 0.6 collective-permute-start.12
  154.0 6.0 %collective-permute-done.15 = bf16[2,2,1,8,4,1280]{5,3,4,1,2,0:T(8,128)(2,1)S(1)} collective-permute-done((bf16[2,2,1,8,4,1280]{5,3,4,1,2,0:T(8,128)(2,1)S(1)}, bf16[2,2,1,8,4,1280]{5,3,4,1,2,0:T(8,128)(2,1)S(1)}, u32[]{:S(2)}, u32[]{:S(2)}) %collective-permute-start.15) | collective-permute-done | bytes 327712 | tf_op jit(solution)/shard_map/ppermute | solution.py:254
  160.2 0.4 collective-permute-done.12
  160.8 2.1 %copy.120 = bf16[64,4,2560]{2,1,0:T(4,128)(2,1)} copy(bf16[64,4,2560]{2,0,1:T(8,128)(2,1)S(1)} %pad_maximum_fusion.2) | data formatting | bytes 2621440
  (78 shorter events, 3.2 us)
Async XLA Ops:
  0.6 38.5 %copy-start = (bf16[2560,512]{1,0:T(8,128)(2,1)S(1)}, bf16[2560,512]{1,0:T(8,128)(2,1)}, u32[]{:S(2)}) copy-start(bf16[2560,512]{1,0:T(8,128)(2,1)} %param.14) | copy-start | bytes 7864324
  0.6 35.6 %copy-start.9 = (f32[2560]{0:T(1024)S(1)}, f32[2560]{0:T(1024)}, u32[]{:S(2)}) copy-start(f32[2560]{0:T(1024)} %param.12) | copy-start | bytes 30724
  4.2 32.0 %collective-permute-start = (bf16[256,2560]{1,0:T(8,128)(2,1)}, bf16[256,2560]{1,0:T(8,128)(2,1)}, u32[]{:S(2)}, u32[]{:S(2)}) collective-permute-start(bf16[256,2560]{1,0:T(8,128)(2,1)} %reshape.1228), channel_id=1, source_target_pairs={{0,8},{8,0},{1,9},{9,1},{2,10},{10,2},{3,11},{11,3},{4,12},{12,4},... | collective-permute-start | bytes 3932168 | tf_op jit(solution)/shard_map/ppermute | solution.py:328
  11.8 24.4 %collective-permute-start.1 = (f32[256]{0:T(256)S(1)}, f32[256]{0:T(256)S(1)}, u32[]{:S(2)}, u32[]{:S(2)}) collective-permute-start(f32[256]{0:T(256)S(1)} %psum.7), channel_id=1, source_target_pairs={{0,8},{8,0},{1,9},{9,1},{2,10},{10,2},{3,11},{11,3},{4,12},{12,4},... | collective-permute-start | bytes 3080 | tf_op jit(solution)/shard_map/ppermute | solution.py:331
  36.3 4.4 %copy-start.10 = (bf16[2560,512]{1,0:T(8,128)(2,1)S(1)}, bf16[2560,512]{1,0:T(8,128)(2,1)}, u32[]{:S(2)}) copy-start(bf16[2560,512]{1,0:T(8,128)(2,1)} %param.15) | copy-start | bytes 7864324
  39.1 3.1 %slice-start = ((s8[10485760]{0:T(1024)(128)(4,1)}), s8[4194304]{0:T(1024)(128)(4,1)S(1)}, s32[]{:S(2)}) async-start(s8[10485760]{0:T(1024)(128)(4,1)} %bitcast.206), calls=%async_computation | async-start | bytes 8388608
  39.1 3.5 %slice-start.1 = ((s8[10485760]{0:T(1024)(128)(4,1)}), s8[4194304]{0:T(1024)(128)(4,1)S(1)}, s32[]{:S(2)}) async-start(s8[10485760]{0:T(1024)(128)(4,1)} %bitcast.206), calls=%async_computation.1 | async-start | bytes 8388608
  40.7 2.7 %slice-start.2 = ((s8[10485760]{0:T(1024)(128)(4,1)}), s8[2097152]{0:T(1024)(128)(4,1)S(1)}, s32[]{:S(2)}) async-start(s8[10485760]{0:T(1024)(128)(4,1)} %bitcast.206), calls=%async_computation.2 | async-start | bytes 4194304
  49.5 1.3 copy-start.3
  50.8 3.8 %collective-permute-start.2 = (bf16[1,256,3072]{2,1,0:T(8,128)(2,1)}, bf16[1,256,3072]{2,1,0:T(8,128)(2,1)}, u32[]{:S(2)}, u32[]{:S(2)}) collective-permute-start(bf16[1,256,3072]{2,1,0:T(8,128)(2,1)} %constant_dynamic-slice_fusion.2), channel_id=1, source_target_pairs={{0,16},{16,0},{1,17},{17,1},{2,18},{18,2},{3,19},{19,3},{4,20},{20... | collective-permute-start | bytes 4718600 | tf_op jit(solution)/shard_map/ppermute | solution.py:238
  58.3 2.7 %copy-start.6 = (bf16[256,4,64]{2,1,0:T(4,128)(2,1)}, bf16[256,4,64]{2,1,0:T(4,128)(2,1)S(1)}, u32[]{:S(2)}) copy-start(bf16[256,4,64]{2,1,0:T(4,128)(2,1)S(1)} %get-tuple-element.28) | copy-start | bytes 393220
  60.5 2.9 %copy-start.4 = (s32[50]{0:T(128)S(1)}, s32[50]{0:T(128)}, u32[]{:S(2)}) copy-start(s32[50]{0:T(128)} %req_ref.1) | copy-start | bytes 604
  60.5 2.9 %copy-start.5 = (s32[50]{0:T(128)S(1)}, s32[50]{0:T(128)}, u32[]{:S(2)}) copy-start(s32[50]{0:T(128)} %blk_ref.1) | copy-start | bytes 604
  82.7 1.3 copy-start.2
  86.8 4.7 %collective-permute-start.3 = (f32[2,2,2,1,8,64]{5,4,3,2,1,0:T(8,128)S(1)}, f32[2,2,2,1,8,64]{5,4,3,2,1,0:T(8,128)S(1)}, u32[]{:S(2)}, u32[]{:S(2)}) collective-permute-start(f32[2,2,2,1,8,64]{5,4,3,2,1,0:T(8,128)S(1)} %get-tuple-element.46), channel_id=1, source_target_pairs={{0,1},{1,0},{2,3},{3,2},{4,5},{5,4},{6,7},{7,6},{8,9},{9,8},{10,11... | collective-permute-start | bytes 49160 | tf_op jit(solution)/shard_map/ppermute | solution.py:285
  91.3 13.8 %collective-permute-start.4 = (bf16[2,2,1,8,64,128]{5,4,3,2,1,0:T(8,128)(2,1)S(1)}, bf16[2,2,1,8,64,128]{5,4,3,2,1,0:T(8,128)(2,1)S(1)}, u32[]{:S(2)}, u32[]{:S(2)}) collective-permute-start(bf16[2,2,1,8,64,128]{5,4,3,2,1,0:T(8,128)(2,1)S(1)} %dynamic-slice_convert_fusion), channel_id=1, source_target_pairs={{0,1},{1,0},{2,3},{3,2},{4,5},{5,4},{6,7},{7,6},{8,9},{9,8},{10,11... | collective-permute-start | bytes 1572872 | tf_op jit(solution)/shard_map/ppermute | solution.py:286
  91.6 3.8 %collective-permute-start.5 = (f32[2,2,1,1,8,64]{5,4,3,2,1,0:T(8,128)S(1)}, f32[2,2,1,1,8,64]{5,4,3,2,1,0:T(8,128)S(1)}, u32[]{:S(2)}, u32[]{:S(2)}) collective-permute-start(f32[2,2,1,1,8,64]{5,4,3,2,1,0:T(8,128)S(1)} %get-tuple-element.50), channel_id=1, source_target_pairs={{0,2},{1,3},{2,0},{3,1},{4,6},{5,7},{6,4},{7,5},{8,10},{9,11},{10,... | collective-permute-start | bytes 24584 | tf_op jit(solution)/shard_map/ppermute | solution.py:285
  95.5 4.6 %collective-permute-start.7 = (f32[2,1,1,1,8,64]{5,4,3,2,1,0:T(8,128)S(1)}, f32[2,1,1,1,8,64]{5,4,3,2,1,0:T(8,128)S(1)}, u32[]{:S(2)}, u32[]{:S(2)}) collective-permute-start(f32[2,1,1,1,8,64]{5,4,3,2,1,0:T(8,128)S(1)} %get-tuple-element.54), channel_id=1, source_target_pairs={{0,4},{1,5},{2,6},{3,7},{4,0},{5,1},{6,2},{7,3},{8,12},{9,13},{10,... | collective-permute-start | bytes 12296 | tf_op jit(solution)/shard_map/ppermute | solution.py:285
  106.9 7.3 %collective-permute-start.6 = (bf16[2,1,1,8,64,128]{5,4,3,2,1,0:T(8,128)(2,1)S(1)}, bf16[2,1,1,8,64,128]{5,4,3,2,1,0:T(8,128)(2,1)S(1)}, u32[]{:S(2)}, u32[]{:S(2)}) collective-permute-start(bf16[2,1,1,8,64,128]{5,4,3,2,1,0:T(8,128)(2,1)S(1)} %dynamic-slice_convert_fusion.1), channel_id=1, source_target_pairs={{0,2},{1,3},{2,0},{3,1},{4,6},{5,7},{6,4},{7,5},{8,10},{9,11},{10,... | collective-permute-start | bytes 786440 | tf_op jit(solution)/shard_map/ppermute | solution.py:286
  114.6 7.3 %collective-permute-start.8 = (bf16[1,1,1,8,64,128]{5,4,3,2,1,0:T(8,128)(2,1)S(1)}, bf16[1,1,1,8,64,128]{5,4,3,2,1,0:T(8,128)(2,1)S(1)}, u32[]{:S(2)}, u32[]{:S(2)}) collective-permute-start(bf16[1,1,1,8,64,128]{5,4,3,2,1,0:T(8,128)(2,1)S(1)} %dynamic-slice_convert_fusion.2), channel_id=1, source_target_pairs={{0,4},{1,5},{2,6},{3,7},{4,0},{5,1},{6,2},{7,3},{8,12},{9,13},{10,... | collective-permute-start | bytes 393224 | tf_op jit(solution)/shard_map/ppermute | solution.py:286
  124.8 7.5 %copy-start.8 = (bf16[256,4,128]{2,1,0:T(4,128)(2,1)S(1)}, bf16[256,4,128]{2,1,0:T(4,128)(2,1)}, u32[]{:S(2)}) copy-start(bf16[256,4,128]{2,1,0:T(4,128)(2,1)} %slice.175) | copy-start | bytes 786436
  124.8 13.7 %copy-start.7 = (bf16[256,4,64]{2,1,0:T(4,128)(2,1)S(1)}, bf16[256,4,64]{2,1,0:T(4,128)(2,1)}, u32[]{:S(2)}) copy-start(bf16[256,4,64]{2,1,0:T(4,128)(2,1)} %copy-done.6) | copy-start | bytes 393220
  130.8 6.3 %collective-permute-start.9 = (bf16[1,8,4,2560]{3,1,2,0:T(8,128)(2,1)S(1)}, bf16[1,8,4,2560]{3,1,2,0:T(8,128)(2,1)S(1)}, u32[]{:S(2)}, u32[]{:S(2)}) collective-permute-start(bf16[1,8,4,2560]{3,1,2,0:T(8,128)(2,1)S(1)} %constant_dynamic-slice_fusion.1), channel_id=1, source_target_pairs={{0,8},{8,0},{1,9},{9,1},{2,10},{10,2},{3,11},{11,3},{4,12},{12,4},... | collective-permute-start | bytes 491528 | tf_op jit(solution)/shard_map/ppermute | solution.py:238
  137.2 6.9 %collective-permute-start.10 = (bf16[1,8,4,1280]{3,1,2,0:T(8,128)(2,1)S(1)}, bf16[1,8,4,1280]{3,1,2,0:T(8,128)(2,1)S(1)}, u32[]{:S(2)}, u32[]{:S(2)}) collective-permute-start(bf16[1,8,4,1280]{3,1,2,0:T(8,128)(2,1)S(1)} %get-tuple-element.38), channel_id=1, source_target_pairs={{0,4},{1,5},{2,6},{3,7},{4,0},{5,1},{6,2},{7,3},{8,12},{9,13},{10,... | collective-permute-start | bytes 245768 | tf_op jit(solution)/shard_map/ppermute | solution.py:254
  139.7 6.6 %collective-permute-start.13 = (bf16[1,8,4,1280]{3,1,2,0:T(8,128)(2,1)S(1)}, bf16[1,8,4,1280]{3,1,2,0:T(8,128)(2,1)S(1)}, u32[]{:S(2)}, u32[]{:S(2)}) collective-permute-start(bf16[1,8,4,1280]{3,1,2,0:T(8,128)(2,1)S(1)} %get-tuple-element.39), channel_id=1, source_target_pairs={{0,4},{1,5},{2,6},{3,7},{4,0},{5,1},{6,2},{7,3},{8,12},{9,13},{10,... | collective-permute-start | bytes 245768 | tf_op jit(solution)/shard_map/ppermute | solution.py:254
  144.2 9.1 %collective-permute-start.11 = (bf16[2,1,8,4,1280]{4,2,3,0,1:T(8,128)(2,1)S(1)}, bf16[2,1,8,4,1280]{4,2,3,0,1:T(8,128)(2,1)S(1)}, u32[]{:S(2)}, u32[]{:S(2)}) collective-permute-start(bf16[2,1,8,4,1280]{4,2,3,0,1:T(8,128)(2,1)S(1)} %maximum_select_fusion.6), channel_id=1, source_target_pairs={{0,2},{1,3},{2,0},{3,1},{4,6},{5,7},{6,4},{7,5},{8,10},{9,11},{10,... | collective-permute-start | bytes 491528 | tf_op jit(solution)/shard_map/ppermute | solution.py:254
  146.3 5.5 %collective-permute-start.14 = (bf16[2,1,8,4,1280]{4,2,3,1,0:T(8,128)(2,1)S(1)}, bf16[2,1,8,4,1280]{4,2,3,1,0:T(8,128)(2,1)S(1)}, u32[]{:S(2)}, u32[]{:S(2)}) collective-permute-start(bf16[2,1,8,4,1280]{4,2,3,1,0:T(8,128)(2,1)S(1)} %bitcast_select_fusion), channel_id=1, source_target_pairs={{0,1},{1,0},{2,3},{3,2},{4,5},{5,4},{6,7},{7,6},{8,9},{9,8},{10,11... | collective-permute-start | bytes 491528 | tf_op jit(solution)/shard_map/ppermute | solution.py:254
  151.9 8.1 %collective-permute-start.15 = (bf16[2,2,1,8,4,1280]{5,3,4,1,2,0:T(8,128)(2,1)S(1)}, bf16[2,2,1,8,4,1280]{5,3,4,1,2,0:T(8,128)(2,1)S(1)}, u32[]{:S(2)}, u32[]{:S(2)}) collective-permute-start(bf16[2,2,1,8,4,1280]{5,3,4,1,2,0:T(8,128)(2,1)S(1)} %maximum_select_fusion.5), channel_id=1, source_target_pairs={{0,2},{1,3},{2,0},{3,1},{4,6},{5,7},{6,4},{7,5},{8,10},{9,11},{10,... | collective-permute-start | bytes 983048 | tf_op jit(solution)/shard_map/ppermute | solution.py:254
  153.3 7.2 %collective-permute-start.12 = (bf16[2,2,1,8,4,1280]{5,3,4,1,2,0:T(8,128)(2,1)S(1)}, bf16[2,2,1,8,4,1280]{5,3,4,1,2,0:T(8,128)(2,1)S(1)}, u32[]{:S(2)}, u32[]{:S(2)}) collective-permute-start(bf16[2,2,1,8,4,1280]{5,3,4,1,2,0:T(8,128)(2,1)S(1)} %maximum_select_fusion.3), channel_id=1, source_target_pairs={{0,1},{1,0},{2,3},{3,2},{4,5},{5,4},{6,7},{7,6},{8,9},{9,8},{10,11... | collective-permute-start | bytes 983048 | tf_op jit(solution)/shard_map/ppermute | solution.py:254
  160.7 2.2 %copy-start.1 = (bf16[2560,512]{1,0:T(8,128)(2,1)S(1)}, bf16[2560,512]{1,0:T(8,128)(2,1)}, u32[]{:S(2)}) copy-start(bf16[2560,512]{1,0:T(8,128)(2,1)} %param.14) | copy-start | bytes 7864324

commit v20 on v16

--- a/solution.py
+++ b/solution.py
@@ -244,23 +244,20 @@
     stages = n.bit_length() - 1
     assert 1 << stages == n
     index = lax.axis_index(axis_name)
-    block = part[None]
     order = list(reversed(range(stages)))
     if swap_last and stages >= 2:
         order[-2], order[-1] = order[-1], order[-2]
+    block = part
+    done = []
     for bit in order:
         pairs = [(s, s ^ (1 << bit)) for s in range(n)]
         got = lax.ppermute(block, axis_name, pairs)
         low = ((index >> bit) & 1) == 0
+        place = sum(1 for d in done if d > bit)
         block = jnp.where(
-            low, jnp.stack([block, got], 0), jnp.stack([got, block], 0)
+            low, jnp.stack([block, got], place), jnp.stack([got, block], place)
         )
-    block = block.reshape((2,) * stages + part.shape)
-    axes = list(reversed(order))
-    block = block.transpose(
-        tuple(axes.index(stages - 1 - p) for p in range(stages))
-        + tuple(range(stages, stages + part.ndim))
-    )
+        done.append(bit)
     return block.reshape((n * part.shape[0],) + part.shape[1:])
 
 

time: 162 us -> 162 us (level)
  no operation moved by 1% of the time
where the time goes in v20:
time: 162 us
  waiting for transfers between devices  63.9 us (39%)
  starting transfers between devices  22.7 us (14%)
  Pallas kernels  19.7 us (12%)
  other arithmetic  17.6 us (11%)
  local copies, waits for them, and re-layouts  16.2 us (10%)
  matrix products  16.2 us (10%)
  blocking collectives  4.46 us (3%)
    ppermute x1, waiting for transfers between devices, on_device(): other_squares = lax.ppermute(squares, 'col', swap)  24.4 us
    pallas_call x1, Pallas kernels, slot_attention(): pl.pallas_call(partial(slot_kernel, ns=ns, heads=heads, qpk=qpk), grid_sp...  19.7 us
    ppermute x6, waiting for transfers between devices, doubling_gather(): got = lax.ppermute(block, axis_name, pairs)  14.8 us
    ppermute x3, waiting for transfers between devices, seq_merge(): lax.ppermute(send_values.astype(jnp.bfloat16), 'seq', pairs)  14.3 us
    dot_general x3, matrix products, on_device(): jnp.dot(gathered, matrix, preferred_element_type=jnp.float32)  8.8 us
    ppermute x6, starting transfers between devices, doubling_gather(): got = lax.ppermute(block, axis_name, pairs)  6.99 us
    ppermute x2, waiting for transfers between devices, pair_scatter(): got = lax.ppermute(send, axis_name, [(0, 1), (1, 0)])  6.82 us
    ppermute x3, starting transfers between devices, seq_merge(): got_stats = lax.ppermute(send_stats, 'seq', pairs)  6.64 us
  transfers between devices with their start and end apart: 16, of which 13 were waited for; matrix products, arithmetic and copies ran while one was open for 5% of the time, Pallas kernels for 0%

profile of v20, /device:TPU:0, one launch (start us, length us, event | category | flops | bytes accessed | tf_op | source)
XLA Modules:
  0.0 161.9 jit_solution(17691886231275767655)
XLA Ops:
  0.7 3.5 %reshape.736 = bf16[256,2560]{1,0:T(8,128)(2,1)} reshape(bf16[64,4,2560]{2,1,0:T(4,128)(2,1)} %param.11) | data formatting | bytes 2621440 | tf_op jit(solution)/shard_map/reshape | solution.py:321
  4.2 2.9 %collective-permute-start = (bf16[256,2560]{1,0:T(8,128)(2,1)}, bf16[256,2560]{1,0:T(8,128)(2,1)}, u32[]{:S(2)}, u32[]{:S(2)}) collective-permute-start(bf16[256,2560]{1,0:T(8,128)(2,1)} %reshape.736), channel_id=1, source_target_pairs={{0,8},{8,0},{1,9},{9,1},{2,10},{10,2},{3,11},{11,3},{4,12},{12,4},... | collective-permute-start | bytes 3932168 | tf_op jit(solution)/shard_map/ppermute | solution.py:324
  7.1 2.1 %multiply_reduce_fusion = f32[64,4]{1,0:T(8,128)S(1)} fusion(bf16[64,4,2560]{2,1,0:T(4,128)(2,1)} %param.11), kind=kLoop, calls=%fused_computation.9 | loop fusion | flops 1965824 | bytes 1311744 | tf_op jit(solution)/shard_map/reduce_sum | solution.py:326
  9.3 2.5 %psum.7 = f32[256]{0:T(256)S(1)} all-reduce(f32[256]{0:T(256)S(1)} %reduce_sum.21), channel_id=1, replica_groups=mesh['row'=2,'col'=2,'seq'=8] {'row'}, use_global_device_ids=true, to_apply=%region_1.0 | all-reduce | flops 256 | bytes 2048 | tf_op jit(solution)/shard_map/psum | solution.py:326
  11.8 24.4 %collective-permute-done.1 = f32[256]{0:T(256)S(1)} collective-permute-done((f32[256]{0:T(256)S(1)}, f32[256]{0:T(256)S(1)}, u32[]{:S(2)}, u32[]{:S(2)}) %collective-permute-start.1) | collective-permute-done | bytes 1056 | tf_op jit(solution)/shard_map/ppermute | solution.py:327
  36.3 2.8 %multiply_convert_fusion.1 = (bf16[256,2560]{1,0:T(8,128)(2,1)S(1)}, bf16[256,2560]{1,0:T(8,128)(2,1)S(1)}) fusion(f32[2560]{0:T(1024)S(1)} %copy-done.5, f32[256]{0:T(256)S(1)} %get-tuple-element.53, bf16[256,2560]{1,0:T(8,128)(2,1)} %reshape.736, bf16[256,2560]{1,0:T(8,128)(2,1)} %collective-permute-done, pred[]{:T(512)S(6)} %eq.18, ...), kind=kLoop, calls=%fused_computation.8 | loop fusion | flops 6553600 | bytes 5255169 | tf_op jit(solution)/shard_map/convert_element_type | solution.py:331
  39.1 1.5 convolution_convert_fusion.2
  40.7 1.5 convolution_convert_fusion.1
  42.2 0.4 slice-done.1
  42.6 0.8 slice-done.2
  43.4 5.8 %convolution_convert_fusion = bf16[512,2048]{1,0:T(8,128)(2,1)S(1)} fusion(bf16[2560,2048]{1,0:T(8,128)(2,1)S(1)} %bitcast.197, bf16[256,2560]{1,0:T(8,128)(2,1)S(1)} %get-tuple-element.32, bf16[256,2560]{1,0:T(8,128)(2,1)S(1)} %get-tuple-element.31), kind=kOutput, calls=%fused_computation.5 | convolution fusion | flops 5375000576 | bytes 15204352 | tf_op jit(solution)/shard_map/dot_general | solution.py:346
  49.2 0.3 pad_maximum_fusion
  49.5 1.6 copy-done.2
  51.1 1.3 constant_dynamic-slice_fusion.2
  52.6 0.5 multiply_cosine_fusion
  53.2 2.9 %collective-permute-done.2 = bf16[1,256,3072]{2,1,0:T(8,128)(2,1)S(1)} collective-permute-done((bf16[1,256,3072]{2,1,0:T(8,128)(2,1)}, bf16[1,256,3072]{2,1,0:T(8,128)(2,1)S(1)}, u32[]{:S(2)}, u32[]{:S(2)}) %collective-permute-start.2) | collective-permute-done | bytes 1572896 | tf_op jit(solution)/shard_map/ppermute | solution.py:237
  56.0 1.9 %add_bitcast_fusion = f32[32,8,24,128]{3,1,2,0:T(8,128)S(1)} fusion(bf16[1,256,3072]{2,1,0:T(8,128)(2,1)S(1)} %collective-permute-done.2, bf16[2,256,3072]{2,1,0:T(8,128)(2,1)} %copy-done.2, s32[]{:T(128)S(6)} %select_n.197), kind=kLoop, calls=%fused_computation.4 | loop fusion | flops 2359296 | bytes 6291460
  58.0 0.6 copy.136
  58.7 0.4 add_convert_fusion.1
  59.1 0.8 subtract_convert_fusion
  59.9 1.4 pad_maximum_fusion.3
  61.3 0.5 copy.120
  62.0 1.3 fusion.8
  63.3 0.5 copy.97
  64.2 19.7 %shard_map.130 = (f32[64,64,1]{2,1,0:T(8,128)}, f32[64,64,1]{2,1,0:T(8,128)}, f32[64,64,128]{2,1,0:T(8,128)}) custom-call(s32[50]{0:T(128)} %req_ref.1, s32[64]{0:T(128)} %len_ref.1, s32[50]{0:T(128)} %blk_ref.1, bf16[64,64,128]{2,1,0:T(8,128)(2,1)} %bitcast.161, bf16[50,128,512]{2,1,0:T(8,128)(2,1)} %k_ref.1, bf16[50,128,512]{2,1,0:T(8,128)(2,1)} %v_ref.1), custom_call_target="tpu_custom_call" | custom-call | tf_op jit(solution)/shard_map/pallas_call | solution.py:209
  83.8 2.4 %reduce.1 = f32[64,64]{1,0:T(8,128)S(1)} reduce(f32[64,64,1]{2,1,0:T(8,128)} %get-tuple-element.7, f32[]{:T(128)} %constant.102), dimensions={2}, to_apply=%get-tuple-element.7.reduce_sub_computation | reduce | bytes 32772 | tf_op jit(solution)/shard_map/pallas_call | solution.py:209
  86.2 0.6 reduce.2
  86.8 1.8 %collective-permute-start.3 = (f32[2,2,2,1,8,64]{5,4,3,2,1,0:T(8,128)S(1)}, f32[2,2,2,1,8,64]{5,4,3,2,1,0:T(8,128)S(1)}, u32[]{:S(2)}, u32[]{:S(2)}) collective-permute-start(f32[2,2,2,1,8,64]{5,4,3,2,1,0:T(8,128)S(1)} %get-tuple-element.44), channel_id=1, source_target_pairs={{0,1},{1,0},{2,3},{3,2},{4,5},{5,4},{6,7},{7,6},{8,9},{9,8},{10,11... | collective-permute-start | bytes 49160 | tf_op jit(solution)/shard_map/ppermute | solution.py:281
  88.7 1.3 dynamic-slice_convert_fusion
  90.0 0.5 copy.104
  90.5 0.3 collective-permute-start.4
  90.9 1.9 %collective-permute-start.5 = (f32[2,2,1,1,8,64]{5,4,3,2,1,0:T(8,128)S(1)}, f32[2,2,1,1,8,64]{5,4,3,2,1,0:T(8,128)S(1)}, u32[]{:S(2)}, u32[]{:S(2)}) collective-permute-start(f32[2,2,1,1,8,64]{5,4,3,2,1,0:T(8,128)S(1)} %get-tuple-element.48), channel_id=1, source_target_pairs={{0,2},{1,3},{2,0},{3,1},{4,6},{5,7},{6,4},{7,5},{8,10},{9,11},{10,... | collective-permute-start | bytes 24584 | tf_op jit(solution)/shard_map/ppermute | solution.py:281
  92.8 1.9 %collective-permute-done.5 = f32[2,2,1,1,8,64]{5,4,3,2,1,0:T(8,128)S(1)} collective-permute-done((f32[2,2,1,1,8,64]{5,4,3,2,1,0:T(8,128)S(1)}, f32[2,2,1,1,8,64]{5,4,3,2,1,0:T(8,128)S(1)}, u32[]{:S(2)}, u32[]{:S(2)}) %collective-permute-start.5) | collective-permute-done | bytes 8224 | tf_op jit(solution)/shard_map/ppermute | solution.py:281
  94.7 2.9 %collective-permute-start.7 = (f32[2,1,1,1,8,64]{5,4,3,2,1,0:T(8,128)S(1)}, f32[2,1,1,1,8,64]{5,4,3,2,1,0:T(8,128)S(1)}, u32[]{:S(2)}, u32[]{:S(2)}) collective-permute-start(f32[2,1,1,1,8,64]{5,4,3,2,1,0:T(8,128)S(1)} %get-tuple-element.52), channel_id=1, source_target_pairs={{0,4},{1,5},{2,6},{3,7},{4,0},{5,1},{6,2},{7,3},{8,12},{9,13},{10,... | collective-permute-start | bytes 12296 | tf_op jit(solution)/shard_map/ppermute | solution.py:281
  97.6 1.7 %collective-permute-done.7 = f32[2,1,1,1,8,64]{5,4,3,2,1,0:T(8,128)S(1)} collective-permute-done((f32[2,1,1,1,8,64]{5,4,3,2,1,0:T(8,128)S(1)}, f32[2,1,1,1,8,64]{5,4,3,2,1,0:T(8,128)S(1)}, u32[]{:S(2)}, u32[]{:S(2)}) %collective-permute-start.7) | collective-permute-done | bytes 4128 | tf_op jit(solution)/shard_map/ppermute | solution.py:281
  99.5 4.8 %collective-permute-done.4 = bf16[2,2,1,8,64,128]{5,4,3,2,1,0:T(8,128)(2,1)S(1)} collective-permute-done((bf16[2,2,1,8,64,128]{5,4,3,2,1,0:T(8,128)(2,1)S(1)}, bf16[2,2,1,8,64,128]{5,4,3,2,1,0:T(8,128)(2,1)S(1)}, u32[]{:S(2)}, u32[]{:S(2)}) %collective-permute-start.4) | collective-permute-done | bytes 524320 | tf_op jit(solution)/shard_map/ppermute | solution.py:282
  104.3 1.8 %multiply_add_fusion = f32[2,2,1,8,64,128]{5,4,3,2,1,0:T(8,128)S(1)} fusion(bf16[2,2,1,8,64,128]{5,4,3,2,1,0:T(8,128)(2,1)S(1)} %collective-permute-done.4, f32[2,2,2,8,64,128]{5,4,3,2,1,0:T(8,128)} %bitcast.171, s32[]{:T(128)S(6)} %select_n.199, f32[2,2,8,64]{3,2,1,0:T(8,128)S(1)} %get-tuple-element.42, f32[2,2,8,64]{3,2,1,0:T(8,128)S(1)} %get-tuple-element.41), kind=kLoop, calls=%fused_computation.17 | loop fusion | flops 1048576 | bytes 2637828 | tf_op jit(solution)/shard_map/add | solution.py:291
  106.2 1.6 %collective-permute-start.6 = (bf16[2,1,1,8,64,128]{5,4,3,2,1,0:T(8,128)(2,1)S(1)}, bf16[2,1,1,8,64,128]{5,4,3,2,1,0:T(8,128)(2,1)S(1)}, u32[]{:S(2)}, u32[]{:S(2)}) collective-permute-start(bf16[2,1,1,8,64,128]{5,4,3,2,1,0:T(8,128)(2,1)S(1)} %dynamic-slice_convert_fusion.1), channel_id=1, source_target_pairs={{0,2},{1,3},{2,0},{3,1},{4,6},{5,7},{6,4},{7,5},{8,10},{9,11},{10,... | collective-permute-start | bytes 786440 | tf_op jit(solution)/shard_map/ppermute | solution.py:282
  108.3 0.2 convolution_multiply_fusion
  108.6 4.8 %collective-permute-done.6 = bf16[2,1,1,8,64,128]{5,4,3,2,1,0:T(8,128)(2,1)S(1)} collective-permute-done((bf16[2,1,1,8,64,128]{5,4,3,2,1,0:T(8,128)(2,1)S(1)}, bf16[2,1,1,8,64,128]{5,4,3,2,1,0:T(8,128)(2,1)S(1)}, u32[]{:S(2)}, u32[]{:S(2)}) %collective-permute-start.6) | collective-permute-done | bytes 262176 | tf_op jit(solution)/shard_map/ppermute | solution.py:282
  113.4 0.3 multiply_add_fusion.1
  113.8 2.7 %collective-permute-start.8 = (bf16[1,1,1,8,64,128]{5,4,3,2,1,0:T(8,128)(2,1)S(1)}, bf16[1,1,1,8,64,128]{5,4,3,2,1,0:T(8,128)(2,1)S(1)}, u32[]{:S(2)}, u32[]{:S(2)}) collective-permute-start(bf16[1,1,1,8,64,128]{5,4,3,2,1,0:T(8,128)(2,1)S(1)} %dynamic-slice_convert_fusion.2), channel_id=1, source_target_pairs={{0,4},{1,5},{2,6},{3,7},{4,0},{5,1},{6,2},{7,3},{8,12},{9,13},{10,... | collective-permute-start | bytes 393224 | tf_op jit(solution)/shard_map/ppermute | solution.py:282
  116.5 4.7 %collective-permute-done.8 = bf16[1,1,1,8,64,128]{5,4,3,2,1,0:T(8,128)(2,1)S(1)} collective-permute-done((bf16[1,1,1,8,64,128]{5,4,3,2,1,0:T(8,128)(2,1)S(1)}, bf16[1,1,1,8,64,128]{5,4,3,2,1,0:T(8,128)(2,1)S(1)}, u32[]{:S(2)}, u32[]{:S(2)}) %collective-permute-start.8) | collective-permute-done | bytes 131104 | tf_op jit(solution)/shard_map/ppermute | solution.py:282
  121.1 0.2 multiply_add_fusion.2
  121.3 0.3 fusion.10
  121.8 2.0 %all_gather.4 = bf16[2,8,4,2048]{3,1,2,0:T(8,128)(2,1)S(1)} all-gather(bf16[1,8,4,2048]{3,1,2,0:T(8,128)(2,1)S(1)} %convert_element_type.114), channel_id=1, replica_groups=mesh['row'=2,'col'=2,'seq'=8] {'row'}, dimensions={0}, use_global_device_ids=true | all-gather | bytes 393216 | tf_op jit(solution)/shard_map/all_gather | solution.py:410
  123.8 5.9 %fusion.2 = bf16[2,8,4,2560]{3,1,2,0:T(8,128)(2,1)S(1)} fusion(bf16[2,8,4,2048]{3,1,2,0:T(8,128)(2,1)S(1)} %all_gather.4, bf16[2048,2560]{1,0:T(8,128)(2,1)} %param.16), kind=kOutput, calls=%fused_computation.2 | convolution fusion | flops 671252480 | bytes 11075584 | tf_op jit(solution)/shard_map/dot_general | solution.py:412
  129.7 1.6 collective-permute-start.9
  131.3 0.8 reshape_reshape.8
  132.1 4.0 %collective-permute-done.9 = bf16[1,8,4,2560]{3,1,2,0:T(8,128)(2,1)S(1)} collective-permute-done((bf16[1,8,4,2560]{3,1,2,0:T(8,128)(2,1)S(1)}, bf16[1,8,4,2560]{3,1,2,0:T(8,128)(2,1)S(1)}, u32[]{:S(2)}, u32[]{:S(2)}) %collective-permute-start.9) | collective-permute-done | bytes 163872 | tf_op jit(solution)/shard_map/ppermute | solution.py:237
  136.1 1.4 collective-permute-start.10
  137.5 0.4 pad_maximum_fusion.7
  137.8 0.8 convert_element_type.120
  138.6 1.6 %collective-permute-start.13 = (bf16[8,4,1280]{2,0,1:T(8,128)(2,1)S(1)}, bf16[8,4,1280]{2,0,1:T(8,128)(2,1)S(1)}, u32[]{:S(2)}, u32[]{:S(2)}) collective-permute-start(bf16[8,4,1280]{2,0,1:T(8,128)(2,1)S(1)} %get-tuple-element.39), channel_id=1, source_target_pairs={{0,4},{1,5},{2,6},{3,7},{4,0},{5,1},{6,2},{7,3},{8,12},{9,13},{10,... | collective-permute-start | bytes 245768 | tf_op jit(solution)/shard_map/ppermute | solution.py:254
  140.3 2.8 %collective-permute-done.10 = bf16[8,4,1280]{2,0,1:T(8,128)(2,1)S(1)} collective-permute-done((bf16[8,4,1280]{2,0,1:T(8,128)(2,1)S(1)}, bf16[8,4,1280]{2,0,1:T(8,128)(2,1)S(1)}, u32[]{:S(2)}, u32[]{:S(2)}) %collective-permute-start.10) | collective-permute-done | bytes 81952 | tf_op jit(solution)/shard_map/ppermute | solution.py:254
  143.1 1.5 collective-permute-start.11
  144.6 0.7 collective-permute-done.13
  145.3 0.5 collective-permute-start.14
  145.9 4.9 %collective-permute-done.14 = bf16[2,8,4,1280]{3,1,2,0:T(8,128)(2,1)S(1)} collective-permute-done((bf16[2,8,4,1280]{3,1,2,0:T(8,128)(2,1)S(1)}, bf16[2,8,4,1280]{3,1,2,0:T(8,128)(2,1)S(1)}, u32[]{:S(2)}, u32[]{:S(2)}) %collective-permute-start.14) | collective-permute-done | bytes 163872 | tf_op jit(solution)/shard_map/ppermute | solution.py:254
  150.8 1.4 collective-permute-start.15
  152.3 0.6 collective-permute-start.12
  153.0 6.0 %collective-permute-done.15 = bf16[2,2,8,4,1280]{4,2,3,0,1:T(8,128)(2,1)S(1)} collective-permute-done((bf16[2,2,8,4,1280]{4,2,3,0,1:T(8,128)(2,1)S(1)}, bf16[2,2,8,4,1280]{4,2,3,0,1:T(8,128)(2,1)S(1)}, u32[]{:S(2)}, u32[]{:S(2)}) %collective-permute-start.15) | collective-permute-done | bytes 327712 | tf_op jit(solution)/shard_map/ppermute | solution.py:254
  159.1 0.4 collective-permute-done.12
  159.8 2.1 %copy.116 = bf16[64,4,2560]{2,1,0:T(4,128)(2,1)} copy(bf16[64,4,2560]{2,0,1:T(8,128)(2,1)S(1)} %pad_maximum_fusion.2) | data formatting | bytes 2621440
  (74 shorter events, 2.9 us)
Async XLA Ops:
  0.6 38.5 %copy-start = (bf16[2560,512]{1,0:T(8,128)(2,1)S(1)}, bf16[2560,512]{1,0:T(8,128)(2,1)}, u32[]{:S(2)}) copy-start(bf16[2560,512]{1,0:T(8,128)(2,1)} %param.14) | copy-start | bytes 7864324
  0.6 35.6 %copy-start.5 = (f32[2560]{0:T(1024)S(1)}, f32[2560]{0:T(1024)}, u32[]{:S(2)}) copy-start(f32[2560]{0:T(1024)} %param.12) | copy-start | bytes 30724
  4.2 32.0 %collective-permute-start = (bf16[256,2560]{1,0:T(8,128)(2,1)}, bf16[256,2560]{1,0:T(8,128)(2,1)}, u32[]{:S(2)}, u32[]{:S(2)}) collective-permute-start(bf16[256,2560]{1,0:T(8,128)(2,1)} %reshape.736), channel_id=1, source_target_pairs={{0,8},{8,0},{1,9},{9,1},{2,10},{10,2},{3,11},{11,3},{4,12},{12,4},... | collective-permute-start | bytes 3932168 | tf_op jit(solution)/shard_map/ppermute | solution.py:324
  11.8 24.4 %collective-permute-start.1 = (f32[256]{0:T(256)S(1)}, f32[256]{0:T(256)S(1)}, u32[]{:S(2)}, u32[]{:S(2)}) collective-permute-start(f32[256]{0:T(256)S(1)} %psum.7), channel_id=1, source_target_pairs={{0,8},{8,0},{1,9},{9,1},{2,10},{10,2},{3,11},{11,3},{4,12},{12,4},... | collective-permute-start | bytes 3080 | tf_op jit(solution)/shard_map/ppermute | solution.py:327
  36.3 4.4 %copy-start.7 = (bf16[2560,512]{1,0:T(8,128)(2,1)S(1)}, bf16[2560,512]{1,0:T(8,128)(2,1)}, u32[]{:S(2)}) copy-start(bf16[2560,512]{1,0:T(8,128)(2,1)} %param.15) | copy-start | bytes 7864324
  39.1 3.1 %slice-start = ((s8[10485760]{0:T(1024)(128)(4,1)}), s8[4194304]{0:T(1024)(128)(4,1)S(1)}, s32[]{:S(2)}) async-start(s8[10485760]{0:T(1024)(128)(4,1)} %bitcast.196), calls=%async_computation | async-start | bytes 8388608
  39.1 3.5 %slice-start.1 = ((s8[10485760]{0:T(1024)(128)(4,1)}), s8[4194304]{0:T(1024)(128)(4,1)S(1)}, s32[]{:S(2)}) async-start(s8[10485760]{0:T(1024)(128)(4,1)} %bitcast.196), calls=%async_computation.1 | async-start | bytes 8388608
  40.7 2.7 %slice-start.2 = ((s8[10485760]{0:T(1024)(128)(4,1)}), s8[2097152]{0:T(1024)(128)(4,1)S(1)}, s32[]{:S(2)}) async-start(s8[10485760]{0:T(1024)(128)(4,1)} %bitcast.196), calls=%async_computation.2 | async-start | bytes 4194304
  49.5 1.6 %copy-start.2 = (bf16[2,256,3072]{2,1,0:T(8,128)(2,1)}, bf16[2,256,3072]{2,1,0:T(8,128)(2,1)S(1)}, u32[]{:S(2)}) copy-start(bf16[2,256,3072]{2,1,0:T(8,128)(2,1)S(1)} %pad_maximum_fusion) | copy-start | bytes 9437188
  51.1 1.3 copy-start.6
  52.4 3.6 %collective-permute-start.2 = (bf16[1,256,3072]{2,1,0:T(8,128)(2,1)}, bf16[1,256,3072]{2,1,0:T(8,128)(2,1)S(1)}, u32[]{:S(2)}, u32[]{:S(2)}) collective-permute-start(bf16[1,256,3072]{2,1,0:T(8,128)(2,1)} %constant_dynamic-slice_fusion.2), channel_id=1, source_target_pairs={{0,16},{16,0},{1,17},{17,1},{2,18},{18,2},{3,19},{19,3},{4,20},{20... | collective-permute-start | bytes 4718600 | tf_op jit(solution)/shard_map/ppermute | solution.py:237
  61.8 2.4 %copy-start.3 = (bf16[64,4,4,4,128]{4,3,1,2,0:T(4,128)(2,1)}, bf16[64,4,4,4,128]{4,3,1,2,0:T(4,128)(2,1)S(1)}, u32[]{:S(2)}) copy-start(bf16[64,4,4,4,128]{4,3,1,2,0:T(4,128)(2,1)S(1)} %copy.120) | copy-start | bytes 3145732
  83.8 2.4 %copy-start.4 = (f32[64,64,1]{2,1,0:T(8,128)S(1)}, f32[64,64,1]{2,1,0:T(8,128)}, u32[]{:S(2)}) copy-start(f32[64,64,1]{2,1,0:T(8,128)} %get-tuple-element.8) | copy-start | bytes 49156
  86.8 4.0 %collective-permute-start.3 = (f32[2,2,2,1,8,64]{5,4,3,2,1,0:T(8,128)S(1)}, f32[2,2,2,1,8,64]{5,4,3,2,1,0:T(8,128)S(1)}, u32[]{:S(2)}, u32[]{:S(2)}) collective-permute-start(f32[2,2,2,1,8,64]{5,4,3,2,1,0:T(8,128)S(1)} %get-tuple-element.44), channel_id=1, source_target_pairs={{0,1},{1,0},{2,3},{3,2},{4,5},{5,4},{6,7},{7,6},{8,9},{9,8},{10,11... | collective-permute-start | bytes 49160 | tf_op jit(solution)/shard_map/ppermute | solution.py:281
  90.5 13.8 %collective-permute-start.4 = (bf16[2,2,1,8,64,128]{5,4,3,2,1,0:T(8,128)(2,1)S(1)}, bf16[2,2,1,8,64,128]{5,4,3,2,1,0:T(8,128)(2,1)S(1)}, u32[]{:S(2)}, u32[]{:S(2)}) collective-permute-start(bf16[2,2,1,8,64,128]{5,4,3,2,1,0:T(8,128)(2,1)S(1)} %dynamic-slice_convert_fusion), channel_id=1, source_target_pairs={{0,1},{1,0},{2,3},{3,2},{4,5},{5,4},{6,7},{7,6},{8,9},{9,8},{10,11... | collective-permute-start | bytes 1572872 | tf_op jit(solution)/shard_map/ppermute | solution.py:282
  90.9 3.8 %collective-permute-start.5 = (f32[2,2,1,1,8,64]{5,4,3,2,1,0:T(8,128)S(1)}, f32[2,2,1,1,8,64]{5,4,3,2,1,0:T(8,128)S(1)}, u32[]{:S(2)}, u32[]{:S(2)}) collective-permute-start(f32[2,2,1,1,8,64]{5,4,3,2,1,0:T(8,128)S(1)} %get-tuple-element.48), channel_id=1, source_target_pairs={{0,2},{1,3},{2,0},{3,1},{4,6},{5,7},{6,4},{7,5},{8,10},{9,11},{10,... | collective-permute-start | bytes 24584 | tf_op jit(solution)/shard_map/ppermute | solution.py:281
  94.7 4.6 %collective-permute-start.7 = (f32[2,1,1,1,8,64]{5,4,3,2,1,0:T(8,128)S(1)}, f32[2,1,1,1,8,64]{5,4,3,2,1,0:T(8,128)S(1)}, u32[]{:S(2)}, u32[]{:S(2)}) collective-permute-start(f32[2,1,1,1,8,64]{5,4,3,2,1,0:T(8,128)S(1)} %get-tuple-element.52), channel_id=1, source_target_pairs={{0,4},{1,5},{2,6},{3,7},{4,0},{5,1},{6,2},{7,3},{8,12},{9,13},{10,... | collective-permute-start | bytes 12296 | tf_op jit(solution)/shard_map/ppermute | solution.py:281
  106.2 7.3 %collective-permute-start.6 = (bf16[2,1,1,8,64,128]{5,4,3,2,1,0:T(8,128)(2,1)S(1)}, bf16[2,1,1,8,64,128]{5,4,3,2,1,0:T(8,128)(2,1)S(1)}, u32[]{:S(2)}, u32[]{:S(2)}) collective-permute-start(bf16[2,1,1,8,64,128]{5,4,3,2,1,0:T(8,128)(2,1)S(1)} %dynamic-slice_convert_fusion.1), channel_id=1, source_target_pairs={{0,2},{1,3},{2,0},{3,1},{4,6},{5,7},{6,4},{7,5},{8,10},{9,11},{10,... | collective-permute-start | bytes 786440 | tf_op jit(solution)/shard_map/ppermute | solution.py:282
  113.8 7.3 %collective-permute-start.8 = (bf16[1,1,1,8,64,128]{5,4,3,2,1,0:T(8,128)(2,1)S(1)}, bf16[1,1,1,8,64,128]{5,4,3,2,1,0:T(8,128)(2,1)S(1)}, u32[]{:S(2)}, u32[]{:S(2)}) collective-permute-start(bf16[1,1,1,8,64,128]{5,4,3,2,1,0:T(8,128)(2,1)S(1)} %dynamic-slice_convert_fusion.2), channel_id=1, source_target_pairs={{0,4},{1,5},{2,6},{3,7},{4,0},{5,1},{6,2},{7,3},{8,12},{9,13},{10,... | collective-permute-start | bytes 393224 | tf_op jit(solution)/shard_map/ppermute | solution.py:282
  129.7 6.3 %collective-permute-start.9 = (bf16[1,8,4,2560]{3,1,2,0:T(8,128)(2,1)S(1)}, bf16[1,8,4,2560]{3,1,2,0:T(8,128)(2,1)S(1)}, u32[]{:S(2)}, u32[]{:S(2)}) collective-permute-start(bf16[1,8,4,2560]{3,1,2,0:T(8,128)(2,1)S(1)} %constant_dynamic-slice_fusion.1), channel_id=1, source_target_pairs={{0,8},{8,0},{1,9},{9,1},{2,10},{10,2},{3,11},{11,3},{4,12},{12,4},... | collective-permute-start | bytes 491528 | tf_op jit(solution)/shard_map/ppermute | solution.py:237
  136.1 6.9 %collective-permute-start.10 = (bf16[8,4,1280]{2,0,1:T(8,128)(2,1)S(1)}, bf16[8,4,1280]{2,0,1:T(8,128)(2,1)S(1)}, u32[]{:S(2)}, u32[]{:S(2)}) collective-permute-start(bf16[8,4,1280]{2,0,1:T(8,128)(2,1)S(1)} %get-tuple-element.40), channel_id=1, source_target_pairs={{0,4},{1,5},{2,6},{3,7},{4,0},{5,1},{6,2},{7,3},{8,12},{9,13},{10,... | collective-permute-start | bytes 245768 | tf_op jit(solution)/shard_map/ppermute | solution.py:254
  138.6 6.6 %collective-permute-start.13 = (bf16[8,4,1280]{2,0,1:T(8,128)(2,1)S(1)}, bf16[8,4,1280]{2,0,1:T(8,128)(2,1)S(1)}, u32[]{:S(2)}, u32[]{:S(2)}) collective-permute-start(bf16[8,4,1280]{2,0,1:T(8,128)(2,1)S(1)} %get-tuple-element.39), channel_id=1, source_target_pairs={{0,4},{1,5},{2,6},{3,7},{4,0},{5,1},{6,2},{7,3},{8,12},{9,13},{10,... | collective-permute-start | bytes 245768 | tf_op jit(solution)/shard_map/ppermute | solution.py:254
  143.1 9.1 %collective-permute-start.11 = (bf16[2,8,4,1280]{3,1,2,0:T(8,128)(2,1)S(1)}, bf16[2,8,4,1280]{3,1,2,0:T(8,128)(2,1)S(1)}, u32[]{:S(2)}, u32[]{:S(2)}) collective-permute-start(bf16[2,8,4,1280]{3,1,2,0:T(8,128)(2,1)S(1)} %maximum_select_fusion.6), channel_id=1, source_target_pairs={{0,2},{1,3},{2,0},{3,1},{4,6},{5,7},{6,4},{7,5},{8,10},{9,11},{10,... | collective-permute-start | bytes 491528 | tf_op jit(solution)/shard_map/ppermute | solution.py:254
  145.3 5.5 %collective-permute-start.14 = (bf16[2,8,4,1280]{3,1,2,0:T(8,128)(2,1)S(1)}, bf16[2,8,4,1280]{3,1,2,0:T(8,128)(2,1)S(1)}, u32[]{:S(2)}, u32[]{:S(2)}) collective-permute-start(bf16[2,8,4,1280]{3,1,2,0:T(8,128)(2,1)S(1)} %maximum_select_fusion.8), channel_id=1, source_target_pairs={{0,1},{1,0},{2,3},{3,2},{4,5},{5,4},{6,7},{7,6},{8,9},{9,8},{10,11... | collective-permute-start | bytes 491528 | tf_op jit(solution)/shard_map/ppermute | solution.py:254
  150.8 8.1 %collective-permute-start.15 = (bf16[2,2,8,4,1280]{4,2,3,0,1:T(8,128)(2,1)S(1)}, bf16[2,2,8,4,1280]{4,2,3,0,1:T(8,128)(2,1)S(1)}, u32[]{:S(2)}, u32[]{:S(2)}) collective-permute-start(bf16[2,2,8,4,1280]{4,2,3,0,1:T(8,128)(2,1)S(1)} %maximum_select_fusion.5), channel_id=1, source_target_pairs={{0,2},{1,3},{2,0},{3,1},{4,6},{5,7},{6,4},{7,5},{8,10},{9,11},{10,... | collective-permute-start | bytes 983048 | tf_op jit(solution)/shard_map/ppermute | solution.py:254
  152.3 7.2 %collective-permute-start.12 = (bf16[2,2,8,4,1280]{4,2,3,0,1:T(8,128)(2,1)S(1)}, bf16[2,2,8,4,1280]{4,2,3,0,1:T(8,128)(2,1)S(1)}, u32[]{:S(2)}, u32[]{:S(2)}) collective-permute-start(bf16[2,2,8,4,1280]{4,2,3,0,1:T(8,128)(2,1)S(1)} %maximum_select_fusion.3), channel_id=1, source_target_pairs={{0,1},{1,0},{2,3},{3,2},{4,5},{5,4},{6,7},{7,6},{8,9},{9,8},{10,11... | collective-permute-start | bytes 983048 | tf_op jit(solution)/shard_map/ppermute | solution.py:254
  159.7 2.2 %copy-start.1 = (bf16[2560,512]{1,0:T(8,128)(2,1)S(1)}, bf16[2560,512]{1,0:T(8,128)(2,1)}, u32[]{:S(2)}) copy-start(bf16[2560,512]{1,0:T(8,128)(2,1)} %param.14) | copy-start | bytes 7864324

commit v21 on v20

--- a/solution.py
+++ b/solution.py
@@ -246,7 +246,7 @@
     index = lax.axis_index(axis_name)
     order = list(reversed(range(stages)))
     if swap_last and stages >= 2:
-        order[-2], order[-1] = order[-1], order[-2]
+        order = [0] + order[:-2] + [order[-2]]
     block = part
     done = []
     for bit in order:

time: 162 us -> 164 us (1.012)
  waiting for transfers between devices: 63.9 us -> 66.7 us
    ppermute x6, waiting for transfers between devices: 14.8 us -> 17.5 us  [doubling_gather(): got = lax.ppermute(block, axis_name, pairs)]
where the time goes in v21:
time: 164 us
  waiting for transfers between devices  66.7 us (41%)
  starting transfers between devices  21.6 us (13%)
  Pallas kernels  19.7 us (12%)
  other arithmetic  17.6 us (11%)
  local copies, waits for them, and re-layouts  16.2 us (10%)
  matrix products  16.2 us (10%)
  blocking collectives  4.46 us (3%)
    ppermute x1, waiting for transfers between devices, on_device(): other_squares = lax.ppermute(squares, 'col', swap)  24.4 us
    pallas_call x1, Pallas kernels, slot_attention(): pl.pallas_call(partial(slot_kernel, ns=ns, heads=heads, qpk=qpk), grid_sp...  19.7 us
    ppermute x6, waiting for transfers between devices, doubling_gather(): got = lax.ppermute(block, axis_name, pairs)  17.5 us
    ppermute x3, waiting for transfers between devices, seq_merge(): lax.ppermute(send_values.astype(jnp.bfloat16), 'seq', pairs)  14.3 us
    dot_general x3, matrix products, on_device(): jnp.dot(gathered, matrix, preferred_element_type=jnp.float32)  8.8 us
    ppermute x2, waiting for transfers between devices, pair_scatter(): got = lax.ppermute(send, axis_name, [(0, 1), (1, 0)])  6.81 us
    ppermute x3, starting transfers between devices, seq_merge(): got_stats = lax.ppermute(send_stats, 'seq', pairs)  6.64 us
    ppermute x6, starting transfers between devices, doubling_gather(): got = lax.ppermute(block, axis_name, pairs)  5.88 us
  transfers between devices with their start and end apart: 16, of which 13 were waited for; matrix products, arithmetic and copies ran while one was open for 5% of the time, Pallas kernels for 0%

profile of v21, /device:TPU:0, one launch (start us, length us, event | category | flops | bytes accessed | tf_op | source)
XLA Modules:
  0.0 163.5 jit_solution(15791454654307680417)
XLA Ops:
  0.7 3.5 %reshape.736 = bf16[256,2560]{1,0:T(8,128)(2,1)} reshape(bf16[64,4,2560]{2,1,0:T(4,128)(2,1)} %param.11) | data formatting | bytes 2621440 | tf_op jit(solution)/shard_map/reshape | solution.py:321
  4.2 2.9 %collective-permute-start = (bf16[256,2560]{1,0:T(8,128)(2,1)}, bf16[256,2560]{1,0:T(8,128)(2,1)}, u32[]{:S(2)}, u32[]{:S(2)}) collective-permute-start(bf16[256,2560]{1,0:T(8,128)(2,1)} %reshape.736), channel_id=1, source_target_pairs={{0,8},{8,0},{1,9},{9,1},{2,10},{10,2},{3,11},{11,3},{4,12},{12,4},... | collective-permute-start | bytes 3932168 | tf_op jit(solution)/shard_map/ppermute | solution.py:324
  7.1 2.1 %multiply_reduce_fusion = f32[64,4]{1,0:T(8,128)S(1)} fusion(bf16[64,4,2560]{2,1,0:T(4,128)(2,1)} %param.11), kind=kLoop, calls=%fused_computation.9 | loop fusion | flops 1965824 | bytes 1311744 | tf_op jit(solution)/shard_map/reduce_sum | solution.py:326
  9.3 2.5 %psum.7 = f32[256]{0:T(256)S(1)} all-reduce(f32[256]{0:T(256)S(1)} %reduce_sum.21), channel_id=1, replica_groups=mesh['row'=2,'col'=2,'seq'=8] {'row'}, use_global_device_ids=true, to_apply=%region_1.0 | all-reduce | flops 256 | bytes 2048 | tf_op jit(solution)/shard_map/psum | solution.py:326
  11.8 24.4 %collective-permute-done.1 = f32[256]{0:T(256)S(1)} collective-permute-done((f32[256]{0:T(256)S(1)}, f32[256]{0:T(256)S(1)}, u32[]{:S(2)}, u32[]{:S(2)}) %collective-permute-start.1) | collective-permute-done | bytes 1056 | tf_op jit(solution)/shard_map/ppermute | solution.py:327
  36.3 2.8 %multiply_convert_fusion.1 = (bf16[256,2560]{1,0:T(8,128)(2,1)S(1)}, bf16[256,2560]{1,0:T(8,128)(2,1)S(1)}) fusion(f32[2560]{0:T(1024)S(1)} %copy-done.5, f32[256]{0:T(256)S(1)} %get-tuple-element.53, bf16[256,2560]{1,0:T(8,128)(2,1)} %reshape.736, bf16[256,2560]{1,0:T(8,128)(2,1)} %collective-permute-done, pred[]{:T(512)S(6)} %eq.18, ...), kind=kLoop, calls=%fused_computation.8 | loop fusion | flops 6553600 | bytes 5255169 | tf_op jit(solution)/shard_map/convert_element_type | solution.py:331
  39.1 1.5 convolution_convert_fusion.2
  40.7 1.5 convolution_convert_fusion.1
  42.2 0.4 slice-done.1
  42.6 0.8 slice-done.2
  43.4 5.8 %convolution_convert_fusion = bf16[512,2048]{1,0:T(8,128)(2,1)S(1)} fusion(bf16[2560,2048]{1,0:T(8,128)(2,1)S(1)} %bitcast.185, bf16[256,2560]{1,0:T(8,128)(2,1)S(1)} %get-tuple-element.32, bf16[256,2560]{1,0:T(8,128)(2,1)S(1)} %get-tuple-element.31), kind=kOutput, calls=%fused_computation.5 | convolution fusion | flops 5375000576 | bytes 15204352 | tf_op jit(solution)/shard_map/dot_general | solution.py:346
  49.2 0.3 pad_maximum_fusion
  49.5 1.6 copy-done.2
  51.1 1.3 constant_dynamic-slice_fusion.2
  52.6 0.5 multiply_cosine_fusion
  53.2 2.9 %collective-permute-done.2 = bf16[1,256,3072]{2,1,0:T(8,128)(2,1)S(1)} collective-permute-done((bf16[1,256,3072]{2,1,0:T(8,128)(2,1)}, bf16[1,256,3072]{2,1,0:T(8,128)(2,1)S(1)}, u32[]{:S(2)}, u32[]{:S(2)}) %collective-permute-start.2) | collective-permute-done | bytes 1572896 | tf_op jit(solution)/shard_map/ppermute | solution.py:237
  56.0 1.9 %add_bitcast_fusion = f32[32,8,24,128]{3,1,2,0:T(8,128)S(1)} fusion(bf16[1,256,3072]{2,1,0:T(8,128)(2,1)S(1)} %collective-permute-done.2, bf16[2,256,3072]{2,1,0:T(8,128)(2,1)} %copy-done.2, s32[]{:T(128)S(6)} %select_n.201), kind=kLoop, calls=%fused_computation.4 | loop fusion | flops 2359296 | bytes 6291460
  58.0 0.6 copy.128
  58.7 0.4 add_convert_fusion.1
  59.1 0.8 subtract_convert_fusion
  59.9 1.4 pad_maximum_fusion.3
  61.3 0.5 copy.112
  62.0 1.3 fusion.7
  63.3 0.5 copy.91
  63.8 0.2 select_reduce_fusion
  64.2 19.7 %shard_map.130 = (f32[64,64,1]{2,1,0:T(8,128)}, f32[64,64,1]{2,1,0:T(8,128)}, f32[64,64,128]{2,1,0:T(8,128)}) custom-call(s32[50]{0:T(128)} %req_ref.1, s32[64]{0:T(128)} %len_ref.1, s32[50]{0:T(128)} %blk_ref.1, bf16[64,64,128]{2,1,0:T(8,128)(2,1)} %bitcast.149, bf16[50,128,512]{2,1,0:T(8,128)(2,1)} %k_ref.1, bf16[50,128,512]{2,1,0:T(8,128)(2,1)} %v_ref.1), custom_call_target="tpu_custom_call" | custom-call | tf_op jit(solution)/shard_map/pallas_call | solution.py:209
  83.8 2.4 %reduce.1 = f32[64,64]{1,0:T(8,128)S(1)} reduce(f32[64,64,1]{2,1,0:T(8,128)} %get-tuple-element.7, f32[]{:T(128)} %constant.102), dimensions={2}, to_apply=%get-tuple-element.7.reduce_sub_computation | reduce | bytes 32772 | tf_op jit(solution)/shard_map/pallas_call | solution.py:209
  86.2 0.6 reduce.2
  86.8 1.8 %collective-permute-start.3 = (f32[2,2,2,1,8,64]{5,4,3,2,1,0:T(8,128)S(1)}, f32[2,2,2,1,8,64]{5,4,3,2,1,0:T(8,128)S(1)}, u32[]{:S(2)}, u32[]{:S(2)}) collective-permute-start(f32[2,2,2,1,8,64]{5,4,3,2,1,0:T(8,128)S(1)} %get-tuple-element.44), channel_id=1, source_target_pairs={{0,1},{1,0},{2,3},{3,2},{4,5},{5,4},{6,7},{7,6},{8,9},{9,8},{10,11... | collective-permute-start | bytes 49160 | tf_op jit(solution)/shard_map/ppermute | solution.py:281
  88.7 1.3 dynamic-slice_convert_fusion
  90.0 0.5 copy.98
  90.5 0.3 collective-permute-start.4
  90.9 1.9 %collective-permute-start.5 = (f32[2,2,1,1,8,64]{5,4,3,2,1,0:T(8,128)S(1)}, f32[2,2,1,1,8,64]{5,4,3,2,1,0:T(8,128)S(1)}, u32[]{:S(2)}, u32[]{:S(2)}) collective-permute-start(f32[2,2,1,1,8,64]{5,4,3,2,1,0:T(8,128)S(1)} %get-tuple-element.48), channel_id=1, source_target_pairs={{0,2},{1,3},{2,0},{3,1},{4,6},{5,7},{6,4},{7,5},{8,10},{9,11},{10,... | collective-permute-start | bytes 24584 | tf_op jit(solution)/shard_map/ppermute | solution.py:281
  92.8 1.9 %collective-permute-done.5 = f32[2,2,1,1,8,64]{5,4,3,2,1,0:T(8,128)S(1)} collective-permute-done((f32[2,2,1,1,8,64]{5,4,3,2,1,0:T(8,128)S(1)}, f32[2,2,1,1,8,64]{5,4,3,2,1,0:T(8,128)S(1)}, u32[]{:S(2)}, u32[]{:S(2)}) %collective-permute-start.5) | collective-permute-done | bytes 8224 | tf_op jit(solution)/shard_map/ppermute | solution.py:281
  94.7 2.9 %collective-permute-start.7 = (f32[2,1,1,1,8,64]{5,4,3,2,1,0:T(8,128)S(1)}, f32[2,1,1,1,8,64]{5,4,3,2,1,0:T(8,128)S(1)}, u32[]{:S(2)}, u32[]{:S(2)}) collective-permute-start(f32[2,1,1,1,8,64]{5,4,3,2,1,0:T(8,128)S(1)} %get-tuple-element.52), channel_id=1, source_target_pairs={{0,4},{1,5},{2,6},{3,7},{4,0},{5,1},{6,2},{7,3},{8,12},{9,13},{10,... | collective-permute-start | bytes 12296 | tf_op jit(solution)/shard_map/ppermute | solution.py:281
  97.6 1.7 %collective-permute-done.7 = f32[2,1,1,1,8,64]{5,4,3,2,1,0:T(8,128)S(1)} collective-permute-done((f32[2,1,1,1,8,64]{5,4,3,2,1,0:T(8,128)S(1)}, f32[2,1,1,1,8,64]{5,4,3,2,1,0:T(8,128)S(1)}, u32[]{:S(2)}, u32[]{:S(2)}) %collective-permute-start.7) | collective-permute-done | bytes 4128 | tf_op jit(solution)/shard_map/ppermute | solution.py:281
  99.5 4.7 %collective-permute-done.4 = bf16[2,2,1,8,64,128]{5,4,3,2,1,0:T(8,128)(2,1)S(1)} collective-permute-done((bf16[2,2,1,8,64,128]{5,4,3,2,1,0:T(8,128)(2,1)S(1)}, bf16[2,2,1,8,64,128]{5,4,3,2,1,0:T(8,128)(2,1)S(1)}, u32[]{:S(2)}, u32[]{:S(2)}) %collective-permute-start.4) | collective-permute-done | bytes 524320 | tf_op jit(solution)/shard_map/ppermute | solution.py:282
  104.3 1.8 %multiply_add_fusion = f32[2,2,1,8,64,128]{5,4,3,2,1,0:T(8,128)S(1)} fusion(bf16[2,2,1,8,64,128]{5,4,3,2,1,0:T(8,128)(2,1)S(1)} %collective-permute-done.4, f32[2,2,2,8,64,128]{5,4,3,2,1,0:T(8,128)} %bitcast.159, s32[]{:T(128)S(6)} %select_n.203, f32[2,2,8,64]{3,2,1,0:T(8,128)S(1)} %get-tuple-element.42, f32[2,2,8,64]{3,2,1,0:T(8,128)S(1)} %get-tuple-element.41), kind=kLoop, calls=%fused_computation.17 | loop fusion | flops 1048576 | bytes 2637828 | tf_op jit(solution)/shard_map/add | solution.py:291
  106.2 1.6 %collective-permute-start.6 = (bf16[2,1,1,8,64,128]{5,4,3,2,1,0:T(8,128)(2,1)S(1)}, bf16[2,1,1,8,64,128]{5,4,3,2,1,0:T(8,128)(2,1)S(1)}, u32[]{:S(2)}, u32[]{:S(2)}) collective-permute-start(bf16[2,1,1,8,64,128]{5,4,3,2,1,0:T(8,128)(2,1)S(1)} %dynamic-slice_convert_fusion.1), channel_id=1, source_target_pairs={{0,2},{1,3},{2,0},{3,1},{4,6},{5,7},{6,4},{7,5},{8,10},{9,11},{10,... | collective-permute-start | bytes 786440 | tf_op jit(solution)/shard_map/ppermute | solution.py:282
  108.3 0.2 convolution_multiply_fusion
  108.6 4.8 %collective-permute-done.6 = bf16[2,1,1,8,64,128]{5,4,3,2,1,0:T(8,128)(2,1)S(1)} collective-permute-done((bf16[2,1,1,8,64,128]{5,4,3,2,1,0:T(8,128)(2,1)S(1)}, bf16[2,1,1,8,64,128]{5,4,3,2,1,0:T(8,128)(2,1)S(1)}, u32[]{:S(2)}, u32[]{:S(2)}) %collective-permute-start.6) | collective-permute-done | bytes 262176 | tf_op jit(solution)/shard_map/ppermute | solution.py:282
  113.4 0.3 multiply_add_fusion.1
  113.8 2.7 %collective-permute-start.8 = (bf16[1,1,1,8,64,128]{5,4,3,2,1,0:T(8,128)(2,1)S(1)}, bf16[1,1,1,8,64,128]{5,4,3,2,1,0:T(8,128)(2,1)S(1)}, u32[]{:S(2)}, u32[]{:S(2)}) collective-permute-start(bf16[1,1,1,8,64,128]{5,4,3,2,1,0:T(8,128)(2,1)S(1)} %dynamic-slice_convert_fusion.2), channel_id=1, source_target_pairs={{0,4},{1,5},{2,6},{3,7},{4,0},{5,1},{6,2},{7,3},{8,12},{9,13},{10,... | collective-permute-start | bytes 393224 | tf_op jit(solution)/shard_map/ppermute | solution.py:282
  116.5 4.7 %collective-permute-done.8 = bf16[1,1,1,8,64,128]{5,4,3,2,1,0:T(8,128)(2,1)S(1)} collective-permute-done((bf16[1,1,1,8,64,128]{5,4,3,2,1,0:T(8,128)(2,1)S(1)}, bf16[1,1,1,8,64,128]{5,4,3,2,1,0:T(8,128)(2,1)S(1)}, u32[]{:S(2)}, u32[]{:S(2)}) %collective-permute-start.8) | collective-permute-done | bytes 131104 | tf_op jit(solution)/shard_map/ppermute | solution.py:282
  121.1 0.2 multiply_add_fusion.2
  121.3 0.3 fusion.9
  121.8 2.0 %all_gather.4 = bf16[2,8,4,2048]{3,1,2,0:T(8,128)(2,1)S(1)} all-gather(bf16[1,8,4,2048]{3,1,2,0:T(8,128)(2,1)S(1)} %convert_element_type.114), channel_id=1, replica_groups=mesh['row'=2,'col'=2,'seq'=8] {'row'}, dimensions={0}, use_global_device_ids=true | all-gather | bytes 393216 | tf_op jit(solution)/shard_map/all_gather | solution.py:410
  123.8 5.9 %fusion.2 = bf16[2,8,4,2560]{3,1,2,0:T(8,128)(2,1)S(1)} fusion(bf16[2,8,4,2048]{3,1,2,0:T(8,128)(2,1)S(1)} %all_gather.4, bf16[2048,2560]{1,0:T(8,128)(2,1)} %param.16), kind=kOutput, calls=%fused_computation.2 | convolution fusion | flops 671252480 | bytes 11075584 | tf_op jit(solution)/shard_map/dot_general | solution.py:412
  129.7 1.6 collective-permute-start.9
  131.3 0.8 reshape_reshape.8
  132.1 4.0 %collective-permute-done.9 = bf16[1,8,4,2560]{3,1,2,0:T(8,128)(2,1)S(1)} collective-permute-done((bf16[1,8,4,2560]{3,1,2,0:T(8,128)(2,1)S(1)}, bf16[1,8,4,2560]{3,1,2,0:T(8,128)(2,1)S(1)}, u32[]{:S(2)}, u32[]{:S(2)}) %collective-permute-start.9) | collective-permute-done | bytes 163872 | tf_op jit(solution)/shard_map/ppermute | solution.py:237
  136.1 1.4 collective-permute-start.10
  137.5 0.4 pad_maximum_fusion.7
  137.8 0.8 convert_element_type.120
  138.6 0.5 collective-permute-start.13
  139.1 3.4 %collective-permute-done.10 = bf16[8,4,1280]{2,0,1:T(8,128)(2,1)S(1)} collective-permute-done((bf16[8,4,1280]{2,0,1:T(8,128)(2,1)S(1)}, bf16[8,4,1280]{2,0,1:T(8,128)(2,1)S(1)}, u32[]{:S(2)}, u32[]{:S(2)}) %collective-permute-start.10) | collective-permute-done | bytes 81952 | tf_op jit(solution)/shard_map/ppermute | solution.py:254
  142.6 0.3 collective-permute-start.11
  143.1 2.8 %collective-permute-start.14 = (bf16[2,8,4,1280]{3,1,2,0:T(8,128)(2,1)S(1)}, bf16[2,8,4,1280]{3,1,2,0:T(8,128)(2,1)S(1)}, u32[]{:S(2)}, u32[]{:S(2)}) collective-permute-start(bf16[2,8,4,1280]{3,1,2,0:T(8,128)(2,1)S(1)} %maximum_select_fusion.9), channel_id=1, source_target_pairs={{0,4},{1,5},{2,6},{3,7},{4,0},{5,1},{6,2},{7,3},{8,12},{9,13},{10,... | collective-permute-start | bytes 491528 | tf_op jit(solution)/shard_map/ppermute | solution.py:254
  146.0 6.9 %collective-permute-done.14 = bf16[2,8,4,1280]{3,1,2,0:T(8,128)(2,1)S(1)} collective-permute-done((bf16[2,8,4,1280]{3,1,2,0:T(8,128)(2,1)S(1)}, bf16[2,8,4,1280]{3,1,2,0:T(8,128)(2,1)S(1)}, u32[]{:S(2)}, u32[]{:S(2)}) %collective-permute-start.14) | collective-permute-done | bytes 163872 | tf_op jit(solution)/shard_map/ppermute | solution.py:254
  152.9 0.3 collective-permute-start.15
  153.2 0.6 collective-permute-start.12
  153.9 6.1 %collective-permute-done.15 = bf16[2,2,8,4,1280]{4,2,3,1,0:T(8,128)(2,1)S(1)} collective-permute-done((bf16[2,2,8,4,1280]{4,2,3,1,0:T(8,128)(2,1)S(1)}, bf16[2,2,8,4,1280]{4,2,3,1,0:T(8,128)(2,1)S(1)}, u32[]{:S(2)}, u32[]{:S(2)}) %collective-permute-start.15) | collective-permute-done | bytes 327712 | tf_op jit(solution)/shard_map/ppermute | solution.py:254
  160.2 1.0 collective-permute-done.12
  161.4 2.1 %copy.108 = bf16[64,4,2560]{2,1,0:T(4,128)(2,1)} copy(bf16[64,4,2560]{2,0,1:T(8,128)(2,1)S(1)} %pad_maximum_fusion.2) | data formatting | bytes 2621440
  (74 shorter events, 2.9 us)
Async XLA Ops:
  0.6 38.5 %copy-start = (bf16[2560,512]{1,0:T(8,128)(2,1)S(1)}, bf16[2560,512]{1,0:T(8,128)(2,1)}, u32[]{:S(2)}) copy-start(bf16[2560,512]{1,0:T(8,128)(2,1)} %param.14) | copy-start | bytes 7864324
  0.6 35.6 %copy-start.5 = (f32[2560]{0:T(1024)S(1)}, f32[2560]{0:T(1024)}, u32[]{:S(2)}) copy-start(f32[2560]{0:T(1024)} %param.12) | copy-start | bytes 30724
  4.2 32.0 %collective-permute-start = (bf16[256,2560]{1,0:T(8,128)(2,1)}, bf16[256,2560]{1,0:T(8,128)(2,1)}, u32[]{:S(2)}, u32[]{:S(2)}) collective-permute-start(bf16[256,2560]{1,0:T(8,128)(2,1)} %reshape.736), channel_id=1, source_target_pairs={{0,8},{8,0},{1,9},{9,1},{2,10},{10,2},{3,11},{11,3},{4,12},{12,4},... | collective-permute-start | bytes 3932168 | tf_op jit(solution)/shard_map/ppermute | solution.py:324
  11.8 24.4 %collective-permute-start.1 = (f32[256]{0:T(256)S(1)}, f32[256]{0:T(256)S(1)}, u32[]{:S(2)}, u32[]{:S(2)}) collective-permute-start(f32[256]{0:T(256)S(1)} %psum.7), channel_id=1, source_target_pairs={{0,8},{8,0},{1,9},{9,1},{2,10},{10,2},{3,11},{11,3},{4,12},{12,4},... | collective-permute-start | bytes 3080 | tf_op jit(solution)/shard_map/ppermute | solution.py:327
  36.3 4.4 %copy-start.7 = (bf16[2560,512]{1,0:T(8,128)(2,1)S(1)}, bf16[2560,512]{1,0:T(8,128)(2,1)}, u32[]{:S(2)}) copy-start(bf16[2560,512]{1,0:T(8,128)(2,1)} %param.15) | copy-start | bytes 7864324
  39.1 3.1 %slice-start = ((s8[10485760]{0:T(1024)(128)(4,1)}), s8[4194304]{0:T(1024)(128)(4,1)S(1)}, s32[]{:S(2)}) async-start(s8[10485760]{0:T(1024)(128)(4,1)} %bitcast.184), calls=%async_computation | async-start | bytes 8388608
  39.1 3.5 %slice-start.1 = ((s8[10485760]{0:T(1024)(128)(4,1)}), s8[4194304]{0:T(1024)(128)(4,1)S(1)}, s32[]{:S(2)}) async-start(s8[10485760]{0:T(1024)(128)(4,1)} %bitcast.184), calls=%async_computation.1 | async-start | bytes 8388608
  40.7 2.7 %slice-start.2 = ((s8[10485760]{0:T(1024)(128)(4,1)}), s8[2097152]{0:T(1024)(128)(4,1)S(1)}, s32[]{:S(2)}) async-start(s8[10485760]{0:T(1024)(128)(4,1)} %bitcast.184), calls=%async_computation.2 | async-start | bytes 4194304
  49.5 1.6 copy-start.2
  51.1 1.3 copy-start.6
  52.4 3.6 %collective-permute-start.2 = (bf16[1,256,3072]{2,1,0:T(8,128)(2,1)}, bf16[1,256,3072]{2,1,0:T(8,128)(2,1)S(1)}, u32[]{:S(2)}, u32[]{:S(2)}) collective-permute-start(bf16[1,256,3072]{2,1,0:T(8,128)(2,1)} %constant_dynamic-slice_fusion.2), channel_id=1, source_target_pairs={{0,16},{16,0},{1,17},{17,1},{2,18},{18,2},{3,19},{19,3},{4,20},{20... | collective-permute-start | bytes 4718600 | tf_op jit(solution)/shard_map/ppermute | solution.py:237
  61.8 2.4 %copy-start.3 = (bf16[64,4,4,4,128]{4,3,1,2,0:T(4,128)(2,1)}, bf16[64,4,4,4,128]{4,3,1,2,0:T(4,128)(2,1)S(1)}, u32[]{:S(2)}) copy-start(bf16[64,4,4,4,128]{4,3,1,2,0:T(4,128)(2,1)S(1)} %copy.112) | copy-start | bytes 3145732
  83.8 2.4 %copy-start.4 = (f32[64,64,1]{2,1,0:T(8,128)S(1)}, f32[64,64,1]{2,1,0:T(8,128)}, u32[]{:S(2)}) copy-start(f32[64,64,1]{2,1,0:T(8,128)} %get-tuple-element.8) | copy-start | bytes 49156
  86.8 4.0 %collective-permute-start.3 = (f32[2,2,2,1,8,64]{5,4,3,2,1,0:T(8,128)S(1)}, f32[2,2,2,1,8,64]{5,4,3,2,1,0:T(8,128)S(1)}, u32[]{:S(2)}, u32[]{:S(2)}) collective-permute-start(f32[2,2,2,1,8,64]{5,4,3,2,1,0:T(8,128)S(1)} %get-tuple-element.44), channel_id=1, source_target_pairs={{0,1},{1,0},{2,3},{3,2},{4,5},{5,4},{6,7},{7,6},{8,9},{9,8},{10,11... | collective-permute-start | bytes 49160 | tf_op jit(solution)/shard_map/ppermute | solution.py:281
  90.5 13.8 %collective-permute-start.4 = (bf16[2,2,1,8,64,128]{5,4,3,2,1,0:T(8,128)(2,1)S(1)}, bf16[2,2,1,8,64,128]{5,4,3,2,1,0:T(8,128)(2,1)S(1)}, u32[]{:S(2)}, u32[]{:S(2)}) collective-permute-start(bf16[2,2,1,8,64,128]{5,4,3,2,1,0:T(8,128)(2,1)S(1)} %dynamic-slice_convert_fusion), channel_id=1, source_target_pairs={{0,1},{1,0},{2,3},{3,2},{4,5},{5,4},{6,7},{7,6},{8,9},{9,8},{10,11... | collective-permute-start | bytes 1572872 | tf_op jit(solution)/shard_map/ppermute | solution.py:282
  90.9 3.8 %collective-permute-start.5 = (f32[2,2,1,1,8,64]{5,4,3,2,1,0:T(8,128)S(1)}, f32[2,2,1,1,8,64]{5,4,3,2,1,0:T(8,128)S(1)}, u32[]{:S(2)}, u32[]{:S(2)}) collective-permute-start(f32[2,2,1,1,8,64]{5,4,3,2,1,0:T(8,128)S(1)} %get-tuple-element.48), channel_id=1, source_target_pairs={{0,2},{1,3},{2,0},{3,1},{4,6},{5,7},{6,4},{7,5},{8,10},{9,11},{10,... | collective-permute-start | bytes 24584 | tf_op jit(solution)/shard_map/ppermute | solution.py:281
  94.7 4.6 %collective-permute-start.7 = (f32[2,1,1,1,8,64]{5,4,3,2,1,0:T(8,128)S(1)}, f32[2,1,1,1,8,64]{5,4,3,2,1,0:T(8,128)S(1)}, u32[]{:S(2)}, u32[]{:S(2)}) collective-permute-start(f32[2,1,1,1,8,64]{5,4,3,2,1,0:T(8,128)S(1)} %get-tuple-element.52), channel_id=1, source_target_pairs={{0,4},{1,5},{2,6},{3,7},{4,0},{5,1},{6,2},{7,3},{8,12},{9,13},{10,... | collective-permute-start | bytes 12296 | tf_op jit(solution)/shard_map/ppermute | solution.py:281
  106.2 7.3 %collective-permute-start.6 = (bf16[2,1,1,8,64,128]{5,4,3,2,1,0:T(8,128)(2,1)S(1)}, bf16[2,1,1,8,64,128]{5,4,3,2,1,0:T(8,128)(2,1)S(1)}, u32[]{:S(2)}, u32[]{:S(2)}) collective-permute-start(bf16[2,1,1,8,64,128]{5,4,3,2,1,0:T(8,128)(2,1)S(1)} %dynamic-slice_convert_fusion.1), channel_id=1, source_target_pairs={{0,2},{1,3},{2,0},{3,1},{4,6},{5,7},{6,4},{7,5},{8,10},{9,11},{10,... | collective-permute-start | bytes 786440 | tf_op jit(solution)/shard_map/ppermute | solution.py:282
  113.8 7.3 %collective-permute-start.8 = (bf16[1,1,1,8,64,128]{5,4,3,2,1,0:T(8,128)(2,1)S(1)}, bf16[1,1,1,8,64,128]{5,4,3,2,1,0:T(8,128)(2,1)S(1)}, u32[]{:S(2)}, u32[]{:S(2)}) collective-permute-start(bf16[1,1,1,8,64,128]{5,4,3,2,1,0:T(8,128)(2,1)S(1)} %dynamic-slice_convert_fusion.2), channel_id=1, source_target_pairs={{0,4},{1,5},{2,6},{3,7},{4,0},{5,1},{6,2},{7,3},{8,12},{9,13},{10,... | collective-permute-start | bytes 393224 | tf_op jit(solution)/shard_map/ppermute | solution.py:282
  129.7 6.3 %collective-permute-start.9 = (bf16[1,8,4,2560]{3,1,2,0:T(8,128)(2,1)S(1)}, bf16[1,8,4,2560]{3,1,2,0:T(8,128)(2,1)S(1)}, u32[]{:S(2)}, u32[]{:S(2)}) collective-permute-start(bf16[1,8,4,2560]{3,1,2,0:T(8,128)(2,1)S(1)} %constant_dynamic-slice_fusion.1), channel_id=1, source_target_pairs={{0,8},{8,0},{1,9},{9,1},{2,10},{10,2},{3,11},{11,3},{4,12},{12,4},... | collective-permute-start | bytes 491528 | tf_op jit(solution)/shard_map/ppermute | solution.py:237
  136.1 6.4 %collective-permute-start.10 = (bf16[8,4,1280]{2,0,1:T(8,128)(2,1)S(1)}, bf16[8,4,1280]{2,0,1:T(8,128)(2,1)S(1)}, u32[]{:S(2)}, u32[]{:S(2)}) collective-permute-start(bf16[8,4,1280]{2,0,1:T(8,128)(2,1)S(1)} %get-tuple-element.40), channel_id=1, source_target_pairs={{0,4},{1,5},{2,6},{3,7},{4,0},{5,1},{6,2},{7,3},{8,12},{9,13},{10,... | collective-permute-start | bytes 245768 | tf_op jit(solution)/shard_map/ppermute | solution.py:254
  138.6 4.4 %collective-permute-start.13 = (bf16[8,4,1280]{2,0,1:T(8,128)(2,1)S(1)}, bf16[8,4,1280]{2,0,1:T(8,128)(2,1)S(1)}, u32[]{:S(2)}, u32[]{:S(2)}) collective-permute-start(bf16[8,4,1280]{2,0,1:T(8,128)(2,1)S(1)} %get-tuple-element.39), channel_id=1, source_target_pairs={{0,1},{1,0},{2,3},{3,2},{4,5},{5,4},{6,7},{7,6},{8,9},{9,8},{10,11... | collective-permute-start | bytes 245768 | tf_op jit(solution)/shard_map/ppermute | solution.py:254
  142.6 10.6 %collective-permute-start.11 = (bf16[2,8,4,1280]{3,1,2,0:T(8,128)(2,1)S(1)}, bf16[2,8,4,1280]{3,1,2,0:T(8,128)(2,1)S(1)}, u32[]{:S(2)}, u32[]{:S(2)}) collective-permute-start(bf16[2,8,4,1280]{3,1,2,0:T(8,128)(2,1)S(1)} %maximum_select_fusion.7), channel_id=1, source_target_pairs={{0,2},{1,3},{2,0},{3,1},{4,6},{5,7},{6,4},{7,5},{8,10},{9,11},{10,... | collective-permute-start | bytes 491528 | tf_op jit(solution)/shard_map/ppermute | solution.py:254
  143.1 9.7 %collective-permute-start.14 = (bf16[2,8,4,1280]{3,1,2,0:T(8,128)(2,1)S(1)}, bf16[2,8,4,1280]{3,1,2,0:T(8,128)(2,1)S(1)}, u32[]{:S(2)}, u32[]{:S(2)}) collective-permute-start(bf16[2,8,4,1280]{3,1,2,0:T(8,128)(2,1)S(1)} %maximum_select_fusion.9), channel_id=1, source_target_pairs={{0,4},{1,5},{2,6},{3,7},{4,0},{5,1},{6,2},{7,3},{8,12},{9,13},{10,... | collective-permute-start | bytes 491528 | tf_op jit(solution)/shard_map/ppermute | solution.py:254
  152.9 7.1 %collective-permute-start.15 = (bf16[2,2,8,4,1280]{4,2,3,1,0:T(8,128)(2,1)S(1)}, bf16[2,2,8,4,1280]{4,2,3,1,0:T(8,128)(2,1)S(1)}, u32[]{:S(2)}, u32[]{:S(2)}) collective-permute-start(bf16[2,2,8,4,1280]{4,2,3,1,0:T(8,128)(2,1)S(1)} %maximum_select_fusion.5), channel_id=1, source_target_pairs={{0,2},{1,3},{2,0},{3,1},{4,6},{5,7},{6,4},{7,5},{8,10},{9,11},{10,... | collective-permute-start | bytes 983048 | tf_op jit(solution)/shard_map/ppermute | solution.py:254
  153.2 7.9 %collective-permute-start.12 = (bf16[2,2,8,4,1280]{4,2,3,0,1:T(8,128)(2,1)S(1)}, bf16[2,2,8,4,1280]{4,2,3,0,1:T(8,128)(2,1)S(1)}, u32[]{:S(2)}, u32[]{:S(2)}) collective-permute-start(bf16[2,2,8,4,1280]{4,2,3,0,1:T(8,128)(2,1)S(1)} %maximum_select_fusion.3), channel_id=1, source_target_pairs={{0,1},{1,0},{2,3},{3,2},{4,5},{5,4},{6,7},{7,6},{8,9},{9,8},{10,11... | collective-permute-start | bytes 983048 | tf_op jit(solution)/shard_map/ppermute | solution.py:254
  161.3 2.2 %copy-start.1 = (bf16[2560,512]{1,0:T(8,128)(2,1)S(1)}, bf16[2560,512]{1,0:T(8,128)(2,1)}, u32[]{:S(2)}) copy-start(bf16[2560,512]{1,0:T(8,128)(2,1)} %param.14) | copy-start | bytes 7864324

commit v22 on v20

--- a/solution.py
+++ b/solution.py
@@ -407,8 +407,8 @@
         .reshape(per, step_count, -1)
         .astype(jnp.bfloat16)
     )
-    piece_rows = lax.all_gather(heads_out, "row", axis=0, tiled=False)
-    n_row = piece_rows.shape[0]
+    n_row = lax.axis_size("row")
+    piece_rows = pair_gather(heads_out, "row")
     product = jnp.dot(
         piece_rows.reshape(n_row * per * step_count, -1), wo, preferred_element_type=jnp.float32
     )

time: 162 us -> 162 us (level)
  blocking collectives: 4.46 us -> 2.47 us
    all_gather x1 -> x0, blocking collectives: 1.99 us -> none  [on_device(): piece_rows = lax.all_gather(heads_out, 'row', axis=0, tiled=False)]
  transfers between devices with their start and end apart: 16 -> 17, of which waited for: 13 -> 14; matrix products, arithmetic and copies ran while one was open for 5% -> 5% of each run, Pallas kernels for 0% -> 0%
where the time goes in v22:
time: 162 us; the launch traced here: 161 us
  waiting for transfers between devices  65.2 us (40%)
  starting transfers between devices  22.8 us (14%)
  Pallas kernels  19.7 us (12%)
  other arithmetic  17.6 us (11%)
  local copies, waits for them, and re-layouts  16.3 us (10%)
  matrix products  16.2 us (10%)
  blocking collectives  2.47 us (2%)
    ppermute x1, waiting for transfers between devices, on_device(): other_squares = lax.ppermute(squares, 'col', swap)  24.4 us
    pallas_call x1, Pallas kernels, slot_attention(): pl.pallas_call(partial(slot_kernel, ns=ns, heads=heads, qpk=qpk), grid_sp...  19.7 us
    ppermute x6, waiting for transfers between devices, doubling_gather(): got = lax.ppermute(block, axis_name, pairs)  14.8 us
    ppermute x3, waiting for transfers between devices, seq_merge(): lax.ppermute(send_values.astype(jnp.bfloat16), 'seq', pairs)  14.3 us
    dot_general x3, matrix products, on_device(): jnp.dot(gathered, matrix, preferred_element_type=jnp.float32)  8.8 us
    ppermute x6, starting transfers between devices, doubling_gather(): got = lax.ppermute(block, axis_name, pairs)  6.98 us
    ppermute x2, waiting for transfers between devices, pair_scatter(): got = lax.ppermute(send, axis_name, [(0, 1), (1, 0)])  6.82 us
    ppermute x3, starting transfers between devices, seq_merge(): got_stats = lax.ppermute(send_stats, 'seq', pairs)  6.64 us
  transfers between devices with their start and end apart: 17, of which 14 were waited for; matrix products, arithmetic and copies ran while one was open for 5% of the time, Pallas kernels for 0%

profile of v22, /device:TPU:0, one launch (start us, length us, event | category | flops | bytes accessed | tf_op | source)
XLA Modules:
  0.0 161.3 jit_solution(2141082406315700296)
XLA Ops:
  0.7 3.5 %reshape.731 = bf16[256,2560]{1,0:T(8,128)(2,1)} reshape(bf16[64,4,2560]{2,1,0:T(4,128)(2,1)} %param.11) | data formatting | bytes 2621440 | tf_op jit(solution)/shard_map/reshape | solution.py:321
  4.2 2.9 %collective-permute-start = (bf16[256,2560]{1,0:T(8,128)(2,1)}, bf16[256,2560]{1,0:T(8,128)(2,1)}, u32[]{:S(2)}, u32[]{:S(2)}) collective-permute-start(bf16[256,2560]{1,0:T(8,128)(2,1)} %reshape.731), channel_id=1, source_target_pairs={{0,8},{8,0},{1,9},{9,1},{2,10},{10,2},{3,11},{11,3},{4,12},{12,4},... | collective-permute-start | bytes 3932168 | tf_op jit(solution)/shard_map/ppermute | solution.py:324
  7.1 2.1 %multiply_reduce_fusion = f32[64,4]{1,0:T(8,128)S(1)} fusion(bf16[64,4,2560]{2,1,0:T(4,128)(2,1)} %param.11), kind=kLoop, calls=%fused_computation.9 | loop fusion | flops 1965824 | bytes 1311744 | tf_op jit(solution)/shard_map/reduce_sum | solution.py:326
  9.3 2.5 %psum.7 = f32[256]{0:T(256)S(1)} all-reduce(f32[256]{0:T(256)S(1)} %reduce_sum.21), channel_id=1, replica_groups=mesh['row'=2,'col'=2,'seq'=8] {'row'}, use_global_device_ids=true, to_apply=%region_1.0 | all-reduce | flops 256 | bytes 2048 | tf_op jit(solution)/shard_map/psum | solution.py:326
  11.8 24.4 %collective-permute-done.1 = f32[256]{0:T(256)S(1)} collective-permute-done((f32[256]{0:T(256)S(1)}, f32[256]{0:T(256)S(1)}, u32[]{:S(2)}, u32[]{:S(2)}) %collective-permute-start.1) | collective-permute-done | bytes 1056 | tf_op jit(solution)/shard_map/ppermute | solution.py:327
  36.3 2.8 %multiply_convert_fusion.1 = (bf16[256,2560]{1,0:T(8,128)(2,1)S(1)}, bf16[256,2560]{1,0:T(8,128)(2,1)S(1)}) fusion(f32[2560]{0:T(1024)S(1)} %copy-done.5, f32[256]{0:T(256)S(1)} %get-tuple-element.53, bf16[256,2560]{1,0:T(8,128)(2,1)} %reshape.731, bf16[256,2560]{1,0:T(8,128)(2,1)} %collective-permute-done, pred[]{:T(512)S(6)} %eq.22, ...), kind=kLoop, calls=%fused_computation.8 | loop fusion | flops 6553600 | bytes 5255169 | tf_op jit(solution)/shard_map/convert_element_type | solution.py:331
  39.1 1.5 convolution_convert_fusion.2
  40.7 1.5 convolution_convert_fusion.1
  42.2 0.4 slice-done.1
  42.6 0.8 slice-done.2
  43.4 5.8 %convolution_convert_fusion = bf16[512,2048]{1,0:T(8,128)(2,1)S(1)} fusion(bf16[2560,2048]{1,0:T(8,128)(2,1)S(1)} %bitcast.200, bf16[256,2560]{1,0:T(8,128)(2,1)S(1)} %get-tuple-element.32, bf16[256,2560]{1,0:T(8,128)(2,1)S(1)} %get-tuple-element.31), kind=kOutput, calls=%fused_computation.5 | convolution fusion | flops 5375000576 | bytes 15204352 | tf_op jit(solution)/shard_map/dot_general | solution.py:346
  49.2 0.3 pad_maximum_fusion
  49.5 1.6 %copy-done.2 = bf16[2,256,3072]{2,1,0:T(8,128)(2,1)} copy-done((bf16[2,256,3072]{2,1,0:T(8,128)(2,1)}, bf16[2,256,3072]{2,1,0:T(8,128)(2,1)S(1)}, u32[]{:S(2)}) %copy-start.2) | copy-done | bytes 3145752
  51.1 1.3 constant_dynamic-slice_fusion.2
  52.6 0.5 multiply_cosine_fusion
  53.2 2.9 %collective-permute-done.2 = bf16[1,256,3072]{2,1,0:T(8,128)(2,1)S(1)} collective-permute-done((bf16[1,256,3072]{2,1,0:T(8,128)(2,1)}, bf16[1,256,3072]{2,1,0:T(8,128)(2,1)S(1)}, u32[]{:S(2)}, u32[]{:S(2)}) %collective-permute-start.2) | collective-permute-done | bytes 1572896 | tf_op jit(solution)/shard_map/ppermute | solution.py:237
  56.0 1.9 %add_bitcast_fusion = f32[32,8,24,128]{3,1,2,0:T(8,128)S(1)} fusion(bf16[1,256,3072]{2,1,0:T(8,128)(2,1)S(1)} %collective-permute-done.2, bf16[2,256,3072]{2,1,0:T(8,128)(2,1)} %copy-done.2, s32[]{:T(128)S(6)} %select_n.211), kind=kLoop, calls=%fused_computation.4 | loop fusion | flops 2359296 | bytes 6291460
  58.0 0.6 copy.139
  58.7 0.4 add_convert_fusion.1
  59.1 0.8 subtract_convert_fusion
  59.9 1.4 pad_maximum_fusion.3
  61.3 0.5 copy.123
  62.0 1.3 fusion.10
  63.3 0.5 copy.99
  64.2 19.7 %shard_map.130 = (f32[64,64,1]{2,1,0:T(8,128)}, f32[64,64,1]{2,1,0:T(8,128)}, f32[64,64,128]{2,1,0:T(8,128)}) custom-call(s32[50]{0:T(128)} %req_ref.1, s32[64]{0:T(128)} %len_ref.1, s32[50]{0:T(128)} %blk_ref.1, bf16[64,64,128]{2,1,0:T(8,128)(2,1)} %bitcast.164, bf16[50,128,512]{2,1,0:T(8,128)(2,1)} %k_ref.1, bf16[50,128,512]{2,1,0:T(8,128)(2,1)} %v_ref.1), custom_call_target="tpu_custom_call" | custom-call | tf_op jit(solution)/shard_map/pallas_call | solution.py:209
  83.9 2.4 %reduce.1 = f32[64,64]{1,0:T(8,128)S(1)} reduce(f32[64,64,1]{2,1,0:T(8,128)} %get-tuple-element.7, f32[]{:T(128)} %constant.102), dimensions={2}, to_apply=%get-tuple-element.7.reduce_sub_computation | reduce | bytes 32772 | tf_op jit(solution)/shard_map/pallas_call | solution.py:209
  86.2 0.6 reduce.2
  86.9 1.8 %collective-permute-start.3 = (f32[2,2,2,1,8,64]{5,4,3,2,1,0:T(8,128)S(1)}, f32[2,2,2,1,8,64]{5,4,3,2,1,0:T(8,128)S(1)}, u32[]{:S(2)}, u32[]{:S(2)}) collective-permute-start(f32[2,2,2,1,8,64]{5,4,3,2,1,0:T(8,128)S(1)} %get-tuple-element.44), channel_id=1, source_target_pairs={{0,1},{1,0},{2,3},{3,2},{4,5},{5,4},{6,7},{7,6},{8,9},{9,8},{10,11... | collective-permute-start | bytes 49160 | tf_op jit(solution)/shard_map/ppermute | solution.py:281
  88.7 1.3 dynamic-slice_convert_fusion
  90.0 0.5 copy.106
  90.5 0.3 collective-permute-start.4
  90.9 1.9 %collective-permute-start.5 = (f32[2,2,1,1,8,64]{5,4,3,2,1,0:T(8,128)S(1)}, f32[2,2,1,1,8,64]{5,4,3,2,1,0:T(8,128)S(1)}, u32[]{:S(2)}, u32[]{:S(2)}) collective-permute-start(f32[2,2,1,1,8,64]{5,4,3,2,1,0:T(8,128)S(1)} %get-tuple-element.48), channel_id=1, source_target_pairs={{0,2},{1,3},{2,0},{3,1},{4,6},{5,7},{6,4},{7,5},{8,10},{9,11},{10,... | collective-permute-start | bytes 24584 | tf_op jit(solution)/shard_map/ppermute | solution.py:281
  92.8 1.9 %collective-permute-done.5 = f32[2,2,1,1,8,64]{5,4,3,2,1,0:T(8,128)S(1)} collective-permute-done((f32[2,2,1,1,8,64]{5,4,3,2,1,0:T(8,128)S(1)}, f32[2,2,1,1,8,64]{5,4,3,2,1,0:T(8,128)S(1)}, u32[]{:S(2)}, u32[]{:S(2)}) %collective-permute-start.5) | collective-permute-done | bytes 8224 | tf_op jit(solution)/shard_map/ppermute | solution.py:281
  94.7 2.9 %collective-permute-start.7 = (f32[2,1,1,1,8,64]{5,4,3,2,1,0:T(8,128)S(1)}, f32[2,1,1,1,8,64]{5,4,3,2,1,0:T(8,128)S(1)}, u32[]{:S(2)}, u32[]{:S(2)}) collective-permute-start(f32[2,1,1,1,8,64]{5,4,3,2,1,0:T(8,128)S(1)} %get-tuple-element.52), channel_id=1, source_target_pairs={{0,4},{1,5},{2,6},{3,7},{4,0},{5,1},{6,2},{7,3},{8,12},{9,13},{10,... | collective-permute-start | bytes 12296 | tf_op jit(solution)/shard_map/ppermute | solution.py:281
  97.7 1.7 %collective-permute-done.7 = f32[2,1,1,1,8,64]{5,4,3,2,1,0:T(8,128)S(1)} collective-permute-done((f32[2,1,1,1,8,64]{5,4,3,2,1,0:T(8,128)S(1)}, f32[2,1,1,1,8,64]{5,4,3,2,1,0:T(8,128)S(1)}, u32[]{:S(2)}, u32[]{:S(2)}) %collective-permute-start.7) | collective-permute-done | bytes 4128 | tf_op jit(solution)/shard_map/ppermute | solution.py:281
  99.5 4.7 %collective-permute-done.4 = bf16[2,2,1,8,64,128]{5,4,3,2,1,0:T(8,128)(2,1)S(1)} collective-permute-done((bf16[2,2,1,8,64,128]{5,4,3,2,1,0:T(8,128)(2,1)S(1)}, bf16[2,2,1,8,64,128]{5,4,3,2,1,0:T(8,128)(2,1)S(1)}, u32[]{:S(2)}, u32[]{:S(2)}) %collective-permute-start.4) | collective-permute-done | bytes 524320 | tf_op jit(solution)/shard_map/ppermute | solution.py:282
  104.3 1.8 %multiply_add_fusion = f32[2,2,1,8,64,128]{5,4,3,2,1,0:T(8,128)S(1)} fusion(bf16[2,2,1,8,64,128]{5,4,3,2,1,0:T(8,128)(2,1)S(1)} %collective-permute-done.4, f32[2,2,2,8,64,128]{5,4,3,2,1,0:T(8,128)} %bitcast.174, s32[]{:T(128)S(6)} %select_n.213, f32[2,2,8,64]{3,2,1,0:T(8,128)S(1)} %get-tuple-element.42, f32[2,2,8,64]{3,2,1,0:T(8,128)S(1)} %get-tuple-element.41), kind=kLoop, calls=%fused_computation.17 | loop fusion | flops 1048576 | bytes 2637828 | tf_op jit(solution)/shard_map/add | solution.py:291
  106.2 1.6 %collective-permute-start.6 = (bf16[2,1,1,8,64,128]{5,4,3,2,1,0:T(8,128)(2,1)S(1)}, bf16[2,1,1,8,64,128]{5,4,3,2,1,0:T(8,128)(2,1)S(1)}, u32[]{:S(2)}, u32[]{:S(2)}) collective-permute-start(bf16[2,1,1,8,64,128]{5,4,3,2,1,0:T(8,128)(2,1)S(1)} %dynamic-slice_convert_fusion.1), channel_id=1, source_target_pairs={{0,2},{1,3},{2,0},{3,1},{4,6},{5,7},{6,4},{7,5},{8,10},{9,11},{10,... | collective-permute-start | bytes 786440 | tf_op jit(solution)/shard_map/ppermute | solution.py:282
  108.4 0.2 convolution_multiply_fusion
  108.6 4.8 %collective-permute-done.6 = bf16[2,1,1,8,64,128]{5,4,3,2,1,0:T(8,128)(2,1)S(1)} collective-permute-done((bf16[2,1,1,8,64,128]{5,4,3,2,1,0:T(8,128)(2,1)S(1)}, bf16[2,1,1,8,64,128]{5,4,3,2,1,0:T(8,128)(2,1)S(1)}, u32[]{:S(2)}, u32[]{:S(2)}) %collective-permute-start.6) | collective-permute-done | bytes 262176 | tf_op jit(solution)/shard_map/ppermute | solution.py:282
  113.4 0.3 multiply_add_fusion.1
  113.8 2.7 %collective-permute-start.8 = (bf16[1,1,1,8,64,128]{5,4,3,2,1,0:T(8,128)(2,1)S(1)}, bf16[1,1,1,8,64,128]{5,4,3,2,1,0:T(8,128)(2,1)S(1)}, u32[]{:S(2)}, u32[]{:S(2)}) collective-permute-start(bf16[1,1,1,8,64,128]{5,4,3,2,1,0:T(8,128)(2,1)S(1)} %dynamic-slice_convert_fusion.2), channel_id=1, source_target_pairs={{0,4},{1,5},{2,6},{3,7},{4,0},{5,1},{6,2},{7,3},{8,12},{9,13},{10,... | collective-permute-start | bytes 393224 | tf_op jit(solution)/shard_map/ppermute | solution.py:282
  116.5 4.7 %collective-permute-done.8 = bf16[1,1,1,8,64,128]{5,4,3,2,1,0:T(8,128)(2,1)S(1)} collective-permute-done((bf16[1,1,1,8,64,128]{5,4,3,2,1,0:T(8,128)(2,1)S(1)}, bf16[1,1,1,8,64,128]{5,4,3,2,1,0:T(8,128)(2,1)S(1)}, u32[]{:S(2)}, u32[]{:S(2)}) %collective-permute-start.8) | collective-permute-done | bytes 131104 | tf_op jit(solution)/shard_map/ppermute | solution.py:282
  121.1 0.2 multiply_add_fusion.2
  121.4 0.3 fusion.12
  121.9 1.3 collective-permute-done.9
  123.2 5.9 %fusion.2 = bf16[2,8,4,2560]{3,1,2,0:T(8,128)(2,1)S(1)} fusion(bf16[2048,2560]{1,0:T(8,128)(2,1)} %param.16, bf16[8,4,2048]{2,0,1:T(8,128)(2,1)S(1)} %collective-permute-done.9, bf16[8,4,2048]{2,0,1:T(8,128)(2,1)S(1)} %convert_element_type.107, pred[]{:T(512)S(6)} %eq.21), kind=kOutput, calls=%fused_computation.2 | convolution fusion | flops 672432128 | bytes 11075585 | tf_op jit(solution)/shard_map/dot_general | solution.py:412
  129.2 1.6 collective-permute-start.10
  130.7 0.8 reshape_reshape.8
  131.5 4.0 %collective-permute-done.10 = bf16[1,8,4,2560]{3,1,2,0:T(8,128)(2,1)S(1)} collective-permute-done((bf16[1,8,4,2560]{3,1,2,0:T(8,128)(2,1)S(1)}, bf16[1,8,4,2560]{3,1,2,0:T(8,128)(2,1)S(1)}, u32[]{:S(2)}, u32[]{:S(2)}) %collective-permute-start.10) | collective-permute-done | bytes 163872 | tf_op jit(solution)/shard_map/ppermute | solution.py:237
  135.6 1.4 collective-permute-start.11
  136.9 0.4 pad_maximum_fusion.7
  137.3 0.8 convert_element_type.113
  138.1 1.6 %collective-permute-start.14 = (bf16[8,4,1280]{2,0,1:T(8,128)(2,1)S(1)}, bf16[8,4,1280]{2,0,1:T(8,128)(2,1)S(1)}, u32[]{:S(2)}, u32[]{:S(2)}) collective-permute-start(bf16[8,4,1280]{2,0,1:T(8,128)(2,1)S(1)} %get-tuple-element.39), channel_id=1, source_target_pairs={{0,4},{1,5},{2,6},{3,7},{4,0},{5,1},{6,2},{7,3},{8,12},{9,13},{10,... | collective-permute-start | bytes 245768 | tf_op jit(solution)/shard_map/ppermute | solution.py:254
  139.7 2.8 %collective-permute-done.11 = bf16[8,4,1280]{2,0,1:T(8,128)(2,1)S(1)} collective-permute-done((bf16[8,4,1280]{2,0,1:T(8,128)(2,1)S(1)}, bf16[8,4,1280]{2,0,1:T(8,128)(2,1)S(1)}, u32[]{:S(2)}, u32[]{:S(2)}) %collective-permute-start.11) | collective-permute-done | bytes 81952 | tf_op jit(solution)/shard_map/ppermute | solution.py:254
  142.6 1.5 collective-permute-start.12
  144.0 0.7 collective-permute-done.14
  144.7 0.5 collective-permute-start.15
  145.3 4.9 %collective-permute-done.15 = bf16[2,8,4,1280]{3,1,2,0:T(8,128)(2,1)S(1)} collective-permute-done((bf16[2,8,4,1280]{3,1,2,0:T(8,128)(2,1)S(1)}, bf16[2,8,4,1280]{3,1,2,0:T(8,128)(2,1)S(1)}, u32[]{:S(2)}, u32[]{:S(2)}) %collective-permute-start.15) | collective-permute-done | bytes 163872 | tf_op jit(solution)/shard_map/ppermute | solution.py:254
  150.3 1.4 collective-permute-start.16
  151.8 0.6 collective-permute-start.13
  152.4 6.0 %collective-permute-done.16 = bf16[2,2,8,4,1280]{4,2,3,0,1:T(8,128)(2,1)S(1)} collective-permute-done((bf16[2,2,8,4,1280]{4,2,3,0,1:T(8,128)(2,1)S(1)}, bf16[2,2,8,4,1280]{4,2,3,0,1:T(8,128)(2,1)S(1)}, u32[]{:S(2)}, u32[]{:S(2)}) %collective-permute-start.16) | collective-permute-done | bytes 327712 | tf_op jit(solution)/shard_map/ppermute | solution.py:254
  158.5 0.4 collective-permute-done.13
  159.2 2.1 %copy.119 = bf16[64,4,2560]{2,1,0:T(4,128)(2,1)} copy(bf16[64,4,2560]{2,0,1:T(8,128)(2,1)S(1)} %pad_maximum_fusion.2) | data formatting | bytes 2621440
  (75 shorter events, 2.9 us)
Async XLA Ops:
  0.6 38.5 %copy-start = (bf16[2560,512]{1,0:T(8,128)(2,1)S(1)}, bf16[2560,512]{1,0:T(8,128)(2,1)}, u32[]{:S(2)}) copy-start(bf16[2560,512]{1,0:T(8,128)(2,1)} %param.14) | copy-start | bytes 7864324
  0.6 35.6 %copy-start.5 = (f32[2560]{0:T(1024)S(1)}, f32[2560]{0:T(1024)}, u32[]{:S(2)}) copy-start(f32[2560]{0:T(1024)} %param.12) | copy-start | bytes 30724
  4.2 32.0 %collective-permute-start = (bf16[256,2560]{1,0:T(8,128)(2,1)}, bf16[256,2560]{1,0:T(8,128)(2,1)}, u32[]{:S(2)}, u32[]{:S(2)}) collective-permute-start(bf16[256,2560]{1,0:T(8,128)(2,1)} %reshape.731), channel_id=1, source_target_pairs={{0,8},{8,0},{1,9},{9,1},{2,10},{10,2},{3,11},{11,3},{4,12},{12,4},... | collective-permute-start | bytes 3932168 | tf_op jit(solution)/shard_map/ppermute | solution.py:324
  11.8 24.4 %collective-permute-start.1 = (f32[256]{0:T(256)S(1)}, f32[256]{0:T(256)S(1)}, u32[]{:S(2)}, u32[]{:S(2)}) collective-permute-start(f32[256]{0:T(256)S(1)} %psum.7), channel_id=1, source_target_pairs={{0,8},{8,0},{1,9},{9,1},{2,10},{10,2},{3,11},{11,3},{4,12},{12,4},... | collective-permute-start | bytes 3080 | tf_op jit(solution)/shard_map/ppermute | solution.py:327
  36.3 4.4 %copy-start.7 = (bf16[2560,512]{1,0:T(8,128)(2,1)S(1)}, bf16[2560,512]{1,0:T(8,128)(2,1)}, u32[]{:S(2)}) copy-start(bf16[2560,512]{1,0:T(8,128)(2,1)} %param.15) | copy-start | bytes 7864324
  39.1 3.1 %slice-start = ((s8[10485760]{0:T(1024)(128)(4,1)}), s8[4194304]{0:T(1024)(128)(4,1)S(1)}, s32[]{:S(2)}) async-start(s8[10485760]{0:T(1024)(128)(4,1)} %bitcast.199), calls=%async_computation | async-start | bytes 8388608
  39.1 3.5 %slice-start.1 = ((s8[10485760]{0:T(1024)(128)(4,1)}), s8[4194304]{0:T(1024)(128)(4,1)S(1)}, s32[]{:S(2)}) async-start(s8[10485760]{0:T(1024)(128)(4,1)} %bitcast.199), calls=%async_computation.1 | async-start | bytes 8388608
  40.7 2.7 %slice-start.2 = ((s8[10485760]{0:T(1024)(128)(4,1)}), s8[2097152]{0:T(1024)(128)(4,1)S(1)}, s32[]{:S(2)}) async-start(s8[10485760]{0:T(1024)(128)(4,1)} %bitcast.199), calls=%async_computation.2 | async-start | bytes 4194304
  49.5 1.6 %copy-start.2 = (bf16[2,256,3072]{2,1,0:T(8,128)(2,1)}, bf16[2,256,3072]{2,1,0:T(8,128)(2,1)S(1)}, u32[]{:S(2)}) copy-start(bf16[2,256,3072]{2,1,0:T(8,128)(2,1)S(1)} %pad_maximum_fusion) | copy-start | bytes 9437188
  51.1 1.3 copy-start.6
  52.4 3.6 %collective-permute-start.2 = (bf16[1,256,3072]{2,1,0:T(8,128)(2,1)}, bf16[1,256,3072]{2,1,0:T(8,128)(2,1)S(1)}, u32[]{:S(2)}, u32[]{:S(2)}) collective-permute-start(bf16[1,256,3072]{2,1,0:T(8,128)(2,1)} %constant_dynamic-slice_fusion.2), channel_id=1, source_target_pairs={{0,16},{16,0},{1,17},{17,1},{2,18},{18,2},{3,19},{19,3},{4,20},{20... | collective-permute-start | bytes 4718600 | tf_op jit(solution)/shard_map/ppermute | solution.py:237
  61.8 2.4 %copy-start.3 = (bf16[64,4,4,4,128]{4,3,1,2,0:T(4,128)(2,1)}, bf16[64,4,4,4,128]{4,3,1,2,0:T(4,128)(2,1)S(1)}, u32[]{:S(2)}) copy-start(bf16[64,4,4,4,128]{4,3,1,2,0:T(4,128)(2,1)S(1)} %copy.123) | copy-start | bytes 3145732
  83.9 2.4 %copy-start.4 = (f32[64,64,1]{2,1,0:T(8,128)S(1)}, f32[64,64,1]{2,1,0:T(8,128)}, u32[]{:S(2)}) copy-start(f32[64,64,1]{2,1,0:T(8,128)} %get-tuple-element.8) | copy-start | bytes 49156
  86.9 4.0 %collective-permute-start.3 = (f32[2,2,2,1,8,64]{5,4,3,2,1,0:T(8,128)S(1)}, f32[2,2,2,1,8,64]{5,4,3,2,1,0:T(8,128)S(1)}, u32[]{:S(2)}, u32[]{:S(2)}) collective-permute-start(f32[2,2,2,1,8,64]{5,4,3,2,1,0:T(8,128)S(1)} %get-tuple-element.44), channel_id=1, source_target_pairs={{0,1},{1,0},{2,3},{3,2},{4,5},{5,4},{6,7},{7,6},{8,9},{9,8},{10,11... | collective-permute-start | bytes 49160 | tf_op jit(solution)/shard_map/ppermute | solution.py:281
  90.5 13.8 %collective-permute-start.4 = (bf16[2,2,1,8,64,128]{5,4,3,2,1,0:T(8,128)(2,1)S(1)}, bf16[2,2,1,8,64,128]{5,4,3,2,1,0:T(8,128)(2,1)S(1)}, u32[]{:S(2)}, u32[]{:S(2)}) collective-permute-start(bf16[2,2,1,8,64,128]{5,4,3,2,1,0:T(8,128)(2,1)S(1)} %dynamic-slice_convert_fusion), channel_id=1, source_target_pairs={{0,1},{1,0},{2,3},{3,2},{4,5},{5,4},{6,7},{7,6},{8,9},{9,8},{10,11... | collective-permute-start | bytes 1572872 | tf_op jit(solution)/shard_map/ppermute | solution.py:282
  90.9 3.8 %collective-permute-start.5 = (f32[2,2,1,1,8,64]{5,4,3,2,1,0:T(8,128)S(1)}, f32[2,2,1,1,8,64]{5,4,3,2,1,0:T(8,128)S(1)}, u32[]{:S(2)}, u32[]{:S(2)}) collective-permute-start(f32[2,2,1,1,8,64]{5,4,3,2,1,0:T(8,128)S(1)} %get-tuple-element.48), channel_id=1, source_target_pairs={{0,2},{1,3},{2,0},{3,1},{4,6},{5,7},{6,4},{7,5},{8,10},{9,11},{10,... | collective-permute-start | bytes 24584 | tf_op jit(solution)/shard_map/ppermute | solution.py:281
  94.7 4.6 %collective-permute-start.7 = (f32[2,1,1,1,8,64]{5,4,3,2,1,0:T(8,128)S(1)}, f32[2,1,1,1,8,64]{5,4,3,2,1,0:T(8,128)S(1)}, u32[]{:S(2)}, u32[]{:S(2)}) collective-permute-start(f32[2,1,1,1,8,64]{5,4,3,2,1,0:T(8,128)S(1)} %get-tuple-element.52), channel_id=1, source_target_pairs={{0,4},{1,5},{2,6},{3,7},{4,0},{5,1},{6,2},{7,3},{8,12},{9,13},{10,... | collective-permute-start | bytes 12296 | tf_op jit(solution)/shard_map/ppermute | solution.py:281
  106.2 7.3 %collective-permute-start.6 = (bf16[2,1,1,8,64,128]{5,4,3,2,1,0:T(8,128)(2,1)S(1)}, bf16[2,1,1,8,64,128]{5,4,3,2,1,0:T(8,128)(2,1)S(1)}, u32[]{:S(2)}, u32[]{:S(2)}) collective-permute-start(bf16[2,1,1,8,64,128]{5,4,3,2,1,0:T(8,128)(2,1)S(1)} %dynamic-slice_convert_fusion.1), channel_id=1, source_target_pairs={{0,2},{1,3},{2,0},{3,1},{4,6},{5,7},{6,4},{7,5},{8,10},{9,11},{10,... | collective-permute-start | bytes 786440 | tf_op jit(solution)/shard_map/ppermute | solution.py:282
  113.8 7.3 %collective-permute-start.8 = (bf16[1,1,1,8,64,128]{5,4,3,2,1,0:T(8,128)(2,1)S(1)}, bf16[1,1,1,8,64,128]{5,4,3,2,1,0:T(8,128)(2,1)S(1)}, u32[]{:S(2)}, u32[]{:S(2)}) collective-permute-start(bf16[1,1,1,8,64,128]{5,4,3,2,1,0:T(8,128)(2,1)S(1)} %dynamic-slice_convert_fusion.2), channel_id=1, source_target_pairs={{0,4},{1,5},{2,6},{3,7},{4,0},{5,1},{6,2},{7,3},{8,12},{9,13},{10,... | collective-permute-start | bytes 393224 | tf_op jit(solution)/shard_map/ppermute | solution.py:282
  121.8 1.4 collective-permute-start.9
  129.2 6.3 %collective-permute-start.10 = (bf16[1,8,4,2560]{3,1,2,0:T(8,128)(2,1)S(1)}, bf16[1,8,4,2560]{3,1,2,0:T(8,128)(2,1)S(1)}, u32[]{:S(2)}, u32[]{:S(2)}) collective-permute-start(bf16[1,8,4,2560]{3,1,2,0:T(8,128)(2,1)S(1)} %constant_dynamic-slice_fusion.1), channel_id=1, source_target_pairs={{0,8},{8,0},{1,9},{9,1},{2,10},{10,2},{3,11},{11,3},{4,12},{12,4},... | collective-permute-start | bytes 491528 | tf_op jit(solution)/shard_map/ppermute | solution.py:237
  135.6 6.9 %collective-permute-start.11 = (bf16[8,4,1280]{2,0,1:T(8,128)(2,1)S(1)}, bf16[8,4,1280]{2,0,1:T(8,128)(2,1)S(1)}, u32[]{:S(2)}, u32[]{:S(2)}) collective-permute-start(bf16[8,4,1280]{2,0,1:T(8,128)(2,1)S(1)} %get-tuple-element.40), channel_id=1, source_target_pairs={{0,4},{1,5},{2,6},{3,7},{4,0},{5,1},{6,2},{7,3},{8,12},{9,13},{10,... | collective-permute-start | bytes 245768 | tf_op jit(solution)/shard_map/ppermute | solution.py:254
  138.1 6.6 %collective-permute-start.14 = (bf16[8,4,1280]{2,0,1:T(8,128)(2,1)S(1)}, bf16[8,4,1280]{2,0,1:T(8,128)(2,1)S(1)}, u32[]{:S(2)}, u32[]{:S(2)}) collective-permute-start(bf16[8,4,1280]{2,0,1:T(8,128)(2,1)S(1)} %get-tuple-element.39), channel_id=1, source_target_pairs={{0,4},{1,5},{2,6},{3,7},{4,0},{5,1},{6,2},{7,3},{8,12},{9,13},{10,... | collective-permute-start | bytes 245768 | tf_op jit(solution)/shard_map/ppermute | solution.py:254
  142.6 9.2 %collective-permute-start.12 = (bf16[2,8,4,1280]{3,1,2,0:T(8,128)(2,1)S(1)}, bf16[2,8,4,1280]{3,1,2,0:T(8,128)(2,1)S(1)}, u32[]{:S(2)}, u32[]{:S(2)}) collective-permute-start(bf16[2,8,4,1280]{3,1,2,0:T(8,128)(2,1)S(1)} %maximum_select_fusion.7), channel_id=1, source_target_pairs={{0,2},{1,3},{2,0},{3,1},{4,6},{5,7},{6,4},{7,5},{8,10},{9,11},{10,... | collective-permute-start | bytes 491528 | tf_op jit(solution)/shard_map/ppermute | solution.py:254
  144.7 5.5 %collective-permute-start.15 = (bf16[2,8,4,1280]{3,1,2,0:T(8,128)(2,1)S(1)}, bf16[2,8,4,1280]{3,1,2,0:T(8,128)(2,1)S(1)}, u32[]{:S(2)}, u32[]{:S(2)}) collective-permute-start(bf16[2,8,4,1280]{3,1,2,0:T(8,128)(2,1)S(1)} %maximum_select_fusion.9), channel_id=1, source_target_pairs={{0,1},{1,0},{2,3},{3,2},{4,5},{5,4},{6,7},{7,6},{8,9},{9,8},{10,11... | collective-permute-start | bytes 491528 | tf_op jit(solution)/shard_map/ppermute | solution.py:254
  150.3 8.1 %collective-permute-start.16 = (bf16[2,2,8,4,1280]{4,2,3,0,1:T(8,128)(2,1)S(1)}, bf16[2,2,8,4,1280]{4,2,3,0,1:T(8,128)(2,1)S(1)}, u32[]{:S(2)}, u32[]{:S(2)}) collective-permute-start(bf16[2,2,8,4,1280]{4,2,3,0,1:T(8,128)(2,1)S(1)} %maximum_select_fusion.5), channel_id=1, source_target_pairs={{0,2},{1,3},{2,0},{3,1},{4,6},{5,7},{6,4},{7,5},{8,10},{9,11},{10,... | collective-permute-start | bytes 983048 | tf_op jit(solution)/shard_map/ppermute | solution.py:254
  151.8 7.2 %collective-permute-start.13 = (bf16[2,2,8,4,1280]{4,2,3,0,1:T(8,128)(2,1)S(1)}, bf16[2,2,8,4,1280]{4,2,3,0,1:T(8,128)(2,1)S(1)}, u32[]{:S(2)}, u32[]{:S(2)}) collective-permute-start(bf16[2,2,8,4,1280]{4,2,3,0,1:T(8,128)(2,1)S(1)} %maximum_select_fusion.3), channel_id=1, source_target_pairs={{0,1},{1,0},{2,3},{3,2},{4,5},{5,4},{6,7},{7,6},{8,9},{9,8},{10,11... | collective-permute-start | bytes 983048 | tf_op jit(solution)/shard_map/ppermute | solution.py:254
  159.1 2.2 %copy-start.1 = (bf16[2560,512]{1,0:T(8,128)(2,1)S(1)}, bf16[2560,512]{1,0:T(8,128)(2,1)}, u32[]{:S(2)}) copy-start(bf16[2560,512]{1,0:T(8,128)(2,1)} %param.14) | copy-start | bytes 7864324
